TPU v7x, 32 devices: a whole 2x2x4 slice. The times are simulated.
32 devices in a mesh: groups: 2 (over y), row: 8 (over z, x), col: 2 (over core).
Axes of the slice: x: 2, y: 2, z: 4, core: 2. Of those that a mesh axis runs over, the one named last changes fastest.
Arguments:
- tokens: bfloat16 [4, 1024, 3584], P('groups', 'row', 'col'), parts along dimension 0, may hold values from -40 to 40
- gain: float32 [3584], replicated, may hold values from 0.5 to 2
- w_query: bfloat16 [3584, 1792], P('row', 'col'), may hold values from -0.125 to 0.125
- b_query: float32 [1792], P('col'), may hold values from -24 to 24
- key_weight: bfloat16 [3584, 256], P('row', 'col'), may hold values from -0.125 to 0.125
- b_key: float32 [256], P('col'), may hold values from -24 to 24
- value_weight: bfloat16 [3584, 256], P('row', 'col'), may hold values from -0.09375 to 0.09375
- value_bias: float32 [256], P('col'), may hold values from -3 to 3
- random_block_index: int32 [4, 16, 14, 2], P('groups'), parts along dimension 0, may hold values from 0 to 15, as said below
- global_block_index: int32 [4, 2, 2], P('groups'), parts along dimension 0, may hold values from 0 to 15
Outputs:
- context: bfloat16 [4, 1024, 1792], P('groups', 'row', 'col'), parts along dimension 0
There are 2 independent parts, one for each index of `groups`. A program takes and returns all parts, laid end to end along the dimension named above; an argument that names none is the same for every part. Nothing has to cross between parts.
Inputs may be any that keep to these rules, and one draw needn't show every extreme that they name: `random_block_index`: A request group is the 56 entries of both passages whose query block lies in one aligned run of 2 blocks and whose head lies in one aligned run of 7 heads. In every request group at most 7 entries name blocks of any one aligned run of 2 blocks, and some run is named exactly 7 times.
All inputs are finite; a program needn't handle non-finite values.
Results may differ from a plain program's by a relative error of at most 0.003.
The roundings to bfloat16 on the way count: a program that leaves them out, or rounds other values in their place, can miss the bound.
Values may be sent and summed in bfloat16 or wider, within the bound.
No kernel may reach another device: no remote copies, remote signals or barrier semaphores. Data moves between devices by JAX's collectives and lax.ppermute only.
A program may use at most 128 MiB of HBM per device.

v0:
```python
import math

import jax
import jax.numpy as jnp
from jax import lax
from jax.sharding import PartitionSpec as P

HEAD_SIZE = 128
BLOCK_TOKENS = 64
RANDOM_BLOCKS = 2
GLOBAL_BLOCKS = 2


rope_base = 1000000.0
norm_eps = 1e-06


def broadcast(block, axis, source):
    block = jnp.where(lax.axis_index(axis) == source, block, jnp.zeros_like(block))
    return lax.psum(block, axis)


def padded_2(shard, sides, width):
    for axis, dim in sides:
        count, length = (lax.axis_size(axis), shard.shape[dim])
        up = [(i, (i + 1) % count) for i in range(count - 1)]
        down = [(j, i) for i, j in up]
        last = lax.slice_in_dim(shard, length - width, length, axis=dim)
        leading = lax.slice_in_dim(shard, 0, width, axis=dim)
        before = lax.ppermute(last, axis, up)
        after = lax.ppermute(leading, axis, down)
        shard = jnp.concatenate([before, shard, after], axis=dim)
    return shard


def apply_rotation(values, token_positions):
    half = values.shape[-1] // 2
    freqs = 1.0 / rope_base ** (jnp.arange(half, dtype=jnp.float32) * 2.0 / values.shape[-1])
    angles = token_positions[:, None] * freqs[None, :]
    cosine = jnp.concatenate([jnp.cos(angles), jnp.cos(angles)], axis=-1)[None, :, None, :]
    sine = jnp.concatenate([jnp.sin(angles), jnp.sin(angles)], axis=-1)[None, :, None, :]
    turned = jnp.concatenate([-values[..., half:], values[..., :half]], axis=-1)
    return values * cosine + turned * sine


def shards(
    tokens,
    gain,
    w_query,
    b_query,
    key_weight,
    b_key,
    value_weight,
    value_bias,
    random_block_index,
    global_block_index,
):
    row_count = lax.axis_size("row")
    here = lax.axis_index("row")
    column = lax.axis_index("col")
    passages, length, _ = tokens.shape
    heads_here = w_query.shape[1] // HEAD_SIZE
    pairs_here = key_weight.shape[1] // HEAD_SIZE
    passage_groups = heads_here // pairs_here
    per_device = length // BLOCK_TOKENS
    scale = 1.0 / math.sqrt(HEAD_SIZE)
    whole = lax.all_gather(tokens, "col", axis=2, tiled=True)
    widened = whole.astype(jnp.float32)
    power = jnp.mean(widened * widened, axis=-1, keepdims=True)
    normed = (
        (widened * lax.rsqrt(power + norm_eps) * gain)
        .astype(jnp.bfloat16)
        .reshape(passages * length, -1)
    )
    token_positions = (here * length + jnp.arange(length, dtype=jnp.int32)).astype(jnp.float32)

    def project(panel):
        return jnp.dot(normed, panel, preferred_element_type=jnp.float32)

    def broadcast_global(own, entry, passage_index, local_head):
        owner = entry // per_device
        offset = entry % per_device
        candidate = lax.dynamic_index_in_dim(
            own[passage_index, :, local_head], offset, 0, keepdims=False
        )
        return broadcast(candidate, "row", owner)

    query_panel, key_panel, value_panel = (
        lax.all_gather(w_query, "row", axis=0, tiled=True),
        lax.all_gather(key_weight, "row", axis=0, tiled=True),
        lax.all_gather(value_weight, "row", axis=0, tiled=True),
    )
    key = apply_rotation(
        (project(key_panel) + b_key).reshape(passages, length, pairs_here, HEAD_SIZE),
        token_positions,
    ).astype(jnp.bfloat16)
    value_rows = (
        (project(value_panel) + value_bias)
        .astype(jnp.bfloat16)
        .reshape(passages, length, pairs_here, HEAD_SIZE)
    )
    pairs = jnp.concatenate([key, value_rows], axis=-1)
    width = pairs_here * 2 * HEAD_SIZE
    padded = padded_2(pairs.reshape(passages, length, width), (("row", 1),), BLOCK_TOKENS)
    padded_blocks = padded.reshape(
        passages, per_device + 2, BLOCK_TOKENS, pairs_here, 2 * HEAD_SIZE
    )
    window = jnp.stack([padded_blocks[:, step : step + per_device] for step in range(3)], axis=2)
    window = window.reshape(passages, per_device, 3 * BLOCK_TOKENS, pairs_here, 2 * HEAD_SIZE)
    own = pairs.reshape(passages, per_device, BLOCK_TOKENS, pairs_here, 2 * HEAD_SIZE).transpose(
        0, 1, 3, 2, 4
    )
    global_here = lax.dynamic_slice_in_dim(global_block_index, column * pairs_here, pairs_here, 1)
    global_pairs = jnp.stack(
        [
            jnp.stack(
                [
                    jnp.stack(
                        [
                            broadcast_global(
                                own, global_here[passage_index, 0, slot], passage_index, 0
                            )
                            for slot in range(GLOBAL_BLOCKS)
                        ]
                    )
                ]
            )
            for passage_index in range(passages)
        ]
    )
    global_pairs = global_pairs.reshape(
        passages, pairs_here, GLOBAL_BLOCKS * BLOCK_TOKENS, 2 * HEAD_SIZE
    )
    selected = lax.dynamic_slice_in_dim(random_block_index, column * heads_here, heads_here, 2)
    rotation_table = selected.reshape(passages, row_count, per_device, heads_here, RANDOM_BLOCKS)
    rotation_table = rotation_table.transpose(1, 0, 2, 3, 4).reshape(row_count, -1)
    owners = rotation_table // per_device
    wanted = rotation_table.shape[1]
    capacity = (wanted + row_count - 1) // row_count
    order = jnp.arange(wanted, dtype=jnp.int32)
    earlier = order[None, :] < order[:, None]
    matches = (owners[:, :, None] == owners[:, None, :]) & earlier[None, :, :]
    rank = jnp.sum(matches, axis=2, dtype=jnp.int32)
    passage_of = order // (per_device * heads_here * RANDOM_BLOCKS)
    head_of = order // RANDOM_BLOCKS % heads_here
    source = (passage_of[None, :] * per_device + rotation_table % per_device) * pairs_here + (
        head_of // passage_groups
    )[None, :]
    slots = jnp.arange(capacity, dtype=jnp.int32)
    chosen = (owners[:, None, :] == here) & (rank[:, None, :] == slots[None, :, None])
    valid = jnp.any(chosen, axis=2)
    pick = jnp.sum(jnp.where(chosen, source[:, None, :], 0), axis=2)
    flat_blocks = own.reshape(-1, BLOCK_TOKENS, 2 * HEAD_SIZE)
    outgoing = jnp.where(valid[:, :, None, None], flat_blocks[pick], jnp.zeros((), jnp.bfloat16))
    incoming = lax.all_to_all(outgoing, "row", split_axis=0, concat_axis=0, tiled=True)
    mine_owner = lax.dynamic_index_in_dim(owners, here, 0, keepdims=False)
    mine_rank = lax.dynamic_index_in_dim(rank, here, 0, keepdims=False)
    arrived = incoming.reshape(row_count * capacity, BLOCK_TOKENS, 2 * HEAD_SIZE)[
        mine_owner * capacity + mine_rank
    ]
    arrived = arrived.reshape(
        passages,
        per_device,
        pairs_here,
        passage_groups,
        RANDOM_BLOCKS * BLOCK_TOKENS,
        2 * HEAD_SIZE,
    )
    window, global_pairs, arrived = (window, global_pairs, arrived)
    shaped = (project(query_panel) + b_query).reshape(passages, length, heads_here, HEAD_SIZE)
    query_rows = apply_rotation(shaped, token_positions).astype(jnp.bfloat16)
    query_block_rows = query_rows.reshape(
        passages, per_device, BLOCK_TOKENS, pairs_here, passage_groups, HEAD_SIZE
    )
    first = jnp.einsum(
        "sqbkgh,sqwkh->sqkgbw",
        query_block_rows,
        window[..., :HEAD_SIZE],
        preferred_element_type=jnp.float32,
    )
    second = jnp.einsum(
        "sqbkgh,skwh->sqkgbw",
        query_block_rows,
        global_pairs[..., :HEAD_SIZE],
        preferred_element_type=jnp.float32,
    )
    third = jnp.einsum(
        "sqbkgh,sqkgwh->sqkgbw",
        query_block_rows,
        arrived[..., :HEAD_SIZE],
        preferred_element_type=jnp.float32,
    )
    scores = jnp.concatenate([first, second, third], axis=-1) * scale
    nearby_blocks = (
        here * per_device
        + jnp.arange(per_device, dtype=jnp.int32)[:, None]
        + jnp.arange(3, dtype=jnp.int32)[None, :]
        - 1
    )
    inside = (nearby_blocks >= 0) & (nearby_blocks < row_count * per_device)
    mask = jnp.concatenate(
        [
            jnp.repeat(inside, BLOCK_TOKENS, axis=1),
            jnp.ones((per_device, (GLOBAL_BLOCKS + RANDOM_BLOCKS) * BLOCK_TOKENS), dtype=jnp.bool_),
        ],
        axis=1,
    )
    scores = jnp.where(mask[None, :, None, None, None, :], scores, -jnp.inf)
    top = jnp.max(scores, axis=-1, keepdims=True)
    weights = jnp.exp(scores - top)
    probs = (weights / jnp.sum(weights, axis=-1, keepdims=True)).astype(jnp.bfloat16)
    near_probs = probs[..., : 3 * BLOCK_TOKENS]
    global_probs = probs[..., 3 * BLOCK_TOKENS : (3 + GLOBAL_BLOCKS) * BLOCK_TOKENS]
    random_probs = probs[..., (3 + GLOBAL_BLOCKS) * BLOCK_TOKENS :]
    mixed = jnp.einsum(
        "sqkgbw,sqwkh->sqbkgh",
        near_probs,
        window[..., HEAD_SIZE:],
        preferred_element_type=jnp.float32,
    )
    mixed = mixed + jnp.einsum(
        "sqkgbw,skwh->sqbkgh",
        global_probs,
        global_pairs[..., HEAD_SIZE:],
        preferred_element_type=jnp.float32,
    )
    mixed = mixed + jnp.einsum(
        "sqkgbw,sqkgwh->sqbkgh",
        random_probs,
        arrived[..., HEAD_SIZE:],
        preferred_element_type=jnp.float32,
    )
    return mixed.reshape(passages, length, heads_here * HEAD_SIZE).astype(jnp.bfloat16)


def solution(mesh):
    placed = (
        P("groups", "row", "col"),
        P(),
        P("row", "col"),
        P("col"),
        P("row", "col"),
        P("col"),
        P("row", "col"),
        P("col"),
        P("groups", None, None, None),
        P("groups", None, None),
    )
    return jax.shard_map(
        shards, mesh=mesh, in_specs=placed, out_specs=P("groups", "row", "col"), check_vma=False
    )
```

profile of v0, /device:TPU:0, one launch (start us, length us, event | category | flops | bytes accessed | tf_op | source)
XLA Modules:
  0.0 309.3 jit_solution(14698062382800990715)
XLA Ops:
  6.5 0.7 all-gather.3.cloned.1.call-update
  7.3 1.4 constant_dynamic-slice_fusion.5
  19.0 36.6 %all_gather.13 = bf16[3584,128]{1,0:T(8,128)(2,1)} all-gather(bf16[448,128]{1,0:T(8,128)(2,1)} %param.14), channel_id=1, replica_groups=mesh['groups'=2,'row'=8,'col'=2] {'row'}, dimensions={0}, use_global_device_ids=true | all-gather | bytes 1032192 | tf_op jit(solution)/shard_map/all_gather | solution.py:90
  55.5 32.6 %all_gather.14 = bf16[3584,128]{1,0:T(8,128)(2,1)S(1)} all-gather(bf16[448,128]{1,0:T(8,128)(2,1)} %param.16), channel_id=1, replica_groups=mesh['groups'=2,'row'=8,'col'=2] {'row'}, dimensions={0}, use_global_device_ids=true | all-gather | bytes 1032192 | tf_op jit(solution)/shard_map/all_gather | solution.py:91
  88.1 2.0 fusion
  90.1 2.0 fusion.2
  95.0 0.7 all-gather.5.cloned.1.call-update
  97.4 2.0 gather_fusion
  99.3 3.0 broadcast_select_fusion
  102.3 5.9 %all-to-all-start = ((bf16[8,7,64,256]{3,2,1,0:T(8,128)(2,1)}), bf16[8,7,64,256]{3,2,1,0:T(8,128)(2,1)}, u32[]{:S(2)}, u32[]{:S(2)}) async-start(bf16[8,7,64,256]{3,2,1,0:T(8,128)(2,1)} %broadcast_select_fusion), calls=%async_computation | async-start | bytes 3670016 | tf_op jit(solution)/shard_map/all_to_all | solution.py:155
  108.8 0.8 pad_maximum_fusion.7
  109.6 3.9 %collective-permute-start = (bf16[2,64,256]{2,1,0:T(8,128)(2,1)S(1)}, bf16[2,64,256]{2,1,0:T(8,128)(2,1)S(1)}, u32[]{:S(2)}, u32[]{:S(2)}) collective-permute-start(bf16[2,64,256]{2,1,0:T(8,128)(2,1)S(1)} %get-tuple-element.16), channel_id=1, source_target_pairs={{0,2},{2,4},{4,6},{6,8},{8,10},{10,12},{12,14},{1,3},{3,5},{5,7},{... | collective-permute-start | bytes 196616 | tf_op jit(solution)/shard_map/ppermute | solution.py:30
  113.5 1.5 collective-permute-start.1
  115.0 0.7 collective-permute-done
  115.7 5.5 %collective-permute-done.1 = bf16[2,64,256]{2,1,0:T(8,128)(2,1)S(1)} collective-permute-done((bf16[2,64,256]{2,1,0:T(8,128)(2,1)S(1)}, bf16[2,64,256]{2,1,0:T(8,128)(2,1)S(1)}, u32[]{:S(2)}, u32[]{:S(2)}) %collective-permute-start.1) | collective-permute-done | bytes 65568 | tf_op jit(solution)/shard_map/ppermute | solution.py:31
  121.2 0.8 pad_maximum_fusion
  122.0 55.7 %all-reduce.4.cloned.1.call-done = (bf16[1,64,256]{2,1,0:T(8,128)(2,1)}, bf16[1,64,256]{2,1,0:T(8,128)(2,1)}, bf16[1,64,256]{2,1,0:T(8,128)(2,1)}, bf16[1,64,256]{2,1,0:T(8,128)(2,1)}) async-done(((bf16[1,64,256]{2,1,0:T(8,128)(2,1)}, bf16[1,64,256]{2,1,0:T(8,128)(2,1)}, bf16[1,64,256]{2,1,0:T(8,128)(2,1)}, bf16[1,64,256]{2,1,0:T(8,128)(2,1)}), (bf16[1,64,256]{2,1,0:T(8,128)(2,1)}, ...) | async-done | bytes 131088 | tf_op jit(solution)/shard_map/psum | solution.py:20
  177.8 0.8 pad_maximum_fusion.9
  178.6 0.8 pad_maximum_fusion.10
  179.3 3.5 %gather_fusion.1 = bf16[56,64,256]{2,1,0:T(8,128)(2,1)} fusion(bf16[56,64,256]{2,1,0:T(8,128)(2,1)} %bitcast.44, s32[1024]{0:T(1024)S(1)} %pad_clamp_fusion), kind=kCustom, calls=%fused_computation.1 | custom fusion | bytes 3670240 | tf_op jit(solution)/shard_map/gather | solution.py:158
  182.8 97.3 %all-gather.5.cloned.1.call-done = bf16[3584,896]{1,0:T(8,128)(2,1)} async-done(((bf16[448,896]{1,0:T(8,128)(2,1)}), bf16[3584,896]{1,0:T(8,128)(2,1)}) %all-gather.5.cloned.1.call-update) | async-done | bytes 6422544 | tf_op jit(solution)/shard_map/all_gather | solution.py:89
  280.2 4.9 %convolution_add_fusion = f32[256,896]{1,0:T(8,128)S(1)} fusion(bf16[256,3584]{1,0:T(8,128)(2,1)S(1)} %bitcast.127, bf16[3584,896]{1,0:T(8,128)(2,1)} %all-gather.5.cloned.1.call-done, f32[896]{0:T(1024)S(1)} %copy-done.7), kind=kOutput, calls=%fused_computation.21 | convolution fusion | flops 1644396544 | bytes 9178624 | tf_op jit(solution)/shard_map/dot_general | solution.py:78
  285.3 1.1 reshape.570
  286.4 1.3 fusion.41
  288.0 0.8 neg.7
  288.8 1.5 copy.94
  290.3 2.0 fusion.10
  292.3 0.7 convolution_bitcast_fusion.5
  293.7 1.5 fusion.11
  295.2 2.4 fusion.4
  297.6 2.4 divide_convert_fusion
  301.5 1.3 convert_element_type.71
  (75 shorter events, 8.2 us)
Async XLA Ops:
  6.5 89.2 %copy-start = (s32[2,16,14,2]{1,3,2,0:T(2,128)S(1)}, s32[2,16,14,2]{1,3,2,0:T(2,128)}, u32[]{:S(2)}) copy-start(s32[2,16,14,2]{1,3,2,0:T(2,128)} %param.18) | copy-start | bytes 10756
  6.5 83.6 %copy-start.4 = (f32[3584]{0:T(1024)S(1)}, f32[3584]{0:T(1024)}, u32[]{:S(2)}) copy-start(f32[3584]{0:T(1024)} %param.11) | copy-start | bytes 43012
  6.5 81.5 %all-gather.3.cloned.1.call-start = ((), (), s32[]{:S(2)}) async-start(), calls=%async_computation.1 | async-start | bytes 2752512 | tf_op jit(solution)/shard_map/all_gather | solution.py:67
  7.3 170.5 %all-reduce.4.cloned.1.call-start = ((), (), s32[]{:S(2)}) async-start(), calls=%async_computation.3 | async-start | bytes 262144 | tf_op jit(solution)/shard_map/psum | solution.py:20
  18.9 73.2 %copy-start.6 = (f32[128]{0:T(128)S(1)}, f32[128]{0:T(128)}, u32[]{:S(2)}) copy-start(f32[128]{0:T(128)} %param.15) | copy-start | bytes 1540
  88.1 4.1 %copy-start.2 = (bf16[3584,128]{1,0:T(8,128)(2,1)S(1)}, bf16[3584,128]{1,0:T(8,128)(2,1)}, u32[]{:S(2)}) copy-start(bf16[3584,128]{1,0:T(8,128)(2,1)} %all_gather.13) | copy-start | bytes 2752516
  90.1 2.8 copy-start.5
  95.0 185.2 %all-gather.5.cloned.1.call-start = ((), (), s32[]{:S(2)}) async-start(), calls=%async_computation.2 | async-start | bytes 7225344 | tf_op jit(solution)/shard_map/all_gather | solution.py:89
  102.3 77.1 %all-to-all-start = ((bf16[8,7,64,256]{3,2,1,0:T(8,128)(2,1)}), bf16[8,7,64,256]{3,2,1,0:T(8,128)(2,1)}, u32[]{:S(2)}, u32[]{:S(2)}) async-start(bf16[8,7,64,256]{3,2,1,0:T(8,128)(2,1)} %broadcast_select_fusion), calls=%async_computation | async-start | bytes 3670016 | tf_op jit(solution)/shard_map/all_to_all | solution.py:155
  108.1 172.0 %copy-start.7 = (f32[896]{0:T(1024)S(1)}, f32[896]{0:T(1024)}, u32[]{:S(2)}) copy-start(f32[896]{0:T(1024)} %param.13) | copy-start | bytes 10756
  109.6 6.1 %collective-permute-start = (bf16[2,64,256]{2,1,0:T(8,128)(2,1)S(1)}, bf16[2,64,256]{2,1,0:T(8,128)(2,1)S(1)}, u32[]{:S(2)}, u32[]{:S(2)}) collective-permute-start(bf16[2,64,256]{2,1,0:T(8,128)(2,1)S(1)} %get-tuple-element.16), channel_id=1, source_target_pairs={{0,2},{2,4},{4,6},{6,8},{8,10},{10,12},{12,14},{1,3},{3,5},{5,7},{... | collective-permute-start | bytes 196616 | tf_op jit(solution)/shard_map/ppermute | solution.py:30
  113.5 7.7 %collective-permute-start.1 = (bf16[2,64,256]{2,1,0:T(8,128)(2,1)S(1)}, bf16[2,64,256]{2,1,0:T(8,128)(2,1)S(1)}, u32[]{:S(2)}, u32[]{:S(2)}) collective-permute-start(bf16[2,64,256]{2,1,0:T(8,128)(2,1)S(1)} %get-tuple-element.17), channel_id=1, source_target_pairs={{2,0},{4,2},{6,4},{8,6},{10,8},{12,10},{14,12},{3,1},{5,3},{7,5},{... | collective-permute-start | bytes 196616 | tf_op jit(solution)/shard_map/ppermute | solution.py:31
  287.7 4.6 %copy-start.1 = (bf16[56,64,256]{2,1,0:T(8,128)(2,1)S(1)}, bf16[56,64,256]{2,1,0:T(8,128)(2,1)}, u32[]{:S(2)}) copy-start(bf16[56,64,256]{2,1,0:T(8,128)(2,1)} %gather_fusion.1) | copy-start | bytes 5505028
  288.8 4.2 %copy-start.3 = (bf16[2,2,3,64,1,256]{5,3,2,1,0,4:T(8,128)(2,1)S(1)}, bf16[2,2,3,64,1,256]{5,3,2,1,0,4:T(8,128)(2,1)}, u32[]{:S(2)}) copy-start(bf16[2,2,3,64,1,256]{5,3,2,1,0,4:T(8,128)(2,1)} %pad_maximum_fusion) | copy-start | bytes 1179652
Sparse Core Ops, SparseCore 0:
  8.9 12.8 all-gather.2
  95.1 82.6 all-reduce.3
  180.2 99.9 all-gather.4
where the time goes:
time: 310 us; the launch traced here: 309 us
  waiting for transfers between devices  161 us (52%)
  blocking collectives  69.1 us (22%)
  between operations  23.3 us (8%)
  other arithmetic  22.5 us (7%)
  local copies, waits for them, and re-layouts  13.6 us (4%)
  starting transfers between devices  11.3 us (4%)
  matrix products  8.79 us (3%)
    all_gather x1, waiting for transfers between devices, shards(): lax.all_gather(w_query, 'row', axis=0, tiled=True)  97.3 us
    psum x1, waiting for transfers between devices, broadcast(): return lax.psum(block, axis)  55.7 us
    all_gather x1, blocking collectives, shards(): lax.all_gather(key_weight, 'row', axis=0, tiled=True)  36.6 us
    all_gather x1, blocking collectives, shards(): lax.all_gather(value_weight, 'row', axis=0, tiled=True)  32.6 us
  transfers between devices with their start and end apart: 6, of which 4 were waited for; matrix products, arithmetic and copies ran while one was open for 5% of the time, Pallas kernels for 0%

commit v1 on v0

v1 whole, which is shorter than its diff:
```python
import math

import jax
import jax.numpy as jnp
from jax import lax
from jax.sharding import PartitionSpec as P

HEAD_SIZE = 128
BLOCK_TOKENS = 64
RANDOM_BLOCKS = 2
GLOBAL_BLOCKS = 2


rope_base = 1000000.0
norm_eps = 1e-06

SWAP = [(0, 1), (1, 0)]


def apply_rotation(values, token_positions):
    half = values.shape[-1] // 2
    freqs = 1.0 / rope_base ** (jnp.arange(half, dtype=jnp.float32) * 2.0 / values.shape[-1])
    angles = token_positions[:, None] * freqs[None, :]
    cosine = jnp.concatenate([jnp.cos(angles), jnp.cos(angles)], axis=-1)[None, :, None, :]
    sine = jnp.concatenate([jnp.sin(angles), jnp.sin(angles)], axis=-1)[None, :, None, :]
    turned = jnp.concatenate([-values[..., half:], values[..., :half]], axis=-1)
    return values * cosine + turned * sine


def shards(
    tokens,
    gain,
    w_query,
    b_query,
    key_weight,
    b_key,
    value_weight,
    value_bias,
    random_block_index,
    global_block_index,
):
    row_count = lax.axis_size("row")
    here = lax.axis_index("row")
    column = lax.axis_index("col")
    group = lax.axis_index("groups")
    passages, length, _ = tokens.shape
    heads_here = w_query.shape[1] // HEAD_SIZE
    pairs_here = key_weight.shape[1] // HEAD_SIZE
    passage_groups = heads_here // pairs_here
    per_device = length // BLOCK_TOKENS
    passage_blocks = row_count * per_device
    scale = 1.0 / math.sqrt(HEAD_SIZE)

    rotary_cols = (heads_here + pairs_here) * HEAD_SIZE
    split = rotary_cols // 2
    value_cols = pairs_here * HEAD_SIZE
    value_split = value_cols // 2
    rotary_w = jnp.concatenate([w_query, key_weight], axis=1)
    rotary_b = jnp.concatenate([b_query, b_key], axis=0)
    first = group == 0
    panel = jnp.where(
        first,
        jnp.concatenate([rotary_w[:, :split], value_weight[:, :value_split]], axis=1),
        jnp.concatenate([rotary_w[:, split:], value_weight[:, value_split:]], axis=1),
    )
    panel_bias = jnp.where(
        first,
        jnp.concatenate([rotary_b[:split], value_bias[:value_split]]),
        jnp.concatenate([rotary_b[split:], value_bias[value_split:]]),
    )
    full_panel = lax.all_gather(panel, "row", axis=0, tiled=True)

    other_half = lax.ppermute(tokens, "col", SWAP)
    whole = jnp.where(
        column == 0,
        jnp.concatenate([tokens, other_half], axis=2),
        jnp.concatenate([other_half, tokens], axis=2),
    )
    partner = lax.ppermute(whole, "groups", SWAP)
    both = jnp.concatenate([whole, partner], axis=0)
    widened = both.astype(jnp.float32)
    power = jnp.mean(widened * widened, axis=-1, keepdims=True)
    normed = (
        (widened * lax.rsqrt(power + norm_eps) * gain)
        .astype(jnp.bfloat16)
        .reshape(2 * passages * length, -1)
    )
    token_positions = (here * length + jnp.arange(length, dtype=jnp.int32)).astype(jnp.float32)

    summed = jnp.dot(normed, full_panel, preferred_element_type=jnp.float32) + panel_bias
    summed = summed.reshape(2 * passages, length, split + value_split)
    turned = apply_rotation(
        summed[..., :split].reshape(2 * passages, length, split // HEAD_SIZE, HEAD_SIZE),
        token_positions,
    ).astype(jnp.bfloat16)
    result = jnp.concatenate(
        [turned.reshape(2 * passages, length, split), summed[..., split:].astype(jnp.bfloat16)],
        axis=-1,
    )
    mine = result[:passages]
    returned = lax.ppermute(result[passages:], "groups", SWAP)
    low = jnp.where(first, mine, returned)
    high = jnp.where(first, returned, mine)
    rotary_rows = jnp.concatenate([low[..., :split], high[..., :split]], axis=-1)
    query_rows = rotary_rows[..., : heads_here * HEAD_SIZE]
    key = rotary_rows[..., heads_here * HEAD_SIZE :]
    value_rows = jnp.concatenate([low[..., split:], high[..., split:]], axis=-1)

    pairs = jnp.concatenate([key, value_rows], axis=-1)
    gathered = lax.all_gather(pairs, "row", axis=0, tiled=False)
    gathered = gathered.transpose(1, 0, 2, 3).reshape(
        passages, passage_blocks, BLOCK_TOKENS, pairs_here, 2 * HEAD_SIZE
    )
    kv_blocks = gathered[:, :, :, 0]

    local_blocks = here * per_device + jnp.arange(per_device, dtype=jnp.int32)
    nearby_blocks = local_blocks[:, None] + jnp.arange(3, dtype=jnp.int32)[None, :] - 1
    inside = (nearby_blocks >= 0) & (nearby_blocks < passage_blocks)
    nearby_clamped = jnp.clip(nearby_blocks, 0, passage_blocks - 1)
    passage_ids = jnp.arange(passages, dtype=jnp.int32)
    window = kv_blocks[passage_ids[:, None, None], nearby_clamped[None]]
    window = window.reshape(passages, per_device, 3 * BLOCK_TOKENS, 2 * HEAD_SIZE)

    global_here = lax.dynamic_slice_in_dim(global_block_index, column * pairs_here, pairs_here, 1)
    global_pairs = kv_blocks[passage_ids[:, None], global_here[:, 0, :]]
    global_pairs = global_pairs.reshape(passages, GLOBAL_BLOCKS * BLOCK_TOKENS, 2 * HEAD_SIZE)

    selected = lax.dynamic_slice_in_dim(random_block_index, column * heads_here, heads_here, 2)
    selected = lax.dynamic_slice_in_dim(selected, here * per_device, per_device, 1)
    arrived = kv_blocks[passage_ids[:, None, None, None], selected]
    arrived = arrived.reshape(
        passages, per_device, heads_here, RANDOM_BLOCKS * BLOCK_TOKENS, 2 * HEAD_SIZE
    )

    query_block_rows = query_rows.reshape(
        passages, per_device, BLOCK_TOKENS, heads_here, HEAD_SIZE
    )
    first_scores = jnp.einsum(
        "sqbgh,sqwh->sqgbw",
        query_block_rows,
        window[..., :HEAD_SIZE],
        preferred_element_type=jnp.float32,
    )
    second_scores = jnp.einsum(
        "sqbgh,swh->sqgbw",
        query_block_rows,
        global_pairs[..., :HEAD_SIZE],
        preferred_element_type=jnp.float32,
    )
    third_scores = jnp.einsum(
        "sqbgh,sqgwh->sqgbw",
        query_block_rows,
        arrived[..., :HEAD_SIZE],
        preferred_element_type=jnp.float32,
    )
    scores = jnp.concatenate([first_scores, second_scores, third_scores], axis=-1) * scale
    mask = jnp.concatenate(
        [
            jnp.repeat(inside, BLOCK_TOKENS, axis=1),
            jnp.ones((per_device, (GLOBAL_BLOCKS + RANDOM_BLOCKS) * BLOCK_TOKENS), dtype=jnp.bool_),
        ],
        axis=1,
    )
    scores = jnp.where(mask[None, :, None, None, :], scores, -jnp.inf)
    top = jnp.max(scores, axis=-1, keepdims=True)
    weights = jnp.exp(scores - top)
    probs = (weights / jnp.sum(weights, axis=-1, keepdims=True)).astype(jnp.bfloat16)
    near_probs = probs[..., : 3 * BLOCK_TOKENS]
    global_probs = probs[..., 3 * BLOCK_TOKENS : (3 + GLOBAL_BLOCKS) * BLOCK_TOKENS]
    random_probs = probs[..., (3 + GLOBAL_BLOCKS) * BLOCK_TOKENS :]
    mixed = jnp.einsum(
        "sqgbw,sqwh->sqbgh",
        near_probs,
        window[..., HEAD_SIZE:],
        preferred_element_type=jnp.float32,
    )
    mixed = mixed + jnp.einsum(
        "sqgbw,swh->sqbgh",
        global_probs,
        global_pairs[..., HEAD_SIZE:],
        preferred_element_type=jnp.float32,
    )
    mixed = mixed + jnp.einsum(
        "sqgbw,sqgwh->sqbgh",
        random_probs,
        arrived[..., HEAD_SIZE:],
        preferred_element_type=jnp.float32,
    )
    return mixed.reshape(passages, length, heads_here * HEAD_SIZE).astype(jnp.bfloat16)


def solution(mesh):
    placed = (
        P("groups", "row", "col"),
        P(),
        P("row", "col"),
        P("col"),
        P("row", "col"),
        P("col"),
        P("row", "col"),
        P("col"),
        P("groups", None, None, None),
        P("groups", None, None),
    )
    return jax.shard_map(
        shards, mesh=mesh, in_specs=placed, out_specs=P("groups", "row", "col"), check_vma=False
    )
```

time: 310 us -> 179 us (0.58)
  blocking collectives: 69.1 us -> 0 us
  waiting for transfers between devices: 161 us -> 109 us
  between operations: 23.3 us -> 13.8 us
  starting transfers between devices: 11.3 us -> 5.05 us
  other arithmetic: 22.5 us -> 27.4 us
    all_gather x2 -> x0, blocking collectives: 69.1 us -> none  [the longest x1 36.6 us: shards(): lax.all_gather(key_weight, 'row', axis=0, tiled=True)]
    psum x1 -> x0, waiting for transfers between devices: 55.7 us -> none  [broadcast(): return lax.psum(block, axis)]
    ppermute x2 -> x3, waiting for transfers between devices: 6.16 us -> 48.2 us  [the longest x1 40 us: shards(): partner = lax.ppermute(whole, 'groups', SWAP)]
    all_gather x2, waiting for transfers between devices: 97.3 us -> 61 us  [the longest x1 35.6 us: shards(): gathered = lax.all_gather(pairs, 'row', axis=0, tiled=False)]
    sub x0 -> x1, other arithmetic: none -> 12 us  [shards(): weights = jnp.exp(scores - top)]
    all_to_all x1 -> x0, starting transfers between devices: 5.87 us -> none  [shards(): lax.all_to_all(outgoing, 'row', split_axis=0, concat_axis=0, tiled=True)]
    gather x2 -> x3, local copies, waits for them, and re-layouts: 5.44 us -> 1.98 us  [the longest x1 0.82 us: shards(): arrived = kv_blocks[passage_ids[:, None, None, None], selected]]
    dot_general x9 -> x7, matrix products: 8.79 us -> 10.6 us  [the longest x1 5.79 us: shards(): jnp.dot(normed, full_panel, preferred_element_type=jnp.float32) + panel_bias]
  transfers between devices with their start and end apart: 6 -> 5, of which waited for: 4 -> 5; matrix products, arithmetic and copies ran while one was open for 5% -> 8% of each run, Pallas kernels for 0% -> 0%
where the time goes in v1:
time: 179 us; the launch traced here: 178 us
  waiting for transfers between devices  109 us (61%)
  other arithmetic  27.4 us (15%)
  between operations  13.8 us (8%)
  local copies, waits for them, and re-layouts  12.1 us (7%)
  matrix products  10.6 us (6%)
  starting transfers between devices  5.05 us (3%)
    ppermute x1, waiting for transfers between devices, shards(): partner = lax.ppermute(whole, 'groups', SWAP)  40 us
    all_gather x1, waiting for transfers between devices, shards(): gathered = lax.all_gather(pairs, 'row', axis=0, tiled=False)  35.6 us
    all_gather x1, waiting for transfers between devices, shards(): full_panel = lax.all_gather(panel, 'row', axis=0, tiled=True)  25.4 us
    sub x1, other arithmetic, shards(): weights = jnp.exp(scores - top)  12 us
    ppermute x1, waiting for transfers between devices, shards(): returned = lax.ppermute(result[passages:], 'groups', SWAP)  5.96 us
    dot_general x1, matrix products, shards(): jnp.dot(normed, full_panel, preferred_element_type=jnp.float32) + panel_bias  5.79 us
  transfers between devices with their start and end apart: 5, of which 5 were waited for; matrix products, arithmetic and copies ran while one was open for 8% of the time, Pallas kernels for 0%

profile of v1, /device:TPU:0, one launch (start us, length us, event | category | flops | bytes accessed | tf_op | source)
XLA Modules:
  0.0 178.2 jit_solution(1244104427801628032)
XLA Ops:
  6.5 1.1 fusion.32
  7.7 1.1 slice.89
  8.8 2.1 %fusion.19 = bf16[448,576]{1,0:T(8,128)(2,1)} fusion(bf16[448,128]{1,0:T(8,128)(2,1)} %param.14, bf16[448,896]{1,0:T(8,128)(2,1)} %param.12, bf16[448,64]{1,0:T(8,128)(2,1)S(1)} %get-tuple-element.10, bf16[448,512]{1,0:T(8,128)(2,1)S(1)} %slice.89, bf16[448,64]{1,0:T(8,128)(2,1)S(1)} %get-tuple-element.9, pred[]{:T(512)S(6)} %eq.6), kind=kLoop, calls=%fused_computation.41 | loop fusion | flops 2838528 | bytes 2007041 | tf_op jit(solution)/shard_map/jit(_where)/select_n | solution.py:61
  11.0 0.5 collective-permute-start
  11.5 2.2 %collective-permute-done = bf16[2,128,1792]{2,1,0:T(8,128)(2,1)} collective-permute-done((bf16[2,128,1792]{2,1,0:T(8,128)(2,1)S(1)}, bf16[2,128,1792]{2,1,0:T(8,128)(2,1)}, u32[]{:S(2)}, u32[]{:S(2)}) %collective-permute-start) | collective-permute-done | bytes 917536 | tf_op jit(solution)/shard_map/ppermute | solution.py:73
  13.7 2.1 %maximum_select_fusion = bf16[2,128,3584]{2,1,0:T(8,128)(2,1)S(1)} fusion(bf16[2,128,1792]{2,1,0:T(8,128)(2,1)} %collective-permute-done, bf16[2,128,1792]{2,1,0:T(8,128)(2,1)S(1)} %copy-done.3, pred[]{:T(512)S(6)} %eq.7), kind=kLoop, calls=%fused_computation.14 | loop fusion | flops 8257536 | bytes 3670017 | tf_op jit(solution)/shard_map/jit(_where)/select_n | solution.py:74
  15.8 3.0 %collective-permute-start.1 = (bf16[2,128,3584]{2,1,0:T(8,128)(2,1)S(1)}, bf16[2,128,3584]{2,1,0:T(8,128)(2,1)}, u32[]{:S(2)}, u32[]{:S(2)}) collective-permute-start(bf16[2,128,3584]{2,1,0:T(8,128)(2,1)S(1)} %maximum_select_fusion), channel_id=1, source_target_pairs={{0,16},{16,0},{1,17},{17,1},{2,18},{18,2},{3,19},{19,3},{4,20},{20... | collective-permute-start | bytes 5505032 | tf_op jit(solution)/shard_map/ppermute | solution.py:79
  19.1 40.0 %collective-permute-done.1 = bf16[2,128,3584]{2,1,0:T(8,128)(2,1)} collective-permute-done((bf16[2,128,3584]{2,1,0:T(8,128)(2,1)S(1)}, bf16[2,128,3584]{2,1,0:T(8,128)(2,1)}, u32[]{:S(2)}, u32[]{:S(2)}) %collective-permute-start.1) | collective-permute-done | bytes 1835040 | tf_op jit(solution)/shard_map/ppermute | solution.py:79
  59.1 2.3 %multiply_reduce_fusion = f32[4,128]{1,0:T(4,128)S(1)} fusion(bf16[2,128,3584]{2,1,0:T(8,128)(2,1)} %collective-permute-done.1, bf16[2,128,3584]{2,1,0:T(8,128)(2,1)S(1)} %maximum_select_fusion), kind=kLoop, calls=%fused_computation.7 | loop fusion | flops 7339520 | bytes 3672064 | tf_op jit(solution)/shard_map/reduce_sum | solution.py:82
  61.5 2.0 %maximum_convert_fusion = f32[4,128,3584]{2,1,0:T(8,128)S(1)} fusion(bf16[2,128,3584]{2,1,0:T(8,128)(2,1)} %collective-permute-done.1, bf16[2,128,3584]{2,1,0:T(8,128)(2,1)S(1)} %maximum_select_fusion), kind=kLoop, calls=%fused_computation.8 | loop fusion | flops 3670016 | bytes 11010048 | tf_op jit(solution)/shard_map/convert_element_type | solution.py:81
  63.5 3.1 %fusion.2 = bf16[512,3584]{1,0:T(8,128)(2,1)} fusion(f32[4,128,3584]{2,1,0:T(8,128)S(1)} %maximum_convert_fusion, f32[3584]{0:T(1024)S(1)} %copy-done.4, f32[512]{0:T(512)S(1)} %rsqrt_bitcast_fusion), kind=kLoop, calls=%fused_computation.6 | loop fusion | flops 5505024 | bytes 11026432 | tf_op jit(solution)/shard_map/convert_element_type | solution.py:85
  66.6 25.4 %all-gather.4.cloned.1.call-done = bf16[3584,576]{1,0:T(8,128)(2,1)} async-done(((bf16[448,576]{1,0:T(8,128)(2,1)}), bf16[3584,576]{1,0:T(8,128)(2,1)}) %all-gather.4.cloned.1.call-update) | async-done | bytes 4128784 | tf_op jit(solution)/shard_map/all_gather | solution.py:71
  92.0 5.8 %convolution_add_fusion = f32[512,576]{0,1:T(8,128)S(1)} fusion(bf16[512,3584]{1,0:T(8,128)(2,1)} %fusion.2, bf16[3584,576]{1,0:T(8,128)(2,1)} %all-gather.4.cloned.1.call-done, f32[576]{0:T(1024)S(1)} %maximum_select_fusion.1), kind=kOutput, calls=%fused_computation.25 | convolution fusion | flops 2114224128 | bytes 8980736 | tf_op jit(solution)/shard_map/dot_general | solution.py:90
  98.9 0.7 fusion.13
  99.6 0.5 fusion.22
  100.1 1.5 collective-permute-start.2
  101.6 6.0 %collective-permute-done.2 = bf16[2,128,576]{1,0,2:T(2,128)(2,1)S(1)} collective-permute-done((bf16[2,128,576]{1,0,2:T(2,128)(2,1)S(1)}, bf16[2,128,576]{1,0,2:T(2,128)(2,1)S(1)}, u32[]{:S(2)}, u32[]{:S(2)}) %collective-permute-start.2) | collective-permute-done | bytes 294944 | tf_op jit(solution)/shard_map/ppermute | solution.py:101
  107.6 0.5 broadcast_select_fusion
  108.5 0.8 copy.50
  110.6 0.6 pad_maximum_fusion.2
  111.6 2.0 %copy.53 = bf16[2,2,64,7,128]{4,2,3,1,0:T(8,128)(2,1)S(1)} copy(bf16[2,2,64,7,128]{2,1,0,4,3:T(2,128)(2,1)S(1)} %reshape.189) | data formatting | bytes 917504 | tf_op jit(solution)/shard_map/reshape | solution.py:135
  113.7 35.6 %all-gather.6.cloned.1.call-done = bf16[16,128,256]{2,1,0:T(8,128)(2,1)} async-done(((bf16[2,128,256]{2,1,0:T(8,128)(2,1)}), bf16[16,128,256]{2,1,0:T(8,128)(2,1)}) %all-gather.6.cloned.1.call-update) | async-done | bytes 1048592 | tf_op jit(solution)/shard_map/all_gather | solution.py:110
  149.2 1.3 copy.51
  150.5 0.6 gather_fusion
  151.2 0.6 gather_fusion.1
  151.7 1.7 convolution_bitcast_fusion
  153.4 1.2 convolution_bitcast_fusion.2
  154.6 0.8 gather_fusion.2
  155.4 0.7 fusion.16
  156.2 12.0 %fusion.34 = (f32[2,2,7,64]{3,2,1,0:T(8,128)S(1)}, f32[2,2,7,64,448]{4,3,2,1,0:T(8,128)S(1)}) fusion(f32[2,2,7,64,128]{4,3,2,1,0:T(8,128)S(1)} %fusion.16, f32[2,2,7,64,128]{4,3,2,1,0:T(8,128)} %convolution_bitcast_fusion.2, f32[2,2,7,64,192]{4,3,2,1,0:T(8,128)} %convolution_bitcast_fusion, pred[2,448]{1,0:T(4,128)(4,1)S(1)} %concatenate.86), kind=kOutput, calls=%fused_computation.83 | output fusion | flops 4817343 | bytes 6430592 | tf_op jit(solution)/shard_map/sub | solution.py:166
  168.9 0.4 convolution_bitcast_fusion.4
  170.1 1.3 convert_element_type.42
  (69 shorter events, 4.8 us)
Async XLA Ops:
  6.5 102.9 %copy-start = (s32[2,2,2]{2,1,0:T(2,128)S(1)}, s32[2,2,2]{2,1,0:T(2,128)}, u32[]{:S(2)}) copy-start(s32[2,2,2]{2,1,0:T(2,128)} %param.19) | copy-start | bytes 100
  6.5 4.4 %copy-start.3 = (bf16[2,128,1792]{2,1,0:T(8,128)(2,1)S(1)}, bf16[2,128,1792]{2,1,0:T(8,128)(2,1)}, u32[]{:S(2)}) copy-start(bf16[2,128,1792]{2,1,0:T(8,128)(2,1)} %param.10) | copy-start | bytes 2752516
  6.5 85.5 %all-gather.4.cloned.1.call-start = ((), (), s32[]{:S(2)}) async-start(), calls=%async_computation | async-start | bytes 5160960 | tf_op jit(solution)/shard_map/all_gather | solution.py:71
  7.7 11.0 %copy-start.5 = (f32[896]{0:T(1024)S(1)}, f32[896]{0:T(1024)}, u32[]{:S(2)}) copy-start(f32[896]{0:T(1024)} %param.13) | copy-start | bytes 10756
  7.7 11.0 %copy-start.8 = (f32[128]{0:T(128)S(1)}, f32[128]{0:T(128)}, u32[]{:S(2)}) copy-start(f32[128]{0:T(128)} %param.15) | copy-start | bytes 1540
  7.7 11.1 %copy-start.7 = (f32[128]{0:T(128)S(1)}, f32[128]{0:T(128)}, u32[]{:S(2)}) copy-start(f32[128]{0:T(128)} %param.17) | copy-start | bytes 1540
  7.7 11.1 %slice-start = ((f32[896]{0:T(1024)}), f32[512]{0:T(512)S(1)}, s32[]{:S(2)}) async-start(f32[896]{0:T(1024)} %param.13), calls=%async_computation.2 | async-start | bytes 4096 | tf_op jit(solution)/shard_map/slice | solution.py:68
  10.9 138.3 %all-gather.6.cloned.1.call-start = ((), (), s32[]{:S(2)}) async-start(), calls=%async_computation.1 | async-start | bytes 1179648 | tf_op jit(solution)/shard_map/all_gather | solution.py:110
  11.0 2.7 %collective-permute-start = (bf16[2,128,1792]{2,1,0:T(8,128)(2,1)S(1)}, bf16[2,128,1792]{2,1,0:T(8,128)(2,1)}, u32[]{:S(2)}, u32[]{:S(2)}) collective-permute-start(bf16[2,128,1792]{2,1,0:T(8,128)(2,1)S(1)} %copy-done.3), channel_id=1, source_target_pairs={{0,1},{1,0},{2,3},{3,2},{4,5},{5,4},{6,7},{7,6},{8,9},{9,8},{10,11... | collective-permute-start | bytes 2752520 | tf_op jit(solution)/shard_map/ppermute | solution.py:73
  15.8 43.4 %collective-permute-start.1 = (bf16[2,128,3584]{2,1,0:T(8,128)(2,1)S(1)}, bf16[2,128,3584]{2,1,0:T(8,128)(2,1)}, u32[]{:S(2)}, u32[]{:S(2)}) collective-permute-start(bf16[2,128,3584]{2,1,0:T(8,128)(2,1)S(1)} %maximum_select_fusion), channel_id=1, source_target_pairs={{0,16},{16,0},{1,17},{17,1},{2,18},{18,2},{3,19},{19,3},{4,20},{20... | collective-permute-start | bytes 5505032 | tf_op jit(solution)/shard_map/ppermute | solution.py:79
  61.5 2.0 %copy-start.4 = (f32[3584]{0:T(1024)S(1)}, f32[3584]{0:T(1024)}, u32[]{:S(2)}) copy-start(f32[3584]{0:T(1024)} %param.11) | copy-start | bytes 43012
  98.8 10.7 %copy-start.6 = (s32[2,16,14,2]{1,3,2,0:T(2,128)S(1)}, s32[2,16,14,2]{1,3,2,0:T(2,128)}, u32[]{:S(2)}) copy-start(s32[2,16,14,2]{1,3,2,0:T(2,128)} %param.18) | copy-start | bytes 10756
  100.1 7.5 %collective-permute-start.2 = (bf16[2,128,576]{1,0,2:T(2,128)(2,1)S(1)}, bf16[2,128,576]{1,0,2:T(2,128)(2,1)S(1)}, u32[]{:S(2)}, u32[]{:S(2)}) collective-permute-start(bf16[2,128,576]{1,0,2:T(2,128)(2,1)S(1)} %fusion.22), channel_id=1, source_target_pairs={{0,16},{16,0},{1,17},{17,1},{2,18},{18,2},{3,19},{19,3},{4,20},{20... | collective-permute-start | bytes 884744 | tf_op jit(solution)/shard_map/ppermute | solution.py:101
  151.1 2.3 %copy-start.1 = (bf16[12,64,256]{2,1,0:T(8,128)(2,1)}, bf16[12,64,256]{2,1,0:T(8,128)(2,1)S(1)}, u32[]{:S(2)}) copy-start(bf16[12,64,256]{2,1,0:T(8,128)(2,1)S(1)} %gather_fusion) | copy-start | bytes 1179652
  168.2 1.1 copy-start.2
Sparse Core Ops, SparseCore 0:
  11.0 80.9 all-gather.3
  109.4 39.8 all-gather.5

commit v2 on v1

--- a/solution.py
+++ b/solution.py
@@ -71,12 +71,18 @@
     full_panel = lax.all_gather(panel, "row", axis=0, tiled=True)
 
     other_half = lax.ppermute(tokens, "col", SWAP)
+    partner_half = lax.ppermute(tokens, "groups", SWAP)
+    partner_other = lax.ppermute(partner_half, "col", SWAP)
     whole = jnp.where(
         column == 0,
         jnp.concatenate([tokens, other_half], axis=2),
         jnp.concatenate([other_half, tokens], axis=2),
     )
-    partner = lax.ppermute(whole, "groups", SWAP)
+    partner = jnp.where(
+        column == 0,
+        jnp.concatenate([partner_half, partner_other], axis=2),
+        jnp.concatenate([partner_other, partner_half], axis=2),
+    )
     both = jnp.concatenate([whole, partner], axis=0)
     widened = both.astype(jnp.float32)
     power = jnp.mean(widened * widened, axis=-1, keepdims=True)
@@ -107,11 +113,25 @@
     value_rows = jnp.concatenate([low[..., split:], high[..., split:]], axis=-1)
 
     pairs = jnp.concatenate([key, value_rows], axis=-1)
-    gathered = lax.all_gather(pairs, "row", axis=0, tiled=False)
-    gathered = gathered.transpose(1, 0, 2, 3).reshape(
-        passages, passage_blocks, BLOCK_TOKENS, pairs_here, 2 * HEAD_SIZE
-    )
-    kv_blocks = gathered[:, :, :, 0]
+    if row_count <= 8:
+        by_shift = [pairs] + [
+            lax.ppermute(pairs, "row", [(i, (i + k) % row_count) for i in range(row_count)])
+            for k in range(1, row_count)
+        ]
+        gathered = jnp.stack(by_shift)
+        owner_slot = (here - jnp.arange(row_count, dtype=jnp.int32)) % row_count
+    else:
+        gathered = lax.all_gather(pairs, "row", axis=0, tiled=False)
+        owner_slot = jnp.arange(row_count, dtype=jnp.int32)
+    gathered = gathered.reshape(
+        row_count, passages, per_device, BLOCK_TOKENS, pairs_here, 2 * HEAD_SIZE
+    )[:, :, :, :, 0]
+    gathered = gathered.transpose(1, 0, 2, 3, 4).reshape(
+        passages, passage_blocks, BLOCK_TOKENS, 2 * HEAD_SIZE
+    )
+    block_ids = jnp.arange(passage_blocks, dtype=jnp.int32)
+    slot_of_block = owner_slot[block_ids // per_device] * per_device + block_ids % per_device
+    kv_blocks = gathered[:, slot_of_block]
 
     local_blocks = here * per_device + jnp.arange(per_device, dtype=jnp.int32)
     nearby_blocks = local_blocks[:, None] + jnp.arange(3, dtype=jnp.int32)[None, :] - 1
@@ -153,21 +173,29 @@
         arrived[..., :HEAD_SIZE],
         preferred_element_type=jnp.float32,
     )
-    scores = jnp.concatenate([first_scores, second_scores, third_scores], axis=-1) * scale
-    mask = jnp.concatenate(
-        [
-            jnp.repeat(inside, BLOCK_TOKENS, axis=1),
-            jnp.ones((per_device, (GLOBAL_BLOCKS + RANDOM_BLOCKS) * BLOCK_TOKENS), dtype=jnp.bool_),
-        ],
-        axis=1,
-    )
-    scores = jnp.where(mask[None, :, None, None, :], scores, -jnp.inf)
-    top = jnp.max(scores, axis=-1, keepdims=True)
-    weights = jnp.exp(scores - top)
-    probs = (weights / jnp.sum(weights, axis=-1, keepdims=True)).astype(jnp.bfloat16)
-    near_probs = probs[..., : 3 * BLOCK_TOKENS]
-    global_probs = probs[..., 3 * BLOCK_TOKENS : (3 + GLOBAL_BLOCKS) * BLOCK_TOKENS]
-    random_probs = probs[..., (3 + GLOBAL_BLOCKS) * BLOCK_TOKENS :]
+    first_scores = first_scores * scale
+    second_scores = second_scores * scale
+    third_scores = third_scores * scale
+    near_mask = jnp.repeat(inside, BLOCK_TOKENS, axis=1)
+    first_scores = jnp.where(near_mask[None, :, None, None, :], first_scores, -jnp.inf)
+    top = jnp.maximum(
+        jnp.max(first_scores, axis=-1, keepdims=True),
+        jnp.maximum(
+            jnp.max(second_scores, axis=-1, keepdims=True),
+            jnp.max(third_scores, axis=-1, keepdims=True),
+        ),
+    )
+    near_weights = jnp.exp(first_scores - top)
+    global_weights = jnp.exp(second_scores - top)
+    random_weights = jnp.exp(third_scores - top)
+    total = (
+        jnp.sum(near_weights, axis=-1, keepdims=True)
+        + jnp.sum(global_weights, axis=-1, keepdims=True)
+        + jnp.sum(random_weights, axis=-1, keepdims=True)
+    )
+    near_probs = (near_weights / total).astype(jnp.bfloat16)
+    global_probs = (global_weights / total).astype(jnp.bfloat16)
+    random_probs = (random_weights / total).astype(jnp.bfloat16)
     mixed = jnp.einsum(
         "sqgbw,sqwh->sqbgh",
         near_probs,

time: 179 us -> 152 us (0.85); the launches traced: 178 us -> 149 us
  waiting for transfers between devices: 109 us -> 82.5 us
  other arithmetic: 27.4 us -> 12.3 us
  starting transfers between devices: 5.05 us -> 16.8 us
    all_gather x1 -> x0, waiting for transfers between devices: 35.6 us -> none  [shards(): gathered = lax.all_gather(pairs, 'row', axis=0, tiled=False)]
    all_gather x1, waiting for transfers between devices: 25.4 us -> 50.2 us  [shards(): full_panel = lax.all_gather(panel, 'row', axis=0, tiled=True)]
    ppermute x1 -> x9, waiting for transfers between devices: 40 us -> 26.3 us  [the longest x1 18.5 us: shards(): partner_half = lax.ppermute(tokens, 'groups', SWAP)]
    ppermute x1 -> x9, starting transfers between devices: 2.95 us -> 15.2 us  [the longest x7 12.2 us: shards(): lax.ppermute(pairs, 'row', [(i, (i + k) % row_count) for i in range(row_c...]
    sub x1 -> x0, other arithmetic: 12 us -> none  [shards(): weights = jnp.exp(scores - top)]
    ppermute x1, waiting for transfers between devices: 2.23 us -> 0.01 us  [shards(): other_half = lax.ppermute(tokens, 'col', SWAP)]
  transfers between devices with their start and end apart: 5 -> 12, of which waited for: 5 -> 7; matrix products, arithmetic and copies ran while one was open for 8% -> 7% of each run, Pallas kernels for 0% -> 0%
where the time goes in v2:
time: 152 us; the launch traced here: 149 us
  waiting for transfers between devices  82.5 us (54%)
  starting transfers between devices  16.8 us (11%)
  between operations  14.1 us (9%)
  local copies, waits for them, and re-layouts  13.3 us (9%)
  other arithmetic  12.3 us (8%)
  matrix products  10.2 us (7%)
    all_gather x1, waiting for transfers between devices, shards(): full_panel = lax.all_gather(panel, 'row', axis=0, tiled=True)  50.2 us
    ppermute x1, waiting for transfers between devices, shards(): partner_half = lax.ppermute(tokens, 'groups', SWAP)  18.5 us
    ppermute x7, starting transfers between devices, shards(): lax.ppermute(pairs, 'row', [(i, (i + k) % row_count) for i in range(row_c...  12.2 us
    ppermute x7, waiting for transfers between devices, shards(): lax.ppermute(pairs, 'row', [(i, (i + k) % row_count) for i in range(row_c...  6.05 us
    ppermute x1, waiting for transfers between devices, shards(): returned = lax.ppermute(result[passages:], 'groups', SWAP)  5.94 us
    dot_general x1, matrix products, shards(): jnp.dot(normed, full_panel, preferred_element_type=jnp.float32) + panel_bias  5.79 us
    convert_element_type x1, other arithmetic, shards(): normed = (widened * lax.rsqrt(power + norm_eps) * gain).astype(jnp.bfloat...  3.13 us
  transfers between devices with their start and end apart: 12, of which 7 were waited for; matrix products, arithmetic and copies ran while one was open for 7% of the time, Pallas kernels for 0%

profile of v2, /device:TPU:0, one launch (start us, length us, event | category | flops | bytes accessed | tf_op | source)
XLA Modules:
  0.0 149.1 jit_solution(4504620474483957747)
XLA Ops:
  6.5 1.1 fusion.39
  7.7 1.1 slice.80
  8.9 2.0 %fusion.19 = bf16[448,576]{1,0:T(8,128)(2,1)} fusion(bf16[448,128]{1,0:T(8,128)(2,1)} %param.14, bf16[448,896]{1,0:T(8,128)(2,1)S(1)} %copy-done.1, bf16[448,64]{1,0:T(8,128)(2,1)S(1)} %get-tuple-element.12, bf16[448,512]{1,0:T(8,128)(2,1)S(1)} %slice.80, bf16[448,64]{1,0:T(8,128)(2,1)S(1)} %get-tuple-element.11, pred[]{:T(512)S(6)} %eq.11), kind=kLoop, calls=%fused_computation.50 | loop fusion | flops 2838528 | bytes 2007041 | tf_op jit(solution)/shard_map/jit(_where)/select_n | solution.py:61
  10.9 3.0 %collective-permute-start.1 = (bf16[2,128,1792]{2,1,0:T(8,128)(2,1)S(1)}, bf16[2,128,1792]{2,1,0:T(8,128)(2,1)S(1)}, u32[]{:S(2)}, u32[]{:S(2)}) collective-permute-start(bf16[2,128,1792]{2,1,0:T(8,128)(2,1)S(1)} %copy-done.2), channel_id=1, source_target_pairs={{0,16},{16,0},{1,17},{17,1},{2,18},{18,2},{3,19},{19,3},{4,20},{20... | collective-permute-start | bytes 2752520 | tf_op jit(solution)/shard_map/ppermute | solution.py:74
  15.0 0.7 gather_fusion
  15.7 18.5 %collective-permute-done.1 = bf16[2,128,1792]{2,1,0:T(8,128)(2,1)S(1)} collective-permute-done((bf16[2,128,1792]{2,1,0:T(8,128)(2,1)S(1)}, bf16[2,128,1792]{2,1,0:T(8,128)(2,1)S(1)}, u32[]{:S(2)}, u32[]{:S(2)}) %collective-permute-start.1) | collective-permute-done | bytes 917536 | tf_op jit(solution)/shard_map/ppermute | solution.py:74
  35.0 1.8 %collective-permute-done.2 = bf16[2,128,1792]{2,1,0:T(8,128)(2,1)S(1)} collective-permute-done((bf16[2,128,1792]{2,1,0:T(8,128)(2,1)S(1)}, bf16[2,128,1792]{2,1,0:T(8,128)(2,1)S(1)}, u32[]{:S(2)}, u32[]{:S(2)}) %collective-permute-start.2) | collective-permute-done | bytes 917536 | tf_op jit(solution)/shard_map/ppermute | solution.py:75
  37.2 0.8 multiply_reduce_fusion
  38.7 3.1 %fusion.1 = bf16[512,3584]{1,0:T(8,128)(2,1)} fusion(f32[4,128,3584]{2,1,0:T(8,128)S(1)} %maximum_convert_fusion, f32[3584]{0:T(1024)S(1)} %copy-done.4, f32[512]{0:T(512)S(1)} %rsqrt_bitcast_fusion), kind=kLoop, calls=%fused_computation.7 | loop fusion | flops 5505024 | bytes 11026432 | tf_op jit(solution)/shard_map/convert_element_type | solution.py:91
  41.8 50.2 %all-gather.2.cloned.1.call-done = bf16[3584,576]{1,0:T(8,128)(2,1)} async-done(((bf16[448,576]{1,0:T(8,128)(2,1)}), bf16[3584,576]{1,0:T(8,128)(2,1)}) %all-gather.2.cloned.1.call-update) | async-done | bytes 4128784 | tf_op jit(solution)/shard_map/all_gather | solution.py:71
  92.0 5.8 %convolution_add_fusion = f32[512,576]{0,1:T(8,128)S(1)} fusion(bf16[512,3584]{1,0:T(8,128)(2,1)} %fusion.1, bf16[3584,576]{1,0:T(8,128)(2,1)} %all-gather.2.cloned.1.call-done, f32[576]{0:T(1024)S(1)} %maximum_select_fusion.2), kind=kOutput, calls=%fused_computation.26 | convolution fusion | flops 2114224128 | bytes 8980736 | tf_op jit(solution)/shard_map/dot_general | solution.py:96
  100.0 1.5 %collective-permute-start.3 = (bf16[2,128,576]{1,0,2:T(2,128)(2,1)S(1)}, bf16[2,128,576]{1,0,2:T(2,128)(2,1)S(1)}, u32[]{:S(2)}, u32[]{:S(2)}) collective-permute-start(bf16[2,128,576]{1,0,2:T(2,128)(2,1)S(1)} %fusion.24), channel_id=1, source_target_pairs={{0,16},{16,0},{1,17},{17,1},{2,18},{18,2},{3,19},{19,3},{4,20},{20... | collective-permute-start | bytes 884744 | tf_op jit(solution)/shard_map/ppermute | solution.py:107
  101.6 5.9 %collective-permute-done.3 = bf16[2,128,576]{1,0,2:T(2,128)(2,1)S(1)} collective-permute-done((bf16[2,128,576]{1,0,2:T(2,128)(2,1)S(1)}, bf16[2,128,576]{1,0,2:T(2,128)(2,1)S(1)}, u32[]{:S(2)}, u32[]{:S(2)}) %collective-permute-start.3) | collective-permute-done | bytes 294944 | tf_op jit(solution)/shard_map/ppermute | solution.py:107
  109.4 0.9 collective-permute-start.5
  110.2 3.5 %collective-permute-start.6 = (bf16[2,128,256]{1,0,2:T(2,128)(2,1)S(1)}, bf16[2,128,256]{1,0,2:T(2,128)(2,1)S(1)}, u32[]{:S(2)}, u32[]{:S(2)}) collective-permute-start(bf16[2,128,256]{1,0,2:T(2,128)(2,1)S(1)} %pad_maximum_fusion.4), channel_id=1, source_target_pairs={{0,6},{2,8},{4,10},{6,12},{8,14},{10,0},{12,2},{14,4},{1,7},{3,9},... | collective-permute-start | bytes 393224 | tf_op jit(solution)/shard_map/ppermute | solution.py:118
  113.8 1.2 collective-permute-start.7
  115.0 1.7 %collective-permute-start.8 = (bf16[2,128,256]{1,0,2:T(2,128)(2,1)S(1)}, bf16[2,128,256]{1,0,2:T(2,128)(2,1)S(1)}, u32[]{:S(2)}, u32[]{:S(2)}) collective-permute-start(bf16[2,128,256]{1,0,2:T(2,128)(2,1)S(1)} %pad_maximum_fusion.4), channel_id=1, source_target_pairs={{0,10},{2,12},{4,14},{6,0},{8,2},{10,4},{12,6},{14,8},{1,11},{3,13... | collective-permute-start | bytes 393224 | tf_op jit(solution)/shard_map/ppermute | solution.py:118
  117.8 1.8 %copy.50 = bf16[2,2,64,7,128]{4,2,3,1,0:T(8,128)(2,1)S(1)} copy(bf16[2,2,64,7,128]{2,1,0,4,3:T(2,128)(2,1)S(1)} %reshape.318) | data formatting | bytes 917504 | tf_op jit(solution)/shard_map/reshape | solution.py:155
  119.7 1.9 %collective-permute-start.9 = (bf16[2,128,256]{1,0,2:T(2,128)(2,1)S(1)}, bf16[2,128,256]{1,0,2:T(2,128)(2,1)S(1)}, u32[]{:S(2)}, u32[]{:S(2)}) collective-permute-start(bf16[2,128,256]{1,0,2:T(2,128)(2,1)S(1)} %pad_maximum_fusion.4), channel_id=1, source_target_pairs={{0,12},{2,14},{4,0},{6,2},{8,4},{10,6},{12,8},{14,10},{1,13},{3,15... | collective-permute-start | bytes 393224 | tf_op jit(solution)/shard_map/ppermute | solution.py:118
  121.7 2.4 %collective-permute-start.10 = (bf16[2,128,256]{1,0,2:T(2,128)(2,1)S(1)}, bf16[2,128,256]{1,0,2:T(2,128)(2,1)S(1)}, u32[]{:S(2)}, u32[]{:S(2)}) collective-permute-start(bf16[2,128,256]{1,0,2:T(2,128)(2,1)S(1)} %pad_maximum_fusion.4), channel_id=1, source_target_pairs={{0,14},{2,0},{4,2},{6,4},{8,6},{10,8},{12,10},{14,12},{1,15},{3,1}... | collective-permute-start | bytes 393224 | tf_op jit(solution)/shard_map/ppermute | solution.py:118
  124.2 1.7 %collective-permute-done.6 = bf16[2,128,256]{1,0,2:T(2,128)(2,1)S(1)} collective-permute-done((bf16[2,128,256]{1,0,2:T(2,128)(2,1)S(1)}, bf16[2,128,256]{1,0,2:T(2,128)(2,1)S(1)}, u32[]{:S(2)}, u32[]{:S(2)}) %collective-permute-start.6) | collective-permute-done | bytes 131104 | tf_op jit(solution)/shard_map/ppermute | solution.py:118
  126.1 1.5 collective-permute-done.7
  127.9 2.9 %collective-permute-done.9 = bf16[2,128,256]{1,0,2:T(2,128)(2,1)S(1)} collective-permute-done((bf16[2,128,256]{1,0,2:T(2,128)(2,1)S(1)}, bf16[2,128,256]{1,0,2:T(2,128)(2,1)S(1)}, u32[]{:S(2)}, u32[]{:S(2)}) %collective-permute-start.9) | collective-permute-done | bytes 131104 | tf_op jit(solution)/shard_map/ppermute | solution.py:118
  131.7 1.4 gather_fusion.2
  133.7 0.8 gather_fusion.4
  135.0 0.8 fusion.42
  136.3 0.7 fusion.3
  137.1 0.9 fusion.16
  138.0 0.9 convolution_bitcast_fusion
  138.9 0.9 convolution_bitcast_fusion.2
  139.8 0.9 fusion.7
  141.0 1.3 convert_element_type.50
  (106 shorter events, 11.5 us)
Async XLA Ops:
  6.5 7.4 %copy-start = (s32[2,2,2]{2,1,0:T(2,128)S(1)}, s32[2,2,2]{2,1,0:T(2,128)}, u32[]{:S(2)}) copy-start(s32[2,2,2]{2,1,0:T(2,128)} %param.19) | copy-start | bytes 100
  6.5 2.3 %copy-start.1 = (bf16[448,896]{1,0:T(8,128)(2,1)S(1)}, bf16[448,896]{1,0:T(8,128)(2,1)}, u32[]{:S(2)}) copy-start(bf16[448,896]{1,0:T(8,128)(2,1)} %param.12) | copy-start | bytes 2408452
  6.5 85.5 %all-gather.2.cloned.1.call-start = ((), (), s32[]{:S(2)}) async-start(), calls=%async_computation | async-start | bytes 5160960 | tf_op jit(solution)/shard_map/all_gather | solution.py:71
  7.7 3.2 %copy-start.2 = (bf16[2,128,1792]{2,1,0:T(8,128)(2,1)S(1)}, bf16[2,128,1792]{2,1,0:T(8,128)(2,1)}, u32[]{:S(2)}) copy-start(bf16[2,128,1792]{2,1,0:T(8,128)(2,1)} %param.10) | copy-start | bytes 2752516
  7.7 6.3 %copy-start.6 = (s32[2,16,14,2]{1,3,2,0:T(2,128)S(1)}, s32[2,16,14,2]{1,3,2,0:T(2,128)}, u32[]{:S(2)}) copy-start(s32[2,16,14,2]{1,3,2,0:T(2,128)} %param.18) | copy-start | bytes 10756
  7.7 6.7 %copy-start.5 = (f32[896]{0:T(1024)S(1)}, f32[896]{0:T(1024)}, u32[]{:S(2)}) copy-start(f32[896]{0:T(1024)} %param.13) | copy-start | bytes 10756
  7.7 6.7 %copy-start.8 = (f32[128]{0:T(128)S(1)}, f32[128]{0:T(128)}, u32[]{:S(2)}) copy-start(f32[128]{0:T(128)} %param.15) | copy-start | bytes 1540
  8.8 6.8 %copy-start.7 = (f32[128]{0:T(128)S(1)}, f32[128]{0:T(128)}, u32[]{:S(2)}) copy-start(f32[128]{0:T(128)} %param.17) | copy-start | bytes 1540
  8.9 6.9 %slice-start = ((f32[896]{0:T(1024)}), f32[512]{0:T(512)S(1)}, s32[]{:S(2)}) async-start(f32[896]{0:T(1024)} %param.13), calls=%async_computation.1 | async-start | bytes 4096 | tf_op jit(solution)/shard_map/slice | solution.py:68
  10.9 23.4 %collective-permute-start.1 = (bf16[2,128,1792]{2,1,0:T(8,128)(2,1)S(1)}, bf16[2,128,1792]{2,1,0:T(8,128)(2,1)S(1)}, u32[]{:S(2)}, u32[]{:S(2)}) collective-permute-start(bf16[2,128,1792]{2,1,0:T(8,128)(2,1)S(1)} %copy-done.2), channel_id=1, source_target_pairs={{0,16},{16,0},{1,17},{17,1},{2,18},{18,2},{3,19},{19,3},{4,20},{20... | collective-permute-start | bytes 2752520 | tf_op jit(solution)/shard_map/ppermute | solution.py:74
  13.9 20.6 %collective-permute-start = (bf16[2,128,1792]{2,1,0:T(8,128)(2,1)S(1)}, bf16[2,128,1792]{2,1,0:T(8,128)(2,1)S(1)}, u32[]{:S(2)}, u32[]{:S(2)}) collective-permute-start(bf16[2,128,1792]{2,1,0:T(8,128)(2,1)S(1)} %copy-done.2), channel_id=1, source_target_pairs={{0,1},{1,0},{2,3},{3,2},{4,5},{5,4},{6,7},{7,6},{8,9},{9,8},{10,11... | collective-permute-start | bytes 2752520 | tf_op jit(solution)/shard_map/ppermute | solution.py:73
  34.3 2.5 %collective-permute-start.2 = (bf16[2,128,1792]{2,1,0:T(8,128)(2,1)S(1)}, bf16[2,128,1792]{2,1,0:T(8,128)(2,1)S(1)}, u32[]{:S(2)}, u32[]{:S(2)}) collective-permute-start(bf16[2,128,1792]{2,1,0:T(8,128)(2,1)S(1)} %collective-permute-done.1), channel_id=1, source_target_pairs={{0,1},{1,0},{2,3},{3,2},{4,5},{5,4},{6,7},{7,6},{8,9},{9,8},{10,11... | collective-permute-start | bytes 2752520 | tf_op jit(solution)/shard_map/ppermute | solution.py:75
  38.0 0.7 copy-start.4
  100.0 7.5 %collective-permute-start.3 = (bf16[2,128,576]{1,0,2:T(2,128)(2,1)S(1)}, bf16[2,128,576]{1,0,2:T(2,128)(2,1)S(1)}, u32[]{:S(2)}, u32[]{:S(2)}) collective-permute-start(bf16[2,128,576]{1,0,2:T(2,128)(2,1)S(1)} %fusion.24), channel_id=1, source_target_pairs={{0,16},{16,0},{1,17},{17,1},{2,18},{18,2},{3,19},{19,3},{4,20},{20... | collective-permute-start | bytes 884744 | tf_op jit(solution)/shard_map/ppermute | solution.py:107
  108.8 10.9 %collective-permute-start.4 = (bf16[2,128,256]{1,0,2:T(2,128)(2,1)S(1)}, bf16[2,128,256]{1,0,2:T(2,128)(2,1)S(1)}, u32[]{:S(2)}, u32[]{:S(2)}) collective-permute-start(bf16[2,128,256]{1,0,2:T(2,128)(2,1)S(1)} %pad_maximum_fusion.4), channel_id=1, source_target_pairs={{0,2},{2,4},{4,6},{6,8},{8,10},{10,12},{12,14},{14,0},{1,3},{3,5},... | collective-permute-start | bytes 393224 | tf_op jit(solution)/shard_map/ppermute | solution.py:118
  109.4 12.3 %collective-permute-start.5 = (bf16[2,128,256]{1,0,2:T(2,128)(2,1)S(1)}, bf16[2,128,256]{1,0,2:T(2,128)(2,1)S(1)}, u32[]{:S(2)}, u32[]{:S(2)}) collective-permute-start(bf16[2,128,256]{1,0,2:T(2,128)(2,1)S(1)} %pad_maximum_fusion.4), channel_id=1, source_target_pairs={{0,4},{2,6},{4,8},{6,10},{8,12},{10,14},{12,0},{14,2},{1,5},{3,7},... | collective-permute-start | bytes 393224 | tf_op jit(solution)/shard_map/ppermute | solution.py:118
  110.2 15.7 %collective-permute-start.6 = (bf16[2,128,256]{1,0,2:T(2,128)(2,1)S(1)}, bf16[2,128,256]{1,0,2:T(2,128)(2,1)S(1)}, u32[]{:S(2)}, u32[]{:S(2)}) collective-permute-start(bf16[2,128,256]{1,0,2:T(2,128)(2,1)S(1)} %pad_maximum_fusion.4), channel_id=1, source_target_pairs={{0,6},{2,8},{4,10},{6,12},{8,14},{10,0},{12,2},{14,4},{1,7},{3,9},... | collective-permute-start | bytes 393224 | tf_op jit(solution)/shard_map/ppermute | solution.py:118
  113.8 13.8 %collective-permute-start.7 = (bf16[2,128,256]{1,0,2:T(2,128)(2,1)S(1)}, bf16[2,128,256]{1,0,2:T(2,128)(2,1)S(1)}, u32[]{:S(2)}, u32[]{:S(2)}) collective-permute-start(bf16[2,128,256]{1,0,2:T(2,128)(2,1)S(1)} %pad_maximum_fusion.4), channel_id=1, source_target_pairs={{0,8},{2,10},{4,12},{6,14},{8,0},{10,2},{12,4},{14,6},{1,9},{3,11}... | collective-permute-start | bytes 393224 | tf_op jit(solution)/shard_map/ppermute | solution.py:118
  115.0 12.7 %collective-permute-start.8 = (bf16[2,128,256]{1,0,2:T(2,128)(2,1)S(1)}, bf16[2,128,256]{1,0,2:T(2,128)(2,1)S(1)}, u32[]{:S(2)}, u32[]{:S(2)}) collective-permute-start(bf16[2,128,256]{1,0,2:T(2,128)(2,1)S(1)} %pad_maximum_fusion.4), channel_id=1, source_target_pairs={{0,10},{2,12},{4,14},{6,0},{8,2},{10,4},{12,6},{14,8},{1,11},{3,13... | collective-permute-start | bytes 393224 | tf_op jit(solution)/shard_map/ppermute | solution.py:118
  119.7 11.1 %collective-permute-start.9 = (bf16[2,128,256]{1,0,2:T(2,128)(2,1)S(1)}, bf16[2,128,256]{1,0,2:T(2,128)(2,1)S(1)}, u32[]{:S(2)}, u32[]{:S(2)}) collective-permute-start(bf16[2,128,256]{1,0,2:T(2,128)(2,1)S(1)} %pad_maximum_fusion.4), channel_id=1, source_target_pairs={{0,12},{2,14},{4,0},{6,2},{8,4},{10,6},{12,8},{14,10},{1,13},{3,15... | collective-permute-start | bytes 393224 | tf_op jit(solution)/shard_map/ppermute | solution.py:118
  121.7 9.2 %collective-permute-start.10 = (bf16[2,128,256]{1,0,2:T(2,128)(2,1)S(1)}, bf16[2,128,256]{1,0,2:T(2,128)(2,1)S(1)}, u32[]{:S(2)}, u32[]{:S(2)}) collective-permute-start(bf16[2,128,256]{1,0,2:T(2,128)(2,1)S(1)} %pad_maximum_fusion.4), channel_id=1, source_target_pairs={{0,14},{2,0},{4,2},{6,4},{8,6},{10,8},{12,10},{14,12},{1,15},{3,1}... | collective-permute-start | bytes 393224 | tf_op jit(solution)/shard_map/ppermute | solution.py:118
  134.5 1.3 copy-start.3
Sparse Core Ops, SparseCore 0:
  11.0 80.9 all-gather.1

commit v3 on v2

--- a/solution.py
+++ b/solution.py
@@ -25,6 +25,37 @@
     sine = jnp.concatenate([jnp.sin(angles), jnp.sin(angles)], axis=-1)[None, :, None, :]
     turned = jnp.concatenate([-values[..., half:], values[..., :half]], axis=-1)
     return values * cosine + turned * sine
+
+
+def snake_order(count):
+    return [2 * z for z in range(count // 2)] + [2 * z + 1 for z in reversed(range(count // 2))]
+
+
+def gather_rows(shard, count, here):
+    if count != 8:
+        return lax.all_gather(shard, "row", axis=0, tiled=True)
+    order = snake_order(count)
+    position = [0] * count
+    for i, d in enumerate(order):
+        position[d] = i
+    forward = [(order[i], order[(i + 1) % count]) for i in range(count)]
+    backward = [(order[i], order[(i - 1) % count]) for i in range(count)]
+    half = shard.shape[0] // 2
+    ahead, behind = shard[:half], shard[half:]
+    ahead_parts, behind_parts = [ahead], [behind]
+    for _ in range(count - 1):
+        ahead = lax.ppermute(ahead, "row", forward)
+        behind = lax.ppermute(behind, "row", backward)
+        ahead_parts.append(ahead)
+        behind_parts.append(behind)
+    table = jnp.array(position, dtype=jnp.int32)
+    mine = table[here]
+    ahead_pick = (mine - table) % count
+    behind_pick = (table - mine) % count
+    joined = jnp.concatenate(
+        [jnp.stack(ahead_parts)[ahead_pick], jnp.stack(behind_parts)[behind_pick]], axis=1
+    )
+    return joined.reshape(count * shard.shape[0], shard.shape[1])
 
 
 def shards(
@@ -68,7 +99,7 @@
         jnp.concatenate([rotary_b[:split], value_bias[:value_split]]),
         jnp.concatenate([rotary_b[split:], value_bias[value_split:]]),
     )
-    full_panel = lax.all_gather(panel, "row", axis=0, tiled=True)
+    full_panel = gather_rows(panel, row_count, here)
 
     other_half = lax.ppermute(tokens, "col", SWAP)
     partner_half = lax.ppermute(tokens, "groups", SWAP)

time: 152 us -> 123 us (0.81)
  waiting for transfers between devices: 82.5 us -> 34.1 us
  local copies, waits for them, and re-layouts: 13.3 us -> 32.7 us
  starting transfers between devices: 16.8 us -> 30.3 us
  between operations: 14.1 us -> 0.77 us
  other arithmetic: 12.3 us -> 16.1 us
  matrix products: 10.2 us -> 6.82 us
    all_gather x1 -> x0, waiting for transfers between devices: 50.2 us -> none  [shards(): full_panel = lax.all_gather(panel, 'row', axis=0, tiled=True)]
    ppermute x0 -> x14, waiting for transfers between devices: none -> 23.9 us  [the longest x7 23.9 us: gather_rows(): ahead = lax.ppermute(ahead, 'row', forward)]
    ppermute x1, waiting for transfers between devices: 18.5 us -> 0.01 us  [shards(): partner_half = lax.ppermute(tokens, 'groups', SWAP)]
    ppermute x0 -> x14, starting transfers between devices: none -> 14.2 us  [the longest x7 11.1 us: gather_rows(): ahead = lax.ppermute(ahead, 'row', forward)]
    unnamed x26 -> x41, local copies, waits for them, and re-layouts: 0.37 us -> 9.93 us
    gather x0 -> x2, local copies, waits for them, and re-layouts: none -> 7.79 us  [the longest x1 3.9 us: gather_rows(): jnp.stack(behind_parts)[behind_pick]]
    dot_general x1, matrix products: 5.79 us -> 2.38 us  [shards(): jnp.dot(normed, full_panel, preferred_element_type=jnp.float32) + panel_bias]
    concatenate x0 -> x1, other arithmetic: none -> 2.75 us  [gather_rows(): jnp.concatenate([jnp.stack(ahead_parts)[ahead_pick], jnp.stack(behind_par...]
  transfers between devices with their start and end apart: 12 -> 25, of which waited for: 7 -> 11; matrix products, arithmetic and copies ran while one was open for 7% -> 29% of each run, Pallas kernels for 0% -> 0%
where the time goes in v3:
time: 123 us; the launch traced here: 121 us
  waiting for transfers between devices  34.1 us (28%)
  local copies, waits for them, and re-layouts  32.7 us (27%)
  starting transfers between devices  30.3 us (25%)
  other arithmetic  16.1 us (13%)
  matrix products  6.82 us (6%)
    ppermute x7, waiting for transfers between devices, gather_rows(): ahead = lax.ppermute(ahead, 'row', forward)  23.9 us
    ppermute x7, starting transfers between devices, shards(): lax.ppermute(pairs, 'row', [(i, (i + k) % row_count) for i in range(row_c...  12.6 us
    ppermute x7, starting transfers between devices, gather_rows(): ahead = lax.ppermute(ahead, 'row', forward)  11.1 us
    unnamed x41, local copies, waits for them, and re-layouts  9.93 us
    ppermute x1, waiting for transfers between devices, shards(): returned = lax.ppermute(result[passages:], 'groups', SWAP)  6.37 us
    gather x1, local copies, waits for them, and re-layouts, gather_rows(): jnp.stack(behind_parts)[behind_pick]  3.9 us
    gather x1, local copies, waits for them, and re-layouts, gather_rows(): jnp.stack(ahead_parts)[ahead_pick]  3.88 us
    ppermute x7, waiting for transfers between devices, shards(): lax.ppermute(pairs, 'row', [(i, (i + k) % row_count) for i in range(row_c...  3.75 us
  transfers between devices with their start and end apart: 25, of which 11 were waited for; matrix products, arithmetic and copies ran while one was open for 29% of the time, Pallas kernels for 0%

profile of v3, /device:TPU:0, one launch (start us, length us, event | category | flops | bytes accessed | tf_op | source)
XLA Modules:
  0.0 120.7 jit_solution(11803320730039611269)
XLA Ops:
  0.0 3.0 %collective-permute-start.1 = (bf16[2,128,1792]{2,1,0:T(8,128)(2,1)}, bf16[2,128,1792]{2,1,0:T(8,128)(2,1)S(1)}, u32[]{:S(2)}, u32[]{:S(2)}) collective-permute-start(bf16[2,128,1792]{2,1,0:T(8,128)(2,1)} %param.11), channel_id=1, source_target_pairs={{0,16},{16,0},{1,17},{17,1},{2,18},{18,2},{3,19},{19,3},{4,20},{20... | collective-permute-start | bytes 2752520 | tf_op jit(solution)/shard_map/ppermute | solution.py:105
  6.5 1.6 %collective-permute-start.3 = (bf16[224,576]{1,0:T(8,128)(2,1)S(1)}, bf16[224,576]{1,0:T(8,128)(2,1)S(1)}, u32[]{:S(2)}, u32[]{:S(2)}) collective-permute-start(bf16[224,576]{1,0:T(8,128)(2,1)S(1)} %get-tuple-element.11), channel_id=1, source_target_pairs={{0,4},{4,8},{8,12},{12,14},{14,10},{10,6},{6,2},{2,0},{1,5},{5,9},... | collective-permute-start | bytes 774152 | tf_op jit(solution)/shard_map/ppermute | solution.py:47
  13.4 2.3 %collective-permute-done.3 = bf16[224,576]{1,0:T(8,128)(2,1)S(1)} collective-permute-done((bf16[224,576]{1,0:T(8,128)(2,1)S(1)}, bf16[224,576]{1,0:T(8,128)(2,1)S(1)}, u32[]{:S(2)}, u32[]{:S(2)}) %collective-permute-start.3) | collective-permute-done | bytes 258080 | tf_op jit(solution)/shard_map/ppermute | solution.py:47
  15.8 1.6 %collective-permute-start.4 = (bf16[224,576]{1,0:T(8,128)(2,1)S(1)}, bf16[224,576]{1,0:T(8,128)(2,1)S(1)}, u32[]{:S(2)}, u32[]{:S(2)}) collective-permute-start(bf16[224,576]{1,0:T(8,128)(2,1)S(1)} %collective-permute-done.3), channel_id=1, source_target_pairs={{0,4},{4,8},{8,12},{12,14},{14,10},{10,6},{6,2},{2,0},{1,5},{5,9},... | collective-permute-start | bytes 774152 | tf_op jit(solution)/shard_map/ppermute | solution.py:47
  19.3 4.9 %collective-permute-done.4 = bf16[224,576]{1,0:T(8,128)(2,1)S(1)} collective-permute-done((bf16[224,576]{1,0:T(8,128)(2,1)S(1)}, bf16[224,576]{1,0:T(8,128)(2,1)S(1)}, u32[]{:S(2)}, u32[]{:S(2)}) %collective-permute-start.4) | collective-permute-done | bytes 258080 | tf_op jit(solution)/shard_map/ppermute | solution.py:47
  24.2 1.6 %collective-permute-start.5 = (bf16[224,576]{1,0:T(8,128)(2,1)S(1)}, bf16[224,576]{1,0:T(8,128)(2,1)S(1)}, u32[]{:S(2)}, u32[]{:S(2)}) collective-permute-start(bf16[224,576]{1,0:T(8,128)(2,1)S(1)} %collective-permute-done.4), channel_id=1, source_target_pairs={{0,4},{4,8},{8,12},{12,14},{14,10},{10,6},{6,2},{2,0},{1,5},{5,9},... | collective-permute-start | bytes 774152 | tf_op jit(solution)/shard_map/ppermute | solution.py:47
  27.7 4.1 %collective-permute-done.5 = bf16[224,576]{1,0:T(8,128)(2,1)S(1)} collective-permute-done((bf16[224,576]{1,0:T(8,128)(2,1)S(1)}, bf16[224,576]{1,0:T(8,128)(2,1)S(1)}, u32[]{:S(2)}, u32[]{:S(2)}) %collective-permute-start.5) | collective-permute-done | bytes 258080 | tf_op jit(solution)/shard_map/ppermute | solution.py:47
  31.8 1.6 %collective-permute-start.6 = (bf16[224,576]{1,0:T(8,128)(2,1)S(1)}, bf16[224,576]{1,0:T(8,128)(2,1)S(1)}, u32[]{:S(2)}, u32[]{:S(2)}) collective-permute-start(bf16[224,576]{1,0:T(8,128)(2,1)S(1)} %collective-permute-done.5), channel_id=1, source_target_pairs={{0,4},{4,8},{8,12},{12,14},{14,10},{10,6},{6,2},{2,0},{1,5},{5,9},... | collective-permute-start | bytes 774152 | tf_op jit(solution)/shard_map/ppermute | solution.py:47
  35.3 2.0 %maximum_select_fusion = bf16[2,128,3584]{2,1,0:T(8,128)(2,1)S(1)} fusion(bf16[2,128,1792]{2,1,0:T(8,128)(2,1)} %collective-permute-done, bf16[2,128,1792]{2,1,0:T(8,128)(2,1)S(1)} %copy-done.1, pred[]{:T(512)S(6)} %eq.14), kind=kLoop, calls=%fused_computation.14 | loop fusion | flops 8257536 | bytes 3670017 | tf_op jit(solution)/shard_map/jit(_where)/select_n | solution.py:107
  38.5 1.6 %collective-permute-start.7 = (bf16[224,576]{1,0:T(8,128)(2,1)S(1)}, bf16[224,576]{1,0:T(8,128)(2,1)S(1)}, u32[]{:S(2)}, u32[]{:S(2)}) collective-permute-start(bf16[224,576]{1,0:T(8,128)(2,1)S(1)} %collective-permute-done.6), channel_id=1, source_target_pairs={{0,4},{4,8},{8,12},{12,14},{14,10},{10,6},{6,2},{2,0},{1,5},{5,9},... | collective-permute-start | bytes 774152 | tf_op jit(solution)/shard_map/ppermute | solution.py:47
  42.0 4.6 %collective-permute-done.7 = bf16[224,576]{1,0:T(8,128)(2,1)S(1)} collective-permute-done((bf16[224,576]{1,0:T(8,128)(2,1)S(1)}, bf16[224,576]{1,0:T(8,128)(2,1)S(1)}, u32[]{:S(2)}, u32[]{:S(2)}) %collective-permute-start.7) | collective-permute-done | bytes 258080 | tf_op jit(solution)/shard_map/ppermute | solution.py:47
  46.6 1.6 %collective-permute-start.8 = (bf16[224,576]{1,0:T(8,128)(2,1)S(1)}, bf16[224,576]{1,0:T(8,128)(2,1)S(1)}, u32[]{:S(2)}, u32[]{:S(2)}) collective-permute-start(bf16[224,576]{1,0:T(8,128)(2,1)S(1)} %collective-permute-done.7), channel_id=1, source_target_pairs={{0,4},{4,8},{8,12},{12,14},{14,10},{10,6},{6,2},{2,0},{1,5},{5,9},... | collective-permute-start | bytes 774152 | tf_op jit(solution)/shard_map/ppermute | solution.py:47
  50.1 3.7 %collective-permute-done.8 = bf16[224,576]{1,0:T(8,128)(2,1)S(1)} collective-permute-done((bf16[224,576]{1,0:T(8,128)(2,1)S(1)}, bf16[224,576]{1,0:T(8,128)(2,1)S(1)}, u32[]{:S(2)}, u32[]{:S(2)}) %collective-permute-start.8) | collective-permute-done | bytes 258080 | tf_op jit(solution)/shard_map/ppermute | solution.py:47
  53.8 1.6 %collective-permute-start.9 = (bf16[224,576]{1,0:T(8,128)(2,1)S(1)}, bf16[224,576]{1,0:T(8,128)(2,1)S(1)}, u32[]{:S(2)}, u32[]{:S(2)}) collective-permute-start(bf16[224,576]{1,0:T(8,128)(2,1)S(1)} %collective-permute-done.8), channel_id=1, source_target_pairs={{0,4},{4,8},{8,12},{12,14},{14,10},{10,6},{6,2},{2,0},{1,5},{5,9},... | collective-permute-start | bytes 774152 | tf_op jit(solution)/shard_map/ppermute | solution.py:47
  57.4 3.1 %collective-permute-done.9 = bf16[224,576]{1,0:T(8,128)(2,1)S(1)} collective-permute-done((bf16[224,576]{1,0:T(8,128)(2,1)S(1)}, bf16[224,576]{1,0:T(8,128)(2,1)S(1)}, u32[]{:S(2)}, u32[]{:S(2)}) %collective-permute-start.9) | collective-permute-done | bytes 258080 | tf_op jit(solution)/shard_map/ppermute | solution.py:47
  61.2 3.9 %gather_fusion = bf16[8,224,576]{2,1,0:T(8,128)(2,1)} fusion(bf16[8,224,576]{2,1,0:T(8,128)(2,1)} %bitcast_dynamic-update-slice_fusion.8, s32[1024]{0:T(1024)S(1)} %get-tuple-element.28), kind=kCustom, calls=%fused_computation | custom fusion | bytes 4128800 | tf_op jit(solution)/shard_map/gather | solution.py:56
  65.9 3.9 %gather_fusion.1 = bf16[8,224,576]{2,1,0:T(8,128)(2,1)} fusion(bf16[8,224,576]{2,1,0:T(8,128)(2,1)} %bitcast_dynamic-update-slice_fusion, s32[1024]{0:T(1024)S(1)} %get-tuple-element.27), kind=kCustom, calls=%fused_computation.1 | custom fusion | bytes 4128800 | tf_op jit(solution)/shard_map/gather | solution.py:56
  69.8 2.8 %pad_maximum_fusion = bf16[8,448,576]{2,1,0:T(8,128)(2,1)S(1)} fusion(bf16[8,224,576]{2,1,0:T(8,128)(2,1)} %gather_fusion.1, bf16[8,224,576]{2,1,0:T(8,128)(2,1)} %gather_fusion), kind=kLoop, calls=%fused_computation.12 | loop fusion | flops 8257536 | bytes 8257536 | tf_op jit(solution)/shard_map/concatenate | solution.py:55
  72.5 1.9 %maximum_select_fusion.1 = bf16[2,128,3584]{2,1,0:T(8,128)(2,1)S(1)} fusion(bf16[2,128,1792]{2,1,0:T(8,128)(2,1)} %collective-permute-done.2, bf16[2,128,1792]{2,1,0:T(8,128)(2,1)S(1)} %collective-permute-done.1, pred[]{:T(512)S(6)} %eq.14), kind=kLoop, calls=%fused_computation.15 | loop fusion | flops 8257536 | bytes 3670017 | tf_op jit(solution)/shard_map/jit(_where)/select_n | solution.py:112
  76.4 2.4 %convolution_add_fusion = f32[512,576]{0,1:T(8,128)S(1)} fusion(bf16[512,3584]{1,0:T(8,128)(2,1)S(1)} %bitcast.140, bf16[3584,576]{1,0:T(8,128)(2,1)S(1)} %bitcast.135, f32[576]{0:T(1024)S(1)} %maximum_select_fusion.2), kind=kOutput, calls=%fused_computation.30 | convolution fusion | flops 2114224128 | bytes 8980736 | tf_op jit(solution)/shard_map/dot_general | solution.py:127
  81.4 6.4 %collective-permute-done.17 = bf16[2,128,576]{1,0,2:T(2,128)(2,1)S(1)} collective-permute-done((bf16[2,128,576]{1,0,2:T(2,128)(2,1)S(1)}, bf16[2,128,576]{1,0,2:T(2,128)(2,1)S(1)}, u32[]{:S(2)}, u32[]{:S(2)}) %collective-permute-start.17) | collective-permute-done | bytes 294944 | tf_op jit(solution)/shard_map/ppermute | solution.py:138
  89.0 1.5 %collective-permute-start.18 = (bf16[2,128,256]{1,0,2:T(2,128)(2,1)S(1)}, bf16[2,128,256]{1,0,2:T(2,128)(2,1)S(1)}, u32[]{:S(2)}, u32[]{:S(2)}) collective-permute-start(bf16[2,128,256]{1,0,2:T(2,128)(2,1)S(1)} %pad_maximum_fusion.6), channel_id=1, source_target_pairs={{0,2},{2,4},{4,6},{6,8},{8,10},{10,12},{12,14},{14,0},{1,3},{3,5},... | collective-permute-start | bytes 393224 | tf_op jit(solution)/shard_map/ppermute | solution.py:149
  90.6 1.6 %collective-permute-start.19 = (bf16[2,128,256]{1,0,2:T(2,128)(2,1)S(1)}, bf16[2,128,256]{1,0,2:T(2,128)(2,1)S(1)}, u32[]{:S(2)}, u32[]{:S(2)}) collective-permute-start(bf16[2,128,256]{1,0,2:T(2,128)(2,1)S(1)} %pad_maximum_fusion.6), channel_id=1, source_target_pairs={{0,4},{2,6},{4,8},{6,10},{8,12},{10,14},{12,0},{14,2},{1,5},{3,7},... | collective-permute-start | bytes 393224 | tf_op jit(solution)/shard_map/ppermute | solution.py:149
  92.2 2.6 %collective-permute-start.20 = (bf16[2,128,256]{1,0,2:T(2,128)(2,1)S(1)}, bf16[2,128,256]{1,0,2:T(2,128)(2,1)S(1)}, u32[]{:S(2)}, u32[]{:S(2)}) collective-permute-start(bf16[2,128,256]{1,0,2:T(2,128)(2,1)S(1)} %pad_maximum_fusion.6), channel_id=1, source_target_pairs={{0,6},{2,8},{4,10},{6,12},{8,14},{10,0},{12,2},{14,4},{1,7},{3,9},... | collective-permute-start | bytes 393224 | tf_op jit(solution)/shard_map/ppermute | solution.py:149
  94.7 1.2 %collective-permute-start.21 = (bf16[2,128,256]{1,0,2:T(2,128)(2,1)S(1)}, bf16[2,128,256]{1,0,2:T(2,128)(2,1)S(1)}, u32[]{:S(2)}, u32[]{:S(2)}) collective-permute-start(bf16[2,128,256]{1,0,2:T(2,128)(2,1)S(1)} %pad_maximum_fusion.6), channel_id=1, source_target_pairs={{0,8},{2,10},{4,12},{6,14},{8,0},{10,2},{12,4},{14,6},{1,9},{3,11}... | collective-permute-start | bytes 393224 | tf_op jit(solution)/shard_map/ppermute | solution.py:149
  96.0 2.6 %collective-permute-start.22 = (bf16[2,128,256]{1,0,2:T(2,128)(2,1)S(1)}, bf16[2,128,256]{1,0,2:T(2,128)(2,1)S(1)}, u32[]{:S(2)}, u32[]{:S(2)}) collective-permute-start(bf16[2,128,256]{1,0,2:T(2,128)(2,1)S(1)} %pad_maximum_fusion.6), channel_id=1, source_target_pairs={{0,10},{2,12},{4,14},{6,0},{8,2},{10,4},{12,6},{14,8},{1,11},{3,13... | collective-permute-start | bytes 393224 | tf_op jit(solution)/shard_map/ppermute | solution.py:149
  99.7 1.8 %copy.51 = bf16[2,2,64,7,128]{4,2,3,1,0:T(8,128)(2,1)S(1)} copy(bf16[2,2,64,7,128]{2,1,0,4,3:T(2,128)(2,1)S(1)} %reshape.378) | data formatting | bytes 917504 | tf_op jit(solution)/shard_map/reshape | solution.py:186
  101.6 1.4 %collective-permute-start.23 = (bf16[2,128,256]{1,0,2:T(2,128)(2,1)S(1)}, bf16[2,128,256]{1,0,2:T(2,128)(2,1)S(1)}, u32[]{:S(2)}, u32[]{:S(2)}) collective-permute-start(bf16[2,128,256]{1,0,2:T(2,128)(2,1)S(1)} %pad_maximum_fusion.6), channel_id=1, source_target_pairs={{0,12},{2,14},{4,0},{6,2},{8,4},{10,6},{12,8},{14,10},{1,13},{3,15... | collective-permute-start | bytes 393224 | tf_op jit(solution)/shard_map/ppermute | solution.py:149
  103.1 1.7 %collective-permute-start.24 = (bf16[2,128,256]{1,0,2:T(2,128)(2,1)S(1)}, bf16[2,128,256]{1,0,2:T(2,128)(2,1)S(1)}, u32[]{:S(2)}, u32[]{:S(2)}) collective-permute-start(bf16[2,128,256]{1,0,2:T(2,128)(2,1)S(1)} %pad_maximum_fusion.6), channel_id=1, source_target_pairs={{0,14},{2,0},{4,2},{6,4},{8,6},{10,8},{12,10},{14,12},{1,15},{3,1}... | collective-permute-start | bytes 393224 | tf_op jit(solution)/shard_map/ppermute | solution.py:149
  106.3 2.8 %collective-permute-done.23 = bf16[2,128,256]{1,0,2:T(2,128)(2,1)S(1)} collective-permute-done((bf16[2,128,256]{1,0,2:T(2,128)(2,1)S(1)}, bf16[2,128,256]{1,0,2:T(2,128)(2,1)S(1)}, u32[]{:S(2)}, u32[]{:S(2)}) %collective-permute-start.23) | collective-permute-done | bytes 131104 | tf_op jit(solution)/shard_map/ppermute | solution.py:149
  110.2 1.4 %gather_fusion.4 = bf16[12,64,256]{2,1,0:T(8,128)(2,1)} fusion(bf16[2,16,64,256]{3,2,0,1:T(8,128)(2,1)S(1)} %bitcast.132, s32[12]{0:T(128)S(1)} %reshape.346), kind=kCustom, calls=%fused_computation.4 | custom fusion | bytes 786528 | tf_op jit(solution)/shard_map/gather | solution.py:172
  119.4 1.3 %convert_element_type.60 = bf16[2,128,896]{2,1,0:T(8,128)(2,1)} reshape(bf16[2,2,64,7,128]{4,3,2,1,0:T(8,128)(2,1)S(1)} %copy.56) | data formatting | bytes 917504 | tf_op jit(solution)/shard_map/convert_element_type | solution.py:248
  (155 shorter events, 39.9 us)
Async XLA Ops:
  0.0 10.8 %copy-start = (s32[2,2,2]{2,1,0:T(2,128)S(1)}, s32[2,2,2]{2,1,0:T(2,128)}, u32[]{:S(2)}) copy-start(s32[2,2,2]{2,1,0:T(2,128)} %param.20) | copy-start | bytes 100
  0.0 35.3 %collective-permute-start.1 = (bf16[2,128,1792]{2,1,0:T(8,128)(2,1)}, bf16[2,128,1792]{2,1,0:T(8,128)(2,1)S(1)}, u32[]{:S(2)}, u32[]{:S(2)}) collective-permute-start(bf16[2,128,1792]{2,1,0:T(8,128)(2,1)} %param.11), channel_id=1, source_target_pairs={{0,16},{16,0},{1,17},{17,1},{2,18},{18,2},{3,19},{19,3},{4,20},{20... | collective-permute-start | bytes 2752520 | tf_op jit(solution)/shard_map/ppermute | solution.py:105
  3.0 32.4 %collective-permute-start = (bf16[2,128,1792]{2,1,0:T(8,128)(2,1)}, bf16[2,128,1792]{2,1,0:T(8,128)(2,1)}, u32[]{:S(2)}, u32[]{:S(2)}) collective-permute-start(bf16[2,128,1792]{2,1,0:T(8,128)(2,1)} %param.11), channel_id=1, source_target_pairs={{0,1},{1,0},{2,3},{3,2},{4,5},{5,4},{6,7},{7,6},{8,9},{9,8},{10,11... | collective-permute-start | bytes 2752520 | tf_op jit(solution)/shard_map/ppermute | solution.py:104
  3.0 7.7 %copy-start.6 = (f32[128]{0:T(128)S(1)}, f32[128]{0:T(128)}, u32[]{:S(2)}) copy-start(f32[128]{0:T(128)} %param.18) | copy-start | bytes 1540
  3.0 7.8 %copy-start.4 = (f32[896]{0:T(1024)S(1)}, f32[896]{0:T(1024)}, u32[]{:S(2)}) copy-start(f32[896]{0:T(1024)} %param.14) | copy-start | bytes 10756
  3.0 7.8 %copy-start.7 = (f32[128]{0:T(128)S(1)}, f32[128]{0:T(128)}, u32[]{:S(2)}) copy-start(f32[128]{0:T(128)} %param.16) | copy-start | bytes 1540
  3.0 7.9 %copy-start.5 = (s32[2,16,14,2]{1,3,2,0:T(2,128)S(1)}, s32[2,16,14,2]{1,3,2,0:T(2,128)}, u32[]{:S(2)}) copy-start(s32[2,16,14,2]{1,3,2,0:T(2,128)} %param.19) | copy-start | bytes 10756
  4.1 7.2 %slice-start = ((f32[896]{0:T(1024)}), f32[512]{0:T(512)S(1)}, s32[]{:S(2)}) async-start(f32[896]{0:T(1024)} %param.14), calls=%async_computation | async-start | bytes 4096 | tf_op jit(solution)/shard_map/slice | solution.py:99
  6.5 9.3 %collective-permute-start.3 = (bf16[224,576]{1,0:T(8,128)(2,1)S(1)}, bf16[224,576]{1,0:T(8,128)(2,1)S(1)}, u32[]{:S(2)}, u32[]{:S(2)}) collective-permute-start(bf16[224,576]{1,0:T(8,128)(2,1)S(1)} %get-tuple-element.11), channel_id=1, source_target_pairs={{0,4},{4,8},{8,12},{12,14},{14,10},{10,6},{6,2},{2,0},{1,5},{5,9},... | collective-permute-start | bytes 774152 | tf_op jit(solution)/shard_map/ppermute | solution.py:47
  8.1 9.2 %collective-permute-start.10 = (bf16[224,576]{1,0:T(8,128)(2,1)S(1)}, bf16[224,576]{1,0:T(8,128)(2,1)S(1)}, u32[]{:S(2)}, u32[]{:S(2)}) collective-permute-start(bf16[224,576]{1,0:T(8,128)(2,1)S(1)} %get-tuple-element.12), channel_id=1, source_target_pairs={{0,2},{4,0},{8,4},{12,8},{14,12},{10,14},{6,10},{2,6},{1,3},{5,1},... | collective-permute-start | bytes 774152 | tf_op jit(solution)/shard_map/ppermute | solution.py:48
  12.6 22.8 %copy-start.1 = (bf16[2,128,1792]{2,1,0:T(8,128)(2,1)S(1)}, bf16[2,128,1792]{2,1,0:T(8,128)(2,1)}, u32[]{:S(2)}) copy-start(bf16[2,128,1792]{2,1,0:T(8,128)(2,1)} %param.11) | copy-start | bytes 2752516
  15.8 8.5 %collective-permute-start.4 = (bf16[224,576]{1,0:T(8,128)(2,1)S(1)}, bf16[224,576]{1,0:T(8,128)(2,1)S(1)}, u32[]{:S(2)}, u32[]{:S(2)}) collective-permute-start(bf16[224,576]{1,0:T(8,128)(2,1)S(1)} %collective-permute-done.3), channel_id=1, source_target_pairs={{0,4},{4,8},{8,12},{12,14},{14,10},{10,6},{6,2},{2,0},{1,5},{5,9},... | collective-permute-start | bytes 774152 | tf_op jit(solution)/shard_map/ppermute | solution.py:47
  17.3 8.5 %collective-permute-start.11 = (bf16[224,576]{1,0:T(8,128)(2,1)S(1)}, bf16[224,576]{1,0:T(8,128)(2,1)S(1)}, u32[]{:S(2)}, u32[]{:S(2)}) collective-permute-start(bf16[224,576]{1,0:T(8,128)(2,1)S(1)} %collective-permute-done.10), channel_id=1, source_target_pairs={{0,2},{4,0},{8,4},{12,8},{14,12},{10,14},{6,10},{2,6},{1,3},{5,1},... | collective-permute-start | bytes 774152 | tf_op jit(solution)/shard_map/ppermute | solution.py:48
  24.2 7.6 %collective-permute-start.5 = (bf16[224,576]{1,0:T(8,128)(2,1)S(1)}, bf16[224,576]{1,0:T(8,128)(2,1)S(1)}, u32[]{:S(2)}, u32[]{:S(2)}) collective-permute-start(bf16[224,576]{1,0:T(8,128)(2,1)S(1)} %collective-permute-done.4), channel_id=1, source_target_pairs={{0,4},{4,8},{8,12},{12,14},{14,10},{10,6},{6,2},{2,0},{1,5},{5,9},... | collective-permute-start | bytes 774152 | tf_op jit(solution)/shard_map/ppermute | solution.py:47
  25.8 7.6 %collective-permute-start.12 = (bf16[224,576]{1,0:T(8,128)(2,1)S(1)}, bf16[224,576]{1,0:T(8,128)(2,1)S(1)}, u32[]{:S(2)}, u32[]{:S(2)}) collective-permute-start(bf16[224,576]{1,0:T(8,128)(2,1)S(1)} %collective-permute-done.11), channel_id=1, source_target_pairs={{0,2},{4,0},{8,4},{12,8},{14,12},{10,14},{6,10},{2,6},{1,3},{5,1},... | collective-permute-start | bytes 774152 | tf_op jit(solution)/shard_map/ppermute | solution.py:48
  31.8 6.7 %collective-permute-start.6 = (bf16[224,576]{1,0:T(8,128)(2,1)S(1)}, bf16[224,576]{1,0:T(8,128)(2,1)S(1)}, u32[]{:S(2)}, u32[]{:S(2)}) collective-permute-start(bf16[224,576]{1,0:T(8,128)(2,1)S(1)} %collective-permute-done.5), channel_id=1, source_target_pairs={{0,4},{4,8},{8,12},{12,14},{14,10},{10,6},{6,2},{2,0},{1,5},{5,9},... | collective-permute-start | bytes 774152 | tf_op jit(solution)/shard_map/ppermute | solution.py:47
  33.4 7.4 %collective-permute-start.13 = (bf16[224,576]{1,0:T(8,128)(2,1)S(1)}, bf16[224,576]{1,0:T(8,128)(2,1)S(1)}, u32[]{:S(2)}, u32[]{:S(2)}) collective-permute-start(bf16[224,576]{1,0:T(8,128)(2,1)S(1)} %collective-permute-done.12), channel_id=1, source_target_pairs={{0,2},{4,0},{8,4},{12,8},{14,12},{10,14},{6,10},{2,6},{1,3},{5,1},... | collective-permute-start | bytes 774152 | tf_op jit(solution)/shard_map/ppermute | solution.py:48
  35.3 37.2 %collective-permute-start.2 = (bf16[2,128,1792]{2,1,0:T(8,128)(2,1)S(1)}, bf16[2,128,1792]{2,1,0:T(8,128)(2,1)}, u32[]{:S(2)}, u32[]{:S(2)}) collective-permute-start(bf16[2,128,1792]{2,1,0:T(8,128)(2,1)S(1)} %collective-permute-done.1), channel_id=1, source_target_pairs={{0,1},{1,0},{2,3},{3,2},{4,5},{5,4},{6,7},{7,6},{8,9},{9,8},{10,11... | collective-permute-start | bytes 2752520 | tf_op jit(solution)/shard_map/ppermute | solution.py:106
  38.5 8.1 %collective-permute-start.7 = (bf16[224,576]{1,0:T(8,128)(2,1)S(1)}, bf16[224,576]{1,0:T(8,128)(2,1)S(1)}, u32[]{:S(2)}, u32[]{:S(2)}) collective-permute-start(bf16[224,576]{1,0:T(8,128)(2,1)S(1)} %collective-permute-done.6), channel_id=1, source_target_pairs={{0,4},{4,8},{8,12},{12,14},{14,10},{10,6},{6,2},{2,0},{1,5},{5,9},... | collective-permute-start | bytes 774152 | tf_op jit(solution)/shard_map/ppermute | solution.py:47
  40.8 8.1 %collective-permute-start.14 = (bf16[224,576]{1,0:T(8,128)(2,1)S(1)}, bf16[224,576]{1,0:T(8,128)(2,1)S(1)}, u32[]{:S(2)}, u32[]{:S(2)}) collective-permute-start(bf16[224,576]{1,0:T(8,128)(2,1)S(1)} %collective-permute-done.13), channel_id=1, source_target_pairs={{0,2},{4,0},{8,4},{12,8},{14,12},{10,14},{6,10},{2,6},{1,3},{5,1},... | collective-permute-start | bytes 774152 | tf_op jit(solution)/shard_map/ppermute | solution.py:48
  46.6 7.2 %collective-permute-start.8 = (bf16[224,576]{1,0:T(8,128)(2,1)S(1)}, bf16[224,576]{1,0:T(8,128)(2,1)S(1)}, u32[]{:S(2)}, u32[]{:S(2)}) collective-permute-start(bf16[224,576]{1,0:T(8,128)(2,1)S(1)} %collective-permute-done.7), channel_id=1, source_target_pairs={{0,4},{4,8},{8,12},{12,14},{14,10},{10,6},{6,2},{2,0},{1,5},{5,9},... | collective-permute-start | bytes 774152 | tf_op jit(solution)/shard_map/ppermute | solution.py:47
  48.9 7.2 %collective-permute-start.15 = (bf16[224,576]{1,0:T(8,128)(2,1)S(1)}, bf16[224,576]{1,0:T(8,128)(2,1)S(1)}, u32[]{:S(2)}, u32[]{:S(2)}) collective-permute-start(bf16[224,576]{1,0:T(8,128)(2,1)S(1)} %collective-permute-done.14), channel_id=1, source_target_pairs={{0,2},{4,0},{8,4},{12,8},{14,12},{10,14},{6,10},{2,6},{1,3},{5,1},... | collective-permute-start | bytes 774152 | tf_op jit(solution)/shard_map/ppermute | solution.py:48
  53.8 6.6 %collective-permute-start.9 = (bf16[224,576]{1,0:T(8,128)(2,1)S(1)}, bf16[224,576]{1,0:T(8,128)(2,1)S(1)}, u32[]{:S(2)}, u32[]{:S(2)}) collective-permute-start(bf16[224,576]{1,0:T(8,128)(2,1)S(1)} %collective-permute-done.8), channel_id=1, source_target_pairs={{0,4},{4,8},{8,12},{12,14},{14,10},{10,6},{6,2},{2,0},{1,5},{5,9},... | collective-permute-start | bytes 774152 | tf_op jit(solution)/shard_map/ppermute | solution.py:47
  56.1 9.0 %collective-permute-start.16 = (bf16[224,576]{1,0:T(8,128)(2,1)S(1)}, bf16[224,576]{1,0:T(8,128)(2,1)S(1)}, u32[]{:S(2)}, u32[]{:S(2)}) collective-permute-start(bf16[224,576]{1,0:T(8,128)(2,1)S(1)} %collective-permute-done.15), channel_id=1, source_target_pairs={{0,2},{4,0},{8,4},{12,8},{14,12},{10,14},{6,10},{2,6},{1,3},{5,1},... | collective-permute-start | bytes 774152 | tf_op jit(solution)/shard_map/ppermute | solution.py:48
  81.0 6.8 %collective-permute-start.17 = (bf16[2,128,576]{1,0,2:T(2,128)(2,1)S(1)}, bf16[2,128,576]{1,0,2:T(2,128)(2,1)S(1)}, u32[]{:S(2)}, u32[]{:S(2)}) collective-permute-start(bf16[2,128,576]{1,0,2:T(2,128)(2,1)S(1)} %fusion.25), channel_id=1, source_target_pairs={{0,16},{16,0},{1,17},{17,1},{2,18},{18,2},{3,19},{19,3},{4,20},{20... | collective-permute-start | bytes 884744 | tf_op jit(solution)/shard_map/ppermute | solution.py:138
  89.0 12.5 %collective-permute-start.18 = (bf16[2,128,256]{1,0,2:T(2,128)(2,1)S(1)}, bf16[2,128,256]{1,0,2:T(2,128)(2,1)S(1)}, u32[]{:S(2)}, u32[]{:S(2)}) collective-permute-start(bf16[2,128,256]{1,0,2:T(2,128)(2,1)S(1)} %pad_maximum_fusion.6), channel_id=1, source_target_pairs={{0,2},{2,4},{4,6},{6,8},{8,10},{10,12},{12,14},{14,0},{1,3},{3,5},... | collective-permute-start | bytes 393224 | tf_op jit(solution)/shard_map/ppermute | solution.py:149
  90.6 12.5 %collective-permute-start.19 = (bf16[2,128,256]{1,0,2:T(2,128)(2,1)S(1)}, bf16[2,128,256]{1,0,2:T(2,128)(2,1)S(1)}, u32[]{:S(2)}, u32[]{:S(2)}) collective-permute-start(bf16[2,128,256]{1,0,2:T(2,128)(2,1)S(1)} %pad_maximum_fusion.6), channel_id=1, source_target_pairs={{0,4},{2,6},{4,8},{6,10},{8,12},{10,14},{12,0},{14,2},{1,5},{3,7},... | collective-permute-start | bytes 393224 | tf_op jit(solution)/shard_map/ppermute | solution.py:149
  92.2 12.9 %collective-permute-start.20 = (bf16[2,128,256]{1,0,2:T(2,128)(2,1)S(1)}, bf16[2,128,256]{1,0,2:T(2,128)(2,1)S(1)}, u32[]{:S(2)}, u32[]{:S(2)}) collective-permute-start(bf16[2,128,256]{1,0,2:T(2,128)(2,1)S(1)} %pad_maximum_fusion.6), channel_id=1, source_target_pairs={{0,6},{2,8},{4,10},{6,12},{8,14},{10,0},{12,2},{14,4},{1,7},{3,9},... | collective-permute-start | bytes 393224 | tf_op jit(solution)/shard_map/ppermute | solution.py:149
  94.7 11.3 %collective-permute-start.21 = (bf16[2,128,256]{1,0,2:T(2,128)(2,1)S(1)}, bf16[2,128,256]{1,0,2:T(2,128)(2,1)S(1)}, u32[]{:S(2)}, u32[]{:S(2)}) collective-permute-start(bf16[2,128,256]{1,0,2:T(2,128)(2,1)S(1)} %pad_maximum_fusion.6), channel_id=1, source_target_pairs={{0,8},{2,10},{4,12},{6,14},{8,0},{10,2},{12,4},{14,6},{1,9},{3,11}... | collective-permute-start | bytes 393224 | tf_op jit(solution)/shard_map/ppermute | solution.py:149
  96.0 10.2 %collective-permute-start.22 = (bf16[2,128,256]{1,0,2:T(2,128)(2,1)S(1)}, bf16[2,128,256]{1,0,2:T(2,128)(2,1)S(1)}, u32[]{:S(2)}, u32[]{:S(2)}) collective-permute-start(bf16[2,128,256]{1,0,2:T(2,128)(2,1)S(1)} %pad_maximum_fusion.6), channel_id=1, source_target_pairs={{0,10},{2,12},{4,14},{6,0},{8,2},{10,4},{12,6},{14,8},{1,11},{3,13... | collective-permute-start | bytes 393224 | tf_op jit(solution)/shard_map/ppermute | solution.py:149
  101.6 7.6 %collective-permute-start.23 = (bf16[2,128,256]{1,0,2:T(2,128)(2,1)S(1)}, bf16[2,128,256]{1,0,2:T(2,128)(2,1)S(1)}, u32[]{:S(2)}, u32[]{:S(2)}) collective-permute-start(bf16[2,128,256]{1,0,2:T(2,128)(2,1)S(1)} %pad_maximum_fusion.6), channel_id=1, source_target_pairs={{0,12},{2,14},{4,0},{6,2},{8,4},{10,6},{12,8},{14,10},{1,13},{3,15... | collective-permute-start | bytes 393224 | tf_op jit(solution)/shard_map/ppermute | solution.py:149
  103.1 6.2 %collective-permute-start.24 = (bf16[2,128,256]{1,0,2:T(2,128)(2,1)S(1)}, bf16[2,128,256]{1,0,2:T(2,128)(2,1)S(1)}, u32[]{:S(2)}, u32[]{:S(2)}) collective-permute-start(bf16[2,128,256]{1,0,2:T(2,128)(2,1)S(1)} %pad_maximum_fusion.6), channel_id=1, source_target_pairs={{0,14},{2,0},{4,2},{6,4},{8,6},{10,8},{12,10},{14,12},{1,15},{3,1}... | collective-permute-start | bytes 393224 | tf_op jit(solution)/shard_map/ppermute | solution.py:149
  (4 other events, 14.9 us)

commit v4 on v2

--- a/solution.py
+++ b/solution.py
@@ -25,6 +25,47 @@
     sine = jnp.concatenate([jnp.sin(angles), jnp.sin(angles)], axis=-1)[None, :, None, :]
     turned = jnp.concatenate([-values[..., half:], values[..., :half]], axis=-1)
     return values * cosine + turned * sine
+
+
+def snake_order(count):
+    return [2 * z for z in range(count // 2)] + [2 * z + 1 for z in reversed(range(count // 2))]
+
+
+def project_rows(normed, shard, count, here, column):
+    features = normed.shape[1]
+    shift = (count // 2) * column
+    if count != 8:
+        full = lax.all_gather(shard, "row", axis=0, tiled=True)
+        full = jnp.where(
+            column == 0,
+            full,
+            jnp.concatenate([full[features // 2 :], full[: features // 2]], axis=0),
+        )
+        return jnp.dot(normed, full, preferred_element_type=jnp.float32)
+    order = snake_order(count)
+    position = [0] * count
+    for i, d in enumerate(order):
+        position[d] = i
+    forward = [(order[i], order[(i + 1) % count]) for i in range(count)]
+    backward = [(order[i], order[(i - 1) % count]) for i in range(count)]
+    half = shard.shape[0] // 2
+    chunks = normed.reshape(normed.shape[0], count, 2, half).transpose(1, 2, 0, 3)
+    table = jnp.array(position, dtype=jnp.int32)
+    ring = jnp.array(order, dtype=jnp.int32)
+    mine = table[here]
+
+    def term(source, part, piece):
+        rows = chunks[(source + shift) % count, part]
+        return jnp.dot(rows, piece, preferred_element_type=jnp.float32)
+
+    ahead, behind = shard[:half], shard[half:]
+    total = term(here, 0, ahead) + term(here, 1, behind)
+    for step in range(1, count):
+        ahead = lax.ppermute(ahead, "row", forward)
+        behind = lax.ppermute(behind, "row", backward)
+        total = total + term(ring[(mine - step) % count], 0, ahead)
+        total = total + term(ring[(mine + step) % count], 1, behind)
+    return total
 
 
 def shards(
@@ -68,32 +109,33 @@
         jnp.concatenate([rotary_b[:split], value_bias[:value_split]]),
         jnp.concatenate([rotary_b[split:], value_bias[value_split:]]),
     )
-    full_panel = lax.all_gather(panel, "row", axis=0, tiled=True)
 
     other_half = lax.ppermute(tokens, "col", SWAP)
     partner_half = lax.ppermute(tokens, "groups", SWAP)
     partner_other = lax.ppermute(partner_half, "col", SWAP)
-    whole = jnp.where(
+    both = jnp.concatenate(
+        [
+            jnp.concatenate([tokens, other_half], axis=2),
+            jnp.concatenate([partner_half, partner_other], axis=2),
+        ],
+        axis=0,
+    )
+    features = both.shape[2]
+    gain_here = jnp.where(
         column == 0,
-        jnp.concatenate([tokens, other_half], axis=2),
-        jnp.concatenate([other_half, tokens], axis=2),
-    )
-    partner = jnp.where(
-        column == 0,
-        jnp.concatenate([partner_half, partner_other], axis=2),
-        jnp.concatenate([partner_other, partner_half], axis=2),
-    )
-    both = jnp.concatenate([whole, partner], axis=0)
+        gain,
+        jnp.concatenate([gain[features // 2 :], gain[: features // 2]]),
+    )
     widened = both.astype(jnp.float32)
     power = jnp.mean(widened * widened, axis=-1, keepdims=True)
     normed = (
-        (widened * lax.rsqrt(power + norm_eps) * gain)
+        (widened * lax.rsqrt(power + norm_eps) * gain_here)
         .astype(jnp.bfloat16)
         .reshape(2 * passages * length, -1)
     )
     token_positions = (here * length + jnp.arange(length, dtype=jnp.int32)).astype(jnp.float32)
 
-    summed = jnp.dot(normed, full_panel, preferred_element_type=jnp.float32) + panel_bias
+    summed = project_rows(normed, panel, row_count, here, column) + panel_bias
     summed = summed.reshape(2 * passages, length, split + value_split)
     turned = apply_rotation(
         summed[..., :split].reshape(2 * passages, length, split // HEAD_SIZE, HEAD_SIZE),

time: 152 us -> 183 us (1.20)
  waiting for transfers between devices: 82.5 us -> 39.9 us
  local copies, waits for them, and re-layouts: 13.3 us -> 50 us
  matrix products: 10.2 us -> 23.7 us
  starting transfers between devices: 16.8 us -> 30.3 us
  other arithmetic: 12.3 us -> 18.3 us
  between operations: 14.1 us -> 19.3 us
    all_gather x1 -> x0, waiting for transfers between devices: 50.2 us -> none  [shards(): full_panel = lax.all_gather(panel, 'row', axis=0, tiled=True)]
    ppermute x0 -> x14, waiting for transfers between devices: none -> 30.8 us  [the longest x7 30.8 us: project_rows(): behind = lax.ppermute(behind, 'row', backward)]
    convert_element_type x0 -> x2, local copies, waits for them, and re-layouts: none -> 29.1 us  [shards(): widened = both.astype(jnp.float32)]
    ppermute x1, waiting for transfers between devices: 18.5 us -> 0.01 us  [shards(): partner_half = lax.ppermute(tokens, 'groups', SWAP)]
    ppermute x0 -> x14, starting transfers between devices: none -> 14.2 us  [the longest x7 10.5 us: project_rows(): behind = lax.ppermute(behind, 'row', backward)]
    dot_general x1 -> x16, matrix products: 5.79 us -> 19.3 us  [term(): return jnp.dot(rows, piece, preferred_element_type=jnp.float32)]
    convert_element_type x1, other arithmetic: 0.48 us -> 4.41 us  [shards(): widened = both.astype(jnp.float32)]
    ppermute x7, waiting for transfers between devices: 6.05 us -> 2.8 us  [shards(): lax.ppermute(pairs, 'row', [(i, (i + k) % row_count) for i in range(row_c...]
  transfers between devices with their start and end apart: 12 -> 25, of which waited for: 7 -> 8; matrix products, arithmetic and copies ran while one was open for 7% -> 40% of each run, Pallas kernels for 0% -> 0%
where the time goes in v4:
time: 183 us; the launch traced here: 182 us
  local copies, waits for them, and re-layouts  50 us (27%)
  waiting for transfers between devices  39.9 us (22%)
  starting transfers between devices  30.3 us (17%)
  matrix products  23.7 us (13%)
  between operations  19.3 us (11%)
  other arithmetic  18.3 us (10%)
    ppermute x7, waiting for transfers between devices, project_rows(): behind = lax.ppermute(behind, 'row', backward)  30.8 us
    convert_element_type x2, local copies, waits for them, and re-layouts, shards(): widened = both.astype(jnp.float32)  29.1 us
    dot_general x16, matrix products, term(): return jnp.dot(rows, piece, preferred_element_type=jnp.float32)  19.3 us
    ppermute x7, starting transfers between devices, shards(): lax.ppermute(pairs, 'row', [(i, (i + k) % row_count) for i in range(row_c...  12.6 us
    ppermute x7, starting transfers between devices, project_rows(): behind = lax.ppermute(behind, 'row', backward)  10.5 us
    ppermute x1, waiting for transfers between devices, shards(): returned = lax.ppermute(result[passages:], 'groups', SWAP)  6.37 us
    convert_element_type x1, other arithmetic, shards(): widened = both.astype(jnp.float32)  4.41 us
    convert_element_type x1, other arithmetic, shards(): normed = (widened * lax.rsqrt(power + norm_eps) * gain_here).astype(jnp.b...  3.76 us
  transfers between devices with their start and end apart: 25, of which 8 were waited for; matrix products, arithmetic and copies ran while one was open for 40% of the time, Pallas kernels for 0%

profile of v4, /device:TPU:0, one launch (start us, length us, event | category | flops | bytes accessed | tf_op | source)
XLA Modules:
  0.0 181.5 jit_solution(12973399427097129765)
XLA Ops:
  0.0 3.0 %collective-permute-start.1 = (bf16[2,128,1792]{2,1,0:T(8,128)(2,1)}, bf16[2,128,1792]{2,1,0:T(8,128)(2,1)S(1)}, u32[]{:S(2)}, u32[]{:S(2)}) collective-permute-start(bf16[2,128,1792]{2,1,0:T(8,128)(2,1)} %param.12), channel_id=1, source_target_pairs={{0,16},{16,0},{1,17},{17,1},{2,18},{18,2},{3,19},{19,3},{4,20},{20... | collective-permute-start | bytes 2752520 | tf_op jit(solution)/shard_map/ppermute | solution.py:114
  4.1 1.8 %slice.94 = bf16[448,512]{1,0:T(8,128)(2,1)} slice(bf16[448,896]{1,0:T(8,128)(2,1)} %param.14), slice={[0:448], [0:512]} | slice | bytes 917504 | tf_op jit(solution)/shard_map/slice | solution.py:104
  8.1 1.5 collective-permute-start.4
  10.6 7.1 %collective-permute-done.4 = bf16[224,576]{1,0:T(8,128)(2,1)} collective-permute-done((bf16[224,576]{1,0:T(8,128)(2,1)}, bf16[224,576]{1,0:T(8,128)(2,1)}, u32[]{:S(2)}, u32[]{:S(2)}) %collective-permute-start.4) | collective-permute-done | bytes 258080 | tf_op jit(solution)/shard_map/ppermute | solution.py:65
  17.7 1.5 collective-permute-start.6
  19.7 6.7 %collective-permute-done.6 = bf16[224,576]{1,0:T(8,128)(2,1)} collective-permute-done((bf16[224,576]{1,0:T(8,128)(2,1)}, bf16[224,576]{1,0:T(8,128)(2,1)}, u32[]{:S(2)}, u32[]{:S(2)}) %collective-permute-start.6) | collective-permute-done | bytes 258080 | tf_op jit(solution)/shard_map/ppermute | solution.py:65
  26.5 1.5 collective-permute-start.8
  28.5 5.8 %collective-permute-done.8 = bf16[224,576]{1,0:T(8,128)(2,1)} collective-permute-done((bf16[224,576]{1,0:T(8,128)(2,1)}, bf16[224,576]{1,0:T(8,128)(2,1)}, u32[]{:S(2)}, u32[]{:S(2)}) %collective-permute-start.8) | collective-permute-done | bytes 258080 | tf_op jit(solution)/shard_map/ppermute | solution.py:65
  34.3 1.5 collective-permute-start.10
  36.5 5.0 %collective-permute-done.10 = bf16[224,576]{1,0:T(8,128)(2,1)} collective-permute-done((bf16[224,576]{1,0:T(8,128)(2,1)}, bf16[224,576]{1,0:T(8,128)(2,1)}, u32[]{:S(2)}, u32[]{:S(2)}) %collective-permute-start.10) | collective-permute-done | bytes 258080 | tf_op jit(solution)/shard_map/ppermute | solution.py:65
  41.6 1.5 collective-permute-start.12
  43.8 6.1 %collective-permute-done.12 = bf16[224,576]{1,0:T(8,128)(2,1)} collective-permute-done((bf16[224,576]{1,0:T(8,128)(2,1)}, bf16[224,576]{1,0:T(8,128)(2,1)}, u32[]{:S(2)}, u32[]{:S(2)}) %collective-permute-start.12) | collective-permute-done | bytes 258080 | tf_op jit(solution)/shard_map/ppermute | solution.py:65
  49.9 1.5 collective-permute-start.14
  74.3 1.5 collective-permute-start.16
  76.4 4.4 %maximum_convert_fusion = f32[4,128,3584]{2,1,0:T(8,128)} fusion(bf16[2,128,1792]{2,1,0:T(8,128)(2,1)} %collective-permute-done.2, bf16[2,128,1792]{2,1,0:T(8,128)(2,1)S(1)} %collective-permute-done.1, bf16[2,128,1792]{2,1,0:T(8,128)(2,1)S(1)} %collective-permute-done, bf16[2,128,1792]{2,1,0:T(8,128)(2,1)S(1)} %copy-done.2), kind=kLoop, calls=%fused_computation.7 | loop fusion | flops 14680064 | bytes 11010048 | tf_op jit(solution)/shard_map/convert_element_type | solution.py:129
  80.8 16.2 %reshape.379 = f32[512,8,2,224]{3,2,1,0:T(2,128)} reshape(f32[4,128,3584]{2,1,0:T(8,128)} %maximum_convert_fusion) | data formatting | bytes 14680064 | tf_op jit(solution)/shard_map/convert_element_type | solution.py:129
  97.0 12.9 %copy.65 = f32[512,8,2,224]{0,3,2,1:T(8,128)} copy(f32[512,8,2,224]{3,2,1,0:T(2,128)} %reshape.379) | data formatting | bytes 14680064 | tf_op jit(solution)/shard_map/convert_element_type | solution.py:129
  109.9 3.7 %multiply_reduce_fusion = f32[4,128]{1,0:T(4,128)S(1)} fusion(bf16[2,128,1792]{2,1,0:T(8,128)(2,1)} %collective-permute-done.2, bf16[2,128,1792]{2,1,0:T(8,128)(2,1)S(1)} %collective-permute-done.1, bf16[2,128,1792]{2,1,0:T(8,128)(2,1)S(1)} %collective-permute-done, bf16[2,128,1792]{2,1,0:T(8,128)(2,1)S(1)} %copy-done.2), kind=kLoop, calls=%fused_computation.6 | loop fusion | flops 18349568 | bytes 3672064 | tf_op jit(solution)/shard_map/reduce_sum | solution.py:130
  113.6 3.8 %multiply_convert_fusion = bf16[512,8,2,224]{0,3,2,1:T(8,128)(2,1)S(1)} fusion(f32[512,8,2,224]{0,3,2,1:T(8,128)} %copy.65, f32[8,2,224]{2,1,0:T(2,128)S(1)} %copy-done.8, f32[512]{0:T(512)S(1)} %rsqrt_bitcast_fusion), kind=kLoop, calls=%fused_computation.5 | loop fusion | flops 5505024 | bytes 11026432 | tf_op jit(solution)/shard_map/convert_element_type | solution.py:133
  126.1 1.3 fusion.8
  131.5 1.3 fusion.4
  135.5 1.4 fusion.2
  139.5 6.4 %collective-permute-done.17 = bf16[2,128,576]{1,0,2:T(2,128)(2,1)S(1)} collective-permute-done((bf16[2,128,576]{1,0,2:T(2,128)(2,1)S(1)}, bf16[2,128,576]{1,0,2:T(2,128)(2,1)S(1)}, u32[]{:S(2)}, u32[]{:S(2)}) %collective-permute-start.17) | collective-permute-done | bytes 294944 | tf_op jit(solution)/shard_map/ppermute | solution.py:149
  147.1 1.5 collective-permute-start.18
  148.7 1.6 collective-permute-start.19
  150.2 2.6 %collective-permute-start.20 = (bf16[2,128,256]{1,0,2:T(2,128)(2,1)S(1)}, bf16[2,128,256]{1,0,2:T(2,128)(2,1)S(1)}, u32[]{:S(2)}, u32[]{:S(2)}) collective-permute-start(bf16[2,128,256]{1,0,2:T(2,128)(2,1)S(1)} %pad_maximum_fusion.4), channel_id=1, source_target_pairs={{0,6},{2,8},{4,10},{6,12},{8,14},{10,0},{12,2},{14,4},{1,7},{3,9},... | collective-permute-start | bytes 393224 | tf_op jit(solution)/shard_map/ppermute | solution.py:160
  154.0 2.6 %collective-permute-start.22 = (bf16[2,128,256]{1,0,2:T(2,128)(2,1)S(1)}, bf16[2,128,256]{1,0,2:T(2,128)(2,1)S(1)}, u32[]{:S(2)}, u32[]{:S(2)}) collective-permute-start(bf16[2,128,256]{1,0,2:T(2,128)(2,1)S(1)} %pad_maximum_fusion.4), channel_id=1, source_target_pairs={{0,10},{2,12},{4,14},{6,0},{8,2},{10,4},{12,6},{14,8},{1,11},{3,13... | collective-permute-start | bytes 393224 | tf_op jit(solution)/shard_map/ppermute | solution.py:160
  157.8 1.8 %copy.55 = bf16[2,2,64,7,128]{4,2,3,1,0:T(8,128)(2,1)S(1)} copy(bf16[2,2,64,7,128]{2,1,0,4,3:T(2,128)(2,1)S(1)} %reshape.380) | data formatting | bytes 917504 | tf_op jit(solution)/shard_map/reshape | solution.py:197
  160.3 1.3 collective-permute-start.23
  162.7 1.7 collective-permute-start.24
  165.0 1.8 collective-permute-done.23
  171.0 1.4 gather_fusion.2
  (162 shorter events, 48.5 us)
Async XLA Ops:
  0.0 10.2 %copy-start = (s32[2,2,2]{2,1,0:T(2,128)S(1)}, s32[2,2,2]{2,1,0:T(2,128)}, u32[]{:S(2)}) copy-start(s32[2,2,2]{2,1,0:T(2,128)} %param.21) | copy-start | bytes 100
  0.0 36.4 %collective-permute-start.1 = (bf16[2,128,1792]{2,1,0:T(8,128)(2,1)}, bf16[2,128,1792]{2,1,0:T(8,128)(2,1)S(1)}, u32[]{:S(2)}, u32[]{:S(2)}) collective-permute-start(bf16[2,128,1792]{2,1,0:T(8,128)(2,1)} %param.12), channel_id=1, source_target_pairs={{0,16},{16,0},{1,17},{17,1},{2,18},{18,2},{3,19},{19,3},{4,20},{20... | collective-permute-start | bytes 2752520 | tf_op jit(solution)/shard_map/ppermute | solution.py:114
  3.0 73.4 %collective-permute-start = (bf16[2,128,1792]{2,1,0:T(8,128)(2,1)}, bf16[2,128,1792]{2,1,0:T(8,128)(2,1)S(1)}, u32[]{:S(2)}, u32[]{:S(2)}) collective-permute-start(bf16[2,128,1792]{2,1,0:T(8,128)(2,1)} %param.12), channel_id=1, source_target_pairs={{0,1},{1,0},{2,3},{3,2},{4,5},{5,4},{6,7},{7,6},{8,9},{9,8},{10,11... | collective-permute-start | bytes 2752520 | tf_op jit(solution)/shard_map/ppermute | solution.py:113
  5.9 13.8 %copy-start.9 = (f32[3584]{0:T(1024)S(1)}, f32[3584]{0:T(1024)}, u32[]{:S(2)}) copy-start(f32[3584]{0:T(1024)} %param.13) | copy-start | bytes 43012
  5.9 22.6 %copy-start.10 = (f32[896]{0:T(1024)S(1)}, f32[896]{0:T(1024)}, u32[]{:S(2)}) copy-start(f32[896]{0:T(1024)} %param.15) | copy-start | bytes 10756
  5.9 22.6 %copy-start.13 = (f32[128]{0:T(128)S(1)}, f32[128]{0:T(128)}, u32[]{:S(2)}) copy-start(f32[128]{0:T(128)} %param.17) | copy-start | bytes 1540
  5.9 56.6 %copy-start.7 = (s32[8]{0:T(128)S(1)}, s32[8]{0:T(128)}, u32[]{:S(2)}) copy-start(s32[8]{0:T(128)} %constant.293.clone) | copy-start | bytes 100
  7.2 67.0 %slice-start = ((f32[896]{0:T(1024)}), f32[512]{0:T(512)S(1)}, s32[]{:S(2)}) async-start(f32[896]{0:T(1024)} %param.15), calls=%async_computation | async-start | bytes 4096 | tf_op jit(solution)/shard_map/slice | solution.py:109
  7.2 69.1 %copy-start.2 = (bf16[2,128,1792]{2,1,0:T(8,128)(2,1)S(1)}, bf16[2,128,1792]{2,1,0:T(8,128)(2,1)}, u32[]{:S(2)}) copy-start(bf16[2,128,1792]{2,1,0:T(8,128)(2,1)} %param.12) | copy-start | bytes 2752516
  8.1 9.6 %collective-permute-start.4 = (bf16[224,576]{1,0:T(8,128)(2,1)}, bf16[224,576]{1,0:T(8,128)(2,1)}, u32[]{:S(2)}, u32[]{:S(2)}) collective-permute-start(bf16[224,576]{1,0:T(8,128)(2,1)} %get-tuple-element.12), channel_id=1, source_target_pairs={{0,2},{4,0},{8,4},{12,8},{14,12},{10,14},{6,10},{2,6},{1,3},{5,1},... | collective-permute-start | bytes 774152 | tf_op jit(solution)/shard_map/ppermute | solution.py:65
  9.6 9.6 %collective-permute-start.3 = (bf16[224,576]{1,0:T(8,128)(2,1)}, bf16[224,576]{1,0:T(8,128)(2,1)}, u32[]{:S(2)}, u32[]{:S(2)}) collective-permute-start(bf16[224,576]{1,0:T(8,128)(2,1)} %get-tuple-element.11), channel_id=1, source_target_pairs={{0,4},{4,8},{8,12},{12,14},{14,10},{10,6},{6,2},{2,0},{1,5},{5,9},... | collective-permute-start | bytes 774152 | tf_op jit(solution)/shard_map/ppermute | solution.py:64
  17.7 8.8 %collective-permute-start.6 = (bf16[224,576]{1,0:T(8,128)(2,1)}, bf16[224,576]{1,0:T(8,128)(2,1)}, u32[]{:S(2)}, u32[]{:S(2)}) collective-permute-start(bf16[224,576]{1,0:T(8,128)(2,1)} %collective-permute-done.4), channel_id=1, source_target_pairs={{0,2},{4,0},{8,4},{12,8},{14,12},{10,14},{6,10},{2,6},{1,3},{5,1},... | collective-permute-start | bytes 774152 | tf_op jit(solution)/shard_map/ppermute | solution.py:65
  19.2 8.8 %collective-permute-start.5 = (bf16[224,576]{1,0:T(8,128)(2,1)}, bf16[224,576]{1,0:T(8,128)(2,1)}, u32[]{:S(2)}, u32[]{:S(2)}) collective-permute-start(bf16[224,576]{1,0:T(8,128)(2,1)} %collective-permute-done.3), channel_id=1, source_target_pairs={{0,4},{4,8},{8,12},{12,14},{14,10},{10,6},{6,2},{2,0},{1,5},{5,9},... | collective-permute-start | bytes 774152 | tf_op jit(solution)/shard_map/ppermute | solution.py:64
  26.5 7.9 %collective-permute-start.8 = (bf16[224,576]{1,0:T(8,128)(2,1)}, bf16[224,576]{1,0:T(8,128)(2,1)}, u32[]{:S(2)}, u32[]{:S(2)}) collective-permute-start(bf16[224,576]{1,0:T(8,128)(2,1)} %collective-permute-done.6), channel_id=1, source_target_pairs={{0,2},{4,0},{8,4},{12,8},{14,12},{10,14},{6,10},{2,6},{1,3},{5,1},... | collective-permute-start | bytes 774152 | tf_op jit(solution)/shard_map/ppermute | solution.py:65
  28.0 7.9 %collective-permute-start.7 = (bf16[224,576]{1,0:T(8,128)(2,1)}, bf16[224,576]{1,0:T(8,128)(2,1)}, u32[]{:S(2)}, u32[]{:S(2)}) collective-permute-start(bf16[224,576]{1,0:T(8,128)(2,1)} %collective-permute-done.5), channel_id=1, source_target_pairs={{0,4},{4,8},{8,12},{12,14},{14,10},{10,6},{6,2},{2,0},{1,5},{5,9},... | collective-permute-start | bytes 774152 | tf_op jit(solution)/shard_map/ppermute | solution.py:64
  34.3 7.2 %collective-permute-start.10 = (bf16[224,576]{1,0:T(8,128)(2,1)}, bf16[224,576]{1,0:T(8,128)(2,1)}, u32[]{:S(2)}, u32[]{:S(2)}) collective-permute-start(bf16[224,576]{1,0:T(8,128)(2,1)} %collective-permute-done.8), channel_id=1, source_target_pairs={{0,2},{4,0},{8,4},{12,8},{14,12},{10,14},{6,10},{2,6},{1,3},{5,1},... | collective-permute-start | bytes 774152 | tf_op jit(solution)/shard_map/ppermute | solution.py:65
  35.8 7.2 %collective-permute-start.9 = (bf16[224,576]{1,0:T(8,128)(2,1)}, bf16[224,576]{1,0:T(8,128)(2,1)}, u32[]{:S(2)}, u32[]{:S(2)}) collective-permute-start(bf16[224,576]{1,0:T(8,128)(2,1)} %collective-permute-done.7), channel_id=1, source_target_pairs={{0,4},{4,8},{8,12},{12,14},{14,10},{10,6},{6,2},{2,0},{1,5},{5,9},... | collective-permute-start | bytes 774152 | tf_op jit(solution)/shard_map/ppermute | solution.py:64
  36.4 40.0 %collective-permute-start.2 = (bf16[2,128,1792]{2,1,0:T(8,128)(2,1)S(1)}, bf16[2,128,1792]{2,1,0:T(8,128)(2,1)}, u32[]{:S(2)}, u32[]{:S(2)}) collective-permute-start(bf16[2,128,1792]{2,1,0:T(8,128)(2,1)S(1)} %collective-permute-done.1), channel_id=1, source_target_pairs={{0,1},{1,0},{2,3},{3,2},{4,5},{5,4},{6,7},{7,6},{8,9},{9,8},{10,11... | collective-permute-start | bytes 2752520 | tf_op jit(solution)/shard_map/ppermute | solution.py:115
  41.6 8.3 %collective-permute-start.12 = (bf16[224,576]{1,0:T(8,128)(2,1)}, bf16[224,576]{1,0:T(8,128)(2,1)}, u32[]{:S(2)}, u32[]{:S(2)}) collective-permute-start(bf16[224,576]{1,0:T(8,128)(2,1)} %collective-permute-done.10), channel_id=1, source_target_pairs={{0,2},{4,0},{8,4},{12,8},{14,12},{10,14},{6,10},{2,6},{1,3},{5,1},... | collective-permute-start | bytes 774152 | tf_op jit(solution)/shard_map/ppermute | solution.py:65
  43.1 8.3 %collective-permute-start.11 = (bf16[224,576]{1,0:T(8,128)(2,1)}, bf16[224,576]{1,0:T(8,128)(2,1)}, u32[]{:S(2)}, u32[]{:S(2)}) collective-permute-start(bf16[224,576]{1,0:T(8,128)(2,1)} %collective-permute-done.9), channel_id=1, source_target_pairs={{0,4},{4,8},{8,12},{12,14},{14,10},{10,6},{6,2},{2,0},{1,5},{5,9},... | collective-permute-start | bytes 774152 | tf_op jit(solution)/shard_map/ppermute | solution.py:64
  49.9 24.4 %collective-permute-start.14 = (bf16[224,576]{1,0:T(8,128)(2,1)}, bf16[224,576]{1,0:T(8,128)(2,1)}, u32[]{:S(2)}, u32[]{:S(2)}) collective-permute-start(bf16[224,576]{1,0:T(8,128)(2,1)} %collective-permute-done.12), channel_id=1, source_target_pairs={{0,2},{4,0},{8,4},{12,8},{14,12},{10,14},{6,10},{2,6},{1,3},{5,1},... | collective-permute-start | bytes 774152 | tf_op jit(solution)/shard_map/ppermute | solution.py:65
  51.4 24.4 %collective-permute-start.13 = (bf16[224,576]{1,0:T(8,128)(2,1)}, bf16[224,576]{1,0:T(8,128)(2,1)}, u32[]{:S(2)}, u32[]{:S(2)}) collective-permute-start(bf16[224,576]{1,0:T(8,128)(2,1)} %collective-permute-done.11), channel_id=1, source_target_pairs={{0,4},{4,8},{8,12},{12,14},{14,10},{10,6},{6,2},{2,0},{1,5},{5,9},... | collective-permute-start | bytes 774152 | tf_op jit(solution)/shard_map/ppermute | solution.py:64
  74.3 59.8 %collective-permute-start.16 = (bf16[224,576]{1,0:T(8,128)(2,1)}, bf16[224,576]{1,0:T(8,128)(2,1)}, u32[]{:S(2)}, u32[]{:S(2)}) collective-permute-start(bf16[224,576]{1,0:T(8,128)(2,1)} %collective-permute-done.14), channel_id=1, source_target_pairs={{0,2},{4,0},{8,4},{12,8},{14,12},{10,14},{6,10},{2,6},{1,3},{5,1},... | collective-permute-start | bytes 774152 | tf_op jit(solution)/shard_map/ppermute | solution.py:65
  75.8 59.6 %collective-permute-start.15 = (bf16[224,576]{1,0:T(8,128)(2,1)}, bf16[224,576]{1,0:T(8,128)(2,1)}, u32[]{:S(2)}, u32[]{:S(2)}) collective-permute-start(bf16[224,576]{1,0:T(8,128)(2,1)} %collective-permute-done.13), channel_id=1, source_target_pairs={{0,4},{4,8},{8,12},{12,14},{14,10},{10,6},{6,2},{2,0},{1,5},{5,9},... | collective-permute-start | bytes 774152 | tf_op jit(solution)/shard_map/ppermute | solution.py:64
  139.1 6.8 %collective-permute-start.17 = (bf16[2,128,576]{1,0,2:T(2,128)(2,1)S(1)}, bf16[2,128,576]{1,0,2:T(2,128)(2,1)S(1)}, u32[]{:S(2)}, u32[]{:S(2)}) collective-permute-start(bf16[2,128,576]{1,0,2:T(2,128)(2,1)S(1)} %fusion.30), channel_id=1, source_target_pairs={{0,16},{16,0},{1,17},{17,1},{2,18},{18,2},{3,19},{19,3},{4,20},{20... | collective-permute-start | bytes 884744 | tf_op jit(solution)/shard_map/ppermute | solution.py:149
  147.1 12.5 %collective-permute-start.18 = (bf16[2,128,256]{1,0,2:T(2,128)(2,1)S(1)}, bf16[2,128,256]{1,0,2:T(2,128)(2,1)S(1)}, u32[]{:S(2)}, u32[]{:S(2)}) collective-permute-start(bf16[2,128,256]{1,0,2:T(2,128)(2,1)S(1)} %pad_maximum_fusion.4), channel_id=1, source_target_pairs={{0,2},{2,4},{4,6},{6,8},{8,10},{10,12},{12,14},{14,0},{1,3},{3,5},... | collective-permute-start | bytes 393224 | tf_op jit(solution)/shard_map/ppermute | solution.py:160
  148.7 14.0 %collective-permute-start.19 = (bf16[2,128,256]{1,0,2:T(2,128)(2,1)S(1)}, bf16[2,128,256]{1,0,2:T(2,128)(2,1)S(1)}, u32[]{:S(2)}, u32[]{:S(2)}) collective-permute-start(bf16[2,128,256]{1,0,2:T(2,128)(2,1)S(1)} %pad_maximum_fusion.4), channel_id=1, source_target_pairs={{0,4},{2,6},{4,8},{6,10},{8,12},{10,14},{12,0},{14,2},{1,5},{3,7},... | collective-permute-start | bytes 393224 | tf_op jit(solution)/shard_map/ppermute | solution.py:160
  150.2 14.3 %collective-permute-start.20 = (bf16[2,128,256]{1,0,2:T(2,128)(2,1)S(1)}, bf16[2,128,256]{1,0,2:T(2,128)(2,1)S(1)}, u32[]{:S(2)}, u32[]{:S(2)}) collective-permute-start(bf16[2,128,256]{1,0,2:T(2,128)(2,1)S(1)} %pad_maximum_fusion.4), channel_id=1, source_target_pairs={{0,6},{2,8},{4,10},{6,12},{8,14},{10,0},{12,2},{14,4},{1,7},{3,9},... | collective-permute-start | bytes 393224 | tf_op jit(solution)/shard_map/ppermute | solution.py:160
  152.8 11.9 %collective-permute-start.21 = (bf16[2,128,256]{1,0,2:T(2,128)(2,1)S(1)}, bf16[2,128,256]{1,0,2:T(2,128)(2,1)S(1)}, u32[]{:S(2)}, u32[]{:S(2)}) collective-permute-start(bf16[2,128,256]{1,0,2:T(2,128)(2,1)S(1)} %pad_maximum_fusion.4), channel_id=1, source_target_pairs={{0,8},{2,10},{4,12},{6,14},{8,0},{10,2},{12,4},{14,6},{1,9},{3,11}... | collective-permute-start | bytes 393224 | tf_op jit(solution)/shard_map/ppermute | solution.py:160
  154.0 10.8 %collective-permute-start.22 = (bf16[2,128,256]{1,0,2:T(2,128)(2,1)S(1)}, bf16[2,128,256]{1,0,2:T(2,128)(2,1)S(1)}, u32[]{:S(2)}, u32[]{:S(2)}) collective-permute-start(bf16[2,128,256]{1,0,2:T(2,128)(2,1)S(1)} %pad_maximum_fusion.4), channel_id=1, source_target_pairs={{0,10},{2,12},{4,14},{6,0},{8,2},{10,4},{12,6},{14,8},{1,11},{3,13... | collective-permute-start | bytes 393224 | tf_op jit(solution)/shard_map/ppermute | solution.py:160
  160.3 6.5 %collective-permute-start.23 = (bf16[2,128,256]{1,0,2:T(2,128)(2,1)S(1)}, bf16[2,128,256]{1,0,2:T(2,128)(2,1)S(1)}, u32[]{:S(2)}, u32[]{:S(2)}) collective-permute-start(bf16[2,128,256]{1,0,2:T(2,128)(2,1)S(1)} %pad_maximum_fusion.4), channel_id=1, source_target_pairs={{0,12},{2,14},{4,0},{6,2},{8,4},{10,6},{12,8},{14,10},{1,13},{3,15... | collective-permute-start | bytes 393224 | tf_op jit(solution)/shard_map/ppermute | solution.py:160
  162.7 5.2 %collective-permute-start.24 = (bf16[2,128,256]{1,0,2:T(2,128)(2,1)S(1)}, bf16[2,128,256]{1,0,2:T(2,128)(2,1)S(1)}, u32[]{:S(2)}, u32[]{:S(2)}) collective-permute-start(bf16[2,128,256]{1,0,2:T(2,128)(2,1)S(1)} %pad_maximum_fusion.4), channel_id=1, source_target_pairs={{0,14},{2,0},{4,2},{6,4},{8,6},{10,8},{12,10},{14,12},{1,15},{3,1}... | collective-permute-start | bytes 393224 | tf_op jit(solution)/shard_map/ppermute | solution.py:160
  (8 other events, 24.2 us)

commit v5 on v3

--- a/solution.py
+++ b/solution.py
@@ -42,19 +42,19 @@
     backward = [(order[i], order[(i - 1) % count]) for i in range(count)]
     half = shard.shape[0] // 2
     ahead, behind = shard[:half], shard[half:]
-    ahead_parts, behind_parts = [ahead], [behind]
-    for _ in range(count - 1):
+    table = jnp.array(position, dtype=jnp.int32)
+    ring = jnp.array(order, dtype=jnp.int32)
+    mine = table[here]
+    joined = jnp.zeros((count, 2, half, shard.shape[1]), shard.dtype)
+    joined = lax.dynamic_update_slice(joined, ahead[None, None], (here, 0, 0, 0))
+    joined = lax.dynamic_update_slice(joined, behind[None, None], (here, 1, 0, 0))
+    for step in range(1, count):
         ahead = lax.ppermute(ahead, "row", forward)
         behind = lax.ppermute(behind, "row", backward)
-        ahead_parts.append(ahead)
-        behind_parts.append(behind)
-    table = jnp.array(position, dtype=jnp.int32)
-    mine = table[here]
-    ahead_pick = (mine - table) % count
-    behind_pick = (table - mine) % count
-    joined = jnp.concatenate(
-        [jnp.stack(ahead_parts)[ahead_pick], jnp.stack(behind_parts)[behind_pick]], axis=1
-    )
+        ahead_source = ring[(mine - step) % count]
+        behind_source = ring[(mine + step) % count]
+        joined = lax.dynamic_update_slice(joined, ahead[None, None], (ahead_source, 0, 0, 0))
+        joined = lax.dynamic_update_slice(joined, behind[None, None], (behind_source, 1, 0, 0))
     return joined.reshape(count * shard.shape[0], shard.shape[1])
 
 
@@ -89,10 +89,12 @@
     rotary_w = jnp.concatenate([w_query, key_weight], axis=1)
     rotary_b = jnp.concatenate([b_query, b_key], axis=0)
     first = group == 0
-    panel = jnp.where(
-        first,
-        jnp.concatenate([rotary_w[:, :split], value_weight[:, :value_split]], axis=1),
-        jnp.concatenate([rotary_w[:, split:], value_weight[:, value_split:]], axis=1),
+    panel = jnp.concatenate(
+        [
+            lax.dynamic_slice_in_dim(rotary_w, group * split, split, 1),
+            lax.dynamic_slice_in_dim(value_weight, group * value_split, value_split, 1),
+        ],
+        axis=1,
     )
     panel_bias = jnp.where(
         first,

time: 123 us -> 157 us (1.28)
  between operations: 0.77 us -> 37 us
  local copies, waits for them, and re-layouts: 32.7 us -> 29.5 us
  matrix products: 6.82 us -> 10 us
  other arithmetic: 16.1 us -> 14.4 us
    dynamic_update_slice x0 -> x14, local copies, waits for them, and re-layouts: none -> 10.3 us  [the longest x7 5.18 us: gather_rows(): lax.dynamic_update_slice(joined, behind[None, None], (behind_source, 1, 0...]
    unnamed x41 -> x36, local copies, waits for them, and re-layouts: 9.93 us -> 0.4 us
    gather x2 -> x0, local copies, waits for them, and re-layouts: 7.79 us -> none  [the longest x1 3.9 us: gather_rows(): jnp.stack(behind_parts)[behind_pick]]
    broadcast_in_dim x0 -> x1, local copies, waits for them, and re-layouts: none -> 2.57 us  [gather_rows(): joined = jnp.zeros((count, 2, half, shard.shape[1]), shard.dtype)]
    select_n x3 -> x0, other arithmetic: 2.54 us -> none  [the longest x1 1.22 us: shards(): jnp.where(first, jnp.concatenate([rotary_w[:, :split], value_weight[:, :v...]
    dot_general x1, matrix products: 2.38 us -> 4.71 us  [shards(): jnp.dot(normed, full_panel, preferred_element_type=jnp.float32) + panel_bias]
    slice x3 -> x0, local copies, waits for them, and re-layouts: 2.19 us -> none  [the longest x1 1.09 us: shards(): value_weight[:, value_split:]]
    dynamic_update_slice x0 -> x2, other arithmetic: none -> 1.7 us  [the longest x1 0.85 us: gather_rows(): lax.dynamic_update_slice(joined, behind[None, None], (here, 1, 0, 0))]
  transfers between devices with their start and end apart: 25 -> 25, of which waited for: 11 -> 11; matrix products, arithmetic and copies ran while one was open for 29% -> 20% of each run, Pallas kernels for 0% -> 0%
where the time goes in v5:
time: 157 us; the launch traced here: 155 us
  between operations  37 us (24%)
  waiting for transfers between devices  34.5 us (22%)
  starting transfers between devices  30 us (19%)
  local copies, waits for them, and re-layouts  29.5 us (19%)
  other arithmetic  14.4 us (9%)
  matrix products  10 us (6%)
    ppermute x7, waiting for transfers between devices, gather_rows(): ahead = lax.ppermute(ahead, 'row', forward)  24.7 us
    ppermute x7, starting transfers between devices, shards(): lax.ppermute(pairs, 'row', [(i, (i + k) % row_count) for i in range(row_c...  12.7 us
    ppermute x7, starting transfers between devices, gather_rows(): ahead = lax.ppermute(ahead, 'row', forward)  10.8 us
    ppermute x1, waiting for transfers between devices, shards(): returned = lax.ppermute(result[passages:], 'groups', SWAP)  6.67 us
    dynamic_update_slice x7, local copies, waits for them, and re-layouts, gather_rows(): lax.dynamic_update_slice(joined, behind[None, None], (behind_source, 1, 0...  5.18 us
    dynamic_update_slice x7, local copies, waits for them, and re-layouts, gather_rows(): lax.dynamic_update_slice(joined, ahead[None, None], (ahead_source, 0, 0, 0))  5.15 us
    dot_general x1, matrix products, shards(): jnp.dot(normed, full_panel, preferred_element_type=jnp.float32) + panel_bias  4.71 us
    ppermute x7, starting transfers between devices, gather_rows(): behind = lax.ppermute(behind, 'row', backward)  3.45 us
  transfers between devices with their start and end apart: 25, of which 11 were waited for; matrix products, arithmetic and copies ran while one was open for 20% of the time, Pallas kernels for 0%

profile of v5, /device:TPU:0, one launch (start us, length us, event | category | flops | bytes accessed | tf_op | source)
XLA Modules:
  0.0 155.4 jit_solution(2906801850519589448)
XLA Ops:
  0.0 3.0 %collective-permute-start.1 = (bf16[2,128,1792]{2,1,0:T(8,128)(2,1)}, bf16[2,128,1792]{2,1,0:T(8,128)(2,1)S(1)}, u32[]{:S(2)}, u32[]{:S(2)}) collective-permute-start(bf16[2,128,1792]{2,1,0:T(8,128)(2,1)} %param.12), channel_id=1, source_target_pairs={{0,16},{16,0},{1,17},{17,1},{2,18},{18,2},{3,19},{19,3},{4,20},{20... | collective-permute-start | bytes 2752520 | tf_op jit(solution)/shard_map/ppermute | solution.py:107
  4.4 2.6 %broadcast_in_dim.60 = bf16[8,2,224,576]{3,2,1,0:T(8,128)(2,1)} broadcast(bf16[]{:T(256)} %constant.205.clone.1), dimensions={} | broadcast | bytes 4128770 | tf_op jit(solution)/shard_map/broadcast_in_dim | solution.py:48
  7.8 1.6 %collective-permute-start.3 = (bf16[224,576]{1,0:T(8,128)(2,1)}, bf16[224,576]{1,0:T(8,128)(2,1)S(1)}, u32[]{:S(2)}, u32[]{:S(2)}) collective-permute-start(bf16[224,576]{1,0:T(8,128)(2,1)} %get-tuple-element.10), channel_id=1, source_target_pairs={{0,4},{4,8},{8,12},{12,14},{14,10},{10,6},{6,2},{2,0},{1,5},{5,9},... | collective-permute-start | bytes 774152 | tf_op jit(solution)/shard_map/ppermute | solution.py:52
  13.7 1.3 dynamic_slice.61
  44.1 1.3 reshape.364
  56.2 1.5 pad_maximum_fusion.6
  57.7 1.5 collective-permute-start.5
  61.2 5.2 %collective-permute-done.5 = bf16[224,576]{1,0:T(8,128)(2,1)S(1)} collective-permute-done((bf16[224,576]{1,0:T(8,128)(2,1)S(1)}, bf16[224,576]{1,0:T(8,128)(2,1)S(1)}, u32[]{:S(2)}, u32[]{:S(2)}) %collective-permute-start.5) | collective-permute-done | bytes 258080 | tf_op jit(solution)/shard_map/ppermute | solution.py:52
  66.3 1.5 collective-permute-start.7
  69.9 4.3 %collective-permute-done.7 = bf16[224,576]{1,0:T(8,128)(2,1)S(1)} collective-permute-done((bf16[224,576]{1,0:T(8,128)(2,1)S(1)}, bf16[224,576]{1,0:T(8,128)(2,1)S(1)}, u32[]{:S(2)}, u32[]{:S(2)}) %collective-permute-start.7) | collective-permute-done | bytes 258080 | tf_op jit(solution)/shard_map/ppermute | solution.py:52
  74.2 1.5 collective-permute-start.9
  78.1 3.0 %collective-permute-done.9 = bf16[224,576]{1,0:T(8,128)(2,1)S(1)} collective-permute-done((bf16[224,576]{1,0:T(8,128)(2,1)S(1)}, bf16[224,576]{1,0:T(8,128)(2,1)S(1)}, u32[]{:S(2)}, u32[]{:S(2)}) %collective-permute-start.9) | collective-permute-done | bytes 258080 | tf_op jit(solution)/shard_map/ppermute | solution.py:52
  81.1 1.5 collective-permute-start.11
  84.6 4.0 %collective-permute-done.11 = bf16[224,576]{1,0:T(8,128)(2,1)S(1)} collective-permute-done((bf16[224,576]{1,0:T(8,128)(2,1)S(1)}, bf16[224,576]{1,0:T(8,128)(2,1)S(1)}, u32[]{:S(2)}, u32[]{:S(2)}) %collective-permute-start.11) | collective-permute-done | bytes 258080 | tf_op jit(solution)/shard_map/ppermute | solution.py:52
  88.6 1.5 collective-permute-start.13
  92.1 5.2 %collective-permute-done.13 = bf16[224,576]{1,0:T(8,128)(2,1)S(1)} collective-permute-done((bf16[224,576]{1,0:T(8,128)(2,1)S(1)}, bf16[224,576]{1,0:T(8,128)(2,1)S(1)}, u32[]{:S(2)}, u32[]{:S(2)}) %collective-permute-start.13) | collective-permute-done | bytes 258080 | tf_op jit(solution)/shard_map/ppermute | solution.py:52
  97.3 1.5 collective-permute-start.15
  100.8 3.1 %collective-permute-done.15 = bf16[224,576]{1,0:T(8,128)(2,1)S(1)} collective-permute-done((bf16[224,576]{1,0:T(8,128)(2,1)S(1)}, bf16[224,576]{1,0:T(8,128)(2,1)S(1)}, u32[]{:S(2)}, u32[]{:S(2)}) %collective-permute-start.15) | collective-permute-done | bytes 258080 | tf_op jit(solution)/shard_map/ppermute | solution.py:52
  108.5 4.7 %convolution_add_fusion = f32[512,576]{0,1:T(8,128)S(1)} fusion(bf16[512,3584]{1,0:T(8,128)(2,1)S(1)} %bitcast.166, bf16[3584,576]{1,0:T(8,128)(2,1)} %bitcast.45, f32[576]{0:T(1024)S(1)} %maximum_select_fusion.2), kind=kOutput, calls=%fused_computation.27 | convolution fusion | flops 2114224128 | bytes 8980736 | tf_op jit(solution)/shard_map/dot_general | solution.py:129
  115.7 6.7 %collective-permute-done.17 = bf16[2,128,576]{1,0,2:T(2,128)(2,1)S(1)} collective-permute-done((bf16[2,128,576]{1,0,2:T(2,128)(2,1)S(1)}, bf16[2,128,576]{1,0,2:T(2,128)(2,1)S(1)}, u32[]{:S(2)}, u32[]{:S(2)}) %collective-permute-start.17) | collective-permute-done | bytes 294944 | tf_op jit(solution)/shard_map/ppermute | solution.py:140
  124.3 1.9 %collective-permute-start.19 = (bf16[2,128,256]{1,0,2:T(2,128)(2,1)S(1)}, bf16[2,128,256]{1,0,2:T(2,128)(2,1)S(1)}, u32[]{:S(2)}, u32[]{:S(2)}) collective-permute-start(bf16[2,128,256]{1,0,2:T(2,128)(2,1)S(1)} %pad_maximum_fusion.5), channel_id=1, source_target_pairs={{0,4},{2,6},{4,8},{6,10},{8,12},{10,14},{12,0},{14,2},{1,5},{3,7},... | collective-permute-start | bytes 393224 | tf_op jit(solution)/shard_map/ppermute | solution.py:151
  126.2 3.1 %collective-permute-start.20 = (bf16[2,128,256]{1,0,2:T(2,128)(2,1)S(1)}, bf16[2,128,256]{1,0,2:T(2,128)(2,1)S(1)}, u32[]{:S(2)}, u32[]{:S(2)}) collective-permute-start(bf16[2,128,256]{1,0,2:T(2,128)(2,1)S(1)} %pad_maximum_fusion.5), channel_id=1, source_target_pairs={{0,6},{2,8},{4,10},{6,12},{8,14},{10,0},{12,2},{14,4},{1,7},{3,9},... | collective-permute-start | bytes 393224 | tf_op jit(solution)/shard_map/ppermute | solution.py:151
  129.3 1.3 collective-permute-start.21
  130.6 2.1 %collective-permute-start.22 = (bf16[2,128,256]{1,0,2:T(2,128)(2,1)S(1)}, bf16[2,128,256]{1,0,2:T(2,128)(2,1)S(1)}, u32[]{:S(2)}, u32[]{:S(2)}) collective-permute-start(bf16[2,128,256]{1,0,2:T(2,128)(2,1)S(1)} %pad_maximum_fusion.5), channel_id=1, source_target_pairs={{0,10},{2,12},{4,14},{6,0},{8,2},{10,4},{12,6},{14,8},{1,11},{3,13... | collective-permute-start | bytes 393224 | tf_op jit(solution)/shard_map/ppermute | solution.py:151
  133.8 1.8 %copy.52 = bf16[2,2,64,7,128]{4,2,3,1,0:T(8,128)(2,1)S(1)} copy(bf16[2,2,64,7,128]{2,1,0,4,3:T(2,128)(2,1)S(1)} %reshape.388) | data formatting | bytes 917504 | tf_op jit(solution)/shard_map/reshape | solution.py:188
  135.7 1.4 collective-permute-start.23
  137.2 2.3 %collective-permute-start.24 = (bf16[2,128,256]{1,0,2:T(2,128)(2,1)S(1)}, bf16[2,128,256]{1,0,2:T(2,128)(2,1)S(1)}, u32[]{:S(2)}, u32[]{:S(2)}) collective-permute-start(bf16[2,128,256]{1,0,2:T(2,128)(2,1)S(1)} %pad_maximum_fusion.5), channel_id=1, source_target_pairs={{0,14},{2,0},{4,2},{6,4},{8,6},{10,8},{12,10},{14,12},{1,15},{3,1}... | collective-permute-start | bytes 393224 | tf_op jit(solution)/shard_map/ppermute | solution.py:151
  140.9 1.2 collective-permute-done.23
  143.3 1.4 gather_fusion.2
  144.7 1.2 gather_fusion.3
  146.8 1.4 fusion.43
  154.1 1.3 convert_element_type.60
  (158 shorter events, 41.6 us)
Async XLA Ops:
  0.0 77.7 %collective-permute-start.1 = (bf16[2,128,1792]{2,1,0:T(8,128)(2,1)}, bf16[2,128,1792]{2,1,0:T(8,128)(2,1)S(1)}, u32[]{:S(2)}, u32[]{:S(2)}) collective-permute-start(bf16[2,128,1792]{2,1,0:T(8,128)(2,1)} %param.12), channel_id=1, source_target_pairs={{0,16},{16,0},{1,17},{17,1},{2,18},{18,2},{3,19},{19,3},{4,20},{20... | collective-permute-start | bytes 2752520 | tf_op jit(solution)/shard_map/ppermute | solution.py:107
  3.0 74.7 %collective-permute-start = (bf16[2,128,1792]{2,1,0:T(8,128)(2,1)}, bf16[2,128,1792]{2,1,0:T(8,128)(2,1)S(1)}, u32[]{:S(2)}, u32[]{:S(2)}) collective-permute-start(bf16[2,128,1792]{2,1,0:T(8,128)(2,1)} %param.12), channel_id=1, source_target_pairs={{0,1},{1,0},{2,3},{3,2},{4,5},{5,4},{6,7},{7,6},{8,9},{9,8},{10,11... | collective-permute-start | bytes 2752520 | tf_op jit(solution)/shard_map/ppermute | solution.py:106
  4.3 7.8 %copy-start.12 = (s32[2,2,2]{2,1,0:T(2,128)S(1)}, s32[2,2,2]{2,1,0:T(2,128)}, u32[]{:S(2)}) copy-start(s32[2,2,2]{2,1,0:T(2,128)} %param.21) | copy-start | bytes 100
  4.3 8.4 %copy-start.9 = (s32[2,16,14,2]{1,3,2,0:T(2,128)S(1)}, s32[2,16,14,2]{1,3,2,0:T(2,128)}, u32[]{:S(2)}) copy-start(s32[2,16,14,2]{1,3,2,0:T(2,128)} %param.20) | copy-start | bytes 10756
  4.3 8.6 %copy-start.7 = (f32[896]{0:T(1024)S(1)}, f32[896]{0:T(1024)}, u32[]{:S(2)}) copy-start(f32[896]{0:T(1024)} %param.15) | copy-start | bytes 10756
  4.3 8.6 %copy-start.11 = (f32[128]{0:T(128)S(1)}, f32[128]{0:T(128)}, u32[]{:S(2)}) copy-start(f32[128]{0:T(128)} %param.17) | copy-start | bytes 1540
  4.3 20.4 %copy-start.5 = (s32[8]{0:T(128)S(1)}, s32[8]{0:T(128)}, u32[]{:S(2)}) copy-start(s32[8]{0:T(128)} %constant.238.clone) | copy-start | bytes 100
  4.3 51.2 %slice-start = ((f32[896]{0:T(1024)}), f32[512]{0:T(512)S(1)}, s32[]{:S(2)}) async-start(f32[896]{0:T(1024)} %param.15), calls=%async_computation | async-start | bytes 4096 | tf_op jit(solution)/shard_map/slice | solution.py:101
  6.9 70.7 %copy-start.1 = (bf16[2,128,1792]{2,1,0:T(8,128)(2,1)S(1)}, bf16[2,128,1792]{2,1,0:T(8,128)(2,1)}, u32[]{:S(2)}) copy-start(bf16[2,128,1792]{2,1,0:T(8,128)(2,1)} %param.12) | copy-start | bytes 2752516
  7.8 49.9 %collective-permute-start.3 = (bf16[224,576]{1,0:T(8,128)(2,1)}, bf16[224,576]{1,0:T(8,128)(2,1)S(1)}, u32[]{:S(2)}, u32[]{:S(2)}) collective-permute-start(bf16[224,576]{1,0:T(8,128)(2,1)} %get-tuple-element.10), channel_id=1, source_target_pairs={{0,4},{4,8},{8,12},{12,14},{14,10},{10,6},{6,2},{2,0},{1,5},{5,9},... | collective-permute-start | bytes 774152 | tf_op jit(solution)/shard_map/ppermute | solution.py:52
  10.2 49.0 %collective-permute-start.4 = (bf16[224,576]{1,0:T(8,128)(2,1)}, bf16[224,576]{1,0:T(8,128)(2,1)S(1)}, u32[]{:S(2)}, u32[]{:S(2)}) collective-permute-start(bf16[224,576]{1,0:T(8,128)(2,1)} %get-tuple-element.8), channel_id=1, source_target_pairs={{0,2},{4,0},{8,4},{12,8},{14,12},{10,14},{6,10},{2,6},{1,3},{5,1},... | collective-permute-start | bytes 774152 | tf_op jit(solution)/shard_map/ppermute | solution.py:53
  57.7 8.7 %collective-permute-start.5 = (bf16[224,576]{1,0:T(8,128)(2,1)S(1)}, bf16[224,576]{1,0:T(8,128)(2,1)S(1)}, u32[]{:S(2)}, u32[]{:S(2)}) collective-permute-start(bf16[224,576]{1,0:T(8,128)(2,1)S(1)} %collective-permute-done.3), channel_id=1, source_target_pairs={{0,4},{4,8},{8,12},{12,14},{14,10},{10,6},{6,2},{2,0},{1,5},{5,9},... | collective-permute-start | bytes 774152 | tf_op jit(solution)/shard_map/ppermute | solution.py:52
  59.2 8.7 %collective-permute-start.6 = (bf16[224,576]{1,0:T(8,128)(2,1)S(1)}, bf16[224,576]{1,0:T(8,128)(2,1)S(1)}, u32[]{:S(2)}, u32[]{:S(2)}) collective-permute-start(bf16[224,576]{1,0:T(8,128)(2,1)S(1)} %collective-permute-done.4), channel_id=1, source_target_pairs={{0,2},{4,0},{8,4},{12,8},{14,12},{10,14},{6,10},{2,6},{1,3},{5,1},... | collective-permute-start | bytes 774152 | tf_op jit(solution)/shard_map/ppermute | solution.py:53
  66.3 7.8 %collective-permute-start.7 = (bf16[224,576]{1,0:T(8,128)(2,1)S(1)}, bf16[224,576]{1,0:T(8,128)(2,1)S(1)}, u32[]{:S(2)}, u32[]{:S(2)}) collective-permute-start(bf16[224,576]{1,0:T(8,128)(2,1)S(1)} %collective-permute-done.5), channel_id=1, source_target_pairs={{0,4},{4,8},{8,12},{12,14},{14,10},{10,6},{6,2},{2,0},{1,5},{5,9},... | collective-permute-start | bytes 774152 | tf_op jit(solution)/shard_map/ppermute | solution.py:52
  67.9 7.8 %collective-permute-start.8 = (bf16[224,576]{1,0:T(8,128)(2,1)S(1)}, bf16[224,576]{1,0:T(8,128)(2,1)S(1)}, u32[]{:S(2)}, u32[]{:S(2)}) collective-permute-start(bf16[224,576]{1,0:T(8,128)(2,1)S(1)} %collective-permute-done.6), channel_id=1, source_target_pairs={{0,2},{4,0},{8,4},{12,8},{14,12},{10,14},{6,10},{2,6},{1,3},{5,1},... | collective-permute-start | bytes 774152 | tf_op jit(solution)/shard_map/ppermute | solution.py:53
  74.2 6.9 %collective-permute-start.9 = (bf16[224,576]{1,0:T(8,128)(2,1)S(1)}, bf16[224,576]{1,0:T(8,128)(2,1)S(1)}, u32[]{:S(2)}, u32[]{:S(2)}) collective-permute-start(bf16[224,576]{1,0:T(8,128)(2,1)S(1)} %collective-permute-done.7), channel_id=1, source_target_pairs={{0,4},{4,8},{8,12},{12,14},{14,10},{10,6},{6,2},{2,0},{1,5},{5,9},... | collective-permute-start | bytes 774152 | tf_op jit(solution)/shard_map/ppermute | solution.py:52
  75.7 6.9 %collective-permute-start.10 = (bf16[224,576]{1,0:T(8,128)(2,1)S(1)}, bf16[224,576]{1,0:T(8,128)(2,1)S(1)}, u32[]{:S(2)}, u32[]{:S(2)}) collective-permute-start(bf16[224,576]{1,0:T(8,128)(2,1)S(1)} %collective-permute-done.8), channel_id=1, source_target_pairs={{0,2},{4,0},{8,4},{12,8},{14,12},{10,14},{6,10},{2,6},{1,3},{5,1},... | collective-permute-start | bytes 774152 | tf_op jit(solution)/shard_map/ppermute | solution.py:53
  77.7 28.5 %collective-permute-start.2 = (bf16[2,128,1792]{2,1,0:T(8,128)(2,1)S(1)}, bf16[2,128,1792]{2,1,0:T(8,128)(2,1)S(1)}, u32[]{:S(2)}, u32[]{:S(2)}) collective-permute-start(bf16[2,128,1792]{2,1,0:T(8,128)(2,1)S(1)} %collective-permute-done.1), channel_id=1, source_target_pairs={{0,1},{1,0},{2,3},{3,2},{4,5},{5,4},{6,7},{7,6},{8,9},{9,8},{10,11... | collective-permute-start | bytes 2752520 | tf_op jit(solution)/shard_map/ppermute | solution.py:108
  81.1 7.5 %collective-permute-start.11 = (bf16[224,576]{1,0:T(8,128)(2,1)S(1)}, bf16[224,576]{1,0:T(8,128)(2,1)S(1)}, u32[]{:S(2)}, u32[]{:S(2)}) collective-permute-start(bf16[224,576]{1,0:T(8,128)(2,1)S(1)} %collective-permute-done.9), channel_id=1, source_target_pairs={{0,4},{4,8},{8,12},{12,14},{14,10},{10,6},{6,2},{2,0},{1,5},{5,9},... | collective-permute-start | bytes 774152 | tf_op jit(solution)/shard_map/ppermute | solution.py:52
  82.6 7.5 %collective-permute-start.12 = (bf16[224,576]{1,0:T(8,128)(2,1)S(1)}, bf16[224,576]{1,0:T(8,128)(2,1)S(1)}, u32[]{:S(2)}, u32[]{:S(2)}) collective-permute-start(bf16[224,576]{1,0:T(8,128)(2,1)S(1)} %collective-permute-done.10), channel_id=1, source_target_pairs={{0,2},{4,0},{8,4},{12,8},{14,12},{10,14},{6,10},{2,6},{1,3},{5,1},... | collective-permute-start | bytes 774152 | tf_op jit(solution)/shard_map/ppermute | solution.py:53
  88.6 8.7 %collective-permute-start.13 = (bf16[224,576]{1,0:T(8,128)(2,1)S(1)}, bf16[224,576]{1,0:T(8,128)(2,1)S(1)}, u32[]{:S(2)}, u32[]{:S(2)}) collective-permute-start(bf16[224,576]{1,0:T(8,128)(2,1)S(1)} %collective-permute-done.11), channel_id=1, source_target_pairs={{0,4},{4,8},{8,12},{12,14},{14,10},{10,6},{6,2},{2,0},{1,5},{5,9},... | collective-permute-start | bytes 774152 | tf_op jit(solution)/shard_map/ppermute | solution.py:52
  90.1 8.6 %collective-permute-start.14 = (bf16[224,576]{1,0:T(8,128)(2,1)S(1)}, bf16[224,576]{1,0:T(8,128)(2,1)S(1)}, u32[]{:S(2)}, u32[]{:S(2)}) collective-permute-start(bf16[224,576]{1,0:T(8,128)(2,1)S(1)} %collective-permute-done.12), channel_id=1, source_target_pairs={{0,2},{4,0},{8,4},{12,8},{14,12},{10,14},{6,10},{2,6},{1,3},{5,1},... | collective-permute-start | bytes 774152 | tf_op jit(solution)/shard_map/ppermute | solution.py:53
  97.3 6.6 %collective-permute-start.15 = (bf16[224,576]{1,0:T(8,128)(2,1)S(1)}, bf16[224,576]{1,0:T(8,128)(2,1)S(1)}, u32[]{:S(2)}, u32[]{:S(2)}) collective-permute-start(bf16[224,576]{1,0:T(8,128)(2,1)S(1)} %collective-permute-done.13), channel_id=1, source_target_pairs={{0,4},{4,8},{8,12},{12,14},{14,10},{10,6},{6,2},{2,0},{1,5},{5,9},... | collective-permute-start | bytes 774152 | tf_op jit(solution)/shard_map/ppermute | solution.py:52
  98.8 6.6 %collective-permute-start.16 = (bf16[224,576]{1,0:T(8,128)(2,1)S(1)}, bf16[224,576]{1,0:T(8,128)(2,1)S(1)}, u32[]{:S(2)}, u32[]{:S(2)}) collective-permute-start(bf16[224,576]{1,0:T(8,128)(2,1)S(1)} %collective-permute-done.14), channel_id=1, source_target_pairs={{0,2},{4,0},{8,4},{12,8},{14,12},{10,14},{6,10},{2,6},{1,3},{5,1},... | collective-permute-start | bytes 774152 | tf_op jit(solution)/shard_map/ppermute | solution.py:53
  115.6 6.8 %collective-permute-start.17 = (bf16[2,128,576]{1,0,2:T(2,128)(2,1)S(1)}, bf16[2,128,576]{1,0,2:T(2,128)(2,1)S(1)}, u32[]{:S(2)}, u32[]{:S(2)}) collective-permute-start(bf16[2,128,576]{1,0,2:T(2,128)(2,1)S(1)} %fusion.24), channel_id=1, source_target_pairs={{0,16},{16,0},{1,17},{17,1},{2,18},{18,2},{3,19},{19,3},{4,20},{20... | collective-permute-start | bytes 884744 | tf_op jit(solution)/shard_map/ppermute | solution.py:140
  123.6 12.0 %collective-permute-start.18 = (bf16[2,128,256]{1,0,2:T(2,128)(2,1)S(1)}, bf16[2,128,256]{1,0,2:T(2,128)(2,1)S(1)}, u32[]{:S(2)}, u32[]{:S(2)}) collective-permute-start(bf16[2,128,256]{1,0,2:T(2,128)(2,1)S(1)} %pad_maximum_fusion.5), channel_id=1, source_target_pairs={{0,2},{2,4},{4,6},{6,8},{8,10},{10,12},{12,14},{14,0},{1,3},{3,5},... | collective-permute-start | bytes 393224 | tf_op jit(solution)/shard_map/ppermute | solution.py:151
  124.3 12.9 %collective-permute-start.19 = (bf16[2,128,256]{1,0,2:T(2,128)(2,1)S(1)}, bf16[2,128,256]{1,0,2:T(2,128)(2,1)S(1)}, u32[]{:S(2)}, u32[]{:S(2)}) collective-permute-start(bf16[2,128,256]{1,0,2:T(2,128)(2,1)S(1)} %pad_maximum_fusion.5), channel_id=1, source_target_pairs={{0,4},{2,6},{4,8},{6,10},{8,12},{10,14},{12,0},{14,2},{1,5},{3,7},... | collective-permute-start | bytes 393224 | tf_op jit(solution)/shard_map/ppermute | solution.py:151
  126.2 13.5 %collective-permute-start.20 = (bf16[2,128,256]{1,0,2:T(2,128)(2,1)S(1)}, bf16[2,128,256]{1,0,2:T(2,128)(2,1)S(1)}, u32[]{:S(2)}, u32[]{:S(2)}) collective-permute-start(bf16[2,128,256]{1,0,2:T(2,128)(2,1)S(1)} %pad_maximum_fusion.5), channel_id=1, source_target_pairs={{0,6},{2,8},{4,10},{6,12},{8,14},{10,0},{12,2},{14,4},{1,7},{3,9},... | collective-permute-start | bytes 393224 | tf_op jit(solution)/shard_map/ppermute | solution.py:151
  129.3 11.3 %collective-permute-start.21 = (bf16[2,128,256]{1,0,2:T(2,128)(2,1)S(1)}, bf16[2,128,256]{1,0,2:T(2,128)(2,1)S(1)}, u32[]{:S(2)}, u32[]{:S(2)}) collective-permute-start(bf16[2,128,256]{1,0,2:T(2,128)(2,1)S(1)} %pad_maximum_fusion.5), channel_id=1, source_target_pairs={{0,8},{2,10},{4,12},{6,14},{8,0},{10,2},{12,4},{14,6},{1,9},{3,11}... | collective-permute-start | bytes 393224 | tf_op jit(solution)/shard_map/ppermute | solution.py:151
  130.6 10.1 %collective-permute-start.22 = (bf16[2,128,256]{1,0,2:T(2,128)(2,1)S(1)}, bf16[2,128,256]{1,0,2:T(2,128)(2,1)S(1)}, u32[]{:S(2)}, u32[]{:S(2)}) collective-permute-start(bf16[2,128,256]{1,0,2:T(2,128)(2,1)S(1)} %pad_maximum_fusion.5), channel_id=1, source_target_pairs={{0,10},{2,12},{4,14},{6,0},{8,2},{10,4},{12,6},{14,8},{1,11},{3,13... | collective-permute-start | bytes 393224 | tf_op jit(solution)/shard_map/ppermute | solution.py:151
  135.7 6.4 %collective-permute-start.23 = (bf16[2,128,256]{1,0,2:T(2,128)(2,1)S(1)}, bf16[2,128,256]{1,0,2:T(2,128)(2,1)S(1)}, u32[]{:S(2)}, u32[]{:S(2)}) collective-permute-start(bf16[2,128,256]{1,0,2:T(2,128)(2,1)S(1)} %pad_maximum_fusion.5), channel_id=1, source_target_pairs={{0,12},{2,14},{4,0},{6,2},{8,4},{10,6},{12,8},{14,10},{1,13},{3,15... | collective-permute-start | bytes 393224 | tf_op jit(solution)/shard_map/ppermute | solution.py:151
  137.2 5.2 %collective-permute-start.24 = (bf16[2,128,256]{1,0,2:T(2,128)(2,1)S(1)}, bf16[2,128,256]{1,0,2:T(2,128)(2,1)S(1)}, u32[]{:S(2)}, u32[]{:S(2)}) collective-permute-start(bf16[2,128,256]{1,0,2:T(2,128)(2,1)S(1)} %pad_maximum_fusion.5), channel_id=1, source_target_pairs={{0,14},{2,0},{4,2},{6,4},{8,6},{10,8},{12,10},{14,12},{1,15},{3,1}... | collective-permute-start | bytes 393224 | tf_op jit(solution)/shard_map/ppermute | solution.py:151
  (8 other events, 23.4 us)

commit v6 on v3

--- a/solution.py
+++ b/solution.py
@@ -89,17 +89,24 @@
     rotary_w = jnp.concatenate([w_query, key_weight], axis=1)
     rotary_b = jnp.concatenate([b_query, b_key], axis=0)
     first = group == 0
-    panel = jnp.where(
-        first,
-        jnp.concatenate([rotary_w[:, :split], value_weight[:, :value_split]], axis=1),
-        jnp.concatenate([rotary_w[:, split:], value_weight[:, value_split:]], axis=1),
-    )
-    panel_bias = jnp.where(
-        first,
-        jnp.concatenate([rotary_b[:split], value_bias[:value_split]]),
-        jnp.concatenate([rotary_b[split:], value_bias[value_split:]]),
-    )
-    full_panel = gather_rows(panel, row_count, here)
+    late_start = group * split + split - HEAD_SIZE
+    early_panel = jnp.concatenate(
+        [
+            lax.dynamic_slice_in_dim(rotary_w, late_start, HEAD_SIZE, 1),
+            lax.dynamic_slice_in_dim(value_weight, group * value_split, value_split, 1),
+        ],
+        axis=1,
+    )
+    early_bias = jnp.concatenate(
+        [
+            lax.dynamic_slice_in_dim(rotary_b, late_start, HEAD_SIZE, 0),
+            lax.dynamic_slice_in_dim(value_bias, group * value_split, value_split, 0),
+        ]
+    )
+    late_panel = lax.dynamic_slice_in_dim(rotary_w, group * split, split - HEAD_SIZE, 1)
+    late_bias = lax.dynamic_slice_in_dim(rotary_b, group * split, split - HEAD_SIZE, 0)
+    early_full = gather_rows(early_panel, row_count, here)
+    late_full = gather_rows(late_panel, row_count, here)
 
     other_half = lax.ppermute(tokens, "col", SWAP)
     partner_half = lax.ppermute(tokens, "groups", SWAP)
@@ -124,24 +131,32 @@
     )
     token_positions = (here * length + jnp.arange(length, dtype=jnp.int32)).astype(jnp.float32)
 
-    summed = jnp.dot(normed, full_panel, preferred_element_type=jnp.float32) + panel_bias
-    summed = summed.reshape(2 * passages, length, split + value_split)
-    turned = apply_rotation(
-        summed[..., :split].reshape(2 * passages, length, split // HEAD_SIZE, HEAD_SIZE),
-        token_positions,
-    ).astype(jnp.bfloat16)
-    result = jnp.concatenate(
-        [turned.reshape(2 * passages, length, split), summed[..., split:].astype(jnp.bfloat16)],
-        axis=-1,
-    )
-    mine = result[:passages]
-    returned = lax.ppermute(result[passages:], "groups", SWAP)
-    low = jnp.where(first, mine, returned)
-    high = jnp.where(first, returned, mine)
-    rotary_rows = jnp.concatenate([low[..., :split], high[..., :split]], axis=-1)
-    query_rows = rotary_rows[..., : heads_here * HEAD_SIZE]
-    key = rotary_rows[..., heads_here * HEAD_SIZE :]
-    value_rows = jnp.concatenate([low[..., split:], high[..., split:]], axis=-1)
+    def project(full, bias, rotary_heads):
+        summed = jnp.dot(normed, full, preferred_element_type=jnp.float32) + bias
+        summed = summed.reshape(2 * passages, length, -1)
+        rotary_width = rotary_heads * HEAD_SIZE
+        turned = apply_rotation(
+            summed[..., :rotary_width].reshape(2 * passages, length, rotary_heads, HEAD_SIZE),
+            token_positions,
+        ).astype(jnp.bfloat16)
+        result = jnp.concatenate(
+            [
+                turned.reshape(2 * passages, length, rotary_width),
+                summed[..., rotary_width:].astype(jnp.bfloat16),
+            ],
+            axis=-1,
+        )
+        mine = result[:passages]
+        returned = lax.ppermute(result[passages:], "groups", SWAP)
+        return jnp.where(first, mine, returned), jnp.where(first, returned, mine)
+
+    early_low, early_high = project(early_full, early_bias, 1)
+    key = early_high[..., :HEAD_SIZE]
+    value_rows = jnp.concatenate(
+        [early_low[..., HEAD_SIZE:], early_high[..., HEAD_SIZE:]], axis=-1
+    )
+    late_low, late_high = project(late_full, late_bias, split // HEAD_SIZE - 1)
+    query_rows = jnp.concatenate([late_low, early_low[..., :HEAD_SIZE], late_high], axis=-1)
 
     pairs = jnp.concatenate([key, value_rows], axis=-1)
     if row_count <= 8:

time: 123 us -> 170 us (1.38)
  starting transfers between devices: 30.3 us -> 51.3 us
  local copies, waits for them, and re-layouts: 32.7 us -> 52.5 us
  matrix products: 6.82 us -> 11.7 us
    ppermute x7 -> x14, starting transfers between devices: 3.15 us -> 24.1 us  [gather_rows(): behind = lax.ppermute(behind, 'row', backward)]
    unnamed x41 -> x71, local copies, waits for them, and re-layouts: 9.93 us -> 20.1 us
    ppermute x7 -> x14, waiting for transfers between devices: 0.02 us -> 9.57 us  [gather_rows(): behind = lax.ppermute(behind, 'row', backward)]
    ppermute x7 -> x14, waiting for transfers between devices: 23.9 us -> 18.7 us  [gather_rows(): ahead = lax.ppermute(ahead, 'row', forward)]
    dot_general x1 -> x2, matrix products: 2.38 us -> 6.37 us  [project(): summed = jnp.dot(normed, full, preferred_element_type=jnp.float32) + bias]
    ppermute x7, local copies, waits for them, and re-layouts: 0.79 us -> 4.38 us  [shards(): lax.ppermute(pairs, 'row', [(i, (i + k) % row_count) for i in range(row_c...]
    ppermute x1 -> x2, waiting for transfers between devices: 6.37 us -> 2.99 us  [project(): returned = lax.ppermute(result[passages:], 'groups', SWAP)]
    concatenate x1 -> x2, other arithmetic: 2.75 us -> 4.82 us  [gather_rows(): jnp.concatenate([jnp.stack(ahead_parts)[ahead_pick], jnp.stack(behind_par...]
  transfers between devices with their start and end apart: 25 -> 40, of which waited for: 11 -> 16; matrix products, arithmetic and copies ran while one was open for 29% -> 29% of each run, Pallas kernels for 0% -> 0%
where the time goes in v6:
time: 170 us; the launch traced here: 167 us
  local copies, waits for them, and re-layouts  52.5 us (31%)
  starting transfers between devices  51.3 us (30%)
  waiting for transfers between devices  33.6 us (20%)
  other arithmetic  16.5 us (10%)
  matrix products  11.7 us (7%)
    ppermute x14, starting transfers between devices, gather_rows(): behind = lax.ppermute(behind, 'row', backward)  24.1 us
    unnamed x71, local copies, waits for them, and re-layouts  20.1 us
    ppermute x14, waiting for transfers between devices, gather_rows(): ahead = lax.ppermute(ahead, 'row', forward)  18.7 us
    ppermute x7, starting transfers between devices, shards(): lax.ppermute(pairs, 'row', [(i, (i + k) % row_count) for i in range(row_c...  11.5 us
    ppermute x14, starting transfers between devices, gather_rows(): ahead = lax.ppermute(ahead, 'row', forward)  10.5 us
    ppermute x14, waiting for transfers between devices, gather_rows(): behind = lax.ppermute(behind, 'row', backward)  9.57 us
    dot_general x2, matrix products, project(): summed = jnp.dot(normed, full, preferred_element_type=jnp.float32) + bias  6.37 us
    gather x2, local copies, waits for them, and re-layouts, gather_rows(): jnp.stack(behind_parts)[behind_pick]  4.99 us
  transfers between devices with their start and end apart: 40, of which 16 were waited for; matrix products, arithmetic and copies ran while one was open for 29% of the time, Pallas kernels for 0%

profile of v6, /device:TPU:0, one launch (start us, length us, event | category | flops | bytes accessed | tf_op | source)
XLA Modules:
  0.0 166.5 jit_solution(11934528081434761401)
XLA Ops:
  0.0 3.0 %collective-permute-start.1 = (bf16[2,128,1792]{2,1,0:T(8,128)(2,1)}, bf16[2,128,1792]{2,1,0:T(8,128)(2,1)}, u32[]{:S(2)}, u32[]{:S(2)}) collective-permute-start(bf16[2,128,1792]{2,1,0:T(8,128)(2,1)} %param.12), channel_id=1, source_target_pairs={{0,16},{16,0},{1,17},{17,1},{2,18},{18,2},{3,19},{19,3},{4,20},{20... | collective-permute-start | bytes 2752520 | tf_op jit(solution)/shard_map/ppermute | solution.py:112
  18.4 2.0 %collective-permute-done.10 = bf16[224,192]{1,0:T(8,128)(2,1)S(1)} collective-permute-done((bf16[224,192]{1,0:T(8,128)(2,1)}, bf16[224,192]{1,0:T(8,128)(2,1)S(1)}, u32[]{:S(2)}, u32[]{:S(2)}) %collective-permute-start.10) | collective-permute-done | bytes 86048 | tf_op jit(solution)/shard_map/ppermute | solution.py:48
  28.7 3.6 %collective-permute-done.5 = bf16[224,192]{1,0:T(8,128)(2,1)S(1)} collective-permute-done((bf16[224,192]{1,0:T(8,128)(2,1)S(1)}, bf16[224,192]{1,0:T(8,128)(2,1)S(1)}, u32[]{:S(2)}, u32[]{:S(2)}) %collective-permute-start.5) | collective-permute-done | bytes 86048 | tf_op jit(solution)/shard_map/ppermute | solution.py:47
  34.6 2.7 %collective-permute-done.12 = bf16[224,192]{1,0:T(8,128)(2,1)S(1)} collective-permute-done((bf16[224,192]{1,0:T(8,128)(2,1)S(1)}, bf16[224,192]{1,0:T(8,128)(2,1)S(1)}, u32[]{:S(2)}, u32[]{:S(2)}) %collective-permute-start.12) | collective-permute-done | bytes 86048 | tf_op jit(solution)/shard_map/ppermute | solution.py:48
  44.9 4.3 %collective-permute-done.7 = bf16[224,192]{1,0:T(8,128)(2,1)S(1)} collective-permute-done((bf16[224,192]{1,0:T(8,128)(2,1)S(1)}, bf16[224,192]{1,0:T(8,128)(2,1)S(1)}, u32[]{:S(2)}, u32[]{:S(2)}) %collective-permute-start.7) | collective-permute-done | bytes 86048 | tf_op jit(solution)/shard_map/ppermute | solution.py:47
  49.2 2.0 %collective-permute-start.14 = (bf16[224,192]{1,0:T(8,128)(2,1)S(1)}, bf16[224,192]{1,0:T(8,128)(2,1)S(1)}, u32[]{:S(2)}, u32[]{:S(2)}) collective-permute-start(bf16[224,192]{1,0:T(8,128)(2,1)S(1)} %collective-permute-done.13), channel_id=1, source_target_pairs={{0,2},{4,0},{8,4},{12,8},{14,12},{10,14},{6,10},{2,6},{1,3},{5,1},... | collective-permute-start | bytes 258056 | tf_op jit(solution)/shard_map/ppermute | solution.py:48
  51.9 2.1 %collective-permute-done.14 = bf16[224,192]{1,0:T(8,128)(2,1)S(1)} collective-permute-done((bf16[224,192]{1,0:T(8,128)(2,1)S(1)}, bf16[224,192]{1,0:T(8,128)(2,1)S(1)}, u32[]{:S(2)}, u32[]{:S(2)}) %collective-permute-start.14) | collective-permute-done | bytes 86048 | tf_op jit(solution)/shard_map/ppermute | solution.py:48
  54.5 4.3 %collective-permute-done.8 = bf16[224,192]{1,0:T(8,128)(2,1)S(1)} collective-permute-done((bf16[224,192]{1,0:T(8,128)(2,1)S(1)}, bf16[224,192]{1,0:T(8,128)(2,1)S(1)}, u32[]{:S(2)}, u32[]{:S(2)}) %collective-permute-start.8) | collective-permute-done | bytes 86048 | tf_op jit(solution)/shard_map/ppermute | solution.py:47
  58.8 2.5 %collective-permute-start.15 = (bf16[224,192]{1,0:T(8,128)(2,1)S(1)}, bf16[224,192]{1,0:T(8,128)(2,1)S(1)}, u32[]{:S(2)}, u32[]{:S(2)}) collective-permute-start(bf16[224,192]{1,0:T(8,128)(2,1)S(1)} %collective-permute-done.14), channel_id=1, source_target_pairs={{0,2},{4,0},{8,4},{12,8},{14,12},{10,14},{6,10},{2,6},{1,3},{5,1},... | collective-permute-start | bytes 258056 | tf_op jit(solution)/shard_map/ppermute | solution.py:48
  62.0 2.8 %collective-permute-done.15 = bf16[224,192]{1,0:T(8,128)(2,1)S(1)} collective-permute-done((bf16[224,192]{1,0:T(8,128)(2,1)S(1)}, bf16[224,192]{1,0:T(8,128)(2,1)S(1)}, u32[]{:S(2)}, u32[]{:S(2)}) %collective-permute-start.15) | collective-permute-done | bytes 86048 | tf_op jit(solution)/shard_map/ppermute | solution.py:48
  64.8 2.7 %collective-permute-start.16 = (bf16[224,192]{1,0:T(8,128)(2,1)S(1)}, bf16[224,192]{1,0:T(8,128)(2,1)S(1)}, u32[]{:S(2)}, u32[]{:S(2)}) collective-permute-start(bf16[224,192]{1,0:T(8,128)(2,1)S(1)} %collective-permute-done.15), channel_id=1, source_target_pairs={{0,2},{4,0},{8,4},{12,8},{14,12},{10,14},{6,10},{2,6},{1,3},{5,1},... | collective-permute-start | bytes 258056 | tf_op jit(solution)/shard_map/ppermute | solution.py:48
  70.2 2.5 %collective-permute-start.35 = (bf16[224,384]{1,0:T(8,128)(2,1)}, bf16[224,384]{1,0:T(8,128)(2,1)}, u32[]{:S(2)}, u32[]{:S(2)}) collective-permute-start(bf16[224,384]{1,0:T(8,128)(2,1)} %collective-permute-done.34), channel_id=1, source_target_pairs={{0,2},{4,0},{8,4},{12,8},{14,12},{10,14},{6,10},{2,6},{1,3},{5,1},... | collective-permute-start | bytes 516104 | tf_op jit(solution)/shard_map/ppermute | solution.py:48
  74.3 1.8 %gather_fusion = bf16[8,224,192]{2,1,0:T(8,128)(2,1)S(1)} fusion(bf16[8,224,192]{2,1,0:T(8,128)(2,1)} %bitcast_dynamic-update-slice_fusion.24, s32[1024]{0:T(1024)S(1)} %get-tuple-element.38), kind=kCustom, calls=%fused_computation | custom fusion | bytes 1376288 | tf_op jit(solution)/shard_map/gather | solution.py:56
  76.1 1.8 %gather_fusion.1 = bf16[8,224,192]{2,1,0:T(8,128)(2,1)S(1)} fusion(bf16[8,224,192]{2,1,0:T(8,128)(2,1)} %copy-done.6, s32[1024]{0:T(1024)S(1)} %get-tuple-element.37), kind=kCustom, calls=%fused_computation.1 | custom fusion | bytes 1376288 | tf_op jit(solution)/shard_map/gather | solution.py:56
  77.9 1.7 pad_maximum_fusion.2
  79.6 2.4 %collective-permute-start.36 = (bf16[224,384]{1,0:T(8,128)(2,1)}, bf16[224,384]{1,0:T(8,128)(2,1)S(1)}, u32[]{:S(2)}, u32[]{:S(2)}) collective-permute-start(bf16[224,384]{1,0:T(8,128)(2,1)} %collective-permute-done.35), channel_id=1, source_target_pairs={{0,2},{4,0},{8,4},{12,8},{14,12},{10,14},{6,10},{2,6},{1,3},{5,1},... | collective-permute-start | bytes 516104 | tf_op jit(solution)/shard_map/ppermute | solution.py:48
  85.5 2.1 %collective-permute-start.37 = (bf16[224,384]{1,0:T(8,128)(2,1)S(1)}, bf16[224,384]{1,0:T(8,128)(2,1)}, u32[]{:S(2)}, u32[]{:S(2)}) collective-permute-start(bf16[224,384]{1,0:T(8,128)(2,1)S(1)} %collective-permute-done.36), channel_id=1, source_target_pairs={{0,2},{4,0},{8,4},{12,8},{14,12},{10,14},{6,10},{2,6},{1,3},{5,1},... | collective-permute-start | bytes 516104 | tf_op jit(solution)/shard_map/ppermute | solution.py:48
  88.4 1.9 %maximum_select_fusion = bf16[2,128,3584]{2,1,0:T(8,128)(2,1)S(1)} fusion(bf16[2,128,1792]{2,1,0:T(8,128)(2,1)} %collective-permute-done, bf16[2,128,1792]{2,1,0:T(8,128)(2,1)S(1)} %copy-done.7, pred[]{:T(512)S(6)} %eq.16), kind=kLoop, calls=%fused_computation.16 | loop fusion | flops 8257536 | bytes 3670017 | tf_op jit(solution)/shard_map/jit(_where)/select_n | solution.py:114
  91.6 2.0 %collective-permute-start.38 = (bf16[224,384]{1,0:T(8,128)(2,1)}, bf16[224,384]{1,0:T(8,128)(2,1)}, u32[]{:S(2)}, u32[]{:S(2)}) collective-permute-start(bf16[224,384]{1,0:T(8,128)(2,1)} %collective-permute-done.37), channel_id=1, source_target_pairs={{0,2},{4,0},{8,4},{12,8},{14,12},{10,14},{6,10},{2,6},{1,3},{5,1},... | collective-permute-start | bytes 516104 | tf_op jit(solution)/shard_map/ppermute | solution.py:48
  94.7 2.7 %collective-permute-done.31 = bf16[224,384]{1,0:T(8,128)(2,1)S(1)} collective-permute-done((bf16[224,384]{1,0:T(8,128)(2,1)S(1)}, bf16[224,384]{1,0:T(8,128)(2,1)S(1)}, u32[]{:S(2)}, u32[]{:S(2)}) %collective-permute-start.31) | collective-permute-done | bytes 172064 | tf_op jit(solution)/shard_map/ppermute | solution.py:47
  98.1 2.2 %gather_fusion.5 = bf16[8,224,384]{2,1,0:T(8,128)(2,1)S(1)} fusion(bf16[8,224,384]{2,1,0:T(8,128)(2,1)} %bitcast_dynamic-update-slice_fusion.8, s32[1024]{0:T(1024)S(1)} %get-tuple-element.38), kind=kCustom, calls=%fused_computation.5 | custom fusion | bytes 2752544 | tf_op jit(solution)/shard_map/gather | solution.py:56
  101.9 3.2 %gather_fusion.6 = bf16[8,224,384]{2,1,0:T(8,128)(2,1)} fusion(bf16[8,224,384]{2,1,0:T(8,128)(2,1)} %bitcast_dynamic-update-slice_fusion, s32[1024]{0:T(1024)S(1)} %get-tuple-element.37), kind=kCustom, calls=%fused_computation.6 | custom fusion | bytes 2752544 | tf_op jit(solution)/shard_map/gather | solution.py:56
  105.1 3.2 %pad_maximum_fusion.1 = bf16[8,448,384]{2,1,0:T(8,128)(2,1)} fusion(bf16[8,224,384]{2,1,0:T(8,128)(2,1)} %gather_fusion.6, bf16[8,224,384]{2,1,0:T(8,128)(2,1)S(1)} %gather_fusion.5), kind=kLoop, calls=%fused_computation.15 | loop fusion | flops 5505024 | bytes 5505024 | tf_op jit(solution)/shard_map/concatenate | solution.py:55
  108.3 2.6 %maximum_select_fusion.1 = bf16[2,128,3584]{2,1,0:T(8,128)(2,1)S(1)} fusion(bf16[2,128,1792]{2,1,0:T(8,128)(2,1)} %collective-permute-done.2, bf16[2,128,1792]{2,1,0:T(8,128)(2,1)} %collective-permute-done.1, pred[]{:T(512)S(6)} %eq.16), kind=kLoop, calls=%fused_computation.17 | loop fusion | flops 8257536 | bytes 3670017 | tf_op jit(solution)/shard_map/jit(_where)/select_n | solution.py:119
  112.9 1.8 %copy-done.1 = bf16[4,128,3584]{2,1,0:T(8,128)(2,1)} copy-done((bf16[4,128,3584]{2,1,0:T(8,128)(2,1)}, bf16[4,128,3584]{2,1,0:T(8,128)(2,1)S(1)}, u32[]{:S(2)}) %copy-start.1) | copy-done | bytes 3670040
  118.8 5.0 %convolution_add_fusion = f32[512,384]{1,0:T(8,128)} fusion(bf16[512,3584]{1,0:T(8,128)(2,1)} %bitcast.171, bf16[3584,384]{1,0:T(8,128)(2,1)S(1)} %bitcast.179, f32[384]{0:T(512)S(1)} %dynamic_slice.39), kind=kOutput, calls=%fused_computation.34 | convolution fusion | flops 1409482752 | bytes 7210496 | tf_op jit(solution)/shard_map/dot_general | solution.py:135
  129.4 3.0 %collective-permute-done.17 = bf16[2,128,192]{1,0,2:T(2,128)(2,1)S(1)} collective-permute-done((bf16[2,128,192]{1,0,2:T(2,128)(2,1)S(1)}, bf16[2,128,192]{1,0,2:T(2,128)(2,1)S(1)}, u32[]{:S(2)}, u32[]{:S(2)}) %collective-permute-start.17) | collective-permute-done | bytes 98336 | tf_op jit(solution)/shard_map/ppermute | solution.py:150
  133.0 1.8 %collective-permute-start.18 = (bf16[2,128,256]{1,0,2:T(2,128)(2,1)S(1)}, bf16[2,128,256]{1,0,2:T(2,128)(2,1)}, u32[]{:S(2)}, u32[]{:S(2)}) collective-permute-start(bf16[2,128,256]{1,0,2:T(2,128)(2,1)S(1)} %pad_maximum_fusion.4), channel_id=1, source_target_pairs={{0,2},{2,4},{4,6},{6,8},{8,10},{10,12},{12,14},{14,0},{1,3},{3,5},... | collective-permute-start | bytes 393224 | tf_op jit(solution)/shard_map/ppermute | solution.py:164
  134.8 1.6 collective-permute-start.19
  136.4 2.2 %collective-permute-start.21 = (bf16[2,128,256]{1,0,2:T(2,128)(2,1)S(1)}, bf16[2,128,256]{1,0,2:T(2,128)(2,1)}, u32[]{:S(2)}, u32[]{:S(2)}) collective-permute-start(bf16[2,128,256]{1,0,2:T(2,128)(2,1)S(1)} %pad_maximum_fusion.4), channel_id=1, source_target_pairs={{0,8},{2,10},{4,12},{6,14},{8,0},{10,2},{12,4},{14,6},{1,9},{3,11}... | collective-permute-start | bytes 393224 | tf_op jit(solution)/shard_map/ppermute | solution.py:164
  140.9 1.6 copy.69
  142.5 2.6 %collective-permute-start.23 = (bf16[2,128,256]{1,0,2:T(2,128)(2,1)S(1)}, bf16[2,128,256]{1,0,2:T(2,128)(2,1)S(1)}, u32[]{:S(2)}, u32[]{:S(2)}) collective-permute-start(bf16[2,128,256]{1,0,2:T(2,128)(2,1)S(1)} %pad_maximum_fusion.4), channel_id=1, source_target_pairs={{0,12},{2,14},{4,0},{6,2},{8,4},{10,6},{12,8},{14,10},{1,13},{3,15... | collective-permute-start | bytes 393224 | tf_op jit(solution)/shard_map/ppermute | solution.py:164
  (226 shorter events, 83.8 us)
Async XLA Ops:
  0.0 88.3 %collective-permute-start.1 = (bf16[2,128,1792]{2,1,0:T(8,128)(2,1)}, bf16[2,128,1792]{2,1,0:T(8,128)(2,1)}, u32[]{:S(2)}, u32[]{:S(2)}) collective-permute-start(bf16[2,128,1792]{2,1,0:T(8,128)(2,1)} %param.12), channel_id=1, source_target_pairs={{0,16},{16,0},{1,17},{17,1},{2,18},{18,2},{3,19},{19,3},{4,20},{20... | collective-permute-start | bytes 2752520 | tf_op jit(solution)/shard_map/ppermute | solution.py:112
  3.0 85.5 %collective-permute-start = (bf16[2,128,1792]{2,1,0:T(8,128)(2,1)}, bf16[2,128,1792]{2,1,0:T(8,128)(2,1)}, u32[]{:S(2)}, u32[]{:S(2)}) collective-permute-start(bf16[2,128,1792]{2,1,0:T(8,128)(2,1)} %param.12), channel_id=1, source_target_pairs={{0,1},{1,0},{2,3},{3,2},{4,5},{5,4},{6,7},{7,6},{8,9},{9,8},{10,11... | collective-permute-start | bytes 2752520 | tf_op jit(solution)/shard_map/ppermute | solution.py:111
  6.0 15.9 %collective-permute-start.25 = (bf16[224,384]{1,0:T(8,128)(2,1)S(1)}, bf16[224,384]{1,0:T(8,128)(2,1)}, u32[]{:S(2)}, u32[]{:S(2)}) collective-permute-start(bf16[224,384]{1,0:T(8,128)(2,1)S(1)} %get-tuple-element.8), channel_id=1, source_target_pairs={{0,4},{4,8},{8,12},{12,14},{14,10},{10,6},{6,2},{2,0},{1,5},{5,9},... | collective-permute-start | bytes 516104 | tf_op jit(solution)/shard_map/ppermute | solution.py:47
  7.6 16.5 %collective-permute-start.32 = (bf16[224,384]{1,0:T(8,128)(2,1)S(1)}, bf16[224,384]{1,0:T(8,128)(2,1)S(1)}, u32[]{:S(2)}, u32[]{:S(2)}) collective-permute-start(bf16[224,384]{1,0:T(8,128)(2,1)S(1)} %get-tuple-element.16), channel_id=1, source_target_pairs={{0,2},{4,0},{8,4},{12,8},{14,12},{10,14},{6,10},{2,6},{1,3},{5,1},... | collective-permute-start | bytes 516104 | tf_op jit(solution)/shard_map/ppermute | solution.py:48
  9.0 6.4 %collective-permute-start.3 = (bf16[224,192]{1,0:T(8,128)(2,1)}, bf16[224,192]{1,0:T(8,128)(2,1)}, u32[]{:S(2)}, u32[]{:S(2)}) collective-permute-start(bf16[224,192]{1,0:T(8,128)(2,1)} %get-tuple-element.12), channel_id=1, source_target_pairs={{0,4},{4,8},{8,12},{12,14},{14,10},{10,6},{6,2},{2,0},{1,5},{5,9},... | collective-permute-start | bytes 258056 | tf_op jit(solution)/shard_map/ppermute | solution.py:47
  22.0 5.6 %collective-permute-start.11 = (bf16[224,192]{1,0:T(8,128)(2,1)S(1)}, bf16[224,192]{1,0:T(8,128)(2,1)S(1)}, u32[]{:S(2)}, u32[]{:S(2)}) collective-permute-start(bf16[224,192]{1,0:T(8,128)(2,1)S(1)} %collective-permute-done.10), channel_id=1, source_target_pairs={{0,2},{4,0},{8,4},{12,8},{14,12},{10,14},{6,10},{2,6},{1,3},{5,1},... | collective-permute-start | bytes 258056 | tf_op jit(solution)/shard_map/ppermute | solution.py:48
  24.1 14.3 %collective-permute-start.26 = (bf16[224,384]{1,0:T(8,128)(2,1)}, bf16[224,384]{1,0:T(8,128)(2,1)S(1)}, u32[]{:S(2)}, u32[]{:S(2)}) collective-permute-start(bf16[224,384]{1,0:T(8,128)(2,1)} %collective-permute-done.25), channel_id=1, source_target_pairs={{0,4},{4,8},{8,12},{12,14},{14,10},{10,6},{6,2},{2,0},{1,5},{5,9},... | collective-permute-start | bytes 516104 | tf_op jit(solution)/shard_map/ppermute | solution.py:47
  25.7 14.4 %collective-permute-start.33 = (bf16[224,384]{1,0:T(8,128)(2,1)S(1)}, bf16[224,384]{1,0:T(8,128)(2,1)S(1)}, u32[]{:S(2)}, u32[]{:S(2)}) collective-permute-start(bf16[224,384]{1,0:T(8,128)(2,1)S(1)} %collective-permute-done.32), channel_id=1, source_target_pairs={{0,2},{4,0},{8,4},{12,8},{14,12},{10,14},{6,10},{2,6},{1,3},{5,1},... | collective-permute-start | bytes 516104 | tf_op jit(solution)/shard_map/ppermute | solution.py:48
  38.3 6.1 %collective-permute-start.13 = (bf16[224,192]{1,0:T(8,128)(2,1)S(1)}, bf16[224,192]{1,0:T(8,128)(2,1)S(1)}, u32[]{:S(2)}, u32[]{:S(2)}) collective-permute-start(bf16[224,192]{1,0:T(8,128)(2,1)S(1)} %collective-permute-done.12), channel_id=1, source_target_pairs={{0,2},{4,0},{8,4},{12,8},{14,12},{10,14},{6,10},{2,6},{1,3},{5,1},... | collective-permute-start | bytes 258056 | tf_op jit(solution)/shard_map/ppermute | solution.py:48
  40.1 24.7 %collective-permute-start.27 = (bf16[224,384]{1,0:T(8,128)(2,1)S(1)}, bf16[224,384]{1,0:T(8,128)(2,1)}, u32[]{:S(2)}, u32[]{:S(2)}) collective-permute-start(bf16[224,384]{1,0:T(8,128)(2,1)S(1)} %collective-permute-done.26), channel_id=1, source_target_pairs={{0,4},{4,8},{8,12},{12,14},{14,10},{10,6},{6,2},{2,0},{1,5},{5,9},... | collective-permute-start | bytes 516104 | tf_op jit(solution)/shard_map/ppermute | solution.py:47
  42.2 27.0 %collective-permute-start.34 = (bf16[224,384]{1,0:T(8,128)(2,1)S(1)}, bf16[224,384]{1,0:T(8,128)(2,1)}, u32[]{:S(2)}, u32[]{:S(2)}) collective-permute-start(bf16[224,384]{1,0:T(8,128)(2,1)S(1)} %collective-permute-done.33), channel_id=1, source_target_pairs={{0,2},{4,0},{8,4},{12,8},{14,12},{10,14},{6,10},{2,6},{1,3},{5,1},... | collective-permute-start | bytes 516104 | tf_op jit(solution)/shard_map/ppermute | solution.py:48
  58.8 6.0 %collective-permute-start.15 = (bf16[224,192]{1,0:T(8,128)(2,1)S(1)}, bf16[224,192]{1,0:T(8,128)(2,1)S(1)}, u32[]{:S(2)}, u32[]{:S(2)}) collective-permute-start(bf16[224,192]{1,0:T(8,128)(2,1)S(1)} %collective-permute-done.14), channel_id=1, source_target_pairs={{0,2},{4,0},{8,4},{12,8},{14,12},{10,14},{6,10},{2,6},{1,3},{5,1},... | collective-permute-start | bytes 258056 | tf_op jit(solution)/shard_map/ppermute | solution.py:48
  64.8 5.5 %collective-permute-start.9 = (bf16[224,192]{1,0:T(8,128)(2,1)S(1)}, bf16[224,192]{1,0:T(8,128)(2,1)S(1)}, u32[]{:S(2)}, u32[]{:S(2)}) collective-permute-start(bf16[224,192]{1,0:T(8,128)(2,1)S(1)} %collective-permute-done.8), channel_id=1, source_target_pairs={{0,4},{4,8},{8,12},{12,14},{14,10},{10,6},{6,2},{2,0},{1,5},{5,9},... | collective-permute-start | bytes 258056 | tf_op jit(solution)/shard_map/ppermute | solution.py:47
  64.8 8.6 %collective-permute-start.16 = (bf16[224,192]{1,0:T(8,128)(2,1)S(1)}, bf16[224,192]{1,0:T(8,128)(2,1)S(1)}, u32[]{:S(2)}, u32[]{:S(2)}) collective-permute-start(bf16[224,192]{1,0:T(8,128)(2,1)S(1)} %collective-permute-done.15), channel_id=1, source_target_pairs={{0,2},{4,0},{8,4},{12,8},{14,12},{10,14},{6,10},{2,6},{1,3},{5,1},... | collective-permute-start | bytes 258056 | tf_op jit(solution)/shard_map/ppermute | solution.py:48
  69.2 10.4 %collective-permute-start.28 = (bf16[224,384]{1,0:T(8,128)(2,1)}, bf16[224,384]{1,0:T(8,128)(2,1)}, u32[]{:S(2)}, u32[]{:S(2)}) collective-permute-start(bf16[224,384]{1,0:T(8,128)(2,1)} %collective-permute-done.27), channel_id=1, source_target_pairs={{0,4},{4,8},{8,12},{12,14},{14,10},{10,6},{6,2},{2,0},{1,5},{5,9},... | collective-permute-start | bytes 516104 | tf_op jit(solution)/shard_map/ppermute | solution.py:47
  70.2 9.4 %collective-permute-start.35 = (bf16[224,384]{1,0:T(8,128)(2,1)}, bf16[224,384]{1,0:T(8,128)(2,1)}, u32[]{:S(2)}, u32[]{:S(2)}) collective-permute-start(bf16[224,384]{1,0:T(8,128)(2,1)} %collective-permute-done.34), channel_id=1, source_target_pairs={{0,2},{4,0},{8,4},{12,8},{14,12},{10,14},{6,10},{2,6},{1,3},{5,1},... | collective-permute-start | bytes 516104 | tf_op jit(solution)/shard_map/ppermute | solution.py:48
  79.6 5.9 %collective-permute-start.29 = (bf16[224,384]{1,0:T(8,128)(2,1)}, bf16[224,384]{1,0:T(8,128)(2,1)S(1)}, u32[]{:S(2)}, u32[]{:S(2)}) collective-permute-start(bf16[224,384]{1,0:T(8,128)(2,1)} %collective-permute-done.28), channel_id=1, source_target_pairs={{0,4},{4,8},{8,12},{12,14},{14,10},{10,6},{6,2},{2,0},{1,5},{5,9},... | collective-permute-start | bytes 516104 | tf_op jit(solution)/shard_map/ppermute | solution.py:47
  79.6 5.9 %collective-permute-start.36 = (bf16[224,384]{1,0:T(8,128)(2,1)}, bf16[224,384]{1,0:T(8,128)(2,1)S(1)}, u32[]{:S(2)}, u32[]{:S(2)}) collective-permute-start(bf16[224,384]{1,0:T(8,128)(2,1)} %collective-permute-done.35), channel_id=1, source_target_pairs={{0,2},{4,0},{8,4},{12,8},{14,12},{10,14},{6,10},{2,6},{1,3},{5,1},... | collective-permute-start | bytes 516104 | tf_op jit(solution)/shard_map/ppermute | solution.py:48
  85.5 5.4 %collective-permute-start.30 = (bf16[224,384]{1,0:T(8,128)(2,1)S(1)}, bf16[224,384]{1,0:T(8,128)(2,1)S(1)}, u32[]{:S(2)}, u32[]{:S(2)}) collective-permute-start(bf16[224,384]{1,0:T(8,128)(2,1)S(1)} %collective-permute-done.29), channel_id=1, source_target_pairs={{0,4},{4,8},{8,12},{12,14},{14,10},{10,6},{6,2},{2,0},{1,5},{5,9},... | collective-permute-start | bytes 516104 | tf_op jit(solution)/shard_map/ppermute | solution.py:47
  85.5 6.1 %collective-permute-start.37 = (bf16[224,384]{1,0:T(8,128)(2,1)S(1)}, bf16[224,384]{1,0:T(8,128)(2,1)}, u32[]{:S(2)}, u32[]{:S(2)}) collective-permute-start(bf16[224,384]{1,0:T(8,128)(2,1)S(1)} %collective-permute-done.36), channel_id=1, source_target_pairs={{0,2},{4,0},{8,4},{12,8},{14,12},{10,14},{6,10},{2,6},{1,3},{5,1},... | collective-permute-start | bytes 516104 | tf_op jit(solution)/shard_map/ppermute | solution.py:48
  88.3 20.0 %collective-permute-start.2 = (bf16[2,128,1792]{2,1,0:T(8,128)(2,1)}, bf16[2,128,1792]{2,1,0:T(8,128)(2,1)}, u32[]{:S(2)}, u32[]{:S(2)}) collective-permute-start(bf16[2,128,1792]{2,1,0:T(8,128)(2,1)} %collective-permute-done.1), channel_id=1, source_target_pairs={{0,1},{1,0},{2,3},{3,2},{4,5},{5,4},{6,7},{7,6},{8,9},{9,8},{10,11... | collective-permute-start | bytes 2752520 | tf_op jit(solution)/shard_map/ppermute | solution.py:113
  90.9 6.5 %collective-permute-start.31 = (bf16[224,384]{1,0:T(8,128)(2,1)S(1)}, bf16[224,384]{1,0:T(8,128)(2,1)S(1)}, u32[]{:S(2)}, u32[]{:S(2)}) collective-permute-start(bf16[224,384]{1,0:T(8,128)(2,1)S(1)} %collective-permute-done.30), channel_id=1, source_target_pairs={{0,4},{4,8},{8,12},{12,14},{14,10},{10,6},{6,2},{2,0},{1,5},{5,9},... | collective-permute-start | bytes 516104 | tf_op jit(solution)/shard_map/ppermute | solution.py:47
  91.6 8.6 %collective-permute-start.38 = (bf16[224,384]{1,0:T(8,128)(2,1)}, bf16[224,384]{1,0:T(8,128)(2,1)}, u32[]{:S(2)}, u32[]{:S(2)}) collective-permute-start(bf16[224,384]{1,0:T(8,128)(2,1)} %collective-permute-done.37), channel_id=1, source_target_pairs={{0,2},{4,0},{8,4},{12,8},{14,12},{10,14},{6,10},{2,6},{1,3},{5,1},... | collective-permute-start | bytes 516104 | tf_op jit(solution)/shard_map/ppermute | solution.py:48
  126.5 5.8 %collective-permute-start.17 = (bf16[2,128,192]{1,0,2:T(2,128)(2,1)S(1)}, bf16[2,128,192]{1,0,2:T(2,128)(2,1)S(1)}, u32[]{:S(2)}, u32[]{:S(2)}) collective-permute-start(bf16[2,128,192]{1,0,2:T(2,128)(2,1)S(1)} %fusion.28), channel_id=1, source_target_pairs={{0,16},{16,0},{1,17},{17,1},{2,18},{18,2},{3,19},{19,3},{4,20},{20... | collective-permute-start | bytes 294920 | tf_op jit(solution)/shard_map/ppermute | solution.py:150
  127.7 11.0 %collective-permute-start.39 = (bf16[2,128,384]{1,2,0:T(8,128)(2,1)S(1)}, bf16[2,128,384]{1,2,0:T(8,128)(2,1)S(1)}, u32[]{:S(2)}, u32[]{:S(2)}) collective-permute-start(bf16[2,128,384]{1,2,0:T(8,128)(2,1)S(1)} %bitcast.193), channel_id=1, source_target_pairs={{0,16},{16,0},{1,17},{17,1},{2,18},{18,2},{3,19},{19,3},{4,20},{20... | collective-permute-start | bytes 589832 | tf_op jit(solution)/shard_map/ppermute | solution.py:150
  133.0 9.5 %collective-permute-start.18 = (bf16[2,128,256]{1,0,2:T(2,128)(2,1)S(1)}, bf16[2,128,256]{1,0,2:T(2,128)(2,1)}, u32[]{:S(2)}, u32[]{:S(2)}) collective-permute-start(bf16[2,128,256]{1,0,2:T(2,128)(2,1)S(1)} %pad_maximum_fusion.4), channel_id=1, source_target_pairs={{0,2},{2,4},{4,6},{6,8},{8,10},{10,12},{12,14},{14,0},{1,3},{3,5},... | collective-permute-start | bytes 393224 | tf_op jit(solution)/shard_map/ppermute | solution.py:164
  134.8 11.4 %collective-permute-start.19 = (bf16[2,128,256]{1,0,2:T(2,128)(2,1)S(1)}, bf16[2,128,256]{1,0,2:T(2,128)(2,1)}, u32[]{:S(2)}, u32[]{:S(2)}) collective-permute-start(bf16[2,128,256]{1,0,2:T(2,128)(2,1)S(1)} %pad_maximum_fusion.4), channel_id=1, source_target_pairs={{0,4},{2,6},{4,8},{6,10},{8,12},{10,14},{12,0},{14,2},{1,5},{3,7},... | collective-permute-start | bytes 393224 | tf_op jit(solution)/shard_map/ppermute | solution.py:164
  136.4 13.5 %collective-permute-start.20 = (bf16[2,128,256]{1,0,2:T(2,128)(2,1)S(1)}, bf16[2,128,256]{1,0,2:T(2,128)(2,1)}, u32[]{:S(2)}, u32[]{:S(2)}) collective-permute-start(bf16[2,128,256]{1,0,2:T(2,128)(2,1)S(1)} %pad_maximum_fusion.4), channel_id=1, source_target_pairs={{0,6},{2,8},{4,10},{6,12},{8,14},{10,0},{12,2},{14,4},{1,7},{3,9},... | collective-permute-start | bytes 393224 | tf_op jit(solution)/shard_map/ppermute | solution.py:164
  136.4 14.5 %collective-permute-start.21 = (bf16[2,128,256]{1,0,2:T(2,128)(2,1)S(1)}, bf16[2,128,256]{1,0,2:T(2,128)(2,1)}, u32[]{:S(2)}, u32[]{:S(2)}) collective-permute-start(bf16[2,128,256]{1,0,2:T(2,128)(2,1)S(1)} %pad_maximum_fusion.4), channel_id=1, source_target_pairs={{0,8},{2,10},{4,12},{6,14},{8,0},{10,2},{12,4},{14,6},{1,9},{3,11}... | collective-permute-start | bytes 393224 | tf_op jit(solution)/shard_map/ppermute | solution.py:164
  138.7 13.3 %collective-permute-start.22 = (bf16[2,128,256]{1,0,2:T(2,128)(2,1)S(1)}, bf16[2,128,256]{1,0,2:T(2,128)(2,1)S(1)}, u32[]{:S(2)}, u32[]{:S(2)}) collective-permute-start(bf16[2,128,256]{1,0,2:T(2,128)(2,1)S(1)} %pad_maximum_fusion.4), channel_id=1, source_target_pairs={{0,10},{2,12},{4,14},{6,0},{8,2},{10,4},{12,6},{14,8},{1,11},{3,13... | collective-permute-start | bytes 393224 | tf_op jit(solution)/shard_map/ppermute | solution.py:164
  142.5 10.9 %collective-permute-start.23 = (bf16[2,128,256]{1,0,2:T(2,128)(2,1)S(1)}, bf16[2,128,256]{1,0,2:T(2,128)(2,1)S(1)}, u32[]{:S(2)}, u32[]{:S(2)}) collective-permute-start(bf16[2,128,256]{1,0,2:T(2,128)(2,1)S(1)} %pad_maximum_fusion.4), channel_id=1, source_target_pairs={{0,12},{2,14},{4,0},{6,2},{8,4},{10,6},{12,8},{14,10},{1,13},{3,15... | collective-permute-start | bytes 393224 | tf_op jit(solution)/shard_map/ppermute | solution.py:164
  146.2 7.4 %collective-permute-start.24 = (bf16[2,128,256]{1,0,2:T(2,128)(2,1)S(1)}, bf16[2,128,256]{1,0,2:T(2,128)(2,1)S(1)}, u32[]{:S(2)}, u32[]{:S(2)}) collective-permute-start(bf16[2,128,256]{1,0,2:T(2,128)(2,1)S(1)} %pad_maximum_fusion.4), channel_id=1, source_target_pairs={{0,14},{2,0},{4,2},{6,4},{8,6},{10,8},{12,10},{14,12},{1,15},{3,1}... | collective-permute-start | bytes 393224 | tf_op jit(solution)/shard_map/ppermute | solution.py:164
  (26 other events, 136.9 us)

commit v7 on v4

--- a/solution.py
+++ b/solution.py
@@ -31,17 +31,10 @@
     return [2 * z for z in range(count // 2)] + [2 * z + 1 for z in reversed(range(count // 2))]
 
 
-def project_rows(normed, shard, count, here, column):
-    features = normed.shape[1]
-    shift = (count // 2) * column
+def gather_rows(shard, count, here, rotate):
     if count != 8:
         full = lax.all_gather(shard, "row", axis=0, tiled=True)
-        full = jnp.where(
-            column == 0,
-            full,
-            jnp.concatenate([full[features // 2 :], full[: features // 2]], axis=0),
-        )
-        return jnp.dot(normed, full, preferred_element_type=jnp.float32)
+        return jnp.roll(full, -rotate * shard.shape[0], axis=0)
     order = snake_order(count)
     position = [0] * count
     for i, d in enumerate(order):
@@ -49,23 +42,23 @@
     forward = [(order[i], order[(i + 1) % count]) for i in range(count)]
     backward = [(order[i], order[(i - 1) % count]) for i in range(count)]
     half = shard.shape[0] // 2
-    chunks = normed.reshape(normed.shape[0], count, 2, half).transpose(1, 2, 0, 3)
-    table = jnp.array(position, dtype=jnp.int32)
-    ring = jnp.array(order, dtype=jnp.int32)
-    mine = table[here]
-
-    def term(source, part, piece):
-        rows = chunks[(source + shift) % count, part]
-        return jnp.dot(rows, piece, preferred_element_type=jnp.float32)
-
     ahead, behind = shard[:half], shard[half:]
-    total = term(here, 0, ahead) + term(here, 1, behind)
-    for step in range(1, count):
+    ahead_parts, behind_parts = [ahead], [behind]
+    for _ in range(count - 1):
         ahead = lax.ppermute(ahead, "row", forward)
         behind = lax.ppermute(behind, "row", backward)
-        total = total + term(ring[(mine - step) % count], 0, ahead)
-        total = total + term(ring[(mine + step) % count], 1, behind)
-    return total
+        ahead_parts.append(ahead)
+        behind_parts.append(behind)
+    table = jnp.array(position, dtype=jnp.int32)
+    mine = table[here]
+    ahead_stack = jnp.stack(ahead_parts)
+    behind_stack = jnp.stack(behind_parts)
+    pieces = []
+    for j in range(count):
+        source = table[(j + rotate) % count]
+        pieces.append(lax.dynamic_index_in_dim(ahead_stack, (mine - source) % count, 0, False))
+        pieces.append(lax.dynamic_index_in_dim(behind_stack, (source - mine) % count, 0, False))
+    return jnp.concatenate(pieces, axis=0)
 
 
 def shards(
@@ -109,6 +102,7 @@
         jnp.concatenate([rotary_b[:split], value_bias[:value_split]]),
         jnp.concatenate([rotary_b[split:], value_bias[value_split:]]),
     )
+    full_panel = gather_rows(panel, row_count, here, (row_count // 2) * column)
 
     other_half = lax.ppermute(tokens, "col", SWAP)
     partner_half = lax.ppermute(tokens, "groups", SWAP)
@@ -135,7 +129,7 @@
     )
     token_positions = (here * length + jnp.arange(length, dtype=jnp.int32)).astype(jnp.float32)
 
-    summed = project_rows(normed, panel, row_count, here, column) + panel_bias
+    summed = jnp.dot(normed, full_panel, preferred_element_type=jnp.float32) + panel_bias
     summed = summed.reshape(2 * passages, length, split + value_split)
     turned = apply_rotation(
         summed[..., :split].reshape(2 * passages, length, split // HEAD_SIZE, HEAD_SIZE),

time: 183 us -> 146 us (0.80)
  matrix products: 23.7 us -> 6.79 us
  waiting for transfers between devices: 39.9 us -> 31.2 us
  local copies, waits for them, and re-layouts: 50 us -> 42.8 us
  other arithmetic: 18.3 us -> 12.4 us
  between operations: 19.3 us -> 21.3 us
    convert_element_type x2 -> x0, local copies, waits for them, and re-layouts: 29.1 us -> none  [shards(): widened = both.astype(jnp.float32)]
    unnamed x36 -> x56, local copies, waits for them, and re-layouts: 1.76 us -> 25.8 us
    dot_general x16 -> x1, matrix products: 19.3 us -> 2.37 us  [shards(): jnp.dot(normed, full_panel, preferred_element_type=jnp.float32) + panel_bias]
    ppermute x14, waiting for transfers between devices: 30.8 us -> 25 us  [the longest x7 23.4 us: gather_rows(): ahead = lax.ppermute(ahead, 'row', forward)]
    convert_element_type x1, other arithmetic: 4.41 us -> 0.9 us  [shards(): widened = both.astype(jnp.float32)]
    ppermute x7, waiting for transfers between devices: 2.8 us -> 0.02 us  [shards(): lax.ppermute(pairs, 'row', [(i, (i + k) % row_count) for i in range(row_c...]
    convert_element_type x1, other arithmetic: 3.76 us -> 1.19 us  [shards(): normed = (widened * lax.rsqrt(power + norm_eps) * gain_here).astype(jnp.b...]
  transfers between devices with their start and end apart: 25 -> 25, of which waited for: 8 -> 12; matrix products, arithmetic and copies ran while one was open for 40% -> 25% of each run, Pallas kernels for 0% -> 0%
where the time goes in v7:
time: 146 us; the launch traced here: 145 us
  local copies, waits for them, and re-layouts  42.8 us (29%)
  waiting for transfers between devices  31.2 us (21%)
  starting transfers between devices  30.6 us (21%)
  between operations  21.3 us (15%)
  other arithmetic  12.4 us (8%)
  matrix products  6.79 us (5%)
    unnamed x56, local copies, waits for them, and re-layouts  25.8 us
    ppermute x7, waiting for transfers between devices, gather_rows(): ahead = lax.ppermute(ahead, 'row', forward)  23.4 us
    ppermute x7, starting transfers between devices, shards(): lax.ppermute(pairs, 'row', [(i, (i + k) % row_count) for i in range(row_c...  12.6 us
    ppermute x7, starting transfers between devices, gather_rows(): ahead = lax.ppermute(ahead, 'row', forward)  11.1 us
    ppermute x1, waiting for transfers between devices, shards(): returned = lax.ppermute(result[passages:], 'groups', SWAP)  6.2 us
    reduce_sum x1, other arithmetic, shards(): power = jnp.mean(widened * widened, axis=-1, keepdims=True)  4.1 us
    ppermute x7, starting transfers between devices, gather_rows(): behind = lax.ppermute(behind, 'row', backward)  3.31 us
    ppermute x1, starting transfers between devices, shards(): partner_half = lax.ppermute(tokens, 'groups', SWAP)  2.97 us
  transfers between devices with their start and end apart: 25, of which 12 were waited for; matrix products, arithmetic and copies ran while one was open for 25% of the time, Pallas kernels for 0%

profile of v7, /device:TPU:0, one launch (start us, length us, event | category | flops | bytes accessed | tf_op | source)
XLA Modules:
  0.0 145.1 jit_solution(811478058647346766)
XLA Ops:
  0.0 3.0 %collective-permute-start.1 = (bf16[2,128,1792]{2,1,0:T(8,128)(2,1)}, bf16[2,128,1792]{2,1,0:T(8,128)(2,1)S(1)}, u32[]{:S(2)}, u32[]{:S(2)}) collective-permute-start(bf16[2,128,1792]{2,1,0:T(8,128)(2,1)} %param.11), channel_id=1, source_target_pairs={{0,16},{16,0},{1,17},{17,1},{2,18},{18,2},{3,19},{19,3},{4,20},{20... | collective-permute-start | bytes 2752520 | tf_op jit(solution)/shard_map/ppermute | solution.py:108
  3.0 1.1 fusion.40
  5.2 1.2 fusion.19
  6.5 1.6 %collective-permute-start.3 = (bf16[224,576]{1,0:T(8,128)(2,1)S(1)}, bf16[224,576]{1,0:T(8,128)(2,1)}, u32[]{:S(2)}, u32[]{:S(2)}) collective-permute-start(bf16[224,576]{1,0:T(8,128)(2,1)S(1)} %get-tuple-element.12), channel_id=1, source_target_pairs={{0,4},{4,8},{8,12},{12,14},{14,10},{10,6},{6,2},{2,0},{1,5},{5,9},... | collective-permute-start | bytes 774152 | tf_op jit(solution)/shard_map/ppermute | solution.py:48
  32.8 1.6 %collective-permute-start.4 = (bf16[224,576]{1,0:T(8,128)(2,1)}, bf16[224,576]{1,0:T(8,128)(2,1)S(1)}, u32[]{:S(2)}, u32[]{:S(2)}) collective-permute-start(bf16[224,576]{1,0:T(8,128)(2,1)} %collective-permute-done.3), channel_id=1, source_target_pairs={{0,4},{4,8},{8,12},{12,14},{14,10},{10,6},{6,2},{2,0},{1,5},{5,9},... | collective-permute-start | bytes 774152 | tf_op jit(solution)/shard_map/ppermute | solution.py:48
  34.4 1.8 %bitcast_dynamic-update-slice_fusion.30 = bf16[8,224,576]{2,1,0:T(8,128)(2,1)} fusion(bf16[8,224,576]{2,1,0:T(8,128)(2,1)} %get-tuple-element.14, bf16[224,576]{1,0:T(8,128)(2,1)} %collective-permute-done.3), kind=kLoop, calls=%fused_computation.87 | loop fusion | bytes 573440
  37.4 4.4 %collective-permute-done.4 = bf16[224,576]{1,0:T(8,128)(2,1)S(1)} collective-permute-done((bf16[224,576]{1,0:T(8,128)(2,1)}, bf16[224,576]{1,0:T(8,128)(2,1)S(1)}, u32[]{:S(2)}, u32[]{:S(2)}) %collective-permute-start.4) | collective-permute-done | bytes 258080 | tf_op jit(solution)/shard_map/ppermute | solution.py:48
  41.8 1.6 %collective-permute-start.5 = (bf16[224,576]{1,0:T(8,128)(2,1)S(1)}, bf16[224,576]{1,0:T(8,128)(2,1)S(1)}, u32[]{:S(2)}, u32[]{:S(2)}) collective-permute-start(bf16[224,576]{1,0:T(8,128)(2,1)S(1)} %collective-permute-done.4), channel_id=1, source_target_pairs={{0,4},{4,8},{8,12},{12,14},{14,10},{10,6},{6,2},{2,0},{1,5},{5,9},... | collective-permute-start | bytes 774152 | tf_op jit(solution)/shard_map/ppermute | solution.py:48
  45.8 3.8 %collective-permute-done.5 = bf16[224,576]{1,0:T(8,128)(2,1)S(1)} collective-permute-done((bf16[224,576]{1,0:T(8,128)(2,1)S(1)}, bf16[224,576]{1,0:T(8,128)(2,1)S(1)}, u32[]{:S(2)}, u32[]{:S(2)}) %collective-permute-start.5) | collective-permute-done | bytes 258080 | tf_op jit(solution)/shard_map/ppermute | solution.py:48
  49.6 1.6 %collective-permute-start.6 = (bf16[224,576]{1,0:T(8,128)(2,1)S(1)}, bf16[224,576]{1,0:T(8,128)(2,1)S(1)}, u32[]{:S(2)}, u32[]{:S(2)}) collective-permute-start(bf16[224,576]{1,0:T(8,128)(2,1)S(1)} %collective-permute-done.5), channel_id=1, source_target_pairs={{0,4},{4,8},{8,12},{12,14},{14,10},{10,6},{6,2},{2,0},{1,5},{5,9},... | collective-permute-start | bytes 774152 | tf_op jit(solution)/shard_map/ppermute | solution.py:48
  53.3 3.2 %collective-permute-done.6 = bf16[224,576]{1,0:T(8,128)(2,1)S(1)} collective-permute-done((bf16[224,576]{1,0:T(8,128)(2,1)S(1)}, bf16[224,576]{1,0:T(8,128)(2,1)S(1)}, u32[]{:S(2)}, u32[]{:S(2)}) %collective-permute-start.6) | collective-permute-done | bytes 258080 | tf_op jit(solution)/shard_map/ppermute | solution.py:48
  56.5 1.6 %collective-permute-start.7 = (bf16[224,576]{1,0:T(8,128)(2,1)S(1)}, bf16[224,576]{1,0:T(8,128)(2,1)S(1)}, u32[]{:S(2)}, u32[]{:S(2)}) collective-permute-start(bf16[224,576]{1,0:T(8,128)(2,1)S(1)} %collective-permute-done.6), channel_id=1, source_target_pairs={{0,4},{4,8},{8,12},{12,14},{14,10},{10,6},{6,2},{2,0},{1,5},{5,9},... | collective-permute-start | bytes 774152 | tf_op jit(solution)/shard_map/ppermute | solution.py:48
  60.2 4.1 %collective-permute-done.7 = bf16[224,576]{1,0:T(8,128)(2,1)S(1)} collective-permute-done((bf16[224,576]{1,0:T(8,128)(2,1)S(1)}, bf16[224,576]{1,0:T(8,128)(2,1)S(1)}, u32[]{:S(2)}, u32[]{:S(2)}) %collective-permute-start.7) | collective-permute-done | bytes 258080 | tf_op jit(solution)/shard_map/ppermute | solution.py:48
  64.2 1.6 %collective-permute-start.8 = (bf16[224,576]{1,0:T(8,128)(2,1)S(1)}, bf16[224,576]{1,0:T(8,128)(2,1)S(1)}, u32[]{:S(2)}, u32[]{:S(2)}) collective-permute-start(bf16[224,576]{1,0:T(8,128)(2,1)S(1)} %collective-permute-done.7), channel_id=1, source_target_pairs={{0,4},{4,8},{8,12},{12,14},{14,10},{10,6},{6,2},{2,0},{1,5},{5,9},... | collective-permute-start | bytes 774152 | tf_op jit(solution)/shard_map/ppermute | solution.py:48
  67.8 5.0 %collective-permute-done.8 = bf16[224,576]{1,0:T(8,128)(2,1)S(1)} collective-permute-done((bf16[224,576]{1,0:T(8,128)(2,1)S(1)}, bf16[224,576]{1,0:T(8,128)(2,1)S(1)}, u32[]{:S(2)}, u32[]{:S(2)}) %collective-permute-start.8) | collective-permute-done | bytes 258080 | tf_op jit(solution)/shard_map/ppermute | solution.py:48
  72.8 1.6 %collective-permute-start.9 = (bf16[224,576]{1,0:T(8,128)(2,1)S(1)}, bf16[224,576]{1,0:T(8,128)(2,1)S(1)}, u32[]{:S(2)}, u32[]{:S(2)}) collective-permute-start(bf16[224,576]{1,0:T(8,128)(2,1)S(1)} %collective-permute-done.8), channel_id=1, source_target_pairs={{0,4},{4,8},{8,12},{12,14},{14,10},{10,6},{6,2},{2,0},{1,5},{5,9},... | collective-permute-start | bytes 774152 | tf_op jit(solution)/shard_map/ppermute | solution.py:48
  76.5 3.0 %collective-permute-done.9 = bf16[224,576]{1,0:T(8,128)(2,1)S(1)} collective-permute-done((bf16[224,576]{1,0:T(8,128)(2,1)S(1)}, bf16[224,576]{1,0:T(8,128)(2,1)S(1)}, u32[]{:S(2)}, u32[]{:S(2)}) %collective-permute-start.9) | collective-permute-done | bytes 258080 | tf_op jit(solution)/shard_map/ppermute | solution.py:48
  82.5 1.1 bitcast_dynamic-update-slice_fusion.14
  92.1 4.1 %multiply_reduce_fusion = f32[4,128]{1,0:T(4,128)S(1)} fusion(bf16[2,128,1792]{2,1,0:T(8,128)(2,1)S(1)} %collective-permute-done.2, bf16[2,128,1792]{2,1,0:T(8,128)(2,1)S(1)} %collective-permute-done.1, bf16[2,128,1792]{2,1,0:T(8,128)(2,1)S(1)} %collective-permute-done, bf16[2,128,1792]{2,1,0:T(8,128)(2,1)S(1)} %copy-done.1), kind=kLoop, calls=%fused_computation.8 | loop fusion | flops 18349568 | bytes 3672064 | tf_op jit(solution)/shard_map/reduce_sum | solution.py:124
  97.1 1.2 fusion.1
  98.3 2.4 %convolution_add_fusion = f32[512,576]{0,1:T(8,128)S(1)} fusion(bf16[512,3584]{1,0:T(8,128)(2,1)S(1)} %fusion.1, bf16[3584,576]{1,0:T(8,128)(2,1)S(1)} %bitcast_dynamic-update-slice_fusion, f32[576]{0:T(1024)S(1)} %maximum_select_fusion.1), kind=kOutput, calls=%fused_computation.24 | convolution fusion | flops 2114224128 | bytes 8980736 | tf_op jit(solution)/shard_map/dot_general | solution.py:132
  103.5 6.2 %collective-permute-done.17 = bf16[2,128,576]{1,0,2:T(2,128)(2,1)S(1)} collective-permute-done((bf16[2,128,576]{1,0,2:T(2,128)(2,1)S(1)}, bf16[2,128,576]{1,0,2:T(2,128)(2,1)S(1)}, u32[]{:S(2)}, u32[]{:S(2)}) %collective-permute-start.17) | collective-permute-done | bytes 294944 | tf_op jit(solution)/shard_map/ppermute | solution.py:143
  110.9 1.3 collective-permute-start.18
  112.2 1.6 %collective-permute-start.19 = (bf16[2,128,256]{1,0,2:T(2,128)(2,1)S(1)}, bf16[2,128,256]{1,0,2:T(2,128)(2,1)S(1)}, u32[]{:S(2)}, u32[]{:S(2)}) collective-permute-start(bf16[2,128,256]{1,0,2:T(2,128)(2,1)S(1)} %pad_maximum_fusion.4), channel_id=1, source_target_pairs={{0,4},{2,6},{4,8},{6,10},{8,12},{10,14},{12,0},{14,2},{1,5},{3,7},... | collective-permute-start | bytes 393224 | tf_op jit(solution)/shard_map/ppermute | solution.py:154
  113.8 3.1 %collective-permute-start.20 = (bf16[2,128,256]{1,0,2:T(2,128)(2,1)S(1)}, bf16[2,128,256]{1,0,2:T(2,128)(2,1)S(1)}, u32[]{:S(2)}, u32[]{:S(2)}) collective-permute-start(bf16[2,128,256]{1,0,2:T(2,128)(2,1)S(1)} %pad_maximum_fusion.4), channel_id=1, source_target_pairs={{0,6},{2,8},{4,10},{6,12},{8,14},{10,0},{12,2},{14,4},{1,7},{3,9},... | collective-permute-start | bytes 393224 | tf_op jit(solution)/shard_map/ppermute | solution.py:154
  117.8 2.4 %collective-permute-start.22 = (bf16[2,128,256]{1,0,2:T(2,128)(2,1)S(1)}, bf16[2,128,256]{1,0,2:T(2,128)(2,1)S(1)}, u32[]{:S(2)}, u32[]{:S(2)}) collective-permute-start(bf16[2,128,256]{1,0,2:T(2,128)(2,1)S(1)} %pad_maximum_fusion.4), channel_id=1, source_target_pairs={{0,10},{2,12},{4,14},{6,0},{8,2},{10,4},{12,6},{14,8},{1,11},{3,13... | collective-permute-start | bytes 393224 | tf_op jit(solution)/shard_map/ppermute | solution.py:154
  122.0 1.8 %copy.51 = bf16[2,2,64,7,128]{4,2,3,1,0:T(8,128)(2,1)S(1)} copy(bf16[2,2,64,7,128]{2,1,0,4,3:T(2,128)(2,1)S(1)} %reshape.334) | data formatting | bytes 917504 | tf_op jit(solution)/shard_map/reshape | solution.py:191
  123.8 1.6 %collective-permute-start.23 = (bf16[2,128,256]{1,0,2:T(2,128)(2,1)S(1)}, bf16[2,128,256]{1,0,2:T(2,128)(2,1)S(1)}, u32[]{:S(2)}, u32[]{:S(2)}) collective-permute-start(bf16[2,128,256]{1,0,2:T(2,128)(2,1)S(1)} %pad_maximum_fusion.4), channel_id=1, source_target_pairs={{0,12},{2,14},{4,0},{6,2},{8,4},{10,6},{12,8},{14,10},{1,13},{3,15... | collective-permute-start | bytes 393224 | tf_op jit(solution)/shard_map/ppermute | solution.py:154
  126.2 1.7 %collective-permute-start.24 = (bf16[2,128,256]{1,0,2:T(2,128)(2,1)S(1)}, bf16[2,128,256]{1,0,2:T(2,128)(2,1)S(1)}, u32[]{:S(2)}, u32[]{:S(2)}) collective-permute-start(bf16[2,128,256]{1,0,2:T(2,128)(2,1)S(1)} %pad_maximum_fusion.4), channel_id=1, source_target_pairs={{0,14},{2,0},{4,2},{6,4},{8,6},{10,8},{12,10},{14,12},{1,15},{3,1}... | collective-permute-start | bytes 393224 | tf_op jit(solution)/shard_map/ppermute | solution.py:154
  132.6 1.3 copy.49
  134.5 1.4 gather_fusion.2
  143.7 1.3 convert_element_type.50
  (166 shorter events, 49.8 us)
Async XLA Ops:
  0.0 8.9 %copy-start = (s32[2,2,2]{2,1,0:T(2,128)S(1)}, s32[2,2,2]{2,1,0:T(2,128)}, u32[]{:S(2)}) copy-start(s32[2,2,2]{2,1,0:T(2,128)} %param.20) | copy-start | bytes 100
  0.0 53.3 %collective-permute-start.1 = (bf16[2,128,1792]{2,1,0:T(8,128)(2,1)}, bf16[2,128,1792]{2,1,0:T(8,128)(2,1)S(1)}, u32[]{:S(2)}, u32[]{:S(2)}) collective-permute-start(bf16[2,128,1792]{2,1,0:T(8,128)(2,1)} %param.11), channel_id=1, source_target_pairs={{0,16},{16,0},{1,17},{17,1},{2,18},{18,2},{3,19},{19,3},{4,20},{20... | collective-permute-start | bytes 2752520 | tf_op jit(solution)/shard_map/ppermute | solution.py:108
  3.0 89.1 %collective-permute-start = (bf16[2,128,1792]{2,1,0:T(8,128)(2,1)}, bf16[2,128,1792]{2,1,0:T(8,128)(2,1)S(1)}, u32[]{:S(2)}, u32[]{:S(2)}) collective-permute-start(bf16[2,128,1792]{2,1,0:T(8,128)(2,1)} %param.11), channel_id=1, source_target_pairs={{0,1},{1,0},{2,3},{3,2},{4,5},{5,4},{6,7},{7,6},{8,9},{9,8},{10,11... | collective-permute-start | bytes 2752520 | tf_op jit(solution)/shard_map/ppermute | solution.py:107
  3.0 5.8 %copy-start.4 = (f32[3584]{0:T(1024)S(1)}, f32[3584]{0:T(1024)}, u32[]{:S(2)}) copy-start(f32[3584]{0:T(1024)} %param.12) | copy-start | bytes 43012
  3.0 5.8 %copy-start.8 = (f32[128]{0:T(128)S(1)}, f32[128]{0:T(128)}, u32[]{:S(2)}) copy-start(f32[128]{0:T(128)} %param.18) | copy-start | bytes 1540
  3.0 5.9 %copy-start.6 = (f32[896]{0:T(1024)S(1)}, f32[896]{0:T(1024)}, u32[]{:S(2)}) copy-start(f32[896]{0:T(1024)} %param.14) | copy-start | bytes 10756
  3.0 5.9 %copy-start.9 = (f32[128]{0:T(128)S(1)}, f32[128]{0:T(128)}, u32[]{:S(2)}) copy-start(f32[128]{0:T(128)} %param.16) | copy-start | bytes 1540
  4.1 5.3 %slice-start = ((f32[896]{0:T(1024)}), f32[512]{0:T(512)S(1)}, s32[]{:S(2)}) async-start(f32[896]{0:T(1024)} %param.14), calls=%async_computation | async-start | bytes 4096 | tf_op jit(solution)/shard_map/slice | solution.py:102
  5.2 5.2 %copy-start.5 = (s32[8]{0:T(128)S(1)}, s32[8]{0:T(128)}, u32[]{:S(2)}) copy-start(s32[8]{0:T(128)} %constant.270.clone) | copy-start | bytes 100
  6.5 26.3 %collective-permute-start.3 = (bf16[224,576]{1,0:T(8,128)(2,1)S(1)}, bf16[224,576]{1,0:T(8,128)(2,1)}, u32[]{:S(2)}, u32[]{:S(2)}) collective-permute-start(bf16[224,576]{1,0:T(8,128)(2,1)S(1)} %get-tuple-element.12), channel_id=1, source_target_pairs={{0,4},{4,8},{8,12},{12,14},{14,10},{10,6},{6,2},{2,0},{1,5},{5,9},... | collective-permute-start | bytes 774152 | tf_op jit(solution)/shard_map/ppermute | solution.py:48
  8.1 28.1 %collective-permute-start.10 = (bf16[224,576]{1,0:T(8,128)(2,1)S(1)}, bf16[224,576]{1,0:T(8,128)(2,1)S(1)}, u32[]{:S(2)}, u32[]{:S(2)}) collective-permute-start(bf16[224,576]{1,0:T(8,128)(2,1)S(1)} %get-tuple-element.11), channel_id=1, source_target_pairs={{0,2},{4,0},{8,4},{12,8},{14,12},{10,14},{6,10},{2,6},{1,3},{5,1},... | collective-permute-start | bytes 774152 | tf_op jit(solution)/shard_map/ppermute | solution.py:49
  32.8 8.9 %collective-permute-start.4 = (bf16[224,576]{1,0:T(8,128)(2,1)}, bf16[224,576]{1,0:T(8,128)(2,1)S(1)}, u32[]{:S(2)}, u32[]{:S(2)}) collective-permute-start(bf16[224,576]{1,0:T(8,128)(2,1)} %collective-permute-done.3), channel_id=1, source_target_pairs={{0,4},{4,8},{8,12},{12,14},{14,10},{10,6},{6,2},{2,0},{1,5},{5,9},... | collective-permute-start | bytes 774152 | tf_op jit(solution)/shard_map/ppermute | solution.py:48
  36.2 8.4 %collective-permute-start.11 = (bf16[224,576]{1,0:T(8,128)(2,1)S(1)}, bf16[224,576]{1,0:T(8,128)(2,1)S(1)}, u32[]{:S(2)}, u32[]{:S(2)}) collective-permute-start(bf16[224,576]{1,0:T(8,128)(2,1)S(1)} %collective-permute-done.10), channel_id=1, source_target_pairs={{0,2},{4,0},{8,4},{12,8},{14,12},{10,14},{6,10},{2,6},{1,3},{5,1},... | collective-permute-start | bytes 774152 | tf_op jit(solution)/shard_map/ppermute | solution.py:49
  41.8 7.8 %collective-permute-start.5 = (bf16[224,576]{1,0:T(8,128)(2,1)S(1)}, bf16[224,576]{1,0:T(8,128)(2,1)S(1)}, u32[]{:S(2)}, u32[]{:S(2)}) collective-permute-start(bf16[224,576]{1,0:T(8,128)(2,1)S(1)} %collective-permute-done.4), channel_id=1, source_target_pairs={{0,4},{4,8},{8,12},{12,14},{14,10},{10,6},{6,2},{2,0},{1,5},{5,9},... | collective-permute-start | bytes 774152 | tf_op jit(solution)/shard_map/ppermute | solution.py:48
  44.6 7.5 %collective-permute-start.12 = (bf16[224,576]{1,0:T(8,128)(2,1)S(1)}, bf16[224,576]{1,0:T(8,128)(2,1)S(1)}, u32[]{:S(2)}, u32[]{:S(2)}) collective-permute-start(bf16[224,576]{1,0:T(8,128)(2,1)S(1)} %collective-permute-done.11), channel_id=1, source_target_pairs={{0,2},{4,0},{8,4},{12,8},{14,12},{10,14},{6,10},{2,6},{1,3},{5,1},... | collective-permute-start | bytes 774152 | tf_op jit(solution)/shard_map/ppermute | solution.py:49
  49.6 6.9 %collective-permute-start.6 = (bf16[224,576]{1,0:T(8,128)(2,1)S(1)}, bf16[224,576]{1,0:T(8,128)(2,1)S(1)}, u32[]{:S(2)}, u32[]{:S(2)}) collective-permute-start(bf16[224,576]{1,0:T(8,128)(2,1)S(1)} %collective-permute-done.5), channel_id=1, source_target_pairs={{0,4},{4,8},{8,12},{12,14},{14,10},{10,6},{6,2},{2,0},{1,5},{5,9},... | collective-permute-start | bytes 774152 | tf_op jit(solution)/shard_map/ppermute | solution.py:48
  52.1 6.9 %collective-permute-start.13 = (bf16[224,576]{1,0:T(8,128)(2,1)S(1)}, bf16[224,576]{1,0:T(8,128)(2,1)S(1)}, u32[]{:S(2)}, u32[]{:S(2)}) collective-permute-start(bf16[224,576]{1,0:T(8,128)(2,1)S(1)} %collective-permute-done.12), channel_id=1, source_target_pairs={{0,2},{4,0},{8,4},{12,8},{14,12},{10,14},{6,10},{2,6},{1,3},{5,1},... | collective-permute-start | bytes 774152 | tf_op jit(solution)/shard_map/ppermute | solution.py:49
  53.3 38.8 %collective-permute-start.2 = (bf16[2,128,1792]{2,1,0:T(8,128)(2,1)S(1)}, bf16[2,128,1792]{2,1,0:T(8,128)(2,1)S(1)}, u32[]{:S(2)}, u32[]{:S(2)}) collective-permute-start(bf16[2,128,1792]{2,1,0:T(8,128)(2,1)S(1)} %collective-permute-done.1), channel_id=1, source_target_pairs={{0,1},{1,0},{2,3},{3,2},{4,5},{5,4},{6,7},{7,6},{8,9},{9,8},{10,11... | collective-permute-start | bytes 2752520 | tf_op jit(solution)/shard_map/ppermute | solution.py:109
  56.5 7.7 %collective-permute-start.7 = (bf16[224,576]{1,0:T(8,128)(2,1)S(1)}, bf16[224,576]{1,0:T(8,128)(2,1)S(1)}, u32[]{:S(2)}, u32[]{:S(2)}) collective-permute-start(bf16[224,576]{1,0:T(8,128)(2,1)S(1)} %collective-permute-done.6), channel_id=1, source_target_pairs={{0,4},{4,8},{8,12},{12,14},{14,10},{10,6},{6,2},{2,0},{1,5},{5,9},... | collective-permute-start | bytes 774152 | tf_op jit(solution)/shard_map/ppermute | solution.py:48
  59.0 7.6 %collective-permute-start.14 = (bf16[224,576]{1,0:T(8,128)(2,1)S(1)}, bf16[224,576]{1,0:T(8,128)(2,1)S(1)}, u32[]{:S(2)}, u32[]{:S(2)}) collective-permute-start(bf16[224,576]{1,0:T(8,128)(2,1)S(1)} %collective-permute-done.13), channel_id=1, source_target_pairs={{0,2},{4,0},{8,4},{12,8},{14,12},{10,14},{6,10},{2,6},{1,3},{5,1},... | collective-permute-start | bytes 774152 | tf_op jit(solution)/shard_map/ppermute | solution.py:49
  64.2 8.6 %collective-permute-start.8 = (bf16[224,576]{1,0:T(8,128)(2,1)S(1)}, bf16[224,576]{1,0:T(8,128)(2,1)S(1)}, u32[]{:S(2)}, u32[]{:S(2)}) collective-permute-start(bf16[224,576]{1,0:T(8,128)(2,1)S(1)} %collective-permute-done.7), channel_id=1, source_target_pairs={{0,4},{4,8},{8,12},{12,14},{14,10},{10,6},{6,2},{2,0},{1,5},{5,9},... | collective-permute-start | bytes 774152 | tf_op jit(solution)/shard_map/ppermute | solution.py:48
  66.6 8.5 %collective-permute-start.15 = (bf16[224,576]{1,0:T(8,128)(2,1)S(1)}, bf16[224,576]{1,0:T(8,128)(2,1)S(1)}, u32[]{:S(2)}, u32[]{:S(2)}) collective-permute-start(bf16[224,576]{1,0:T(8,128)(2,1)S(1)} %collective-permute-done.14), channel_id=1, source_target_pairs={{0,2},{4,0},{8,4},{12,8},{14,12},{10,14},{6,10},{2,6},{1,3},{5,1},... | collective-permute-start | bytes 774152 | tf_op jit(solution)/shard_map/ppermute | solution.py:49
  72.8 6.6 %collective-permute-start.9 = (bf16[224,576]{1,0:T(8,128)(2,1)S(1)}, bf16[224,576]{1,0:T(8,128)(2,1)S(1)}, u32[]{:S(2)}, u32[]{:S(2)}) collective-permute-start(bf16[224,576]{1,0:T(8,128)(2,1)S(1)} %collective-permute-done.8), channel_id=1, source_target_pairs={{0,4},{4,8},{8,12},{12,14},{14,10},{10,6},{6,2},{2,0},{1,5},{5,9},... | collective-permute-start | bytes 774152 | tf_op jit(solution)/shard_map/ppermute | solution.py:48
  75.1 6.6 %collective-permute-start.16 = (bf16[224,576]{1,0:T(8,128)(2,1)S(1)}, bf16[224,576]{1,0:T(8,128)(2,1)S(1)}, u32[]{:S(2)}, u32[]{:S(2)}) collective-permute-start(bf16[224,576]{1,0:T(8,128)(2,1)S(1)} %collective-permute-done.15), channel_id=1, source_target_pairs={{0,2},{4,0},{8,4},{12,8},{14,12},{10,14},{6,10},{2,6},{1,3},{5,1},... | collective-permute-start | bytes 774152 | tf_op jit(solution)/shard_map/ppermute | solution.py:49
  102.9 6.8 %collective-permute-start.17 = (bf16[2,128,576]{1,0,2:T(2,128)(2,1)S(1)}, bf16[2,128,576]{1,0,2:T(2,128)(2,1)S(1)}, u32[]{:S(2)}, u32[]{:S(2)}) collective-permute-start(bf16[2,128,576]{1,0,2:T(2,128)(2,1)S(1)} %fusion.24), channel_id=1, source_target_pairs={{0,16},{16,0},{1,17},{17,1},{2,18},{18,2},{3,19},{19,3},{4,20},{20... | collective-permute-start | bytes 884744 | tf_op jit(solution)/shard_map/ppermute | solution.py:143
  110.9 12.9 %collective-permute-start.18 = (bf16[2,128,256]{1,0,2:T(2,128)(2,1)S(1)}, bf16[2,128,256]{1,0,2:T(2,128)(2,1)S(1)}, u32[]{:S(2)}, u32[]{:S(2)}) collective-permute-start(bf16[2,128,256]{1,0,2:T(2,128)(2,1)S(1)} %pad_maximum_fusion.4), channel_id=1, source_target_pairs={{0,2},{2,4},{4,6},{6,8},{8,10},{10,12},{12,14},{14,0},{1,3},{3,5},... | collective-permute-start | bytes 393224 | tf_op jit(solution)/shard_map/ppermute | solution.py:154
  112.2 14.0 %collective-permute-start.19 = (bf16[2,128,256]{1,0,2:T(2,128)(2,1)S(1)}, bf16[2,128,256]{1,0,2:T(2,128)(2,1)S(1)}, u32[]{:S(2)}, u32[]{:S(2)}) collective-permute-start(bf16[2,128,256]{1,0,2:T(2,128)(2,1)S(1)} %pad_maximum_fusion.4), channel_id=1, source_target_pairs={{0,4},{2,6},{4,8},{6,10},{8,12},{10,14},{12,0},{14,2},{1,5},{3,7},... | collective-permute-start | bytes 393224 | tf_op jit(solution)/shard_map/ppermute | solution.py:154
  113.8 14.9 %collective-permute-start.20 = (bf16[2,128,256]{1,0,2:T(2,128)(2,1)S(1)}, bf16[2,128,256]{1,0,2:T(2,128)(2,1)S(1)}, u32[]{:S(2)}, u32[]{:S(2)}) collective-permute-start(bf16[2,128,256]{1,0,2:T(2,128)(2,1)S(1)} %pad_maximum_fusion.4), channel_id=1, source_target_pairs={{0,6},{2,8},{4,10},{6,12},{8,14},{10,0},{12,2},{14,4},{1,7},{3,9},... | collective-permute-start | bytes 393224 | tf_op jit(solution)/shard_map/ppermute | solution.py:154
  116.8 12.6 %collective-permute-start.21 = (bf16[2,128,256]{1,0,2:T(2,128)(2,1)S(1)}, bf16[2,128,256]{1,0,2:T(2,128)(2,1)S(1)}, u32[]{:S(2)}, u32[]{:S(2)}) collective-permute-start(bf16[2,128,256]{1,0,2:T(2,128)(2,1)S(1)} %pad_maximum_fusion.4), channel_id=1, source_target_pairs={{0,8},{2,10},{4,12},{6,14},{8,0},{10,2},{12,4},{14,6},{1,9},{3,11}... | collective-permute-start | bytes 393224 | tf_op jit(solution)/shard_map/ppermute | solution.py:154
  117.8 12.4 %collective-permute-start.22 = (bf16[2,128,256]{1,0,2:T(2,128)(2,1)S(1)}, bf16[2,128,256]{1,0,2:T(2,128)(2,1)S(1)}, u32[]{:S(2)}, u32[]{:S(2)}) collective-permute-start(bf16[2,128,256]{1,0,2:T(2,128)(2,1)S(1)} %pad_maximum_fusion.4), channel_id=1, source_target_pairs={{0,10},{2,12},{4,14},{6,0},{8,2},{10,4},{12,6},{14,8},{1,11},{3,13... | collective-permute-start | bytes 393224 | tf_op jit(solution)/shard_map/ppermute | solution.py:154
  123.8 7.2 %collective-permute-start.23 = (bf16[2,128,256]{1,0,2:T(2,128)(2,1)S(1)}, bf16[2,128,256]{1,0,2:T(2,128)(2,1)S(1)}, u32[]{:S(2)}, u32[]{:S(2)}) collective-permute-start(bf16[2,128,256]{1,0,2:T(2,128)(2,1)S(1)} %pad_maximum_fusion.4), channel_id=1, source_target_pairs={{0,12},{2,14},{4,0},{6,2},{8,4},{10,6},{12,8},{14,10},{1,13},{3,15... | collective-permute-start | bytes 393224 | tf_op jit(solution)/shard_map/ppermute | solution.py:154
  126.2 5.6 %collective-permute-start.24 = (bf16[2,128,256]{1,0,2:T(2,128)(2,1)S(1)}, bf16[2,128,256]{1,0,2:T(2,128)(2,1)S(1)}, u32[]{:S(2)}, u32[]{:S(2)}) collective-permute-start(bf16[2,128,256]{1,0,2:T(2,128)(2,1)S(1)} %pad_maximum_fusion.4), channel_id=1, source_target_pairs={{0,14},{2,0},{4,2},{6,4},{8,6},{10,8},{12,10},{14,12},{1,15},{3,1}... | collective-permute-start | bytes 393224 | tf_op jit(solution)/shard_map/ppermute | solution.py:154
  (4 other events, 14.7 us)

commit v8 on v3

--- a/solution.py
+++ b/solution.py
@@ -114,28 +114,29 @@
         jnp.concatenate([partner_half, partner_other], axis=2),
         jnp.concatenate([partner_other, partner_half], axis=2),
     )
-    both = jnp.concatenate([whole, partner], axis=0)
-    widened = both.astype(jnp.float32)
-    power = jnp.mean(widened * widened, axis=-1, keepdims=True)
-    normed = (
-        (widened * lax.rsqrt(power + norm_eps) * gain)
-        .astype(jnp.bfloat16)
-        .reshape(2 * passages * length, -1)
-    )
     token_positions = (here * length + jnp.arange(length, dtype=jnp.int32)).astype(jnp.float32)
 
-    summed = jnp.dot(normed, full_panel, preferred_element_type=jnp.float32) + panel_bias
-    summed = summed.reshape(2 * passages, length, split + value_split)
-    turned = apply_rotation(
-        summed[..., :split].reshape(2 * passages, length, split // HEAD_SIZE, HEAD_SIZE),
-        token_positions,
-    ).astype(jnp.bfloat16)
-    result = jnp.concatenate(
-        [turned.reshape(2 * passages, length, split), summed[..., split:].astype(jnp.bfloat16)],
-        axis=-1,
-    )
-    mine = result[:passages]
-    returned = lax.ppermute(result[passages:], "groups", SWAP)
+    def project(rows):
+        widened = rows.astype(jnp.float32)
+        power = jnp.mean(widened * widened, axis=-1, keepdims=True)
+        normed = (
+            (widened * lax.rsqrt(power + norm_eps) * gain)
+            .astype(jnp.bfloat16)
+            .reshape(passages * length, -1)
+        )
+        summed = jnp.dot(normed, full_panel, preferred_element_type=jnp.float32) + panel_bias
+        summed = summed.reshape(passages, length, split + value_split)
+        turned = apply_rotation(
+            summed[..., :split].reshape(passages, length, split // HEAD_SIZE, HEAD_SIZE),
+            token_positions,
+        ).astype(jnp.bfloat16)
+        return jnp.concatenate(
+            [turned.reshape(passages, length, split), summed[..., split:].astype(jnp.bfloat16)],
+            axis=-1,
+        )
+
+    returned = lax.ppermute(project(partner), "groups", SWAP)
+    mine = project(whole)
     low = jnp.where(first, mine, returned)
     high = jnp.where(first, returned, mine)
     rotary_rows = jnp.concatenate([low[..., :split], high[..., :split]], axis=-1)

time: 123 us -> 129 us (1.049); the launches traced: 121 us -> 128 us
  waiting for transfers between devices: 34.1 us -> 43.3 us
  matrix products: 6.82 us -> 10.6 us
  local copies, waits for them, and re-layouts: 32.7 us -> 29 us
  other arithmetic: 16.1 us -> 13.9 us
    ppermute x7, waiting for transfers between devices: 23.9 us -> 33.5 us  [gather_rows(): ahead = lax.ppermute(ahead, 'row', forward)]
    select_n x2 -> x0, other arithmetic: 3.91 us -> none  [the longest x1 1.97 us: shards(): jnp.where(column == 0, jnp.concatenate([tokens, other_half], axis=2), jnp...]
    dot_general x1 -> x2, matrix products: 2.38 us -> 6.2 us  [project(): jnp.dot(normed, full_panel, preferred_element_type=jnp.float32) + panel_bias]
    unnamed x41 -> x54, local copies, waits for them, and re-layouts: 9.93 us -> 7.09 us
    reduce_sum x1 -> x2, other arithmetic: 0.79 us -> 3.47 us  [project(): power = jnp.mean(widened * widened, axis=-1, keepdims=True)]
  transfers between devices with their start and end apart: 25 -> 25, of which waited for: 11 -> 10; matrix products, arithmetic and copies ran while one was open for 29% -> 22% of each run, Pallas kernels for 0% -> 0%
where the time goes in v8:
time: 129 us; the launch traced here: 128 us
  waiting for transfers between devices  43.3 us (34%)
  starting transfers between devices  30.4 us (24%)
  local copies, waits for them, and re-layouts  29 us (22%)
  other arithmetic  13.9 us (11%)
  matrix products  10.6 us (8%)
    ppermute x7, waiting for transfers between devices, gather_rows(): ahead = lax.ppermute(ahead, 'row', forward)  33.5 us
    ppermute x7, starting transfers between devices, shards(): lax.ppermute(pairs, 'row', [(i, (i + k) % row_count) for i in range(row_c...  12.4 us
    ppermute x7, starting transfers between devices, gather_rows(): ahead = lax.ppermute(ahead, 'row', forward)  11.1 us
    unnamed x54, local copies, waits for them, and re-layouts  7.09 us
    ppermute x1, waiting for transfers between devices, shards(): returned = lax.ppermute(project(partner), 'groups', SWAP)  6.45 us
    dot_general x2, matrix products, project(): jnp.dot(normed, full_panel, preferred_element_type=jnp.float32) + panel_bias  6.2 us
    gather x1, local copies, waits for them, and re-layouts, gather_rows(): jnp.stack(behind_parts)[behind_pick]  3.89 us
    ppermute x7, starting transfers between devices, gather_rows(): behind = lax.ppermute(behind, 'row', backward)  3.57 us
  transfers between devices with their start and end apart: 25, of which 10 were waited for; matrix products, arithmetic and copies ran while one was open for 22% of the time, Pallas kernels for 0%

profile of v8, /device:TPU:0, one launch (start us, length us, event | category | flops | bytes accessed | tf_op | source)
XLA Modules:
  0.0 128.2 jit_solution(17409932444148961160)
XLA Ops:
  0.0 3.0 %collective-permute-start = (bf16[2,128,1792]{2,1,0:T(8,128)(2,1)}, bf16[2,128,1792]{2,1,0:T(8,128)(2,1)}, u32[]{:S(2)}, u32[]{:S(2)}) collective-permute-start(bf16[2,128,1792]{2,1,0:T(8,128)(2,1)} %param.11), channel_id=1, source_target_pairs={{0,16},{16,0},{1,17},{17,1},{2,18},{18,2},{3,19},{19,3},{4,20},{20... | collective-permute-start | bytes 2752520 | tf_op jit(solution)/shard_map/ppermute | solution.py:105
  6.5 1.6 %collective-permute-start.2 = (bf16[224,576]{1,0:T(8,128)(2,1)S(1)}, bf16[224,576]{1,0:T(8,128)(2,1)}, u32[]{:S(2)}, u32[]{:S(2)}) collective-permute-start(bf16[224,576]{1,0:T(8,128)(2,1)S(1)} %get-tuple-element.9), channel_id=1, source_target_pairs={{0,4},{4,8},{8,12},{12,14},{14,10},{10,6},{6,2},{2,0},{1,5},{5,9},... | collective-permute-start | bytes 774152 | tf_op jit(solution)/shard_map/ppermute | solution.py:47
  12.6 3.2 %collective-permute-done.2 = bf16[224,576]{1,0:T(8,128)(2,1)} collective-permute-done((bf16[224,576]{1,0:T(8,128)(2,1)S(1)}, bf16[224,576]{1,0:T(8,128)(2,1)}, u32[]{:S(2)}, u32[]{:S(2)}) %collective-permute-start.2) | collective-permute-done | bytes 258080 | tf_op jit(solution)/shard_map/ppermute | solution.py:47
  15.9 1.6 %collective-permute-start.3 = (bf16[224,576]{1,0:T(8,128)(2,1)}, bf16[224,576]{1,0:T(8,128)(2,1)S(1)}, u32[]{:S(2)}, u32[]{:S(2)}) collective-permute-start(bf16[224,576]{1,0:T(8,128)(2,1)} %collective-permute-done.2), channel_id=1, source_target_pairs={{0,4},{4,8},{8,12},{12,14},{14,10},{10,6},{6,2},{2,0},{1,5},{5,9},... | collective-permute-start | bytes 774152 | tf_op jit(solution)/shard_map/ppermute | solution.py:47
  19.9 4.7 %collective-permute-done.3 = bf16[224,576]{1,0:T(8,128)(2,1)S(1)} collective-permute-done((bf16[224,576]{1,0:T(8,128)(2,1)}, bf16[224,576]{1,0:T(8,128)(2,1)S(1)}, u32[]{:S(2)}, u32[]{:S(2)}) %collective-permute-start.3) | collective-permute-done | bytes 258080 | tf_op jit(solution)/shard_map/ppermute | solution.py:47
  24.6 1.6 %collective-permute-start.4 = (bf16[224,576]{1,0:T(8,128)(2,1)S(1)}, bf16[224,576]{1,0:T(8,128)(2,1)S(1)}, u32[]{:S(2)}, u32[]{:S(2)}) collective-permute-start(bf16[224,576]{1,0:T(8,128)(2,1)S(1)} %collective-permute-done.3), channel_id=1, source_target_pairs={{0,4},{4,8},{8,12},{12,14},{14,10},{10,6},{6,2},{2,0},{1,5},{5,9},... | collective-permute-start | bytes 774152 | tf_op jit(solution)/shard_map/ppermute | solution.py:47
  26.7 5.6 %collective-permute-done.4 = bf16[224,576]{1,0:T(8,128)(2,1)S(1)} collective-permute-done((bf16[224,576]{1,0:T(8,128)(2,1)S(1)}, bf16[224,576]{1,0:T(8,128)(2,1)S(1)}, u32[]{:S(2)}, u32[]{:S(2)}) %collective-permute-start.4) | collective-permute-done | bytes 258080 | tf_op jit(solution)/shard_map/ppermute | solution.py:47
  32.2 1.6 %collective-permute-start.5 = (bf16[224,576]{1,0:T(8,128)(2,1)S(1)}, bf16[224,576]{1,0:T(8,128)(2,1)S(1)}, u32[]{:S(2)}, u32[]{:S(2)}) collective-permute-start(bf16[224,576]{1,0:T(8,128)(2,1)S(1)} %collective-permute-done.4), channel_id=1, source_target_pairs={{0,4},{4,8},{8,12},{12,14},{14,10},{10,6},{6,2},{2,0},{1,5},{5,9},... | collective-permute-start | bytes 774152 | tf_op jit(solution)/shard_map/ppermute | solution.py:47
  35.0 4.2 %collective-permute-done.5 = bf16[224,576]{1,0:T(8,128)(2,1)S(1)} collective-permute-done((bf16[224,576]{1,0:T(8,128)(2,1)S(1)}, bf16[224,576]{1,0:T(8,128)(2,1)S(1)}, u32[]{:S(2)}, u32[]{:S(2)}) %collective-permute-start.5) | collective-permute-done | bytes 258080 | tf_op jit(solution)/shard_map/ppermute | solution.py:47
  39.2 1.6 %collective-permute-start.6 = (bf16[224,576]{1,0:T(8,128)(2,1)S(1)}, bf16[224,576]{1,0:T(8,128)(2,1)S(1)}, u32[]{:S(2)}, u32[]{:S(2)}) collective-permute-start(bf16[224,576]{1,0:T(8,128)(2,1)S(1)} %collective-permute-done.5), channel_id=1, source_target_pairs={{0,4},{4,8},{8,12},{12,14},{14,10},{10,6},{6,2},{2,0},{1,5},{5,9},... | collective-permute-start | bytes 774152 | tf_op jit(solution)/shard_map/ppermute | solution.py:47
  41.4 5.8 %collective-permute-done.6 = bf16[224,576]{1,0:T(8,128)(2,1)S(1)} collective-permute-done((bf16[224,576]{1,0:T(8,128)(2,1)S(1)}, bf16[224,576]{1,0:T(8,128)(2,1)S(1)}, u32[]{:S(2)}, u32[]{:S(2)}) %collective-permute-start.6) | collective-permute-done | bytes 258080 | tf_op jit(solution)/shard_map/ppermute | solution.py:47
  47.2 1.6 %collective-permute-start.7 = (bf16[224,576]{1,0:T(8,128)(2,1)S(1)}, bf16[224,576]{1,0:T(8,128)(2,1)S(1)}, u32[]{:S(2)}, u32[]{:S(2)}) collective-permute-start(bf16[224,576]{1,0:T(8,128)(2,1)S(1)} %collective-permute-done.6), channel_id=1, source_target_pairs={{0,4},{4,8},{8,12},{12,14},{14,10},{10,6},{6,2},{2,0},{1,5},{5,9},... | collective-permute-start | bytes 774152 | tf_op jit(solution)/shard_map/ppermute | solution.py:47
  49.4 6.7 %collective-permute-done.7 = bf16[224,576]{1,0:T(8,128)(2,1)S(1)} collective-permute-done((bf16[224,576]{1,0:T(8,128)(2,1)S(1)}, bf16[224,576]{1,0:T(8,128)(2,1)S(1)}, u32[]{:S(2)}, u32[]{:S(2)}) %collective-permute-start.7) | collective-permute-done | bytes 258080 | tf_op jit(solution)/shard_map/ppermute | solution.py:47
  56.2 1.6 %collective-permute-start.8 = (bf16[224,576]{1,0:T(8,128)(2,1)S(1)}, bf16[224,576]{1,0:T(8,128)(2,1)S(1)}, u32[]{:S(2)}, u32[]{:S(2)}) collective-permute-start(bf16[224,576]{1,0:T(8,128)(2,1)S(1)} %collective-permute-done.7), channel_id=1, source_target_pairs={{0,4},{4,8},{8,12},{12,14},{14,10},{10,6},{6,2},{2,0},{1,5},{5,9},... | collective-permute-start | bytes 774152 | tf_op jit(solution)/shard_map/ppermute | solution.py:47
  59.5 3.3 %collective-permute-done.8 = bf16[224,576]{1,0:T(8,128)(2,1)S(1)} collective-permute-done((bf16[224,576]{1,0:T(8,128)(2,1)S(1)}, bf16[224,576]{1,0:T(8,128)(2,1)S(1)}, u32[]{:S(2)}, u32[]{:S(2)}) %collective-permute-start.8) | collective-permute-done | bytes 258080 | tf_op jit(solution)/shard_map/ppermute | solution.py:47
  62.9 1.4 %copy-done.4 = bf16[8,224,576]{2,1,0:T(8,128)(2,1)} copy-done((bf16[8,224,576]{2,1,0:T(8,128)(2,1)}, bf16[8,224,576]{2,1,0:T(8,128)(2,1)S(1)}, u32[]{:S(2)}) %copy-start.4) | copy-done | bytes 2064408
  64.3 2.6 %gather_fusion = bf16[8,224,576]{2,1,0:T(8,128)(2,1)S(1)} fusion(bf16[8,224,576]{2,1,0:T(8,128)(2,1)} %copy-done.4, s32[1024]{0:T(1024)S(1)} %get-tuple-element.32), kind=kCustom, calls=%fused_computation | custom fusion | bytes 4128800 | tf_op jit(solution)/shard_map/gather | solution.py:56
  66.9 1.7 %bitcast_dynamic-update-slice_fusion = bf16[8,224,576]{2,1,0:T(8,128)(2,1)} fusion(bf16[8,224,576]{2,1,0:T(8,128)(2,1)} %copy-done.3, bf16[224,576]{1,0:T(8,128)(2,1)} %collective-permute-done.15), kind=kLoop, calls=%fused_computation.83 | loop fusion | bytes 573440 | tf_op jit(solution)/shard_map/stack | solution.py:56
  68.6 3.9 %gather_fusion.1 = bf16[8,224,576]{2,1,0:T(8,128)(2,1)} fusion(bf16[8,224,576]{2,1,0:T(8,128)(2,1)} %bitcast_dynamic-update-slice_fusion, s32[1024]{0:T(1024)S(1)} %get-tuple-element.31), kind=kCustom, calls=%fused_computation.1 | custom fusion | bytes 4128800 | tf_op jit(solution)/shard_map/gather | solution.py:56
  72.5 2.1 %pad_maximum_fusion = bf16[8,448,576]{2,1,0:T(8,128)(2,1)S(1)} fusion(bf16[8,224,576]{2,1,0:T(8,128)(2,1)} %gather_fusion.1, bf16[8,224,576]{2,1,0:T(8,128)(2,1)S(1)} %gather_fusion), kind=kLoop, calls=%fused_computation.7 | loop fusion | flops 8257536 | bytes 8257536 | tf_op jit(solution)/shard_map/concatenate | solution.py:55
  74.7 2.1 %copy-done.1 = bf16[8,448,576]{2,1,0:T(8,128)(2,1)} copy-done((bf16[8,448,576]{2,1,0:T(8,128)(2,1)}, bf16[8,448,576]{2,1,0:T(8,128)(2,1)S(1)}, u32[]{:S(2)}) %copy-start.1) | copy-done | bytes 4128792
  76.8 2.0 %fusion.24 = f32[256,576]{0,1:T(8,128)S(1)} fusion(bf16[3584,576]{1,0:T(8,128)(2,1)S(1)} %bitcast.153, bf16[256,1792]{1,0:T(8,128)(2,1)S(1)} %bitcast.164, bf16[256,1792]{1,0:T(8,128)(2,1)S(1)} %bitcast.163, f32[256]{0:T(256)S(1)} %rsqrt_bitcast_fusion, f32[3584]{0:T(1024)S(1)} %copy-done.13, pred[]{:T(512)S(6)} %eq.14, f32[576]{0:T(1024)S(1)} %maximum_select_fusion.6), kind=kOutput, calls=%fused_computation.49 | convolution fusion | flops 1069039616 | bytes 6571265 | tf_op jit(solution)/shard_map/dot_general | solution.py:127
  79.6 2.9 %multiply_reduce_fusion.1 = f32[2,128]{1,0:T(2,128)S(1)} fusion(bf16[2,128,1792]{2,1,0:T(8,128)(2,1)} %collective-permute-done.1, bf16[2,128,1792]{2,1,0:T(8,128)(2,1)} %collective-permute-done, pred[]{:T(512)S(6)} %eq.14), kind=kLoop, calls=%fused_computation.11 | loop fusion | flops 11009792 | bytes 1836033 | tf_op jit(solution)/shard_map/reduce_sum | solution.py:121
  82.5 4.2 %fusion.25 = f32[256,576]{0,1:T(8,128)S(1)} fusion(bf16[3584,576]{1,0:T(8,128)(2,1)S(1)} %bitcast.154, bf16[256,1792]{1,0:T(8,128)(2,1)} %bitcast.1, bf16[256,1792]{1,0:T(8,128)(2,1)} %bitcast, f32[3584]{0:T(1024)S(1)} %copy-done.13, f32[256]{0:T(256)S(1)} %rsqrt_bitcast_fusion.1, pred[]{:T(512)S(6)} %eq.14, f32[576]{0:T(1024)S(1)} %maximum_select_fusion.6), kind=kOutput, calls=%fused_computation.50 | convolution fusion | flops 1069039616 | bytes 6571265 | tf_op jit(solution)/shard_map/dot_general | solution.py:127
  89.3 6.5 %collective-permute-done.16 = bf16[2,128,576]{1,0,2:T(2,128)(2,1)S(1)} collective-permute-done((bf16[2,128,576]{1,0,2:T(2,128)(2,1)S(1)}, bf16[2,128,576]{1,0,2:T(2,128)(2,1)S(1)}, u32[]{:S(2)}, u32[]{:S(2)}) %collective-permute-start.16) | collective-permute-done | bytes 294944 | tf_op jit(solution)/shard_map/ppermute | solution.py:138
  97.1 1.7 %collective-permute-start.18 = (bf16[2,128,256]{1,0,2:T(2,128)(2,1)S(1)}, bf16[2,128,256]{1,0,2:T(2,128)(2,1)S(1)}, u32[]{:S(2)}, u32[]{:S(2)}) collective-permute-start(bf16[2,128,256]{1,0,2:T(2,128)(2,1)S(1)} %pad_maximum_fusion.7), channel_id=1, source_target_pairs={{0,2},{2,4},{4,6},{6,8},{8,10},{10,12},{12,14},{14,0},{1,3},{3,5},... | collective-permute-start | bytes 393224 | tf_op jit(solution)/shard_map/ppermute | solution.py:150
  98.9 1.6 %collective-permute-start.19 = (bf16[2,128,256]{1,0,2:T(2,128)(2,1)S(1)}, bf16[2,128,256]{1,0,2:T(2,128)(2,1)S(1)}, u32[]{:S(2)}, u32[]{:S(2)}) collective-permute-start(bf16[2,128,256]{1,0,2:T(2,128)(2,1)S(1)} %pad_maximum_fusion.7), channel_id=1, source_target_pairs={{0,4},{2,6},{4,8},{6,10},{8,12},{10,14},{12,0},{14,2},{1,5},{3,7},... | collective-permute-start | bytes 393224 | tf_op jit(solution)/shard_map/ppermute | solution.py:150
  100.4 2.5 %collective-permute-start.20 = (bf16[2,128,256]{1,0,2:T(2,128)(2,1)S(1)}, bf16[2,128,256]{1,0,2:T(2,128)(2,1)S(1)}, u32[]{:S(2)}, u32[]{:S(2)}) collective-permute-start(bf16[2,128,256]{1,0,2:T(2,128)(2,1)S(1)} %pad_maximum_fusion.7), channel_id=1, source_target_pairs={{0,6},{2,8},{4,10},{6,12},{8,14},{10,0},{12,2},{14,4},{1,7},{3,9},... | collective-permute-start | bytes 393224 | tf_op jit(solution)/shard_map/ppermute | solution.py:150
  104.1 2.8 %collective-permute-start.22 = (bf16[2,128,256]{1,0,2:T(2,128)(2,1)S(1)}, bf16[2,128,256]{1,0,2:T(2,128)(2,1)S(1)}, u32[]{:S(2)}, u32[]{:S(2)}) collective-permute-start(bf16[2,128,256]{1,0,2:T(2,128)(2,1)S(1)} %pad_maximum_fusion.7), channel_id=1, source_target_pairs={{0,10},{2,12},{4,14},{6,0},{8,2},{10,4},{12,6},{14,8},{1,11},{3,13... | collective-permute-start | bytes 393224 | tf_op jit(solution)/shard_map/ppermute | solution.py:150
  108.0 1.8 %copy.55 = bf16[2,2,64,7,128]{4,2,3,1,0:T(8,128)(2,1)S(1)} copy(bf16[2,2,64,7,128]{2,1,0,4,3:T(2,128)(2,1)S(1)} %reshape.373) | data formatting | bytes 917504 | tf_op jit(solution)/shard_map/reshape | solution.py:187
  109.8 1.4 %collective-permute-start.23 = (bf16[2,128,256]{1,0,2:T(2,128)(2,1)S(1)}, bf16[2,128,256]{1,0,2:T(2,128)(2,1)S(1)}, u32[]{:S(2)}, u32[]{:S(2)}) collective-permute-start(bf16[2,128,256]{1,0,2:T(2,128)(2,1)S(1)} %pad_maximum_fusion.7), channel_id=1, source_target_pairs={{0,12},{2,14},{4,0},{6,2},{8,4},{10,6},{12,8},{14,10},{1,13},{3,15... | collective-permute-start | bytes 393224 | tf_op jit(solution)/shard_map/ppermute | solution.py:150
  114.5 2.1 %collective-permute-done.23 = bf16[2,128,256]{1,0,2:T(2,128)(2,1)S(1)} collective-permute-done((bf16[2,128,256]{1,0,2:T(2,128)(2,1)S(1)}, bf16[2,128,256]{1,0,2:T(2,128)(2,1)S(1)}, u32[]{:S(2)}, u32[]{:S(2)}) %collective-permute-start.23) | collective-permute-done | bytes 131104 | tf_op jit(solution)/shard_map/ppermute | solution.py:150
  (174 shorter events, 36.4 us)
Async XLA Ops:
  0.0 10.8 %copy-start = (s32[2,2,2]{2,1,0:T(2,128)S(1)}, s32[2,2,2]{2,1,0:T(2,128)}, u32[]{:S(2)}) copy-start(s32[2,2,2]{2,1,0:T(2,128)} %param.20) | copy-start | bytes 100
  0.0 35.0 %collective-permute-start = (bf16[2,128,1792]{2,1,0:T(8,128)(2,1)}, bf16[2,128,1792]{2,1,0:T(8,128)(2,1)}, u32[]{:S(2)}, u32[]{:S(2)}) collective-permute-start(bf16[2,128,1792]{2,1,0:T(8,128)(2,1)} %param.11), channel_id=1, source_target_pairs={{0,16},{16,0},{1,17},{17,1},{2,18},{18,2},{3,19},{19,3},{4,20},{20... | collective-permute-start | bytes 2752520 | tf_op jit(solution)/shard_map/ppermute | solution.py:105
  3.0 31.4 %collective-permute-start.17 = (bf16[2,128,1792]{2,1,0:T(8,128)(2,1)}, bf16[2,128,1792]{2,1,0:T(8,128)(2,1)S(1)}, u32[]{:S(2)}, u32[]{:S(2)}) collective-permute-start(bf16[2,128,1792]{2,1,0:T(8,128)(2,1)} %param.11), channel_id=1, source_target_pairs={{0,1},{1,0},{2,3},{3,2},{4,5},{5,4},{6,7},{7,6},{8,9},{9,8},{10,11... | collective-permute-start | bytes 2752520 | tf_op jit(solution)/shard_map/ppermute | solution.py:104
  3.0 7.7 %copy-start.11 = (f32[128]{0:T(128)S(1)}, f32[128]{0:T(128)}, u32[]{:S(2)}) copy-start(f32[128]{0:T(128)} %param.18) | copy-start | bytes 1540
  3.0 7.8 %copy-start.9 = (f32[896]{0:T(1024)S(1)}, f32[896]{0:T(1024)}, u32[]{:S(2)}) copy-start(f32[896]{0:T(1024)} %param.14) | copy-start | bytes 10756
  3.0 7.8 %copy-start.12 = (f32[128]{0:T(128)S(1)}, f32[128]{0:T(128)}, u32[]{:S(2)}) copy-start(f32[128]{0:T(128)} %param.16) | copy-start | bytes 1540
  3.0 7.9 %copy-start.10 = (s32[2,16,14,2]{1,3,2,0:T(2,128)S(1)}, s32[2,16,14,2]{1,3,2,0:T(2,128)}, u32[]{:S(2)}) copy-start(s32[2,16,14,2]{1,3,2,0:T(2,128)} %param.19) | copy-start | bytes 10756
  6.5 9.4 %collective-permute-start.2 = (bf16[224,576]{1,0:T(8,128)(2,1)S(1)}, bf16[224,576]{1,0:T(8,128)(2,1)}, u32[]{:S(2)}, u32[]{:S(2)}) collective-permute-start(bf16[224,576]{1,0:T(8,128)(2,1)S(1)} %get-tuple-element.9), channel_id=1, source_target_pairs={{0,4},{4,8},{8,12},{12,14},{14,10},{10,6},{6,2},{2,0},{1,5},{5,9},... | collective-permute-start | bytes 774152 | tf_op jit(solution)/shard_map/ppermute | solution.py:47
  8.1 9.4 %collective-permute-start.9 = (bf16[224,576]{1,0:T(8,128)(2,1)S(1)}, bf16[224,576]{1,0:T(8,128)(2,1)}, u32[]{:S(2)}, u32[]{:S(2)}) collective-permute-start(bf16[224,576]{1,0:T(8,128)(2,1)S(1)} %get-tuple-element.10), channel_id=1, source_target_pairs={{0,2},{4,0},{8,4},{12,8},{14,12},{10,14},{6,10},{2,6},{1,3},{5,1},... | collective-permute-start | bytes 774152 | tf_op jit(solution)/shard_map/ppermute | solution.py:48
  12.6 21.8 %copy-start.5 = (bf16[2,128,1792]{2,1,0:T(8,128)(2,1)S(1)}, bf16[2,128,1792]{2,1,0:T(8,128)(2,1)}, u32[]{:S(2)}) copy-start(bf16[2,128,1792]{2,1,0:T(8,128)(2,1)} %param.11) | copy-start | bytes 2752516
  15.9 8.7 %collective-permute-start.3 = (bf16[224,576]{1,0:T(8,128)(2,1)}, bf16[224,576]{1,0:T(8,128)(2,1)S(1)}, u32[]{:S(2)}, u32[]{:S(2)}) collective-permute-start(bf16[224,576]{1,0:T(8,128)(2,1)} %collective-permute-done.2), channel_id=1, source_target_pairs={{0,4},{4,8},{8,12},{12,14},{14,10},{10,6},{6,2},{2,0},{1,5},{5,9},... | collective-permute-start | bytes 774152 | tf_op jit(solution)/shard_map/ppermute | solution.py:47
  17.5 8.7 %collective-permute-start.10 = (bf16[224,576]{1,0:T(8,128)(2,1)}, bf16[224,576]{1,0:T(8,128)(2,1)S(1)}, u32[]{:S(2)}, u32[]{:S(2)}) collective-permute-start(bf16[224,576]{1,0:T(8,128)(2,1)} %collective-permute-done.9), channel_id=1, source_target_pairs={{0,2},{4,0},{8,4},{12,8},{14,12},{10,14},{6,10},{2,6},{1,3},{5,1},... | collective-permute-start | bytes 774152 | tf_op jit(solution)/shard_map/ppermute | solution.py:48
  24.6 7.7 %collective-permute-start.4 = (bf16[224,576]{1,0:T(8,128)(2,1)S(1)}, bf16[224,576]{1,0:T(8,128)(2,1)S(1)}, u32[]{:S(2)}, u32[]{:S(2)}) collective-permute-start(bf16[224,576]{1,0:T(8,128)(2,1)S(1)} %collective-permute-done.3), channel_id=1, source_target_pairs={{0,4},{4,8},{8,12},{12,14},{14,10},{10,6},{6,2},{2,0},{1,5},{5,9},... | collective-permute-start | bytes 774152 | tf_op jit(solution)/shard_map/ppermute | solution.py:47
  26.1 7.7 %collective-permute-start.11 = (bf16[224,576]{1,0:T(8,128)(2,1)S(1)}, bf16[224,576]{1,0:T(8,128)(2,1)S(1)}, u32[]{:S(2)}, u32[]{:S(2)}) collective-permute-start(bf16[224,576]{1,0:T(8,128)(2,1)S(1)} %collective-permute-done.10), channel_id=1, source_target_pairs={{0,2},{4,0},{8,4},{12,8},{14,12},{10,14},{6,10},{2,6},{1,3},{5,1},... | collective-permute-start | bytes 774152 | tf_op jit(solution)/shard_map/ppermute | solution.py:48
  32.2 7.0 %collective-permute-start.5 = (bf16[224,576]{1,0:T(8,128)(2,1)S(1)}, bf16[224,576]{1,0:T(8,128)(2,1)S(1)}, u32[]{:S(2)}, u32[]{:S(2)}) collective-permute-start(bf16[224,576]{1,0:T(8,128)(2,1)S(1)} %collective-permute-done.4), channel_id=1, source_target_pairs={{0,4},{4,8},{8,12},{12,14},{14,10},{10,6},{6,2},{2,0},{1,5},{5,9},... | collective-permute-start | bytes 774152 | tf_op jit(solution)/shard_map/ppermute | solution.py:47
  33.8 7.0 %collective-permute-start.12 = (bf16[224,576]{1,0:T(8,128)(2,1)S(1)}, bf16[224,576]{1,0:T(8,128)(2,1)S(1)}, u32[]{:S(2)}, u32[]{:S(2)}) collective-permute-start(bf16[224,576]{1,0:T(8,128)(2,1)S(1)} %collective-permute-done.11), channel_id=1, source_target_pairs={{0,2},{4,0},{8,4},{12,8},{14,12},{10,14},{6,10},{2,6},{1,3},{5,1},... | collective-permute-start | bytes 774152 | tf_op jit(solution)/shard_map/ppermute | solution.py:48
  34.4 23.4 %copy-start.6 = (bf16[2,128,1792]{2,1,0:T(8,128)(2,1)}, bf16[2,128,1792]{2,1,0:T(8,128)(2,1)S(1)}, u32[]{:S(2)}) copy-start(bf16[2,128,1792]{2,1,0:T(8,128)(2,1)S(1)} %collective-permute-done.17) | copy-start | bytes 2752516
  35.0 44.6 %collective-permute-start.1 = (bf16[2,128,1792]{2,1,0:T(8,128)(2,1)}, bf16[2,128,1792]{2,1,0:T(8,128)(2,1)}, u32[]{:S(2)}, u32[]{:S(2)}) collective-permute-start(bf16[2,128,1792]{2,1,0:T(8,128)(2,1)} %collective-permute-done), channel_id=1, source_target_pairs={{0,1},{1,0},{2,3},{3,2},{4,5},{5,4},{6,7},{7,6},{8,9},{9,8},{10,11... | collective-permute-start | bytes 2752520 | tf_op jit(solution)/shard_map/ppermute | solution.py:106
  39.2 8.0 %collective-permute-start.6 = (bf16[224,576]{1,0:T(8,128)(2,1)S(1)}, bf16[224,576]{1,0:T(8,128)(2,1)S(1)}, u32[]{:S(2)}, u32[]{:S(2)}) collective-permute-start(bf16[224,576]{1,0:T(8,128)(2,1)S(1)} %collective-permute-done.5), channel_id=1, source_target_pairs={{0,4},{4,8},{8,12},{12,14},{14,10},{10,6},{6,2},{2,0},{1,5},{5,9},... | collective-permute-start | bytes 774152 | tf_op jit(solution)/shard_map/ppermute | solution.py:47
  40.9 8.0 %collective-permute-start.13 = (bf16[224,576]{1,0:T(8,128)(2,1)S(1)}, bf16[224,576]{1,0:T(8,128)(2,1)S(1)}, u32[]{:S(2)}, u32[]{:S(2)}) collective-permute-start(bf16[224,576]{1,0:T(8,128)(2,1)S(1)} %collective-permute-done.12), channel_id=1, source_target_pairs={{0,2},{4,0},{8,4},{12,8},{14,12},{10,14},{6,10},{2,6},{1,3},{5,1},... | collective-permute-start | bytes 774152 | tf_op jit(solution)/shard_map/ppermute | solution.py:48
  47.2 9.0 %collective-permute-start.7 = (bf16[224,576]{1,0:T(8,128)(2,1)S(1)}, bf16[224,576]{1,0:T(8,128)(2,1)S(1)}, u32[]{:S(2)}, u32[]{:S(2)}) collective-permute-start(bf16[224,576]{1,0:T(8,128)(2,1)S(1)} %collective-permute-done.6), channel_id=1, source_target_pairs={{0,4},{4,8},{8,12},{12,14},{14,10},{10,6},{6,2},{2,0},{1,5},{5,9},... | collective-permute-start | bytes 774152 | tf_op jit(solution)/shard_map/ppermute | solution.py:47
  48.8 9.0 %collective-permute-start.14 = (bf16[224,576]{1,0:T(8,128)(2,1)S(1)}, bf16[224,576]{1,0:T(8,128)(2,1)}, u32[]{:S(2)}, u32[]{:S(2)}) collective-permute-start(bf16[224,576]{1,0:T(8,128)(2,1)S(1)} %collective-permute-done.13), channel_id=1, source_target_pairs={{0,2},{4,0},{8,4},{12,8},{14,12},{10,14},{6,10},{2,6},{1,3},{5,1},... | collective-permute-start | bytes 774152 | tf_op jit(solution)/shard_map/ppermute | solution.py:48
  56.2 6.6 %collective-permute-start.8 = (bf16[224,576]{1,0:T(8,128)(2,1)S(1)}, bf16[224,576]{1,0:T(8,128)(2,1)S(1)}, u32[]{:S(2)}, u32[]{:S(2)}) collective-permute-start(bf16[224,576]{1,0:T(8,128)(2,1)S(1)} %collective-permute-done.7), channel_id=1, source_target_pairs={{0,4},{4,8},{8,12},{12,14},{14,10},{10,6},{6,2},{2,0},{1,5},{5,9},... | collective-permute-start | bytes 774152 | tf_op jit(solution)/shard_map/ppermute | solution.py:47
  57.8 9.1 %collective-permute-start.15 = (bf16[224,576]{1,0:T(8,128)(2,1)}, bf16[224,576]{1,0:T(8,128)(2,1)}, u32[]{:S(2)}, u32[]{:S(2)}) collective-permute-start(bf16[224,576]{1,0:T(8,128)(2,1)} %collective-permute-done.14), channel_id=1, source_target_pairs={{0,2},{4,0},{8,4},{12,8},{14,12},{10,14},{6,10},{2,6},{1,3},{5,1},... | collective-permute-start | bytes 774152 | tf_op jit(solution)/shard_map/ppermute | solution.py:48
  89.0 6.8 %collective-permute-start.16 = (bf16[2,128,576]{1,0,2:T(2,128)(2,1)S(1)}, bf16[2,128,576]{1,0,2:T(2,128)(2,1)S(1)}, u32[]{:S(2)}, u32[]{:S(2)}) collective-permute-start(bf16[2,128,576]{1,0,2:T(2,128)(2,1)S(1)} %pad_maximum_fusion.5), channel_id=1, source_target_pairs={{0,16},{16,0},{1,17},{17,1},{2,18},{18,2},{3,19},{19,3},{4,20},{20... | collective-permute-start | bytes 884744 | tf_op jit(solution)/shard_map/ppermute | solution.py:138
  97.1 12.7 %collective-permute-start.18 = (bf16[2,128,256]{1,0,2:T(2,128)(2,1)S(1)}, bf16[2,128,256]{1,0,2:T(2,128)(2,1)S(1)}, u32[]{:S(2)}, u32[]{:S(2)}) collective-permute-start(bf16[2,128,256]{1,0,2:T(2,128)(2,1)S(1)} %pad_maximum_fusion.7), channel_id=1, source_target_pairs={{0,2},{2,4},{4,6},{6,8},{8,10},{10,12},{12,14},{14,0},{1,3},{3,5},... | collective-permute-start | bytes 393224 | tf_op jit(solution)/shard_map/ppermute | solution.py:150
  98.9 12.5 %collective-permute-start.19 = (bf16[2,128,256]{1,0,2:T(2,128)(2,1)S(1)}, bf16[2,128,256]{1,0,2:T(2,128)(2,1)S(1)}, u32[]{:S(2)}, u32[]{:S(2)}) collective-permute-start(bf16[2,128,256]{1,0,2:T(2,128)(2,1)S(1)} %pad_maximum_fusion.7), channel_id=1, source_target_pairs={{0,4},{2,6},{4,8},{6,10},{8,12},{10,14},{12,0},{14,2},{1,5},{3,7},... | collective-permute-start | bytes 393224 | tf_op jit(solution)/shard_map/ppermute | solution.py:150
  100.4 12.4 %collective-permute-start.20 = (bf16[2,128,256]{1,0,2:T(2,128)(2,1)S(1)}, bf16[2,128,256]{1,0,2:T(2,128)(2,1)S(1)}, u32[]{:S(2)}, u32[]{:S(2)}) collective-permute-start(bf16[2,128,256]{1,0,2:T(2,128)(2,1)S(1)} %pad_maximum_fusion.7), channel_id=1, source_target_pairs={{0,6},{2,8},{4,10},{6,12},{8,14},{10,0},{12,2},{14,4},{1,7},{3,9},... | collective-permute-start | bytes 393224 | tf_op jit(solution)/shard_map/ppermute | solution.py:150
  102.9 11.3 %collective-permute-start.21 = (bf16[2,128,256]{1,0,2:T(2,128)(2,1)S(1)}, bf16[2,128,256]{1,0,2:T(2,128)(2,1)S(1)}, u32[]{:S(2)}, u32[]{:S(2)}) collective-permute-start(bf16[2,128,256]{1,0,2:T(2,128)(2,1)S(1)} %pad_maximum_fusion.7), channel_id=1, source_target_pairs={{0,8},{2,10},{4,12},{6,14},{8,0},{10,2},{12,4},{14,6},{1,9},{3,11}... | collective-permute-start | bytes 393224 | tf_op jit(solution)/shard_map/ppermute | solution.py:150
  104.1 10.3 %collective-permute-start.22 = (bf16[2,128,256]{1,0,2:T(2,128)(2,1)S(1)}, bf16[2,128,256]{1,0,2:T(2,128)(2,1)S(1)}, u32[]{:S(2)}, u32[]{:S(2)}) collective-permute-start(bf16[2,128,256]{1,0,2:T(2,128)(2,1)S(1)} %pad_maximum_fusion.7), channel_id=1, source_target_pairs={{0,10},{2,12},{4,14},{6,0},{8,2},{10,4},{12,6},{14,8},{1,11},{3,13... | collective-permute-start | bytes 393224 | tf_op jit(solution)/shard_map/ppermute | solution.py:150
  109.8 6.8 %collective-permute-start.23 = (bf16[2,128,256]{1,0,2:T(2,128)(2,1)S(1)}, bf16[2,128,256]{1,0,2:T(2,128)(2,1)S(1)}, u32[]{:S(2)}, u32[]{:S(2)}) collective-permute-start(bf16[2,128,256]{1,0,2:T(2,128)(2,1)S(1)} %pad_maximum_fusion.7), channel_id=1, source_target_pairs={{0,12},{2,14},{4,0},{6,2},{8,4},{10,6},{12,8},{14,10},{1,13},{3,15... | collective-permute-start | bytes 393224 | tf_op jit(solution)/shard_map/ppermute | solution.py:150
  111.4 5.4 %collective-permute-start.24 = (bf16[2,128,256]{1,0,2:T(2,128)(2,1)S(1)}, bf16[2,128,256]{1,0,2:T(2,128)(2,1)S(1)}, u32[]{:S(2)}, u32[]{:S(2)}) collective-permute-start(bf16[2,128,256]{1,0,2:T(2,128)(2,1)S(1)} %pad_maximum_fusion.7), channel_id=1, source_target_pairs={{0,14},{2,0},{4,2},{6,4},{8,6},{10,8},{12,10},{14,12},{1,15},{3,1}... | collective-permute-start | bytes 393224 | tf_op jit(solution)/shard_map/ppermute | solution.py:150
  (10 other events, 40.1 us)

commit v9 on v3

--- a/solution.py
+++ b/solution.py
@@ -31,9 +31,9 @@
     return [2 * z for z in range(count // 2)] + [2 * z + 1 for z in reversed(range(count // 2))]
 
 
-def gather_rows(shard, count, here):
+def gather_rows(shard, count, here, tie=None, tie_step=0):
     if count != 8:
-        return lax.all_gather(shard, "row", axis=0, tiled=True)
+        return lax.all_gather(shard, "row", axis=0, tiled=True), tie
     order = snake_order(count)
     position = [0] * count
     for i, d in enumerate(order):
@@ -43,7 +43,9 @@
     half = shard.shape[0] // 2
     ahead, behind = shard[:half], shard[half:]
     ahead_parts, behind_parts = [ahead], [behind]
-    for _ in range(count - 1):
+    for step in range(1, count):
+        if step == tie_step:
+            ahead, tie = lax.optimization_barrier((ahead, tie))
         ahead = lax.ppermute(ahead, "row", forward)
         behind = lax.ppermute(behind, "row", backward)
         ahead_parts.append(ahead)
@@ -55,7 +57,7 @@
     joined = jnp.concatenate(
         [jnp.stack(ahead_parts)[ahead_pick], jnp.stack(behind_parts)[behind_pick]], axis=1
     )
-    return joined.reshape(count * shard.shape[0], shard.shape[1])
+    return joined.reshape(count * shard.shape[0], shard.shape[1]), tie
 
 
 def shards(
@@ -99,7 +101,6 @@
         jnp.concatenate([rotary_b[:split], value_bias[:value_split]]),
         jnp.concatenate([rotary_b[split:], value_bias[value_split:]]),
     )
-    full_panel = gather_rows(panel, row_count, here)
 
     other_half = lax.ppermute(tokens, "col", SWAP)
     partner_half = lax.ppermute(tokens, "groups", SWAP)
@@ -124,6 +125,7 @@
     )
     token_positions = (here * length + jnp.arange(length, dtype=jnp.int32)).astype(jnp.float32)
 
+    full_panel, normed = gather_rows(panel, row_count, here, normed, 6)
     summed = jnp.dot(normed, full_panel, preferred_element_type=jnp.float32) + panel_bias
     summed = summed.reshape(2 * passages, length, split + value_split)
     turned = apply_rotation(

time: 123 us -> 133 us (1.081); the launches traced: 121 us -> 133 us
  waiting for transfers between devices: 34.1 us -> 49 us
  local copies, waits for them, and re-layouts: 32.7 us -> 28 us
  matrix products: 6.82 us -> 9.5 us
    ppermute x7, waiting for transfers between devices: 0.02 us -> 21.2 us  [gather_rows(): behind = lax.ppermute(behind, 'row', backward)]
    ppermute x7, waiting for transfers between devices: 23.9 us -> 18.6 us  [gather_rows(): ahead = lax.ppermute(ahead, 'row', forward)]
    unnamed x41 -> x51, local copies, waits for them, and re-layouts: 9.93 us -> 5.37 us
    convert_element_type x1, other arithmetic: 1.09 us -> 3.11 us  [shards(): normed = (widened * lax.rsqrt(power + norm_eps) * gain).astype(jnp.bfloat...]
    select_n x1, other arithmetic: 1.95 us -> 0.43 us  [shards(): jnp.where(column == 0, jnp.concatenate([partner_half, partner_other], axi...]
    select_n x1, other arithmetic: 1.97 us -> 0.47 us  [shards(): jnp.where(column == 0, jnp.concatenate([tokens, other_half], axis=2), jnp...]
  transfers between devices with their start and end apart: 25 -> 25, of which waited for: 11 -> 11; matrix products, arithmetic and copies ran while one was open for 29% -> 18% of each run, Pallas kernels for 0% -> 0%
where the time goes in v9:
time: 133 us
  waiting for transfers between devices  49 us (37%)
  starting transfers between devices  30.3 us (23%)
  local copies, waits for them, and re-layouts  28 us (21%)
  other arithmetic  15.1 us (11%)
  matrix products  9.5 us (7%)
    ppermute x7, waiting for transfers between devices, gather_rows(): behind = lax.ppermute(behind, 'row', backward)  21.2 us
    ppermute x7, waiting for transfers between devices, gather_rows(): ahead = lax.ppermute(ahead, 'row', forward)  18.6 us
    ppermute x7, starting transfers between devices, shards(): lax.ppermute(pairs, 'row', [(i, (i + k) % row_count) for i in range(row_c...  12.6 us
    ppermute x7, starting transfers between devices, gather_rows(): ahead = lax.ppermute(ahead, 'row', forward)  11.1 us
    ppermute x1, waiting for transfers between devices, shards(): returned = lax.ppermute(result[passages:], 'groups', SWAP)  6.48 us
    unnamed x51, local copies, waits for them, and re-layouts  5.37 us
    gather x1, local copies, waits for them, and re-layouts, gather_rows(): jnp.stack(ahead_parts)[ahead_pick]  3.93 us
    ppermute x7, starting transfers between devices, gather_rows(): behind = lax.ppermute(behind, 'row', backward)  3.15 us
  transfers between devices with their start and end apart: 25, of which 11 were waited for; matrix products, arithmetic and copies ran while one was open for 18% of the time, Pallas kernels for 0%

profile of v9, /device:TPU:0, one launch (start us, length us, event | category | flops | bytes accessed | tf_op | source)
XLA Modules:
  0.0 132.8 jit_solution(4599735601127776807)
XLA Ops:
  0.0 3.0 %collective-permute-start.6 = (bf16[2,128,1792]{2,1,0:T(8,128)(2,1)}, bf16[2,128,1792]{2,1,0:T(8,128)(2,1)S(1)}, u32[]{:S(2)}, u32[]{:S(2)}) collective-permute-start(bf16[2,128,1792]{2,1,0:T(8,128)(2,1)} %param.11), channel_id=1, source_target_pairs={{0,16},{16,0},{1,17},{17,1},{2,18},{18,2},{3,19},{19,3},{4,20},{20... | collective-permute-start | bytes 2752520 | tf_op jit(solution)/shard_map/ppermute | solution.py:106
  6.5 1.6 %collective-permute-start = (bf16[224,576]{1,0:T(8,128)(2,1)S(1)}, bf16[224,576]{1,0:T(8,128)(2,1)}, u32[]{:S(2)}, u32[]{:S(2)}) collective-permute-start(bf16[224,576]{1,0:T(8,128)(2,1)S(1)} %get-tuple-element.18), channel_id=1, source_target_pairs={{0,4},{4,8},{8,12},{12,14},{14,10},{10,6},{6,2},{2,0},{1,5},{5,9},... | collective-permute-start | bytes 774152 | tf_op jit(solution)/shard_map/ppermute | solution.py:49
  12.7 3.2 %collective-permute-done = bf16[224,576]{1,0:T(8,128)(2,1)} collective-permute-done((bf16[224,576]{1,0:T(8,128)(2,1)S(1)}, bf16[224,576]{1,0:T(8,128)(2,1)}, u32[]{:S(2)}, u32[]{:S(2)}) %collective-permute-start) | collective-permute-done | bytes 258080 | tf_op jit(solution)/shard_map/ppermute | solution.py:49
  15.9 1.6 %collective-permute-start.1 = (bf16[224,576]{1,0:T(8,128)(2,1)}, bf16[224,576]{1,0:T(8,128)(2,1)S(1)}, u32[]{:S(2)}, u32[]{:S(2)}) collective-permute-start(bf16[224,576]{1,0:T(8,128)(2,1)} %collective-permute-done), channel_id=1, source_target_pairs={{0,4},{4,8},{8,12},{12,14},{14,10},{10,6},{6,2},{2,0},{1,5},{5,9},... | collective-permute-start | bytes 774152 | tf_op jit(solution)/shard_map/ppermute | solution.py:49
  20.0 4.6 %collective-permute-done.1 = bf16[224,576]{1,0:T(8,128)(2,1)S(1)} collective-permute-done((bf16[224,576]{1,0:T(8,128)(2,1)}, bf16[224,576]{1,0:T(8,128)(2,1)S(1)}, u32[]{:S(2)}, u32[]{:S(2)}) %collective-permute-start.1) | collective-permute-done | bytes 258080 | tf_op jit(solution)/shard_map/ppermute | solution.py:49
  24.6 1.6 %collective-permute-start.2 = (bf16[224,576]{1,0:T(8,128)(2,1)S(1)}, bf16[224,576]{1,0:T(8,128)(2,1)S(1)}, u32[]{:S(2)}, u32[]{:S(2)}) collective-permute-start(bf16[224,576]{1,0:T(8,128)(2,1)S(1)} %collective-permute-done.1), channel_id=1, source_target_pairs={{0,4},{4,8},{8,12},{12,14},{14,10},{10,6},{6,2},{2,0},{1,5},{5,9},... | collective-permute-start | bytes 774152 | tf_op jit(solution)/shard_map/ppermute | solution.py:49
  26.7 5.5 %collective-permute-done.2 = bf16[224,576]{1,0:T(8,128)(2,1)S(1)} collective-permute-done((bf16[224,576]{1,0:T(8,128)(2,1)S(1)}, bf16[224,576]{1,0:T(8,128)(2,1)S(1)}, u32[]{:S(2)}, u32[]{:S(2)}) %collective-permute-start.2) | collective-permute-done | bytes 258080 | tf_op jit(solution)/shard_map/ppermute | solution.py:49
  32.1 1.6 %collective-permute-start.3 = (bf16[224,576]{1,0:T(8,128)(2,1)S(1)}, bf16[224,576]{1,0:T(8,128)(2,1)S(1)}, u32[]{:S(2)}, u32[]{:S(2)}) collective-permute-start(bf16[224,576]{1,0:T(8,128)(2,1)S(1)} %collective-permute-done.2), channel_id=1, source_target_pairs={{0,4},{4,8},{8,12},{12,14},{14,10},{10,6},{6,2},{2,0},{1,5},{5,9},... | collective-permute-start | bytes 774152 | tf_op jit(solution)/shard_map/ppermute | solution.py:49
  34.4 6.6 %collective-permute-done.13 = bf16[224,576]{1,0:T(8,128)(2,1)S(1)} collective-permute-done((bf16[224,576]{1,0:T(8,128)(2,1)S(1)}, bf16[224,576]{1,0:T(8,128)(2,1)S(1)}, u32[]{:S(2)}, u32[]{:S(2)}) %collective-permute-start.13) | collective-permute-done | bytes 258080 | tf_op jit(solution)/shard_map/ppermute | solution.py:50
  41.9 1.6 %collective-permute-start.4 = (bf16[224,576]{1,0:T(8,128)(2,1)S(1)}, bf16[224,576]{1,0:T(8,128)(2,1)S(1)}, u32[]{:S(2)}, u32[]{:S(2)}) collective-permute-start(bf16[224,576]{1,0:T(8,128)(2,1)S(1)} %collective-permute-done.3), channel_id=1, source_target_pairs={{0,4},{4,8},{8,12},{12,14},{14,10},{10,6},{6,2},{2,0},{1,5},{5,9},... | collective-permute-start | bytes 774152 | tf_op jit(solution)/shard_map/ppermute | solution.py:49
  43.5 5.7 %collective-permute-done.14 = bf16[224,576]{1,0:T(8,128)(2,1)S(1)} collective-permute-done((bf16[224,576]{1,0:T(8,128)(2,1)S(1)}, bf16[224,576]{1,0:T(8,128)(2,1)S(1)}, u32[]{:S(2)}, u32[]{:S(2)}) %collective-permute-start.14) | collective-permute-done | bytes 258080 | tf_op jit(solution)/shard_map/ppermute | solution.py:50
  49.7 8.9 %collective-permute-done.15 = bf16[224,576]{1,0:T(8,128)(2,1)S(1)} collective-permute-done((bf16[224,576]{1,0:T(8,128)(2,1)S(1)}, bf16[224,576]{1,0:T(8,128)(2,1)S(1)}, u32[]{:S(2)}, u32[]{:S(2)}) %collective-permute-start.15) | collective-permute-done | bytes 258080 | tf_op jit(solution)/shard_map/ppermute | solution.py:50
  60.8 3.1 %fusion.1 = bf16[512,3584]{1,0:T(8,128)(2,1)} fusion(f32[4,128,3584]{2,1,0:T(8,128)S(1)} %maximum_convert_fusion, f32[3584]{0:T(1024)S(1)} %copy-done.8, f32[512]{0:T(512)S(1)} %rsqrt_bitcast_fusion), kind=kLoop, calls=%fused_computation.9 | loop fusion | flops 5505024 | bytes 11026432 | tf_op jit(solution)/shard_map/convert_element_type | solution.py:123
  64.0 1.6 %collective-permute-start.8 = (bf16[224,576]{1,0:T(8,128)(2,1)S(1)}, bf16[224,576]{1,0:T(8,128)(2,1)S(1)}, u32[]{:S(2)}, u32[]{:S(2)}) collective-permute-start(bf16[224,576]{1,0:T(8,128)(2,1)S(1)} %collective-permute-done.4), channel_id=1, source_target_pairs={{0,4},{4,8},{8,12},{12,14},{14,10},{10,6},{6,2},{2,0},{1,5},{5,9},... | collective-permute-start | bytes 774152 | tf_op jit(solution)/shard_map/ppermute | solution.py:49
  65.6 5.0 %collective-permute-done.8 = bf16[224,576]{1,0:T(8,128)(2,1)S(1)} collective-permute-done((bf16[224,576]{1,0:T(8,128)(2,1)S(1)}, bf16[224,576]{1,0:T(8,128)(2,1)S(1)}, u32[]{:S(2)}, u32[]{:S(2)}) %collective-permute-start.8) | collective-permute-done | bytes 258080 | tf_op jit(solution)/shard_map/ppermute | solution.py:49
  70.6 1.6 %collective-permute-start.9 = (bf16[224,576]{1,0:T(8,128)(2,1)S(1)}, bf16[224,576]{1,0:T(8,128)(2,1)}, u32[]{:S(2)}, u32[]{:S(2)}) collective-permute-start(bf16[224,576]{1,0:T(8,128)(2,1)S(1)} %collective-permute-done.8), channel_id=1, source_target_pairs={{0,4},{4,8},{8,12},{12,14},{14,10},{10,6},{6,2},{2,0},{1,5},{5,9},... | collective-permute-start | bytes 774152 | tf_op jit(solution)/shard_map/ppermute | solution.py:49
  72.2 1.4 %copy-done.5 = bf16[8,224,576]{2,1,0:T(8,128)(2,1)} copy-done((bf16[8,224,576]{2,1,0:T(8,128)(2,1)}, bf16[8,224,576]{2,1,0:T(8,128)(2,1)S(1)}, u32[]{:S(2)}) %copy-start.5) | copy-done | bytes 2064408
  73.7 2.6 %gather_fusion.1 = bf16[8,224,576]{2,1,0:T(8,128)(2,1)S(1)} fusion(bf16[8,224,576]{2,1,0:T(8,128)(2,1)} %copy-done.5, s32[1024]{0:T(1024)S(1)} %get-tuple-element.31), kind=kCustom, calls=%fused_computation.1 | custom fusion | bytes 4128800 | tf_op jit(solution)/shard_map/gather | solution.py:58
  77.3 1.7 %bitcast_dynamic-update-slice_fusion.8 = bf16[8,224,576]{2,1,0:T(8,128)(2,1)} fusion(bf16[8,224,576]{2,1,0:T(8,128)(2,1)} %bitcast_dynamic-update-slice_fusion.9, bf16[224,576]{1,0:T(8,128)(2,1)} %collective-permute-done.9), kind=kLoop, calls=%fused_computation.70 | loop fusion | bytes 573440 | tf_op jit(solution)/shard_map/stack | solution.py:58
  79.0 3.9 %gather_fusion = bf16[8,224,576]{2,1,0:T(8,128)(2,1)} fusion(bf16[8,224,576]{2,1,0:T(8,128)(2,1)} %bitcast_dynamic-update-slice_fusion.8, s32[1024]{0:T(1024)S(1)} %get-tuple-element.32), kind=kCustom, calls=%fused_computation | custom fusion | bytes 4128800 | tf_op jit(solution)/shard_map/gather | solution.py:58
  83.0 2.2 %pad_maximum_fusion = bf16[8,448,576]{2,1,0:T(8,128)(2,1)S(1)} fusion(bf16[8,224,576]{2,1,0:T(8,128)(2,1)S(1)} %gather_fusion.1, bf16[8,224,576]{2,1,0:T(8,128)(2,1)} %gather_fusion), kind=kLoop, calls=%fused_computation.11 | loop fusion | flops 8257536 | bytes 8257536 | tf_op jit(solution)/shard_map/concatenate | solution.py:57
  85.7 2.4 %convolution_add_fusion = f32[512,576]{0,1:T(8,128)S(1)} fusion(bf16[512,3584]{1,0:T(8,128)(2,1)S(1)} %copy-done.3, bf16[3584,576]{1,0:T(8,128)(2,1)S(1)} %bitcast.142, f32[576]{0:T(1024)S(1)} %maximum_select_fusion.2), kind=kOutput, calls=%fused_computation.29 | convolution fusion | flops 2114224128 | bytes 8980736 | tf_op jit(solution)/shard_map/dot_general | solution.py:129
  90.6 6.5 %collective-permute-done.17 = bf16[2,128,576]{1,0,2:T(2,128)(2,1)S(1)} collective-permute-done((bf16[2,128,576]{1,0,2:T(2,128)(2,1)S(1)}, bf16[2,128,576]{1,0,2:T(2,128)(2,1)S(1)}, u32[]{:S(2)}, u32[]{:S(2)}) %collective-permute-start.17) | collective-permute-done | bytes 294944 | tf_op jit(solution)/shard_map/ppermute | solution.py:140
  97.9 1.5 %collective-permute-start.18 = (bf16[2,128,256]{1,0,2:T(2,128)(2,1)S(1)}, bf16[2,128,256]{1,0,2:T(2,128)(2,1)}, u32[]{:S(2)}, u32[]{:S(2)}) collective-permute-start(bf16[2,128,256]{1,0,2:T(2,128)(2,1)S(1)} %pad_maximum_fusion.5), channel_id=1, source_target_pairs={{0,2},{2,4},{4,6},{6,8},{8,10},{10,12},{12,14},{14,0},{1,3},{3,5},... | collective-permute-start | bytes 393224 | tf_op jit(solution)/shard_map/ppermute | solution.py:151
  99.5 1.6 %collective-permute-start.19 = (bf16[2,128,256]{1,0,2:T(2,128)(2,1)S(1)}, bf16[2,128,256]{1,0,2:T(2,128)(2,1)S(1)}, u32[]{:S(2)}, u32[]{:S(2)}) collective-permute-start(bf16[2,128,256]{1,0,2:T(2,128)(2,1)S(1)} %pad_maximum_fusion.5), channel_id=1, source_target_pairs={{0,4},{2,6},{4,8},{6,10},{8,12},{10,14},{12,0},{14,2},{1,5},{3,7},... | collective-permute-start | bytes 393224 | tf_op jit(solution)/shard_map/ppermute | solution.py:151
  101.1 2.6 %collective-permute-start.20 = (bf16[2,128,256]{1,0,2:T(2,128)(2,1)S(1)}, bf16[2,128,256]{1,0,2:T(2,128)(2,1)S(1)}, u32[]{:S(2)}, u32[]{:S(2)}) collective-permute-start(bf16[2,128,256]{1,0,2:T(2,128)(2,1)S(1)} %pad_maximum_fusion.5), channel_id=1, source_target_pairs={{0,6},{2,8},{4,10},{6,12},{8,14},{10,0},{12,2},{14,4},{1,7},{3,9},... | collective-permute-start | bytes 393224 | tf_op jit(solution)/shard_map/ppermute | solution.py:151
  104.9 2.6 %collective-permute-start.22 = (bf16[2,128,256]{1,0,2:T(2,128)(2,1)S(1)}, bf16[2,128,256]{1,0,2:T(2,128)(2,1)S(1)}, u32[]{:S(2)}, u32[]{:S(2)}) collective-permute-start(bf16[2,128,256]{1,0,2:T(2,128)(2,1)S(1)} %pad_maximum_fusion.5), channel_id=1, source_target_pairs={{0,10},{2,12},{4,14},{6,0},{8,2},{10,4},{12,6},{14,8},{1,11},{3,13... | collective-permute-start | bytes 393224 | tf_op jit(solution)/shard_map/ppermute | solution.py:151
  109.0 1.8 %copy.51 = bf16[2,2,64,7,128]{4,2,3,1,0:T(8,128)(2,1)S(1)} copy(bf16[2,2,64,7,128]{2,1,0,4,3:T(2,128)(2,1)S(1)} %reshape.340) | data formatting | bytes 917504 | tf_op jit(solution)/shard_map/reshape | solution.py:188
  113.3 1.7 %collective-permute-start.24 = (bf16[2,128,256]{1,0,2:T(2,128)(2,1)S(1)}, bf16[2,128,256]{1,0,2:T(2,128)(2,1)S(1)}, u32[]{:S(2)}, u32[]{:S(2)}) collective-permute-start(bf16[2,128,256]{1,0,2:T(2,128)(2,1)S(1)} %pad_maximum_fusion.5), channel_id=1, source_target_pairs={{0,14},{2,0},{4,2},{6,4},{8,6},{10,8},{12,10},{14,12},{1,15},{3,1}... | collective-permute-start | bytes 393224 | tf_op jit(solution)/shard_map/ppermute | solution.py:151
  116.0 2.5 %collective-permute-done.24 = bf16[2,128,256]{1,0,2:T(2,128)(2,1)S(1)} collective-permute-done((bf16[2,128,256]{1,0,2:T(2,128)(2,1)S(1)}, bf16[2,128,256]{1,0,2:T(2,128)(2,1)S(1)}, u32[]{:S(2)}, u32[]{:S(2)}) %collective-permute-start.24) | collective-permute-done | bytes 131104 | tf_op jit(solution)/shard_map/ppermute | solution.py:151
  120.8 1.7 %fusion.45 = (f32[2,2,7,64]{3,2,1,0:T(8,128)S(1)}, f32[2,2,7,64,128]{4,3,2,1,0:T(8,128)}) fusion(bf16[2,2,64,7,128]{4,2,3,1,0:T(8,128)(2,1)S(1)} %copy.51, bf16[2,2,7,128,256]{4,3,2,1,0:T(8,128)(2,1)S(1)} %bitcast.145), kind=kOutput, calls=%fused_computation.154 | convolution fusion | flops 59177216 | bytes 2300928 | tf_op jit(solution)/shard_map/sqbgh,sqgwh->sqgbw/dot_general | solution.py:203
  125.1 1.6 %bitcast_reduce_fusion = (f32[2,2,7,64]{3,2,1,0:T(8,128)S(1)}, f32[2,2,192,64,7]{2,3,4,1,0:T(8,128)S(1)}) fusion(pred[2,192]{1,0:T(4,128)(4,1)S(1)} %broadcast_in_dim.31, bf16[2,2,64,7,128]{4,2,3,1,0:T(8,128)(2,1)S(1)} %copy.51, bf16[2,2,192,256]{3,2,1,0:T(8,128)(2,1)} %bitcast.150), kind=kOutput, calls=%fused_computation.16 | convolution fusion | flops 89110784 | bytes 2039168 | tf_op jit(solution)/shard_map/sqbgh,sqwh->sqgbw/dot_general | solution.py:191
  (166 shorter events, 36.9 us)
Async XLA Ops:
  0.0 11.1 %copy-start = (s32[2,2,2]{2,1,0:T(2,128)S(1)}, s32[2,2,2]{2,1,0:T(2,128)}, u32[]{:S(2)}) copy-start(s32[2,2,2]{2,1,0:T(2,128)} %param.20) | copy-start | bytes 100
  0.0 34.3 %collective-permute-start.6 = (bf16[2,128,1792]{2,1,0:T(8,128)(2,1)}, bf16[2,128,1792]{2,1,0:T(8,128)(2,1)S(1)}, u32[]{:S(2)}, u32[]{:S(2)}) collective-permute-start(bf16[2,128,1792]{2,1,0:T(8,128)(2,1)} %param.11), channel_id=1, source_target_pairs={{0,16},{16,0},{1,17},{17,1},{2,18},{18,2},{3,19},{19,3},{4,20},{20... | collective-permute-start | bytes 2752520 | tf_op jit(solution)/shard_map/ppermute | solution.py:106
  3.0 38.4 %collective-permute-start.5 = (bf16[2,128,1792]{2,1,0:T(8,128)(2,1)}, bf16[2,128,1792]{2,1,0:T(8,128)(2,1)S(1)}, u32[]{:S(2)}, u32[]{:S(2)}) collective-permute-start(bf16[2,128,1792]{2,1,0:T(8,128)(2,1)} %param.11), channel_id=1, source_target_pairs={{0,1},{1,0},{2,3},{3,2},{4,5},{5,4},{6,7},{7,6},{8,9},{9,8},{10,11... | collective-permute-start | bytes 2752520 | tf_op jit(solution)/shard_map/ppermute | solution.py:105
  3.0 7.7 %copy-start.11 = (f32[128]{0:T(128)S(1)}, f32[128]{0:T(128)}, u32[]{:S(2)}) copy-start(f32[128]{0:T(128)} %param.18) | copy-start | bytes 1540
  3.0 7.8 %copy-start.9 = (f32[896]{0:T(1024)S(1)}, f32[896]{0:T(1024)}, u32[]{:S(2)}) copy-start(f32[896]{0:T(1024)} %param.14) | copy-start | bytes 10756
  3.0 7.8 %copy-start.12 = (f32[128]{0:T(128)S(1)}, f32[128]{0:T(128)}, u32[]{:S(2)}) copy-start(f32[128]{0:T(128)} %param.16) | copy-start | bytes 1540
  3.0 7.8 %copy-start.10 = (s32[2,16,14,2]{1,3,2,0:T(2,128)S(1)}, s32[2,16,14,2]{1,3,2,0:T(2,128)}, u32[]{:S(2)}) copy-start(s32[2,16,14,2]{1,3,2,0:T(2,128)} %param.19) | copy-start | bytes 10756
  4.1 7.2 %slice-start = ((f32[896]{0:T(1024)}), f32[512]{0:T(512)S(1)}, s32[]{:S(2)}) async-start(f32[896]{0:T(1024)} %param.14), calls=%async_computation | async-start | bytes 4096 | tf_op jit(solution)/shard_map/slice | solution.py:101
  6.5 9.4 %collective-permute-start = (bf16[224,576]{1,0:T(8,128)(2,1)S(1)}, bf16[224,576]{1,0:T(8,128)(2,1)}, u32[]{:S(2)}, u32[]{:S(2)}) collective-permute-start(bf16[224,576]{1,0:T(8,128)(2,1)S(1)} %get-tuple-element.18), channel_id=1, source_target_pairs={{0,4},{4,8},{8,12},{12,14},{14,10},{10,6},{6,2},{2,0},{1,5},{5,9},... | collective-permute-start | bytes 774152 | tf_op jit(solution)/shard_map/ppermute | solution.py:49
  8.1 9.4 %collective-permute-start.10 = (bf16[224,576]{1,0:T(8,128)(2,1)S(1)}, bf16[224,576]{1,0:T(8,128)(2,1)}, u32[]{:S(2)}, u32[]{:S(2)}) collective-permute-start(bf16[224,576]{1,0:T(8,128)(2,1)S(1)} %get-tuple-element.17), channel_id=1, source_target_pairs={{0,2},{4,0},{8,4},{12,8},{14,12},{10,14},{6,10},{2,6},{1,3},{5,1},... | collective-permute-start | bytes 774152 | tf_op jit(solution)/shard_map/ppermute | solution.py:50
  12.6 28.8 %copy-start.6 = (bf16[2,128,1792]{2,1,0:T(8,128)(2,1)S(1)}, bf16[2,128,1792]{2,1,0:T(8,128)(2,1)}, u32[]{:S(2)}) copy-start(bf16[2,128,1792]{2,1,0:T(8,128)(2,1)} %param.11) | copy-start | bytes 2752516
  15.9 8.7 %collective-permute-start.1 = (bf16[224,576]{1,0:T(8,128)(2,1)}, bf16[224,576]{1,0:T(8,128)(2,1)S(1)}, u32[]{:S(2)}, u32[]{:S(2)}) collective-permute-start(bf16[224,576]{1,0:T(8,128)(2,1)} %collective-permute-done), channel_id=1, source_target_pairs={{0,4},{4,8},{8,12},{12,14},{14,10},{10,6},{6,2},{2,0},{1,5},{5,9},... | collective-permute-start | bytes 774152 | tf_op jit(solution)/shard_map/ppermute | solution.py:49
  17.5 8.7 %collective-permute-start.11 = (bf16[224,576]{1,0:T(8,128)(2,1)}, bf16[224,576]{1,0:T(8,128)(2,1)S(1)}, u32[]{:S(2)}, u32[]{:S(2)}) collective-permute-start(bf16[224,576]{1,0:T(8,128)(2,1)} %collective-permute-done.10), channel_id=1, source_target_pairs={{0,2},{4,0},{8,4},{12,8},{14,12},{10,14},{6,10},{2,6},{1,3},{5,1},... | collective-permute-start | bytes 774152 | tf_op jit(solution)/shard_map/ppermute | solution.py:50
  24.6 7.6 %collective-permute-start.2 = (bf16[224,576]{1,0:T(8,128)(2,1)S(1)}, bf16[224,576]{1,0:T(8,128)(2,1)S(1)}, u32[]{:S(2)}, u32[]{:S(2)}) collective-permute-start(bf16[224,576]{1,0:T(8,128)(2,1)S(1)} %collective-permute-done.1), channel_id=1, source_target_pairs={{0,4},{4,8},{8,12},{12,14},{14,10},{10,6},{6,2},{2,0},{1,5},{5,9},... | collective-permute-start | bytes 774152 | tf_op jit(solution)/shard_map/ppermute | solution.py:49
  26.2 7.6 %collective-permute-start.12 = (bf16[224,576]{1,0:T(8,128)(2,1)S(1)}, bf16[224,576]{1,0:T(8,128)(2,1)S(1)}, u32[]{:S(2)}, u32[]{:S(2)}) collective-permute-start(bf16[224,576]{1,0:T(8,128)(2,1)S(1)} %collective-permute-done.11), channel_id=1, source_target_pairs={{0,2},{4,0},{8,4},{12,8},{14,12},{10,14},{6,10},{2,6},{1,3},{5,1},... | collective-permute-start | bytes 774152 | tf_op jit(solution)/shard_map/ppermute | solution.py:50
  32.1 9.7 %collective-permute-start.3 = (bf16[224,576]{1,0:T(8,128)(2,1)S(1)}, bf16[224,576]{1,0:T(8,128)(2,1)S(1)}, u32[]{:S(2)}, u32[]{:S(2)}) collective-permute-start(bf16[224,576]{1,0:T(8,128)(2,1)S(1)} %collective-permute-done.2), channel_id=1, source_target_pairs={{0,4},{4,8},{8,12},{12,14},{14,10},{10,6},{6,2},{2,0},{1,5},{5,9},... | collective-permute-start | bytes 774152 | tf_op jit(solution)/shard_map/ppermute | solution.py:49
  33.7 7.2 %collective-permute-start.13 = (bf16[224,576]{1,0:T(8,128)(2,1)S(1)}, bf16[224,576]{1,0:T(8,128)(2,1)S(1)}, u32[]{:S(2)}, u32[]{:S(2)}) collective-permute-start(bf16[224,576]{1,0:T(8,128)(2,1)S(1)} %collective-permute-done.12), channel_id=1, source_target_pairs={{0,2},{4,0},{8,4},{12,8},{14,12},{10,14},{6,10},{2,6},{1,3},{5,1},... | collective-permute-start | bytes 774152 | tf_op jit(solution)/shard_map/ppermute | solution.py:50
  34.3 24.8 %collective-permute-start.7 = (bf16[2,128,1792]{2,1,0:T(8,128)(2,1)S(1)}, bf16[2,128,1792]{2,1,0:T(8,128)(2,1)S(1)}, u32[]{:S(2)}, u32[]{:S(2)}) collective-permute-start(bf16[2,128,1792]{2,1,0:T(8,128)(2,1)S(1)} %collective-permute-done.6), channel_id=1, source_target_pairs={{0,1},{1,0},{2,3},{3,2},{4,5},{5,4},{6,7},{7,6},{8,9},{9,8},{10,11... | collective-permute-start | bytes 2752520 | tf_op jit(solution)/shard_map/ppermute | solution.py:107
  40.9 8.3 %collective-permute-start.14 = (bf16[224,576]{1,0:T(8,128)(2,1)S(1)}, bf16[224,576]{1,0:T(8,128)(2,1)S(1)}, u32[]{:S(2)}, u32[]{:S(2)}) collective-permute-start(bf16[224,576]{1,0:T(8,128)(2,1)S(1)} %collective-permute-done.13), channel_id=1, source_target_pairs={{0,2},{4,0},{8,4},{12,8},{14,12},{10,14},{6,10},{2,6},{1,3},{5,1},... | collective-permute-start | bytes 774152 | tf_op jit(solution)/shard_map/ppermute | solution.py:50
  41.9 22.1 %collective-permute-start.4 = (bf16[224,576]{1,0:T(8,128)(2,1)S(1)}, bf16[224,576]{1,0:T(8,128)(2,1)S(1)}, u32[]{:S(2)}, u32[]{:S(2)}) collective-permute-start(bf16[224,576]{1,0:T(8,128)(2,1)S(1)} %collective-permute-done.3), channel_id=1, source_target_pairs={{0,4},{4,8},{8,12},{12,14},{14,10},{10,6},{6,2},{2,0},{1,5},{5,9},... | collective-permute-start | bytes 774152 | tf_op jit(solution)/shard_map/ppermute | solution.py:49
  49.2 9.4 %collective-permute-start.15 = (bf16[224,576]{1,0:T(8,128)(2,1)S(1)}, bf16[224,576]{1,0:T(8,128)(2,1)S(1)}, u32[]{:S(2)}, u32[]{:S(2)}) collective-permute-start(bf16[224,576]{1,0:T(8,128)(2,1)S(1)} %collective-permute-done.14), channel_id=1, source_target_pairs={{0,2},{4,0},{8,4},{12,8},{14,12},{10,14},{6,10},{2,6},{1,3},{5,1},... | collective-permute-start | bytes 774152 | tf_op jit(solution)/shard_map/ppermute | solution.py:50
  58.6 13.5 %collective-permute-start.16 = (bf16[224,576]{1,0:T(8,128)(2,1)S(1)}, bf16[224,576]{1,0:T(8,128)(2,1)S(1)}, u32[]{:S(2)}, u32[]{:S(2)}) collective-permute-start(bf16[224,576]{1,0:T(8,128)(2,1)S(1)} %collective-permute-done.15), channel_id=1, source_target_pairs={{0,2},{4,0},{8,4},{12,8},{14,12},{10,14},{6,10},{2,6},{1,3},{5,1},... | collective-permute-start | bytes 774152 | tf_op jit(solution)/shard_map/ppermute | solution.py:50
  64.0 6.6 %collective-permute-start.8 = (bf16[224,576]{1,0:T(8,128)(2,1)S(1)}, bf16[224,576]{1,0:T(8,128)(2,1)S(1)}, u32[]{:S(2)}, u32[]{:S(2)}) collective-permute-start(bf16[224,576]{1,0:T(8,128)(2,1)S(1)} %collective-permute-done.4), channel_id=1, source_target_pairs={{0,4},{4,8},{8,12},{12,14},{14,10},{10,6},{6,2},{2,0},{1,5},{5,9},... | collective-permute-start | bytes 774152 | tf_op jit(solution)/shard_map/ppermute | solution.py:49
  70.6 6.7 %collective-permute-start.9 = (bf16[224,576]{1,0:T(8,128)(2,1)S(1)}, bf16[224,576]{1,0:T(8,128)(2,1)}, u32[]{:S(2)}, u32[]{:S(2)}) collective-permute-start(bf16[224,576]{1,0:T(8,128)(2,1)S(1)} %collective-permute-done.8), channel_id=1, source_target_pairs={{0,4},{4,8},{8,12},{12,14},{14,10},{10,6},{6,2},{2,0},{1,5},{5,9},... | collective-permute-start | bytes 774152 | tf_op jit(solution)/shard_map/ppermute | solution.py:49
  90.3 6.8 %collective-permute-start.17 = (bf16[2,128,576]{1,0,2:T(2,128)(2,1)S(1)}, bf16[2,128,576]{1,0,2:T(2,128)(2,1)S(1)}, u32[]{:S(2)}, u32[]{:S(2)}) collective-permute-start(bf16[2,128,576]{1,0,2:T(2,128)(2,1)S(1)} %fusion.24), channel_id=1, source_target_pairs={{0,16},{16,0},{1,17},{17,1},{2,18},{18,2},{3,19},{19,3},{4,20},{20... | collective-permute-start | bytes 884744 | tf_op jit(solution)/shard_map/ppermute | solution.py:140
  97.9 12.9 %collective-permute-start.18 = (bf16[2,128,256]{1,0,2:T(2,128)(2,1)S(1)}, bf16[2,128,256]{1,0,2:T(2,128)(2,1)}, u32[]{:S(2)}, u32[]{:S(2)}) collective-permute-start(bf16[2,128,256]{1,0,2:T(2,128)(2,1)S(1)} %pad_maximum_fusion.5), channel_id=1, source_target_pairs={{0,2},{2,4},{4,6},{6,8},{8,10},{10,12},{12,14},{14,0},{1,3},{3,5},... | collective-permute-start | bytes 393224 | tf_op jit(solution)/shard_map/ppermute | solution.py:151
  99.5 13.8 %collective-permute-start.19 = (bf16[2,128,256]{1,0,2:T(2,128)(2,1)S(1)}, bf16[2,128,256]{1,0,2:T(2,128)(2,1)S(1)}, u32[]{:S(2)}, u32[]{:S(2)}) collective-permute-start(bf16[2,128,256]{1,0,2:T(2,128)(2,1)S(1)} %pad_maximum_fusion.5), channel_id=1, source_target_pairs={{0,4},{2,6},{4,8},{6,10},{8,12},{10,14},{12,0},{14,2},{1,5},{3,7},... | collective-permute-start | bytes 393224 | tf_op jit(solution)/shard_map/ppermute | solution.py:151
  101.1 14.1 %collective-permute-start.20 = (bf16[2,128,256]{1,0,2:T(2,128)(2,1)S(1)}, bf16[2,128,256]{1,0,2:T(2,128)(2,1)S(1)}, u32[]{:S(2)}, u32[]{:S(2)}) collective-permute-start(bf16[2,128,256]{1,0,2:T(2,128)(2,1)S(1)} %pad_maximum_fusion.5), channel_id=1, source_target_pairs={{0,6},{2,8},{4,10},{6,12},{8,14},{10,0},{12,2},{14,4},{1,7},{3,9},... | collective-permute-start | bytes 393224 | tf_op jit(solution)/shard_map/ppermute | solution.py:151
  103.6 11.7 %collective-permute-start.21 = (bf16[2,128,256]{1,0,2:T(2,128)(2,1)S(1)}, bf16[2,128,256]{1,0,2:T(2,128)(2,1)S(1)}, u32[]{:S(2)}, u32[]{:S(2)}) collective-permute-start(bf16[2,128,256]{1,0,2:T(2,128)(2,1)S(1)} %pad_maximum_fusion.5), channel_id=1, source_target_pairs={{0,8},{2,10},{4,12},{6,14},{8,0},{10,2},{12,4},{14,6},{1,9},{3,11}... | collective-permute-start | bytes 393224 | tf_op jit(solution)/shard_map/ppermute | solution.py:151
  104.9 10.6 %collective-permute-start.22 = (bf16[2,128,256]{1,0,2:T(2,128)(2,1)S(1)}, bf16[2,128,256]{1,0,2:T(2,128)(2,1)S(1)}, u32[]{:S(2)}, u32[]{:S(2)}) collective-permute-start(bf16[2,128,256]{1,0,2:T(2,128)(2,1)S(1)} %pad_maximum_fusion.5), channel_id=1, source_target_pairs={{0,10},{2,12},{4,14},{6,0},{8,2},{10,4},{12,6},{14,8},{1,11},{3,13... | collective-permute-start | bytes 393224 | tf_op jit(solution)/shard_map/ppermute | solution.py:151
  110.9 5.0 %collective-permute-start.23 = (bf16[2,128,256]{1,0,2:T(2,128)(2,1)S(1)}, bf16[2,128,256]{1,0,2:T(2,128)(2,1)S(1)}, u32[]{:S(2)}, u32[]{:S(2)}) collective-permute-start(bf16[2,128,256]{1,0,2:T(2,128)(2,1)S(1)} %pad_maximum_fusion.5), channel_id=1, source_target_pairs={{0,12},{2,14},{4,0},{6,2},{8,4},{10,6},{12,8},{14,10},{1,13},{3,15... | collective-permute-start | bytes 393224 | tf_op jit(solution)/shard_map/ppermute | solution.py:151
  113.3 5.2 %collective-permute-start.24 = (bf16[2,128,256]{1,0,2:T(2,128)(2,1)S(1)}, bf16[2,128,256]{1,0,2:T(2,128)(2,1)S(1)}, u32[]{:S(2)}, u32[]{:S(2)}) collective-permute-start(bf16[2,128,256]{1,0,2:T(2,128)(2,1)S(1)} %pad_maximum_fusion.5), channel_id=1, source_target_pairs={{0,14},{2,0},{4,2},{6,4},{8,6},{10,8},{12,10},{14,12},{1,15},{3,1}... | collective-permute-start | bytes 393224 | tf_op jit(solution)/shard_map/ppermute | solution.py:151
  (9 other events, 30.2 us)

commit v10 on v3

--- a/solution.py
+++ b/solution.py
@@ -144,13 +144,21 @@
     value_rows = jnp.concatenate([low[..., split:], high[..., split:]], axis=-1)
 
     pairs = jnp.concatenate([key, value_rows], axis=-1)
-    if row_count <= 8:
-        by_shift = [pairs] + [
-            lax.ppermute(pairs, "row", [(i, (i + k) % row_count) for i in range(row_count)])
-            for k in range(1, row_count)
+    if row_count == 8:
+        beside = lax.ppermute(pairs, "row", [(i, i ^ 1) for i in range(row_count)])
+        couple = jnp.where(
+            here % 2 == 0, jnp.stack([pairs, beside]), jnp.stack([beside, pairs])
+        )
+        lines = row_count // 2
+        by_shift = [couple] + [
+            lax.ppermute(
+                couple, "row", [(i, (i + 2 * k) % row_count) for i in range(row_count)]
+            )
+            for k in range(1, lines)
         ]
         gathered = jnp.stack(by_shift)
-        owner_slot = (here - jnp.arange(row_count, dtype=jnp.int32)) % row_count
+        rows = jnp.arange(row_count, dtype=jnp.int32)
+        owner_slot = ((here // 2 - rows // 2) % lines) * 2 + rows % 2
     else:
         gathered = lax.all_gather(pairs, "row", axis=0, tiled=False)
         owner_slot = jnp.arange(row_count, dtype=jnp.int32)

time: 123 us -> 127 us (1.033)
  waiting for transfers between devices: 34.1 us -> 41.5 us
  starting transfers between devices: 30.3 us -> 24.7 us
  other arithmetic: 16.1 us -> 19.3 us
    ppermute x7 -> x4, waiting for transfers between devices: 3.75 us -> 10.5 us  [the longest x3 8.13 us: shards(): lax.ppermute(couple, 'row', [(i, (i + 2 * k) % row_count) for i in range(...]
    ppermute x7 -> x4, starting transfers between devices: 12.6 us -> 7.13 us  [the longest x3 5.57 us: shards(): lax.ppermute(couple, 'row', [(i, (i + 2 * k) % row_count) for i in range(...]
    another operation x0 -> x3, other arithmetic: none -> 2.31 us  [the longest x1 1.93 us: shards(): gathered = jnp.stack(by_shift)]
    unnamed x41 -> x34, local copies, waits for them, and re-layouts: 9.93 us -> 9.74 us
  transfers between devices with their start and end apart: 25 -> 22, of which waited for: 11 -> 11; matrix products, arithmetic and copies ran while one was open for 29% -> 28% of each run, Pallas kernels for 0% -> 0%
where the time goes in v10:
time: 127 us; the launch traced here: 125 us
  waiting for transfers between devices  41.5 us (33%)
  local copies, waits for them, and re-layouts  32.3 us (25%)
  starting transfers between devices  24.7 us (19%)
  other arithmetic  19.3 us (15%)
  matrix products  6.8 us (5%)
    ppermute x7, waiting for transfers between devices, gather_rows(): ahead = lax.ppermute(ahead, 'row', forward)  24.8 us
    ppermute x7, starting transfers between devices, gather_rows(): ahead = lax.ppermute(ahead, 'row', forward)  11.1 us
    unnamed x34, local copies, waits for them, and re-layouts  9.74 us
    ppermute x3, waiting for transfers between devices, shards(): lax.ppermute(couple, 'row', [(i, (i + 2 * k) % row_count) for i in range(...  8.13 us
    ppermute x1, waiting for transfers between devices, shards(): returned = lax.ppermute(result[passages:], 'groups', SWAP)  6.16 us
    ppermute x3, starting transfers between devices, shards(): lax.ppermute(couple, 'row', [(i, (i + 2 * k) % row_count) for i in range(...  5.57 us
    gather x1, local copies, waits for them, and re-layouts, gather_rows(): jnp.stack(ahead_parts)[ahead_pick]  3.9 us
    gather x1, local copies, waits for them, and re-layouts, gather_rows(): jnp.stack(behind_parts)[behind_pick]  3.9 us
  transfers between devices with their start and end apart: 22, of which 11 were waited for; matrix products, arithmetic and copies ran while one was open for 28% of the time, Pallas kernels for 0%

profile of v10, /device:TPU:0, one launch (start us, length us, event | category | flops | bytes accessed | tf_op | source)
XLA Modules:
  0.0 125.2 jit_solution(6447539880193991436)
XLA Ops:
  0.0 3.0 %collective-permute-start.1 = (bf16[2,128,1792]{2,1,0:T(8,128)(2,1)}, bf16[2,128,1792]{2,1,0:T(8,128)(2,1)S(1)}, u32[]{:S(2)}, u32[]{:S(2)}) collective-permute-start(bf16[2,128,1792]{2,1,0:T(8,128)(2,1)} %param.11), channel_id=1, source_target_pairs={{0,16},{16,0},{1,17},{17,1},{2,18},{18,2},{3,19},{19,3},{4,20},{20... | collective-permute-start | bytes 2752520 | tf_op jit(solution)/shard_map/ppermute | solution.py:105
  6.5 1.6 %collective-permute-start.3 = (bf16[224,576]{1,0:T(8,128)(2,1)S(1)}, bf16[224,576]{1,0:T(8,128)(2,1)S(1)}, u32[]{:S(2)}, u32[]{:S(2)}) collective-permute-start(bf16[224,576]{1,0:T(8,128)(2,1)S(1)} %get-tuple-element.11), channel_id=1, source_target_pairs={{0,4},{4,8},{8,12},{12,14},{14,10},{10,6},{6,2},{2,0},{1,5},{5,9},... | collective-permute-start | bytes 774152 | tf_op jit(solution)/shard_map/ppermute | solution.py:47
  12.7 3.0 %collective-permute-done.3 = bf16[224,576]{1,0:T(8,128)(2,1)S(1)} collective-permute-done((bf16[224,576]{1,0:T(8,128)(2,1)S(1)}, bf16[224,576]{1,0:T(8,128)(2,1)S(1)}, u32[]{:S(2)}, u32[]{:S(2)}) %collective-permute-start.3) | collective-permute-done | bytes 258080 | tf_op jit(solution)/shard_map/ppermute | solution.py:47
  15.8 1.6 %collective-permute-start.4 = (bf16[224,576]{1,0:T(8,128)(2,1)S(1)}, bf16[224,576]{1,0:T(8,128)(2,1)S(1)}, u32[]{:S(2)}, u32[]{:S(2)}) collective-permute-start(bf16[224,576]{1,0:T(8,128)(2,1)S(1)} %collective-permute-done.3), channel_id=1, source_target_pairs={{0,4},{4,8},{8,12},{12,14},{14,10},{10,6},{6,2},{2,0},{1,5},{5,9},... | collective-permute-start | bytes 774152 | tf_op jit(solution)/shard_map/ppermute | solution.py:47
  19.3 5.0 %collective-permute-done.4 = bf16[224,576]{1,0:T(8,128)(2,1)S(1)} collective-permute-done((bf16[224,576]{1,0:T(8,128)(2,1)S(1)}, bf16[224,576]{1,0:T(8,128)(2,1)S(1)}, u32[]{:S(2)}, u32[]{:S(2)}) %collective-permute-start.4) | collective-permute-done | bytes 258080 | tf_op jit(solution)/shard_map/ppermute | solution.py:47
  24.2 1.6 %collective-permute-start.5 = (bf16[224,576]{1,0:T(8,128)(2,1)S(1)}, bf16[224,576]{1,0:T(8,128)(2,1)S(1)}, u32[]{:S(2)}, u32[]{:S(2)}) collective-permute-start(bf16[224,576]{1,0:T(8,128)(2,1)S(1)} %collective-permute-done.4), channel_id=1, source_target_pairs={{0,4},{4,8},{8,12},{12,14},{14,10},{10,6},{6,2},{2,0},{1,5},{5,9},... | collective-permute-start | bytes 774152 | tf_op jit(solution)/shard_map/ppermute | solution.py:47
  27.7 4.1 %collective-permute-done.5 = bf16[224,576]{1,0:T(8,128)(2,1)S(1)} collective-permute-done((bf16[224,576]{1,0:T(8,128)(2,1)S(1)}, bf16[224,576]{1,0:T(8,128)(2,1)S(1)}, u32[]{:S(2)}, u32[]{:S(2)}) %collective-permute-start.5) | collective-permute-done | bytes 258080 | tf_op jit(solution)/shard_map/ppermute | solution.py:47
  31.8 1.6 %collective-permute-start.6 = (bf16[224,576]{1,0:T(8,128)(2,1)S(1)}, bf16[224,576]{1,0:T(8,128)(2,1)S(1)}, u32[]{:S(2)}, u32[]{:S(2)}) collective-permute-start(bf16[224,576]{1,0:T(8,128)(2,1)S(1)} %collective-permute-done.5), channel_id=1, source_target_pairs={{0,4},{4,8},{8,12},{12,14},{14,10},{10,6},{6,2},{2,0},{1,5},{5,9},... | collective-permute-start | bytes 774152 | tf_op jit(solution)/shard_map/ppermute | solution.py:47
  35.3 2.0 %maximum_select_fusion = bf16[2,128,3584]{2,1,0:T(8,128)(2,1)S(1)} fusion(bf16[2,128,1792]{2,1,0:T(8,128)(2,1)} %collective-permute-done, bf16[2,128,1792]{2,1,0:T(8,128)(2,1)S(1)} %copy-done.1, pred[]{:T(512)S(6)} %eq.21), kind=kLoop, calls=%fused_computation.14 | loop fusion | flops 8257536 | bytes 3670017 | tf_op jit(solution)/shard_map/jit(_where)/select_n | solution.py:107
  38.5 1.6 %collective-permute-start.7 = (bf16[224,576]{1,0:T(8,128)(2,1)S(1)}, bf16[224,576]{1,0:T(8,128)(2,1)S(1)}, u32[]{:S(2)}, u32[]{:S(2)}) collective-permute-start(bf16[224,576]{1,0:T(8,128)(2,1)S(1)} %collective-permute-done.6), channel_id=1, source_target_pairs={{0,4},{4,8},{8,12},{12,14},{14,10},{10,6},{6,2},{2,0},{1,5},{5,9},... | collective-permute-start | bytes 774152 | tf_op jit(solution)/shard_map/ppermute | solution.py:47
  42.0 4.7 %collective-permute-done.7 = bf16[224,576]{1,0:T(8,128)(2,1)S(1)} collective-permute-done((bf16[224,576]{1,0:T(8,128)(2,1)S(1)}, bf16[224,576]{1,0:T(8,128)(2,1)S(1)}, u32[]{:S(2)}, u32[]{:S(2)}) %collective-permute-start.7) | collective-permute-done | bytes 258080 | tf_op jit(solution)/shard_map/ppermute | solution.py:47
  46.6 1.6 %collective-permute-start.8 = (bf16[224,576]{1,0:T(8,128)(2,1)S(1)}, bf16[224,576]{1,0:T(8,128)(2,1)S(1)}, u32[]{:S(2)}, u32[]{:S(2)}) collective-permute-start(bf16[224,576]{1,0:T(8,128)(2,1)S(1)} %collective-permute-done.7), channel_id=1, source_target_pairs={{0,4},{4,8},{8,12},{12,14},{14,10},{10,6},{6,2},{2,0},{1,5},{5,9},... | collective-permute-start | bytes 774152 | tf_op jit(solution)/shard_map/ppermute | solution.py:47
  50.1 3.8 %collective-permute-done.8 = bf16[224,576]{1,0:T(8,128)(2,1)S(1)} collective-permute-done((bf16[224,576]{1,0:T(8,128)(2,1)S(1)}, bf16[224,576]{1,0:T(8,128)(2,1)S(1)}, u32[]{:S(2)}, u32[]{:S(2)}) %collective-permute-start.8) | collective-permute-done | bytes 258080 | tf_op jit(solution)/shard_map/ppermute | solution.py:47
  53.9 1.6 %collective-permute-start.9 = (bf16[224,576]{1,0:T(8,128)(2,1)S(1)}, bf16[224,576]{1,0:T(8,128)(2,1)S(1)}, u32[]{:S(2)}, u32[]{:S(2)}) collective-permute-start(bf16[224,576]{1,0:T(8,128)(2,1)S(1)} %collective-permute-done.8), channel_id=1, source_target_pairs={{0,4},{4,8},{8,12},{12,14},{14,10},{10,6},{6,2},{2,0},{1,5},{5,9},... | collective-permute-start | bytes 774152 | tf_op jit(solution)/shard_map/ppermute | solution.py:47
  57.4 3.1 %collective-permute-done.9 = bf16[224,576]{1,0:T(8,128)(2,1)S(1)} collective-permute-done((bf16[224,576]{1,0:T(8,128)(2,1)S(1)}, bf16[224,576]{1,0:T(8,128)(2,1)S(1)}, u32[]{:S(2)}, u32[]{:S(2)}) %collective-permute-start.9) | collective-permute-done | bytes 258080 | tf_op jit(solution)/shard_map/ppermute | solution.py:47
  61.3 3.9 %gather_fusion = bf16[8,224,576]{2,1,0:T(8,128)(2,1)} fusion(bf16[8,224,576]{2,1,0:T(8,128)(2,1)} %bitcast_dynamic-update-slice_fusion.8, s32[1024]{0:T(1024)S(1)} %get-tuple-element.28), kind=kCustom, calls=%fused_computation | custom fusion | bytes 4128800 | tf_op jit(solution)/shard_map/gather | solution.py:56
  65.9 3.9 %gather_fusion.1 = bf16[8,224,576]{2,1,0:T(8,128)(2,1)} fusion(bf16[8,224,576]{2,1,0:T(8,128)(2,1)} %bitcast_dynamic-update-slice_fusion, s32[1024]{0:T(1024)S(1)} %get-tuple-element.27), kind=kCustom, calls=%fused_computation.1 | custom fusion | bytes 4128800 | tf_op jit(solution)/shard_map/gather | solution.py:56
  69.8 2.8 %pad_maximum_fusion = bf16[8,448,576]{2,1,0:T(8,128)(2,1)S(1)} fusion(bf16[8,224,576]{2,1,0:T(8,128)(2,1)} %gather_fusion.1, bf16[8,224,576]{2,1,0:T(8,128)(2,1)} %gather_fusion), kind=kLoop, calls=%fused_computation.12 | loop fusion | flops 8257536 | bytes 8257536 | tf_op jit(solution)/shard_map/concatenate | solution.py:55
  72.6 1.9 %maximum_select_fusion.1 = bf16[2,128,3584]{2,1,0:T(8,128)(2,1)S(1)} fusion(bf16[2,128,1792]{2,1,0:T(8,128)(2,1)} %collective-permute-done.2, bf16[2,128,1792]{2,1,0:T(8,128)(2,1)S(1)} %collective-permute-done.1, pred[]{:T(512)S(6)} %eq.21), kind=kLoop, calls=%fused_computation.15 | loop fusion | flops 8257536 | bytes 3670017 | tf_op jit(solution)/shard_map/jit(_where)/select_n | solution.py:112
  76.4 2.4 %convolution_add_fusion = f32[512,576]{0,1:T(8,128)S(1)} fusion(bf16[512,3584]{1,0:T(8,128)(2,1)S(1)} %bitcast.144, bf16[3584,576]{1,0:T(8,128)(2,1)S(1)} %bitcast.139, f32[576]{0:T(1024)S(1)} %maximum_select_fusion.2), kind=kOutput, calls=%fused_computation.30 | convolution fusion | flops 2114224128 | bytes 8980736 | tf_op jit(solution)/shard_map/dot_general | solution.py:127
  81.7 6.2 %collective-permute-done.17 = bf16[2,128,576]{1,0,2:T(2,128)(2,1)S(1)} collective-permute-done((bf16[2,128,576]{1,0,2:T(2,128)(2,1)S(1)}, bf16[2,128,576]{1,0,2:T(2,128)(2,1)S(1)}, u32[]{:S(2)}, u32[]{:S(2)}) %collective-permute-start.17) | collective-permute-done | bytes 294944 | tf_op jit(solution)/shard_map/ppermute | solution.py:138
  88.7 1.6 %collective-permute-start.18 = (bf16[2,128,256]{1,0,2:T(2,128)(2,1)S(1)}, bf16[2,128,256]{1,0,2:T(2,128)(2,1)S(1)}, u32[]{:S(2)}, u32[]{:S(2)}) collective-permute-start(bf16[2,128,256]{1,0,2:T(2,128)(2,1)S(1)} %pad_maximum_fusion.7), channel_id=1, source_target_pairs={{0,2},{2,0},{4,6},{6,4},{8,10},{10,8},{12,14},{14,12},{1,3},{3,1},... | collective-permute-start | bytes 393224 | tf_op jit(solution)/shard_map/ppermute | solution.py:148
  91.4 2.4 %collective-permute-done.18 = bf16[2,128,256]{1,0,2:T(2,128)(2,1)S(1)} collective-permute-done((bf16[2,128,256]{1,0,2:T(2,128)(2,1)S(1)}, bf16[2,128,256]{1,0,2:T(2,128)(2,1)S(1)}, u32[]{:S(2)}, u32[]{:S(2)}) %collective-permute-start.18) | collective-permute-done | bytes 131104 | tf_op jit(solution)/shard_map/ppermute | solution.py:148
  94.2 1.6 %collective-permute-start.19 = (bf16[2,2,128,256]{2,1,3,0:T(2,128)(2,1)S(1)}, bf16[2,2,128,256]{2,1,3,0:T(2,128)(2,1)S(1)}, u32[]{:S(2)}, u32[]{:S(2)}) collective-permute-start(bf16[2,2,128,256]{2,1,3,0:T(2,128)(2,1)S(1)} %broadcast_select_fusion.2), channel_id=1, source_target_pairs={{0,4},{2,6},{4,8},{6,10},{8,12},{10,14},{12,0},{14,2},{1,5},{3,7},... | collective-permute-start | bytes 786440 | tf_op jit(solution)/shard_map/ppermute | solution.py:154
  95.8 2.6 %collective-permute-start.20 = (bf16[2,2,128,256]{2,1,3,0:T(2,128)(2,1)S(1)}, bf16[2,2,128,256]{2,1,3,0:T(2,128)(2,1)S(1)}, u32[]{:S(2)}, u32[]{:S(2)}) collective-permute-start(bf16[2,2,128,256]{2,1,3,0:T(2,128)(2,1)S(1)} %broadcast_select_fusion.2), channel_id=1, source_target_pairs={{0,8},{2,10},{4,12},{6,14},{8,0},{10,2},{12,4},{14,6},{1,9},{3,11}... | collective-permute-start | bytes 786440 | tf_op jit(solution)/shard_map/ppermute | solution.py:154
  98.4 1.3 %collective-permute-start.21 = (bf16[2,2,128,256]{2,1,3,0:T(2,128)(2,1)S(1)}, bf16[2,2,128,256]{2,1,3,0:T(2,128)(2,1)S(1)}, u32[]{:S(2)}, u32[]{:S(2)}) collective-permute-start(bf16[2,2,128,256]{2,1,3,0:T(2,128)(2,1)S(1)} %broadcast_select_fusion.2), channel_id=1, source_target_pairs={{0,12},{2,14},{4,0},{6,2},{8,4},{10,6},{12,8},{14,10},{1,13},{3,15... | collective-permute-start | bytes 786440 | tf_op jit(solution)/shard_map/ppermute | solution.py:154
  100.7 1.8 %copy.37 = bf16[2,2,64,7,128]{4,2,3,1,0:T(8,128)(2,1)S(1)} copy(bf16[2,2,64,7,128]{2,1,0,4,3:T(2,128)(2,1)S(1)} %reshape.421) | data formatting | bytes 917504 | tf_op jit(solution)/shard_map/reshape | solution.py:194
  103.1 1.2 collective-permute-done.19
  104.4 6.9 %collective-permute-done.20 = bf16[2,2,128,256]{2,1,3,0:T(2,128)(2,1)S(1)} collective-permute-done((bf16[2,2,128,256]{2,1,3,0:T(2,128)(2,1)S(1)}, bf16[2,2,128,256]{2,1,3,0:T(2,128)(2,1)S(1)}, u32[]{:S(2)}, u32[]{:S(2)}) %collective-permute-start.20) | collective-permute-done | bytes 262176 | tf_op jit(solution)/shard_map/ppermute | solution.py:154
  111.3 1.9 %pad_maximum_fusion.3 = bf16[4,2,2,128,256]{3,2,4,1,0:T(2,128)(2,1)S(1)} fusion(bf16[1,2,2,128,256]{3,2,4,1,0:T(2,128)(2,1)S(1)} %bitcast.155, bf16[1,2,2,128,256]{3,2,4,1,0:T(2,128)(2,1)S(1)} %bitcast.154, bf16[1,2,2,128,256]{3,2,4,1,0:T(2,128)(2,1)S(1)} %bitcast.153, bf16[1,2,2,128,256]{3,2,4,1,0:T(2,128)(2,1)S(1)} %broadcast_select_fusion.3), kind=kLoop, calls=%fused_computation.33 | loop fusion | flops 1572864 | bytes 2097152 | tf_op jit(solution)/shard_map/stack | solution.py:159
  114.7 1.4 %gather_fusion.4 = bf16[12,64,256]{2,1,0:T(8,128)(2,1)} fusion(bf16[2,16,64,256]{3,2,0,1:T(8,128)(2,1)S(1)} %bitcast.136, s32[12]{0:T(128)S(1)} %reshape.389), kind=kCustom, calls=%fused_computation.4 | custom fusion | bytes 786528 | tf_op jit(solution)/shard_map/gather | solution.py:180
  123.9 1.3 %convert_element_type.60 = bf16[2,128,896]{2,1,0:T(8,128)(2,1)} reshape(bf16[2,2,64,7,128]{4,3,2,1,0:T(8,128)(2,1)S(1)} %copy.42) | data formatting | bytes 917504 | tf_op jit(solution)/shard_map/convert_element_type | solution.py:256
  (138 shorter events, 39.7 us)
Async XLA Ops:
  0.0 11.5 %copy-start = (s32[2,2,2]{2,1,0:T(2,128)S(1)}, s32[2,2,2]{2,1,0:T(2,128)}, u32[]{:S(2)}) copy-start(s32[2,2,2]{2,1,0:T(2,128)} %param.20) | copy-start | bytes 100
  0.0 35.3 %collective-permute-start.1 = (bf16[2,128,1792]{2,1,0:T(8,128)(2,1)}, bf16[2,128,1792]{2,1,0:T(8,128)(2,1)S(1)}, u32[]{:S(2)}, u32[]{:S(2)}) collective-permute-start(bf16[2,128,1792]{2,1,0:T(8,128)(2,1)} %param.11), channel_id=1, source_target_pairs={{0,16},{16,0},{1,17},{17,1},{2,18},{18,2},{3,19},{19,3},{4,20},{20... | collective-permute-start | bytes 2752520 | tf_op jit(solution)/shard_map/ppermute | solution.py:105
  3.0 32.3 %collective-permute-start = (bf16[2,128,1792]{2,1,0:T(8,128)(2,1)}, bf16[2,128,1792]{2,1,0:T(8,128)(2,1)}, u32[]{:S(2)}, u32[]{:S(2)}) collective-permute-start(bf16[2,128,1792]{2,1,0:T(8,128)(2,1)} %param.11), channel_id=1, source_target_pairs={{0,1},{1,0},{2,3},{3,2},{4,5},{5,4},{6,7},{7,6},{8,9},{9,8},{10,11... | collective-permute-start | bytes 2752520 | tf_op jit(solution)/shard_map/ppermute | solution.py:104
  3.0 5.8 %copy-start.9 = (s32[8]{0:T(128)S(1)}, s32[8]{0:T(128)}, u32[]{:S(2)}) copy-start(s32[8]{0:T(128)} %constant.180.clone) | copy-start | bytes 100
  3.0 7.0 %copy-start.8 = (s32[8]{0:T(128)S(1)}, s32[8]{0:T(128)}, u32[]{:S(2)}) copy-start(s32[8]{0:T(128)} %constant.181) | copy-start | bytes 100
  3.0 7.7 %copy-start.6 = (f32[128]{0:T(128)S(1)}, f32[128]{0:T(128)}, u32[]{:S(2)}) copy-start(f32[128]{0:T(128)} %param.18) | copy-start | bytes 1540
  3.0 7.8 %copy-start.4 = (f32[896]{0:T(1024)S(1)}, f32[896]{0:T(1024)}, u32[]{:S(2)}) copy-start(f32[896]{0:T(1024)} %param.14) | copy-start | bytes 10756
  3.0 7.7 %copy-start.7 = (f32[128]{0:T(128)S(1)}, f32[128]{0:T(128)}, u32[]{:S(2)}) copy-start(f32[128]{0:T(128)} %param.16) | copy-start | bytes 1540
  5.2 6.6 %slice-start = ((f32[896]{0:T(1024)}), f32[512]{0:T(512)S(1)}, s32[]{:S(2)}) async-start(f32[896]{0:T(1024)} %param.14), calls=%async_computation | async-start | bytes 4096 | tf_op jit(solution)/shard_map/slice | solution.py:99
  6.5 9.3 %collective-permute-start.3 = (bf16[224,576]{1,0:T(8,128)(2,1)S(1)}, bf16[224,576]{1,0:T(8,128)(2,1)S(1)}, u32[]{:S(2)}, u32[]{:S(2)}) collective-permute-start(bf16[224,576]{1,0:T(8,128)(2,1)S(1)} %get-tuple-element.11), channel_id=1, source_target_pairs={{0,4},{4,8},{8,12},{12,14},{14,10},{10,6},{6,2},{2,0},{1,5},{5,9},... | collective-permute-start | bytes 774152 | tf_op jit(solution)/shard_map/ppermute | solution.py:47
  8.1 9.2 %collective-permute-start.10 = (bf16[224,576]{1,0:T(8,128)(2,1)S(1)}, bf16[224,576]{1,0:T(8,128)(2,1)S(1)}, u32[]{:S(2)}, u32[]{:S(2)}) collective-permute-start(bf16[224,576]{1,0:T(8,128)(2,1)S(1)} %get-tuple-element.12), channel_id=1, source_target_pairs={{0,2},{4,0},{8,4},{12,8},{14,12},{10,14},{6,10},{2,6},{1,3},{5,1},... | collective-permute-start | bytes 774152 | tf_op jit(solution)/shard_map/ppermute | solution.py:48
  11.8 23.5 %copy-start.1 = (bf16[2,128,1792]{2,1,0:T(8,128)(2,1)S(1)}, bf16[2,128,1792]{2,1,0:T(8,128)(2,1)}, u32[]{:S(2)}) copy-start(bf16[2,128,1792]{2,1,0:T(8,128)(2,1)} %param.11) | copy-start | bytes 2752516
  15.8 8.5 %collective-permute-start.4 = (bf16[224,576]{1,0:T(8,128)(2,1)S(1)}, bf16[224,576]{1,0:T(8,128)(2,1)S(1)}, u32[]{:S(2)}, u32[]{:S(2)}) collective-permute-start(bf16[224,576]{1,0:T(8,128)(2,1)S(1)} %collective-permute-done.3), channel_id=1, source_target_pairs={{0,4},{4,8},{8,12},{12,14},{14,10},{10,6},{6,2},{2,0},{1,5},{5,9},... | collective-permute-start | bytes 774152 | tf_op jit(solution)/shard_map/ppermute | solution.py:47
  17.3 8.5 %collective-permute-start.11 = (bf16[224,576]{1,0:T(8,128)(2,1)S(1)}, bf16[224,576]{1,0:T(8,128)(2,1)S(1)}, u32[]{:S(2)}, u32[]{:S(2)}) collective-permute-start(bf16[224,576]{1,0:T(8,128)(2,1)S(1)} %collective-permute-done.10), channel_id=1, source_target_pairs={{0,2},{4,0},{8,4},{12,8},{14,12},{10,14},{6,10},{2,6},{1,3},{5,1},... | collective-permute-start | bytes 774152 | tf_op jit(solution)/shard_map/ppermute | solution.py:48
  24.2 7.6 %collective-permute-start.5 = (bf16[224,576]{1,0:T(8,128)(2,1)S(1)}, bf16[224,576]{1,0:T(8,128)(2,1)S(1)}, u32[]{:S(2)}, u32[]{:S(2)}) collective-permute-start(bf16[224,576]{1,0:T(8,128)(2,1)S(1)} %collective-permute-done.4), channel_id=1, source_target_pairs={{0,4},{4,8},{8,12},{12,14},{14,10},{10,6},{6,2},{2,0},{1,5},{5,9},... | collective-permute-start | bytes 774152 | tf_op jit(solution)/shard_map/ppermute | solution.py:47
  25.8 7.6 %collective-permute-start.12 = (bf16[224,576]{1,0:T(8,128)(2,1)S(1)}, bf16[224,576]{1,0:T(8,128)(2,1)S(1)}, u32[]{:S(2)}, u32[]{:S(2)}) collective-permute-start(bf16[224,576]{1,0:T(8,128)(2,1)S(1)} %collective-permute-done.11), channel_id=1, source_target_pairs={{0,2},{4,0},{8,4},{12,8},{14,12},{10,14},{6,10},{2,6},{1,3},{5,1},... | collective-permute-start | bytes 774152 | tf_op jit(solution)/shard_map/ppermute | solution.py:48
  31.8 6.7 %collective-permute-start.6 = (bf16[224,576]{1,0:T(8,128)(2,1)S(1)}, bf16[224,576]{1,0:T(8,128)(2,1)S(1)}, u32[]{:S(2)}, u32[]{:S(2)}) collective-permute-start(bf16[224,576]{1,0:T(8,128)(2,1)S(1)} %collective-permute-done.5), channel_id=1, source_target_pairs={{0,4},{4,8},{8,12},{12,14},{14,10},{10,6},{6,2},{2,0},{1,5},{5,9},... | collective-permute-start | bytes 774152 | tf_op jit(solution)/shard_map/ppermute | solution.py:47
  33.4 7.4 %collective-permute-start.13 = (bf16[224,576]{1,0:T(8,128)(2,1)S(1)}, bf16[224,576]{1,0:T(8,128)(2,1)S(1)}, u32[]{:S(2)}, u32[]{:S(2)}) collective-permute-start(bf16[224,576]{1,0:T(8,128)(2,1)S(1)} %collective-permute-done.12), channel_id=1, source_target_pairs={{0,2},{4,0},{8,4},{12,8},{14,12},{10,14},{6,10},{2,6},{1,3},{5,1},... | collective-permute-start | bytes 774152 | tf_op jit(solution)/shard_map/ppermute | solution.py:48
  35.3 37.3 %collective-permute-start.2 = (bf16[2,128,1792]{2,1,0:T(8,128)(2,1)S(1)}, bf16[2,128,1792]{2,1,0:T(8,128)(2,1)}, u32[]{:S(2)}, u32[]{:S(2)}) collective-permute-start(bf16[2,128,1792]{2,1,0:T(8,128)(2,1)S(1)} %collective-permute-done.1), channel_id=1, source_target_pairs={{0,1},{1,0},{2,3},{3,2},{4,5},{5,4},{6,7},{7,6},{8,9},{9,8},{10,11... | collective-permute-start | bytes 2752520 | tf_op jit(solution)/shard_map/ppermute | solution.py:106
  38.5 8.2 %collective-permute-start.7 = (bf16[224,576]{1,0:T(8,128)(2,1)S(1)}, bf16[224,576]{1,0:T(8,128)(2,1)S(1)}, u32[]{:S(2)}, u32[]{:S(2)}) collective-permute-start(bf16[224,576]{1,0:T(8,128)(2,1)S(1)} %collective-permute-done.6), channel_id=1, source_target_pairs={{0,4},{4,8},{8,12},{12,14},{14,10},{10,6},{6,2},{2,0},{1,5},{5,9},... | collective-permute-start | bytes 774152 | tf_op jit(solution)/shard_map/ppermute | solution.py:47
  40.8 8.2 %collective-permute-start.14 = (bf16[224,576]{1,0:T(8,128)(2,1)S(1)}, bf16[224,576]{1,0:T(8,128)(2,1)S(1)}, u32[]{:S(2)}, u32[]{:S(2)}) collective-permute-start(bf16[224,576]{1,0:T(8,128)(2,1)S(1)} %collective-permute-done.13), channel_id=1, source_target_pairs={{0,2},{4,0},{8,4},{12,8},{14,12},{10,14},{6,10},{2,6},{1,3},{5,1},... | collective-permute-start | bytes 774152 | tf_op jit(solution)/shard_map/ppermute | solution.py:48
  46.6 7.3 %collective-permute-start.8 = (bf16[224,576]{1,0:T(8,128)(2,1)S(1)}, bf16[224,576]{1,0:T(8,128)(2,1)S(1)}, u32[]{:S(2)}, u32[]{:S(2)}) collective-permute-start(bf16[224,576]{1,0:T(8,128)(2,1)S(1)} %collective-permute-done.7), channel_id=1, source_target_pairs={{0,4},{4,8},{8,12},{12,14},{14,10},{10,6},{6,2},{2,0},{1,5},{5,9},... | collective-permute-start | bytes 774152 | tf_op jit(solution)/shard_map/ppermute | solution.py:47
  48.9 7.3 %collective-permute-start.15 = (bf16[224,576]{1,0:T(8,128)(2,1)S(1)}, bf16[224,576]{1,0:T(8,128)(2,1)S(1)}, u32[]{:S(2)}, u32[]{:S(2)}) collective-permute-start(bf16[224,576]{1,0:T(8,128)(2,1)S(1)} %collective-permute-done.14), channel_id=1, source_target_pairs={{0,2},{4,0},{8,4},{12,8},{14,12},{10,14},{6,10},{2,6},{1,3},{5,1},... | collective-permute-start | bytes 774152 | tf_op jit(solution)/shard_map/ppermute | solution.py:48
  53.9 6.6 %collective-permute-start.9 = (bf16[224,576]{1,0:T(8,128)(2,1)S(1)}, bf16[224,576]{1,0:T(8,128)(2,1)S(1)}, u32[]{:S(2)}, u32[]{:S(2)}) collective-permute-start(bf16[224,576]{1,0:T(8,128)(2,1)S(1)} %collective-permute-done.8), channel_id=1, source_target_pairs={{0,4},{4,8},{8,12},{12,14},{14,10},{10,6},{6,2},{2,0},{1,5},{5,9},... | collective-permute-start | bytes 774152 | tf_op jit(solution)/shard_map/ppermute | solution.py:47
  56.2 9.0 %collective-permute-start.16 = (bf16[224,576]{1,0:T(8,128)(2,1)S(1)}, bf16[224,576]{1,0:T(8,128)(2,1)S(1)}, u32[]{:S(2)}, u32[]{:S(2)}) collective-permute-start(bf16[224,576]{1,0:T(8,128)(2,1)S(1)} %collective-permute-done.15), channel_id=1, source_target_pairs={{0,2},{4,0},{8,4},{12,8},{14,12},{10,14},{6,10},{2,6},{1,3},{5,1},... | collective-permute-start | bytes 774152 | tf_op jit(solution)/shard_map/ppermute | solution.py:48
  79.8 1.7 %copy-start.5 = (s32[2,16,14,2]{1,3,2,0:T(2,128)S(1)}, s32[2,16,14,2]{1,3,2,0:T(2,128)}, u32[]{:S(2)}) copy-start(s32[2,16,14,2]{1,3,2,0:T(2,128)} %param.19) | copy-start | bytes 10756
  81.1 6.8 %collective-permute-start.17 = (bf16[2,128,576]{1,0,2:T(2,128)(2,1)S(1)}, bf16[2,128,576]{1,0,2:T(2,128)(2,1)S(1)}, u32[]{:S(2)}, u32[]{:S(2)}) collective-permute-start(bf16[2,128,576]{1,0,2:T(2,128)(2,1)S(1)} %fusion.25), channel_id=1, source_target_pairs={{0,16},{16,0},{1,17},{17,1},{2,18},{18,2},{3,19},{19,3},{4,20},{20... | collective-permute-start | bytes 884744 | tf_op jit(solution)/shard_map/ppermute | solution.py:138
  88.7 5.0 %collective-permute-start.18 = (bf16[2,128,256]{1,0,2:T(2,128)(2,1)S(1)}, bf16[2,128,256]{1,0,2:T(2,128)(2,1)S(1)}, u32[]{:S(2)}, u32[]{:S(2)}) collective-permute-start(bf16[2,128,256]{1,0,2:T(2,128)(2,1)S(1)} %pad_maximum_fusion.7), channel_id=1, source_target_pairs={{0,2},{2,0},{4,6},{6,4},{8,10},{10,8},{12,14},{14,12},{1,3},{3,1},... | collective-permute-start | bytes 393224 | tf_op jit(solution)/shard_map/ppermute | solution.py:148
  94.2 10.2 %collective-permute-start.19 = (bf16[2,2,128,256]{2,1,3,0:T(2,128)(2,1)S(1)}, bf16[2,2,128,256]{2,1,3,0:T(2,128)(2,1)S(1)}, u32[]{:S(2)}, u32[]{:S(2)}) collective-permute-start(bf16[2,2,128,256]{2,1,3,0:T(2,128)(2,1)S(1)} %broadcast_select_fusion.2), channel_id=1, source_target_pairs={{0,4},{2,6},{4,8},{6,10},{8,12},{10,14},{12,0},{14,2},{1,5},{3,7},... | collective-permute-start | bytes 786440 | tf_op jit(solution)/shard_map/ppermute | solution.py:154
  95.8 15.5 %collective-permute-start.20 = (bf16[2,2,128,256]{2,1,3,0:T(2,128)(2,1)S(1)}, bf16[2,2,128,256]{2,1,3,0:T(2,128)(2,1)S(1)}, u32[]{:S(2)}, u32[]{:S(2)}) collective-permute-start(bf16[2,2,128,256]{2,1,3,0:T(2,128)(2,1)S(1)} %broadcast_select_fusion.2), channel_id=1, source_target_pairs={{0,8},{2,10},{4,12},{6,14},{8,0},{10,2},{12,4},{14,6},{1,9},{3,11}... | collective-permute-start | bytes 786440 | tf_op jit(solution)/shard_map/ppermute | solution.py:154
  98.4 12.9 %collective-permute-start.21 = (bf16[2,2,128,256]{2,1,3,0:T(2,128)(2,1)S(1)}, bf16[2,2,128,256]{2,1,3,0:T(2,128)(2,1)S(1)}, u32[]{:S(2)}, u32[]{:S(2)}) collective-permute-start(bf16[2,2,128,256]{2,1,3,0:T(2,128)(2,1)S(1)} %broadcast_select_fusion.2), channel_id=1, source_target_pairs={{0,12},{2,14},{4,0},{6,2},{8,4},{10,6},{12,8},{14,10},{1,13},{3,15... | collective-permute-start | bytes 786440 | tf_op jit(solution)/shard_map/ppermute | solution.py:154
  117.4 1.3 %copy-start.2 = (bf16[12,64,256]{2,1,0:T(8,128)(2,1)S(1)}, bf16[12,64,256]{2,1,0:T(8,128)(2,1)}, u32[]{:S(2)}) copy-start(bf16[12,64,256]{2,1,0:T(8,128)(2,1)} %gather_fusion.4) | copy-start | bytes 1179652
  (1 other events, 0.8 us)

commit v11 on v3

--- a/solution.py
+++ b/solution.py
@@ -52,8 +52,16 @@
     mine = table[here]
     ahead_pick = (mine - table) % count
     behind_pick = (table - mine) % count
+    slots = jnp.arange(count, dtype=jnp.int32)
+
+    def reorder(parts, pick):
+        stacked = jnp.stack(parts).reshape(count, -1)
+        choose = (slots[None, :] == pick[:, None]).astype(stacked.dtype)
+        moved = jnp.dot(choose, stacked, preferred_element_type=stacked.dtype)
+        return moved.reshape(count, half, shard.shape[1])
+
     joined = jnp.concatenate(
-        [jnp.stack(ahead_parts)[ahead_pick], jnp.stack(behind_parts)[behind_pick]], axis=1
+        [reorder(ahead_parts, ahead_pick), reorder(behind_parts, behind_pick)], axis=1
     )
     return joined.reshape(count * shard.shape[0], shard.shape[1])
 

time: 123 us -> 207 us (1.68)
  the two profiles are of different devices: /device:TPU:0 before, /device:TPU:11 now
where the time goes in v11:
time: 207 us; the launch traced here: 204 us
  local copies, waits for them, and re-layouts  99.2 us (48%)
  waiting for transfers between devices  48.9 us (24%)
  starting transfers between devices  27 us (13%)
  other arithmetic  17.3 us (8%)
  matrix products  10.4 us (5%)
    another operation x18, local copies, waits for them, and re-layouts, reorder(): stacked = jnp.stack(parts).reshape(count, -1)  46.7 us
    ppermute x7, waiting for transfers between devices, gather_rows(): behind = lax.ppermute(behind, 'row', backward)  25.5 us
    unnamed x58, local copies, waits for them, and re-layouts  19.7 us
    ppermute x7, waiting for transfers between devices, shards(): lax.ppermute(pairs, 'row', [(i, (i + k) % row_count) for i in range(row_c...  15.3 us
    reshape x1, local copies, waits for them, and re-layouts, gather_rows(): return joined.reshape(count * shard.shape[0], shard.shape[1])  9.21 us
    ppermute x7, starting transfers between devices, gather_rows(): behind = lax.ppermute(behind, 'row', backward)  9.13 us
    concatenate x1, local copies, waits for them, and re-layouts, gather_rows(): jnp.concatenate([reorder(ahead_parts, ahead_pick), reorder(behind_parts,...  9 us
    ppermute x7, starting transfers between devices, shards(): lax.ppermute(pairs, 'row', [(i, (i + k) % row_count) for i in range(row_c...  8.65 us
  transfers between devices with their start and end apart: 25, of which 11 were waited for; matrix products, arithmetic and copies ran while one was open for 50% of the time, Pallas kernels for 0%

profile of v11, /device:TPU:11, one launch (start us, length us, event | category | flops | bytes accessed | tf_op | source)
XLA Modules:
  0.0 203.7 jit_solution(5944669439161619294)
XLA Ops:
  8.9 5.3 %collective-permute-done.10 = bf16[224,576]{1,0:T(8,128)(2,1)S(1)} collective-permute-done((bf16[224,576]{1,0:T(8,128)(2,1)S(1)}, bf16[224,576]{1,0:T(8,128)(2,1)S(1)}, u32[]{:S(2)}, u32[]{:S(2)}) %collective-permute-start.10) | collective-permute-done | bytes 258080 | tf_op jit(solution)/shard_map/ppermute | solution.py:48
  15.8 6.2 %collective-permute-done.11 = bf16[224,576]{1,0:T(8,128)(2,1)S(1)} collective-permute-done((bf16[224,576]{1,0:T(8,128)(2,1)S(1)}, bf16[224,576]{1,0:T(8,128)(2,1)S(1)}, u32[]{:S(2)}, u32[]{:S(2)}) %collective-permute-start.11) | collective-permute-done | bytes 258080 | tf_op jit(solution)/shard_map/ppermute | solution.py:48
  23.5 5.4 %collective-permute-done.12 = bf16[224,576]{1,0:T(8,128)(2,1)S(1)} collective-permute-done((bf16[224,576]{1,0:T(8,128)(2,1)S(1)}, bf16[224,576]{1,0:T(8,128)(2,1)S(1)}, u32[]{:S(2)}, u32[]{:S(2)}) %collective-permute-start.12) | collective-permute-done | bytes 258080 | tf_op jit(solution)/shard_map/ppermute | solution.py:48
  30.4 4.5 %collective-permute-done.13 = bf16[224,576]{1,0:T(8,128)(2,1)S(1)} collective-permute-done((bf16[224,576]{1,0:T(8,128)(2,1)S(1)}, bf16[224,576]{1,0:T(8,128)(2,1)S(1)}, u32[]{:S(2)}, u32[]{:S(2)}) %collective-permute-start.13) | collective-permute-done | bytes 258080 | tf_op jit(solution)/shard_map/ppermute | solution.py:48
  36.5 4.1 %collective-permute-done.14 = bf16[224,576]{1,0:T(8,128)(2,1)} collective-permute-done((bf16[224,576]{1,0:T(8,128)(2,1)S(1)}, bf16[224,576]{1,0:T(8,128)(2,1)}, u32[]{:S(2)}, u32[]{:S(2)}) %collective-permute-start.14) | collective-permute-done | bytes 258080 | tf_op jit(solution)/shard_map/ppermute | solution.py:48
  51.3 5.5 %collective-permute-start.2 = (bf16[2,128,1792]{2,1,0:T(8,128)(2,1)}, bf16[2,128,1792]{2,1,0:T(8,128)(2,1)}, u32[]{:S(2)}, u32[]{:S(2)}) collective-permute-start(bf16[2,128,1792]{2,1,0:T(8,128)(2,1)} %collective-permute-done.1), channel_id=1, source_target_pairs={{0,1},{1,0},{2,3},{3,2},{4,5},{5,4},{6,7},{7,6},{8,9},{9,8},{10,11... | collective-permute-start | bytes 2752520 | tf_op jit(solution)/shard_map/ppermute | solution.py:114
  58.3 2.5 %maximum_select_fusion = bf16[2,128,3584]{2,1,0:T(8,128)(2,1)S(1)} fusion(bf16[2,128,1792]{2,1,0:T(8,128)(2,1)} %collective-permute-done, bf16[2,128,1792]{2,1,0:T(8,128)(2,1)} %param.11, pred[]{:T(512)S(6)} %eq.40), kind=kLoop, calls=%fused_computation.16 | loop fusion | flops 8257536 | bytes 3670017 | tf_op jit(solution)/shard_map/jit(_where)/select_n | solution.py:115
  60.8 2.1 %stack.94 = bf16[1,129024]{1,0:T(2,128)(2,1)} reshape(bf16[224,576]{1,0:T(8,128)(2,1)} %copy-done.8) | data formatting | bytes 516096 | tf_op jit(solution)/shard_map/stack | solution.py:58
  63.0 2.1 %stack.85 = bf16[1,129024]{1,0:T(2,128)(2,1)} reshape(bf16[224,576]{1,0:T(8,128)(2,1)} %copy-done.11) | data formatting | bytes 516096 | tf_op jit(solution)/shard_map/stack | solution.py:58
  65.1 2.1 %stack.95 = bf16[1,129024]{1,0:T(2,128)(2,1)} reshape(bf16[224,576]{1,0:T(8,128)(2,1)} %collective-permute-done.14) | data formatting | bytes 516096 | tf_op jit(solution)/shard_map/stack | solution.py:58
  67.2 2.1 %stack.86 = bf16[1,129024]{1,0:T(2,128)(2,1)} reshape(bf16[224,576]{1,0:T(8,128)(2,1)} %collective-permute-done.7) | data formatting | bytes 516096 | tf_op jit(solution)/shard_map/stack | solution.py:58
  69.3 2.2 %stack.96 = bf16[1,129024]{1,0:T(2,128)(2,1)} reshape(bf16[224,576]{1,0:T(8,128)(2,1)} %collective-permute-done.15) | data formatting | bytes 516096 | tf_op jit(solution)/shard_map/stack | solution.py:58
  71.5 2.1 %stack.87 = bf16[1,129024]{1,0:T(2,128)(2,1)} reshape(bf16[224,576]{1,0:T(8,128)(2,1)} %collective-permute-done.8) | data formatting | bytes 516096 | tf_op jit(solution)/shard_map/stack | solution.py:58
  73.6 2.2 %stack.97 = bf16[1,129024]{1,0:T(2,128)(2,1)} reshape(bf16[224,576]{1,0:T(8,128)(2,1)} %collective-permute-done.16) | data formatting | bytes 516096 | tf_op jit(solution)/shard_map/stack | solution.py:58
  75.8 11.5 %stack.98 = bf16[8,129024]{1,0:T(8,128)(2,1)} concatenate(bf16[1,129024]{1,0:T(2,128)(2,1)S(1)} %stack.90, bf16[1,129024]{1,0:T(2,128)(2,1)} %stack.91, bf16[1,129024]{1,0:T(2,128)(2,1)} %stack.92, bf16[1,129024]{1,0:T(2,128)(2,1)} %stack.93, bf16[1,129024]{1,0:T(2,128)(2,1)} %stack.94, bf16[1,129024]{1,0:T(2,128)(2,1)} %stack.95, bf16[1,129024]{1,0:T(2,128)(2,1)} %stack.96, ...), dimensions={0} | concatenate | bytes 4128768 | tf_op jit(solution)/shard_map/stack | solution.py:58
  87.3 3.8 %reshape.403 = bf16[1032192]{0:T(1024)(128)(2,1)} reshape(bf16[8,129024]{1,0:T(8,128)(2,1)} %stack.98) | data formatting | bytes 4128768
  91.1 5.0 %reshape.404 = bf16[8,224,576]{2,1,0:T(8,128)(2,1)} reshape(bf16[1032192]{0:T(1024)(128)(2,1)} %reshape.403) | data formatting | bytes 4128768
  96.1 2.1 %stack.88 = bf16[1,129024]{1,0:T(2,128)(2,1)} reshape(bf16[224,576]{1,0:T(8,128)(2,1)} %collective-permute-done.9) | data formatting | bytes 516096 | tf_op jit(solution)/shard_map/stack | solution.py:58
  98.2 11.2 %stack.89 = bf16[8,129024]{1,0:T(8,128)(2,1)} concatenate(bf16[1,129024]{1,0:T(2,128)(2,1)S(1)} %stack.81, bf16[1,129024]{1,0:T(2,128)(2,1)S(1)} %stack.82, bf16[1,129024]{1,0:T(2,128)(2,1)S(1)} %copy-done.4, bf16[1,129024]{1,0:T(2,128)(2,1)} %stack.84, bf16[1,129024]{1,0:T(2,128)(2,1)} %stack.85, bf16[1,129024]{1,0:T(2,128)(2,1)} %stack.86, bf16[1,129024]{1,0:T(2,128)(2,1)} %stack.87, ...), dimensions={0} | concatenate | bytes 4128768 | tf_op jit(solution)/shard_map/stack | solution.py:58
  109.5 3.9 %reshape.405 = bf16[1032192]{0:T(1024)(128)(2,1)} reshape(bf16[8,129024]{1,0:T(8,128)(2,1)} %stack.89) | data formatting | bytes 4128768
  113.3 5.0 %reshape.406 = bf16[8,224,576]{2,1,0:T(8,128)(2,1)} reshape(bf16[1032192]{0:T(1024)(128)(2,1)} %reshape.405) | data formatting | bytes 4128768
  118.3 2.7 %fusion.3 = bf16[8,224,576]{2,0,1:T(8,128)(2,1)S(1)} fusion(bf16[224,576,8]{1,0,2:T(8,128)(2,1)} %bitcast.118, s32[8]{0:T(128)S(1)} %get-tuple-element.26), kind=kOutput, calls=%fused_computation.12 | convolution fusion | flops 16515136 | bytes 4128800 | tf_op jit(solution)/shard_map/dot_general | solution.py:60
  122.0 2.8 %pad_maximum_fusion = bf16[8,448,576]{2,0,1:T(8,128)(2,1)} fusion(bf16[8,224,576]{2,0,1:T(8,128)(2,1)S(1)} %fusion.3, bf16[8,224,576]{2,0,1:T(8,128)(2,1)S(1)} %fusion.5), kind=kLoop, calls=%fused_computation.10 | loop fusion | flops 2064384 | bytes 8257536 | tf_op jit(solution)/shard_map/concatenate | solution.py:63
  124.7 9.0 %copy.47 = bf16[8,448,576]{1,0,2:T(8,128)(2,1)} copy(bf16[8,448,576]{2,0,1:T(8,128)(2,1)} %pad_maximum_fusion) | data formatting | bytes 8257536 | tf_op jit(solution)/shard_map/concatenate | solution.py:63
  133.7 9.2 %reshape.346 = bf16[3584,576]{0,1:T(8,128)(2,1)} reshape(bf16[8,448,576]{1,0,2:T(8,128)(2,1)} %copy.47) | data formatting | bytes 8257536 | tf_op jit(solution)/shard_map/reshape | solution.py:66
  143.0 2.5 %maximum_select_fusion.1 = bf16[2,128,3584]{2,1,0:T(8,128)(2,1)S(1)} fusion(bf16[2,128,1792]{2,1,0:T(8,128)(2,1)} %collective-permute-done.2, bf16[2,128,1792]{2,1,0:T(8,128)(2,1)} %collective-permute-done.1, pred[]{:T(512)S(6)} %eq.40), kind=kLoop, calls=%fused_computation.17 | loop fusion | flops 8257536 | bytes 3670017 | tf_op jit(solution)/shard_map/jit(_where)/select_n | solution.py:120
  148.4 2.3 %convolution_add_fusion = f32[512,576]{0,1:T(8,128)S(1)} fusion(bf16[512,3584]{1,0:T(8,128)(2,1)S(1)} %bitcast.124, bf16[3584,576]{0,1:T(8,128)(2,1)S(1)} %copy-done.3, f32[576]{0:T(1024)S(1)} %maximum_select_fusion.2), kind=kOutput, calls=%fused_computation.32 | convolution fusion | flops 2114224128 | bytes 8980736 | tf_op jit(solution)/shard_map/dot_general | solution.py:135
  153.3 7.7 %collective-permute-done.17 = bf16[2,128,576]{1,0,2:T(2,128)(2,1)S(1)} collective-permute-done((bf16[2,128,576]{1,0,2:T(2,128)(2,1)S(1)}, bf16[2,128,576]{1,0,2:T(2,128)(2,1)S(1)}, u32[]{:S(2)}, u32[]{:S(2)}) %collective-permute-start.17) | collective-permute-done | bytes 294944 | tf_op jit(solution)/shard_map/ppermute | solution.py:146
  169.6 1.8 copy.60
  174.2 7.9 %collective-permute-done.20 = bf16[2,128,256]{1,0,2:T(2,128)(2,1)S(1)} collective-permute-done((bf16[2,128,256]{1,0,2:T(2,128)(2,1)S(1)}, bf16[2,128,256]{1,0,2:T(2,128)(2,1)S(1)}, u32[]{:S(2)}, u32[]{:S(2)}) %collective-permute-start.20) | collective-permute-done | bytes 131104 | tf_op jit(solution)/shard_map/ppermute | solution.py:157
  182.2 2.7 %collective-permute-done.21 = bf16[2,128,256]{1,0,2:T(2,128)(2,1)S(1)} collective-permute-done((bf16[2,128,256]{1,0,2:T(2,128)(2,1)S(1)}, bf16[2,128,256]{1,0,2:T(2,128)(2,1)S(1)}, u32[]{:S(2)}, u32[]{:S(2)}) %collective-permute-start.21) | collective-permute-done | bytes 131104 | tf_op jit(solution)/shard_map/ppermute | solution.py:157
  185.2 3.3 %collective-permute-done.23 = bf16[2,128,256]{1,0,2:T(2,128)(2,1)S(1)} collective-permute-done((bf16[2,128,256]{1,0,2:T(2,128)(2,1)S(1)}, bf16[2,128,256]{1,0,2:T(2,128)(2,1)S(1)}, u32[]{:S(2)}, u32[]{:S(2)}) %collective-permute-start.23) | collective-permute-done | bytes 131104 | tf_op jit(solution)/shard_map/ppermute | solution.py:157
  (188 shorter events, 60.0 us)
Async XLA Ops:
  0.0 15.7 %copy-start = (s32[2,2,2]{2,1,0:T(2,128)S(1)}, s32[2,2,2]{2,1,0:T(2,128)}, u32[]{:S(2)}) copy-start(s32[2,2,2]{2,1,0:T(2,128)} %param.20) | copy-start | bytes 100
  0.0 51.3 %collective-permute-start.1 = (bf16[2,128,1792]{2,1,0:T(8,128)(2,1)}, bf16[2,128,1792]{2,1,0:T(8,128)(2,1)}, u32[]{:S(2)}, u32[]{:S(2)}) collective-permute-start(bf16[2,128,1792]{2,1,0:T(8,128)(2,1)} %param.11), channel_id=1, source_target_pairs={{0,16},{16,0},{1,17},{17,1},{2,18},{18,2},{3,19},{19,3},{4,20},{20... | collective-permute-start | bytes 2752520 | tf_op jit(solution)/shard_map/ppermute | solution.py:113
  1.2 57.1 %collective-permute-start = (bf16[2,128,1792]{2,1,0:T(8,128)(2,1)}, bf16[2,128,1792]{2,1,0:T(8,128)(2,1)}, u32[]{:S(2)}, u32[]{:S(2)}) collective-permute-start(bf16[2,128,1792]{2,1,0:T(8,128)(2,1)} %param.11), channel_id=1, source_target_pairs={{0,1},{1,0},{2,3},{3,2},{4,5},{5,4},{6,7},{7,6},{8,9},{9,8},{10,11... | collective-permute-start | bytes 2752520 | tf_op jit(solution)/shard_map/ppermute | solution.py:112
  4.4 32.0 %copy-start.17 = (f32[896]{0:T(1024)S(1)}, f32[896]{0:T(1024)}, u32[]{:S(2)}) copy-start(f32[896]{0:T(1024)} %param.14) | copy-start | bytes 10756
  4.4 32.0 %copy-start.20 = (f32[128]{0:T(128)S(1)}, f32[128]{0:T(128)}, u32[]{:S(2)}) copy-start(f32[128]{0:T(128)} %param.16) | copy-start | bytes 1540
  4.4 38.0 %slice-start = ((f32[896]{0:T(1024)}), f32[512]{0:T(512)S(1)}, s32[]{:S(2)}) async-start(f32[896]{0:T(1024)} %param.14), calls=%async_computation | async-start | bytes 4096 | tf_op jit(solution)/shard_map/slice | solution.py:107
  5.5 38.9 %copy-start.22 = (s32[8]{0:T(128)S(1)}, s32[8]{0:T(128)}, u32[]{:S(2)}) copy-start(s32[8]{0:T(128)} %constant.140) | copy-start | bytes 100
  5.6 8.6 %collective-permute-start.10 = (bf16[224,576]{1,0:T(8,128)(2,1)S(1)}, bf16[224,576]{1,0:T(8,128)(2,1)S(1)}, u32[]{:S(2)}, u32[]{:S(2)}) collective-permute-start(bf16[224,576]{1,0:T(8,128)(2,1)S(1)} %get-tuple-element.12), channel_id=1, source_target_pairs={{0,2},{4,0},{8,4},{12,8},{14,12},{10,14},{6,10},{2,6},{1,3},{5,1},... | collective-permute-start | bytes 774152 | tf_op jit(solution)/shard_map/ppermute | solution.py:48
  6.9 8.6 %collective-permute-start.3 = (bf16[224,576]{1,0:T(8,128)(2,1)S(1)}, bf16[224,576]{1,0:T(8,128)(2,1)S(1)}, u32[]{:S(2)}, u32[]{:S(2)}) collective-permute-start(bf16[224,576]{1,0:T(8,128)(2,1)S(1)} %get-tuple-element.11), channel_id=1, source_target_pairs={{0,4},{4,8},{8,12},{12,14},{14,10},{10,6},{6,2},{2,0},{1,5},{5,9},... | collective-permute-start | bytes 774152 | tf_op jit(solution)/shard_map/ppermute | solution.py:47
  14.2 7.8 %collective-permute-start.11 = (bf16[224,576]{1,0:T(8,128)(2,1)S(1)}, bf16[224,576]{1,0:T(8,128)(2,1)S(1)}, u32[]{:S(2)}, u32[]{:S(2)}) collective-permute-start(bf16[224,576]{1,0:T(8,128)(2,1)S(1)} %collective-permute-done.10), channel_id=1, source_target_pairs={{0,2},{4,0},{8,4},{12,8},{14,12},{10,14},{6,10},{2,6},{1,3},{5,1},... | collective-permute-start | bytes 774152 | tf_op jit(solution)/shard_map/ppermute | solution.py:48
  15.5 7.8 %collective-permute-start.4 = (bf16[224,576]{1,0:T(8,128)(2,1)S(1)}, bf16[224,576]{1,0:T(8,128)(2,1)S(1)}, u32[]{:S(2)}, u32[]{:S(2)}) collective-permute-start(bf16[224,576]{1,0:T(8,128)(2,1)S(1)} %collective-permute-done.3), channel_id=1, source_target_pairs={{0,4},{4,8},{8,12},{12,14},{14,10},{10,6},{6,2},{2,0},{1,5},{5,9},... | collective-permute-start | bytes 774152 | tf_op jit(solution)/shard_map/ppermute | solution.py:47
  22.0 6.9 %collective-permute-start.12 = (bf16[224,576]{1,0:T(8,128)(2,1)S(1)}, bf16[224,576]{1,0:T(8,128)(2,1)S(1)}, u32[]{:S(2)}, u32[]{:S(2)}) collective-permute-start(bf16[224,576]{1,0:T(8,128)(2,1)S(1)} %collective-permute-done.11), channel_id=1, source_target_pairs={{0,2},{4,0},{8,4},{12,8},{14,12},{10,14},{6,10},{2,6},{1,3},{5,1},... | collective-permute-start | bytes 774152 | tf_op jit(solution)/shard_map/ppermute | solution.py:48
  23.3 11.5 %copy-start.9 = (bf16[224,576]{1,0:T(8,128)(2,1)}, bf16[224,576]{1,0:T(8,128)(2,1)S(1)}, u32[]{:S(2)}) copy-start(bf16[224,576]{1,0:T(8,128)(2,1)S(1)} %collective-permute-done.4) | copy-start | bytes 774148
  23.3 6.9 %collective-permute-start.5 = (bf16[224,576]{1,0:T(8,128)(2,1)S(1)}, bf16[224,576]{1,0:T(8,128)(2,1)S(1)}, u32[]{:S(2)}, u32[]{:S(2)}) collective-permute-start(bf16[224,576]{1,0:T(8,128)(2,1)S(1)} %collective-permute-done.4), channel_id=1, source_target_pairs={{0,4},{4,8},{8,12},{12,14},{14,10},{10,6},{6,2},{2,0},{1,5},{5,9},... | collective-permute-start | bytes 774152 | tf_op jit(solution)/shard_map/ppermute | solution.py:47
  28.9 6.0 %collective-permute-start.13 = (bf16[224,576]{1,0:T(8,128)(2,1)S(1)}, bf16[224,576]{1,0:T(8,128)(2,1)S(1)}, u32[]{:S(2)}, u32[]{:S(2)}) collective-permute-start(bf16[224,576]{1,0:T(8,128)(2,1)S(1)} %collective-permute-done.12), channel_id=1, source_target_pairs={{0,2},{4,0},{8,4},{12,8},{14,12},{10,14},{6,10},{2,6},{1,3},{5,1},... | collective-permute-start | bytes 774152 | tf_op jit(solution)/shard_map/ppermute | solution.py:48
  30.2 6.0 %collective-permute-start.6 = (bf16[224,576]{1,0:T(8,128)(2,1)S(1)}, bf16[224,576]{1,0:T(8,128)(2,1)S(1)}, u32[]{:S(2)}, u32[]{:S(2)}) collective-permute-start(bf16[224,576]{1,0:T(8,128)(2,1)S(1)} %collective-permute-done.5), channel_id=1, source_target_pairs={{0,4},{4,8},{8,12},{12,14},{14,10},{10,6},{6,2},{2,0},{1,5},{5,9},... | collective-permute-start | bytes 774152 | tf_op jit(solution)/shard_map/ppermute | solution.py:47
  34.9 11.8 %copy-start.8 = (bf16[224,576]{1,0:T(8,128)(2,1)}, bf16[224,576]{1,0:T(8,128)(2,1)S(1)}, u32[]{:S(2)}) copy-start(bf16[224,576]{1,0:T(8,128)(2,1)S(1)} %collective-permute-done.13) | copy-start | bytes 774148
  34.9 5.8 %collective-permute-start.14 = (bf16[224,576]{1,0:T(8,128)(2,1)S(1)}, bf16[224,576]{1,0:T(8,128)(2,1)}, u32[]{:S(2)}, u32[]{:S(2)}) collective-permute-start(bf16[224,576]{1,0:T(8,128)(2,1)S(1)} %collective-permute-done.13), channel_id=1, source_target_pairs={{0,2},{4,0},{8,4},{12,8},{14,12},{10,14},{6,10},{2,6},{1,3},{5,1},... | collective-permute-start | bytes 774152 | tf_op jit(solution)/shard_map/ppermute | solution.py:48
  36.2 6.1 %collective-permute-start.7 = (bf16[224,576]{1,0:T(8,128)(2,1)S(1)}, bf16[224,576]{1,0:T(8,128)(2,1)}, u32[]{:S(2)}, u32[]{:S(2)}) collective-permute-start(bf16[224,576]{1,0:T(8,128)(2,1)S(1)} %collective-permute-done.6), channel_id=1, source_target_pairs={{0,4},{4,8},{8,12},{12,14},{14,10},{10,6},{6,2},{2,0},{1,5},{5,9},... | collective-permute-start | bytes 774152 | tf_op jit(solution)/shard_map/ppermute | solution.py:47
  40.6 16.2 %collective-permute-start.15 = (bf16[224,576]{1,0:T(8,128)(2,1)}, bf16[224,576]{1,0:T(8,128)(2,1)}, u32[]{:S(2)}, u32[]{:S(2)}) collective-permute-start(bf16[224,576]{1,0:T(8,128)(2,1)} %collective-permute-done.14), channel_id=1, source_target_pairs={{0,2},{4,0},{8,4},{12,8},{14,12},{10,14},{6,10},{2,6},{1,3},{5,1},... | collective-permute-start | bytes 774152 | tf_op jit(solution)/shard_map/ppermute | solution.py:48
  42.3 15.9 %collective-permute-start.8 = (bf16[224,576]{1,0:T(8,128)(2,1)}, bf16[224,576]{1,0:T(8,128)(2,1)}, u32[]{:S(2)}, u32[]{:S(2)}) collective-permute-start(bf16[224,576]{1,0:T(8,128)(2,1)} %collective-permute-done.7), channel_id=1, source_target_pairs={{0,4},{4,8},{8,12},{12,14},{14,10},{10,6},{6,2},{2,0},{1,5},{5,9},... | collective-permute-start | bytes 774152 | tf_op jit(solution)/shard_map/ppermute | solution.py:47
  51.3 91.6 %collective-permute-start.2 = (bf16[2,128,1792]{2,1,0:T(8,128)(2,1)}, bf16[2,128,1792]{2,1,0:T(8,128)(2,1)}, u32[]{:S(2)}, u32[]{:S(2)}) collective-permute-start(bf16[2,128,1792]{2,1,0:T(8,128)(2,1)} %collective-permute-done.1), channel_id=1, source_target_pairs={{0,1},{1,0},{2,3},{3,2},{4,5},{5,4},{6,7},{7,6},{8,9},{9,8},{10,11... | collective-permute-start | bytes 2752520 | tf_op jit(solution)/shard_map/ppermute | solution.py:114
  56.9 16.7 %collective-permute-start.16 = (bf16[224,576]{1,0:T(8,128)(2,1)}, bf16[224,576]{1,0:T(8,128)(2,1)}, u32[]{:S(2)}, u32[]{:S(2)}) collective-permute-start(bf16[224,576]{1,0:T(8,128)(2,1)} %collective-permute-done.15), channel_id=1, source_target_pairs={{0,2},{4,0},{8,4},{12,8},{14,12},{10,14},{6,10},{2,6},{1,3},{5,1},... | collective-permute-start | bytes 774152 | tf_op jit(solution)/shard_map/ppermute | solution.py:48
  58.2 38.0 %collective-permute-start.9 = (bf16[224,576]{1,0:T(8,128)(2,1)}, bf16[224,576]{1,0:T(8,128)(2,1)}, u32[]{:S(2)}, u32[]{:S(2)}) collective-permute-start(bf16[224,576]{1,0:T(8,128)(2,1)} %collective-permute-done.8), channel_id=1, source_target_pairs={{0,4},{4,8},{8,12},{12,14},{14,10},{10,6},{6,2},{2,0},{1,5},{5,9},... | collective-permute-start | bytes 774152 | tf_op jit(solution)/shard_map/ppermute | solution.py:47
  153.0 8.0 %collective-permute-start.17 = (bf16[2,128,576]{1,0,2:T(2,128)(2,1)S(1)}, bf16[2,128,576]{1,0,2:T(2,128)(2,1)S(1)}, u32[]{:S(2)}, u32[]{:S(2)}) collective-permute-start(bf16[2,128,576]{1,0,2:T(2,128)(2,1)S(1)} %fusion.29), channel_id=1, source_target_pairs={{0,16},{16,0},{1,17},{17,1},{2,18},{18,2},{3,19},{19,3},{4,20},{20... | collective-permute-start | bytes 884744 | tf_op jit(solution)/shard_map/ppermute | solution.py:146
  162.3 9.2 %collective-permute-start.18 = (bf16[2,128,256]{1,0,2:T(2,128)(2,1)S(1)}, bf16[2,128,256]{1,0,2:T(2,128)(2,1)S(1)}, u32[]{:S(2)}, u32[]{:S(2)}) collective-permute-start(bf16[2,128,256]{1,0,2:T(2,128)(2,1)S(1)} %pad_maximum_fusion.6), channel_id=1, source_target_pairs={{0,2},{2,4},{4,6},{6,8},{8,10},{10,12},{12,14},{14,0},{1,3},{3,5},... | collective-permute-start | bytes 393224 | tf_op jit(solution)/shard_map/ppermute | solution.py:157
  163.9 8.9 %collective-permute-start.19 = (bf16[2,128,256]{1,0,2:T(2,128)(2,1)S(1)}, bf16[2,128,256]{1,0,2:T(2,128)(2,1)S(1)}, u32[]{:S(2)}, u32[]{:S(2)}) collective-permute-start(bf16[2,128,256]{1,0,2:T(2,128)(2,1)S(1)} %pad_maximum_fusion.6), channel_id=1, source_target_pairs={{0,4},{2,6},{4,8},{6,10},{8,12},{10,14},{12,0},{14,2},{1,5},{3,7},... | collective-permute-start | bytes 393224 | tf_op jit(solution)/shard_map/ppermute | solution.py:157
  165.2 16.9 %collective-permute-start.20 = (bf16[2,128,256]{1,0,2:T(2,128)(2,1)S(1)}, bf16[2,128,256]{1,0,2:T(2,128)(2,1)S(1)}, u32[]{:S(2)}, u32[]{:S(2)}) collective-permute-start(bf16[2,128,256]{1,0,2:T(2,128)(2,1)S(1)} %pad_maximum_fusion.6), channel_id=1, source_target_pairs={{0,6},{2,8},{4,10},{6,12},{8,14},{10,0},{12,2},{14,4},{1,7},{3,9},... | collective-permute-start | bytes 393224 | tf_op jit(solution)/shard_map/ppermute | solution.py:157
  165.8 19.1 %collective-permute-start.21 = (bf16[2,128,256]{1,0,2:T(2,128)(2,1)S(1)}, bf16[2,128,256]{1,0,2:T(2,128)(2,1)S(1)}, u32[]{:S(2)}, u32[]{:S(2)}) collective-permute-start(bf16[2,128,256]{1,0,2:T(2,128)(2,1)S(1)} %pad_maximum_fusion.6), channel_id=1, source_target_pairs={{0,8},{2,10},{4,12},{6,14},{8,0},{10,2},{12,4},{14,6},{1,9},{3,11}... | collective-permute-start | bytes 393224 | tf_op jit(solution)/shard_map/ppermute | solution.py:157
  167.2 17.8 %collective-permute-start.22 = (bf16[2,128,256]{1,0,2:T(2,128)(2,1)S(1)}, bf16[2,128,256]{1,0,2:T(2,128)(2,1)S(1)}, u32[]{:S(2)}, u32[]{:S(2)}) collective-permute-start(bf16[2,128,256]{1,0,2:T(2,128)(2,1)S(1)} %pad_maximum_fusion.6), channel_id=1, source_target_pairs={{0,10},{2,12},{4,14},{6,0},{8,2},{10,4},{12,6},{14,8},{1,11},{3,13... | collective-permute-start | bytes 393224 | tf_op jit(solution)/shard_map/ppermute | solution.py:157
  171.5 17.0 %collective-permute-start.23 = (bf16[2,128,256]{1,0,2:T(2,128)(2,1)S(1)}, bf16[2,128,256]{1,0,2:T(2,128)(2,1)S(1)}, u32[]{:S(2)}, u32[]{:S(2)}) collective-permute-start(bf16[2,128,256]{1,0,2:T(2,128)(2,1)S(1)} %pad_maximum_fusion.6), channel_id=1, source_target_pairs={{0,12},{2,14},{4,0},{6,2},{8,4},{10,6},{12,8},{14,10},{1,13},{3,15... | collective-permute-start | bytes 393224 | tf_op jit(solution)/shard_map/ppermute | solution.py:157
  172.8 17.2 %collective-permute-start.24 = (bf16[2,128,256]{1,0,2:T(2,128)(2,1)S(1)}, bf16[2,128,256]{1,0,2:T(2,128)(2,1)S(1)}, u32[]{:S(2)}, u32[]{:S(2)}) collective-permute-start(bf16[2,128,256]{1,0,2:T(2,128)(2,1)S(1)} %pad_maximum_fusion.6), channel_id=1, source_target_pairs={{0,14},{2,0},{4,2},{6,4},{8,6},{10,8},{12,10},{14,12},{1,15},{3,1}... | collective-permute-start | bytes 393224 | tf_op jit(solution)/shard_map/ppermute | solution.py:157
  (17 other events, 73.6 us)

commit v12 on v3

--- a/solution.py
+++ b/solution.py
@@ -50,11 +50,21 @@
         behind_parts.append(behind)
     table = jnp.array(position, dtype=jnp.int32)
     mine = table[here]
-    ahead_pick = (mine - table) % count
-    behind_pick = (table - mine) % count
-    joined = jnp.concatenate(
-        [jnp.stack(ahead_parts)[ahead_pick], jnp.stack(behind_parts)[behind_pick]], axis=1
-    )
+    ahead_stack, behind_stack = jnp.stack(ahead_parts), jnp.stack(behind_parts)
+
+    def placed(at):
+        def build(ahead_stack, behind_stack):
+            return jnp.concatenate(
+                [
+                    jnp.stack([ahead_stack[(at - position[d]) % count] for d in range(count)]),
+                    jnp.stack([behind_stack[(position[d] - at) % count] for d in range(count)]),
+                ],
+                axis=1,
+            )
+
+        return build
+
+    joined = lax.switch(mine, [placed(at) for at in range(count)], ahead_stack, behind_stack)
     return joined.reshape(count * shard.shape[0], shard.shape[1])
 
 

time: 123 us -> 123 us (level); the launches traced: 121 us -> 123 us
  local copies, waits for them, and re-layouts: 32.7 us -> 25 us
  other arithmetic: 16.1 us -> 20.2 us
  waiting for transfers between devices: 34.1 us -> 38.1 us
    gather x2 -> x0, local copies, waits for them, and re-layouts: 7.79 us -> none  [the longest x1 3.9 us: gather_rows(): jnp.stack(behind_parts)[behind_pick]]
    ppermute x7, waiting for transfers between devices: 23.9 us -> 29.8 us  [gather_rows(): ahead = lax.ppermute(ahead, 'row', forward)]
    unnamed x41 -> x42, local copies, waits for them, and re-layouts: 9.93 us -> 5.44 us
    ppermute x7, waiting for transfers between devices: 3.75 us -> 0.02 us  [shards(): lax.ppermute(pairs, 'row', [(i, (i + k) % row_count) for i in range(row_c...]
    cond x0 -> x14, local copies, waits for them, and re-layouts: none -> 2.41 us
    ppermute x7, waiting for transfers between devices: 0.02 us -> 2.04 us  [gather_rows(): behind = lax.ppermute(behind, 'row', backward)]
    select_n x1, other arithmetic: 1.97 us -> 3.74 us  [shards(): jnp.where(column == 0, jnp.concatenate([tokens, other_half], axis=2), jnp...]
    concatenate x1, other arithmetic: 0.01 us -> 1.47 us  [apply_rotation(): jnp.concatenate([jnp.cos(angles), jnp.cos(angles)], axis=-1)]
  transfers between devices with their start and end apart: 25 -> 25, of which waited for: 11 -> 10; matrix products, arithmetic and copies ran while one was open for 29% -> 22% of each run, Pallas kernels for 0% -> 0%
where the time goes in v12:
time: 123 us
  waiting for transfers between devices  38.1 us (31%)
  starting transfers between devices  30.6 us (25%)
  local copies, waits for them, and re-layouts  25 us (20%)
  other arithmetic  20.2 us (16%)
  matrix products  7.69 us (6%)
  between operations  1.28 us (1%)
    ppermute x7, waiting for transfers between devices, gather_rows(): ahead = lax.ppermute(ahead, 'row', forward)  29.8 us
    ppermute x7, starting transfers between devices, shards(): lax.ppermute(pairs, 'row', [(i, (i + k) % row_count) for i in range(row_c...  12.4 us
    ppermute x7, starting transfers between devices, gather_rows(): ahead = lax.ppermute(ahead, 'row', forward)  10.9 us
    ppermute x1, waiting for transfers between devices, shards(): returned = lax.ppermute(result[passages:], 'groups', SWAP)  6.2 us
    unnamed x42, local copies, waits for them, and re-layouts  5.44 us
    select_n x1, other arithmetic, shards(): jnp.where(column == 0, jnp.concatenate([tokens, other_half], axis=2), jnp...  3.74 us
    ppermute x7, starting transfers between devices, gather_rows(): behind = lax.ppermute(behind, 'row', backward)  3.69 us
    ppermute x1, starting transfers between devices, shards(): partner_half = lax.ppermute(tokens, 'groups', SWAP)  2.97 us
  transfers between devices with their start and end apart: 25, of which 10 were waited for; matrix products, arithmetic and copies ran while one was open for 22% of the time, Pallas kernels for 0%

profile of v12, /device:TPU:0, one launch (start us, length us, event | category | flops | bytes accessed | tf_op | source)
XLA Modules:
  0.0 122.9 jit_solution(10198527642509741545)
XLA Ops:
  0.0 3.0 %collective-permute-start.1 = (bf16[2,128,1792]{2,1,0:T(8,128)(2,1)}, bf16[2,128,1792]{2,1,0:T(8,128)(2,1)}, u32[]{:S(2)}, u32[]{:S(2)}) collective-permute-start(bf16[2,128,1792]{2,1,0:T(8,128)(2,1)} %param.19), channel_id=1, source_target_pairs={{0,16},{16,0},{1,17},{17,1},{2,18},{18,2},{3,19},{19,3},{4,20},{20... | collective-permute-start | bytes 2752520 | tf_op jit(solution)/shard_map/ppermute | solution.py:115
  6.5 1.6 %collective-permute-start.3 = (bf16[224,576]{1,0:T(8,128)(2,1)S(1)}, bf16[224,576]{1,0:T(8,128)(2,1)S(1)}, u32[]{:S(2)}, u32[]{:S(2)}) collective-permute-start(bf16[224,576]{1,0:T(8,128)(2,1)S(1)} %get-tuple-element.424), channel_id=1, source_target_pairs={{0,4},{4,8},{8,12},{12,14},{14,10},{10,6},{6,2},{2,0},{1,5},{5,9},... | collective-permute-start | bytes 774152 | tf_op jit(solution)/shard_map/ppermute | solution.py:47
  8.8 7.0 %collective-permute-done.3 = bf16[224,576]{1,0:T(8,128)(2,1)S(1)} collective-permute-done((bf16[224,576]{1,0:T(8,128)(2,1)S(1)}, bf16[224,576]{1,0:T(8,128)(2,1)S(1)}, u32[]{:S(2)}, u32[]{:S(2)}) %collective-permute-start.3) | collective-permute-done | bytes 258080 | tf_op jit(solution)/shard_map/ppermute | solution.py:47
  15.8 1.6 %collective-permute-start.4 = (bf16[224,576]{1,0:T(8,128)(2,1)S(1)}, bf16[224,576]{1,0:T(8,128)(2,1)S(1)}, u32[]{:S(2)}, u32[]{:S(2)}) collective-permute-start(bf16[224,576]{1,0:T(8,128)(2,1)S(1)} %collective-permute-done.3), channel_id=1, source_target_pairs={{0,4},{4,8},{8,12},{12,14},{14,10},{10,6},{6,2},{2,0},{1,5},{5,9},... | collective-permute-start | bytes 774152 | tf_op jit(solution)/shard_map/ppermute | solution.py:47
  18.0 6.4 %collective-permute-done.4 = bf16[224,576]{1,0:T(8,128)(2,1)S(1)} collective-permute-done((bf16[224,576]{1,0:T(8,128)(2,1)S(1)}, bf16[224,576]{1,0:T(8,128)(2,1)S(1)}, u32[]{:S(2)}, u32[]{:S(2)}) %collective-permute-start.4) | collective-permute-done | bytes 258080 | tf_op jit(solution)/shard_map/ppermute | solution.py:47
  24.4 1.6 %collective-permute-start.5 = (bf16[224,576]{1,0:T(8,128)(2,1)S(1)}, bf16[224,576]{1,0:T(8,128)(2,1)S(1)}, u32[]{:S(2)}, u32[]{:S(2)}) collective-permute-start(bf16[224,576]{1,0:T(8,128)(2,1)S(1)} %collective-permute-done.4), channel_id=1, source_target_pairs={{0,4},{4,8},{8,12},{12,14},{14,10},{10,6},{6,2},{2,0},{1,5},{5,9},... | collective-permute-start | bytes 774152 | tf_op jit(solution)/shard_map/ppermute | solution.py:47
  26.6 5.6 %collective-permute-done.5 = bf16[224,576]{1,0:T(8,128)(2,1)S(1)} collective-permute-done((bf16[224,576]{1,0:T(8,128)(2,1)S(1)}, bf16[224,576]{1,0:T(8,128)(2,1)S(1)}, u32[]{:S(2)}, u32[]{:S(2)}) %collective-permute-start.5) | collective-permute-done | bytes 258080 | tf_op jit(solution)/shard_map/ppermute | solution.py:47
  32.2 1.6 %collective-permute-start.6 = (bf16[224,576]{1,0:T(8,128)(2,1)S(1)}, bf16[224,576]{1,0:T(8,128)(2,1)S(1)}, u32[]{:S(2)}, u32[]{:S(2)}) collective-permute-start(bf16[224,576]{1,0:T(8,128)(2,1)S(1)} %collective-permute-done.5), channel_id=1, source_target_pairs={{0,4},{4,8},{8,12},{12,14},{14,10},{10,6},{6,2},{2,0},{1,5},{5,9},... | collective-permute-start | bytes 774152 | tf_op jit(solution)/shard_map/ppermute | solution.py:47
  35.0 4.2 %collective-permute-done.6 = bf16[224,576]{1,0:T(8,128)(2,1)S(1)} collective-permute-done((bf16[224,576]{1,0:T(8,128)(2,1)S(1)}, bf16[224,576]{1,0:T(8,128)(2,1)S(1)}, u32[]{:S(2)}, u32[]{:S(2)}) %collective-permute-start.6) | collective-permute-done | bytes 258080 | tf_op jit(solution)/shard_map/ppermute | solution.py:47
  39.2 1.6 %collective-permute-start.7 = (bf16[224,576]{1,0:T(8,128)(2,1)S(1)}, bf16[224,576]{1,0:T(8,128)(2,1)S(1)}, u32[]{:S(2)}, u32[]{:S(2)}) collective-permute-start(bf16[224,576]{1,0:T(8,128)(2,1)S(1)} %collective-permute-done.6), channel_id=1, source_target_pairs={{0,4},{4,8},{8,12},{12,14},{14,10},{10,6},{6,2},{2,0},{1,5},{5,9},... | collective-permute-start | bytes 774152 | tf_op jit(solution)/shard_map/ppermute | solution.py:47
  41.4 5.7 %collective-permute-done.7 = bf16[224,576]{1,0:T(8,128)(2,1)S(1)} collective-permute-done((bf16[224,576]{1,0:T(8,128)(2,1)S(1)}, bf16[224,576]{1,0:T(8,128)(2,1)S(1)}, u32[]{:S(2)}, u32[]{:S(2)}) %collective-permute-start.7) | collective-permute-done | bytes 258080 | tf_op jit(solution)/shard_map/ppermute | solution.py:47
  47.0 1.6 %collective-permute-start.8 = (bf16[224,576]{1,0:T(8,128)(2,1)S(1)}, bf16[224,576]{1,0:T(8,128)(2,1)}, u32[]{:S(2)}, u32[]{:S(2)}) collective-permute-start(bf16[224,576]{1,0:T(8,128)(2,1)S(1)} %collective-permute-done.7), channel_id=1, source_target_pairs={{0,4},{4,8},{8,12},{12,14},{14,10},{10,6},{6,2},{2,0},{1,5},{5,9},... | collective-permute-start | bytes 774152 | tf_op jit(solution)/shard_map/ppermute | solution.py:47
  53.4 1.5 %pad_maximum_fusion.13 = (f32[128,128]{0,1:T(8,128)}, f32[128,128]{0,1:T(8,128)S(1)}) fusion(f32[128,64]{0,1:T(8,128)S(1)} %get-tuple-element.427, f32[128,64]{0,1:T(8,128)} %get-tuple-element.428), kind=kLoop, calls=%fused_computation.202 | loop fusion | flops 32768 | bytes 196608 | tf_op jit(solution)/shard_map/concatenate | solution.py:24
  55.3 1.4 %collective-permute-start.9 = (bf16[224,576]{1,0:T(8,128)(2,1)}, bf16[224,576]{1,0:T(8,128)(2,1)S(1)}, u32[]{:S(2)}, u32[]{:S(2)}) collective-permute-start(bf16[224,576]{1,0:T(8,128)(2,1)} %collective-permute-done.8), channel_id=1, source_target_pairs={{0,4},{4,8},{8,12},{12,14},{14,10},{10,6},{6,2},{2,0},{1,5},{5,9},... | collective-permute-start | bytes 774152 | tf_op jit(solution)/shard_map/ppermute | solution.py:47
  57.9 3.7 %maximum_select_fusion = bf16[2,128,3584]{2,1,0:T(8,128)(2,1)} fusion(bf16[2,128,1792]{2,1,0:T(8,128)(2,1)} %collective-permute-done, bf16[2,128,1792]{2,1,0:T(8,128)(2,1)} %param.19, pred[]{:T(512)S(6)} %eq.12), kind=kLoop, calls=%fused_computation.146 | loop fusion | flops 8257536 | bytes 3670017 | tf_op jit(solution)/shard_map/jit(_where)/select_n | solution.py:117
  62.2 1.7 %collective-permute-done.16 = bf16[224,576]{1,0:T(8,128)(2,1)S(1)} collective-permute-done((bf16[224,576]{1,0:T(8,128)(2,1)}, bf16[224,576]{1,0:T(8,128)(2,1)S(1)}, u32[]{:S(2)}, u32[]{:S(2)}) %collective-permute-start.16) | collective-permute-done | bytes 258080 | tf_op jit(solution)/shard_map/ppermute | solution.py:48
  63.9 5.2 %conditional.1 = (bf16[3584,576]{1,0:T(8,128)(2,1)}) conditional(s32[]{:T(128)} %bitcast.10, (bf16[1,224,576]{2,1,0:T(8,128)(2,1)S(1)}, bf16[1,224,576]{2,1,0:T(8,128)(2,1)S(1)}, bf16[1,224,576]{2,1,0:T(8,128)(2,1)S(1)}, bf16[1,224,576]{2,1,0:T(8,128)(2,1)S(1)}, bf16[1,224,576]{2,1,0:T(8,128)(2,1)}, ...), branch_computations={%region_1.2_spmd, %region_2.3_spmd, %region_3.4_spmd, %region_4.5_... | conditional | flops 8257536 | bytes 17346568 | solution.py:67
  66.5 2.5 %pad_maximum_fusion = bf16[8,448,576]{2,1,0:T(8,128)(2,1)} fusion(bf16[8,224,576]{2,1,0:T(8,128)(2,1)S(1)} %get-tuple-element.402, bf16[8,224,576]{2,1,0:T(8,128)(2,1)S(1)} %get-tuple-element.401), kind=kLoop, calls=%fused_computation.5 | loop fusion | flops 8257536 | bytes 8257536 | tf_op jit(solution)/shard_map/cond/branch_0_fun/concatenate | solution.py:57
  69.0 2.6 %maximum_select_fusion.1 = bf16[2,128,3584]{2,1,0:T(8,128)(2,1)S(1)} fusion(bf16[2,128,1792]{2,1,0:T(8,128)(2,1)} %collective-permute-done.2, bf16[2,128,1792]{2,1,0:T(8,128)(2,1)} %collective-permute-done.1, pred[]{:T(512)S(6)} %eq.12), kind=kLoop, calls=%fused_computation.147 | loop fusion | flops 8257536 | bytes 3670017 | tf_op jit(solution)/shard_map/jit(_where)/select_n | solution.py:122
  74.6 2.4 %convolution_add_fusion = f32[512,576]{0,1:T(8,128)S(1)} fusion(bf16[512,3584]{1,0:T(8,128)(2,1)S(1)} %fusion.1, bf16[3584,576]{1,0:T(8,128)(2,1)S(1)} %bitcast.240, f32[576]{0:T(1024)S(1)} %copy-done.10), kind=kOutput, calls=%fused_computation.162 | convolution fusion | flops 2114224128 | bytes 8980736 | tf_op jit(solution)/shard_map/dot_general | solution.py:137
  80.0 6.2 %collective-permute-done.17 = bf16[2,128,576]{1,0,2:T(2,128)(2,1)S(1)} collective-permute-done((bf16[2,128,576]{1,0,2:T(2,128)(2,1)S(1)}, bf16[2,128,576]{1,0,2:T(2,128)(2,1)S(1)}, u32[]{:S(2)}, u32[]{:S(2)}) %collective-permute-start.17) | collective-permute-done | bytes 294944 | tf_op jit(solution)/shard_map/ppermute | solution.py:148
  88.4 1.9 %collective-permute-start.19 = (bf16[2,128,256]{1,0,2:T(2,128)(2,1)S(1)}, bf16[2,128,256]{1,0,2:T(2,128)(2,1)S(1)}, u32[]{:S(2)}, u32[]{:S(2)}) collective-permute-start(bf16[2,128,256]{1,0,2:T(2,128)(2,1)S(1)} %pad_maximum_fusion.12), channel_id=1, source_target_pairs={{0,4},{2,6},{4,8},{6,10},{8,12},{10,14},{12,0},{14,2},{1,5},{3,7},... | collective-permute-start | bytes 393224 | tf_op jit(solution)/shard_map/ppermute | solution.py:159
  90.3 2.7 %collective-permute-start.20 = (bf16[2,128,256]{1,0,2:T(2,128)(2,1)S(1)}, bf16[2,128,256]{1,0,2:T(2,128)(2,1)S(1)}, u32[]{:S(2)}, u32[]{:S(2)}) collective-permute-start(bf16[2,128,256]{1,0,2:T(2,128)(2,1)S(1)} %pad_maximum_fusion.12), channel_id=1, source_target_pairs={{0,6},{2,8},{4,10},{6,12},{8,14},{10,0},{12,2},{14,4},{1,7},{3,9},... | collective-permute-start | bytes 393224 | tf_op jit(solution)/shard_map/ppermute | solution.py:159
  93.1 1.3 %collective-permute-start.21 = (bf16[2,128,256]{1,0,2:T(2,128)(2,1)S(1)}, bf16[2,128,256]{1,0,2:T(2,128)(2,1)S(1)}, u32[]{:S(2)}, u32[]{:S(2)}) collective-permute-start(bf16[2,128,256]{1,0,2:T(2,128)(2,1)S(1)} %pad_maximum_fusion.12), channel_id=1, source_target_pairs={{0,8},{2,10},{4,12},{6,14},{8,0},{10,2},{12,4},{14,6},{1,9},{3,11}... | collective-permute-start | bytes 393224 | tf_op jit(solution)/shard_map/ppermute | solution.py:159
  94.4 2.1 %collective-permute-start.22 = (bf16[2,128,256]{1,0,2:T(2,128)(2,1)S(1)}, bf16[2,128,256]{1,0,2:T(2,128)(2,1)S(1)}, u32[]{:S(2)}, u32[]{:S(2)}) collective-permute-start(bf16[2,128,256]{1,0,2:T(2,128)(2,1)S(1)} %pad_maximum_fusion.12), channel_id=1, source_target_pairs={{0,10},{2,12},{4,14},{6,0},{8,2},{10,4},{12,6},{14,8},{1,11},{3,13... | collective-permute-start | bytes 393224 | tf_op jit(solution)/shard_map/ppermute | solution.py:159
  98.3 1.8 %copy.51 = bf16[2,2,64,7,128]{4,2,3,1,0:T(8,128)(2,1)S(1)} copy(bf16[2,2,64,7,128]{2,1,0,4,3:T(2,128)(2,1)S(1)} %reshape.359) | data formatting | bytes 917504 | tf_op jit(solution)/shard_map/reshape | solution.py:196
  100.2 1.6 %collective-permute-start.23 = (bf16[2,128,256]{1,0,2:T(2,128)(2,1)S(1)}, bf16[2,128,256]{1,0,2:T(2,128)(2,1)S(1)}, u32[]{:S(2)}, u32[]{:S(2)}) collective-permute-start(bf16[2,128,256]{1,0,2:T(2,128)(2,1)S(1)} %pad_maximum_fusion.12), channel_id=1, source_target_pairs={{0,12},{2,14},{4,0},{6,2},{8,4},{10,6},{12,8},{14,10},{1,13},{3,15... | collective-permute-start | bytes 393224 | tf_op jit(solution)/shard_map/ppermute | solution.py:159
  102.5 1.7 %collective-permute-start.24 = (bf16[2,128,256]{1,0,2:T(2,128)(2,1)S(1)}, bf16[2,128,256]{1,0,2:T(2,128)(2,1)S(1)}, u32[]{:S(2)}, u32[]{:S(2)}) collective-permute-start(bf16[2,128,256]{1,0,2:T(2,128)(2,1)S(1)} %pad_maximum_fusion.12), channel_id=1, source_target_pairs={{0,14},{2,0},{4,2},{6,4},{8,6},{10,8},{12,10},{14,12},{1,15},{3,1}... | collective-permute-start | bytes 393224 | tf_op jit(solution)/shard_map/ppermute | solution.py:159
  108.9 1.3 %copy.49 = bf16[2,8,2,64,256]{4,3,2,1,0:T(8,128)(2,1)S(1)} copy(bf16[2,8,2,64,256]{4,3,2,0,1:T(8,128)(2,1)} %bitcast.39) | data formatting | bytes 2097152 | tf_op jit(solution)/shard_map/transpose | solution.py:170
  110.8 1.4 %gather_fusion.2 = bf16[12,64,256]{2,1,0:T(8,128)(2,1)} fusion(bf16[2,16,64,256]{3,2,0,1:T(8,128)(2,1)S(1)} %bitcast.228, s32[12]{0:T(128)S(1)} %reshape.329), kind=kCustom, calls=%fused_computation.2 | custom fusion | bytes 786528 | tf_op jit(solution)/shard_map/gather | solution.py:182
  114.3 1.4 %fusion.42 = (f32[2,2,7,64]{3,2,1,0:T(8,128)S(1)}, f32[2,2,7,64,128]{4,3,2,1,0:T(8,128)S(1)}) fusion(bf16[2,2,64,7,128]{4,2,3,1,0:T(8,128)(2,1)S(1)} %copy.51, bf16[2,128,256]{2,1,0:T(8,128)(2,1)} %bitcast.257), kind=kOutput, calls=%fused_computation.260 | convolution fusion | flops 59177216 | bytes 1448960 | tf_op jit(solution)/shard_map/sqbgh,swh->sqgbw/dot_general | solution.py:205
  121.6 1.3 %convert_element_type.54 = bf16[2,128,896]{2,1,0:T(8,128)(2,1)} reshape(bf16[2,2,64,7,128]{4,3,2,1,0:T(8,128)(2,1)S(1)} %copy.56) | data formatting | bytes 917504 | tf_op jit(solution)/shard_map/convert_element_type | solution.py:258
  (167 shorter events, 39.5 us)
Async XLA Ops:
  0.0 8.7 %copy-start = (s32[2,2,2]{2,1,0:T(2,128)S(1)}, s32[2,2,2]{2,1,0:T(2,128)}, u32[]{:S(2)}) copy-start(s32[2,2,2]{2,1,0:T(2,128)} %param.28) | copy-start | bytes 100
  0.0 41.3 %collective-permute-start.1 = (bf16[2,128,1792]{2,1,0:T(8,128)(2,1)}, bf16[2,128,1792]{2,1,0:T(8,128)(2,1)}, u32[]{:S(2)}, u32[]{:S(2)}) collective-permute-start(bf16[2,128,1792]{2,1,0:T(8,128)(2,1)} %param.19), channel_id=1, source_target_pairs={{0,16},{16,0},{1,17},{17,1},{2,18},{18,2},{3,19},{19,3},{4,20},{20... | collective-permute-start | bytes 2752520 | tf_op jit(solution)/shard_map/ppermute | solution.py:115
  3.0 54.9 %collective-permute-start = (bf16[2,128,1792]{2,1,0:T(8,128)(2,1)}, bf16[2,128,1792]{2,1,0:T(8,128)(2,1)}, u32[]{:S(2)}, u32[]{:S(2)}) collective-permute-start(bf16[2,128,1792]{2,1,0:T(8,128)(2,1)} %param.19), channel_id=1, source_target_pairs={{0,1},{1,0},{2,3},{3,2},{4,5},{5,4},{6,7},{7,6},{8,9},{9,8},{10,11... | collective-permute-start | bytes 2752520 | tf_op jit(solution)/shard_map/ppermute | solution.py:114
  4.0 4.6 %copy-start.11 = (f32[128]{0:T(128)S(1)}, f32[128]{0:T(128)}, u32[]{:S(2)}) copy-start(f32[128]{0:T(128)} %param.26) | copy-start | bytes 1540
  4.1 13.9 %copy-start.9 = (s32[2,16,14,2]{1,3,2,0:T(2,128)S(1)}, s32[2,16,14,2]{1,3,2,0:T(2,128)}, u32[]{:S(2)}) copy-start(s32[2,16,14,2]{1,3,2,0:T(2,128)} %param.27) | copy-start | bytes 10756
  4.1 37.3 %copy-start.7 = (f32[896]{0:T(1024)S(1)}, f32[896]{0:T(1024)}, u32[]{:S(2)}) copy-start(f32[896]{0:T(1024)} %param.22) | copy-start | bytes 10756
  4.1 37.3 %copy-start.12 = (f32[128]{0:T(128)S(1)}, f32[128]{0:T(128)}, u32[]{:S(2)}) copy-start(f32[128]{0:T(128)} %param.24) | copy-start | bytes 1540
  5.2 45.1 %copy-start.14 = (s32[8]{0:T(128)S(1)}, s32[8]{0:T(128)}, u32[]{:S(2)}) copy-start(s32[8]{0:T(128)} %constant.133.clone) | copy-start | bytes 100
  5.2 47.6 %slice-start.2 = ((f32[896]{0:T(1024)}), f32[512]{0:T(512)S(1)}, s32[]{:S(2)}) async-start(f32[896]{0:T(1024)} %param.22), calls=%async_computation.2 | async-start | bytes 4096 | tf_op jit(solution)/shard_map/slice | solution.py:109
  6.5 9.3 %collective-permute-start.3 = (bf16[224,576]{1,0:T(8,128)(2,1)S(1)}, bf16[224,576]{1,0:T(8,128)(2,1)S(1)}, u32[]{:S(2)}, u32[]{:S(2)}) collective-permute-start(bf16[224,576]{1,0:T(8,128)(2,1)S(1)} %get-tuple-element.424), channel_id=1, source_target_pairs={{0,4},{4,8},{8,12},{12,14},{14,10},{10,6},{6,2},{2,0},{1,5},{5,9},... | collective-permute-start | bytes 774152 | tf_op jit(solution)/shard_map/ppermute | solution.py:47
  8.2 9.2 %collective-permute-start.10 = (bf16[224,576]{1,0:T(8,128)(2,1)S(1)}, bf16[224,576]{1,0:T(8,128)(2,1)S(1)}, u32[]{:S(2)}, u32[]{:S(2)}) collective-permute-start(bf16[224,576]{1,0:T(8,128)(2,1)S(1)} %get-tuple-element.421), channel_id=1, source_target_pairs={{0,2},{4,0},{8,4},{12,8},{14,12},{10,14},{6,10},{2,6},{1,3},{5,1},... | collective-permute-start | bytes 774152 | tf_op jit(solution)/shard_map/ppermute | solution.py:48
  15.8 8.6 %collective-permute-start.4 = (bf16[224,576]{1,0:T(8,128)(2,1)S(1)}, bf16[224,576]{1,0:T(8,128)(2,1)S(1)}, u32[]{:S(2)}, u32[]{:S(2)}) collective-permute-start(bf16[224,576]{1,0:T(8,128)(2,1)S(1)} %collective-permute-done.3), channel_id=1, source_target_pairs={{0,4},{4,8},{8,12},{12,14},{14,10},{10,6},{6,2},{2,0},{1,5},{5,9},... | collective-permute-start | bytes 774152 | tf_op jit(solution)/shard_map/ppermute | solution.py:47
  17.4 8.6 %collective-permute-start.11 = (bf16[224,576]{1,0:T(8,128)(2,1)S(1)}, bf16[224,576]{1,0:T(8,128)(2,1)S(1)}, u32[]{:S(2)}, u32[]{:S(2)}) collective-permute-start(bf16[224,576]{1,0:T(8,128)(2,1)S(1)} %collective-permute-done.10), channel_id=1, source_target_pairs={{0,2},{4,0},{8,4},{12,8},{14,12},{10,14},{6,10},{2,6},{1,3},{5,1},... | collective-permute-start | bytes 774152 | tf_op jit(solution)/shard_map/ppermute | solution.py:48
  24.4 7.8 %collective-permute-start.5 = (bf16[224,576]{1,0:T(8,128)(2,1)S(1)}, bf16[224,576]{1,0:T(8,128)(2,1)S(1)}, u32[]{:S(2)}, u32[]{:S(2)}) collective-permute-start(bf16[224,576]{1,0:T(8,128)(2,1)S(1)} %collective-permute-done.4), channel_id=1, source_target_pairs={{0,4},{4,8},{8,12},{12,14},{14,10},{10,6},{6,2},{2,0},{1,5},{5,9},... | collective-permute-start | bytes 774152 | tf_op jit(solution)/shard_map/ppermute | solution.py:47
  26.0 7.8 %collective-permute-start.12 = (bf16[224,576]{1,0:T(8,128)(2,1)S(1)}, bf16[224,576]{1,0:T(8,128)(2,1)S(1)}, u32[]{:S(2)}, u32[]{:S(2)}) collective-permute-start(bf16[224,576]{1,0:T(8,128)(2,1)S(1)} %collective-permute-done.11), channel_id=1, source_target_pairs={{0,2},{4,0},{8,4},{12,8},{14,12},{10,14},{6,10},{2,6},{1,3},{5,1},... | collective-permute-start | bytes 774152 | tf_op jit(solution)/shard_map/ppermute | solution.py:48
  32.2 7.0 %collective-permute-start.6 = (bf16[224,576]{1,0:T(8,128)(2,1)S(1)}, bf16[224,576]{1,0:T(8,128)(2,1)S(1)}, u32[]{:S(2)}, u32[]{:S(2)}) collective-permute-start(bf16[224,576]{1,0:T(8,128)(2,1)S(1)} %collective-permute-done.5), channel_id=1, source_target_pairs={{0,4},{4,8},{8,12},{12,14},{14,10},{10,6},{6,2},{2,0},{1,5},{5,9},... | collective-permute-start | bytes 774152 | tf_op jit(solution)/shard_map/ppermute | solution.py:47
  33.8 7.0 %collective-permute-start.13 = (bf16[224,576]{1,0:T(8,128)(2,1)S(1)}, bf16[224,576]{1,0:T(8,128)(2,1)S(1)}, u32[]{:S(2)}, u32[]{:S(2)}) collective-permute-start(bf16[224,576]{1,0:T(8,128)(2,1)S(1)} %collective-permute-done.12), channel_id=1, source_target_pairs={{0,2},{4,0},{8,4},{12,8},{14,12},{10,14},{6,10},{2,6},{1,3},{5,1},... | collective-permute-start | bytes 774152 | tf_op jit(solution)/shard_map/ppermute | solution.py:48
  39.2 7.8 %collective-permute-start.7 = (bf16[224,576]{1,0:T(8,128)(2,1)S(1)}, bf16[224,576]{1,0:T(8,128)(2,1)S(1)}, u32[]{:S(2)}, u32[]{:S(2)}) collective-permute-start(bf16[224,576]{1,0:T(8,128)(2,1)S(1)} %collective-permute-done.6), channel_id=1, source_target_pairs={{0,4},{4,8},{8,12},{12,14},{14,10},{10,6},{6,2},{2,0},{1,5},{5,9},... | collective-permute-start | bytes 774152 | tf_op jit(solution)/shard_map/ppermute | solution.py:47
  40.8 7.8 %collective-permute-start.14 = (bf16[224,576]{1,0:T(8,128)(2,1)S(1)}, bf16[224,576]{1,0:T(8,128)(2,1)S(1)}, u32[]{:S(2)}, u32[]{:S(2)}) collective-permute-start(bf16[224,576]{1,0:T(8,128)(2,1)S(1)} %collective-permute-done.13), channel_id=1, source_target_pairs={{0,2},{4,0},{8,4},{12,8},{14,12},{10,14},{6,10},{2,6},{1,3},{5,1},... | collective-permute-start | bytes 774152 | tf_op jit(solution)/shard_map/ppermute | solution.py:48
  41.3 27.8 %collective-permute-start.2 = (bf16[2,128,1792]{2,1,0:T(8,128)(2,1)}, bf16[2,128,1792]{2,1,0:T(8,128)(2,1)}, u32[]{:S(2)}, u32[]{:S(2)}) collective-permute-start(bf16[2,128,1792]{2,1,0:T(8,128)(2,1)} %collective-permute-done.1), channel_id=1, source_target_pairs={{0,1},{1,0},{2,3},{3,2},{4,5},{5,4},{6,7},{7,6},{8,9},{9,8},{10,11... | collective-permute-start | bytes 2752520 | tf_op jit(solution)/shard_map/ppermute | solution.py:116
  47.0 8.3 %collective-permute-start.8 = (bf16[224,576]{1,0:T(8,128)(2,1)S(1)}, bf16[224,576]{1,0:T(8,128)(2,1)}, u32[]{:S(2)}, u32[]{:S(2)}) collective-permute-start(bf16[224,576]{1,0:T(8,128)(2,1)S(1)} %collective-permute-done.7), channel_id=1, source_target_pairs={{0,4},{4,8},{8,12},{12,14},{14,10},{10,6},{6,2},{2,0},{1,5},{5,9},... | collective-permute-start | bytes 774152 | tf_op jit(solution)/shard_map/ppermute | solution.py:47
  48.6 8.4 %collective-permute-start.15 = (bf16[224,576]{1,0:T(8,128)(2,1)S(1)}, bf16[224,576]{1,0:T(8,128)(2,1)}, u32[]{:S(2)}, u32[]{:S(2)}) collective-permute-start(bf16[224,576]{1,0:T(8,128)(2,1)S(1)} %collective-permute-done.14), channel_id=1, source_target_pairs={{0,2},{4,0},{8,4},{12,8},{14,12},{10,14},{6,10},{2,6},{1,3},{5,1},... | collective-permute-start | bytes 774152 | tf_op jit(solution)/shard_map/ppermute | solution.py:48
  55.3 6.8 %collective-permute-start.9 = (bf16[224,576]{1,0:T(8,128)(2,1)}, bf16[224,576]{1,0:T(8,128)(2,1)S(1)}, u32[]{:S(2)}, u32[]{:S(2)}) collective-permute-start(bf16[224,576]{1,0:T(8,128)(2,1)} %collective-permute-done.8), channel_id=1, source_target_pairs={{0,4},{4,8},{8,12},{12,14},{14,10},{10,6},{6,2},{2,0},{1,5},{5,9},... | collective-permute-start | bytes 774152 | tf_op jit(solution)/shard_map/ppermute | solution.py:47
  57.0 6.8 %collective-permute-start.16 = (bf16[224,576]{1,0:T(8,128)(2,1)}, bf16[224,576]{1,0:T(8,128)(2,1)S(1)}, u32[]{:S(2)}, u32[]{:S(2)}) collective-permute-start(bf16[224,576]{1,0:T(8,128)(2,1)} %collective-permute-done.15), channel_id=1, source_target_pairs={{0,2},{4,0},{8,4},{12,8},{14,12},{10,14},{6,10},{2,6},{1,3},{5,1},... | collective-permute-start | bytes 774152 | tf_op jit(solution)/shard_map/ppermute | solution.py:48
  79.4 6.8 %collective-permute-start.17 = (bf16[2,128,576]{1,0,2:T(2,128)(2,1)S(1)}, bf16[2,128,576]{1,0,2:T(2,128)(2,1)S(1)}, u32[]{:S(2)}, u32[]{:S(2)}) collective-permute-start(bf16[2,128,576]{1,0,2:T(2,128)(2,1)S(1)} %fusion.24), channel_id=1, source_target_pairs={{0,16},{16,0},{1,17},{17,1},{2,18},{18,2},{3,19},{19,3},{4,20},{20... | collective-permute-start | bytes 884744 | tf_op jit(solution)/shard_map/ppermute | solution.py:148
  87.5 12.7 %collective-permute-start.18 = (bf16[2,128,256]{1,0,2:T(2,128)(2,1)S(1)}, bf16[2,128,256]{1,0,2:T(2,128)(2,1)S(1)}, u32[]{:S(2)}, u32[]{:S(2)}) collective-permute-start(bf16[2,128,256]{1,0,2:T(2,128)(2,1)S(1)} %pad_maximum_fusion.12), channel_id=1, source_target_pairs={{0,2},{2,4},{4,6},{6,8},{8,10},{10,12},{12,14},{14,0},{1,3},{3,5},... | collective-permute-start | bytes 393224 | tf_op jit(solution)/shard_map/ppermute | solution.py:159
  88.4 14.1 %collective-permute-start.19 = (bf16[2,128,256]{1,0,2:T(2,128)(2,1)S(1)}, bf16[2,128,256]{1,0,2:T(2,128)(2,1)S(1)}, u32[]{:S(2)}, u32[]{:S(2)}) collective-permute-start(bf16[2,128,256]{1,0,2:T(2,128)(2,1)S(1)} %pad_maximum_fusion.12), channel_id=1, source_target_pairs={{0,4},{2,6},{4,8},{6,10},{8,12},{10,14},{12,0},{14,2},{1,5},{3,7},... | collective-permute-start | bytes 393224 | tf_op jit(solution)/shard_map/ppermute | solution.py:159
  90.3 14.7 %collective-permute-start.20 = (bf16[2,128,256]{1,0,2:T(2,128)(2,1)S(1)}, bf16[2,128,256]{1,0,2:T(2,128)(2,1)S(1)}, u32[]{:S(2)}, u32[]{:S(2)}) collective-permute-start(bf16[2,128,256]{1,0,2:T(2,128)(2,1)S(1)} %pad_maximum_fusion.12), channel_id=1, source_target_pairs={{0,6},{2,8},{4,10},{6,12},{8,14},{10,0},{12,2},{14,4},{1,7},{3,9},... | collective-permute-start | bytes 393224 | tf_op jit(solution)/shard_map/ppermute | solution.py:159
  93.1 12.7 %collective-permute-start.21 = (bf16[2,128,256]{1,0,2:T(2,128)(2,1)S(1)}, bf16[2,128,256]{1,0,2:T(2,128)(2,1)S(1)}, u32[]{:S(2)}, u32[]{:S(2)}) collective-permute-start(bf16[2,128,256]{1,0,2:T(2,128)(2,1)S(1)} %pad_maximum_fusion.12), channel_id=1, source_target_pairs={{0,8},{2,10},{4,12},{6,14},{8,0},{10,2},{12,4},{14,6},{1,9},{3,11}... | collective-permute-start | bytes 393224 | tf_op jit(solution)/shard_map/ppermute | solution.py:159
  94.4 12.2 %collective-permute-start.22 = (bf16[2,128,256]{1,0,2:T(2,128)(2,1)S(1)}, bf16[2,128,256]{1,0,2:T(2,128)(2,1)S(1)}, u32[]{:S(2)}, u32[]{:S(2)}) collective-permute-start(bf16[2,128,256]{1,0,2:T(2,128)(2,1)S(1)} %pad_maximum_fusion.12), channel_id=1, source_target_pairs={{0,10},{2,12},{4,14},{6,0},{8,2},{10,4},{12,6},{14,8},{1,11},{3,13... | collective-permute-start | bytes 393224 | tf_op jit(solution)/shard_map/ppermute | solution.py:159
  100.2 7.2 %collective-permute-start.23 = (bf16[2,128,256]{1,0,2:T(2,128)(2,1)S(1)}, bf16[2,128,256]{1,0,2:T(2,128)(2,1)S(1)}, u32[]{:S(2)}, u32[]{:S(2)}) collective-permute-start(bf16[2,128,256]{1,0,2:T(2,128)(2,1)S(1)} %pad_maximum_fusion.12), channel_id=1, source_target_pairs={{0,12},{2,14},{4,0},{6,2},{8,4},{10,6},{12,8},{14,10},{1,13},{3,15... | collective-permute-start | bytes 393224 | tf_op jit(solution)/shard_map/ppermute | solution.py:159
  102.5 5.6 %collective-permute-start.24 = (bf16[2,128,256]{1,0,2:T(2,128)(2,1)S(1)}, bf16[2,128,256]{1,0,2:T(2,128)(2,1)S(1)}, u32[]{:S(2)}, u32[]{:S(2)}) collective-permute-start(bf16[2,128,256]{1,0,2:T(2,128)(2,1)S(1)} %pad_maximum_fusion.12), channel_id=1, source_target_pairs={{0,14},{2,0},{4,2},{6,4},{8,6},{10,8},{12,10},{14,12},{1,15},{3,1}... | collective-permute-start | bytes 393224 | tf_op jit(solution)/shard_map/ppermute | solution.py:159
  (11 other events, 21.6 us)

commit v13 on v3

--- a/solution.py
+++ b/solution.py
@@ -145,15 +145,11 @@
 
     pairs = jnp.concatenate([key, value_rows], axis=-1)
     if row_count <= 8:
-        by_shift = [pairs] + [
-            lax.ppermute(pairs, "row", [(i, (i + k) % row_count) for i in range(row_count)])
-            for k in range(1, row_count)
-        ]
-        gathered = jnp.stack(by_shift)
-        owner_slot = (here - jnp.arange(row_count, dtype=jnp.int32)) % row_count
+        spread = jnp.broadcast_to(pairs[None], (row_count,) + pairs.shape)
+        gathered = lax.all_to_all(spread, "row", 0, 0, tiled=True)
     else:
         gathered = lax.all_gather(pairs, "row", axis=0, tiled=False)
-        owner_slot = jnp.arange(row_count, dtype=jnp.int32)
+    owner_slot = jnp.arange(row_count, dtype=jnp.int32)
     gathered = gathered.reshape(
         row_count, passages, per_device, BLOCK_TOKENS, pairs_here, 2 * HEAD_SIZE
     )[:, :, :, :, 0]

time: 123 us -> 130 us (1.057); the launches traced: 121 us -> 130 us
  waiting for transfers between devices: 34.1 us -> 48.8 us
  starting transfers between devices: 30.3 us -> 23.4 us
    all_to_all x0 -> x1, waiting for transfers between devices: none -> 16.7 us  [shards(): gathered = lax.all_to_all(spread, 'row', 0, 0, tiled=True)]
    ppermute x7 -> x0, starting transfers between devices: 12.6 us -> none  [shards(): lax.ppermute(pairs, 'row', [(i, (i + k) % row_count) for i in range(row_c...]
    all_to_all x0 -> x1, starting transfers between devices: none -> 5.81 us  [shards(): gathered = lax.all_to_all(spread, 'row', 0, 0, tiled=True)]
    ppermute x7 -> x0, waiting for transfers between devices: 3.75 us -> none  [shards(): lax.ppermute(pairs, 'row', [(i, (i + k) % row_count) for i in range(row_c...]
    ppermute x7, waiting for transfers between devices: 23.9 us -> 25.7 us  [gather_rows(): ahead = lax.ppermute(ahead, 'row', forward)]
    unnamed x41 -> x34, local copies, waits for them, and re-layouts: 9.93 us -> 9.77 us
  transfers between devices with their start and end apart: 25 -> 19, of which waited for: 11 -> 9; matrix products, arithmetic and copies ran while one was open for 29% -> 26% of each run, Pallas kernels for 0% -> 0%
where the time goes in v13:
time: 130 us
  waiting for transfers between devices  48.8 us (38%)
  local copies, waits for them, and re-layouts  34 us (26%)
  starting transfers between devices  23.4 us (18%)
  other arithmetic  16.2 us (12%)
  matrix products  6.81 us (5%)
    ppermute x7, waiting for transfers between devices, gather_rows(): ahead = lax.ppermute(ahead, 'row', forward)  25.7 us
    all_to_all x1, waiting for transfers between devices, shards(): gathered = lax.all_to_all(spread, 'row', 0, 0, tiled=True)  16.7 us
    ppermute x7, starting transfers between devices, gather_rows(): ahead = lax.ppermute(ahead, 'row', forward)  11.1 us
    unnamed x34, local copies, waits for them, and re-layouts  9.77 us
    ppermute x1, waiting for transfers between devices, shards(): returned = lax.ppermute(result[passages:], 'groups', SWAP)  6.38 us
    all_to_all x1, starting transfers between devices, shards(): gathered = lax.all_to_all(spread, 'row', 0, 0, tiled=True)  5.81 us
    gather x1, local copies, waits for them, and re-layouts, gather_rows(): jnp.stack(behind_parts)[behind_pick]  3.89 us
    gather x1, local copies, waits for them, and re-layouts, gather_rows(): jnp.stack(ahead_parts)[ahead_pick]  3.87 us
  transfers between devices with their start and end apart: 19, of which 9 were waited for; matrix products, arithmetic and copies ran while one was open for 26% of the time, Pallas kernels for 0%

profile of v13, /device:TPU:0, one launch (start us, length us, event | category | flops | bytes accessed | tf_op | source)
XLA Modules:
  0.0 129.8 jit_solution(8689555895759119806)
XLA Ops:
  0.0 3.0 %collective-permute-start.1 = (bf16[2,128,1792]{2,1,0:T(8,128)(2,1)}, bf16[2,128,1792]{2,1,0:T(8,128)(2,1)S(1)}, u32[]{:S(2)}, u32[]{:S(2)}) collective-permute-start(bf16[2,128,1792]{2,1,0:T(8,128)(2,1)} %param.11), channel_id=1, source_target_pairs={{0,16},{16,0},{1,17},{17,1},{2,18},{18,2},{3,19},{19,3},{4,20},{20... | collective-permute-start | bytes 2752520 | tf_op jit(solution)/shard_map/ppermute | solution.py:105
  3.0 1.1 fusion.42
  5.2 1.2 fusion.20
  6.5 1.6 %collective-permute-start.3 = (bf16[224,576]{1,0:T(8,128)(2,1)S(1)}, bf16[224,576]{1,0:T(8,128)(2,1)S(1)}, u32[]{:S(2)}, u32[]{:S(2)}) collective-permute-start(bf16[224,576]{1,0:T(8,128)(2,1)S(1)} %get-tuple-element.11), channel_id=1, source_target_pairs={{0,4},{4,8},{8,12},{12,14},{14,10},{10,6},{6,2},{2,0},{1,5},{5,9},... | collective-permute-start | bytes 774152 | tf_op jit(solution)/shard_map/ppermute | solution.py:47
  11.8 4.0 %collective-permute-done.3 = bf16[224,576]{1,0:T(8,128)(2,1)S(1)} collective-permute-done((bf16[224,576]{1,0:T(8,128)(2,1)S(1)}, bf16[224,576]{1,0:T(8,128)(2,1)S(1)}, u32[]{:S(2)}, u32[]{:S(2)}) %collective-permute-start.3) | collective-permute-done | bytes 258080 | tf_op jit(solution)/shard_map/ppermute | solution.py:47
  15.8 1.6 %collective-permute-start.4 = (bf16[224,576]{1,0:T(8,128)(2,1)S(1)}, bf16[224,576]{1,0:T(8,128)(2,1)S(1)}, u32[]{:S(2)}, u32[]{:S(2)}) collective-permute-start(bf16[224,576]{1,0:T(8,128)(2,1)S(1)} %collective-permute-done.3), channel_id=1, source_target_pairs={{0,4},{4,8},{8,12},{12,14},{14,10},{10,6},{6,2},{2,0},{1,5},{5,9},... | collective-permute-start | bytes 774152 | tf_op jit(solution)/shard_map/ppermute | solution.py:47
  19.3 5.0 %collective-permute-done.4 = bf16[224,576]{1,0:T(8,128)(2,1)S(1)} collective-permute-done((bf16[224,576]{1,0:T(8,128)(2,1)S(1)}, bf16[224,576]{1,0:T(8,128)(2,1)S(1)}, u32[]{:S(2)}, u32[]{:S(2)}) %collective-permute-start.4) | collective-permute-done | bytes 258080 | tf_op jit(solution)/shard_map/ppermute | solution.py:47
  24.2 1.6 %collective-permute-start.5 = (bf16[224,576]{1,0:T(8,128)(2,1)S(1)}, bf16[224,576]{1,0:T(8,128)(2,1)S(1)}, u32[]{:S(2)}, u32[]{:S(2)}) collective-permute-start(bf16[224,576]{1,0:T(8,128)(2,1)S(1)} %collective-permute-done.4), channel_id=1, source_target_pairs={{0,4},{4,8},{8,12},{12,14},{14,10},{10,6},{6,2},{2,0},{1,5},{5,9},... | collective-permute-start | bytes 774152 | tf_op jit(solution)/shard_map/ppermute | solution.py:47
  27.8 4.1 %collective-permute-done.5 = bf16[224,576]{1,0:T(8,128)(2,1)S(1)} collective-permute-done((bf16[224,576]{1,0:T(8,128)(2,1)S(1)}, bf16[224,576]{1,0:T(8,128)(2,1)S(1)}, u32[]{:S(2)}, u32[]{:S(2)}) %collective-permute-start.5) | collective-permute-done | bytes 258080 | tf_op jit(solution)/shard_map/ppermute | solution.py:47
  31.8 1.6 %collective-permute-start.6 = (bf16[224,576]{1,0:T(8,128)(2,1)S(1)}, bf16[224,576]{1,0:T(8,128)(2,1)S(1)}, u32[]{:S(2)}, u32[]{:S(2)}) collective-permute-start(bf16[224,576]{1,0:T(8,128)(2,1)S(1)} %collective-permute-done.5), channel_id=1, source_target_pairs={{0,4},{4,8},{8,12},{12,14},{14,10},{10,6},{6,2},{2,0},{1,5},{5,9},... | collective-permute-start | bytes 774152 | tf_op jit(solution)/shard_map/ppermute | solution.py:47
  35.3 2.0 %maximum_select_fusion = bf16[2,128,3584]{2,1,0:T(8,128)(2,1)S(1)} fusion(bf16[2,128,1792]{2,1,0:T(8,128)(2,1)} %collective-permute-done, bf16[2,128,1792]{2,1,0:T(8,128)(2,1)S(1)} %copy-done.1, pred[]{:T(512)S(6)} %eq.13), kind=kLoop, calls=%fused_computation.14 | loop fusion | flops 8257536 | bytes 3670017 | tf_op jit(solution)/shard_map/jit(_where)/select_n | solution.py:107
  37.4 1.1 collective-permute-done.6
  38.5 1.6 %collective-permute-start.7 = (bf16[224,576]{1,0:T(8,128)(2,1)S(1)}, bf16[224,576]{1,0:T(8,128)(2,1)S(1)}, u32[]{:S(2)}, u32[]{:S(2)}) collective-permute-start(bf16[224,576]{1,0:T(8,128)(2,1)S(1)} %collective-permute-done.6), channel_id=1, source_target_pairs={{0,4},{4,8},{8,12},{12,14},{14,10},{10,6},{6,2},{2,0},{1,5},{5,9},... | collective-permute-start | bytes 774152 | tf_op jit(solution)/shard_map/ppermute | solution.py:47
  42.0 4.7 %collective-permute-done.7 = bf16[224,576]{1,0:T(8,128)(2,1)S(1)} collective-permute-done((bf16[224,576]{1,0:T(8,128)(2,1)S(1)}, bf16[224,576]{1,0:T(8,128)(2,1)S(1)}, u32[]{:S(2)}, u32[]{:S(2)}) %collective-permute-start.7) | collective-permute-done | bytes 258080 | tf_op jit(solution)/shard_map/ppermute | solution.py:47
  46.6 1.6 %collective-permute-start.8 = (bf16[224,576]{1,0:T(8,128)(2,1)S(1)}, bf16[224,576]{1,0:T(8,128)(2,1)S(1)}, u32[]{:S(2)}, u32[]{:S(2)}) collective-permute-start(bf16[224,576]{1,0:T(8,128)(2,1)S(1)} %collective-permute-done.7), channel_id=1, source_target_pairs={{0,4},{4,8},{8,12},{12,14},{14,10},{10,6},{6,2},{2,0},{1,5},{5,9},... | collective-permute-start | bytes 774152 | tf_op jit(solution)/shard_map/ppermute | solution.py:47
  50.1 3.8 %collective-permute-done.8 = bf16[224,576]{1,0:T(8,128)(2,1)S(1)} collective-permute-done((bf16[224,576]{1,0:T(8,128)(2,1)S(1)}, bf16[224,576]{1,0:T(8,128)(2,1)S(1)}, u32[]{:S(2)}, u32[]{:S(2)}) %collective-permute-start.8) | collective-permute-done | bytes 258080 | tf_op jit(solution)/shard_map/ppermute | solution.py:47
  53.9 1.6 %collective-permute-start.9 = (bf16[224,576]{1,0:T(8,128)(2,1)S(1)}, bf16[224,576]{1,0:T(8,128)(2,1)S(1)}, u32[]{:S(2)}, u32[]{:S(2)}) collective-permute-start(bf16[224,576]{1,0:T(8,128)(2,1)S(1)} %collective-permute-done.8), channel_id=1, source_target_pairs={{0,4},{4,8},{8,12},{12,14},{14,10},{10,6},{6,2},{2,0},{1,5},{5,9},... | collective-permute-start | bytes 774152 | tf_op jit(solution)/shard_map/ppermute | solution.py:47
  57.4 3.1 %collective-permute-done.9 = bf16[224,576]{1,0:T(8,128)(2,1)S(1)} collective-permute-done((bf16[224,576]{1,0:T(8,128)(2,1)S(1)}, bf16[224,576]{1,0:T(8,128)(2,1)S(1)}, u32[]{:S(2)}, u32[]{:S(2)}) %collective-permute-start.9) | collective-permute-done | bytes 258080 | tf_op jit(solution)/shard_map/ppermute | solution.py:47
  61.3 3.9 %gather_fusion = bf16[8,224,576]{2,1,0:T(8,128)(2,1)} fusion(bf16[8,224,576]{2,1,0:T(8,128)(2,1)} %bitcast_dynamic-update-slice_fusion.8, s32[1024]{0:T(1024)S(1)} %get-tuple-element.28), kind=kCustom, calls=%fused_computation | custom fusion | bytes 4128800 | tf_op jit(solution)/shard_map/gather | solution.py:56
  65.9 3.9 %gather_fusion.1 = bf16[8,224,576]{2,1,0:T(8,128)(2,1)} fusion(bf16[8,224,576]{2,1,0:T(8,128)(2,1)} %bitcast_dynamic-update-slice_fusion, s32[1024]{0:T(1024)S(1)} %get-tuple-element.27), kind=kCustom, calls=%fused_computation.1 | custom fusion | bytes 4128800 | tf_op jit(solution)/shard_map/gather | solution.py:56
  69.8 2.8 %pad_maximum_fusion = bf16[8,448,576]{2,1,0:T(8,128)(2,1)S(1)} fusion(bf16[8,224,576]{2,1,0:T(8,128)(2,1)} %gather_fusion.1, bf16[8,224,576]{2,1,0:T(8,128)(2,1)} %gather_fusion), kind=kLoop, calls=%fused_computation.12 | loop fusion | flops 8257536 | bytes 8257536 | tf_op jit(solution)/shard_map/concatenate | solution.py:55
  72.6 1.9 %maximum_select_fusion.1 = bf16[2,128,3584]{2,1,0:T(8,128)(2,1)S(1)} fusion(bf16[2,128,1792]{2,1,0:T(8,128)(2,1)} %collective-permute-done.2, bf16[2,128,1792]{2,1,0:T(8,128)(2,1)S(1)} %collective-permute-done.1, pred[]{:T(512)S(6)} %eq.13), kind=kLoop, calls=%fused_computation.15 | loop fusion | flops 8257536 | bytes 3670017 | tf_op jit(solution)/shard_map/jit(_where)/select_n | solution.py:112
  75.3 1.1 fusion.2
  76.4 2.4 %convolution_add_fusion = f32[512,576]{0,1:T(8,128)S(1)} fusion(bf16[512,3584]{1,0:T(8,128)(2,1)S(1)} %bitcast.135, bf16[3584,576]{1,0:T(8,128)(2,1)S(1)} %bitcast.130, f32[576]{0:T(1024)S(1)} %maximum_select_fusion.2), kind=kOutput, calls=%fused_computation.30 | convolution fusion | flops 2114224128 | bytes 8980736 | tf_op jit(solution)/shard_map/dot_general | solution.py:127
  81.5 6.4 %collective-permute-done.17 = bf16[2,128,576]{1,0,2:T(2,128)(2,1)S(1)} collective-permute-done((bf16[2,128,576]{1,0,2:T(2,128)(2,1)S(1)}, bf16[2,128,576]{1,0,2:T(2,128)(2,1)S(1)}, u32[]{:S(2)}, u32[]{:S(2)}) %collective-permute-start.17) | collective-permute-done | bytes 294944 | tf_op jit(solution)/shard_map/ppermute | solution.py:138
  88.8 1.1 broadcast_in_dim.30
  89.9 5.8 %all-to-all-start = ((bf16[8,2,128,256]{3,2,1,0:T(8,128)(2,1)}), bf16[8,2,128,256]{3,2,1,0:T(8,128)(2,1)}, u32[]{:S(2)}, u32[]{:S(2)}) async-start(bf16[8,2,128,256]{3,2,1,0:T(8,128)(2,1)} %broadcast_in_dim.30), calls=%async_computation | async-start | bytes 2097152 | tf_op jit(solution)/shard_map/all_to_all | solution.py:149
  98.8 1.8 %copy.46 = bf16[2,2,64,7,128]{4,2,3,1,0:T(8,128)(2,1)S(1)} copy(bf16[2,2,64,7,128]{2,1,0,4,3:T(2,128)(2,1)S(1)} %reshape.363) | data formatting | bytes 917504 | tf_op jit(solution)/shard_map/reshape | solution.py:182
  100.6 16.7 %all-to-all-done = bf16[8,2,128,256]{3,2,1,0:T(8,128)(2,1)} async-done(((bf16[8,2,128,256]{3,2,1,0:T(8,128)(2,1)}), bf16[8,2,128,256]{3,2,1,0:T(8,128)(2,1)}, u32[]{:S(2)}, u32[]{:S(2)}) %all-to-all-start) | async-done | bytes 1048608 | tf_op jit(solution)/shard_map/all_to_all | solution.py:149
  117.3 1.3 copy.44
  119.3 1.4 %gather_fusion.4 = bf16[12,64,256]{2,1,0:T(8,128)(2,1)} fusion(bf16[2,16,64,256]{3,2,0,1:T(8,128)(2,1)S(1)} %bitcast.127, s32[12]{0:T(128)S(1)} %reshape.331), kind=kCustom, calls=%fused_computation.4 | custom fusion | bytes 786528 | tf_op jit(solution)/shard_map/gather | solution.py:168
  128.5 1.3 %convert_element_type.60 = bf16[2,128,896]{2,1,0:T(8,128)(2,1)} reshape(bf16[2,2,64,7,128]{4,3,2,1,0:T(8,128)(2,1)S(1)} %copy.51) | data formatting | bytes 917504 | tf_op jit(solution)/shard_map/convert_element_type | solution.py:244
  (129 shorter events, 33.4 us)
Async XLA Ops:
  0.0 96.1 %copy-start = (s32[2,2,2]{2,1,0:T(2,128)S(1)}, s32[2,2,2]{2,1,0:T(2,128)}, u32[]{:S(2)}) copy-start(s32[2,2,2]{2,1,0:T(2,128)} %param.20) | copy-start | bytes 100
  0.0 35.3 %collective-permute-start.1 = (bf16[2,128,1792]{2,1,0:T(8,128)(2,1)}, bf16[2,128,1792]{2,1,0:T(8,128)(2,1)S(1)}, u32[]{:S(2)}, u32[]{:S(2)}) collective-permute-start(bf16[2,128,1792]{2,1,0:T(8,128)(2,1)} %param.11), channel_id=1, source_target_pairs={{0,16},{16,0},{1,17},{17,1},{2,18},{18,2},{3,19},{19,3},{4,20},{20... | collective-permute-start | bytes 2752520 | tf_op jit(solution)/shard_map/ppermute | solution.py:105
  3.0 32.4 %collective-permute-start = (bf16[2,128,1792]{2,1,0:T(8,128)(2,1)}, bf16[2,128,1792]{2,1,0:T(8,128)(2,1)}, u32[]{:S(2)}, u32[]{:S(2)}) collective-permute-start(bf16[2,128,1792]{2,1,0:T(8,128)(2,1)} %param.11), channel_id=1, source_target_pairs={{0,1},{1,0},{2,3},{3,2},{4,5},{5,4},{6,7},{7,6},{8,9},{9,8},{10,11... | collective-permute-start | bytes 2752520 | tf_op jit(solution)/shard_map/ppermute | solution.py:104
  3.0 5.6 %copy-start.9 = (s32[8]{0:T(128)S(1)}, s32[8]{0:T(128)}, u32[]{:S(2)}) copy-start(s32[8]{0:T(128)} %constant.136.clone) | copy-start | bytes 100
  3.0 6.8 %copy-start.8 = (s32[8]{0:T(128)S(1)}, s32[8]{0:T(128)}, u32[]{:S(2)}) copy-start(s32[8]{0:T(128)} %constant.137) | copy-start | bytes 100
  3.0 7.5 %copy-start.6 = (f32[128]{0:T(128)S(1)}, f32[128]{0:T(128)}, u32[]{:S(2)}) copy-start(f32[128]{0:T(128)} %param.18) | copy-start | bytes 1540
  3.0 7.6 %copy-start.4 = (f32[896]{0:T(1024)S(1)}, f32[896]{0:T(1024)}, u32[]{:S(2)}) copy-start(f32[896]{0:T(1024)} %param.14) | copy-start | bytes 10756
  3.0 7.6 %copy-start.7 = (f32[128]{0:T(128)S(1)}, f32[128]{0:T(128)}, u32[]{:S(2)}) copy-start(f32[128]{0:T(128)} %param.16) | copy-start | bytes 1540
  4.1 6.7 %slice-start = ((f32[896]{0:T(1024)}), f32[512]{0:T(512)S(1)}, s32[]{:S(2)}) async-start(f32[896]{0:T(1024)} %param.14), calls=%async_computation.1 | async-start | bytes 4096 | tf_op jit(solution)/shard_map/slice | solution.py:99
  6.5 9.3 %collective-permute-start.3 = (bf16[224,576]{1,0:T(8,128)(2,1)S(1)}, bf16[224,576]{1,0:T(8,128)(2,1)S(1)}, u32[]{:S(2)}, u32[]{:S(2)}) collective-permute-start(bf16[224,576]{1,0:T(8,128)(2,1)S(1)} %get-tuple-element.11), channel_id=1, source_target_pairs={{0,4},{4,8},{8,12},{12,14},{14,10},{10,6},{6,2},{2,0},{1,5},{5,9},... | collective-permute-start | bytes 774152 | tf_op jit(solution)/shard_map/ppermute | solution.py:47
  8.1 9.2 %collective-permute-start.10 = (bf16[224,576]{1,0:T(8,128)(2,1)S(1)}, bf16[224,576]{1,0:T(8,128)(2,1)S(1)}, u32[]{:S(2)}, u32[]{:S(2)}) collective-permute-start(bf16[224,576]{1,0:T(8,128)(2,1)S(1)} %get-tuple-element.12), channel_id=1, source_target_pairs={{0,2},{4,0},{8,4},{12,8},{14,12},{10,14},{6,10},{2,6},{1,3},{5,1},... | collective-permute-start | bytes 774152 | tf_op jit(solution)/shard_map/ppermute | solution.py:48
  10.9 24.5 %copy-start.1 = (bf16[2,128,1792]{2,1,0:T(8,128)(2,1)S(1)}, bf16[2,128,1792]{2,1,0:T(8,128)(2,1)}, u32[]{:S(2)}) copy-start(bf16[2,128,1792]{2,1,0:T(8,128)(2,1)} %param.11) | copy-start | bytes 2752516
  15.8 8.5 %collective-permute-start.4 = (bf16[224,576]{1,0:T(8,128)(2,1)S(1)}, bf16[224,576]{1,0:T(8,128)(2,1)S(1)}, u32[]{:S(2)}, u32[]{:S(2)}) collective-permute-start(bf16[224,576]{1,0:T(8,128)(2,1)S(1)} %collective-permute-done.3), channel_id=1, source_target_pairs={{0,4},{4,8},{8,12},{12,14},{14,10},{10,6},{6,2},{2,0},{1,5},{5,9},... | collective-permute-start | bytes 774152 | tf_op jit(solution)/shard_map/ppermute | solution.py:47
  17.4 8.5 %collective-permute-start.11 = (bf16[224,576]{1,0:T(8,128)(2,1)S(1)}, bf16[224,576]{1,0:T(8,128)(2,1)S(1)}, u32[]{:S(2)}, u32[]{:S(2)}) collective-permute-start(bf16[224,576]{1,0:T(8,128)(2,1)S(1)} %collective-permute-done.10), channel_id=1, source_target_pairs={{0,2},{4,0},{8,4},{12,8},{14,12},{10,14},{6,10},{2,6},{1,3},{5,1},... | collective-permute-start | bytes 774152 | tf_op jit(solution)/shard_map/ppermute | solution.py:48
  24.2 7.6 %collective-permute-start.5 = (bf16[224,576]{1,0:T(8,128)(2,1)S(1)}, bf16[224,576]{1,0:T(8,128)(2,1)S(1)}, u32[]{:S(2)}, u32[]{:S(2)}) collective-permute-start(bf16[224,576]{1,0:T(8,128)(2,1)S(1)} %collective-permute-done.4), channel_id=1, source_target_pairs={{0,4},{4,8},{8,12},{12,14},{14,10},{10,6},{6,2},{2,0},{1,5},{5,9},... | collective-permute-start | bytes 774152 | tf_op jit(solution)/shard_map/ppermute | solution.py:47
  25.8 7.6 %collective-permute-start.12 = (bf16[224,576]{1,0:T(8,128)(2,1)S(1)}, bf16[224,576]{1,0:T(8,128)(2,1)S(1)}, u32[]{:S(2)}, u32[]{:S(2)}) collective-permute-start(bf16[224,576]{1,0:T(8,128)(2,1)S(1)} %collective-permute-done.11), channel_id=1, source_target_pairs={{0,2},{4,0},{8,4},{12,8},{14,12},{10,14},{6,10},{2,6},{1,3},{5,1},... | collective-permute-start | bytes 774152 | tf_op jit(solution)/shard_map/ppermute | solution.py:48
  31.8 6.7 %collective-permute-start.6 = (bf16[224,576]{1,0:T(8,128)(2,1)S(1)}, bf16[224,576]{1,0:T(8,128)(2,1)S(1)}, u32[]{:S(2)}, u32[]{:S(2)}) collective-permute-start(bf16[224,576]{1,0:T(8,128)(2,1)S(1)} %collective-permute-done.5), channel_id=1, source_target_pairs={{0,4},{4,8},{8,12},{12,14},{14,10},{10,6},{6,2},{2,0},{1,5},{5,9},... | collective-permute-start | bytes 774152 | tf_op jit(solution)/shard_map/ppermute | solution.py:47
  33.4 7.4 %collective-permute-start.13 = (bf16[224,576]{1,0:T(8,128)(2,1)S(1)}, bf16[224,576]{1,0:T(8,128)(2,1)S(1)}, u32[]{:S(2)}, u32[]{:S(2)}) collective-permute-start(bf16[224,576]{1,0:T(8,128)(2,1)S(1)} %collective-permute-done.12), channel_id=1, source_target_pairs={{0,2},{4,0},{8,4},{12,8},{14,12},{10,14},{6,10},{2,6},{1,3},{5,1},... | collective-permute-start | bytes 774152 | tf_op jit(solution)/shard_map/ppermute | solution.py:48
  35.3 37.2 %collective-permute-start.2 = (bf16[2,128,1792]{2,1,0:T(8,128)(2,1)S(1)}, bf16[2,128,1792]{2,1,0:T(8,128)(2,1)}, u32[]{:S(2)}, u32[]{:S(2)}) collective-permute-start(bf16[2,128,1792]{2,1,0:T(8,128)(2,1)S(1)} %collective-permute-done.1), channel_id=1, source_target_pairs={{0,1},{1,0},{2,3},{3,2},{4,5},{5,4},{6,7},{7,6},{8,9},{9,8},{10,11... | collective-permute-start | bytes 2752520 | tf_op jit(solution)/shard_map/ppermute | solution.py:106
  38.5 8.2 %collective-permute-start.7 = (bf16[224,576]{1,0:T(8,128)(2,1)S(1)}, bf16[224,576]{1,0:T(8,128)(2,1)S(1)}, u32[]{:S(2)}, u32[]{:S(2)}) collective-permute-start(bf16[224,576]{1,0:T(8,128)(2,1)S(1)} %collective-permute-done.6), channel_id=1, source_target_pairs={{0,4},{4,8},{8,12},{12,14},{14,10},{10,6},{6,2},{2,0},{1,5},{5,9},... | collective-permute-start | bytes 774152 | tf_op jit(solution)/shard_map/ppermute | solution.py:47
  40.8 8.2 %collective-permute-start.14 = (bf16[224,576]{1,0:T(8,128)(2,1)S(1)}, bf16[224,576]{1,0:T(8,128)(2,1)S(1)}, u32[]{:S(2)}, u32[]{:S(2)}) collective-permute-start(bf16[224,576]{1,0:T(8,128)(2,1)S(1)} %collective-permute-done.13), channel_id=1, source_target_pairs={{0,2},{4,0},{8,4},{12,8},{14,12},{10,14},{6,10},{2,6},{1,3},{5,1},... | collective-permute-start | bytes 774152 | tf_op jit(solution)/shard_map/ppermute | solution.py:48
  46.6 7.3 %collective-permute-start.8 = (bf16[224,576]{1,0:T(8,128)(2,1)S(1)}, bf16[224,576]{1,0:T(8,128)(2,1)S(1)}, u32[]{:S(2)}, u32[]{:S(2)}) collective-permute-start(bf16[224,576]{1,0:T(8,128)(2,1)S(1)} %collective-permute-done.7), channel_id=1, source_target_pairs={{0,4},{4,8},{8,12},{12,14},{14,10},{10,6},{6,2},{2,0},{1,5},{5,9},... | collective-permute-start | bytes 774152 | tf_op jit(solution)/shard_map/ppermute | solution.py:47
  49.0 7.3 %collective-permute-start.15 = (bf16[224,576]{1,0:T(8,128)(2,1)S(1)}, bf16[224,576]{1,0:T(8,128)(2,1)S(1)}, u32[]{:S(2)}, u32[]{:S(2)}) collective-permute-start(bf16[224,576]{1,0:T(8,128)(2,1)S(1)} %collective-permute-done.14), channel_id=1, source_target_pairs={{0,2},{4,0},{8,4},{12,8},{14,12},{10,14},{6,10},{2,6},{1,3},{5,1},... | collective-permute-start | bytes 774152 | tf_op jit(solution)/shard_map/ppermute | solution.py:48
  53.9 6.6 %collective-permute-start.9 = (bf16[224,576]{1,0:T(8,128)(2,1)S(1)}, bf16[224,576]{1,0:T(8,128)(2,1)S(1)}, u32[]{:S(2)}, u32[]{:S(2)}) collective-permute-start(bf16[224,576]{1,0:T(8,128)(2,1)S(1)} %collective-permute-done.8), channel_id=1, source_target_pairs={{0,4},{4,8},{8,12},{12,14},{14,10},{10,6},{6,2},{2,0},{1,5},{5,9},... | collective-permute-start | bytes 774152 | tf_op jit(solution)/shard_map/ppermute | solution.py:47
  56.2 8.9 %collective-permute-start.16 = (bf16[224,576]{1,0:T(8,128)(2,1)S(1)}, bf16[224,576]{1,0:T(8,128)(2,1)S(1)}, u32[]{:S(2)}, u32[]{:S(2)}) collective-permute-start(bf16[224,576]{1,0:T(8,128)(2,1)S(1)} %collective-permute-done.15), channel_id=1, source_target_pairs={{0,2},{4,0},{8,4},{12,8},{14,12},{10,14},{6,10},{2,6},{1,3},{5,1},... | collective-permute-start | bytes 774152 | tf_op jit(solution)/shard_map/ppermute | solution.py:48
  74.5 0.8 copy-start.3
  81.1 6.8 %collective-permute-start.17 = (bf16[2,128,576]{1,0,2:T(2,128)(2,1)S(1)}, bf16[2,128,576]{1,0,2:T(2,128)(2,1)S(1)}, u32[]{:S(2)}, u32[]{:S(2)}) collective-permute-start(bf16[2,128,576]{1,0,2:T(2,128)(2,1)S(1)} %fusion.25), channel_id=1, source_target_pairs={{0,16},{16,0},{1,17},{17,1},{2,18},{18,2},{3,19},{19,3},{4,20},{20... | collective-permute-start | bytes 884744 | tf_op jit(solution)/shard_map/ppermute | solution.py:138
  88.4 7.9 %copy-start.5 = (s32[2,16,14,2]{1,3,2,0:T(2,128)S(1)}, s32[2,16,14,2]{1,3,2,0:T(2,128)}, u32[]{:S(2)}) copy-start(s32[2,16,14,2]{1,3,2,0:T(2,128)} %param.19) | copy-start | bytes 10756
  89.9 27.4 %all-to-all-start = ((bf16[8,2,128,256]{3,2,1,0:T(8,128)(2,1)}), bf16[8,2,128,256]{3,2,1,0:T(8,128)(2,1)}, u32[]{:S(2)}, u32[]{:S(2)}) async-start(bf16[8,2,128,256]{3,2,1,0:T(8,128)(2,1)} %broadcast_in_dim.30), calls=%async_computation | async-start | bytes 2097152 | tf_op jit(solution)/shard_map/all_to_all | solution.py:149
  122.0 1.3 %copy-start.2 = (bf16[12,64,256]{2,1,0:T(8,128)(2,1)S(1)}, bf16[12,64,256]{2,1,0:T(8,128)(2,1)}, u32[]{:S(2)}) copy-start(bf16[12,64,256]{2,1,0:T(8,128)(2,1)} %gather_fusion.4) | copy-start | bytes 1179652

commit v14 on v3

--- a/solution.py
+++ b/solution.py
@@ -31,17 +31,17 @@
     return [2 * z for z in range(count // 2)] + [2 * z + 1 for z in reversed(range(count // 2))]
 
 
-def gather_rows(shard, count, here):
+def gather_rows(ahead, behind, count, here):
     if count != 8:
-        return lax.all_gather(shard, "row", axis=0, tiled=True)
+        shard = jnp.concatenate([ahead, behind], axis=0)
+        return lax.all_gather(shard, "row", axis=0, tiled=True), ahead
     order = snake_order(count)
     position = [0] * count
     for i, d in enumerate(order):
         position[d] = i
     forward = [(order[i], order[(i + 1) % count]) for i in range(count)]
     backward = [(order[i], order[(i - 1) % count]) for i in range(count)]
-    half = shard.shape[0] // 2
-    ahead, behind = shard[:half], shard[half:]
+    half = ahead.shape[0]
     ahead_parts, behind_parts = [ahead], [behind]
     for _ in range(count - 1):
         ahead = lax.ppermute(ahead, "row", forward)
@@ -55,7 +55,7 @@
     joined = jnp.concatenate(
         [jnp.stack(ahead_parts)[ahead_pick], jnp.stack(behind_parts)[behind_pick]], axis=1
     )
-    return joined.reshape(count * shard.shape[0], shard.shape[1])
+    return joined.reshape(count * 2 * half, ahead.shape[1]), ahead_parts[1]
 
 
 def shards(
@@ -89,20 +89,34 @@
     rotary_w = jnp.concatenate([w_query, key_weight], axis=1)
     rotary_b = jnp.concatenate([b_query, b_key], axis=0)
     first = group == 0
-    panel = jnp.where(
-        first,
-        jnp.concatenate([rotary_w[:, :split], value_weight[:, :value_split]], axis=1),
-        jnp.concatenate([rotary_w[:, split:], value_weight[:, value_split:]], axis=1),
+    rows_here = w_query.shape[0]
+
+    def panel_rows(start, stop):
+        return jnp.concatenate(
+            [
+                lax.dynamic_slice_in_dim(rotary_w[start:stop], group * split, split, 1),
+                lax.dynamic_slice_in_dim(
+                    value_weight[start:stop], group * value_split, value_split, 1
+                ),
+            ],
+            axis=1,
+        )
+
+    full_panel, first_arrival = gather_rows(
+        panel_rows(0, rows_here // 2),
+        panel_rows(rows_here // 2, rows_here),
+        row_count,
+        here,
     )
     panel_bias = jnp.where(
         first,
         jnp.concatenate([rotary_b[:split], value_bias[:value_split]]),
         jnp.concatenate([rotary_b[split:], value_bias[value_split:]]),
     )
-    full_panel = gather_rows(panel, row_count, here)
 
     other_half = lax.ppermute(tokens, "col", SWAP)
-    partner_half = lax.ppermute(tokens, "groups", SWAP)
+    late_tokens, _ = lax.optimization_barrier((tokens, first_arrival))
+    partner_half = lax.ppermute(late_tokens, "groups", SWAP)
     partner_other = lax.ppermute(partner_half, "col", SWAP)
     whole = jnp.where(
         column == 0,

time: 123 us -> 119 us (0.967)
  waiting for transfers between devices: 34.1 us -> 30.5 us
    ppermute x7, waiting for transfers between devices: 23.9 us -> 20.8 us  [gather_rows(): ahead = lax.ppermute(ahead, 'row', forward)]
    slice x3 -> x2, local copies, waits for them, and re-layouts: 2.19 us -> 0.07 us  [the longest x1 0.06 us: panel_rows(): rotary_w[start:stop]]
    unnamed x0 -> x2, other arithmetic: none -> 1.5 us
    ppermute x7, starting transfers between devices: 11.1 us -> 12.5 us  [gather_rows(): ahead = lax.ppermute(ahead, 'row', forward)]
    unnamed x41 -> x43, local copies, waits for them, and re-layouts: 9.93 us -> 10.4 us
  transfers between devices with their start and end apart: 25 -> 25, of which waited for: 11 -> 13; matrix products, arithmetic and copies ran while one was open for 29% -> 27% of each run, Pallas kernels for 0% -> 0%
where the time goes in v14:
time: 119 us; the launch traced here: 117 us
  local copies, waits for them, and re-layouts  32.2 us (27%)
  waiting for transfers between devices  30.5 us (26%)
  starting transfers between devices  30.1 us (25%)
  other arithmetic  16.5 us (14%)
  matrix products  6.82 us (6%)
    ppermute x7, waiting for transfers between devices, gather_rows(): ahead = lax.ppermute(ahead, 'row', forward)  20.8 us
    ppermute x7, starting transfers between devices, shards(): lax.ppermute(pairs, 'row', [(i, (i + k) % row_count) for i in range(row_c...  12.6 us
    ppermute x7, starting transfers between devices, gather_rows(): ahead = lax.ppermute(ahead, 'row', forward)  12.5 us
    unnamed x43, local copies, waits for them, and re-layouts  10.4 us
    ppermute x1, waiting for transfers between devices, shards(): returned = lax.ppermute(result[passages:], 'groups', SWAP)  6.42 us
    gather x1, local copies, waits for them, and re-layouts, gather_rows(): jnp.stack(behind_parts)[behind_pick]  3.9 us
    gather x1, local copies, waits for them, and re-layouts, gather_rows(): jnp.stack(ahead_parts)[ahead_pick]  3.88 us
    ppermute x7, waiting for transfers between devices, shards(): lax.ppermute(pairs, 'row', [(i, (i + k) % row_count) for i in range(row_c...  2.83 us
  transfers between devices with their start and end apart: 25, of which 13 were waited for; matrix products, arithmetic and copies ran while one was open for 27% of the time, Pallas kernels for 0%

profile of v14, /device:TPU:0, one launch (start us, length us, event | category | flops | bytes accessed | tf_op | source)
XLA Modules:
  0.0 117.0 jit_solution(8533901123085998046)
XLA Ops:
  0.0 1.3 %constant_dynamic-update-slice_fusion.1 = bf16[448,1024]{1,0:T(8,128)(2,1)S(1)} fusion(bf16[448,896]{1,0:T(8,128)(2,1)} %param.13), kind=kLoop, calls=%fused_computation.89 | loop fusion | bytes 1605632
  2.7 3.1 %collective-permute-start.1 = (bf16[224,576]{1,0:T(8,128)(2,1)S(1)}, bf16[224,576]{1,0:T(8,128)(2,1)S(1)}, u32[]{:S(2)}, u32[]{:S(2)}) collective-permute-start(bf16[224,576]{1,0:T(8,128)(2,1)S(1)} %pad_maximum_fusion.5), channel_id=1, source_target_pairs={{0,4},{4,8},{8,12},{12,14},{14,10},{10,6},{6,2},{2,0},{1,5},{5,9},... | collective-permute-start | bytes 774152 | tf_op jit(solution)/shard_map/ppermute | solution.py:47
  12.5 1.8 %collective-permute-start.2 = (bf16[2,128,1792]{2,1,0:T(8,128)(2,1)S(1)}, bf16[2,128,1792]{2,1,0:T(8,128)(2,1)}, u32[]{:S(2)}, u32[]{:S(2)}) collective-permute-start(bf16[2,128,1792]{2,1,0:T(8,128)(2,1)S(1)} %copy-done.1), channel_id=1, source_target_pairs={{0,16},{16,0},{1,17},{17,1},{2,18},{18,2},{3,19},{19,3},{4,20},{20... | collective-permute-start | bytes 2752520 | tf_op jit(solution)/shard_map/ppermute | solution.py:119
  14.3 1.6 %collective-permute-start.4 = (bf16[224,576]{1,0:T(8,128)(2,1)S(1)}, bf16[224,576]{1,0:T(8,128)(2,1)S(1)}, u32[]{:S(2)}, u32[]{:S(2)}) collective-permute-start(bf16[224,576]{1,0:T(8,128)(2,1)S(1)} %collective-permute-done.1), channel_id=1, source_target_pairs={{0,4},{4,8},{8,12},{12,14},{14,10},{10,6},{6,2},{2,0},{1,5},{5,9},... | collective-permute-start | bytes 774152 | tf_op jit(solution)/shard_map/ppermute | solution.py:47
  17.8 4.6 %collective-permute-done.4 = bf16[224,576]{1,0:T(8,128)(2,1)S(1)} collective-permute-done((bf16[224,576]{1,0:T(8,128)(2,1)S(1)}, bf16[224,576]{1,0:T(8,128)(2,1)S(1)}, u32[]{:S(2)}, u32[]{:S(2)}) %collective-permute-start.4) | collective-permute-done | bytes 258080 | tf_op jit(solution)/shard_map/ppermute | solution.py:47
  22.4 1.6 %collective-permute-start.5 = (bf16[224,576]{1,0:T(8,128)(2,1)S(1)}, bf16[224,576]{1,0:T(8,128)(2,1)S(1)}, u32[]{:S(2)}, u32[]{:S(2)}) collective-permute-start(bf16[224,576]{1,0:T(8,128)(2,1)S(1)} %collective-permute-done.4), channel_id=1, source_target_pairs={{0,4},{4,8},{8,12},{12,14},{14,10},{10,6},{6,2},{2,0},{1,5},{5,9},... | collective-permute-start | bytes 774152 | tf_op jit(solution)/shard_map/ppermute | solution.py:47
  25.9 3.8 %collective-permute-done.5 = bf16[224,576]{1,0:T(8,128)(2,1)S(1)} collective-permute-done((bf16[224,576]{1,0:T(8,128)(2,1)S(1)}, bf16[224,576]{1,0:T(8,128)(2,1)S(1)}, u32[]{:S(2)}, u32[]{:S(2)}) %collective-permute-start.5) | collective-permute-done | bytes 258080 | tf_op jit(solution)/shard_map/ppermute | solution.py:47
  29.7 1.6 %collective-permute-start.6 = (bf16[224,576]{1,0:T(8,128)(2,1)S(1)}, bf16[224,576]{1,0:T(8,128)(2,1)S(1)}, u32[]{:S(2)}, u32[]{:S(2)}) collective-permute-start(bf16[224,576]{1,0:T(8,128)(2,1)S(1)} %collective-permute-done.5), channel_id=1, source_target_pairs={{0,4},{4,8},{8,12},{12,14},{14,10},{10,6},{6,2},{2,0},{1,5},{5,9},... | collective-permute-start | bytes 774152 | tf_op jit(solution)/shard_map/ppermute | solution.py:47
  33.2 2.0 %maximum_select_fusion = bf16[2,128,3584]{2,1,0:T(8,128)(2,1)S(1)} fusion(bf16[2,128,1792]{2,1,0:T(8,128)(2,1)} %collective-permute-done, bf16[2,128,1792]{2,1,0:T(8,128)(2,1)S(1)} %copy-done.1, pred[]{:T(512)S(6)} %eq.14), kind=kLoop, calls=%fused_computation.14 | loop fusion | flops 8257536 | bytes 3670017 | tf_op jit(solution)/shard_map/jit(_where)/select_n | solution.py:121
  35.2 1.5 %collective-permute-done.6 = bf16[224,576]{1,0:T(8,128)(2,1)S(1)} collective-permute-done((bf16[224,576]{1,0:T(8,128)(2,1)S(1)}, bf16[224,576]{1,0:T(8,128)(2,1)S(1)}, u32[]{:S(2)}, u32[]{:S(2)}) %collective-permute-start.6) | collective-permute-done | bytes 258080 | tf_op jit(solution)/shard_map/ppermute | solution.py:47
  36.7 1.6 %collective-permute-start.7 = (bf16[224,576]{1,0:T(8,128)(2,1)S(1)}, bf16[224,576]{1,0:T(8,128)(2,1)S(1)}, u32[]{:S(2)}, u32[]{:S(2)}) collective-permute-start(bf16[224,576]{1,0:T(8,128)(2,1)S(1)} %collective-permute-done.6), channel_id=1, source_target_pairs={{0,4},{4,8},{8,12},{12,14},{14,10},{10,6},{6,2},{2,0},{1,5},{5,9},... | collective-permute-start | bytes 774152 | tf_op jit(solution)/shard_map/ppermute | solution.py:47
  40.2 3.1 %collective-permute-done.7 = bf16[224,576]{1,0:T(8,128)(2,1)S(1)} collective-permute-done((bf16[224,576]{1,0:T(8,128)(2,1)S(1)}, bf16[224,576]{1,0:T(8,128)(2,1)S(1)}, u32[]{:S(2)}, u32[]{:S(2)}) %collective-permute-start.7) | collective-permute-done | bytes 258080 | tf_op jit(solution)/shard_map/ppermute | solution.py:47
  43.3 1.6 %collective-permute-start.8 = (bf16[224,576]{1,0:T(8,128)(2,1)S(1)}, bf16[224,576]{1,0:T(8,128)(2,1)S(1)}, u32[]{:S(2)}, u32[]{:S(2)}) collective-permute-start(bf16[224,576]{1,0:T(8,128)(2,1)S(1)} %collective-permute-done.7), channel_id=1, source_target_pairs={{0,4},{4,8},{8,12},{12,14},{14,10},{10,6},{6,2},{2,0},{1,5},{5,9},... | collective-permute-start | bytes 774152 | tf_op jit(solution)/shard_map/ppermute | solution.py:47
  47.0 4.0 %collective-permute-done.8 = bf16[224,576]{1,0:T(8,128)(2,1)S(1)} collective-permute-done((bf16[224,576]{1,0:T(8,128)(2,1)S(1)}, bf16[224,576]{1,0:T(8,128)(2,1)S(1)}, u32[]{:S(2)}, u32[]{:S(2)}) %collective-permute-start.8) | collective-permute-done | bytes 258080 | tf_op jit(solution)/shard_map/ppermute | solution.py:47
  51.0 1.6 %collective-permute-start.9 = (bf16[224,576]{1,0:T(8,128)(2,1)S(1)}, bf16[224,576]{1,0:T(8,128)(2,1)S(1)}, u32[]{:S(2)}, u32[]{:S(2)}) collective-permute-start(bf16[224,576]{1,0:T(8,128)(2,1)S(1)} %collective-permute-done.8), channel_id=1, source_target_pairs={{0,4},{4,8},{8,12},{12,14},{14,10},{10,6},{6,2},{2,0},{1,5},{5,9},... | collective-permute-start | bytes 774152 | tf_op jit(solution)/shard_map/ppermute | solution.py:47
  54.7 2.9 %collective-permute-done.9 = bf16[224,576]{1,0:T(8,128)(2,1)S(1)} collective-permute-done((bf16[224,576]{1,0:T(8,128)(2,1)S(1)}, bf16[224,576]{1,0:T(8,128)(2,1)S(1)}, u32[]{:S(2)}, u32[]{:S(2)}) %collective-permute-start.9) | collective-permute-done | bytes 258080 | tf_op jit(solution)/shard_map/ppermute | solution.py:47
  58.4 3.9 %gather_fusion = bf16[8,224,576]{2,1,0:T(8,128)(2,1)} fusion(bf16[8,224,576]{2,1,0:T(8,128)(2,1)} %bitcast_dynamic-update-slice_fusion.8, s32[1024]{0:T(1024)S(1)} %get-tuple-element.28), kind=kCustom, calls=%fused_computation | custom fusion | bytes 4128800 | tf_op jit(solution)/shard_map/gather | solution.py:56
  63.1 3.9 %gather_fusion.1 = bf16[8,224,576]{2,1,0:T(8,128)(2,1)} fusion(bf16[8,224,576]{2,1,0:T(8,128)(2,1)} %bitcast_dynamic-update-slice_fusion, s32[1024]{0:T(1024)S(1)} %get-tuple-element.27), kind=kCustom, calls=%fused_computation.1 | custom fusion | bytes 4128800 | tf_op jit(solution)/shard_map/gather | solution.py:56
  67.0 2.8 %pad_maximum_fusion = bf16[8,448,576]{2,1,0:T(8,128)(2,1)S(1)} fusion(bf16[8,224,576]{2,1,0:T(8,128)(2,1)} %gather_fusion.1, bf16[8,224,576]{2,1,0:T(8,128)(2,1)} %gather_fusion), kind=kLoop, calls=%fused_computation.12 | loop fusion | flops 8257536 | bytes 8257536 | tf_op jit(solution)/shard_map/concatenate | solution.py:55
  69.7 2.0 %maximum_select_fusion.1 = bf16[2,128,3584]{2,1,0:T(8,128)(2,1)S(1)} fusion(bf16[2,128,1792]{2,1,0:T(8,128)(2,1)S(1)} %collective-permute-done.3, bf16[2,128,1792]{2,1,0:T(8,128)(2,1)} %collective-permute-done.2, pred[]{:T(512)S(6)} %eq.14), kind=kLoop, calls=%fused_computation.15 | loop fusion | flops 8257536 | bytes 3670017 | tf_op jit(solution)/shard_map/jit(_where)/select_n | solution.py:126
  73.6 2.4 %convolution_add_fusion = f32[512,576]{0,1:T(8,128)S(1)} fusion(bf16[512,3584]{1,0:T(8,128)(2,1)S(1)} %bitcast.140, bf16[3584,576]{1,0:T(8,128)(2,1)S(1)} %bitcast.135, f32[576]{0:T(1024)S(1)} %maximum_select_fusion.2), kind=kOutput, calls=%fused_computation.30 | convolution fusion | flops 2114224128 | bytes 8980736 | tf_op jit(solution)/shard_map/dot_general | solution.py:141
  78.6 6.4 %collective-permute-done.17 = bf16[2,128,576]{1,0,2:T(2,128)(2,1)S(1)} collective-permute-done((bf16[2,128,576]{1,0,2:T(2,128)(2,1)S(1)}, bf16[2,128,576]{1,0,2:T(2,128)(2,1)S(1)}, u32[]{:S(2)}, u32[]{:S(2)}) %collective-permute-start.17) | collective-permute-done | bytes 294944 | tf_op jit(solution)/shard_map/ppermute | solution.py:152
  86.3 1.5 %collective-permute-start.18 = (bf16[2,128,256]{1,0,2:T(2,128)(2,1)S(1)}, bf16[2,128,256]{1,0,2:T(2,128)(2,1)S(1)}, u32[]{:S(2)}, u32[]{:S(2)}) collective-permute-start(bf16[2,128,256]{1,0,2:T(2,128)(2,1)S(1)} %pad_maximum_fusion.7), channel_id=1, source_target_pairs={{0,2},{2,4},{4,6},{6,8},{8,10},{10,12},{12,14},{14,0},{1,3},{3,5},... | collective-permute-start | bytes 393224 | tf_op jit(solution)/shard_map/ppermute | solution.py:163
  87.8 1.6 %collective-permute-start.19 = (bf16[2,128,256]{1,0,2:T(2,128)(2,1)S(1)}, bf16[2,128,256]{1,0,2:T(2,128)(2,1)S(1)}, u32[]{:S(2)}, u32[]{:S(2)}) collective-permute-start(bf16[2,128,256]{1,0,2:T(2,128)(2,1)S(1)} %pad_maximum_fusion.7), channel_id=1, source_target_pairs={{0,4},{2,6},{4,8},{6,10},{8,12},{10,14},{12,0},{14,2},{1,5},{3,7},... | collective-permute-start | bytes 393224 | tf_op jit(solution)/shard_map/ppermute | solution.py:163
  89.4 2.6 %collective-permute-start.20 = (bf16[2,128,256]{1,0,2:T(2,128)(2,1)S(1)}, bf16[2,128,256]{1,0,2:T(2,128)(2,1)S(1)}, u32[]{:S(2)}, u32[]{:S(2)}) collective-permute-start(bf16[2,128,256]{1,0,2:T(2,128)(2,1)S(1)} %pad_maximum_fusion.7), channel_id=1, source_target_pairs={{0,6},{2,8},{4,10},{6,12},{8,14},{10,0},{12,2},{14,4},{1,7},{3,9},... | collective-permute-start | bytes 393224 | tf_op jit(solution)/shard_map/ppermute | solution.py:163
  93.2 2.6 %collective-permute-start.22 = (bf16[2,128,256]{1,0,2:T(2,128)(2,1)S(1)}, bf16[2,128,256]{1,0,2:T(2,128)(2,1)S(1)}, u32[]{:S(2)}, u32[]{:S(2)}) collective-permute-start(bf16[2,128,256]{1,0,2:T(2,128)(2,1)S(1)} %pad_maximum_fusion.7), channel_id=1, source_target_pairs={{0,10},{2,12},{4,14},{6,0},{8,2},{10,4},{12,6},{14,8},{1,11},{3,13... | collective-permute-start | bytes 393224 | tf_op jit(solution)/shard_map/ppermute | solution.py:163
  96.9 1.8 %copy.51 = bf16[2,2,64,7,128]{4,2,3,1,0:T(8,128)(2,1)S(1)} copy(bf16[2,2,64,7,128]{2,1,0,4,3:T(2,128)(2,1)S(1)} %reshape.378) | data formatting | bytes 917504 | tf_op jit(solution)/shard_map/reshape | solution.py:200
  98.8 1.4 %collective-permute-start.23 = (bf16[2,128,256]{1,0,2:T(2,128)(2,1)S(1)}, bf16[2,128,256]{1,0,2:T(2,128)(2,1)S(1)}, u32[]{:S(2)}, u32[]{:S(2)}) collective-permute-start(bf16[2,128,256]{1,0,2:T(2,128)(2,1)S(1)} %pad_maximum_fusion.7), channel_id=1, source_target_pairs={{0,12},{2,14},{4,0},{6,2},{8,4},{10,6},{12,8},{14,10},{1,13},{3,15... | collective-permute-start | bytes 393224 | tf_op jit(solution)/shard_map/ppermute | solution.py:163
  100.3 1.7 %collective-permute-start.24 = (bf16[2,128,256]{1,0,2:T(2,128)(2,1)S(1)}, bf16[2,128,256]{1,0,2:T(2,128)(2,1)S(1)}, u32[]{:S(2)}, u32[]{:S(2)}) collective-permute-start(bf16[2,128,256]{1,0,2:T(2,128)(2,1)S(1)} %pad_maximum_fusion.7), channel_id=1, source_target_pairs={{0,14},{2,0},{4,2},{6,4},{8,6},{10,8},{12,10},{14,12},{1,15},{3,1}... | collective-permute-start | bytes 393224 | tf_op jit(solution)/shard_map/ppermute | solution.py:163
  103.5 1.7 %collective-permute-done.23 = bf16[2,128,256]{1,0,2:T(2,128)(2,1)S(1)} collective-permute-done((bf16[2,128,256]{1,0,2:T(2,128)(2,1)S(1)}, bf16[2,128,256]{1,0,2:T(2,128)(2,1)S(1)}, u32[]{:S(2)}, u32[]{:S(2)}) %collective-permute-start.23) | collective-permute-done | bytes 131104 | tf_op jit(solution)/shard_map/ppermute | solution.py:163
  106.4 1.4 %gather_fusion.4 = bf16[12,64,256]{2,1,0:T(8,128)(2,1)} fusion(bf16[2,16,64,256]{3,2,0,1:T(8,128)(2,1)S(1)} %bitcast.132, s32[12]{0:T(128)S(1)} %reshape.346), kind=kCustom, calls=%fused_computation.4 | custom fusion | bytes 786528 | tf_op jit(solution)/shard_map/gather | solution.py:186
  115.7 1.3 %convert_element_type.60 = bf16[2,128,896]{2,1,0:T(8,128)(2,1)} reshape(bf16[2,2,64,7,128]{4,3,2,1,0:T(8,128)(2,1)S(1)} %copy.56) | data formatting | bytes 917504 | tf_op jit(solution)/shard_map/convert_element_type | solution.py:262
  (164 shorter events, 39.7 us)
Async XLA Ops:
  0.0 8.3 %copy-start = (s32[2,2,2]{2,1,0:T(2,128)S(1)}, s32[2,2,2]{2,1,0:T(2,128)}, u32[]{:S(2)}) copy-start(s32[2,2,2]{2,1,0:T(2,128)} %param.20) | copy-start | bytes 100
  1.3 6.2 %copy-start.9 = (s32[8]{0:T(128)S(1)}, s32[8]{0:T(128)}, u32[]{:S(2)}) copy-start(s32[8]{0:T(128)} %constant.148) | copy-start | bytes 100
  1.3 6.8 %copy-start.7 = (f32[128]{0:T(128)S(1)}, f32[128]{0:T(128)}, u32[]{:S(2)}) copy-start(f32[128]{0:T(128)} %param.18) | copy-start | bytes 1540
  1.3 6.9 %copy-start.5 = (f32[896]{0:T(1024)S(1)}, f32[896]{0:T(1024)}, u32[]{:S(2)}) copy-start(f32[896]{0:T(1024)} %param.14) | copy-start | bytes 10756
  1.4 6.9 %copy-start.8 = (f32[128]{0:T(128)S(1)}, f32[128]{0:T(128)}, u32[]{:S(2)}) copy-start(f32[128]{0:T(128)} %param.16) | copy-start | bytes 1540
  2.4 6.0 %copy-start.6 = (s32[2,16,14,2]{1,3,2,0:T(2,128)S(1)}, s32[2,16,14,2]{1,3,2,0:T(2,128)}, u32[]{:S(2)}) copy-start(s32[2,16,14,2]{1,3,2,0:T(2,128)} %param.19) | copy-start | bytes 10756
  2.4 6.4 %slice-start = ((f32[896]{0:T(1024)}), f32[512]{0:T(512)S(1)}, s32[]{:S(2)}) async-start(f32[896]{0:T(1024)} %param.14), calls=%async_computation | async-start | bytes 4096 | tf_op jit(solution)/shard_map/slice | solution.py:113
  2.7 9.8 %collective-permute-start.1 = (bf16[224,576]{1,0:T(8,128)(2,1)S(1)}, bf16[224,576]{1,0:T(8,128)(2,1)S(1)}, u32[]{:S(2)}, u32[]{:S(2)}) collective-permute-start(bf16[224,576]{1,0:T(8,128)(2,1)S(1)} %pad_maximum_fusion.5), channel_id=1, source_target_pairs={{0,4},{4,8},{8,12},{12,14},{14,10},{10,6},{6,2},{2,0},{1,5},{5,9},... | collective-permute-start | bytes 774152 | tf_op jit(solution)/shard_map/ppermute | solution.py:47
  5.9 9.9 %collective-permute-start.10 = (bf16[224,576]{1,0:T(8,128)(2,1)S(1)}, bf16[224,576]{1,0:T(8,128)(2,1)S(1)}, u32[]{:S(2)}, u32[]{:S(2)}) collective-permute-start(bf16[224,576]{1,0:T(8,128)(2,1)S(1)} %pad_maximum_fusion.6), channel_id=1, source_target_pairs={{0,2},{4,0},{8,4},{12,8},{14,12},{10,14},{6,10},{2,6},{1,3},{5,1},... | collective-permute-start | bytes 774152 | tf_op jit(solution)/shard_map/ppermute | solution.py:48
  6.0 27.3 %collective-permute-start = (bf16[2,128,1792]{2,1,0:T(8,128)(2,1)S(1)}, bf16[2,128,1792]{2,1,0:T(8,128)(2,1)}, u32[]{:S(2)}, u32[]{:S(2)}) collective-permute-start(bf16[2,128,1792]{2,1,0:T(8,128)(2,1)S(1)} %copy-done.1), channel_id=1, source_target_pairs={{0,1},{1,0},{2,3},{3,2},{4,5},{5,4},{6,7},{7,6},{8,9},{9,8},{10,11... | collective-permute-start | bytes 2752520 | tf_op jit(solution)/shard_map/ppermute | solution.py:117
  12.5 27.7 %collective-permute-start.2 = (bf16[2,128,1792]{2,1,0:T(8,128)(2,1)S(1)}, bf16[2,128,1792]{2,1,0:T(8,128)(2,1)}, u32[]{:S(2)}, u32[]{:S(2)}) collective-permute-start(bf16[2,128,1792]{2,1,0:T(8,128)(2,1)S(1)} %copy-done.1), channel_id=1, source_target_pairs={{0,16},{16,0},{1,17},{17,1},{2,18},{18,2},{3,19},{19,3},{4,20},{20... | collective-permute-start | bytes 2752520 | tf_op jit(solution)/shard_map/ppermute | solution.py:119
  14.3 8.1 %collective-permute-start.4 = (bf16[224,576]{1,0:T(8,128)(2,1)S(1)}, bf16[224,576]{1,0:T(8,128)(2,1)S(1)}, u32[]{:S(2)}, u32[]{:S(2)}) collective-permute-start(bf16[224,576]{1,0:T(8,128)(2,1)S(1)} %collective-permute-done.1), channel_id=1, source_target_pairs={{0,4},{4,8},{8,12},{12,14},{14,10},{10,6},{6,2},{2,0},{1,5},{5,9},... | collective-permute-start | bytes 774152 | tf_op jit(solution)/shard_map/ppermute | solution.py:47
  15.8 8.1 %collective-permute-start.11 = (bf16[224,576]{1,0:T(8,128)(2,1)S(1)}, bf16[224,576]{1,0:T(8,128)(2,1)S(1)}, u32[]{:S(2)}, u32[]{:S(2)}) collective-permute-start(bf16[224,576]{1,0:T(8,128)(2,1)S(1)} %collective-permute-done.10), channel_id=1, source_target_pairs={{0,2},{4,0},{8,4},{12,8},{14,12},{10,14},{6,10},{2,6},{1,3},{5,1},... | collective-permute-start | bytes 774152 | tf_op jit(solution)/shard_map/ppermute | solution.py:48
  22.4 7.3 %collective-permute-start.5 = (bf16[224,576]{1,0:T(8,128)(2,1)S(1)}, bf16[224,576]{1,0:T(8,128)(2,1)S(1)}, u32[]{:S(2)}, u32[]{:S(2)}) collective-permute-start(bf16[224,576]{1,0:T(8,128)(2,1)S(1)} %collective-permute-done.4), channel_id=1, source_target_pairs={{0,4},{4,8},{8,12},{12,14},{14,10},{10,6},{6,2},{2,0},{1,5},{5,9},... | collective-permute-start | bytes 774152 | tf_op jit(solution)/shard_map/ppermute | solution.py:47
  24.0 7.3 %collective-permute-start.12 = (bf16[224,576]{1,0:T(8,128)(2,1)S(1)}, bf16[224,576]{1,0:T(8,128)(2,1)S(1)}, u32[]{:S(2)}, u32[]{:S(2)}) collective-permute-start(bf16[224,576]{1,0:T(8,128)(2,1)S(1)} %collective-permute-done.11), channel_id=1, source_target_pairs={{0,2},{4,0},{8,4},{12,8},{14,12},{10,14},{6,10},{2,6},{1,3},{5,1},... | collective-permute-start | bytes 774152 | tf_op jit(solution)/shard_map/ppermute | solution.py:48
  29.7 7.0 %collective-permute-start.6 = (bf16[224,576]{1,0:T(8,128)(2,1)S(1)}, bf16[224,576]{1,0:T(8,128)(2,1)S(1)}, u32[]{:S(2)}, u32[]{:S(2)}) collective-permute-start(bf16[224,576]{1,0:T(8,128)(2,1)S(1)} %collective-permute-done.5), channel_id=1, source_target_pairs={{0,4},{4,8},{8,12},{12,14},{14,10},{10,6},{6,2},{2,0},{1,5},{5,9},... | collective-permute-start | bytes 774152 | tf_op jit(solution)/shard_map/ppermute | solution.py:47
  31.3 7.7 %collective-permute-start.13 = (bf16[224,576]{1,0:T(8,128)(2,1)S(1)}, bf16[224,576]{1,0:T(8,128)(2,1)S(1)}, u32[]{:S(2)}, u32[]{:S(2)}) collective-permute-start(bf16[224,576]{1,0:T(8,128)(2,1)S(1)} %collective-permute-done.12), channel_id=1, source_target_pairs={{0,2},{4,0},{8,4},{12,8},{14,12},{10,14},{6,10},{2,6},{1,3},{5,1},... | collective-permute-start | bytes 774152 | tf_op jit(solution)/shard_map/ppermute | solution.py:48
  36.7 6.6 %collective-permute-start.7 = (bf16[224,576]{1,0:T(8,128)(2,1)S(1)}, bf16[224,576]{1,0:T(8,128)(2,1)S(1)}, u32[]{:S(2)}, u32[]{:S(2)}) collective-permute-start(bf16[224,576]{1,0:T(8,128)(2,1)S(1)} %collective-permute-done.6), channel_id=1, source_target_pairs={{0,4},{4,8},{8,12},{12,14},{14,10},{10,6},{6,2},{2,0},{1,5},{5,9},... | collective-permute-start | bytes 774152 | tf_op jit(solution)/shard_map/ppermute | solution.py:47
  39.0 6.9 %collective-permute-start.14 = (bf16[224,576]{1,0:T(8,128)(2,1)S(1)}, bf16[224,576]{1,0:T(8,128)(2,1)S(1)}, u32[]{:S(2)}, u32[]{:S(2)}) collective-permute-start(bf16[224,576]{1,0:T(8,128)(2,1)S(1)} %collective-permute-done.13), channel_id=1, source_target_pairs={{0,2},{4,0},{8,4},{12,8},{14,12},{10,14},{6,10},{2,6},{1,3},{5,1},... | collective-permute-start | bytes 774152 | tf_op jit(solution)/shard_map/ppermute | solution.py:48
  40.2 29.5 %collective-permute-start.3 = (bf16[2,128,1792]{2,1,0:T(8,128)(2,1)}, bf16[2,128,1792]{2,1,0:T(8,128)(2,1)S(1)}, u32[]{:S(2)}, u32[]{:S(2)}) collective-permute-start(bf16[2,128,1792]{2,1,0:T(8,128)(2,1)} %collective-permute-done.2), channel_id=1, source_target_pairs={{0,1},{1,0},{2,3},{3,2},{4,5},{5,4},{6,7},{7,6},{8,9},{9,8},{10,11... | collective-permute-start | bytes 2752520 | tf_op jit(solution)/shard_map/ppermute | solution.py:120
  43.3 7.7 %collective-permute-start.8 = (bf16[224,576]{1,0:T(8,128)(2,1)S(1)}, bf16[224,576]{1,0:T(8,128)(2,1)S(1)}, u32[]{:S(2)}, u32[]{:S(2)}) collective-permute-start(bf16[224,576]{1,0:T(8,128)(2,1)S(1)} %collective-permute-done.7), channel_id=1, source_target_pairs={{0,4},{4,8},{8,12},{12,14},{14,10},{10,6},{6,2},{2,0},{1,5},{5,9},... | collective-permute-start | bytes 774152 | tf_op jit(solution)/shard_map/ppermute | solution.py:47
  45.9 7.7 %collective-permute-start.15 = (bf16[224,576]{1,0:T(8,128)(2,1)S(1)}, bf16[224,576]{1,0:T(8,128)(2,1)S(1)}, u32[]{:S(2)}, u32[]{:S(2)}) collective-permute-start(bf16[224,576]{1,0:T(8,128)(2,1)S(1)} %collective-permute-done.14), channel_id=1, source_target_pairs={{0,2},{4,0},{8,4},{12,8},{14,12},{10,14},{6,10},{2,6},{1,3},{5,1},... | collective-permute-start | bytes 774152 | tf_op jit(solution)/shard_map/ppermute | solution.py:48
  51.0 6.6 %collective-permute-start.9 = (bf16[224,576]{1,0:T(8,128)(2,1)S(1)}, bf16[224,576]{1,0:T(8,128)(2,1)S(1)}, u32[]{:S(2)}, u32[]{:S(2)}) collective-permute-start(bf16[224,576]{1,0:T(8,128)(2,1)S(1)} %collective-permute-done.8), channel_id=1, source_target_pairs={{0,4},{4,8},{8,12},{12,14},{14,10},{10,6},{6,2},{2,0},{1,5},{5,9},... | collective-permute-start | bytes 774152 | tf_op jit(solution)/shard_map/ppermute | solution.py:47
  53.5 8.8 %collective-permute-start.16 = (bf16[224,576]{1,0:T(8,128)(2,1)S(1)}, bf16[224,576]{1,0:T(8,128)(2,1)S(1)}, u32[]{:S(2)}, u32[]{:S(2)}) collective-permute-start(bf16[224,576]{1,0:T(8,128)(2,1)S(1)} %collective-permute-done.15), channel_id=1, source_target_pairs={{0,2},{4,0},{8,4},{12,8},{14,12},{10,14},{6,10},{2,6},{1,3},{5,1},... | collective-permute-start | bytes 774152 | tf_op jit(solution)/shard_map/ppermute | solution.py:48
  78.2 6.8 %collective-permute-start.17 = (bf16[2,128,576]{1,0,2:T(2,128)(2,1)S(1)}, bf16[2,128,576]{1,0,2:T(2,128)(2,1)S(1)}, u32[]{:S(2)}, u32[]{:S(2)}) collective-permute-start(bf16[2,128,576]{1,0,2:T(2,128)(2,1)S(1)} %fusion.23), channel_id=1, source_target_pairs={{0,16},{16,0},{1,17},{17,1},{2,18},{18,2},{3,19},{19,3},{4,20},{20... | collective-permute-start | bytes 884744 | tf_op jit(solution)/shard_map/ppermute | solution.py:152
  86.3 12.5 %collective-permute-start.18 = (bf16[2,128,256]{1,0,2:T(2,128)(2,1)S(1)}, bf16[2,128,256]{1,0,2:T(2,128)(2,1)S(1)}, u32[]{:S(2)}, u32[]{:S(2)}) collective-permute-start(bf16[2,128,256]{1,0,2:T(2,128)(2,1)S(1)} %pad_maximum_fusion.7), channel_id=1, source_target_pairs={{0,2},{2,4},{4,6},{6,8},{8,10},{10,12},{12,14},{14,0},{1,3},{3,5},... | collective-permute-start | bytes 393224 | tf_op jit(solution)/shard_map/ppermute | solution.py:163
  87.8 12.5 %collective-permute-start.19 = (bf16[2,128,256]{1,0,2:T(2,128)(2,1)S(1)}, bf16[2,128,256]{1,0,2:T(2,128)(2,1)S(1)}, u32[]{:S(2)}, u32[]{:S(2)}) collective-permute-start(bf16[2,128,256]{1,0,2:T(2,128)(2,1)S(1)} %pad_maximum_fusion.7), channel_id=1, source_target_pairs={{0,4},{2,6},{4,8},{6,10},{8,12},{10,14},{12,0},{14,2},{1,5},{3,7},... | collective-permute-start | bytes 393224 | tf_op jit(solution)/shard_map/ppermute | solution.py:163
  89.4 12.8 %collective-permute-start.20 = (bf16[2,128,256]{1,0,2:T(2,128)(2,1)S(1)}, bf16[2,128,256]{1,0,2:T(2,128)(2,1)S(1)}, u32[]{:S(2)}, u32[]{:S(2)}) collective-permute-start(bf16[2,128,256]{1,0,2:T(2,128)(2,1)S(1)} %pad_maximum_fusion.7), channel_id=1, source_target_pairs={{0,6},{2,8},{4,10},{6,12},{8,14},{10,0},{12,2},{14,4},{1,7},{3,9},... | collective-permute-start | bytes 393224 | tf_op jit(solution)/shard_map/ppermute | solution.py:163
  91.9 11.2 %collective-permute-start.21 = (bf16[2,128,256]{1,0,2:T(2,128)(2,1)S(1)}, bf16[2,128,256]{1,0,2:T(2,128)(2,1)S(1)}, u32[]{:S(2)}, u32[]{:S(2)}) collective-permute-start(bf16[2,128,256]{1,0,2:T(2,128)(2,1)S(1)} %pad_maximum_fusion.7), channel_id=1, source_target_pairs={{0,8},{2,10},{4,12},{6,14},{8,0},{10,2},{12,4},{14,6},{1,9},{3,11}... | collective-permute-start | bytes 393224 | tf_op jit(solution)/shard_map/ppermute | solution.py:163
  93.2 10.1 %collective-permute-start.22 = (bf16[2,128,256]{1,0,2:T(2,128)(2,1)S(1)}, bf16[2,128,256]{1,0,2:T(2,128)(2,1)S(1)}, u32[]{:S(2)}, u32[]{:S(2)}) collective-permute-start(bf16[2,128,256]{1,0,2:T(2,128)(2,1)S(1)} %pad_maximum_fusion.7), channel_id=1, source_target_pairs={{0,10},{2,12},{4,14},{6,0},{8,2},{10,4},{12,6},{14,8},{1,11},{3,13... | collective-permute-start | bytes 393224 | tf_op jit(solution)/shard_map/ppermute | solution.py:163
  98.8 6.4 %collective-permute-start.23 = (bf16[2,128,256]{1,0,2:T(2,128)(2,1)S(1)}, bf16[2,128,256]{1,0,2:T(2,128)(2,1)S(1)}, u32[]{:S(2)}, u32[]{:S(2)}) collective-permute-start(bf16[2,128,256]{1,0,2:T(2,128)(2,1)S(1)} %pad_maximum_fusion.7), channel_id=1, source_target_pairs={{0,12},{2,14},{4,0},{6,2},{8,4},{10,6},{12,8},{14,10},{1,13},{3,15... | collective-permute-start | bytes 393224 | tf_op jit(solution)/shard_map/ppermute | solution.py:163
  100.3 5.2 %collective-permute-start.24 = (bf16[2,128,256]{1,0,2:T(2,128)(2,1)S(1)}, bf16[2,128,256]{1,0,2:T(2,128)(2,1)S(1)}, u32[]{:S(2)}, u32[]{:S(2)}) collective-permute-start(bf16[2,128,256]{1,0,2:T(2,128)(2,1)S(1)} %pad_maximum_fusion.7), channel_id=1, source_target_pairs={{0,14},{2,0},{4,2},{6,4},{8,6},{10,8},{12,10},{14,12},{1,15},{3,1}... | collective-permute-start | bytes 393224 | tf_op jit(solution)/shard_map/ppermute | solution.py:163
  (5 other events, 14.2 us)

commit v15 on v14

--- a/solution.py
+++ b/solution.py
@@ -31,10 +31,11 @@
     return [2 * z for z in range(count // 2)] + [2 * z + 1 for z in reversed(range(count // 2))]
 
 
-def gather_rows(ahead, behind, count, here):
+def gather_rows(ahead, behind, count, here, rotate):
     if count != 8:
         shard = jnp.concatenate([ahead, behind], axis=0)
-        return lax.all_gather(shard, "row", axis=0, tiled=True), ahead
+        full = lax.all_gather(shard, "row", axis=0, tiled=True)
+        return jnp.roll(full, -rotate * shard.shape[0], axis=0), ahead
     order = snake_order(count)
     position = [0] * count
     for i, d in enumerate(order):
@@ -50,8 +51,9 @@
         behind_parts.append(behind)
     table = jnp.array(position, dtype=jnp.int32)
     mine = table[here]
-    ahead_pick = (mine - table) % count
-    behind_pick = (table - mine) % count
+    source = table[(jnp.arange(count, dtype=jnp.int32) + rotate) % count]
+    ahead_pick = (mine - source) % count
+    behind_pick = (source - mine) % count
     joined = jnp.concatenate(
         [jnp.stack(ahead_parts)[ahead_pick], jnp.stack(behind_parts)[behind_pick]], axis=1
     )
@@ -107,6 +109,7 @@
         panel_rows(rows_here // 2, rows_here),
         row_count,
         here,
+        (row_count // 2) * column,
     )
     panel_bias = jnp.where(
         first,
@@ -118,21 +121,23 @@
     late_tokens, _ = lax.optimization_barrier((tokens, first_arrival))
     partner_half = lax.ppermute(late_tokens, "groups", SWAP)
     partner_other = lax.ppermute(partner_half, "col", SWAP)
-    whole = jnp.where(
+    both = jnp.concatenate(
+        [
+            jnp.concatenate([tokens, other_half], axis=2),
+            jnp.concatenate([partner_half, partner_other], axis=2),
+        ],
+        axis=0,
+    )
+    features = both.shape[2]
+    gain_here = jnp.where(
         column == 0,
-        jnp.concatenate([tokens, other_half], axis=2),
-        jnp.concatenate([other_half, tokens], axis=2),
-    )
-    partner = jnp.where(
-        column == 0,
-        jnp.concatenate([partner_half, partner_other], axis=2),
-        jnp.concatenate([partner_other, partner_half], axis=2),
-    )
-    both = jnp.concatenate([whole, partner], axis=0)
+        gain,
+        jnp.concatenate([gain[features // 2 :], gain[: features // 2]]),
+    )
     widened = both.astype(jnp.float32)
     power = jnp.mean(widened * widened, axis=-1, keepdims=True)
     normed = (
-        (widened * lax.rsqrt(power + norm_eps) * gain)
+        (widened * lax.rsqrt(power + norm_eps) * gain_here)
         .astype(jnp.bfloat16)
         .reshape(2 * passages * length, -1)
     )

time: 119 us -> 127 us (1.067)
  waiting for transfers between devices: 30.5 us -> 36.4 us
  other arithmetic: 16.5 us -> 18.6 us
    ppermute x7, waiting for transfers between devices: 20.8 us -> 25.7 us  [gather_rows(): ahead = lax.ppermute(ahead, 'row', forward)]
    select_n x3 -> x2, other arithmetic: 4.57 us -> 0.02 us  [the longest x1 0.01 us: gather_rows(): source = table[(jnp.arange(count, dtype=jnp.int32) + rotate) % count]]
    reduce_sum x1, other arithmetic: 0.79 us -> 4.47 us  [shards(): power = jnp.mean(widened * widened, axis=-1, keepdims=True)]
    unnamed x43 -> x47, local copies, waits for them, and re-layouts: 10.4 us -> 8.41 us
    ppermute x7, waiting for transfers between devices: 0.42 us -> 1.97 us  [gather_rows(): behind = lax.ppermute(behind, 'row', backward)]
    concatenate x2, other arithmetic: 0.06 us -> 1.5 us  [panel_rows(): jnp.concatenate([lax.dynamic_slice_in_dim(rotary_w[start:stop], group * s...]
    convert_element_type x1, other arithmetic: 1.09 us -> 2.39 us  [shards(): normed = (widened * lax.rsqrt(power + norm_eps) * gain_here).astype(jnp.b...]
    gather x1, local copies, waits for them, and re-layouts: 3.88 us -> 2.61 us  [gather_rows(): jnp.stack(ahead_parts)[ahead_pick]]
  transfers between devices with their start and end apart: 25 -> 25, of which waited for: 13 -> 15; matrix products, arithmetic and copies ran while one was open for 27% -> 24% of each run, Pallas kernels for 0% -> 0%
where the time goes in v15:
time: 127 us; the launch traced here: 125 us
  waiting for transfers between devices  36.4 us (29%)
  local copies, waits for them, and re-layouts  31.8 us (25%)
  starting transfers between devices  30.6 us (24%)
  other arithmetic  18.6 us (15%)
  matrix products  6.81 us (5%)
    ppermute x7, waiting for transfers between devices, gather_rows(): ahead = lax.ppermute(ahead, 'row', forward)  25.7 us
    ppermute x7, starting transfers between devices, shards(): lax.ppermute(pairs, 'row', [(i, (i + k) % row_count) for i in range(row_c...  12.6 us
    ppermute x7, starting transfers between devices, gather_rows(): ahead = lax.ppermute(ahead, 'row', forward)  12.5 us
    unnamed x47, local copies, waits for them, and re-layouts  8.41 us
    ppermute x1, waiting for transfers between devices, shards(): returned = lax.ppermute(result[passages:], 'groups', SWAP)  5.58 us
    reduce_sum x1, other arithmetic, shards(): power = jnp.mean(widened * widened, axis=-1, keepdims=True)  4.47 us
    gather x1, local copies, waits for them, and re-layouts, gather_rows(): jnp.stack(behind_parts)[behind_pick]  3.86 us
    ppermute x7, waiting for transfers between devices, shards(): lax.ppermute(pairs, 'row', [(i, (i + k) % row_count) for i in range(row_c...  3.14 us
  transfers between devices with their start and end apart: 25, of which 15 were waited for; matrix products, arithmetic and copies ran while one was open for 24% of the time, Pallas kernels for 0%

profile of v15, /device:TPU:0, one launch (start us, length us, event | category | flops | bytes accessed | tf_op | source)
XLA Modules:
  0.0 125.1 jit_solution(8213622896469532905)
XLA Ops:
  3.4 3.0 %collective-permute-start.1 = (bf16[224,576]{1,0:T(8,128)(2,1)}, bf16[224,576]{1,0:T(8,128)(2,1)}, u32[]{:S(2)}, u32[]{:S(2)}) collective-permute-start(bf16[224,576]{1,0:T(8,128)(2,1)} %pad_maximum_fusion.4), channel_id=1, source_target_pairs={{0,4},{4,8},{8,12},{12,14},{14,10},{10,6},{6,2},{2,0},{1,5},{5,9},... | collective-permute-start | bytes 774152 | tf_op jit(solution)/shard_map/ppermute | solution.py:48
  14.6 2.0 %collective-permute-start.2 = (bf16[2,128,1792]{2,1,0:T(8,128)(2,1)S(1)}, bf16[2,128,1792]{2,1,0:T(8,128)(2,1)}, u32[]{:S(2)}, u32[]{:S(2)}) collective-permute-start(bf16[2,128,1792]{2,1,0:T(8,128)(2,1)S(1)} %copy-done.2), channel_id=1, source_target_pairs={{0,16},{16,0},{1,17},{17,1},{2,18},{18,2},{3,19},{19,3},{4,20},{20... | collective-permute-start | bytes 2752520 | tf_op jit(solution)/shard_map/ppermute | solution.py:122
  16.5 1.6 %collective-permute-start.4 = (bf16[224,576]{1,0:T(8,128)(2,1)}, bf16[224,576]{1,0:T(8,128)(2,1)S(1)}, u32[]{:S(2)}, u32[]{:S(2)}) collective-permute-start(bf16[224,576]{1,0:T(8,128)(2,1)} %collective-permute-done.1), channel_id=1, source_target_pairs={{0,4},{4,8},{8,12},{12,14},{14,10},{10,6},{6,2},{2,0},{1,5},{5,9},... | collective-permute-start | bytes 774152 | tf_op jit(solution)/shard_map/ppermute | solution.py:48
  18.1 1.7 %bitcast_dynamic-update-slice_fusion.14 = bf16[8,224,576]{2,1,0:T(8,128)(2,1)} fusion(bf16[8,224,576]{2,1,0:T(8,128)(2,1)} %bitcast_dynamic-update-slice_fusion.15, bf16[224,576]{1,0:T(8,128)(2,1)} %collective-permute-done.1), kind=kLoop, calls=%fused_computation.75 | loop fusion | bytes 573440
  21.3 4.4 %collective-permute-done.4 = bf16[224,576]{1,0:T(8,128)(2,1)S(1)} collective-permute-done((bf16[224,576]{1,0:T(8,128)(2,1)}, bf16[224,576]{1,0:T(8,128)(2,1)S(1)}, u32[]{:S(2)}, u32[]{:S(2)}) %collective-permute-start.4) | collective-permute-done | bytes 258080 | tf_op jit(solution)/shard_map/ppermute | solution.py:48
  25.7 1.6 %collective-permute-start.5 = (bf16[224,576]{1,0:T(8,128)(2,1)S(1)}, bf16[224,576]{1,0:T(8,128)(2,1)S(1)}, u32[]{:S(2)}, u32[]{:S(2)}) collective-permute-start(bf16[224,576]{1,0:T(8,128)(2,1)S(1)} %collective-permute-done.4), channel_id=1, source_target_pairs={{0,4},{4,8},{8,12},{12,14},{14,10},{10,6},{6,2},{2,0},{1,5},{5,9},... | collective-permute-start | bytes 774152 | tf_op jit(solution)/shard_map/ppermute | solution.py:48
  29.2 4.7 %collective-permute-done.5 = bf16[224,576]{1,0:T(8,128)(2,1)S(1)} collective-permute-done((bf16[224,576]{1,0:T(8,128)(2,1)S(1)}, bf16[224,576]{1,0:T(8,128)(2,1)S(1)}, u32[]{:S(2)}, u32[]{:S(2)}) %collective-permute-start.5) | collective-permute-done | bytes 258080 | tf_op jit(solution)/shard_map/ppermute | solution.py:48
  34.0 1.6 %collective-permute-start.6 = (bf16[224,576]{1,0:T(8,128)(2,1)S(1)}, bf16[224,576]{1,0:T(8,128)(2,1)S(1)}, u32[]{:S(2)}, u32[]{:S(2)}) collective-permute-start(bf16[224,576]{1,0:T(8,128)(2,1)S(1)} %collective-permute-done.5), channel_id=1, source_target_pairs={{0,4},{4,8},{8,12},{12,14},{14,10},{10,6},{6,2},{2,0},{1,5},{5,9},... | collective-permute-start | bytes 774152 | tf_op jit(solution)/shard_map/ppermute | solution.py:48
  37.2 4.2 %collective-permute-done.6 = bf16[224,576]{1,0:T(8,128)(2,1)S(1)} collective-permute-done((bf16[224,576]{1,0:T(8,128)(2,1)S(1)}, bf16[224,576]{1,0:T(8,128)(2,1)S(1)}, u32[]{:S(2)}, u32[]{:S(2)}) %collective-permute-start.6) | collective-permute-done | bytes 258080 | tf_op jit(solution)/shard_map/ppermute | solution.py:48
  41.4 1.6 %collective-permute-start.7 = (bf16[224,576]{1,0:T(8,128)(2,1)S(1)}, bf16[224,576]{1,0:T(8,128)(2,1)S(1)}, u32[]{:S(2)}, u32[]{:S(2)}) collective-permute-start(bf16[224,576]{1,0:T(8,128)(2,1)S(1)} %collective-permute-done.6), channel_id=1, source_target_pairs={{0,4},{4,8},{8,12},{12,14},{14,10},{10,6},{6,2},{2,0},{1,5},{5,9},... | collective-permute-start | bytes 774152 | tf_op jit(solution)/shard_map/ppermute | solution.py:48
  44.4 4.2 %collective-permute-done.7 = bf16[224,576]{1,0:T(8,128)(2,1)S(1)} collective-permute-done((bf16[224,576]{1,0:T(8,128)(2,1)S(1)}, bf16[224,576]{1,0:T(8,128)(2,1)S(1)}, u32[]{:S(2)}, u32[]{:S(2)}) %collective-permute-start.7) | collective-permute-done | bytes 258080 | tf_op jit(solution)/shard_map/ppermute | solution.py:48
  48.6 1.6 %collective-permute-start.8 = (bf16[224,576]{1,0:T(8,128)(2,1)S(1)}, bf16[224,576]{1,0:T(8,128)(2,1)S(1)}, u32[]{:S(2)}, u32[]{:S(2)}) collective-permute-start(bf16[224,576]{1,0:T(8,128)(2,1)S(1)} %collective-permute-done.7), channel_id=1, source_target_pairs={{0,4},{4,8},{8,12},{12,14},{14,10},{10,6},{6,2},{2,0},{1,5},{5,9},... | collective-permute-start | bytes 774152 | tf_op jit(solution)/shard_map/ppermute | solution.py:48
  51.7 4.8 %collective-permute-done.8 = bf16[224,576]{1,0:T(8,128)(2,1)S(1)} collective-permute-done((bf16[224,576]{1,0:T(8,128)(2,1)S(1)}, bf16[224,576]{1,0:T(8,128)(2,1)S(1)}, u32[]{:S(2)}, u32[]{:S(2)}) %collective-permute-start.8) | collective-permute-done | bytes 258080 | tf_op jit(solution)/shard_map/ppermute | solution.py:48
  56.5 1.6 %collective-permute-start.9 = (bf16[224,576]{1,0:T(8,128)(2,1)S(1)}, bf16[224,576]{1,0:T(8,128)(2,1)S(1)}, u32[]{:S(2)}, u32[]{:S(2)}) collective-permute-start(bf16[224,576]{1,0:T(8,128)(2,1)S(1)} %collective-permute-done.8), channel_id=1, source_target_pairs={{0,4},{4,8},{8,12},{12,14},{14,10},{10,6},{6,2},{2,0},{1,5},{5,9},... | collective-permute-start | bytes 774152 | tf_op jit(solution)/shard_map/ppermute | solution.py:48
  59.8 3.3 %collective-permute-done.9 = bf16[224,576]{1,0:T(8,128)(2,1)S(1)} collective-permute-done((bf16[224,576]{1,0:T(8,128)(2,1)S(1)}, bf16[224,576]{1,0:T(8,128)(2,1)S(1)}, u32[]{:S(2)}, u32[]{:S(2)}) %collective-permute-start.9) | collective-permute-done | bytes 258080 | tf_op jit(solution)/shard_map/ppermute | solution.py:48
  63.9 2.6 %gather_fusion.1 = bf16[8,224,576]{2,1,0:T(8,128)(2,1)S(1)} fusion(bf16[8,224,576]{2,1,0:T(8,128)(2,1)} %bitcast_dynamic-update-slice_fusion.8, s32[1024]{0:T(1024)S(1)} %pad_clamp_fusion.3), kind=kCustom, calls=%fused_computation.1 | custom fusion | bytes 4128800 | tf_op jit(solution)/shard_map/gather | solution.py:58
  66.5 1.7 %bitcast_dynamic-update-slice_fusion = bf16[8,224,576]{2,1,0:T(8,128)(2,1)} fusion(bf16[8,224,576]{2,1,0:T(8,128)(2,1)} %copy-done.3, bf16[224,576]{1,0:T(8,128)(2,1)} %collective-permute-done.16), kind=kLoop, calls=%fused_computation.61 | loop fusion | bytes 573440 | tf_op jit(solution)/shard_map/stack | solution.py:58
  68.2 3.9 %gather_fusion.2 = bf16[8,224,576]{2,1,0:T(8,128)(2,1)} fusion(bf16[8,224,576]{2,1,0:T(8,128)(2,1)} %bitcast_dynamic-update-slice_fusion, s32[1024]{0:T(1024)S(1)} %pad_clamp_fusion.2), kind=kCustom, calls=%fused_computation.2 | custom fusion | bytes 4128800 | tf_op jit(solution)/shard_map/gather | solution.py:58
  72.0 2.1 %pad_maximum_fusion = bf16[8,448,576]{2,1,0:T(8,128)(2,1)S(1)} fusion(bf16[8,224,576]{2,1,0:T(8,128)(2,1)} %gather_fusion.2, bf16[8,224,576]{2,1,0:T(8,128)(2,1)S(1)} %gather_fusion.1), kind=kLoop, calls=%fused_computation.13 | loop fusion | flops 8257536 | bytes 8257536 | tf_op jit(solution)/shard_map/concatenate | solution.py:57
  74.1 4.5 %fusion = f32[4,128]{1,0:T(4,128)S(1)} fusion(bf16[2,128,1792]{2,1,0:T(8,128)(2,1)} %collective-permute-done.3, bf16[2,128,1792]{2,1,0:T(8,128)(2,1)} %collective-permute-done.2, bf16[2,128,1792]{2,1,0:T(8,128)(2,1)} %collective-permute-done, bf16[2,128,1792]{2,1,0:T(8,128)(2,1)S(1)} %copy-done.2), kind=kLoop, calls=%fused_computation.10 | loop fusion | flops 18349568 | bytes 3672064 | tf_op jit(solution)/shard_map/reduce_sum | solution.py:138
  78.6 2.4 %fusion.2 = bf16[4,128,3584]{2,1,0:T(8,128)(2,1)S(1)} fusion(f32[3584]{0:T(1024)S(1)} %maximum_select_fusion, f32[4,128]{1,0:T(4,128)S(1)} %add_rsqrt_fusion, bf16[2,128,1792]{2,1,0:T(8,128)(2,1)} %collective-permute-done.3, bf16[2,128,1792]{2,1,0:T(8,128)(2,1)} %collective-permute-done.2, bf16[2,128,1792]{2,1,0:T(8,128)(2,1)} %collective-permute-done, ...), kind=kLoop, calls=%fused_computation.12 | loop fusion | flops 20185088 | bytes 7356416 | tf_op jit(solution)/shard_map/convert_element_type | solution.py:141
  81.0 2.4 %convolution_add_fusion = f32[512,576]{0,1:T(8,128)S(1)} fusion(bf16[512,3584]{1,0:T(8,128)(2,1)S(1)} %bitcast.150, bf16[3584,576]{1,0:T(8,128)(2,1)S(1)} %bitcast.145, f32[576]{0:T(1024)S(1)} %maximum_select_fusion.1), kind=kOutput, calls=%fused_computation.29 | convolution fusion | flops 2114224128 | bytes 8980736 | tf_op jit(solution)/shard_map/dot_general | solution.py:146
  87.2 5.6 %collective-permute-done.17 = bf16[2,128,576]{1,0,2:T(2,128)(2,1)S(1)} collective-permute-done((bf16[2,128,576]{1,0,2:T(2,128)(2,1)S(1)}, bf16[2,128,576]{1,0,2:T(2,128)(2,1)S(1)}, u32[]{:S(2)}, u32[]{:S(2)}) %collective-permute-start.17) | collective-permute-done | bytes 294944 | tf_op jit(solution)/shard_map/ppermute | solution.py:157
  94.0 1.9 %collective-permute-start.18 = (bf16[2,128,256]{1,0,2:T(2,128)(2,1)S(1)}, bf16[2,128,256]{1,0,2:T(2,128)(2,1)S(1)}, u32[]{:S(2)}, u32[]{:S(2)}) collective-permute-start(bf16[2,128,256]{1,0,2:T(2,128)(2,1)S(1)} %pad_maximum_fusion.6), channel_id=1, source_target_pairs={{0,2},{2,4},{4,6},{6,8},{8,10},{10,12},{12,14},{14,0},{1,3},{3,5},... | collective-permute-start | bytes 393224 | tf_op jit(solution)/shard_map/ppermute | solution.py:168
  95.9 1.6 %collective-permute-start.19 = (bf16[2,128,256]{1,0,2:T(2,128)(2,1)S(1)}, bf16[2,128,256]{1,0,2:T(2,128)(2,1)S(1)}, u32[]{:S(2)}, u32[]{:S(2)}) collective-permute-start(bf16[2,128,256]{1,0,2:T(2,128)(2,1)S(1)} %pad_maximum_fusion.6), channel_id=1, source_target_pairs={{0,4},{2,6},{4,8},{6,10},{8,12},{10,14},{12,0},{14,2},{1,5},{3,7},... | collective-permute-start | bytes 393224 | tf_op jit(solution)/shard_map/ppermute | solution.py:168
  97.5 2.3 %collective-permute-start.20 = (bf16[2,128,256]{1,0,2:T(2,128)(2,1)S(1)}, bf16[2,128,256]{1,0,2:T(2,128)(2,1)S(1)}, u32[]{:S(2)}, u32[]{:S(2)}) collective-permute-start(bf16[2,128,256]{1,0,2:T(2,128)(2,1)S(1)} %pad_maximum_fusion.6), channel_id=1, source_target_pairs={{0,6},{2,8},{4,10},{6,12},{8,14},{10,0},{12,2},{14,4},{1,7},{3,9},... | collective-permute-start | bytes 393224 | tf_op jit(solution)/shard_map/ppermute | solution.py:168
  101.0 2.9 %collective-permute-start.22 = (bf16[2,128,256]{1,0,2:T(2,128)(2,1)S(1)}, bf16[2,128,256]{1,0,2:T(2,128)(2,1)S(1)}, u32[]{:S(2)}, u32[]{:S(2)}) collective-permute-start(bf16[2,128,256]{1,0,2:T(2,128)(2,1)S(1)} %pad_maximum_fusion.6), channel_id=1, source_target_pairs={{0,10},{2,12},{4,14},{6,0},{8,2},{10,4},{12,6},{14,8},{1,11},{3,13... | collective-permute-start | bytes 393224 | tf_op jit(solution)/shard_map/ppermute | solution.py:168
  105.0 1.8 %copy.51 = bf16[2,2,64,7,128]{4,2,3,1,0:T(8,128)(2,1)S(1)} copy(bf16[2,2,64,7,128]{2,1,0,4,3:T(2,128)(2,1)S(1)} %reshape.535) | data formatting | bytes 917504 | tf_op jit(solution)/shard_map/reshape | solution.py:205
  106.9 1.4 %collective-permute-start.23 = (bf16[2,128,256]{1,0,2:T(2,128)(2,1)S(1)}, bf16[2,128,256]{1,0,2:T(2,128)(2,1)S(1)}, u32[]{:S(2)}, u32[]{:S(2)}) collective-permute-start(bf16[2,128,256]{1,0,2:T(2,128)(2,1)S(1)} %pad_maximum_fusion.6), channel_id=1, source_target_pairs={{0,12},{2,14},{4,0},{6,2},{8,4},{10,6},{12,8},{14,10},{1,13},{3,15... | collective-permute-start | bytes 393224 | tf_op jit(solution)/shard_map/ppermute | solution.py:168
  108.4 1.4 %collective-permute-start.24 = (bf16[2,128,256]{1,0,2:T(2,128)(2,1)S(1)}, bf16[2,128,256]{1,0,2:T(2,128)(2,1)S(1)}, u32[]{:S(2)}, u32[]{:S(2)}) collective-permute-start(bf16[2,128,256]{1,0,2:T(2,128)(2,1)S(1)} %pad_maximum_fusion.6), channel_id=1, source_target_pairs={{0,14},{2,0},{4,2},{6,4},{8,6},{10,8},{12,10},{14,12},{1,15},{3,1}... | collective-permute-start | bytes 393224 | tf_op jit(solution)/shard_map/ppermute | solution.py:168
  111.4 1.9 %collective-permute-done.23 = bf16[2,128,256]{1,0,2:T(2,128)(2,1)S(1)} collective-permute-done((bf16[2,128,256]{1,0,2:T(2,128)(2,1)S(1)}, bf16[2,128,256]{1,0,2:T(2,128)(2,1)S(1)}, u32[]{:S(2)}, u32[]{:S(2)}) %collective-permute-start.23) | collective-permute-done | bytes 131104 | tf_op jit(solution)/shard_map/ppermute | solution.py:168
  114.5 1.4 %gather_fusion.5 = bf16[12,64,256]{2,1,0:T(8,128)(2,1)} fusion(bf16[2,16,64,256]{3,2,0,1:T(8,128)(2,1)S(1)} %bitcast.142, s32[12]{0:T(128)S(1)} %reshape.505), kind=kCustom, calls=%fused_computation.5 | custom fusion | bytes 786528 | tf_op jit(solution)/shard_map/gather | solution.py:191
  (170 shorter events, 40.8 us)
Async XLA Ops:
  0.0 11.5 %copy-start = (s32[2,2,2]{2,1,0:T(2,128)S(1)}, s32[2,2,2]{2,1,0:T(2,128)}, u32[]{:S(2)}) copy-start(s32[2,2,2]{2,1,0:T(2,128)} %param.20) | copy-start | bytes 100
  2.4 7.0 %copy-start.1 = (s32[8]{0:T(128)S(1)}, s32[8]{0:T(128)}, u32[]{:S(2)}) copy-start(s32[8]{0:T(128)} %constant.154.clone) | copy-start | bytes 100
  2.4 8.9 %copy-start.8 = (f32[3584]{0:T(1024)S(1)}, f32[3584]{0:T(1024)}, u32[]{:S(2)}) copy-start(f32[3584]{0:T(1024)} %param.12) | copy-start | bytes 43012
  2.4 9.0 %copy-start.11 = (f32[128]{0:T(128)S(1)}, f32[128]{0:T(128)}, u32[]{:S(2)}) copy-start(f32[128]{0:T(128)} %param.18) | copy-start | bytes 1540
  2.4 10.5 %copy-start.9 = (f32[896]{0:T(1024)S(1)}, f32[896]{0:T(1024)}, u32[]{:S(2)}) copy-start(f32[896]{0:T(1024)} %param.14) | copy-start | bytes 10756
  2.5 10.5 %copy-start.12 = (f32[128]{0:T(128)S(1)}, f32[128]{0:T(128)}, u32[]{:S(2)}) copy-start(f32[128]{0:T(128)} %param.16) | copy-start | bytes 1540
  2.5 10.5 %slice-start = ((f32[896]{0:T(1024)}), f32[512]{0:T(512)S(1)}, s32[]{:S(2)}) async-start(f32[896]{0:T(1024)} %param.14), calls=%async_computation | async-start | bytes 4096 | tf_op jit(solution)/shard_map/slice | solution.py:116
  3.4 11.2 %collective-permute-start.1 = (bf16[224,576]{1,0:T(8,128)(2,1)}, bf16[224,576]{1,0:T(8,128)(2,1)}, u32[]{:S(2)}, u32[]{:S(2)}) collective-permute-start(bf16[224,576]{1,0:T(8,128)(2,1)} %pad_maximum_fusion.4), channel_id=1, source_target_pairs={{0,4},{4,8},{8,12},{12,14},{14,10},{10,6},{6,2},{2,0},{1,5},{5,9},... | collective-permute-start | bytes 774152 | tf_op jit(solution)/shard_map/ppermute | solution.py:48
  7.3 12.6 %collective-permute-start.10 = (bf16[224,576]{1,0:T(8,128)(2,1)}, bf16[224,576]{1,0:T(8,128)(2,1)}, u32[]{:S(2)}, u32[]{:S(2)}) collective-permute-start(bf16[224,576]{1,0:T(8,128)(2,1)} %pad_maximum_fusion.5), channel_id=1, source_target_pairs={{0,2},{4,0},{8,4},{12,8},{14,12},{10,14},{6,10},{2,6},{1,3},{5,1},... | collective-permute-start | bytes 774152 | tf_op jit(solution)/shard_map/ppermute | solution.py:49
  7.3 66.9 %collective-permute-start = (bf16[2,128,1792]{2,1,0:T(8,128)(2,1)S(1)}, bf16[2,128,1792]{2,1,0:T(8,128)(2,1)}, u32[]{:S(2)}, u32[]{:S(2)}) collective-permute-start(bf16[2,128,1792]{2,1,0:T(8,128)(2,1)S(1)} %copy-done.2), channel_id=1, source_target_pairs={{0,1},{1,0},{2,3},{3,2},{4,5},{5,4},{6,7},{7,6},{8,9},{9,8},{10,11... | collective-permute-start | bytes 2752520 | tf_op jit(solution)/shard_map/ppermute | solution.py:120
  14.6 29.7 %collective-permute-start.2 = (bf16[2,128,1792]{2,1,0:T(8,128)(2,1)S(1)}, bf16[2,128,1792]{2,1,0:T(8,128)(2,1)}, u32[]{:S(2)}, u32[]{:S(2)}) collective-permute-start(bf16[2,128,1792]{2,1,0:T(8,128)(2,1)S(1)} %copy-done.2), channel_id=1, source_target_pairs={{0,16},{16,0},{1,17},{17,1},{2,18},{18,2},{3,19},{19,3},{4,20},{20... | collective-permute-start | bytes 2752520 | tf_op jit(solution)/shard_map/ppermute | solution.py:122
  16.5 9.2 %collective-permute-start.4 = (bf16[224,576]{1,0:T(8,128)(2,1)}, bf16[224,576]{1,0:T(8,128)(2,1)S(1)}, u32[]{:S(2)}, u32[]{:S(2)}) collective-permute-start(bf16[224,576]{1,0:T(8,128)(2,1)} %collective-permute-done.1), channel_id=1, source_target_pairs={{0,4},{4,8},{8,12},{12,14},{14,10},{10,6},{6,2},{2,0},{1,5},{5,9},... | collective-permute-start | bytes 774152 | tf_op jit(solution)/shard_map/ppermute | solution.py:48
  19.9 8.9 %collective-permute-start.11 = (bf16[224,576]{1,0:T(8,128)(2,1)}, bf16[224,576]{1,0:T(8,128)(2,1)S(1)}, u32[]{:S(2)}, u32[]{:S(2)}) collective-permute-start(bf16[224,576]{1,0:T(8,128)(2,1)} %collective-permute-done.10), channel_id=1, source_target_pairs={{0,2},{4,0},{8,4},{12,8},{14,12},{10,14},{6,10},{2,6},{1,3},{5,1},... | collective-permute-start | bytes 774152 | tf_op jit(solution)/shard_map/ppermute | solution.py:49
  25.7 8.3 %collective-permute-start.5 = (bf16[224,576]{1,0:T(8,128)(2,1)S(1)}, bf16[224,576]{1,0:T(8,128)(2,1)S(1)}, u32[]{:S(2)}, u32[]{:S(2)}) collective-permute-start(bf16[224,576]{1,0:T(8,128)(2,1)S(1)} %collective-permute-done.4), channel_id=1, source_target_pairs={{0,4},{4,8},{8,12},{12,14},{14,10},{10,6},{6,2},{2,0},{1,5},{5,9},... | collective-permute-start | bytes 774152 | tf_op jit(solution)/shard_map/ppermute | solution.py:48
  28.7 7.9 %collective-permute-start.12 = (bf16[224,576]{1,0:T(8,128)(2,1)S(1)}, bf16[224,576]{1,0:T(8,128)(2,1)S(1)}, u32[]{:S(2)}, u32[]{:S(2)}) collective-permute-start(bf16[224,576]{1,0:T(8,128)(2,1)S(1)} %collective-permute-done.11), channel_id=1, source_target_pairs={{0,2},{4,0},{8,4},{12,8},{14,12},{10,14},{6,10},{2,6},{1,3},{5,1},... | collective-permute-start | bytes 774152 | tf_op jit(solution)/shard_map/ppermute | solution.py:49
  34.0 7.4 %collective-permute-start.6 = (bf16[224,576]{1,0:T(8,128)(2,1)S(1)}, bf16[224,576]{1,0:T(8,128)(2,1)S(1)}, u32[]{:S(2)}, u32[]{:S(2)}) collective-permute-start(bf16[224,576]{1,0:T(8,128)(2,1)S(1)} %collective-permute-done.5), channel_id=1, source_target_pairs={{0,4},{4,8},{8,12},{12,14},{14,10},{10,6},{6,2},{2,0},{1,5},{5,9},... | collective-permute-start | bytes 774152 | tf_op jit(solution)/shard_map/ppermute | solution.py:48
  36.7 7.1 %collective-permute-start.13 = (bf16[224,576]{1,0:T(8,128)(2,1)S(1)}, bf16[224,576]{1,0:T(8,128)(2,1)S(1)}, u32[]{:S(2)}, u32[]{:S(2)}) collective-permute-start(bf16[224,576]{1,0:T(8,128)(2,1)S(1)} %collective-permute-done.12), channel_id=1, source_target_pairs={{0,2},{4,0},{8,4},{12,8},{14,12},{10,14},{6,10},{2,6},{1,3},{5,1},... | collective-permute-start | bytes 774152 | tf_op jit(solution)/shard_map/ppermute | solution.py:49
  41.4 7.1 %collective-permute-start.7 = (bf16[224,576]{1,0:T(8,128)(2,1)S(1)}, bf16[224,576]{1,0:T(8,128)(2,1)S(1)}, u32[]{:S(2)}, u32[]{:S(2)}) collective-permute-start(bf16[224,576]{1,0:T(8,128)(2,1)S(1)} %collective-permute-done.6), channel_id=1, source_target_pairs={{0,4},{4,8},{8,12},{12,14},{14,10},{10,6},{6,2},{2,0},{1,5},{5,9},... | collective-permute-start | bytes 774152 | tf_op jit(solution)/shard_map/ppermute | solution.py:48
  43.8 7.4 %collective-permute-start.14 = (bf16[224,576]{1,0:T(8,128)(2,1)S(1)}, bf16[224,576]{1,0:T(8,128)(2,1)S(1)}, u32[]{:S(2)}, u32[]{:S(2)}) collective-permute-start(bf16[224,576]{1,0:T(8,128)(2,1)S(1)} %collective-permute-done.13), channel_id=1, source_target_pairs={{0,2},{4,0},{8,4},{12,8},{14,12},{10,14},{6,10},{2,6},{1,3},{5,1},... | collective-permute-start | bytes 774152 | tf_op jit(solution)/shard_map/ppermute | solution.py:49
  44.3 29.8 %collective-permute-start.3 = (bf16[2,128,1792]{2,1,0:T(8,128)(2,1)}, bf16[2,128,1792]{2,1,0:T(8,128)(2,1)}, u32[]{:S(2)}, u32[]{:S(2)}) collective-permute-start(bf16[2,128,1792]{2,1,0:T(8,128)(2,1)} %collective-permute-done.2), channel_id=1, source_target_pairs={{0,1},{1,0},{2,3},{3,2},{4,5},{5,4},{6,7},{7,6},{8,9},{9,8},{10,11... | collective-permute-start | bytes 2752520 | tf_op jit(solution)/shard_map/ppermute | solution.py:123
  48.6 7.9 %collective-permute-start.8 = (bf16[224,576]{1,0:T(8,128)(2,1)S(1)}, bf16[224,576]{1,0:T(8,128)(2,1)S(1)}, u32[]{:S(2)}, u32[]{:S(2)}) collective-permute-start(bf16[224,576]{1,0:T(8,128)(2,1)S(1)} %collective-permute-done.7), channel_id=1, source_target_pairs={{0,4},{4,8},{8,12},{12,14},{14,10},{10,6},{6,2},{2,0},{1,5},{5,9},... | collective-permute-start | bytes 774152 | tf_op jit(solution)/shard_map/ppermute | solution.py:48
  51.2 8.2 %collective-permute-start.15 = (bf16[224,576]{1,0:T(8,128)(2,1)S(1)}, bf16[224,576]{1,0:T(8,128)(2,1)S(1)}, u32[]{:S(2)}, u32[]{:S(2)}) collective-permute-start(bf16[224,576]{1,0:T(8,128)(2,1)S(1)} %collective-permute-done.14), channel_id=1, source_target_pairs={{0,2},{4,0},{8,4},{12,8},{14,12},{10,14},{6,10},{2,6},{1,3},{5,1},... | collective-permute-start | bytes 774152 | tf_op jit(solution)/shard_map/ppermute | solution.py:49
  56.5 6.6 %collective-permute-start.9 = (bf16[224,576]{1,0:T(8,128)(2,1)S(1)}, bf16[224,576]{1,0:T(8,128)(2,1)S(1)}, u32[]{:S(2)}, u32[]{:S(2)}) collective-permute-start(bf16[224,576]{1,0:T(8,128)(2,1)S(1)} %collective-permute-done.8), channel_id=1, source_target_pairs={{0,4},{4,8},{8,12},{12,14},{14,10},{10,6},{6,2},{2,0},{1,5},{5,9},... | collective-permute-start | bytes 774152 | tf_op jit(solution)/shard_map/ppermute | solution.py:48
  59.3 7.2 %collective-permute-start.16 = (bf16[224,576]{1,0:T(8,128)(2,1)S(1)}, bf16[224,576]{1,0:T(8,128)(2,1)}, u32[]{:S(2)}, u32[]{:S(2)}) collective-permute-start(bf16[224,576]{1,0:T(8,128)(2,1)S(1)} %collective-permute-done.15), channel_id=1, source_target_pairs={{0,2},{4,0},{8,4},{12,8},{14,12},{10,14},{6,10},{2,6},{1,3},{5,1},... | collective-permute-start | bytes 774152 | tf_op jit(solution)/shard_map/ppermute | solution.py:49
  86.0 6.8 %collective-permute-start.17 = (bf16[2,128,576]{1,0,2:T(2,128)(2,1)S(1)}, bf16[2,128,576]{1,0,2:T(2,128)(2,1)S(1)}, u32[]{:S(2)}, u32[]{:S(2)}) collective-permute-start(bf16[2,128,576]{1,0,2:T(2,128)(2,1)S(1)} %fusion.23), channel_id=1, source_target_pairs={{0,16},{16,0},{1,17},{17,1},{2,18},{18,2},{3,19},{19,3},{4,20},{20... | collective-permute-start | bytes 884744 | tf_op jit(solution)/shard_map/ppermute | solution.py:157
  94.0 12.8 %collective-permute-start.18 = (bf16[2,128,256]{1,0,2:T(2,128)(2,1)S(1)}, bf16[2,128,256]{1,0,2:T(2,128)(2,1)S(1)}, u32[]{:S(2)}, u32[]{:S(2)}) collective-permute-start(bf16[2,128,256]{1,0,2:T(2,128)(2,1)S(1)} %pad_maximum_fusion.6), channel_id=1, source_target_pairs={{0,2},{2,4},{4,6},{6,8},{8,10},{10,12},{12,14},{14,0},{1,3},{3,5},... | collective-permute-start | bytes 393224 | tf_op jit(solution)/shard_map/ppermute | solution.py:168
  95.9 12.5 %collective-permute-start.19 = (bf16[2,128,256]{1,0,2:T(2,128)(2,1)S(1)}, bf16[2,128,256]{1,0,2:T(2,128)(2,1)S(1)}, u32[]{:S(2)}, u32[]{:S(2)}) collective-permute-start(bf16[2,128,256]{1,0,2:T(2,128)(2,1)S(1)} %pad_maximum_fusion.6), channel_id=1, source_target_pairs={{0,4},{2,6},{4,8},{6,10},{8,12},{10,14},{12,0},{14,2},{1,5},{3,7},... | collective-permute-start | bytes 393224 | tf_op jit(solution)/shard_map/ppermute | solution.py:168
  97.5 12.5 %collective-permute-start.20 = (bf16[2,128,256]{1,0,2:T(2,128)(2,1)S(1)}, bf16[2,128,256]{1,0,2:T(2,128)(2,1)S(1)}, u32[]{:S(2)}, u32[]{:S(2)}) collective-permute-start(bf16[2,128,256]{1,0,2:T(2,128)(2,1)S(1)} %pad_maximum_fusion.6), channel_id=1, source_target_pairs={{0,6},{2,8},{4,10},{6,12},{8,14},{10,0},{12,2},{14,4},{1,7},{3,9},... | collective-permute-start | bytes 393224 | tf_op jit(solution)/shard_map/ppermute | solution.py:168
  99.8 11.3 %collective-permute-start.21 = (bf16[2,128,256]{1,0,2:T(2,128)(2,1)S(1)}, bf16[2,128,256]{1,0,2:T(2,128)(2,1)S(1)}, u32[]{:S(2)}, u32[]{:S(2)}) collective-permute-start(bf16[2,128,256]{1,0,2:T(2,128)(2,1)S(1)} %pad_maximum_fusion.6), channel_id=1, source_target_pairs={{0,8},{2,10},{4,12},{6,14},{8,0},{10,2},{12,4},{14,6},{1,9},{3,11}... | collective-permute-start | bytes 393224 | tf_op jit(solution)/shard_map/ppermute | solution.py:168
  101.0 10.3 %collective-permute-start.22 = (bf16[2,128,256]{1,0,2:T(2,128)(2,1)S(1)}, bf16[2,128,256]{1,0,2:T(2,128)(2,1)S(1)}, u32[]{:S(2)}, u32[]{:S(2)}) collective-permute-start(bf16[2,128,256]{1,0,2:T(2,128)(2,1)S(1)} %pad_maximum_fusion.6), channel_id=1, source_target_pairs={{0,10},{2,12},{4,14},{6,0},{8,2},{10,4},{12,6},{14,8},{1,11},{3,13... | collective-permute-start | bytes 393224 | tf_op jit(solution)/shard_map/ppermute | solution.py:168
  106.9 6.4 %collective-permute-start.23 = (bf16[2,128,256]{1,0,2:T(2,128)(2,1)S(1)}, bf16[2,128,256]{1,0,2:T(2,128)(2,1)S(1)}, u32[]{:S(2)}, u32[]{:S(2)}) collective-permute-start(bf16[2,128,256]{1,0,2:T(2,128)(2,1)S(1)} %pad_maximum_fusion.6), channel_id=1, source_target_pairs={{0,12},{2,14},{4,0},{6,2},{8,4},{10,6},{12,8},{14,10},{1,13},{3,15... | collective-permute-start | bytes 393224 | tf_op jit(solution)/shard_map/ppermute | solution.py:168
  108.4 5.2 %collective-permute-start.24 = (bf16[2,128,256]{1,0,2:T(2,128)(2,1)S(1)}, bf16[2,128,256]{1,0,2:T(2,128)(2,1)S(1)}, u32[]{:S(2)}, u32[]{:S(2)}) collective-permute-start(bf16[2,128,256]{1,0,2:T(2,128)(2,1)S(1)} %pad_maximum_fusion.6), channel_id=1, source_target_pairs={{0,14},{2,0},{4,2},{6,4},{8,6},{10,8},{12,10},{14,12},{1,15},{3,1}... | collective-permute-start | bytes 393224 | tf_op jit(solution)/shard_map/ppermute | solution.py:168
  (7 other events, 16.8 us)

commit v16 on v14

--- a/solution.py
+++ b/solution.py
@@ -50,11 +50,21 @@
         behind_parts.append(behind)
     table = jnp.array(position, dtype=jnp.int32)
     mine = table[here]
-    ahead_pick = (mine - table) % count
-    behind_pick = (table - mine) % count
-    joined = jnp.concatenate(
-        [jnp.stack(ahead_parts)[ahead_pick], jnp.stack(behind_parts)[behind_pick]], axis=1
-    )
+    ahead_stack, behind_stack = jnp.stack(ahead_parts), jnp.stack(behind_parts)
+
+    def placed(at):
+        def build(ahead_stack, behind_stack):
+            return jnp.concatenate(
+                [
+                    jnp.stack([ahead_stack[(at - position[d]) % count] for d in range(count)]),
+                    jnp.stack([behind_stack[(position[d] - at) % count] for d in range(count)]),
+                ],
+                axis=1,
+            )
+
+        return build
+
+    joined = lax.switch(mine, [placed(at) for at in range(count)], ahead_stack, behind_stack)
     return joined.reshape(count * 2 * half, ahead.shape[1]), ahead_parts[1]
 
 

time: 119 us -> 120 us (level); the launches traced: 117 us -> 119 us
  local copies, waits for them, and re-layouts: 32.2 us -> 25.2 us
  waiting for transfers between devices: 30.5 us -> 34 us
  other arithmetic: 16.5 us -> 19.1 us
  starting transfers between devices: 30.1 us -> 32 us
    gather x2 -> x0, local copies, waits for them, and re-layouts: 7.79 us -> none  [the longest x1 3.9 us: gather_rows(): jnp.stack(behind_parts)[behind_pick]]
    ppermute x7, waiting for transfers between devices: 20.8 us -> 24.8 us  [gather_rows(): ahead = lax.ppermute(ahead, 'row', forward)]
    unnamed x43 -> x45, local copies, waits for them, and re-layouts: 10.4 us -> 6.78 us
    ppermute x7, waiting for transfers between devices: 0.42 us -> 3.91 us  [gather_rows(): behind = lax.ppermute(behind, 'row', backward)]
    ppermute x7, waiting for transfers between devices: 2.83 us -> 0.02 us  [shards(): lax.ppermute(pairs, 'row', [(i, (i + k) % row_count) for i in range(row_c...]
    cond x0 -> x14, local copies, waits for them, and re-layouts: none -> 2.41 us
    select_n x1, other arithmetic: 1.96 us -> 3.77 us  [shards(): jnp.where(column == 0, jnp.concatenate([tokens, other_half], axis=2), jnp...]
    unnamed x2 -> x1, other arithmetic: 1.5 us -> 0.01 us
  transfers between devices with their start and end apart: 25 -> 25, of which waited for: 13 -> 10; matrix products, arithmetic and copies ran while one was open for 27% -> 20% of each run, Pallas kernels for 0% -> 0%
where the time goes in v16:
time: 120 us; the launch traced here: 119 us
  waiting for transfers between devices  34 us (28%)
  starting transfers between devices  32 us (27%)
  local copies, waits for them, and re-layouts  25.2 us (21%)
  other arithmetic  19.1 us (16%)
  matrix products  7.68 us (6%)
  between operations  1.34 us (1%)
    ppermute x7, waiting for transfers between devices, gather_rows(): ahead = lax.ppermute(ahead, 'row', forward)  24.8 us
    ppermute x7, starting transfers between devices, gather_rows(): ahead = lax.ppermute(ahead, 'row', forward)  12.4 us
    ppermute x7, starting transfers between devices, shards(): lax.ppermute(pairs, 'row', [(i, (i + k) % row_count) for i in range(row_c...  12.4 us
    unnamed x45, local copies, waits for them, and re-layouts  6.78 us
    ppermute x1, waiting for transfers between devices, shards(): returned = lax.ppermute(result[passages:], 'groups', SWAP)  5.18 us
    ppermute x7, waiting for transfers between devices, gather_rows(): behind = lax.ppermute(behind, 'row', backward)  3.91 us
    ppermute x7, starting transfers between devices, gather_rows(): behind = lax.ppermute(behind, 'row', backward)  3.79 us
    select_n x1, other arithmetic, shards(): jnp.where(column == 0, jnp.concatenate([tokens, other_half], axis=2), jnp...  3.77 us
  transfers between devices with their start and end apart: 25, of which 10 were waited for; matrix products, arithmetic and copies ran while one was open for 20% of the time, Pallas kernels for 0%

profile of v16, /device:TPU:0, one launch (start us, length us, event | category | flops | bytes accessed | tf_op | source)
XLA Modules:
  0.0 119.4 jit_solution(11383660980982520594)
XLA Ops:
  2.6 3.1 %collective-permute-start.1 = (bf16[224,576]{1,0:T(8,128)(2,1)S(1)}, bf16[224,576]{1,0:T(8,128)(2,1)S(1)}, u32[]{:S(2)}, u32[]{:S(2)}) collective-permute-start(bf16[224,576]{1,0:T(8,128)(2,1)S(1)} %get-tuple-element.428), channel_id=1, source_target_pairs={{0,4},{4,8},{8,12},{12,14},{14,10},{10,6},{6,2},{2,0},{1,5},{5,9},... | collective-permute-start | bytes 774152 | tf_op jit(solution)/shard_map/ppermute | solution.py:47
  6.1 6.3 %collective-permute-done.1 = bf16[224,576]{1,0:T(8,128)(2,1)S(1)} collective-permute-done((bf16[224,576]{1,0:T(8,128)(2,1)S(1)}, bf16[224,576]{1,0:T(8,128)(2,1)S(1)}, u32[]{:S(2)}, u32[]{:S(2)}) %collective-permute-start.1) | collective-permute-done | bytes 258080 | tf_op jit(solution)/shard_map/ppermute | solution.py:47
  12.5 1.8 %collective-permute-start.4 = (bf16[224,576]{1,0:T(8,128)(2,1)S(1)}, bf16[224,576]{1,0:T(8,128)(2,1)S(1)}, u32[]{:S(2)}, u32[]{:S(2)}) collective-permute-start(bf16[224,576]{1,0:T(8,128)(2,1)S(1)} %collective-permute-done.1), channel_id=1, source_target_pairs={{0,4},{4,8},{8,12},{12,14},{14,10},{10,6},{6,2},{2,0},{1,5},{5,9},... | collective-permute-start | bytes 774152 | tf_op jit(solution)/shard_map/ppermute | solution.py:47
  14.6 1.8 %collective-permute-start.2 = (bf16[2,128,1792]{2,1,0:T(8,128)(2,1)}, bf16[2,128,1792]{2,1,0:T(8,128)(2,1)}, u32[]{:S(2)}, u32[]{:S(2)}) collective-permute-start(bf16[2,128,1792]{2,1,0:T(8,128)(2,1)} %param.19), channel_id=1, source_target_pairs={{0,16},{16,0},{1,17},{17,1},{2,18},{18,2},{3,19},{19,3},{4,20},{20... | collective-permute-start | bytes 2752520 | tf_op jit(solution)/shard_map/ppermute | solution.py:129
  16.4 4.0 %collective-permute-done.4 = bf16[224,576]{1,0:T(8,128)(2,1)S(1)} collective-permute-done((bf16[224,576]{1,0:T(8,128)(2,1)S(1)}, bf16[224,576]{1,0:T(8,128)(2,1)S(1)}, u32[]{:S(2)}, u32[]{:S(2)}) %collective-permute-start.4) | collective-permute-done | bytes 258080 | tf_op jit(solution)/shard_map/ppermute | solution.py:47
  20.5 1.5 %collective-permute-start.5 = (bf16[224,576]{1,0:T(8,128)(2,1)S(1)}, bf16[224,576]{1,0:T(8,128)(2,1)S(1)}, u32[]{:S(2)}, u32[]{:S(2)}) collective-permute-start(bf16[224,576]{1,0:T(8,128)(2,1)S(1)} %collective-permute-done.4), channel_id=1, source_target_pairs={{0,4},{4,8},{8,12},{12,14},{14,10},{10,6},{6,2},{2,0},{1,5},{5,9},... | collective-permute-start | bytes 774152 | tf_op jit(solution)/shard_map/ppermute | solution.py:47
  22.6 5.0 %collective-permute-done.5 = bf16[224,576]{1,0:T(8,128)(2,1)S(1)} collective-permute-done((bf16[224,576]{1,0:T(8,128)(2,1)S(1)}, bf16[224,576]{1,0:T(8,128)(2,1)S(1)}, u32[]{:S(2)}, u32[]{:S(2)}) %collective-permute-start.5) | collective-permute-done | bytes 258080 | tf_op jit(solution)/shard_map/ppermute | solution.py:47
  30.5 4.2 %collective-permute-done.6 = bf16[224,576]{1,0:T(8,128)(2,1)S(1)} collective-permute-done((bf16[224,576]{1,0:T(8,128)(2,1)S(1)}, bf16[224,576]{1,0:T(8,128)(2,1)S(1)}, u32[]{:S(2)}, u32[]{:S(2)}) %collective-permute-start.6) | collective-permute-done | bytes 258080 | tf_op jit(solution)/shard_map/ppermute | solution.py:47
  34.7 1.5 %collective-permute-start.7 = (bf16[224,576]{1,0:T(8,128)(2,1)S(1)}, bf16[224,576]{1,0:T(8,128)(2,1)S(1)}, u32[]{:S(2)}, u32[]{:S(2)}) collective-permute-start(bf16[224,576]{1,0:T(8,128)(2,1)S(1)} %collective-permute-done.6), channel_id=1, source_target_pairs={{0,4},{4,8},{8,12},{12,14},{14,10},{10,6},{6,2},{2,0},{1,5},{5,9},... | collective-permute-start | bytes 774152 | tf_op jit(solution)/shard_map/ppermute | solution.py:47
  37.2 5.2 %collective-permute-done.7 = bf16[224,576]{1,0:T(8,128)(2,1)S(1)} collective-permute-done((bf16[224,576]{1,0:T(8,128)(2,1)S(1)}, bf16[224,576]{1,0:T(8,128)(2,1)S(1)}, u32[]{:S(2)}, u32[]{:S(2)}) %collective-permute-start.7) | collective-permute-done | bytes 258080 | tf_op jit(solution)/shard_map/ppermute | solution.py:47
  42.4 1.7 %collective-permute-start.8 = (bf16[224,576]{1,0:T(8,128)(2,1)S(1)}, bf16[224,576]{1,0:T(8,128)(2,1)}, u32[]{:S(2)}, u32[]{:S(2)}) collective-permute-start(bf16[224,576]{1,0:T(8,128)(2,1)S(1)} %collective-permute-done.7), channel_id=1, source_target_pairs={{0,4},{4,8},{8,12},{12,14},{14,10},{10,6},{6,2},{2,0},{1,5},{5,9},... | collective-permute-start | bytes 774152 | tf_op jit(solution)/shard_map/ppermute | solution.py:47
  49.4 1.5 %pad_maximum_fusion.14 = (f32[128,128]{0,1:T(8,128)}, f32[128,128]{0,1:T(8,128)S(1)}) fusion(f32[128,64]{0,1:T(8,128)S(1)} %get-tuple-element.431, f32[128,64]{0,1:T(8,128)} %get-tuple-element.432), kind=kLoop, calls=%fused_computation.201 | loop fusion | flops 32768 | bytes 196608 | tf_op jit(solution)/shard_map/concatenate | solution.py:24
  50.8 1.5 %collective-permute-start.9 = (bf16[224,576]{1,0:T(8,128)(2,1)}, bf16[224,576]{1,0:T(8,128)(2,1)S(1)}, u32[]{:S(2)}, u32[]{:S(2)}) collective-permute-start(bf16[224,576]{1,0:T(8,128)(2,1)} %collective-permute-done.8), channel_id=1, source_target_pairs={{0,4},{4,8},{8,12},{12,14},{14,10},{10,6},{6,2},{2,0},{1,5},{5,9},... | collective-permute-start | bytes 774152 | tf_op jit(solution)/shard_map/ppermute | solution.py:47
  54.4 3.8 %maximum_select_fusion = bf16[2,128,3584]{2,1,0:T(8,128)(2,1)} fusion(bf16[2,128,1792]{2,1,0:T(8,128)(2,1)} %collective-permute-done, bf16[2,128,1792]{2,1,0:T(8,128)(2,1)} %param.19, pred[]{:T(512)S(6)} %eq.12), kind=kLoop, calls=%fused_computation.146 | loop fusion | flops 8257536 | bytes 3670017 | tf_op jit(solution)/shard_map/jit(_where)/select_n | solution.py:131
  58.2 2.1 %collective-permute-done.16 = bf16[224,576]{1,0:T(8,128)(2,1)S(1)} collective-permute-done((bf16[224,576]{1,0:T(8,128)(2,1)}, bf16[224,576]{1,0:T(8,128)(2,1)S(1)}, u32[]{:S(2)}, u32[]{:S(2)}) %collective-permute-start.16) | collective-permute-done | bytes 258080 | tf_op jit(solution)/shard_map/ppermute | solution.py:48
  60.3 5.2 %conditional.1 = (bf16[3584,576]{1,0:T(8,128)(2,1)}) conditional(s32[]{:T(128)} %bitcast.10, (bf16[1,224,576]{2,1,0:T(8,128)(2,1)S(1)}, bf16[1,224,576]{2,1,0:T(8,128)(2,1)S(1)}, bf16[1,224,576]{2,1,0:T(8,128)(2,1)S(1)}, bf16[1,224,576]{2,1,0:T(8,128)(2,1)S(1)}, bf16[1,224,576]{2,1,0:T(8,128)(2,1)}, ...), branch_computations={%region_1.0_spmd, %region_2.0_spmd, %region_3.0_spmd, %region_4.0_... | conditional | flops 8257536 | bytes 17346568 | solution.py:67
  62.9 2.5 %pad_maximum_fusion = bf16[8,448,576]{2,1,0:T(8,128)(2,1)} fusion(bf16[8,224,576]{2,1,0:T(8,128)(2,1)S(1)} %get-tuple-element.404, bf16[8,224,576]{2,1,0:T(8,128)(2,1)S(1)} %get-tuple-element.403), kind=kLoop, calls=%fused_computation.5 | loop fusion | flops 8257536 | bytes 8257536 | tf_op jit(solution)/shard_map/cond/branch_0_fun/concatenate | solution.py:57
  65.5 2.6 %maximum_select_fusion.1 = bf16[2,128,3584]{2,1,0:T(8,128)(2,1)S(1)} fusion(bf16[2,128,1792]{2,1,0:T(8,128)(2,1)} %collective-permute-done.3, bf16[2,128,1792]{2,1,0:T(8,128)(2,1)} %collective-permute-done.2, pred[]{:T(512)S(6)} %eq.12), kind=kLoop, calls=%fused_computation.147 | loop fusion | flops 8257536 | bytes 3670017 | tf_op jit(solution)/shard_map/jit(_where)/select_n | solution.py:136
  71.0 2.4 %convolution_add_fusion = f32[512,576]{0,1:T(8,128)S(1)} fusion(bf16[512,3584]{1,0:T(8,128)(2,1)S(1)} %fusion.1, bf16[3584,576]{1,0:T(8,128)(2,1)S(1)} %bitcast.240, f32[576]{0:T(1024)S(1)} %copy-done.11), kind=kOutput, calls=%fused_computation.162 | convolution fusion | flops 2114224128 | bytes 8980736 | tf_op jit(solution)/shard_map/dot_general | solution.py:151
  75.9 1.6 %collective-permute-start.17 = (bf16[2,128,576]{1,0,2:T(2,128)(2,1)S(1)}, bf16[2,128,576]{1,0,2:T(2,128)(2,1)S(1)}, u32[]{:S(2)}, u32[]{:S(2)}) collective-permute-start(bf16[2,128,576]{1,0,2:T(2,128)(2,1)S(1)} %fusion.22), channel_id=1, source_target_pairs={{0,16},{16,0},{1,17},{17,1},{2,18},{18,2},{3,19},{19,3},{4,20},{20... | collective-permute-start | bytes 884744 | tf_op jit(solution)/shard_map/ppermute | solution.py:162
  77.5 5.2 %collective-permute-done.17 = bf16[2,128,576]{1,0,2:T(2,128)(2,1)S(1)} collective-permute-done((bf16[2,128,576]{1,0,2:T(2,128)(2,1)S(1)}, bf16[2,128,576]{1,0,2:T(2,128)(2,1)S(1)}, u32[]{:S(2)}, u32[]{:S(2)}) %collective-permute-start.17) | collective-permute-done | bytes 294944 | tf_op jit(solution)/shard_map/ppermute | solution.py:162
  84.9 1.3 %collective-permute-start.19 = (bf16[2,128,256]{1,0,2:T(2,128)(2,1)S(1)}, bf16[2,128,256]{1,0,2:T(2,128)(2,1)S(1)}, u32[]{:S(2)}, u32[]{:S(2)}) collective-permute-start(bf16[2,128,256]{1,0,2:T(2,128)(2,1)S(1)} %pad_maximum_fusion.13), channel_id=1, source_target_pairs={{0,4},{2,6},{4,8},{6,10},{8,12},{10,14},{12,0},{14,2},{1,5},{3,7},... | collective-permute-start | bytes 393224 | tf_op jit(solution)/shard_map/ppermute | solution.py:173
  86.2 3.3 %collective-permute-start.20 = (bf16[2,128,256]{1,0,2:T(2,128)(2,1)S(1)}, bf16[2,128,256]{1,0,2:T(2,128)(2,1)S(1)}, u32[]{:S(2)}, u32[]{:S(2)}) collective-permute-start(bf16[2,128,256]{1,0,2:T(2,128)(2,1)S(1)} %pad_maximum_fusion.13), channel_id=1, source_target_pairs={{0,6},{2,8},{4,10},{6,12},{8,14},{10,0},{12,2},{14,4},{1,7},{3,9},... | collective-permute-start | bytes 393224 | tf_op jit(solution)/shard_map/ppermute | solution.py:173
  89.5 1.3 %collective-permute-start.21 = (bf16[2,128,256]{1,0,2:T(2,128)(2,1)S(1)}, bf16[2,128,256]{1,0,2:T(2,128)(2,1)S(1)}, u32[]{:S(2)}, u32[]{:S(2)}) collective-permute-start(bf16[2,128,256]{1,0,2:T(2,128)(2,1)S(1)} %pad_maximum_fusion.13), channel_id=1, source_target_pairs={{0,8},{2,10},{4,12},{6,14},{8,0},{10,2},{12,4},{14,6},{1,9},{3,11}... | collective-permute-start | bytes 393224 | tf_op jit(solution)/shard_map/ppermute | solution.py:173
  90.8 1.8 %collective-permute-start.22 = (bf16[2,128,256]{1,0,2:T(2,128)(2,1)S(1)}, bf16[2,128,256]{1,0,2:T(2,128)(2,1)S(1)}, u32[]{:S(2)}, u32[]{:S(2)}) collective-permute-start(bf16[2,128,256]{1,0,2:T(2,128)(2,1)S(1)} %pad_maximum_fusion.13), channel_id=1, source_target_pairs={{0,10},{2,12},{4,14},{6,0},{8,2},{10,4},{12,6},{14,8},{1,11},{3,13... | collective-permute-start | bytes 393224 | tf_op jit(solution)/shard_map/ppermute | solution.py:173
  94.4 1.8 %copy.51 = bf16[2,2,64,7,128]{4,2,3,1,0:T(8,128)(2,1)S(1)} copy(bf16[2,2,64,7,128]{2,1,0,4,3:T(2,128)(2,1)S(1)} %reshape.359) | data formatting | bytes 917504 | tf_op jit(solution)/shard_map/reshape | solution.py:210
  96.3 1.4 %collective-permute-start.23 = (bf16[2,128,256]{1,0,2:T(2,128)(2,1)S(1)}, bf16[2,128,256]{1,0,2:T(2,128)(2,1)S(1)}, u32[]{:S(2)}, u32[]{:S(2)}) collective-permute-start(bf16[2,128,256]{1,0,2:T(2,128)(2,1)S(1)} %pad_maximum_fusion.13), channel_id=1, source_target_pairs={{0,12},{2,14},{4,0},{6,2},{8,4},{10,6},{12,8},{14,10},{1,13},{3,15... | collective-permute-start | bytes 393224 | tf_op jit(solution)/shard_map/ppermute | solution.py:173
  98.4 2.3 %collective-permute-start.24 = (bf16[2,128,256]{1,0,2:T(2,128)(2,1)S(1)}, bf16[2,128,256]{1,0,2:T(2,128)(2,1)S(1)}, u32[]{:S(2)}, u32[]{:S(2)}) collective-permute-start(bf16[2,128,256]{1,0,2:T(2,128)(2,1)S(1)} %pad_maximum_fusion.13), channel_id=1, source_target_pairs={{0,14},{2,0},{4,2},{6,4},{8,6},{10,8},{12,10},{14,12},{1,15},{3,1}... | collective-permute-start | bytes 393224 | tf_op jit(solution)/shard_map/ppermute | solution.py:173
  105.4 1.3 %copy.49 = bf16[2,8,2,64,256]{4,3,2,1,0:T(8,128)(2,1)S(1)} copy(bf16[2,8,2,64,256]{4,3,2,0,1:T(8,128)(2,1)} %bitcast.39) | data formatting | bytes 2097152 | tf_op jit(solution)/shard_map/transpose | solution.py:184
  107.3 1.4 %gather_fusion.2 = bf16[12,64,256]{2,1,0:T(8,128)(2,1)} fusion(bf16[2,16,64,256]{3,2,0,1:T(8,128)(2,1)S(1)} %bitcast.228, s32[12]{0:T(128)S(1)} %reshape.329), kind=kCustom, calls=%fused_computation.2 | custom fusion | bytes 786528 | tf_op jit(solution)/shard_map/gather | solution.py:196
  110.7 1.4 %fusion.42 = (f32[2,2,7,64]{3,2,1,0:T(8,128)S(1)}, f32[2,2,7,64,128]{4,3,2,1,0:T(8,128)S(1)}) fusion(bf16[2,2,64,7,128]{4,2,3,1,0:T(8,128)(2,1)S(1)} %copy.51, bf16[2,128,256]{2,1,0:T(8,128)(2,1)} %bitcast.257), kind=kOutput, calls=%fused_computation.265 | convolution fusion | flops 59177216 | bytes 1448960 | tf_op jit(solution)/shard_map/sqbgh,swh->sqgbw/dot_general | solution.py:219
  118.1 1.3 %convert_element_type.54 = bf16[2,128,896]{2,1,0:T(8,128)(2,1)} reshape(bf16[2,2,64,7,128]{4,3,2,1,0:T(8,128)(2,1)S(1)} %copy.56) | data formatting | bytes 917504 | tf_op jit(solution)/shard_map/convert_element_type | solution.py:272
  (173 shorter events, 40.0 us)
Async XLA Ops:
  0.0 6.0 %copy-start = (s32[2,2,2]{2,1,0:T(2,128)S(1)}, s32[2,2,2]{2,1,0:T(2,128)}, u32[]{:S(2)}) copy-start(s32[2,2,2]{2,1,0:T(2,128)} %param.28) | copy-start | bytes 100
  2.2 3.7 %copy-start.12 = (f32[128]{0:T(128)S(1)}, f32[128]{0:T(128)}, u32[]{:S(2)}) copy-start(f32[128]{0:T(128)} %param.26) | copy-start | bytes 1540
  2.2 14.1 %copy-start.10 = (s32[2,16,14,2]{1,3,2,0:T(2,128)S(1)}, s32[2,16,14,2]{1,3,2,0:T(2,128)}, u32[]{:S(2)}) copy-start(s32[2,16,14,2]{1,3,2,0:T(2,128)} %param.27) | copy-start | bytes 10756
  2.3 34.9 %copy-start.8 = (f32[896]{0:T(1024)S(1)}, f32[896]{0:T(1024)}, u32[]{:S(2)}) copy-start(f32[896]{0:T(1024)} %param.22) | copy-start | bytes 10756
  2.3 34.9 %copy-start.13 = (f32[128]{0:T(128)S(1)}, f32[128]{0:T(128)}, u32[]{:S(2)}) copy-start(f32[128]{0:T(128)} %param.24) | copy-start | bytes 1540
  2.3 44.0 %copy-start.15 = (s32[8]{0:T(128)S(1)}, s32[8]{0:T(128)}, u32[]{:S(2)}) copy-start(s32[8]{0:T(128)} %constant.139.clone) | copy-start | bytes 100
  2.4 46.4 %slice-start.2 = ((f32[896]{0:T(1024)}), f32[512]{0:T(512)S(1)}, s32[]{:S(2)}) async-start(f32[896]{0:T(1024)} %param.22), calls=%async_computation.2 | async-start | bytes 4096 | tf_op jit(solution)/shard_map/slice | solution.py:123
  2.6 9.8 %collective-permute-start.1 = (bf16[224,576]{1,0:T(8,128)(2,1)S(1)}, bf16[224,576]{1,0:T(8,128)(2,1)S(1)}, u32[]{:S(2)}, u32[]{:S(2)}) collective-permute-start(bf16[224,576]{1,0:T(8,128)(2,1)S(1)} %get-tuple-element.428), channel_id=1, source_target_pairs={{0,4},{4,8},{8,12},{12,14},{14,10},{10,6},{6,2},{2,0},{1,5},{5,9},... | collective-permute-start | bytes 774152 | tf_op jit(solution)/shard_map/ppermute | solution.py:47
  5.8 8.5 %collective-permute-start.10 = (bf16[224,576]{1,0:T(8,128)(2,1)S(1)}, bf16[224,576]{1,0:T(8,128)(2,1)S(1)}, u32[]{:S(2)}, u32[]{:S(2)}) collective-permute-start(bf16[224,576]{1,0:T(8,128)(2,1)S(1)} %get-tuple-element.425), channel_id=1, source_target_pairs={{0,2},{4,0},{8,4},{12,8},{14,12},{10,14},{6,10},{2,6},{1,3},{5,1},... | collective-permute-start | bytes 774152 | tf_op jit(solution)/shard_map/ppermute | solution.py:48
  5.8 48.6 %collective-permute-start = (bf16[2,128,1792]{2,1,0:T(8,128)(2,1)}, bf16[2,128,1792]{2,1,0:T(8,128)(2,1)}, u32[]{:S(2)}, u32[]{:S(2)}) collective-permute-start(bf16[2,128,1792]{2,1,0:T(8,128)(2,1)} %param.19), channel_id=1, source_target_pairs={{0,1},{1,0},{2,3},{3,2},{4,5},{5,4},{6,7},{7,6},{8,9},{9,8},{10,11... | collective-permute-start | bytes 2752520 | tf_op jit(solution)/shard_map/ppermute | solution.py:127
  12.5 8.0 %collective-permute-start.4 = (bf16[224,576]{1,0:T(8,128)(2,1)S(1)}, bf16[224,576]{1,0:T(8,128)(2,1)S(1)}, u32[]{:S(2)}, u32[]{:S(2)}) collective-permute-start(bf16[224,576]{1,0:T(8,128)(2,1)S(1)} %collective-permute-done.1), channel_id=1, source_target_pairs={{0,4},{4,8},{8,12},{12,14},{14,10},{10,6},{6,2},{2,0},{1,5},{5,9},... | collective-permute-start | bytes 774152 | tf_op jit(solution)/shard_map/ppermute | solution.py:47
  14.3 7.7 %collective-permute-start.11 = (bf16[224,576]{1,0:T(8,128)(2,1)S(1)}, bf16[224,576]{1,0:T(8,128)(2,1)S(1)}, u32[]{:S(2)}, u32[]{:S(2)}) collective-permute-start(bf16[224,576]{1,0:T(8,128)(2,1)S(1)} %collective-permute-done.10), channel_id=1, source_target_pairs={{0,2},{4,0},{8,4},{12,8},{14,12},{10,14},{6,10},{2,6},{1,3},{5,1},... | collective-permute-start | bytes 774152 | tf_op jit(solution)/shard_map/ppermute | solution.py:48
  14.6 22.5 %collective-permute-start.2 = (bf16[2,128,1792]{2,1,0:T(8,128)(2,1)}, bf16[2,128,1792]{2,1,0:T(8,128)(2,1)}, u32[]{:S(2)}, u32[]{:S(2)}) collective-permute-start(bf16[2,128,1792]{2,1,0:T(8,128)(2,1)} %param.19), channel_id=1, source_target_pairs={{0,16},{16,0},{1,17},{17,1},{2,18},{18,2},{3,19},{19,3},{4,20},{20... | collective-permute-start | bytes 2752520 | tf_op jit(solution)/shard_map/ppermute | solution.py:129
  20.5 7.2 %collective-permute-start.5 = (bf16[224,576]{1,0:T(8,128)(2,1)S(1)}, bf16[224,576]{1,0:T(8,128)(2,1)S(1)}, u32[]{:S(2)}, u32[]{:S(2)}) collective-permute-start(bf16[224,576]{1,0:T(8,128)(2,1)S(1)} %collective-permute-done.4), channel_id=1, source_target_pairs={{0,4},{4,8},{8,12},{12,14},{14,10},{10,6},{6,2},{2,0},{1,5},{5,9},... | collective-permute-start | bytes 774152 | tf_op jit(solution)/shard_map/ppermute | solution.py:47
  22.0 6.9 %collective-permute-start.12 = (bf16[224,576]{1,0:T(8,128)(2,1)S(1)}, bf16[224,576]{1,0:T(8,128)(2,1)S(1)}, u32[]{:S(2)}, u32[]{:S(2)}) collective-permute-start(bf16[224,576]{1,0:T(8,128)(2,1)S(1)} %collective-permute-done.11), channel_id=1, source_target_pairs={{0,2},{4,0},{8,4},{12,8},{14,12},{10,14},{6,10},{2,6},{1,3},{5,1},... | collective-permute-start | bytes 774152 | tf_op jit(solution)/shard_map/ppermute | solution.py:48
  27.7 7.1 %collective-permute-start.6 = (bf16[224,576]{1,0:T(8,128)(2,1)S(1)}, bf16[224,576]{1,0:T(8,128)(2,1)S(1)}, u32[]{:S(2)}, u32[]{:S(2)}) collective-permute-start(bf16[224,576]{1,0:T(8,128)(2,1)S(1)} %collective-permute-done.5), channel_id=1, source_target_pairs={{0,4},{4,8},{8,12},{12,14},{14,10},{10,6},{6,2},{2,0},{1,5},{5,9},... | collective-permute-start | bytes 774152 | tf_op jit(solution)/shard_map/ppermute | solution.py:47
  28.9 7.6 %collective-permute-start.13 = (bf16[224,576]{1,0:T(8,128)(2,1)S(1)}, bf16[224,576]{1,0:T(8,128)(2,1)S(1)}, u32[]{:S(2)}, u32[]{:S(2)}) collective-permute-start(bf16[224,576]{1,0:T(8,128)(2,1)S(1)} %collective-permute-done.12), channel_id=1, source_target_pairs={{0,2},{4,0},{8,4},{12,8},{14,12},{10,14},{6,10},{2,6},{1,3},{5,1},... | collective-permute-start | bytes 774152 | tf_op jit(solution)/shard_map/ppermute | solution.py:48
  34.7 7.6 %collective-permute-start.7 = (bf16[224,576]{1,0:T(8,128)(2,1)S(1)}, bf16[224,576]{1,0:T(8,128)(2,1)S(1)}, u32[]{:S(2)}, u32[]{:S(2)}) collective-permute-start(bf16[224,576]{1,0:T(8,128)(2,1)S(1)} %collective-permute-done.6), channel_id=1, source_target_pairs={{0,4},{4,8},{8,12},{12,14},{14,10},{10,6},{6,2},{2,0},{1,5},{5,9},... | collective-permute-start | bytes 774152 | tf_op jit(solution)/shard_map/ppermute | solution.py:47
  36.4 8.2 %collective-permute-start.14 = (bf16[224,576]{1,0:T(8,128)(2,1)S(1)}, bf16[224,576]{1,0:T(8,128)(2,1)S(1)}, u32[]{:S(2)}, u32[]{:S(2)}) collective-permute-start(bf16[224,576]{1,0:T(8,128)(2,1)S(1)} %collective-permute-done.13), channel_id=1, source_target_pairs={{0,2},{4,0},{8,4},{12,8},{14,12},{10,14},{6,10},{2,6},{1,3},{5,1},... | collective-permute-start | bytes 774152 | tf_op jit(solution)/shard_map/ppermute | solution.py:48
  37.1 28.4 %collective-permute-start.3 = (bf16[2,128,1792]{2,1,0:T(8,128)(2,1)}, bf16[2,128,1792]{2,1,0:T(8,128)(2,1)}, u32[]{:S(2)}, u32[]{:S(2)}) collective-permute-start(bf16[2,128,1792]{2,1,0:T(8,128)(2,1)} %collective-permute-done.2), channel_id=1, source_target_pairs={{0,1},{1,0},{2,3},{3,2},{4,5},{5,4},{6,7},{7,6},{8,9},{9,8},{10,11... | collective-permute-start | bytes 2752520 | tf_op jit(solution)/shard_map/ppermute | solution.py:130
  42.4 8.5 %collective-permute-start.8 = (bf16[224,576]{1,0:T(8,128)(2,1)S(1)}, bf16[224,576]{1,0:T(8,128)(2,1)}, u32[]{:S(2)}, u32[]{:S(2)}) collective-permute-start(bf16[224,576]{1,0:T(8,128)(2,1)S(1)} %collective-permute-done.7), channel_id=1, source_target_pairs={{0,4},{4,8},{8,12},{12,14},{14,10},{10,6},{6,2},{2,0},{1,5},{5,9},... | collective-permute-start | bytes 774152 | tf_op jit(solution)/shard_map/ppermute | solution.py:47
  44.6 8.8 %collective-permute-start.15 = (bf16[224,576]{1,0:T(8,128)(2,1)S(1)}, bf16[224,576]{1,0:T(8,128)(2,1)}, u32[]{:S(2)}, u32[]{:S(2)}) collective-permute-start(bf16[224,576]{1,0:T(8,128)(2,1)S(1)} %collective-permute-done.14), channel_id=1, source_target_pairs={{0,2},{4,0},{8,4},{12,8},{14,12},{10,14},{6,10},{2,6},{1,3},{5,1},... | collective-permute-start | bytes 774152 | tf_op jit(solution)/shard_map/ppermute | solution.py:48
  50.8 7.3 %collective-permute-start.9 = (bf16[224,576]{1,0:T(8,128)(2,1)}, bf16[224,576]{1,0:T(8,128)(2,1)S(1)}, u32[]{:S(2)}, u32[]{:S(2)}) collective-permute-start(bf16[224,576]{1,0:T(8,128)(2,1)} %collective-permute-done.8), channel_id=1, source_target_pairs={{0,4},{4,8},{8,12},{12,14},{14,10},{10,6},{6,2},{2,0},{1,5},{5,9},... | collective-permute-start | bytes 774152 | tf_op jit(solution)/shard_map/ppermute | solution.py:47
  53.5 6.8 %collective-permute-start.16 = (bf16[224,576]{1,0:T(8,128)(2,1)}, bf16[224,576]{1,0:T(8,128)(2,1)S(1)}, u32[]{:S(2)}, u32[]{:S(2)}) collective-permute-start(bf16[224,576]{1,0:T(8,128)(2,1)} %collective-permute-done.15), channel_id=1, source_target_pairs={{0,2},{4,0},{8,4},{12,8},{14,12},{10,14},{6,10},{2,6},{1,3},{5,1},... | collective-permute-start | bytes 774152 | tf_op jit(solution)/shard_map/ppermute | solution.py:48
  75.9 6.8 %collective-permute-start.17 = (bf16[2,128,576]{1,0,2:T(2,128)(2,1)S(1)}, bf16[2,128,576]{1,0,2:T(2,128)(2,1)S(1)}, u32[]{:S(2)}, u32[]{:S(2)}) collective-permute-start(bf16[2,128,576]{1,0,2:T(2,128)(2,1)S(1)} %fusion.22), channel_id=1, source_target_pairs={{0,16},{16,0},{1,17},{17,1},{2,18},{18,2},{3,19},{19,3},{4,20},{20... | collective-permute-start | bytes 884744 | tf_op jit(solution)/shard_map/ppermute | solution.py:162
  83.9 12.4 %collective-permute-start.18 = (bf16[2,128,256]{1,0,2:T(2,128)(2,1)S(1)}, bf16[2,128,256]{1,0,2:T(2,128)(2,1)S(1)}, u32[]{:S(2)}, u32[]{:S(2)}) collective-permute-start(bf16[2,128,256]{1,0,2:T(2,128)(2,1)S(1)} %pad_maximum_fusion.13), channel_id=1, source_target_pairs={{0,2},{2,4},{4,6},{6,8},{8,10},{10,12},{12,14},{14,0},{1,3},{3,5},... | collective-permute-start | bytes 393224 | tf_op jit(solution)/shard_map/ppermute | solution.py:173
  84.9 13.5 %collective-permute-start.19 = (bf16[2,128,256]{1,0,2:T(2,128)(2,1)S(1)}, bf16[2,128,256]{1,0,2:T(2,128)(2,1)S(1)}, u32[]{:S(2)}, u32[]{:S(2)}) collective-permute-start(bf16[2,128,256]{1,0,2:T(2,128)(2,1)S(1)} %pad_maximum_fusion.13), channel_id=1, source_target_pairs={{0,4},{2,6},{4,8},{6,10},{8,12},{10,14},{12,0},{14,2},{1,5},{3,7},... | collective-permute-start | bytes 393224 | tf_op jit(solution)/shard_map/ppermute | solution.py:173
  86.2 15.3 %collective-permute-start.20 = (bf16[2,128,256]{1,0,2:T(2,128)(2,1)S(1)}, bf16[2,128,256]{1,0,2:T(2,128)(2,1)S(1)}, u32[]{:S(2)}, u32[]{:S(2)}) collective-permute-start(bf16[2,128,256]{1,0,2:T(2,128)(2,1)S(1)} %pad_maximum_fusion.13), channel_id=1, source_target_pairs={{0,6},{2,8},{4,10},{6,12},{8,14},{10,0},{12,2},{14,4},{1,7},{3,9},... | collective-permute-start | bytes 393224 | tf_op jit(solution)/shard_map/ppermute | solution.py:173
  89.5 12.8 %collective-permute-start.21 = (bf16[2,128,256]{1,0,2:T(2,128)(2,1)S(1)}, bf16[2,128,256]{1,0,2:T(2,128)(2,1)S(1)}, u32[]{:S(2)}, u32[]{:S(2)}) collective-permute-start(bf16[2,128,256]{1,0,2:T(2,128)(2,1)S(1)} %pad_maximum_fusion.13), channel_id=1, source_target_pairs={{0,8},{2,10},{4,12},{6,14},{8,0},{10,2},{12,4},{14,6},{1,9},{3,11}... | collective-permute-start | bytes 393224 | tf_op jit(solution)/shard_map/ppermute | solution.py:173
  90.8 12.2 %collective-permute-start.22 = (bf16[2,128,256]{1,0,2:T(2,128)(2,1)S(1)}, bf16[2,128,256]{1,0,2:T(2,128)(2,1)S(1)}, u32[]{:S(2)}, u32[]{:S(2)}) collective-permute-start(bf16[2,128,256]{1,0,2:T(2,128)(2,1)S(1)} %pad_maximum_fusion.13), channel_id=1, source_target_pairs={{0,10},{2,12},{4,14},{6,0},{8,2},{10,4},{12,6},{14,8},{1,11},{3,13... | collective-permute-start | bytes 393224 | tf_op jit(solution)/shard_map/ppermute | solution.py:173
  96.3 7.5 %collective-permute-start.23 = (bf16[2,128,256]{1,0,2:T(2,128)(2,1)S(1)}, bf16[2,128,256]{1,0,2:T(2,128)(2,1)S(1)}, u32[]{:S(2)}, u32[]{:S(2)}) collective-permute-start(bf16[2,128,256]{1,0,2:T(2,128)(2,1)S(1)} %pad_maximum_fusion.13), channel_id=1, source_target_pairs={{0,12},{2,14},{4,0},{6,2},{8,4},{10,6},{12,8},{14,10},{1,13},{3,15... | collective-permute-start | bytes 393224 | tf_op jit(solution)/shard_map/ppermute | solution.py:173
  98.4 6.2 %collective-permute-start.24 = (bf16[2,128,256]{1,0,2:T(2,128)(2,1)S(1)}, bf16[2,128,256]{1,0,2:T(2,128)(2,1)S(1)}, u32[]{:S(2)}, u32[]{:S(2)}) collective-permute-start(bf16[2,128,256]{1,0,2:T(2,128)(2,1)S(1)} %pad_maximum_fusion.13), channel_id=1, source_target_pairs={{0,14},{2,0},{4,2},{6,4},{8,6},{10,8},{12,10},{14,12},{1,15},{3,1}... | collective-permute-start | bytes 393224 | tf_op jit(solution)/shard_map/ppermute | solution.py:173
  (12 other events, 25.0 us)

commit v17 on v14

--- a/solution.py
+++ b/solution.py
@@ -158,13 +158,25 @@
     value_rows = jnp.concatenate([low[..., split:], high[..., split:]], axis=-1)
 
     pairs = jnp.concatenate([key, value_rows], axis=-1)
-    if row_count <= 8:
-        by_shift = [pairs] + [
-            lax.ppermute(pairs, "row", [(i, (i + k) % row_count) for i in range(row_count)])
-            for k in range(1, row_count)
-        ]
-        gathered = jnp.stack(by_shift)
-        owner_slot = (here - jnp.arange(row_count, dtype=jnp.int32)) % row_count
+    if row_count == 8:
+        order = snake_order(row_count)
+        position = [0] * row_count
+        for i, d in enumerate(order):
+            position[d] = i
+        forward = [(order[i], order[(i + 1) % row_count]) for i in range(row_count)]
+        backward = [(order[i], order[(i - 1) % row_count]) for i in range(row_count)]
+        ahead, behind = pairs, pairs
+        ahead_parts, behind_parts = [], []
+        for step in range(1, row_count // 2 + 1):
+            ahead = lax.ppermute(ahead, "row", forward)
+            ahead_parts.append(ahead)
+            if step < row_count // 2:
+                behind = lax.ppermute(behind, "row", backward)
+                behind_parts.append(behind)
+        gathered = jnp.stack([pairs] + ahead_parts + behind_parts)
+        table = jnp.array(position, dtype=jnp.int32)
+        delta = (table[here] - table) % row_count
+        owner_slot = jnp.where(delta <= row_count // 2, delta, row_count // 2 + row_count - delta)
     else:
         gathered = lax.all_gather(pairs, "row", axis=0, tiled=False)
         owner_slot = jnp.arange(row_count, dtype=jnp.int32)

time: 119 us -> 118 us (level); the launches traced: 117 us -> 118 us
  waiting for transfers between devices: 30.5 us -> 36.2 us
  starting transfers between devices: 30.1 us -> 25.5 us
    ppermute x7, waiting for transfers between devices: 2.83 us -> 8.65 us  [the longest x4 6.49 us: shards(): ahead = lax.ppermute(ahead, 'row', forward)]
    ppermute x7, starting transfers between devices: 12.6 us -> 7.85 us  [the longest x4 6 us: shards(): ahead = lax.ppermute(ahead, 'row', forward)]
  transfers between devices with their start and end apart: 25 -> 25, of which waited for: 13 -> 16; matrix products, arithmetic and copies ran while one was open for 27% -> 28% of each run, Pallas kernels for 0% -> 0%
where the time goes in v17:
time: 118 us
  waiting for transfers between devices  36.2 us (31%)
  local copies, waits for them, and re-layouts  32.2 us (27%)
  starting transfers between devices  25.5 us (22%)
  other arithmetic  16.4 us (14%)
  matrix products  6.81 us (6%)
    ppermute x7, waiting for transfers between devices, gather_rows(): ahead = lax.ppermute(ahead, 'row', forward)  21.2 us
    ppermute x7, starting transfers between devices, gather_rows(): ahead = lax.ppermute(ahead, 'row', forward)  12.5 us
    unnamed x43, local copies, waits for them, and re-layouts  10.3 us
    ppermute x4, waiting for transfers between devices, shards(): ahead = lax.ppermute(ahead, 'row', forward)  6.49 us
    ppermute x4, starting transfers between devices, shards(): ahead = lax.ppermute(ahead, 'row', forward)  6 us
    ppermute x1, waiting for transfers between devices, shards(): returned = lax.ppermute(result[passages:], 'groups', SWAP)  5.63 us
    gather x1, local copies, waits for them, and re-layouts, gather_rows(): jnp.stack(behind_parts)[behind_pick]  3.9 us
    gather x1, local copies, waits for them, and re-layouts, gather_rows(): jnp.stack(ahead_parts)[ahead_pick]  3.9 us
  transfers between devices with their start and end apart: 25, of which 16 were waited for; matrix products, arithmetic and copies ran while one was open for 28% of the time, Pallas kernels for 0%

profile of v17, /device:TPU:0, one launch (start us, length us, event | category | flops | bytes accessed | tf_op | source)
XLA Modules:
  0.0 117.9 jit_solution(7168364047584975813)
XLA Ops:
  0.0 1.3 %constant_dynamic-update-slice_fusion.1 = bf16[448,1024]{1,0:T(8,128)(2,1)S(1)} fusion(bf16[448,896]{1,0:T(8,128)(2,1)} %param.14), kind=kLoop, calls=%fused_computation.89 | loop fusion | bytes 1605632
  2.7 3.1 %collective-permute-start.1 = (bf16[224,576]{1,0:T(8,128)(2,1)S(1)}, bf16[224,576]{1,0:T(8,128)(2,1)S(1)}, u32[]{:S(2)}, u32[]{:S(2)}) collective-permute-start(bf16[224,576]{1,0:T(8,128)(2,1)S(1)} %pad_maximum_fusion.5), channel_id=1, source_target_pairs={{0,4},{4,8},{8,12},{12,14},{14,10},{10,6},{6,2},{2,0},{1,5},{5,9},... | collective-permute-start | bytes 774152 | tf_op jit(solution)/shard_map/ppermute | solution.py:47
  10.3 2.2 %collective-permute-done.1 = bf16[224,576]{1,0:T(8,128)(2,1)S(1)} collective-permute-done((bf16[224,576]{1,0:T(8,128)(2,1)S(1)}, bf16[224,576]{1,0:T(8,128)(2,1)S(1)}, u32[]{:S(2)}, u32[]{:S(2)}) %collective-permute-start.1) | collective-permute-done | bytes 258080 | tf_op jit(solution)/shard_map/ppermute | solution.py:47
  12.5 1.8 %collective-permute-start.2 = (bf16[2,128,1792]{2,1,0:T(8,128)(2,1)S(1)}, bf16[2,128,1792]{2,1,0:T(8,128)(2,1)}, u32[]{:S(2)}, u32[]{:S(2)}) collective-permute-start(bf16[2,128,1792]{2,1,0:T(8,128)(2,1)S(1)} %copy-done.1), channel_id=1, source_target_pairs={{0,16},{16,0},{1,17},{17,1},{2,18},{18,2},{3,19},{19,3},{4,20},{20... | collective-permute-start | bytes 2752520 | tf_op jit(solution)/shard_map/ppermute | solution.py:119
  14.3 1.6 %collective-permute-start.4 = (bf16[224,576]{1,0:T(8,128)(2,1)S(1)}, bf16[224,576]{1,0:T(8,128)(2,1)S(1)}, u32[]{:S(2)}, u32[]{:S(2)}) collective-permute-start(bf16[224,576]{1,0:T(8,128)(2,1)S(1)} %collective-permute-done.1), channel_id=1, source_target_pairs={{0,4},{4,8},{8,12},{12,14},{14,10},{10,6},{6,2},{2,0},{1,5},{5,9},... | collective-permute-start | bytes 774152 | tf_op jit(solution)/shard_map/ppermute | solution.py:47
  17.8 3.9 %collective-permute-done.4 = bf16[224,576]{1,0:T(8,128)(2,1)S(1)} collective-permute-done((bf16[224,576]{1,0:T(8,128)(2,1)S(1)}, bf16[224,576]{1,0:T(8,128)(2,1)S(1)}, u32[]{:S(2)}, u32[]{:S(2)}) %collective-permute-start.4) | collective-permute-done | bytes 258080 | tf_op jit(solution)/shard_map/ppermute | solution.py:47
  21.7 1.6 %collective-permute-start.5 = (bf16[224,576]{1,0:T(8,128)(2,1)S(1)}, bf16[224,576]{1,0:T(8,128)(2,1)S(1)}, u32[]{:S(2)}, u32[]{:S(2)}) collective-permute-start(bf16[224,576]{1,0:T(8,128)(2,1)S(1)} %collective-permute-done.4), channel_id=1, source_target_pairs={{0,4},{4,8},{8,12},{12,14},{14,10},{10,6},{6,2},{2,0},{1,5},{5,9},... | collective-permute-start | bytes 774152 | tf_op jit(solution)/shard_map/ppermute | solution.py:47
  25.2 3.3 %collective-permute-done.5 = bf16[224,576]{1,0:T(8,128)(2,1)S(1)} collective-permute-done((bf16[224,576]{1,0:T(8,128)(2,1)S(1)}, bf16[224,576]{1,0:T(8,128)(2,1)S(1)}, u32[]{:S(2)}, u32[]{:S(2)}) %collective-permute-start.5) | collective-permute-done | bytes 258080 | tf_op jit(solution)/shard_map/ppermute | solution.py:47
  28.5 1.6 %collective-permute-start.6 = (bf16[224,576]{1,0:T(8,128)(2,1)S(1)}, bf16[224,576]{1,0:T(8,128)(2,1)S(1)}, u32[]{:S(2)}, u32[]{:S(2)}) collective-permute-start(bf16[224,576]{1,0:T(8,128)(2,1)S(1)} %collective-permute-done.5), channel_id=1, source_target_pairs={{0,4},{4,8},{8,12},{12,14},{14,10},{10,6},{6,2},{2,0},{1,5},{5,9},... | collective-permute-start | bytes 774152 | tf_op jit(solution)/shard_map/ppermute | solution.py:47
  32.3 2.0 %maximum_select_fusion = bf16[2,128,3584]{2,1,0:T(8,128)(2,1)S(1)} fusion(bf16[2,128,1792]{2,1,0:T(8,128)(2,1)} %collective-permute-done, bf16[2,128,1792]{2,1,0:T(8,128)(2,1)S(1)} %copy-done.1, pred[]{:T(512)S(6)} %eq.14), kind=kLoop, calls=%fused_computation.14 | loop fusion | flops 8257536 | bytes 3670017 | tf_op jit(solution)/shard_map/jit(_where)/select_n | solution.py:121
  34.3 1.8 %collective-permute-done.6 = bf16[224,576]{1,0:T(8,128)(2,1)S(1)} collective-permute-done((bf16[224,576]{1,0:T(8,128)(2,1)S(1)}, bf16[224,576]{1,0:T(8,128)(2,1)S(1)}, u32[]{:S(2)}, u32[]{:S(2)}) %collective-permute-start.6) | collective-permute-done | bytes 258080 | tf_op jit(solution)/shard_map/ppermute | solution.py:47
  36.1 1.6 %collective-permute-start.7 = (bf16[224,576]{1,0:T(8,128)(2,1)S(1)}, bf16[224,576]{1,0:T(8,128)(2,1)S(1)}, u32[]{:S(2)}, u32[]{:S(2)}) collective-permute-start(bf16[224,576]{1,0:T(8,128)(2,1)S(1)} %collective-permute-done.6), channel_id=1, source_target_pairs={{0,4},{4,8},{8,12},{12,14},{14,10},{10,6},{6,2},{2,0},{1,5},{5,9},... | collective-permute-start | bytes 774152 | tf_op jit(solution)/shard_map/ppermute | solution.py:47
  39.6 3.1 %collective-permute-done.7 = bf16[224,576]{1,0:T(8,128)(2,1)S(1)} collective-permute-done((bf16[224,576]{1,0:T(8,128)(2,1)S(1)}, bf16[224,576]{1,0:T(8,128)(2,1)S(1)}, u32[]{:S(2)}, u32[]{:S(2)}) %collective-permute-start.7) | collective-permute-done | bytes 258080 | tf_op jit(solution)/shard_map/ppermute | solution.py:47
  42.7 1.6 %collective-permute-start.8 = (bf16[224,576]{1,0:T(8,128)(2,1)S(1)}, bf16[224,576]{1,0:T(8,128)(2,1)S(1)}, u32[]{:S(2)}, u32[]{:S(2)}) collective-permute-start(bf16[224,576]{1,0:T(8,128)(2,1)S(1)} %collective-permute-done.7), channel_id=1, source_target_pairs={{0,4},{4,8},{8,12},{12,14},{14,10},{10,6},{6,2},{2,0},{1,5},{5,9},... | collective-permute-start | bytes 774152 | tf_op jit(solution)/shard_map/ppermute | solution.py:47
  46.5 4.0 %collective-permute-done.8 = bf16[224,576]{1,0:T(8,128)(2,1)S(1)} collective-permute-done((bf16[224,576]{1,0:T(8,128)(2,1)S(1)}, bf16[224,576]{1,0:T(8,128)(2,1)S(1)}, u32[]{:S(2)}, u32[]{:S(2)}) %collective-permute-start.8) | collective-permute-done | bytes 258080 | tf_op jit(solution)/shard_map/ppermute | solution.py:47
  50.4 1.6 %collective-permute-start.9 = (bf16[224,576]{1,0:T(8,128)(2,1)S(1)}, bf16[224,576]{1,0:T(8,128)(2,1)S(1)}, u32[]{:S(2)}, u32[]{:S(2)}) collective-permute-start(bf16[224,576]{1,0:T(8,128)(2,1)S(1)} %collective-permute-done.8), channel_id=1, source_target_pairs={{0,4},{4,8},{8,12},{12,14},{14,10},{10,6},{6,2},{2,0},{1,5},{5,9},... | collective-permute-start | bytes 774152 | tf_op jit(solution)/shard_map/ppermute | solution.py:47
  54.1 2.9 %collective-permute-done.9 = bf16[224,576]{1,0:T(8,128)(2,1)S(1)} collective-permute-done((bf16[224,576]{1,0:T(8,128)(2,1)S(1)}, bf16[224,576]{1,0:T(8,128)(2,1)S(1)}, u32[]{:S(2)}, u32[]{:S(2)}) %collective-permute-start.9) | collective-permute-done | bytes 258080 | tf_op jit(solution)/shard_map/ppermute | solution.py:47
  57.8 3.9 %gather_fusion = bf16[8,224,576]{2,1,0:T(8,128)(2,1)} fusion(bf16[8,224,576]{2,1,0:T(8,128)(2,1)} %bitcast_dynamic-update-slice_fusion.8, s32[1024]{0:T(1024)S(1)} %get-tuple-element.30), kind=kCustom, calls=%fused_computation | custom fusion | bytes 4128800 | tf_op jit(solution)/shard_map/gather | solution.py:56
  62.5 3.9 %gather_fusion.1 = bf16[8,224,576]{2,1,0:T(8,128)(2,1)} fusion(bf16[8,224,576]{2,1,0:T(8,128)(2,1)} %bitcast_dynamic-update-slice_fusion, s32[1024]{0:T(1024)S(1)} %get-tuple-element.29), kind=kCustom, calls=%fused_computation.1 | custom fusion | bytes 4128800 | tf_op jit(solution)/shard_map/gather | solution.py:56
  66.4 2.8 %pad_maximum_fusion = bf16[8,448,576]{2,1,0:T(8,128)(2,1)S(1)} fusion(bf16[8,224,576]{2,1,0:T(8,128)(2,1)} %gather_fusion.1, bf16[8,224,576]{2,1,0:T(8,128)(2,1)} %gather_fusion), kind=kLoop, calls=%fused_computation.12 | loop fusion | flops 8257536 | bytes 8257536 | tf_op jit(solution)/shard_map/concatenate | solution.py:55
  69.2 1.9 %maximum_select_fusion.1 = bf16[2,128,3584]{2,1,0:T(8,128)(2,1)S(1)} fusion(bf16[2,128,1792]{2,1,0:T(8,128)(2,1)S(1)} %collective-permute-done.3, bf16[2,128,1792]{2,1,0:T(8,128)(2,1)} %collective-permute-done.2, pred[]{:T(512)S(6)} %eq.14), kind=kLoop, calls=%fused_computation.15 | loop fusion | flops 8257536 | bytes 3670017 | tf_op jit(solution)/shard_map/jit(_where)/select_n | solution.py:126
  73.0 2.4 %convolution_add_fusion = f32[512,576]{0,1:T(8,128)S(1)} fusion(bf16[512,3584]{1,0:T(8,128)(2,1)S(1)} %bitcast.140, bf16[3584,576]{1,0:T(8,128)(2,1)S(1)} %bitcast.135, f32[576]{0:T(1024)S(1)} %maximum_select_fusion.2), kind=kOutput, calls=%fused_computation.30 | convolution fusion | flops 2114224128 | bytes 8980736 | tf_op jit(solution)/shard_map/dot_general | solution.py:141
  78.7 5.6 %collective-permute-done.17 = bf16[2,128,576]{1,0,2:T(2,128)(2,1)S(1)} collective-permute-done((bf16[2,128,576]{1,0,2:T(2,128)(2,1)S(1)}, bf16[2,128,576]{1,0,2:T(2,128)(2,1)S(1)}, u32[]{:S(2)}, u32[]{:S(2)}) %collective-permute-start.17) | collective-permute-done | bytes 294944 | tf_op jit(solution)/shard_map/ppermute | solution.py:152
  85.2 1.6 %collective-permute-start.18 = (bf16[2,128,256]{1,0,2:T(2,128)(2,1)S(1)}, bf16[2,128,256]{1,0,2:T(2,128)(2,1)S(1)}, u32[]{:S(2)}, u32[]{:S(2)}) collective-permute-start(bf16[2,128,256]{1,0,2:T(2,128)(2,1)S(1)} %pad_maximum_fusion.7), channel_id=1, source_target_pairs={{0,4},{4,8},{8,12},{12,14},{14,10},{10,6},{6,2},{2,0},{1,5},{5,9},... | collective-permute-start | bytes 393224 | tf_op jit(solution)/shard_map/ppermute | solution.py:171
  87.3 3.0 %collective-permute-done.18 = bf16[2,128,256]{1,0,2:T(2,128)(2,1)S(1)} collective-permute-done((bf16[2,128,256]{1,0,2:T(2,128)(2,1)S(1)}, bf16[2,128,256]{1,0,2:T(2,128)(2,1)S(1)}, u32[]{:S(2)}, u32[]{:S(2)}) %collective-permute-start.18) | collective-permute-done | bytes 131104 | tf_op jit(solution)/shard_map/ppermute | solution.py:171
  90.3 1.6 %collective-permute-start.19 = (bf16[2,128,256]{1,0,2:T(2,128)(2,1)S(1)}, bf16[2,128,256]{1,0,2:T(2,128)(2,1)S(1)}, u32[]{:S(2)}, u32[]{:S(2)}) collective-permute-start(bf16[2,128,256]{1,0,2:T(2,128)(2,1)S(1)} %collective-permute-done.18), channel_id=1, source_target_pairs={{0,4},{4,8},{8,12},{12,14},{14,10},{10,6},{6,2},{2,0},{1,5},{5,9},... | collective-permute-start | bytes 393224 | tf_op jit(solution)/shard_map/ppermute | solution.py:171
  94.1 2.0 %collective-permute-done.19 = bf16[2,128,256]{1,0,2:T(2,128)(2,1)S(1)} collective-permute-done((bf16[2,128,256]{1,0,2:T(2,128)(2,1)S(1)}, bf16[2,128,256]{1,0,2:T(2,128)(2,1)S(1)}, u32[]{:S(2)}, u32[]{:S(2)}) %collective-permute-start.19) | collective-permute-done | bytes 131104 | tf_op jit(solution)/shard_map/ppermute | solution.py:171
  96.0 1.6 %collective-permute-start.20 = (bf16[2,128,256]{1,0,2:T(2,128)(2,1)S(1)}, bf16[2,128,256]{1,0,2:T(2,128)(2,1)S(1)}, u32[]{:S(2)}, u32[]{:S(2)}) collective-permute-start(bf16[2,128,256]{1,0,2:T(2,128)(2,1)S(1)} %collective-permute-done.19), channel_id=1, source_target_pairs={{0,4},{4,8},{8,12},{12,14},{14,10},{10,6},{6,2},{2,0},{1,5},{5,9},... | collective-permute-start | bytes 393224 | tf_op jit(solution)/shard_map/ppermute | solution.py:171
  98.0 1.8 %copy.52 = bf16[2,2,64,7,128]{4,2,3,1,0:T(8,128)(2,1)S(1)} copy(bf16[2,2,64,7,128]{2,1,0,4,3:T(2,128)(2,1)S(1)} %reshape.378) | data formatting | bytes 917504 | tf_op jit(solution)/shard_map/reshape | solution.py:212
  102.9 2.1 %collective-permute-done.24 = bf16[2,128,256]{1,0,2:T(2,128)(2,1)S(1)} collective-permute-done((bf16[2,128,256]{1,0,2:T(2,128)(2,1)S(1)}, bf16[2,128,256]{1,0,2:T(2,128)(2,1)S(1)}, u32[]{:S(2)}, u32[]{:S(2)}) %collective-permute-start.24) | collective-permute-done | bytes 131104 | tf_op jit(solution)/shard_map/ppermute | solution.py:174
  107.4 1.4 %gather_fusion.4 = bf16[12,64,256]{2,1,0:T(8,128)(2,1)} fusion(bf16[2,16,64,256]{3,2,0,1:T(8,128)(2,1)S(1)} %bitcast.132, s32[12]{0:T(128)S(1)} %reshape.346), kind=kCustom, calls=%fused_computation.4 | custom fusion | bytes 786528 | tf_op jit(solution)/shard_map/gather | solution.py:198
  116.6 1.3 %convert_element_type.60 = bf16[2,128,896]{2,1,0:T(8,128)(2,1)} reshape(bf16[2,2,64,7,128]{4,3,2,1,0:T(8,128)(2,1)S(1)} %copy.57) | data formatting | bytes 917504 | tf_op jit(solution)/shard_map/convert_element_type | solution.py:274
  (164 shorter events, 41.4 us)
Async XLA Ops:
  0.0 9.8 %copy-start = (s32[2,2,2]{2,1,0:T(2,128)S(1)}, s32[2,2,2]{2,1,0:T(2,128)}, u32[]{:S(2)}) copy-start(s32[2,2,2]{2,1,0:T(2,128)} %param.21) | copy-start | bytes 100
  2.4 6.6 %copy-start.9 = (s32[8]{0:T(128)S(1)}, s32[8]{0:T(128)}, u32[]{:S(2)}) copy-start(s32[8]{0:T(128)} %constant.152) | copy-start | bytes 100
  2.4 7.2 %copy-start.7 = (f32[128]{0:T(128)S(1)}, f32[128]{0:T(128)}, u32[]{:S(2)}) copy-start(f32[128]{0:T(128)} %param.19) | copy-start | bytes 1540
  2.4 7.3 %copy-start.5 = (f32[896]{0:T(1024)S(1)}, f32[896]{0:T(1024)}, u32[]{:S(2)}) copy-start(f32[896]{0:T(1024)} %param.15) | copy-start | bytes 10756
  2.4 7.3 %copy-start.8 = (f32[128]{0:T(128)S(1)}, f32[128]{0:T(128)}, u32[]{:S(2)}) copy-start(f32[128]{0:T(128)} %param.17) | copy-start | bytes 1540
  2.5 7.6 %copy-start.6 = (s32[2,16,14,2]{1,3,2,0:T(2,128)S(1)}, s32[2,16,14,2]{1,3,2,0:T(2,128)}, u32[]{:S(2)}) copy-start(s32[2,16,14,2]{1,3,2,0:T(2,128)} %param.20) | copy-start | bytes 10756
  2.5 7.7 %slice-start = ((f32[896]{0:T(1024)}), f32[512]{0:T(512)S(1)}, s32[]{:S(2)}) async-start(f32[896]{0:T(1024)} %param.15), calls=%async_computation | async-start | bytes 4096 | tf_op jit(solution)/shard_map/slice | solution.py:113
  2.7 9.8 %collective-permute-start.1 = (bf16[224,576]{1,0:T(8,128)(2,1)S(1)}, bf16[224,576]{1,0:T(8,128)(2,1)S(1)}, u32[]{:S(2)}, u32[]{:S(2)}) collective-permute-start(bf16[224,576]{1,0:T(8,128)(2,1)S(1)} %pad_maximum_fusion.5), channel_id=1, source_target_pairs={{0,4},{4,8},{8,12},{12,14},{14,10},{10,6},{6,2},{2,0},{1,5},{5,9},... | collective-permute-start | bytes 774152 | tf_op jit(solution)/shard_map/ppermute | solution.py:47
  5.9 9.9 %collective-permute-start.10 = (bf16[224,576]{1,0:T(8,128)(2,1)S(1)}, bf16[224,576]{1,0:T(8,128)(2,1)S(1)}, u32[]{:S(2)}, u32[]{:S(2)}) collective-permute-start(bf16[224,576]{1,0:T(8,128)(2,1)S(1)} %pad_maximum_fusion.6), channel_id=1, source_target_pairs={{0,2},{4,0},{8,4},{12,8},{14,12},{10,14},{6,10},{2,6},{1,3},{5,1},... | collective-permute-start | bytes 774152 | tf_op jit(solution)/shard_map/ppermute | solution.py:48
  6.0 26.4 %collective-permute-start = (bf16[2,128,1792]{2,1,0:T(8,128)(2,1)S(1)}, bf16[2,128,1792]{2,1,0:T(8,128)(2,1)}, u32[]{:S(2)}, u32[]{:S(2)}) collective-permute-start(bf16[2,128,1792]{2,1,0:T(8,128)(2,1)S(1)} %copy-done.1), channel_id=1, source_target_pairs={{0,1},{1,0},{2,3},{3,2},{4,5},{5,4},{6,7},{7,6},{8,9},{9,8},{10,11... | collective-permute-start | bytes 2752520 | tf_op jit(solution)/shard_map/ppermute | solution.py:117
  12.5 27.1 %collective-permute-start.2 = (bf16[2,128,1792]{2,1,0:T(8,128)(2,1)S(1)}, bf16[2,128,1792]{2,1,0:T(8,128)(2,1)}, u32[]{:S(2)}, u32[]{:S(2)}) collective-permute-start(bf16[2,128,1792]{2,1,0:T(8,128)(2,1)S(1)} %copy-done.1), channel_id=1, source_target_pairs={{0,16},{16,0},{1,17},{17,1},{2,18},{18,2},{3,19},{19,3},{4,20},{20... | collective-permute-start | bytes 2752520 | tf_op jit(solution)/shard_map/ppermute | solution.py:119
  14.3 7.4 %collective-permute-start.4 = (bf16[224,576]{1,0:T(8,128)(2,1)S(1)}, bf16[224,576]{1,0:T(8,128)(2,1)S(1)}, u32[]{:S(2)}, u32[]{:S(2)}) collective-permute-start(bf16[224,576]{1,0:T(8,128)(2,1)S(1)} %collective-permute-done.1), channel_id=1, source_target_pairs={{0,4},{4,8},{8,12},{12,14},{14,10},{10,6},{6,2},{2,0},{1,5},{5,9},... | collective-permute-start | bytes 774152 | tf_op jit(solution)/shard_map/ppermute | solution.py:47
  15.8 7.4 %collective-permute-start.11 = (bf16[224,576]{1,0:T(8,128)(2,1)S(1)}, bf16[224,576]{1,0:T(8,128)(2,1)S(1)}, u32[]{:S(2)}, u32[]{:S(2)}) collective-permute-start(bf16[224,576]{1,0:T(8,128)(2,1)S(1)} %collective-permute-done.10), channel_id=1, source_target_pairs={{0,2},{4,0},{8,4},{12,8},{14,12},{10,14},{6,10},{2,6},{1,3},{5,1},... | collective-permute-start | bytes 774152 | tf_op jit(solution)/shard_map/ppermute | solution.py:48
  21.7 6.9 %collective-permute-start.5 = (bf16[224,576]{1,0:T(8,128)(2,1)S(1)}, bf16[224,576]{1,0:T(8,128)(2,1)S(1)}, u32[]{:S(2)}, u32[]{:S(2)}) collective-permute-start(bf16[224,576]{1,0:T(8,128)(2,1)S(1)} %collective-permute-done.4), channel_id=1, source_target_pairs={{0,4},{4,8},{8,12},{12,14},{14,10},{10,6},{6,2},{2,0},{1,5},{5,9},... | collective-permute-start | bytes 774152 | tf_op jit(solution)/shard_map/ppermute | solution.py:47
  23.3 7.1 %collective-permute-start.12 = (bf16[224,576]{1,0:T(8,128)(2,1)S(1)}, bf16[224,576]{1,0:T(8,128)(2,1)S(1)}, u32[]{:S(2)}, u32[]{:S(2)}) collective-permute-start(bf16[224,576]{1,0:T(8,128)(2,1)S(1)} %collective-permute-done.11), channel_id=1, source_target_pairs={{0,2},{4,0},{8,4},{12,8},{14,12},{10,14},{6,10},{2,6},{1,3},{5,1},... | collective-permute-start | bytes 774152 | tf_op jit(solution)/shard_map/ppermute | solution.py:48
  28.5 7.5 %collective-permute-start.6 = (bf16[224,576]{1,0:T(8,128)(2,1)S(1)}, bf16[224,576]{1,0:T(8,128)(2,1)S(1)}, u32[]{:S(2)}, u32[]{:S(2)}) collective-permute-start(bf16[224,576]{1,0:T(8,128)(2,1)S(1)} %collective-permute-done.5), channel_id=1, source_target_pairs={{0,4},{4,8},{8,12},{12,14},{14,10},{10,6},{6,2},{2,0},{1,5},{5,9},... | collective-permute-start | bytes 774152 | tf_op jit(solution)/shard_map/ppermute | solution.py:47
  30.4 8.0 %collective-permute-start.13 = (bf16[224,576]{1,0:T(8,128)(2,1)S(1)}, bf16[224,576]{1,0:T(8,128)(2,1)S(1)}, u32[]{:S(2)}, u32[]{:S(2)}) collective-permute-start(bf16[224,576]{1,0:T(8,128)(2,1)S(1)} %collective-permute-done.12), channel_id=1, source_target_pairs={{0,2},{4,0},{8,4},{12,8},{14,12},{10,14},{6,10},{2,6},{1,3},{5,1},... | collective-permute-start | bytes 774152 | tf_op jit(solution)/shard_map/ppermute | solution.py:48
  36.1 6.6 %collective-permute-start.7 = (bf16[224,576]{1,0:T(8,128)(2,1)S(1)}, bf16[224,576]{1,0:T(8,128)(2,1)S(1)}, u32[]{:S(2)}, u32[]{:S(2)}) collective-permute-start(bf16[224,576]{1,0:T(8,128)(2,1)S(1)} %collective-permute-done.6), channel_id=1, source_target_pairs={{0,4},{4,8},{8,12},{12,14},{14,10},{10,6},{6,2},{2,0},{1,5},{5,9},... | collective-permute-start | bytes 774152 | tf_op jit(solution)/shard_map/ppermute | solution.py:47
  38.4 6.9 %collective-permute-start.14 = (bf16[224,576]{1,0:T(8,128)(2,1)S(1)}, bf16[224,576]{1,0:T(8,128)(2,1)S(1)}, u32[]{:S(2)}, u32[]{:S(2)}) collective-permute-start(bf16[224,576]{1,0:T(8,128)(2,1)S(1)} %collective-permute-done.13), channel_id=1, source_target_pairs={{0,2},{4,0},{8,4},{12,8},{14,12},{10,14},{6,10},{2,6},{1,3},{5,1},... | collective-permute-start | bytes 774152 | tf_op jit(solution)/shard_map/ppermute | solution.py:48
  39.6 29.6 %collective-permute-start.3 = (bf16[2,128,1792]{2,1,0:T(8,128)(2,1)}, bf16[2,128,1792]{2,1,0:T(8,128)(2,1)S(1)}, u32[]{:S(2)}, u32[]{:S(2)}) collective-permute-start(bf16[2,128,1792]{2,1,0:T(8,128)(2,1)} %collective-permute-done.2), channel_id=1, source_target_pairs={{0,1},{1,0},{2,3},{3,2},{4,5},{5,4},{6,7},{7,6},{8,9},{9,8},{10,11... | collective-permute-start | bytes 2752520 | tf_op jit(solution)/shard_map/ppermute | solution.py:120
  42.7 7.7 %collective-permute-start.8 = (bf16[224,576]{1,0:T(8,128)(2,1)S(1)}, bf16[224,576]{1,0:T(8,128)(2,1)S(1)}, u32[]{:S(2)}, u32[]{:S(2)}) collective-permute-start(bf16[224,576]{1,0:T(8,128)(2,1)S(1)} %collective-permute-done.7), channel_id=1, source_target_pairs={{0,4},{4,8},{8,12},{12,14},{14,10},{10,6},{6,2},{2,0},{1,5},{5,9},... | collective-permute-start | bytes 774152 | tf_op jit(solution)/shard_map/ppermute | solution.py:47
  45.3 7.7 %collective-permute-start.15 = (bf16[224,576]{1,0:T(8,128)(2,1)S(1)}, bf16[224,576]{1,0:T(8,128)(2,1)S(1)}, u32[]{:S(2)}, u32[]{:S(2)}) collective-permute-start(bf16[224,576]{1,0:T(8,128)(2,1)S(1)} %collective-permute-done.14), channel_id=1, source_target_pairs={{0,2},{4,0},{8,4},{12,8},{14,12},{10,14},{6,10},{2,6},{1,3},{5,1},... | collective-permute-start | bytes 774152 | tf_op jit(solution)/shard_map/ppermute | solution.py:48
  50.4 6.6 %collective-permute-start.9 = (bf16[224,576]{1,0:T(8,128)(2,1)S(1)}, bf16[224,576]{1,0:T(8,128)(2,1)S(1)}, u32[]{:S(2)}, u32[]{:S(2)}) collective-permute-start(bf16[224,576]{1,0:T(8,128)(2,1)S(1)} %collective-permute-done.8), channel_id=1, source_target_pairs={{0,4},{4,8},{8,12},{12,14},{14,10},{10,6},{6,2},{2,0},{1,5},{5,9},... | collective-permute-start | bytes 774152 | tf_op jit(solution)/shard_map/ppermute | solution.py:47
  52.9 8.8 %collective-permute-start.16 = (bf16[224,576]{1,0:T(8,128)(2,1)S(1)}, bf16[224,576]{1,0:T(8,128)(2,1)S(1)}, u32[]{:S(2)}, u32[]{:S(2)}) collective-permute-start(bf16[224,576]{1,0:T(8,128)(2,1)S(1)} %collective-permute-done.15), channel_id=1, source_target_pairs={{0,2},{4,0},{8,4},{12,8},{14,12},{10,14},{6,10},{2,6},{1,3},{5,1},... | collective-permute-start | bytes 774152 | tf_op jit(solution)/shard_map/ppermute | solution.py:48
  77.6 6.8 %collective-permute-start.17 = (bf16[2,128,576]{1,0,2:T(2,128)(2,1)S(1)}, bf16[2,128,576]{1,0,2:T(2,128)(2,1)S(1)}, u32[]{:S(2)}, u32[]{:S(2)}) collective-permute-start(bf16[2,128,576]{1,0,2:T(2,128)(2,1)S(1)} %fusion.23), channel_id=1, source_target_pairs={{0,16},{16,0},{1,17},{17,1},{2,18},{18,2},{3,19},{19,3},{4,20},{20... | collective-permute-start | bytes 884744 | tf_op jit(solution)/shard_map/ppermute | solution.py:152
  85.2 5.1 %collective-permute-start.18 = (bf16[2,128,256]{1,0,2:T(2,128)(2,1)S(1)}, bf16[2,128,256]{1,0,2:T(2,128)(2,1)S(1)}, u32[]{:S(2)}, u32[]{:S(2)}) collective-permute-start(bf16[2,128,256]{1,0,2:T(2,128)(2,1)S(1)} %pad_maximum_fusion.7), channel_id=1, source_target_pairs={{0,4},{4,8},{8,12},{12,14},{14,10},{10,6},{6,2},{2,0},{1,5},{5,9},... | collective-permute-start | bytes 393224 | tf_op jit(solution)/shard_map/ppermute | solution.py:171
  86.8 6.0 %collective-permute-start.22 = (bf16[2,128,256]{1,0,2:T(2,128)(2,1)S(1)}, bf16[2,128,256]{1,0,2:T(2,128)(2,1)S(1)}, u32[]{:S(2)}, u32[]{:S(2)}) collective-permute-start(bf16[2,128,256]{1,0,2:T(2,128)(2,1)S(1)} %pad_maximum_fusion.7), channel_id=1, source_target_pairs={{0,2},{4,0},{8,4},{12,8},{14,12},{10,14},{6,10},{2,6},{1,3},{5,1},... | collective-permute-start | bytes 393224 | tf_op jit(solution)/shard_map/ppermute | solution.py:174
  90.3 5.7 %collective-permute-start.19 = (bf16[2,128,256]{1,0,2:T(2,128)(2,1)S(1)}, bf16[2,128,256]{1,0,2:T(2,128)(2,1)S(1)}, u32[]{:S(2)}, u32[]{:S(2)}) collective-permute-start(bf16[2,128,256]{1,0,2:T(2,128)(2,1)S(1)} %collective-permute-done.18), channel_id=1, source_target_pairs={{0,4},{4,8},{8,12},{12,14},{14,10},{10,6},{6,2},{2,0},{1,5},{5,9},... | collective-permute-start | bytes 393224 | tf_op jit(solution)/shard_map/ppermute | solution.py:171
  92.8 7.2 %collective-permute-start.23 = (bf16[2,128,256]{1,0,2:T(2,128)(2,1)S(1)}, bf16[2,128,256]{1,0,2:T(2,128)(2,1)S(1)}, u32[]{:S(2)}, u32[]{:S(2)}) collective-permute-start(bf16[2,128,256]{1,0,2:T(2,128)(2,1)S(1)} %collective-permute-done.22), channel_id=1, source_target_pairs={{0,2},{4,0},{8,4},{12,8},{14,12},{10,14},{6,10},{2,6},{1,3},{5,1},... | collective-permute-start | bytes 393224 | tf_op jit(solution)/shard_map/ppermute | solution.py:174
  96.0 5.4 %collective-permute-start.20 = (bf16[2,128,256]{1,0,2:T(2,128)(2,1)S(1)}, bf16[2,128,256]{1,0,2:T(2,128)(2,1)S(1)}, u32[]{:S(2)}, u32[]{:S(2)}) collective-permute-start(bf16[2,128,256]{1,0,2:T(2,128)(2,1)S(1)} %collective-permute-done.19), channel_id=1, source_target_pairs={{0,4},{4,8},{8,12},{12,14},{14,10},{10,6},{6,2},{2,0},{1,5},{5,9},... | collective-permute-start | bytes 393224 | tf_op jit(solution)/shard_map/ppermute | solution.py:171
  100.0 5.0 %collective-permute-start.24 = (bf16[2,128,256]{1,0,2:T(2,128)(2,1)S(1)}, bf16[2,128,256]{1,0,2:T(2,128)(2,1)S(1)}, u32[]{:S(2)}, u32[]{:S(2)}) collective-permute-start(bf16[2,128,256]{1,0,2:T(2,128)(2,1)S(1)} %collective-permute-done.23), channel_id=1, source_target_pairs={{0,2},{4,0},{8,4},{12,8},{14,12},{10,14},{6,10},{2,6},{1,3},{5,1},... | collective-permute-start | bytes 393224 | tf_op jit(solution)/shard_map/ppermute | solution.py:174
  101.4 5.0 %collective-permute-start.21 = (bf16[2,128,256]{1,0,2:T(2,128)(2,1)S(1)}, bf16[2,128,256]{1,0,2:T(2,128)(2,1)S(1)}, u32[]{:S(2)}, u32[]{:S(2)}) collective-permute-start(bf16[2,128,256]{1,0,2:T(2,128)(2,1)S(1)} %collective-permute-done.20), channel_id=1, source_target_pairs={{0,4},{4,8},{8,12},{12,14},{14,10},{10,6},{6,2},{2,0},{1,5},{5,9},... | collective-permute-start | bytes 393224 | tf_op jit(solution)/shard_map/ppermute | solution.py:171
  (5 other events, 14.6 us)

commit v18 on v17

--- a/solution.py
+++ b/solution.py
@@ -165,15 +165,16 @@
             position[d] = i
         forward = [(order[i], order[(i + 1) % row_count]) for i in range(row_count)]
         backward = [(order[i], order[(i - 1) % row_count]) for i in range(row_count)]
+        across = [(order[i], order[(i + row_count // 2) % row_count]) for i in range(row_count)]
+        opposite = lax.ppermute(pairs, "row", across)
         ahead, behind = pairs, pairs
         ahead_parts, behind_parts = [], []
-        for step in range(1, row_count // 2 + 1):
+        for step in range(1, row_count // 2):
             ahead = lax.ppermute(ahead, "row", forward)
+            behind = lax.ppermute(behind, "row", backward)
             ahead_parts.append(ahead)
-            if step < row_count // 2:
-                behind = lax.ppermute(behind, "row", backward)
-                behind_parts.append(behind)
-        gathered = jnp.stack([pairs] + ahead_parts + behind_parts)
+            behind_parts.append(behind)
+        gathered = jnp.stack([pairs] + ahead_parts + [opposite] + behind_parts)
         table = jnp.array(position, dtype=jnp.int32)
         delta = (table[here] - table) % row_count
         owner_slot = jnp.where(delta <= row_count // 2, delta, row_count // 2 + row_count - delta)

time: 118 us -> 119 us (level)
  starting transfers between devices: 25.5 us -> 30 us
  waiting for transfers between devices: 36.2 us -> 32.7 us
    ppermute x0 -> x1, starting transfers between devices: none -> 3.47 us  [shards(): opposite = lax.ppermute(pairs, 'row', across)]
    ppermute x3, starting transfers between devices: 1.86 us -> 4.61 us  [shards(): behind = lax.ppermute(behind, 'row', backward)]
    ppermute x4 -> x3, waiting for transfers between devices: 6.49 us -> 4.05 us  [shards(): ahead = lax.ppermute(ahead, 'row', forward)]
    ppermute x4 -> x3, starting transfers between devices: 6 us -> 4.25 us  [shards(): ahead = lax.ppermute(ahead, 'row', forward)]
  transfers between devices with their start and end apart: 25 -> 25, of which waited for: 16 -> 15; matrix products, arithmetic and copies ran while one was open for 28% -> 27% of each run, Pallas kernels for 0% -> 0%
where the time goes in v18:
time: 119 us
  waiting for transfers between devices  32.7 us (27%)
  local copies, waits for them, and re-layouts  32.2 us (27%)
  starting transfers between devices  30 us (25%)
  other arithmetic  16.4 us (14%)
  matrix products  6.81 us (6%)
    ppermute x7, waiting for transfers between devices, gather_rows(): ahead = lax.ppermute(ahead, 'row', forward)  21.2 us
    ppermute x7, starting transfers between devices, gather_rows(): ahead = lax.ppermute(ahead, 'row', forward)  12.5 us
    unnamed x43, local copies, waits for them, and re-layouts  10.3 us
    ppermute x1, waiting for transfers between devices, shards(): returned = lax.ppermute(result[passages:], 'groups', SWAP)  5.63 us
    ppermute x3, starting transfers between devices, shards(): behind = lax.ppermute(behind, 'row', backward)  4.61 us
    ppermute x3, starting transfers between devices, shards(): ahead = lax.ppermute(ahead, 'row', forward)  4.25 us
    ppermute x3, waiting for transfers between devices, shards(): ahead = lax.ppermute(ahead, 'row', forward)  4.05 us
    gather x1, local copies, waits for them, and re-layouts, gather_rows(): jnp.stack(behind_parts)[behind_pick]  3.9 us
  transfers between devices with their start and end apart: 25, of which 15 were waited for; matrix products, arithmetic and copies ran while one was open for 27% of the time, Pallas kernels for 0%

profile of v18, /device:TPU:0, one launch (start us, length us, event | category | flops | bytes accessed | tf_op | source)
XLA Modules:
  0.0 118.9 jit_solution(10919495514993286966)
XLA Ops:
  2.7 3.1 %collective-permute-start.1 = (bf16[224,576]{1,0:T(8,128)(2,1)S(1)}, bf16[224,576]{1,0:T(8,128)(2,1)S(1)}, u32[]{:S(2)}, u32[]{:S(2)}) collective-permute-start(bf16[224,576]{1,0:T(8,128)(2,1)S(1)} %pad_maximum_fusion.5), channel_id=1, source_target_pairs={{0,4},{4,8},{8,12},{12,14},{14,10},{10,6},{6,2},{2,0},{1,5},{5,9},... | collective-permute-start | bytes 774152 | tf_op jit(solution)/shard_map/ppermute | solution.py:47
  10.3 2.2 %collective-permute-done.1 = bf16[224,576]{1,0:T(8,128)(2,1)S(1)} collective-permute-done((bf16[224,576]{1,0:T(8,128)(2,1)S(1)}, bf16[224,576]{1,0:T(8,128)(2,1)S(1)}, u32[]{:S(2)}, u32[]{:S(2)}) %collective-permute-start.1) | collective-permute-done | bytes 258080 | tf_op jit(solution)/shard_map/ppermute | solution.py:47
  12.5 1.8 %collective-permute-start.2 = (bf16[2,128,1792]{2,1,0:T(8,128)(2,1)S(1)}, bf16[2,128,1792]{2,1,0:T(8,128)(2,1)}, u32[]{:S(2)}, u32[]{:S(2)}) collective-permute-start(bf16[2,128,1792]{2,1,0:T(8,128)(2,1)S(1)} %copy-done.1), channel_id=1, source_target_pairs={{0,16},{16,0},{1,17},{17,1},{2,18},{18,2},{3,19},{19,3},{4,20},{20... | collective-permute-start | bytes 2752520 | tf_op jit(solution)/shard_map/ppermute | solution.py:119
  14.3 1.6 %collective-permute-start.4 = (bf16[224,576]{1,0:T(8,128)(2,1)S(1)}, bf16[224,576]{1,0:T(8,128)(2,1)S(1)}, u32[]{:S(2)}, u32[]{:S(2)}) collective-permute-start(bf16[224,576]{1,0:T(8,128)(2,1)S(1)} %collective-permute-done.1), channel_id=1, source_target_pairs={{0,4},{4,8},{8,12},{12,14},{14,10},{10,6},{6,2},{2,0},{1,5},{5,9},... | collective-permute-start | bytes 774152 | tf_op jit(solution)/shard_map/ppermute | solution.py:47
  17.8 3.9 %collective-permute-done.4 = bf16[224,576]{1,0:T(8,128)(2,1)S(1)} collective-permute-done((bf16[224,576]{1,0:T(8,128)(2,1)S(1)}, bf16[224,576]{1,0:T(8,128)(2,1)S(1)}, u32[]{:S(2)}, u32[]{:S(2)}) %collective-permute-start.4) | collective-permute-done | bytes 258080 | tf_op jit(solution)/shard_map/ppermute | solution.py:47
  21.7 1.6 %collective-permute-start.5 = (bf16[224,576]{1,0:T(8,128)(2,1)S(1)}, bf16[224,576]{1,0:T(8,128)(2,1)S(1)}, u32[]{:S(2)}, u32[]{:S(2)}) collective-permute-start(bf16[224,576]{1,0:T(8,128)(2,1)S(1)} %collective-permute-done.4), channel_id=1, source_target_pairs={{0,4},{4,8},{8,12},{12,14},{14,10},{10,6},{6,2},{2,0},{1,5},{5,9},... | collective-permute-start | bytes 774152 | tf_op jit(solution)/shard_map/ppermute | solution.py:47
  25.2 3.3 %collective-permute-done.5 = bf16[224,576]{1,0:T(8,128)(2,1)S(1)} collective-permute-done((bf16[224,576]{1,0:T(8,128)(2,1)S(1)}, bf16[224,576]{1,0:T(8,128)(2,1)S(1)}, u32[]{:S(2)}, u32[]{:S(2)}) %collective-permute-start.5) | collective-permute-done | bytes 258080 | tf_op jit(solution)/shard_map/ppermute | solution.py:47
  28.5 1.6 %collective-permute-start.6 = (bf16[224,576]{1,0:T(8,128)(2,1)S(1)}, bf16[224,576]{1,0:T(8,128)(2,1)S(1)}, u32[]{:S(2)}, u32[]{:S(2)}) collective-permute-start(bf16[224,576]{1,0:T(8,128)(2,1)S(1)} %collective-permute-done.5), channel_id=1, source_target_pairs={{0,4},{4,8},{8,12},{12,14},{14,10},{10,6},{6,2},{2,0},{1,5},{5,9},... | collective-permute-start | bytes 774152 | tf_op jit(solution)/shard_map/ppermute | solution.py:47
  32.3 2.0 %maximum_select_fusion = bf16[2,128,3584]{2,1,0:T(8,128)(2,1)S(1)} fusion(bf16[2,128,1792]{2,1,0:T(8,128)(2,1)} %collective-permute-done, bf16[2,128,1792]{2,1,0:T(8,128)(2,1)S(1)} %copy-done.1, pred[]{:T(512)S(6)} %eq.14), kind=kLoop, calls=%fused_computation.14 | loop fusion | flops 8257536 | bytes 3670017 | tf_op jit(solution)/shard_map/jit(_where)/select_n | solution.py:121
  34.3 1.8 %collective-permute-done.6 = bf16[224,576]{1,0:T(8,128)(2,1)S(1)} collective-permute-done((bf16[224,576]{1,0:T(8,128)(2,1)S(1)}, bf16[224,576]{1,0:T(8,128)(2,1)S(1)}, u32[]{:S(2)}, u32[]{:S(2)}) %collective-permute-start.6) | collective-permute-done | bytes 258080 | tf_op jit(solution)/shard_map/ppermute | solution.py:47
  36.1 1.6 %collective-permute-start.7 = (bf16[224,576]{1,0:T(8,128)(2,1)S(1)}, bf16[224,576]{1,0:T(8,128)(2,1)S(1)}, u32[]{:S(2)}, u32[]{:S(2)}) collective-permute-start(bf16[224,576]{1,0:T(8,128)(2,1)S(1)} %collective-permute-done.6), channel_id=1, source_target_pairs={{0,4},{4,8},{8,12},{12,14},{14,10},{10,6},{6,2},{2,0},{1,5},{5,9},... | collective-permute-start | bytes 774152 | tf_op jit(solution)/shard_map/ppermute | solution.py:47
  39.6 3.1 %collective-permute-done.7 = bf16[224,576]{1,0:T(8,128)(2,1)S(1)} collective-permute-done((bf16[224,576]{1,0:T(8,128)(2,1)S(1)}, bf16[224,576]{1,0:T(8,128)(2,1)S(1)}, u32[]{:S(2)}, u32[]{:S(2)}) %collective-permute-start.7) | collective-permute-done | bytes 258080 | tf_op jit(solution)/shard_map/ppermute | solution.py:47
  42.7 1.6 %collective-permute-start.8 = (bf16[224,576]{1,0:T(8,128)(2,1)S(1)}, bf16[224,576]{1,0:T(8,128)(2,1)S(1)}, u32[]{:S(2)}, u32[]{:S(2)}) collective-permute-start(bf16[224,576]{1,0:T(8,128)(2,1)S(1)} %collective-permute-done.7), channel_id=1, source_target_pairs={{0,4},{4,8},{8,12},{12,14},{14,10},{10,6},{6,2},{2,0},{1,5},{5,9},... | collective-permute-start | bytes 774152 | tf_op jit(solution)/shard_map/ppermute | solution.py:47
  46.5 4.0 %collective-permute-done.8 = bf16[224,576]{1,0:T(8,128)(2,1)S(1)} collective-permute-done((bf16[224,576]{1,0:T(8,128)(2,1)S(1)}, bf16[224,576]{1,0:T(8,128)(2,1)S(1)}, u32[]{:S(2)}, u32[]{:S(2)}) %collective-permute-start.8) | collective-permute-done | bytes 258080 | tf_op jit(solution)/shard_map/ppermute | solution.py:47
  50.4 1.6 %collective-permute-start.9 = (bf16[224,576]{1,0:T(8,128)(2,1)S(1)}, bf16[224,576]{1,0:T(8,128)(2,1)S(1)}, u32[]{:S(2)}, u32[]{:S(2)}) collective-permute-start(bf16[224,576]{1,0:T(8,128)(2,1)S(1)} %collective-permute-done.8), channel_id=1, source_target_pairs={{0,4},{4,8},{8,12},{12,14},{14,10},{10,6},{6,2},{2,0},{1,5},{5,9},... | collective-permute-start | bytes 774152 | tf_op jit(solution)/shard_map/ppermute | solution.py:47
  54.1 2.9 %collective-permute-done.9 = bf16[224,576]{1,0:T(8,128)(2,1)S(1)} collective-permute-done((bf16[224,576]{1,0:T(8,128)(2,1)S(1)}, bf16[224,576]{1,0:T(8,128)(2,1)S(1)}, u32[]{:S(2)}, u32[]{:S(2)}) %collective-permute-start.9) | collective-permute-done | bytes 258080 | tf_op jit(solution)/shard_map/ppermute | solution.py:47
  57.8 3.9 %gather_fusion = bf16[8,224,576]{2,1,0:T(8,128)(2,1)} fusion(bf16[8,224,576]{2,1,0:T(8,128)(2,1)} %bitcast_dynamic-update-slice_fusion.8, s32[1024]{0:T(1024)S(1)} %get-tuple-element.30), kind=kCustom, calls=%fused_computation | custom fusion | bytes 4128800 | tf_op jit(solution)/shard_map/gather | solution.py:56
  62.5 3.9 %gather_fusion.1 = bf16[8,224,576]{2,1,0:T(8,128)(2,1)} fusion(bf16[8,224,576]{2,1,0:T(8,128)(2,1)} %bitcast_dynamic-update-slice_fusion, s32[1024]{0:T(1024)S(1)} %get-tuple-element.29), kind=kCustom, calls=%fused_computation.1 | custom fusion | bytes 4128800 | tf_op jit(solution)/shard_map/gather | solution.py:56
  66.4 2.8 %pad_maximum_fusion = bf16[8,448,576]{2,1,0:T(8,128)(2,1)S(1)} fusion(bf16[8,224,576]{2,1,0:T(8,128)(2,1)} %gather_fusion.1, bf16[8,224,576]{2,1,0:T(8,128)(2,1)} %gather_fusion), kind=kLoop, calls=%fused_computation.12 | loop fusion | flops 8257536 | bytes 8257536 | tf_op jit(solution)/shard_map/concatenate | solution.py:55
  69.2 1.9 %maximum_select_fusion.1 = bf16[2,128,3584]{2,1,0:T(8,128)(2,1)S(1)} fusion(bf16[2,128,1792]{2,1,0:T(8,128)(2,1)S(1)} %collective-permute-done.3, bf16[2,128,1792]{2,1,0:T(8,128)(2,1)} %collective-permute-done.2, pred[]{:T(512)S(6)} %eq.14), kind=kLoop, calls=%fused_computation.15 | loop fusion | flops 8257536 | bytes 3670017 | tf_op jit(solution)/shard_map/jit(_where)/select_n | solution.py:126
  73.0 2.4 %convolution_add_fusion = f32[512,576]{0,1:T(8,128)S(1)} fusion(bf16[512,3584]{1,0:T(8,128)(2,1)S(1)} %bitcast.140, bf16[3584,576]{1,0:T(8,128)(2,1)S(1)} %bitcast.135, f32[576]{0:T(1024)S(1)} %maximum_select_fusion.2), kind=kOutput, calls=%fused_computation.30 | convolution fusion | flops 2114224128 | bytes 8980736 | tf_op jit(solution)/shard_map/dot_general | solution.py:141
  78.7 5.6 %collective-permute-done.17 = bf16[2,128,576]{1,0,2:T(2,128)(2,1)S(1)} collective-permute-done((bf16[2,128,576]{1,0,2:T(2,128)(2,1)S(1)}, bf16[2,128,576]{1,0,2:T(2,128)(2,1)S(1)}, u32[]{:S(2)}, u32[]{:S(2)}) %collective-permute-start.17) | collective-permute-done | bytes 294944 | tf_op jit(solution)/shard_map/ppermute | solution.py:152
  85.2 1.6 %collective-permute-start.18 = (bf16[2,128,256]{1,0,2:T(2,128)(2,1)S(1)}, bf16[2,128,256]{1,0,2:T(2,128)(2,1)S(1)}, u32[]{:S(2)}, u32[]{:S(2)}) collective-permute-start(bf16[2,128,256]{1,0,2:T(2,128)(2,1)S(1)} %pad_maximum_fusion.7), channel_id=1, source_target_pairs={{0,4},{4,8},{8,12},{12,14},{14,10},{10,6},{6,2},{2,0},{1,5},{5,9},... | collective-permute-start | bytes 393224 | tf_op jit(solution)/shard_map/ppermute | solution.py:173
  88.2 2.0 %collective-permute-done.18 = bf16[2,128,256]{1,0,2:T(2,128)(2,1)S(1)} collective-permute-done((bf16[2,128,256]{1,0,2:T(2,128)(2,1)S(1)}, bf16[2,128,256]{1,0,2:T(2,128)(2,1)S(1)}, u32[]{:S(2)}, u32[]{:S(2)}) %collective-permute-start.18) | collective-permute-done | bytes 131104 | tf_op jit(solution)/shard_map/ppermute | solution.py:173
  90.2 2.6 %collective-permute-start.19 = (bf16[2,128,256]{1,0,2:T(2,128)(2,1)S(1)}, bf16[2,128,256]{1,0,2:T(2,128)(2,1)S(1)}, u32[]{:S(2)}, u32[]{:S(2)}) collective-permute-start(bf16[2,128,256]{1,0,2:T(2,128)(2,1)S(1)} %collective-permute-done.18), channel_id=1, source_target_pairs={{0,4},{4,8},{8,12},{12,14},{14,10},{10,6},{6,2},{2,0},{1,5},{5,9},... | collective-permute-start | bytes 393224 | tf_op jit(solution)/shard_map/ppermute | solution.py:173
  93.5 3.5 %collective-permute-start.21 = (bf16[2,128,256]{1,0,2:T(2,128)(2,1)S(1)}, bf16[2,128,256]{1,0,2:T(2,128)(2,1)S(1)}, u32[]{:S(2)}, u32[]{:S(2)}) collective-permute-start(bf16[2,128,256]{1,0,2:T(2,128)(2,1)S(1)} %pad_maximum_fusion.7), channel_id=1, source_target_pairs={{0,14},{4,10},{8,6},{12,2},{14,0},{10,4},{6,8},{2,12},{1,15},{5,11... | collective-permute-start | bytes 393224 | tf_op jit(solution)/shard_map/ppermute | solution.py:169
  97.0 2.0 %collective-permute-start.23 = (bf16[2,128,256]{1,0,2:T(2,128)(2,1)S(1)}, bf16[2,128,256]{1,0,2:T(2,128)(2,1)S(1)}, u32[]{:S(2)}, u32[]{:S(2)}) collective-permute-start(bf16[2,128,256]{1,0,2:T(2,128)(2,1)S(1)} %collective-permute-done.22), channel_id=1, source_target_pairs={{0,2},{4,0},{8,4},{12,8},{14,12},{10,14},{6,10},{2,6},{1,3},{5,1},... | collective-permute-start | bytes 393224 | tf_op jit(solution)/shard_map/ppermute | solution.py:174
  99.4 1.8 %copy.52 = bf16[2,2,64,7,128]{4,2,3,1,0:T(8,128)(2,1)S(1)} copy(bf16[2,2,64,7,128]{2,1,0,4,3:T(2,128)(2,1)S(1)} %reshape.378) | data formatting | bytes 917504 | tf_op jit(solution)/shard_map/reshape | solution.py:213
  102.2 2.1 %collective-permute-start.24 = (bf16[2,128,256]{1,0,2:T(2,128)(2,1)S(1)}, bf16[2,128,256]{1,0,2:T(2,128)(2,1)S(1)}, u32[]{:S(2)}, u32[]{:S(2)}) collective-permute-start(bf16[2,128,256]{1,0,2:T(2,128)(2,1)S(1)} %collective-permute-done.23), channel_id=1, source_target_pairs={{0,2},{4,0},{8,4},{12,8},{14,12},{10,14},{6,10},{2,6},{1,3},{5,1},... | collective-permute-start | bytes 393224 | tf_op jit(solution)/shard_map/ppermute | solution.py:174
  104.4 2.0 %collective-permute-done.20 = bf16[2,128,256]{1,0,2:T(2,128)(2,1)S(1)} collective-permute-done((bf16[2,128,256]{1,0,2:T(2,128)(2,1)S(1)}, bf16[2,128,256]{1,0,2:T(2,128)(2,1)S(1)}, u32[]{:S(2)}, u32[]{:S(2)}) %collective-permute-start.20) | collective-permute-done | bytes 131104 | tf_op jit(solution)/shard_map/ppermute | solution.py:173
  108.4 1.4 %gather_fusion.4 = bf16[12,64,256]{2,1,0:T(8,128)(2,1)} fusion(bf16[2,16,64,256]{3,2,0,1:T(8,128)(2,1)S(1)} %bitcast.132, s32[12]{0:T(128)S(1)} %reshape.346), kind=kCustom, calls=%fused_computation.4 | custom fusion | bytes 786528 | tf_op jit(solution)/shard_map/gather | solution.py:199
  117.6 1.3 %convert_element_type.60 = bf16[2,128,896]{2,1,0:T(8,128)(2,1)} reshape(bf16[2,2,64,7,128]{4,3,2,1,0:T(8,128)(2,1)S(1)} %copy.57) | data formatting | bytes 917504 | tf_op jit(solution)/shard_map/convert_element_type | solution.py:275
  (164 shorter events, 39.8 us)
Async XLA Ops:
  0.0 9.8 %copy-start = (s32[2,2,2]{2,1,0:T(2,128)S(1)}, s32[2,2,2]{2,1,0:T(2,128)}, u32[]{:S(2)}) copy-start(s32[2,2,2]{2,1,0:T(2,128)} %param.21) | copy-start | bytes 100
  2.4 6.6 %copy-start.9 = (s32[8]{0:T(128)S(1)}, s32[8]{0:T(128)}, u32[]{:S(2)}) copy-start(s32[8]{0:T(128)} %constant.152) | copy-start | bytes 100
  2.4 7.2 %copy-start.7 = (f32[128]{0:T(128)S(1)}, f32[128]{0:T(128)}, u32[]{:S(2)}) copy-start(f32[128]{0:T(128)} %param.19) | copy-start | bytes 1540
  2.4 7.3 %copy-start.5 = (f32[896]{0:T(1024)S(1)}, f32[896]{0:T(1024)}, u32[]{:S(2)}) copy-start(f32[896]{0:T(1024)} %param.15) | copy-start | bytes 10756
  2.4 7.3 %copy-start.8 = (f32[128]{0:T(128)S(1)}, f32[128]{0:T(128)}, u32[]{:S(2)}) copy-start(f32[128]{0:T(128)} %param.17) | copy-start | bytes 1540
  2.5 7.6 %copy-start.6 = (s32[2,16,14,2]{1,3,2,0:T(2,128)S(1)}, s32[2,16,14,2]{1,3,2,0:T(2,128)}, u32[]{:S(2)}) copy-start(s32[2,16,14,2]{1,3,2,0:T(2,128)} %param.20) | copy-start | bytes 10756
  2.5 7.7 %slice-start = ((f32[896]{0:T(1024)}), f32[512]{0:T(512)S(1)}, s32[]{:S(2)}) async-start(f32[896]{0:T(1024)} %param.15), calls=%async_computation | async-start | bytes 4096 | tf_op jit(solution)/shard_map/slice | solution.py:113
  2.7 9.8 %collective-permute-start.1 = (bf16[224,576]{1,0:T(8,128)(2,1)S(1)}, bf16[224,576]{1,0:T(8,128)(2,1)S(1)}, u32[]{:S(2)}, u32[]{:S(2)}) collective-permute-start(bf16[224,576]{1,0:T(8,128)(2,1)S(1)} %pad_maximum_fusion.5), channel_id=1, source_target_pairs={{0,4},{4,8},{8,12},{12,14},{14,10},{10,6},{6,2},{2,0},{1,5},{5,9},... | collective-permute-start | bytes 774152 | tf_op jit(solution)/shard_map/ppermute | solution.py:47
  5.9 9.9 %collective-permute-start.10 = (bf16[224,576]{1,0:T(8,128)(2,1)S(1)}, bf16[224,576]{1,0:T(8,128)(2,1)S(1)}, u32[]{:S(2)}, u32[]{:S(2)}) collective-permute-start(bf16[224,576]{1,0:T(8,128)(2,1)S(1)} %pad_maximum_fusion.6), channel_id=1, source_target_pairs={{0,2},{4,0},{8,4},{12,8},{14,12},{10,14},{6,10},{2,6},{1,3},{5,1},... | collective-permute-start | bytes 774152 | tf_op jit(solution)/shard_map/ppermute | solution.py:48
  6.0 26.4 %collective-permute-start = (bf16[2,128,1792]{2,1,0:T(8,128)(2,1)S(1)}, bf16[2,128,1792]{2,1,0:T(8,128)(2,1)}, u32[]{:S(2)}, u32[]{:S(2)}) collective-permute-start(bf16[2,128,1792]{2,1,0:T(8,128)(2,1)S(1)} %copy-done.1), channel_id=1, source_target_pairs={{0,1},{1,0},{2,3},{3,2},{4,5},{5,4},{6,7},{7,6},{8,9},{9,8},{10,11... | collective-permute-start | bytes 2752520 | tf_op jit(solution)/shard_map/ppermute | solution.py:117
  12.5 27.1 %collective-permute-start.2 = (bf16[2,128,1792]{2,1,0:T(8,128)(2,1)S(1)}, bf16[2,128,1792]{2,1,0:T(8,128)(2,1)}, u32[]{:S(2)}, u32[]{:S(2)}) collective-permute-start(bf16[2,128,1792]{2,1,0:T(8,128)(2,1)S(1)} %copy-done.1), channel_id=1, source_target_pairs={{0,16},{16,0},{1,17},{17,1},{2,18},{18,2},{3,19},{19,3},{4,20},{20... | collective-permute-start | bytes 2752520 | tf_op jit(solution)/shard_map/ppermute | solution.py:119
  14.3 7.4 %collective-permute-start.4 = (bf16[224,576]{1,0:T(8,128)(2,1)S(1)}, bf16[224,576]{1,0:T(8,128)(2,1)S(1)}, u32[]{:S(2)}, u32[]{:S(2)}) collective-permute-start(bf16[224,576]{1,0:T(8,128)(2,1)S(1)} %collective-permute-done.1), channel_id=1, source_target_pairs={{0,4},{4,8},{8,12},{12,14},{14,10},{10,6},{6,2},{2,0},{1,5},{5,9},... | collective-permute-start | bytes 774152 | tf_op jit(solution)/shard_map/ppermute | solution.py:47
  15.8 7.4 %collective-permute-start.11 = (bf16[224,576]{1,0:T(8,128)(2,1)S(1)}, bf16[224,576]{1,0:T(8,128)(2,1)S(1)}, u32[]{:S(2)}, u32[]{:S(2)}) collective-permute-start(bf16[224,576]{1,0:T(8,128)(2,1)S(1)} %collective-permute-done.10), channel_id=1, source_target_pairs={{0,2},{4,0},{8,4},{12,8},{14,12},{10,14},{6,10},{2,6},{1,3},{5,1},... | collective-permute-start | bytes 774152 | tf_op jit(solution)/shard_map/ppermute | solution.py:48
  21.7 6.9 %collective-permute-start.5 = (bf16[224,576]{1,0:T(8,128)(2,1)S(1)}, bf16[224,576]{1,0:T(8,128)(2,1)S(1)}, u32[]{:S(2)}, u32[]{:S(2)}) collective-permute-start(bf16[224,576]{1,0:T(8,128)(2,1)S(1)} %collective-permute-done.4), channel_id=1, source_target_pairs={{0,4},{4,8},{8,12},{12,14},{14,10},{10,6},{6,2},{2,0},{1,5},{5,9},... | collective-permute-start | bytes 774152 | tf_op jit(solution)/shard_map/ppermute | solution.py:47
  23.3 7.1 %collective-permute-start.12 = (bf16[224,576]{1,0:T(8,128)(2,1)S(1)}, bf16[224,576]{1,0:T(8,128)(2,1)S(1)}, u32[]{:S(2)}, u32[]{:S(2)}) collective-permute-start(bf16[224,576]{1,0:T(8,128)(2,1)S(1)} %collective-permute-done.11), channel_id=1, source_target_pairs={{0,2},{4,0},{8,4},{12,8},{14,12},{10,14},{6,10},{2,6},{1,3},{5,1},... | collective-permute-start | bytes 774152 | tf_op jit(solution)/shard_map/ppermute | solution.py:48
  28.5 7.5 %collective-permute-start.6 = (bf16[224,576]{1,0:T(8,128)(2,1)S(1)}, bf16[224,576]{1,0:T(8,128)(2,1)S(1)}, u32[]{:S(2)}, u32[]{:S(2)}) collective-permute-start(bf16[224,576]{1,0:T(8,128)(2,1)S(1)} %collective-permute-done.5), channel_id=1, source_target_pairs={{0,4},{4,8},{8,12},{12,14},{14,10},{10,6},{6,2},{2,0},{1,5},{5,9},... | collective-permute-start | bytes 774152 | tf_op jit(solution)/shard_map/ppermute | solution.py:47
  30.4 8.0 %collective-permute-start.13 = (bf16[224,576]{1,0:T(8,128)(2,1)S(1)}, bf16[224,576]{1,0:T(8,128)(2,1)S(1)}, u32[]{:S(2)}, u32[]{:S(2)}) collective-permute-start(bf16[224,576]{1,0:T(8,128)(2,1)S(1)} %collective-permute-done.12), channel_id=1, source_target_pairs={{0,2},{4,0},{8,4},{12,8},{14,12},{10,14},{6,10},{2,6},{1,3},{5,1},... | collective-permute-start | bytes 774152 | tf_op jit(solution)/shard_map/ppermute | solution.py:48
  36.1 6.6 %collective-permute-start.7 = (bf16[224,576]{1,0:T(8,128)(2,1)S(1)}, bf16[224,576]{1,0:T(8,128)(2,1)S(1)}, u32[]{:S(2)}, u32[]{:S(2)}) collective-permute-start(bf16[224,576]{1,0:T(8,128)(2,1)S(1)} %collective-permute-done.6), channel_id=1, source_target_pairs={{0,4},{4,8},{8,12},{12,14},{14,10},{10,6},{6,2},{2,0},{1,5},{5,9},... | collective-permute-start | bytes 774152 | tf_op jit(solution)/shard_map/ppermute | solution.py:47
  38.4 6.9 %collective-permute-start.14 = (bf16[224,576]{1,0:T(8,128)(2,1)S(1)}, bf16[224,576]{1,0:T(8,128)(2,1)S(1)}, u32[]{:S(2)}, u32[]{:S(2)}) collective-permute-start(bf16[224,576]{1,0:T(8,128)(2,1)S(1)} %collective-permute-done.13), channel_id=1, source_target_pairs={{0,2},{4,0},{8,4},{12,8},{14,12},{10,14},{6,10},{2,6},{1,3},{5,1},... | collective-permute-start | bytes 774152 | tf_op jit(solution)/shard_map/ppermute | solution.py:48
  39.6 29.6 %collective-permute-start.3 = (bf16[2,128,1792]{2,1,0:T(8,128)(2,1)}, bf16[2,128,1792]{2,1,0:T(8,128)(2,1)S(1)}, u32[]{:S(2)}, u32[]{:S(2)}) collective-permute-start(bf16[2,128,1792]{2,1,0:T(8,128)(2,1)} %collective-permute-done.2), channel_id=1, source_target_pairs={{0,1},{1,0},{2,3},{3,2},{4,5},{5,4},{6,7},{7,6},{8,9},{9,8},{10,11... | collective-permute-start | bytes 2752520 | tf_op jit(solution)/shard_map/ppermute | solution.py:120
  42.7 7.7 %collective-permute-start.8 = (bf16[224,576]{1,0:T(8,128)(2,1)S(1)}, bf16[224,576]{1,0:T(8,128)(2,1)S(1)}, u32[]{:S(2)}, u32[]{:S(2)}) collective-permute-start(bf16[224,576]{1,0:T(8,128)(2,1)S(1)} %collective-permute-done.7), channel_id=1, source_target_pairs={{0,4},{4,8},{8,12},{12,14},{14,10},{10,6},{6,2},{2,0},{1,5},{5,9},... | collective-permute-start | bytes 774152 | tf_op jit(solution)/shard_map/ppermute | solution.py:47
  45.3 7.7 %collective-permute-start.15 = (bf16[224,576]{1,0:T(8,128)(2,1)S(1)}, bf16[224,576]{1,0:T(8,128)(2,1)S(1)}, u32[]{:S(2)}, u32[]{:S(2)}) collective-permute-start(bf16[224,576]{1,0:T(8,128)(2,1)S(1)} %collective-permute-done.14), channel_id=1, source_target_pairs={{0,2},{4,0},{8,4},{12,8},{14,12},{10,14},{6,10},{2,6},{1,3},{5,1},... | collective-permute-start | bytes 774152 | tf_op jit(solution)/shard_map/ppermute | solution.py:48
  50.4 6.6 %collective-permute-start.9 = (bf16[224,576]{1,0:T(8,128)(2,1)S(1)}, bf16[224,576]{1,0:T(8,128)(2,1)S(1)}, u32[]{:S(2)}, u32[]{:S(2)}) collective-permute-start(bf16[224,576]{1,0:T(8,128)(2,1)S(1)} %collective-permute-done.8), channel_id=1, source_target_pairs={{0,4},{4,8},{8,12},{12,14},{14,10},{10,6},{6,2},{2,0},{1,5},{5,9},... | collective-permute-start | bytes 774152 | tf_op jit(solution)/shard_map/ppermute | solution.py:47
  52.9 8.8 %collective-permute-start.16 = (bf16[224,576]{1,0:T(8,128)(2,1)S(1)}, bf16[224,576]{1,0:T(8,128)(2,1)S(1)}, u32[]{:S(2)}, u32[]{:S(2)}) collective-permute-start(bf16[224,576]{1,0:T(8,128)(2,1)S(1)} %collective-permute-done.15), channel_id=1, source_target_pairs={{0,2},{4,0},{8,4},{12,8},{14,12},{10,14},{6,10},{2,6},{1,3},{5,1},... | collective-permute-start | bytes 774152 | tf_op jit(solution)/shard_map/ppermute | solution.py:48
  77.6 6.8 %collective-permute-start.17 = (bf16[2,128,576]{1,0,2:T(2,128)(2,1)S(1)}, bf16[2,128,576]{1,0,2:T(2,128)(2,1)S(1)}, u32[]{:S(2)}, u32[]{:S(2)}) collective-permute-start(bf16[2,128,576]{1,0,2:T(2,128)(2,1)S(1)} %fusion.23), channel_id=1, source_target_pairs={{0,16},{16,0},{1,17},{17,1},{2,18},{18,2},{3,19},{19,3},{4,20},{20... | collective-permute-start | bytes 884744 | tf_op jit(solution)/shard_map/ppermute | solution.py:152
  85.2 5.0 %collective-permute-start.18 = (bf16[2,128,256]{1,0,2:T(2,128)(2,1)S(1)}, bf16[2,128,256]{1,0,2:T(2,128)(2,1)S(1)}, u32[]{:S(2)}, u32[]{:S(2)}) collective-permute-start(bf16[2,128,256]{1,0,2:T(2,128)(2,1)S(1)} %pad_maximum_fusion.7), channel_id=1, source_target_pairs={{0,4},{4,8},{8,12},{12,14},{14,10},{10,6},{6,2},{2,0},{1,5},{5,9},... | collective-permute-start | bytes 393224 | tf_op jit(solution)/shard_map/ppermute | solution.py:173
  86.9 10.1 %collective-permute-start.22 = (bf16[2,128,256]{1,0,2:T(2,128)(2,1)S(1)}, bf16[2,128,256]{1,0,2:T(2,128)(2,1)S(1)}, u32[]{:S(2)}, u32[]{:S(2)}) collective-permute-start(bf16[2,128,256]{1,0,2:T(2,128)(2,1)S(1)} %pad_maximum_fusion.7), channel_id=1, source_target_pairs={{0,2},{4,0},{8,4},{12,8},{14,12},{10,14},{6,10},{2,6},{1,3},{5,1},... | collective-permute-start | bytes 393224 | tf_op jit(solution)/shard_map/ppermute | solution.py:174
  90.2 11.2 %collective-permute-start.19 = (bf16[2,128,256]{1,0,2:T(2,128)(2,1)S(1)}, bf16[2,128,256]{1,0,2:T(2,128)(2,1)S(1)}, u32[]{:S(2)}, u32[]{:S(2)}) collective-permute-start(bf16[2,128,256]{1,0,2:T(2,128)(2,1)S(1)} %collective-permute-done.18), channel_id=1, source_target_pairs={{0,4},{4,8},{8,12},{12,14},{14,10},{10,6},{6,2},{2,0},{1,5},{5,9},... | collective-permute-start | bytes 393224 | tf_op jit(solution)/shard_map/ppermute | solution.py:173
  93.5 8.1 %collective-permute-start.21 = (bf16[2,128,256]{1,0,2:T(2,128)(2,1)S(1)}, bf16[2,128,256]{1,0,2:T(2,128)(2,1)S(1)}, u32[]{:S(2)}, u32[]{:S(2)}) collective-permute-start(bf16[2,128,256]{1,0,2:T(2,128)(2,1)S(1)} %pad_maximum_fusion.7), channel_id=1, source_target_pairs={{0,14},{4,10},{8,6},{12,2},{14,0},{10,4},{6,8},{2,12},{1,15},{5,11... | collective-permute-start | bytes 393224 | tf_op jit(solution)/shard_map/ppermute | solution.py:169
  97.0 5.1 %collective-permute-start.23 = (bf16[2,128,256]{1,0,2:T(2,128)(2,1)S(1)}, bf16[2,128,256]{1,0,2:T(2,128)(2,1)S(1)}, u32[]{:S(2)}, u32[]{:S(2)}) collective-permute-start(bf16[2,128,256]{1,0,2:T(2,128)(2,1)S(1)} %collective-permute-done.22), channel_id=1, source_target_pairs={{0,2},{4,0},{8,4},{12,8},{14,12},{10,14},{6,10},{2,6},{1,3},{5,1},... | collective-permute-start | bytes 393224 | tf_op jit(solution)/shard_map/ppermute | solution.py:174
  101.4 5.0 %collective-permute-start.20 = (bf16[2,128,256]{1,0,2:T(2,128)(2,1)S(1)}, bf16[2,128,256]{1,0,2:T(2,128)(2,1)S(1)}, u32[]{:S(2)}, u32[]{:S(2)}) collective-permute-start(bf16[2,128,256]{1,0,2:T(2,128)(2,1)S(1)} %collective-permute-done.19), channel_id=1, source_target_pairs={{0,4},{4,8},{8,12},{12,14},{14,10},{10,6},{6,2},{2,0},{1,5},{5,9},... | collective-permute-start | bytes 393224 | tf_op jit(solution)/shard_map/ppermute | solution.py:173
  102.2 5.2 %collective-permute-start.24 = (bf16[2,128,256]{1,0,2:T(2,128)(2,1)S(1)}, bf16[2,128,256]{1,0,2:T(2,128)(2,1)S(1)}, u32[]{:S(2)}, u32[]{:S(2)}) collective-permute-start(bf16[2,128,256]{1,0,2:T(2,128)(2,1)S(1)} %collective-permute-done.23), channel_id=1, source_target_pairs={{0,2},{4,0},{8,4},{12,8},{14,12},{10,14},{6,10},{2,6},{1,3},{5,1},... | collective-permute-start | bytes 393224 | tf_op jit(solution)/shard_map/ppermute | solution.py:174
  (5 other events, 14.6 us)

commit v19 on v17

--- a/solution.py
+++ b/solution.py
@@ -31,10 +31,10 @@
     return [2 * z for z in range(count // 2)] + [2 * z + 1 for z in reversed(range(count // 2))]
 
 
-def gather_rows(ahead, behind, count, here):
+def gather_rows(ahead, behind, count, here, between, tie_step):
     if count != 8:
         shard = jnp.concatenate([ahead, behind], axis=0)
-        return lax.all_gather(shard, "row", axis=0, tiled=True), ahead
+        return lax.all_gather(shard, "row", axis=0, tiled=True), between(ahead)
     order = snake_order(count)
     position = [0] * count
     for i, d in enumerate(order):
@@ -43,11 +43,16 @@
     backward = [(order[i], order[(i - 1) % count]) for i in range(count)]
     half = ahead.shape[0]
     ahead_parts, behind_parts = [ahead], [behind]
-    for _ in range(count - 1):
+    tied = None
+    for step in range(1, count):
+        if step == tie_step:
+            ahead, tied = lax.optimization_barrier((ahead, tied))
         ahead = lax.ppermute(ahead, "row", forward)
         behind = lax.ppermute(behind, "row", backward)
         ahead_parts.append(ahead)
         behind_parts.append(behind)
+        if step == 1:
+            tied = between(ahead)
     table = jnp.array(position, dtype=jnp.int32)
     mine = table[here]
     ahead_pick = (mine - table) % count
@@ -55,7 +60,7 @@
     joined = jnp.concatenate(
         [jnp.stack(ahead_parts)[ahead_pick], jnp.stack(behind_parts)[behind_pick]], axis=1
     )
-    return joined.reshape(count * 2 * half, ahead.shape[1]), ahead_parts[1]
+    return joined.reshape(count * 2 * half, ahead.shape[1]), tied
 
 
 def shards(
@@ -102,42 +107,46 @@
             axis=1,
         )
 
-    full_panel, first_arrival = gather_rows(
+    panel_bias = jnp.where(
+        first,
+        jnp.concatenate([rotary_b[:split], value_bias[:value_split]]),
+        jnp.concatenate([rotary_b[split:], value_bias[value_split:]]),
+    )
+
+    def tokens_normed(first_arrival):
+        other_half = lax.ppermute(tokens, "col", SWAP)
+        late_tokens, _ = lax.optimization_barrier((tokens, first_arrival))
+        partner_half = lax.ppermute(late_tokens, "groups", SWAP)
+        partner_other = lax.ppermute(partner_half, "col", SWAP)
+        whole = jnp.where(
+            column == 0,
+            jnp.concatenate([tokens, other_half], axis=2),
+            jnp.concatenate([other_half, tokens], axis=2),
+        )
+        partner = jnp.where(
+            column == 0,
+            jnp.concatenate([partner_half, partner_other], axis=2),
+            jnp.concatenate([partner_other, partner_half], axis=2),
+        )
+        both = jnp.concatenate([whole, partner], axis=0)
+        widened = both.astype(jnp.float32)
+        power = jnp.mean(widened * widened, axis=-1, keepdims=True)
+        normed = (
+            (widened * lax.rsqrt(power + norm_eps) * gain)
+            .astype(jnp.bfloat16)
+            .reshape(2 * passages * length, -1)
+        )
+        return normed
+
+    full_panel, normed = gather_rows(
         panel_rows(0, rows_here // 2),
         panel_rows(rows_here // 2, rows_here),
         row_count,
         here,
-    )
-    panel_bias = jnp.where(
-        first,
-        jnp.concatenate([rotary_b[:split], value_bias[:value_split]]),
-        jnp.concatenate([rotary_b[split:], value_bias[value_split:]]),
-    )
-
-    other_half = lax.ppermute(tokens, "col", SWAP)
-    late_tokens, _ = lax.optimization_barrier((tokens, first_arrival))
-    partner_half = lax.ppermute(late_tokens, "groups", SWAP)
-    partner_other = lax.ppermute(partner_half, "col", SWAP)
-    whole = jnp.where(
-        column == 0,
-        jnp.concatenate([tokens, other_half], axis=2),
-        jnp.concatenate([other_half, tokens], axis=2),
-    )
-    partner = jnp.where(
-        column == 0,
-        jnp.concatenate([partner_half, partner_other], axis=2),
-        jnp.concatenate([partner_other, partner_half], axis=2),
-    )
-    both = jnp.concatenate([whole, partner], axis=0)
-    widened = both.astype(jnp.float32)
-    power = jnp.mean(widened * widened, axis=-1, keepdims=True)
-    normed = (
-        (widened * lax.rsqrt(power + norm_eps) * gain)
-        .astype(jnp.bfloat16)
-        .reshape(2 * passages * length, -1)
+        tokens_normed,
+        row_count - 1,
     )
     token_positions = (here * length + jnp.arange(length, dtype=jnp.int32)).astype(jnp.float32)
-
     summed = jnp.dot(normed, full_panel, preferred_element_type=jnp.float32) + panel_bias
     summed = summed.reshape(2 * passages, length, split + value_split)
     turned = apply_rotation(

time: 118 us -> 124 us (1.051)
  other arithmetic: 16.4 us -> 20.4 us
  local copies, waits for them, and re-layouts: 32.2 us -> 29.3 us
  matrix products: 6.81 us -> 9.5 us
  waiting for transfers between devices: 36.2 us -> 37.8 us
    ppermute x7, waiting for transfers between devices: 0.7 us -> 7.35 us  [gather_rows(): behind = lax.ppermute(behind, 'row', backward)]
    ppermute x7, waiting for transfers between devices: 21.2 us -> 17.3 us  [gather_rows(): ahead = lax.ppermute(ahead, 'row', forward)]
    convert_element_type x1 -> x2, other arithmetic: 1.09 us -> 3.6 us  [the longest x1 3.12 us: tokens_normed(): normed = (widened * lax.rsqrt(power + norm_eps) * gain).astype(jnp.bfloat...]
    unnamed x43 -> x53, local copies, waits for them, and re-layouts: 10.3 us -> 8.48 us
    concatenate x2, other arithmetic: 0.05 us -> 1.48 us  [panel_rows(): jnp.concatenate([lax.dynamic_slice_in_dim(rotary_w[start:stop], group * s...]
  transfers between devices with their start and end apart: 25 -> 25, of which waited for: 16 -> 14; matrix products, arithmetic and copies ran while one was open for 28% -> 21% of each run, Pallas kernels for 0% -> 0%
where the time goes in v19:
time: 124 us
  waiting for transfers between devices  37.8 us (30%)
  local copies, waits for them, and re-layouts  29.3 us (24%)
  starting transfers between devices  25.8 us (21%)
  other arithmetic  20.4 us (16%)
  matrix products  9.5 us (8%)
    ppermute x7, waiting for transfers between devices, gather_rows(): ahead = lax.ppermute(ahead, 'row', forward)  17.3 us
    ppermute x7, starting transfers between devices, gather_rows(): ahead = lax.ppermute(ahead, 'row', forward)  12.3 us
    unnamed x53, local copies, waits for them, and re-layouts  8.48 us
    ppermute x7, waiting for transfers between devices, gather_rows(): behind = lax.ppermute(behind, 'row', backward)  7.35 us
    ppermute x4, starting transfers between devices, shards(): ahead = lax.ppermute(ahead, 'row', forward)  6.2 us
    ppermute x4, waiting for transfers between devices, shards(): ahead = lax.ppermute(ahead, 'row', forward)  5.76 us
    ppermute x1, waiting for transfers between devices, shards(): returned = lax.ppermute(result[passages:], 'groups', SWAP)  5.16 us
    gather x1, local copies, waits for them, and re-layouts, gather_rows(): jnp.stack(ahead_parts)[ahead_pick]  3.92 us
  transfers between devices with their start and end apart: 25, of which 14 were waited for; matrix products, arithmetic and copies ran while one was open for 21% of the time, Pallas kernels for 0%

profile of v19, /device:TPU:0, one launch (start us, length us, event | category | flops | bytes accessed | tf_op | source)
XLA Modules:
  0.0 123.5 jit_solution(18264890859385178895)
XLA Ops:
  4.1 3.0 %collective-permute-start = (bf16[224,576]{1,0:T(8,128)(2,1)}, bf16[224,576]{1,0:T(8,128)(2,1)S(1)}, u32[]{:S(2)}, u32[]{:S(2)}) collective-permute-start(bf16[224,576]{1,0:T(8,128)(2,1)} %pad_maximum_fusion.4), channel_id=1, source_target_pairs={{0,4},{4,8},{8,12},{12,14},{14,10},{10,6},{6,2},{2,0},{1,5},{5,9},... | collective-permute-start | bytes 774152 | tf_op jit(solution)/shard_map/ppermute | solution.py:50
  14.1 1.8 %collective-permute-start.7 = (bf16[2,128,1792]{2,1,0:T(8,128)(2,1)}, bf16[2,128,1792]{2,1,0:T(8,128)(2,1)S(1)}, u32[]{:S(2)}, u32[]{:S(2)}) collective-permute-start(bf16[2,128,1792]{2,1,0:T(8,128)(2,1)} %param.12), channel_id=1, source_target_pairs={{0,16},{16,0},{1,17},{17,1},{2,18},{18,2},{3,19},{19,3},{4,20},{20... | collective-permute-start | bytes 2752520 | tf_op jit(solution)/shard_map/ppermute | solution.py:119
  15.8 1.6 %collective-permute-start.1 = (bf16[224,576]{1,0:T(8,128)(2,1)S(1)}, bf16[224,576]{1,0:T(8,128)(2,1)S(1)}, u32[]{:S(2)}, u32[]{:S(2)}) collective-permute-start(bf16[224,576]{1,0:T(8,128)(2,1)S(1)} %collective-permute-done), channel_id=1, source_target_pairs={{0,4},{4,8},{8,12},{12,14},{14,10},{10,6},{6,2},{2,0},{1,5},{5,9},... | collective-permute-start | bytes 774152 | tf_op jit(solution)/shard_map/ppermute | solution.py:50
  18.7 5.8 %collective-permute-done.1 = bf16[224,576]{1,0:T(8,128)(2,1)S(1)} collective-permute-done((bf16[224,576]{1,0:T(8,128)(2,1)S(1)}, bf16[224,576]{1,0:T(8,128)(2,1)S(1)}, u32[]{:S(2)}, u32[]{:S(2)}) %collective-permute-start.1) | collective-permute-done | bytes 258080 | tf_op jit(solution)/shard_map/ppermute | solution.py:50
  24.5 1.6 %collective-permute-start.2 = (bf16[224,576]{1,0:T(8,128)(2,1)S(1)}, bf16[224,576]{1,0:T(8,128)(2,1)S(1)}, u32[]{:S(2)}, u32[]{:S(2)}) collective-permute-start(bf16[224,576]{1,0:T(8,128)(2,1)S(1)} %collective-permute-done.1), channel_id=1, source_target_pairs={{0,4},{4,8},{8,12},{12,14},{14,10},{10,6},{6,2},{2,0},{1,5},{5,9},... | collective-permute-start | bytes 774152 | tf_op jit(solution)/shard_map/ppermute | solution.py:50
  27.3 5.0 %collective-permute-done.2 = bf16[224,576]{1,0:T(8,128)(2,1)S(1)} collective-permute-done((bf16[224,576]{1,0:T(8,128)(2,1)S(1)}, bf16[224,576]{1,0:T(8,128)(2,1)S(1)}, u32[]{:S(2)}, u32[]{:S(2)}) %collective-permute-start.2) | collective-permute-done | bytes 258080 | tf_op jit(solution)/shard_map/ppermute | solution.py:50
  32.3 1.6 %collective-permute-start.3 = (bf16[224,576]{1,0:T(8,128)(2,1)S(1)}, bf16[224,576]{1,0:T(8,128)(2,1)S(1)}, u32[]{:S(2)}, u32[]{:S(2)}) collective-permute-start(bf16[224,576]{1,0:T(8,128)(2,1)S(1)} %collective-permute-done.2), channel_id=1, source_target_pairs={{0,4},{4,8},{8,12},{12,14},{14,10},{10,6},{6,2},{2,0},{1,5},{5,9},... | collective-permute-start | bytes 774152 | tf_op jit(solution)/shard_map/ppermute | solution.py:50
  35.1 2.5 %maximum_select_fusion = bf16[2,128,3584]{2,1,0:T(8,128)(2,1)S(1)} fusion(bf16[2,128,1792]{2,1,0:T(8,128)(2,1)} %collective-permute-done.6, bf16[2,128,1792]{2,1,0:T(8,128)(2,1)} %param.12, pred[]{:T(512)S(6)} %eq.14), kind=kLoop, calls=%fused_computation.13 | loop fusion | flops 8257536 | bytes 3670017 | tf_op jit(solution)/shard_map/jit(_where)/select_n | solution.py:121
  37.6 1.7 %collective-permute-done.3 = bf16[224,576]{1,0:T(8,128)(2,1)S(1)} collective-permute-done((bf16[224,576]{1,0:T(8,128)(2,1)S(1)}, bf16[224,576]{1,0:T(8,128)(2,1)S(1)}, u32[]{:S(2)}, u32[]{:S(2)}) %collective-permute-start.3) | collective-permute-done | bytes 258080 | tf_op jit(solution)/shard_map/ppermute | solution.py:50
  39.3 1.6 %collective-permute-start.4 = (bf16[224,576]{1,0:T(8,128)(2,1)S(1)}, bf16[224,576]{1,0:T(8,128)(2,1)S(1)}, u32[]{:S(2)}, u32[]{:S(2)}) collective-permute-start(bf16[224,576]{1,0:T(8,128)(2,1)S(1)} %collective-permute-done.3), channel_id=1, source_target_pairs={{0,4},{4,8},{8,12},{12,14},{14,10},{10,6},{6,2},{2,0},{1,5},{5,9},... | collective-permute-start | bytes 774152 | tf_op jit(solution)/shard_map/ppermute | solution.py:50
  42.2 4.3 %collective-permute-done.4 = bf16[224,576]{1,0:T(8,128)(2,1)S(1)} collective-permute-done((bf16[224,576]{1,0:T(8,128)(2,1)S(1)}, bf16[224,576]{1,0:T(8,128)(2,1)S(1)}, u32[]{:S(2)}, u32[]{:S(2)}) %collective-permute-start.4) | collective-permute-done | bytes 258080 | tf_op jit(solution)/shard_map/ppermute | solution.py:50
  46.5 1.6 %collective-permute-start.5 = (bf16[224,576]{1,0:T(8,128)(2,1)S(1)}, bf16[224,576]{1,0:T(8,128)(2,1)S(1)}, u32[]{:S(2)}, u32[]{:S(2)}) collective-permute-start(bf16[224,576]{1,0:T(8,128)(2,1)S(1)} %collective-permute-done.4), channel_id=1, source_target_pairs={{0,4},{4,8},{8,12},{12,14},{14,10},{10,6},{6,2},{2,0},{1,5},{5,9},... | collective-permute-start | bytes 774152 | tf_op jit(solution)/shard_map/ppermute | solution.py:50
  49.6 7.0 %collective-permute-done.15 = bf16[224,576]{1,0:T(8,128)(2,1)S(1)} collective-permute-done((bf16[224,576]{1,0:T(8,128)(2,1)S(1)}, bf16[224,576]{1,0:T(8,128)(2,1)S(1)}, u32[]{:S(2)}, u32[]{:S(2)}) %collective-permute-start.15) | collective-permute-done | bytes 258080 | tf_op jit(solution)/shard_map/ppermute | solution.py:51
  59.1 3.1 %fusion.1 = bf16[512,3584]{1,0:T(8,128)(2,1)} fusion(f32[4,128,3584]{2,1,0:T(8,128)S(1)} %maximum_convert_fusion, f32[3584]{0:T(1024)S(1)} %copy-done.7, f32[512]{0:T(512)S(1)} %rsqrt_bitcast_fusion), kind=kLoop, calls=%fused_computation.9 | loop fusion | flops 5505024 | bytes 11026432 | tf_op jit(solution)/shard_map/convert_element_type | solution.py:136
  62.2 1.4 %collective-permute-start.9 = (bf16[224,576]{1,0:T(8,128)(2,1)S(1)}, bf16[224,576]{1,0:T(8,128)(2,1)S(1)}, u32[]{:S(2)}, u32[]{:S(2)}) collective-permute-start(bf16[224,576]{1,0:T(8,128)(2,1)S(1)} %collective-permute-done.5), channel_id=1, source_target_pairs={{0,4},{4,8},{8,12},{12,14},{14,10},{10,6},{6,2},{2,0},{1,5},{5,9},... | collective-permute-start | bytes 774152 | tf_op jit(solution)/shard_map/ppermute | solution.py:50
  64.4 1.4 %copy-done.4 = bf16[8,224,576]{2,1,0:T(8,128)(2,1)} copy-done((bf16[8,224,576]{2,1,0:T(8,128)(2,1)}, bf16[8,224,576]{2,1,0:T(8,128)(2,1)S(1)}, u32[]{:S(2)}) %copy-start.4) | copy-done | bytes 2064408
  65.8 2.7 %gather_fusion.1 = bf16[8,224,576]{2,1,0:T(8,128)(2,1)S(1)} fusion(bf16[8,224,576]{2,1,0:T(8,128)(2,1)} %copy-done.4, s32[1024]{0:T(1024)} %get-tuple-element.33), kind=kCustom, calls=%fused_computation.1 | custom fusion | bytes 4128800 | tf_op jit(solution)/shard_map/gather | solution.py:61
  69.6 3.9 %gather_fusion = bf16[8,224,576]{2,1,0:T(8,128)(2,1)} fusion(bf16[8,224,576]{2,1,0:T(8,128)(2,1)} %bitcast_dynamic-update-slice_fusion.8, s32[1024]{0:T(1024)S(1)} %get-tuple-element.34), kind=kCustom, calls=%fused_computation | custom fusion | bytes 4128800 | tf_op jit(solution)/shard_map/gather | solution.py:61
  73.5 2.2 %pad_maximum_fusion = bf16[8,448,576]{2,1,0:T(8,128)(2,1)S(1)} fusion(bf16[8,224,576]{2,1,0:T(8,128)(2,1)S(1)} %gather_fusion.1, bf16[8,224,576]{2,1,0:T(8,128)(2,1)} %gather_fusion), kind=kLoop, calls=%fused_computation.11 | loop fusion | flops 8257536 | bytes 8257536 | tf_op jit(solution)/shard_map/concatenate | solution.py:60
  76.2 2.4 %convolution_add_fusion = f32[512,576]{0,1:T(8,128)S(1)} fusion(bf16[512,3584]{1,0:T(8,128)(2,1)S(1)} %copy-done.3, bf16[3584,576]{1,0:T(8,128)(2,1)S(1)} %bitcast.142, f32[576]{0:T(1024)S(1)} %maximum_select_fusion.2), kind=kOutput, calls=%fused_computation.29 | convolution fusion | flops 2114224128 | bytes 8980736 | tf_op jit(solution)/shard_map/dot_general | solution.py:150
  82.8 5.2 %collective-permute-done.17 = bf16[2,128,576]{1,0,2:T(2,128)(2,1)S(1)} collective-permute-done((bf16[2,128,576]{1,0,2:T(2,128)(2,1)S(1)}, bf16[2,128,576]{1,0,2:T(2,128)(2,1)S(1)}, u32[]{:S(2)}, u32[]{:S(2)}) %collective-permute-start.17) | collective-permute-done | bytes 294944 | tf_op jit(solution)/shard_map/ppermute | solution.py:161
  88.8 1.4 %collective-permute-start.18 = (bf16[2,128,256]{1,0,2:T(2,128)(2,1)S(1)}, bf16[2,128,256]{1,0,2:T(2,128)(2,1)S(1)}, u32[]{:S(2)}, u32[]{:S(2)}) collective-permute-start(bf16[2,128,256]{1,0,2:T(2,128)(2,1)S(1)} %pad_maximum_fusion.6), channel_id=1, source_target_pairs={{0,4},{4,8},{8,12},{12,14},{14,10},{10,6},{6,2},{2,0},{1,5},{5,9},... | collective-permute-start | bytes 393224 | tf_op jit(solution)/shard_map/ppermute | solution.py:180
  90.9 3.4 %collective-permute-done.18 = bf16[2,128,256]{1,0,2:T(2,128)(2,1)S(1)} collective-permute-done((bf16[2,128,256]{1,0,2:T(2,128)(2,1)S(1)}, bf16[2,128,256]{1,0,2:T(2,128)(2,1)S(1)}, u32[]{:S(2)}, u32[]{:S(2)}) %collective-permute-start.18) | collective-permute-done | bytes 131104 | tf_op jit(solution)/shard_map/ppermute | solution.py:180
  94.3 1.6 %collective-permute-start.19 = (bf16[2,128,256]{1,0,2:T(2,128)(2,1)S(1)}, bf16[2,128,256]{1,0,2:T(2,128)(2,1)S(1)}, u32[]{:S(2)}, u32[]{:S(2)}) collective-permute-start(bf16[2,128,256]{1,0,2:T(2,128)(2,1)S(1)} %collective-permute-done.18), channel_id=1, source_target_pairs={{0,4},{4,8},{8,12},{12,14},{14,10},{10,6},{6,2},{2,0},{1,5},{5,9},... | collective-permute-start | bytes 393224 | tf_op jit(solution)/shard_map/ppermute | solution.py:180
  99.3 1.6 %collective-permute-start.20 = (bf16[2,128,256]{1,0,2:T(2,128)(2,1)S(1)}, bf16[2,128,256]{1,0,2:T(2,128)(2,1)S(1)}, u32[]{:S(2)}, u32[]{:S(2)}) collective-permute-start(bf16[2,128,256]{1,0,2:T(2,128)(2,1)S(1)} %collective-permute-done.19), channel_id=1, source_target_pairs={{0,4},{4,8},{8,12},{12,14},{14,10},{10,6},{6,2},{2,0},{1,5},{5,9},... | collective-permute-start | bytes 393224 | tf_op jit(solution)/shard_map/ppermute | solution.py:180
  101.3 1.8 %copy.52 = bf16[2,2,64,7,128]{4,2,3,1,0:T(8,128)(2,1)S(1)} copy(bf16[2,2,64,7,128]{2,1,0,4,3:T(2,128)(2,1)S(1)} %reshape.340) | data formatting | bytes 917504 | tf_op jit(solution)/shard_map/reshape | solution.py:221
  104.3 1.6 %collective-permute-start.21 = (bf16[2,128,256]{1,0,2:T(2,128)(2,1)S(1)}, bf16[2,128,256]{1,0,2:T(2,128)(2,1)S(1)}, u32[]{:S(2)}, u32[]{:S(2)}) collective-permute-start(bf16[2,128,256]{1,0,2:T(2,128)(2,1)S(1)} %collective-permute-done.20), channel_id=1, source_target_pairs={{0,4},{4,8},{8,12},{12,14},{14,10},{10,6},{6,2},{2,0},{1,5},{5,9},... | collective-permute-start | bytes 393224 | tf_op jit(solution)/shard_map/ppermute | solution.py:180
  106.1 2.2 %collective-permute-done.24 = bf16[2,128,256]{1,0,2:T(2,128)(2,1)S(1)} collective-permute-done((bf16[2,128,256]{1,0,2:T(2,128)(2,1)S(1)}, bf16[2,128,256]{1,0,2:T(2,128)(2,1)S(1)}, u32[]{:S(2)}, u32[]{:S(2)}) %collective-permute-start.24) | collective-permute-done | bytes 131104 | tf_op jit(solution)/shard_map/ppermute | solution.py:183
  111.6 1.7 %fusion.42 = (f32[2,2,7,64]{3,2,1,0:T(8,128)S(1)}, f32[2,2,7,64,128]{4,3,2,1,0:T(8,128)}) fusion(bf16[2,2,64,7,128]{4,2,3,1,0:T(8,128)(2,1)S(1)} %copy.52, bf16[2,2,7,128,256]{4,3,2,1,0:T(8,128)(2,1)S(1)} %bitcast.145), kind=kOutput, calls=%fused_computation.156 | convolution fusion | flops 59177216 | bytes 2300928 | tf_op jit(solution)/shard_map/sqbgh,sqgwh->sqgbw/dot_general | solution.py:236
  114.5 1.4 %gather_fusion.4 = bf16[12,64,256]{2,1,0:T(8,128)(2,1)} fusion(bf16[2,16,64,256]{3,2,0,1:T(8,128)(2,1)S(1)} %bitcast.141, s32[12]{0:T(128)S(1)} %reshape.308), kind=kCustom, calls=%fused_computation.4 | custom fusion | bytes 786528 | tf_op jit(solution)/shard_map/gather | solution.py:207
  115.9 1.6 %bitcast_reduce_fusion = (f32[2,2,7,64]{3,2,1,0:T(8,128)S(1)}, f32[2,2,192,64,7]{2,3,4,1,0:T(8,128)S(1)}) fusion(pred[2,192]{1,0:T(4,128)(4,1)S(1)} %broadcast_in_dim.31, bf16[2,2,64,7,128]{4,2,3,1,0:T(8,128)(2,1)S(1)} %copy.52, bf16[2,2,192,256]{3,2,1,0:T(8,128)(2,1)} %bitcast.150), kind=kOutput, calls=%fused_computation.16 | convolution fusion | flops 89110784 | bytes 2039168 | tf_op jit(solution)/shard_map/sqbgh,sqwh->sqgbw/dot_general | solution.py:224
  122.2 1.3 %convert_element_type.50 = bf16[2,128,896]{2,1,0:T(8,128)(2,1)} reshape(bf16[2,2,64,7,128]{4,3,2,1,0:T(8,128)(2,1)S(1)} %copy.57) | data formatting | bytes 917504 | tf_op jit(solution)/shard_map/convert_element_type | solution.py:283
  (175 shorter events, 41.8 us)
Async XLA Ops:
  0.0 11.5 %copy-start = (s32[2,2,2]{2,1,0:T(2,128)S(1)}, s32[2,2,2]{2,1,0:T(2,128)}, u32[]{:S(2)}) copy-start(s32[2,2,2]{2,1,0:T(2,128)} %param.21) | copy-start | bytes 100
  3.1 8.3 %copy-start.8 = (f32[896]{0:T(1024)S(1)}, f32[896]{0:T(1024)}, u32[]{:S(2)}) copy-start(f32[896]{0:T(1024)} %param.15) | copy-start | bytes 10756
  3.1 8.3 %copy-start.12 = (f32[128]{0:T(128)S(1)}, f32[128]{0:T(128)}, u32[]{:S(2)}) copy-start(f32[128]{0:T(128)} %param.17) | copy-start | bytes 1540
  3.2 10.3 %copy-start.9 = (s32[2,16,14,2]{1,3,2,0:T(2,128)S(1)}, s32[2,16,14,2]{1,3,2,0:T(2,128)}, u32[]{:S(2)}) copy-start(s32[2,16,14,2]{1,3,2,0:T(2,128)} %param.20) | copy-start | bytes 10756
  3.2 10.4 %slice-start = ((f32[896]{0:T(1024)}), f32[512]{0:T(512)S(1)}, s32[]{:S(2)}) async-start(f32[896]{0:T(1024)} %param.15), calls=%async_computation | async-start | bytes 4096 | tf_op jit(solution)/shard_map/slice | solution.py:112
  4.1 10.0 %collective-permute-start = (bf16[224,576]{1,0:T(8,128)(2,1)}, bf16[224,576]{1,0:T(8,128)(2,1)S(1)}, u32[]{:S(2)}, u32[]{:S(2)}) collective-permute-start(bf16[224,576]{1,0:T(8,128)(2,1)} %pad_maximum_fusion.4), channel_id=1, source_target_pairs={{0,4},{4,8},{8,12},{12,14},{14,10},{10,6},{6,2},{2,0},{1,5},{5,9},... | collective-permute-start | bytes 774152 | tf_op jit(solution)/shard_map/ppermute | solution.py:50
  7.1 28.0 %collective-permute-start.6 = (bf16[2,128,1792]{2,1,0:T(8,128)(2,1)}, bf16[2,128,1792]{2,1,0:T(8,128)(2,1)}, u32[]{:S(2)}, u32[]{:S(2)}) collective-permute-start(bf16[2,128,1792]{2,1,0:T(8,128)(2,1)} %param.12), channel_id=1, source_target_pairs={{0,1},{1,0},{2,3},{3,2},{4,5},{5,4},{6,7},{7,6},{8,9},{9,8},{10,11... | collective-permute-start | bytes 2752520 | tf_op jit(solution)/shard_map/ppermute | solution.py:117
  8.0 9.5 %collective-permute-start.10 = (bf16[224,576]{1,0:T(8,128)(2,1)}, bf16[224,576]{1,0:T(8,128)(2,1)S(1)}, u32[]{:S(2)}, u32[]{:S(2)}) collective-permute-start(bf16[224,576]{1,0:T(8,128)(2,1)} %pad_maximum_fusion.5), channel_id=1, source_target_pairs={{0,2},{4,0},{8,4},{12,8},{14,12},{10,14},{6,10},{2,6},{1,3},{5,1},... | collective-permute-start | bytes 774152 | tf_op jit(solution)/shard_map/ppermute | solution.py:51
  14.1 27.3 %collective-permute-start.7 = (bf16[2,128,1792]{2,1,0:T(8,128)(2,1)}, bf16[2,128,1792]{2,1,0:T(8,128)(2,1)S(1)}, u32[]{:S(2)}, u32[]{:S(2)}) collective-permute-start(bf16[2,128,1792]{2,1,0:T(8,128)(2,1)} %param.12), channel_id=1, source_target_pairs={{0,16},{16,0},{1,17},{17,1},{2,18},{18,2},{3,19},{19,3},{4,20},{20... | collective-permute-start | bytes 2752520 | tf_op jit(solution)/shard_map/ppermute | solution.py:119
  15.8 8.7 %collective-permute-start.1 = (bf16[224,576]{1,0:T(8,128)(2,1)S(1)}, bf16[224,576]{1,0:T(8,128)(2,1)S(1)}, u32[]{:S(2)}, u32[]{:S(2)}) collective-permute-start(bf16[224,576]{1,0:T(8,128)(2,1)S(1)} %collective-permute-done), channel_id=1, source_target_pairs={{0,4},{4,8},{8,12},{12,14},{14,10},{10,6},{6,2},{2,0},{1,5},{5,9},... | collective-permute-start | bytes 774152 | tf_op jit(solution)/shard_map/ppermute | solution.py:50
  17.4 8.6 %collective-permute-start.11 = (bf16[224,576]{1,0:T(8,128)(2,1)S(1)}, bf16[224,576]{1,0:T(8,128)(2,1)S(1)}, u32[]{:S(2)}, u32[]{:S(2)}) collective-permute-start(bf16[224,576]{1,0:T(8,128)(2,1)S(1)} %collective-permute-done.10), channel_id=1, source_target_pairs={{0,2},{4,0},{8,4},{12,8},{14,12},{10,14},{6,10},{2,6},{1,3},{5,1},... | collective-permute-start | bytes 774152 | tf_op jit(solution)/shard_map/ppermute | solution.py:51
  24.5 7.8 %collective-permute-start.2 = (bf16[224,576]{1,0:T(8,128)(2,1)S(1)}, bf16[224,576]{1,0:T(8,128)(2,1)S(1)}, u32[]{:S(2)}, u32[]{:S(2)}) collective-permute-start(bf16[224,576]{1,0:T(8,128)(2,1)S(1)} %collective-permute-done.1), channel_id=1, source_target_pairs={{0,4},{4,8},{8,12},{12,14},{14,10},{10,6},{6,2},{2,0},{1,5},{5,9},... | collective-permute-start | bytes 774152 | tf_op jit(solution)/shard_map/ppermute | solution.py:50
  26.1 7.8 %collective-permute-start.12 = (bf16[224,576]{1,0:T(8,128)(2,1)S(1)}, bf16[224,576]{1,0:T(8,128)(2,1)S(1)}, u32[]{:S(2)}, u32[]{:S(2)}) collective-permute-start(bf16[224,576]{1,0:T(8,128)(2,1)S(1)} %collective-permute-done.11), channel_id=1, source_target_pairs={{0,2},{4,0},{8,4},{12,8},{14,12},{10,14},{6,10},{2,6},{1,3},{5,1},... | collective-permute-start | bytes 774152 | tf_op jit(solution)/shard_map/ppermute | solution.py:51
  32.3 7.0 %collective-permute-start.3 = (bf16[224,576]{1,0:T(8,128)(2,1)S(1)}, bf16[224,576]{1,0:T(8,128)(2,1)S(1)}, u32[]{:S(2)}, u32[]{:S(2)}) collective-permute-start(bf16[224,576]{1,0:T(8,128)(2,1)S(1)} %collective-permute-done.2), channel_id=1, source_target_pairs={{0,4},{4,8},{8,12},{12,14},{14,10},{10,6},{6,2},{2,0},{1,5},{5,9},... | collective-permute-start | bytes 774152 | tf_op jit(solution)/shard_map/ppermute | solution.py:50
  33.9 7.0 %collective-permute-start.13 = (bf16[224,576]{1,0:T(8,128)(2,1)S(1)}, bf16[224,576]{1,0:T(8,128)(2,1)S(1)}, u32[]{:S(2)}, u32[]{:S(2)}) collective-permute-start(bf16[224,576]{1,0:T(8,128)(2,1)S(1)} %collective-permute-done.12), channel_id=1, source_target_pairs={{0,2},{4,0},{8,4},{12,8},{14,12},{10,14},{6,10},{2,6},{1,3},{5,1},... | collective-permute-start | bytes 774152 | tf_op jit(solution)/shard_map/ppermute | solution.py:51
  39.3 7.2 %collective-permute-start.4 = (bf16[224,576]{1,0:T(8,128)(2,1)S(1)}, bf16[224,576]{1,0:T(8,128)(2,1)S(1)}, u32[]{:S(2)}, u32[]{:S(2)}) collective-permute-start(bf16[224,576]{1,0:T(8,128)(2,1)S(1)} %collective-permute-done.3), channel_id=1, source_target_pairs={{0,4},{4,8},{8,12},{12,14},{14,10},{10,6},{6,2},{2,0},{1,5},{5,9},... | collective-permute-start | bytes 774152 | tf_op jit(solution)/shard_map/ppermute | solution.py:50
  40.9 7.5 %collective-permute-start.14 = (bf16[224,576]{1,0:T(8,128)(2,1)S(1)}, bf16[224,576]{1,0:T(8,128)(2,1)S(1)}, u32[]{:S(2)}, u32[]{:S(2)}) collective-permute-start(bf16[224,576]{1,0:T(8,128)(2,1)S(1)} %collective-permute-done.13), channel_id=1, source_target_pairs={{0,2},{4,0},{8,4},{12,8},{14,12},{10,14},{6,10},{2,6},{1,3},{5,1},... | collective-permute-start | bytes 774152 | tf_op jit(solution)/shard_map/ppermute | solution.py:51
  41.4 16.0 %collective-permute-start.8 = (bf16[2,128,1792]{2,1,0:T(8,128)(2,1)S(1)}, bf16[2,128,1792]{2,1,0:T(8,128)(2,1)S(1)}, u32[]{:S(2)}, u32[]{:S(2)}) collective-permute-start(bf16[2,128,1792]{2,1,0:T(8,128)(2,1)S(1)} %collective-permute-done.7), channel_id=1, source_target_pairs={{0,1},{1,0},{2,3},{3,2},{4,5},{5,4},{6,7},{7,6},{8,9},{9,8},{10,11... | collective-permute-start | bytes 2752520 | tf_op jit(solution)/shard_map/ppermute | solution.py:120
  46.5 15.7 %collective-permute-start.5 = (bf16[224,576]{1,0:T(8,128)(2,1)S(1)}, bf16[224,576]{1,0:T(8,128)(2,1)S(1)}, u32[]{:S(2)}, u32[]{:S(2)}) collective-permute-start(bf16[224,576]{1,0:T(8,128)(2,1)S(1)} %collective-permute-done.4), channel_id=1, source_target_pairs={{0,4},{4,8},{8,12},{12,14},{14,10},{10,6},{6,2},{2,0},{1,5},{5,9},... | collective-permute-start | bytes 774152 | tf_op jit(solution)/shard_map/ppermute | solution.py:50
  48.3 8.3 %collective-permute-start.15 = (bf16[224,576]{1,0:T(8,128)(2,1)S(1)}, bf16[224,576]{1,0:T(8,128)(2,1)S(1)}, u32[]{:S(2)}, u32[]{:S(2)}) collective-permute-start(bf16[224,576]{1,0:T(8,128)(2,1)S(1)} %collective-permute-done.14), channel_id=1, source_target_pairs={{0,2},{4,0},{8,4},{12,8},{14,12},{10,14},{6,10},{2,6},{1,3},{5,1},... | collective-permute-start | bytes 774152 | tf_op jit(solution)/shard_map/ppermute | solution.py:51
  56.6 7.7 %collective-permute-start.16 = (bf16[224,576]{1,0:T(8,128)(2,1)S(1)}, bf16[224,576]{1,0:T(8,128)(2,1)S(1)}, u32[]{:S(2)}, u32[]{:S(2)}) collective-permute-start(bf16[224,576]{1,0:T(8,128)(2,1)S(1)} %collective-permute-done.15), channel_id=1, source_target_pairs={{0,2},{4,0},{8,4},{12,8},{14,12},{10,14},{6,10},{2,6},{1,3},{5,1},... | collective-permute-start | bytes 774152 | tf_op jit(solution)/shard_map/ppermute | solution.py:51
  62.2 6.6 %collective-permute-start.9 = (bf16[224,576]{1,0:T(8,128)(2,1)S(1)}, bf16[224,576]{1,0:T(8,128)(2,1)S(1)}, u32[]{:S(2)}, u32[]{:S(2)}) collective-permute-start(bf16[224,576]{1,0:T(8,128)(2,1)S(1)} %collective-permute-done.5), channel_id=1, source_target_pairs={{0,4},{4,8},{8,12},{12,14},{14,10},{10,6},{6,2},{2,0},{1,5},{5,9},... | collective-permute-start | bytes 774152 | tf_op jit(solution)/shard_map/ppermute | solution.py:50
  80.6 15.5 %copy-start.11 = (s32[2,2,1]{1,0,2:T(2,128)S(1)}, s32[2,2,1]{1,0,2:T(2,128)}, u32[]{:S(2)}) copy-start(s32[2,2,1]{1,0,2:T(2,128)} %fusion.30) | copy-start | bytes 52
  80.6 15.6 %copy-start.14 = (pred[2,3]{1,0:T(4,128)(4,1)S(1)}, pred[2,3]{1,0:T(4,128)(4,1)}, u32[]{:S(2)}) copy-start(pred[2,3]{1,0:T(4,128)(4,1)} %compare_and_fusion) | copy-start | bytes 22
  81.1 6.8 %collective-permute-start.17 = (bf16[2,128,576]{1,0,2:T(2,128)(2,1)S(1)}, bf16[2,128,576]{1,0,2:T(2,128)(2,1)S(1)}, u32[]{:S(2)}, u32[]{:S(2)}) collective-permute-start(bf16[2,128,576]{1,0,2:T(2,128)(2,1)S(1)} %fusion.22), channel_id=1, source_target_pairs={{0,16},{16,0},{1,17},{17,1},{2,18},{18,2},{3,19},{19,3},{4,20},{20... | collective-permute-start | bytes 884744 | tf_op jit(solution)/shard_map/ppermute | solution.py:161
  88.8 5.5 %collective-permute-start.18 = (bf16[2,128,256]{1,0,2:T(2,128)(2,1)S(1)}, bf16[2,128,256]{1,0,2:T(2,128)(2,1)S(1)}, u32[]{:S(2)}, u32[]{:S(2)}) collective-permute-start(bf16[2,128,256]{1,0,2:T(2,128)(2,1)S(1)} %pad_maximum_fusion.6), channel_id=1, source_target_pairs={{0,4},{4,8},{8,12},{12,14},{14,10},{10,6},{6,2},{2,0},{1,5},{5,9},... | collective-permute-start | bytes 393224 | tf_op jit(solution)/shard_map/ppermute | solution.py:180
  90.2 6.6 %collective-permute-start.22 = (bf16[2,128,256]{1,0,2:T(2,128)(2,1)S(1)}, bf16[2,128,256]{1,0,2:T(2,128)(2,1)S(1)}, u32[]{:S(2)}, u32[]{:S(2)}) collective-permute-start(bf16[2,128,256]{1,0,2:T(2,128)(2,1)S(1)} %pad_maximum_fusion.6), channel_id=1, source_target_pairs={{0,2},{4,0},{8,4},{12,8},{14,12},{10,14},{6,10},{2,6},{1,3},{5,1},... | collective-permute-start | bytes 393224 | tf_op jit(solution)/shard_map/ppermute | solution.py:183
  94.3 5.0 %collective-permute-start.19 = (bf16[2,128,256]{1,0,2:T(2,128)(2,1)S(1)}, bf16[2,128,256]{1,0,2:T(2,128)(2,1)S(1)}, u32[]{:S(2)}, u32[]{:S(2)}) collective-permute-start(bf16[2,128,256]{1,0,2:T(2,128)(2,1)S(1)} %collective-permute-done.18), channel_id=1, source_target_pairs={{0,4},{4,8},{8,12},{12,14},{14,10},{10,6},{6,2},{2,0},{1,5},{5,9},... | collective-permute-start | bytes 393224 | tf_op jit(solution)/shard_map/ppermute | solution.py:180
  96.8 6.4 %collective-permute-start.23 = (bf16[2,128,256]{1,0,2:T(2,128)(2,1)S(1)}, bf16[2,128,256]{1,0,2:T(2,128)(2,1)S(1)}, u32[]{:S(2)}, u32[]{:S(2)}) collective-permute-start(bf16[2,128,256]{1,0,2:T(2,128)(2,1)S(1)} %collective-permute-done.22), channel_id=1, source_target_pairs={{0,2},{4,0},{8,4},{12,8},{14,12},{10,14},{6,10},{2,6},{1,3},{5,1},... | collective-permute-start | bytes 393224 | tf_op jit(solution)/shard_map/ppermute | solution.py:183
  99.3 5.0 %collective-permute-start.20 = (bf16[2,128,256]{1,0,2:T(2,128)(2,1)S(1)}, bf16[2,128,256]{1,0,2:T(2,128)(2,1)S(1)}, u32[]{:S(2)}, u32[]{:S(2)}) collective-permute-start(bf16[2,128,256]{1,0,2:T(2,128)(2,1)S(1)} %collective-permute-done.19), channel_id=1, source_target_pairs={{0,4},{4,8},{8,12},{12,14},{14,10},{10,6},{6,2},{2,0},{1,5},{5,9},... | collective-permute-start | bytes 393224 | tf_op jit(solution)/shard_map/ppermute | solution.py:180
  103.3 5.0 %collective-permute-start.24 = (bf16[2,128,256]{1,0,2:T(2,128)(2,1)S(1)}, bf16[2,128,256]{1,0,2:T(2,128)(2,1)S(1)}, u32[]{:S(2)}, u32[]{:S(2)}) collective-permute-start(bf16[2,128,256]{1,0,2:T(2,128)(2,1)S(1)} %collective-permute-done.23), channel_id=1, source_target_pairs={{0,2},{4,0},{8,4},{12,8},{14,12},{10,14},{6,10},{2,6},{1,3},{5,1},... | collective-permute-start | bytes 393224 | tf_op jit(solution)/shard_map/ppermute | solution.py:183
  104.3 5.0 %collective-permute-start.21 = (bf16[2,128,256]{1,0,2:T(2,128)(2,1)S(1)}, bf16[2,128,256]{1,0,2:T(2,128)(2,1)S(1)}, u32[]{:S(2)}, u32[]{:S(2)}) collective-permute-start(bf16[2,128,256]{1,0,2:T(2,128)(2,1)S(1)} %collective-permute-done.20), channel_id=1, source_target_pairs={{0,4},{4,8},{8,12},{12,14},{14,10},{10,6},{6,2},{2,0},{1,5},{5,9},... | collective-permute-start | bytes 393224 | tf_op jit(solution)/shard_map/ppermute | solution.py:180
  (10 other events, 33.8 us)

commit v20 on v17

--- a/solution.py
+++ b/solution.py
@@ -118,16 +118,14 @@
     late_tokens, _ = lax.optimization_barrier((tokens, first_arrival))
     partner_half = lax.ppermute(late_tokens, "groups", SWAP)
     partner_other = lax.ppermute(partner_half, "col", SWAP)
-    whole = jnp.where(
-        column == 0,
-        jnp.concatenate([tokens, other_half], axis=2),
-        jnp.concatenate([other_half, tokens], axis=2),
-    )
-    partner = jnp.where(
-        column == 0,
-        jnp.concatenate([partner_half, partner_other], axis=2),
-        jnp.concatenate([partner_other, partner_half], axis=2),
-    )
+    def in_feature_order(own, other):
+        half = own.shape[2]
+        placed = jnp.zeros(own.shape[:2] + (2 * half,), own.dtype)
+        placed = lax.dynamic_update_slice(placed, own, (0, 0, column * half))
+        return lax.dynamic_update_slice(placed, other, (0, 0, (1 - column) * half))
+
+    whole = in_feature_order(tokens, other_half)
+    partner = in_feature_order(partner_half, partner_other)
     both = jnp.concatenate([whole, partner], axis=0)
     widened = both.astype(jnp.float32)
     power = jnp.mean(widened * widened, axis=-1, keepdims=True)

time: 118 us -> 119 us (level)
  local copies, waits for them, and re-layouts: 32.2 us -> 35.7 us
  other arithmetic: 16.4 us -> 13.8 us
    select_n x2 -> x0, other arithmetic: 3.9 us -> none  [the longest x1 1.97 us: shards(): jnp.where(column == 0, jnp.concatenate([tokens, other_half], axis=2), jnp...]
    dynamic_update_slice x0 -> x4, local copies, waits for them, and re-layouts: none -> 1.65 us  [the longest x2 1.47 us: in_feature_order(): return lax.dynamic_update_slice(placed, other, (0, 0, (1 - column) * half))]
    unnamed x43 -> x51, local copies, waits for them, and re-layouts: 10.3 us -> 12 us
  transfers between devices with their start and end apart: 25 -> 25, of which waited for: 16 -> 14; matrix products, arithmetic and copies ran while one was open for 28% -> 28% of each run, Pallas kernels for 0% -> 0%
where the time goes in v20:
time: 119 us; the launch traced here: 118 us
  local copies, waits for them, and re-layouts  35.7 us (30%)
  waiting for transfers between devices  35.4 us (30%)
  starting transfers between devices  25.7 us (22%)
  other arithmetic  13.8 us (12%)
  matrix products  6.81 us (6%)
    ppermute x7, waiting for transfers between devices, gather_rows(): ahead = lax.ppermute(ahead, 'row', forward)  21.8 us
    ppermute x7, starting transfers between devices, gather_rows(): ahead = lax.ppermute(ahead, 'row', forward)  12.5 us
    unnamed x51, local copies, waits for them, and re-layouts  12 us
    ppermute x4, starting transfers between devices, shards(): ahead = lax.ppermute(ahead, 'row', forward)  6.54 us
    ppermute x4, waiting for transfers between devices, shards(): ahead = lax.ppermute(ahead, 'row', forward)  5.78 us
    ppermute x1, waiting for transfers between devices, shards(): returned = lax.ppermute(result[passages:], 'groups', SWAP)  5.4 us
    gather x1, local copies, waits for them, and re-layouts, gather_rows(): jnp.stack(ahead_parts)[ahead_pick]  3.89 us
    gather x1, local copies, waits for them, and re-layouts, gather_rows(): jnp.stack(behind_parts)[behind_pick]  3.89 us
  transfers between devices with their start and end apart: 25, of which 14 were waited for; matrix products, arithmetic and copies ran while one was open for 28% of the time, Pallas kernels for 0%

profile of v20, /device:TPU:0, one launch (start us, length us, event | category | flops | bytes accessed | tf_op | source)
XLA Modules:
  0.0 118.3 jit_solution(12318366644082305909)
XLA Ops:
  0.0 1.3 %constant_dynamic-update-slice_fusion.1 = bf16[448,1024]{1,0:T(8,128)(2,1)S(1)} fusion(bf16[448,896]{1,0:T(8,128)(2,1)} %param.14), kind=kLoop, calls=%fused_computation.87 | loop fusion | bytes 1605632
  2.7 3.1 %collective-permute-start.1 = (bf16[224,576]{1,0:T(8,128)(2,1)S(1)}, bf16[224,576]{1,0:T(8,128)(2,1)S(1)}, u32[]{:S(2)}, u32[]{:S(2)}) collective-permute-start(bf16[224,576]{1,0:T(8,128)(2,1)S(1)} %pad_maximum_fusion.5), channel_id=1, source_target_pairs={{0,4},{4,8},{8,12},{12,14},{14,10},{10,6},{6,2},{2,0},{1,5},{5,9},... | collective-permute-start | bytes 774152 | tf_op jit(solution)/shard_map/ppermute | solution.py:47
  12.5 1.8 %collective-permute-start.2 = (bf16[2,128,1792]{2,1,0:T(8,128)(2,1)S(1)}, bf16[2,128,1792]{2,1,0:T(8,128)(2,1)S(1)}, u32[]{:S(2)}, u32[]{:S(2)}) collective-permute-start(bf16[2,128,1792]{2,1,0:T(8,128)(2,1)S(1)} %copy-done.3), channel_id=1, source_target_pairs={{0,16},{16,0},{1,17},{17,1},{2,18},{18,2},{3,19},{19,3},{4,20},{20... | collective-permute-start | bytes 2752520 | tf_op jit(solution)/shard_map/ppermute | solution.py:119
  14.3 1.6 %collective-permute-start.4 = (bf16[224,576]{1,0:T(8,128)(2,1)S(1)}, bf16[224,576]{1,0:T(8,128)(2,1)S(1)}, u32[]{:S(2)}, u32[]{:S(2)}) collective-permute-start(bf16[224,576]{1,0:T(8,128)(2,1)S(1)} %collective-permute-done.1), channel_id=1, source_target_pairs={{0,4},{4,8},{8,12},{12,14},{14,10},{10,6},{6,2},{2,0},{1,5},{5,9},... | collective-permute-start | bytes 774152 | tf_op jit(solution)/shard_map/ppermute | solution.py:47
  17.0 1.7 %bitcast_dynamic-update-slice_fusion.6 = bf16[8,224,576]{2,1,0:T(8,128)(2,1)} fusion(bf16[8,224,576]{2,1,0:T(8,128)(2,1)} %bitcast_dynamic-update-slice_fusion.7, bf16[224,576]{1,0:T(8,128)(2,1)} %collective-permute-done.10), kind=kLoop, calls=%fused_computation.66 | loop fusion | bytes 573440
  18.7 4.0 %collective-permute-done.4 = bf16[224,576]{1,0:T(8,128)(2,1)S(1)} collective-permute-done((bf16[224,576]{1,0:T(8,128)(2,1)S(1)}, bf16[224,576]{1,0:T(8,128)(2,1)S(1)}, u32[]{:S(2)}, u32[]{:S(2)}) %collective-permute-start.4) | collective-permute-done | bytes 258080 | tf_op jit(solution)/shard_map/ppermute | solution.py:47
  22.8 1.6 %collective-permute-start.5 = (bf16[224,576]{1,0:T(8,128)(2,1)S(1)}, bf16[224,576]{1,0:T(8,128)(2,1)S(1)}, u32[]{:S(2)}, u32[]{:S(2)}) collective-permute-start(bf16[224,576]{1,0:T(8,128)(2,1)S(1)} %collective-permute-done.4), channel_id=1, source_target_pairs={{0,4},{4,8},{8,12},{12,14},{14,10},{10,6},{6,2},{2,0},{1,5},{5,9},... | collective-permute-start | bytes 774152 | tf_op jit(solution)/shard_map/ppermute | solution.py:47
  26.3 4.1 %collective-permute-done.5 = bf16[224,576]{1,0:T(8,128)(2,1)S(1)} collective-permute-done((bf16[224,576]{1,0:T(8,128)(2,1)S(1)}, bf16[224,576]{1,0:T(8,128)(2,1)S(1)}, u32[]{:S(2)}, u32[]{:S(2)}) %collective-permute-start.5) | collective-permute-done | bytes 258080 | tf_op jit(solution)/shard_map/ppermute | solution.py:47
  30.4 1.6 %collective-permute-start.6 = (bf16[224,576]{1,0:T(8,128)(2,1)S(1)}, bf16[224,576]{1,0:T(8,128)(2,1)S(1)}, u32[]{:S(2)}, u32[]{:S(2)}) collective-permute-start(bf16[224,576]{1,0:T(8,128)(2,1)S(1)} %collective-permute-done.5), channel_id=1, source_target_pairs={{0,4},{4,8},{8,12},{12,14},{14,10},{10,6},{6,2},{2,0},{1,5},{5,9},... | collective-permute-start | bytes 774152 | tf_op jit(solution)/shard_map/ppermute | solution.py:47
  33.9 3.4 %collective-permute-done.6 = bf16[224,576]{1,0:T(8,128)(2,1)S(1)} collective-permute-done((bf16[224,576]{1,0:T(8,128)(2,1)S(1)}, bf16[224,576]{1,0:T(8,128)(2,1)S(1)}, u32[]{:S(2)}, u32[]{:S(2)}) %collective-permute-start.6) | collective-permute-done | bytes 258080 | tf_op jit(solution)/shard_map/ppermute | solution.py:47
  37.3 1.6 %collective-permute-start.7 = (bf16[224,576]{1,0:T(8,128)(2,1)S(1)}, bf16[224,576]{1,0:T(8,128)(2,1)S(1)}, u32[]{:S(2)}, u32[]{:S(2)}) collective-permute-start(bf16[224,576]{1,0:T(8,128)(2,1)S(1)} %collective-permute-done.6), channel_id=1, source_target_pairs={{0,4},{4,8},{8,12},{12,14},{14,10},{10,6},{6,2},{2,0},{1,5},{5,9},... | collective-permute-start | bytes 774152 | tf_op jit(solution)/shard_map/ppermute | solution.py:47
  41.3 2.7 %collective-permute-done.7 = bf16[224,576]{1,0:T(8,128)(2,1)S(1)} collective-permute-done((bf16[224,576]{1,0:T(8,128)(2,1)S(1)}, bf16[224,576]{1,0:T(8,128)(2,1)S(1)}, u32[]{:S(2)}, u32[]{:S(2)}) %collective-permute-start.7) | collective-permute-done | bytes 258080 | tf_op jit(solution)/shard_map/ppermute | solution.py:47
  44.0 1.6 %collective-permute-start.8 = (bf16[224,576]{1,0:T(8,128)(2,1)S(1)}, bf16[224,576]{1,0:T(8,128)(2,1)S(1)}, u32[]{:S(2)}, u32[]{:S(2)}) collective-permute-start(bf16[224,576]{1,0:T(8,128)(2,1)S(1)} %collective-permute-done.7), channel_id=1, source_target_pairs={{0,4},{4,8},{8,12},{12,14},{14,10},{10,6},{6,2},{2,0},{1,5},{5,9},... | collective-permute-start | bytes 774152 | tf_op jit(solution)/shard_map/ppermute | solution.py:47
  47.5 3.7 %collective-permute-done.8 = bf16[224,576]{1,0:T(8,128)(2,1)S(1)} collective-permute-done((bf16[224,576]{1,0:T(8,128)(2,1)S(1)}, bf16[224,576]{1,0:T(8,128)(2,1)S(1)}, u32[]{:S(2)}, u32[]{:S(2)}) %collective-permute-start.8) | collective-permute-done | bytes 258080 | tf_op jit(solution)/shard_map/ppermute | solution.py:47
  51.2 1.6 %collective-permute-start.9 = (bf16[224,576]{1,0:T(8,128)(2,1)S(1)}, bf16[224,576]{1,0:T(8,128)(2,1)S(1)}, u32[]{:S(2)}, u32[]{:S(2)}) collective-permute-start(bf16[224,576]{1,0:T(8,128)(2,1)S(1)} %collective-permute-done.8), channel_id=1, source_target_pairs={{0,4},{4,8},{8,12},{12,14},{14,10},{10,6},{6,2},{2,0},{1,5},{5,9},... | collective-permute-start | bytes 774152 | tf_op jit(solution)/shard_map/ppermute | solution.py:47
  54.7 3.1 %collective-permute-done.9 = bf16[224,576]{1,0:T(8,128)(2,1)S(1)} collective-permute-done((bf16[224,576]{1,0:T(8,128)(2,1)S(1)}, bf16[224,576]{1,0:T(8,128)(2,1)S(1)}, u32[]{:S(2)}, u32[]{:S(2)}) %collective-permute-start.9) | collective-permute-done | bytes 258080 | tf_op jit(solution)/shard_map/ppermute | solution.py:47
  58.6 3.9 %gather_fusion = bf16[8,224,576]{2,1,0:T(8,128)(2,1)} fusion(bf16[8,224,576]{2,1,0:T(8,128)(2,1)} %bitcast_dynamic-update-slice_fusion.8, s32[1024]{0:T(1024)S(1)} %get-tuple-element.30), kind=kCustom, calls=%fused_computation | custom fusion | bytes 4128800 | tf_op jit(solution)/shard_map/gather | solution.py:56
  63.3 3.9 %gather_fusion.1 = bf16[8,224,576]{2,1,0:T(8,128)(2,1)} fusion(bf16[8,224,576]{2,1,0:T(8,128)(2,1)} %bitcast_dynamic-update-slice_fusion, s32[1024]{0:T(1024)S(1)} %get-tuple-element.29), kind=kCustom, calls=%fused_computation.1 | custom fusion | bytes 4128800 | tf_op jit(solution)/shard_map/gather | solution.py:56
  67.1 2.8 %pad_maximum_fusion = bf16[8,448,576]{2,1,0:T(8,128)(2,1)S(1)} fusion(bf16[8,224,576]{2,1,0:T(8,128)(2,1)} %gather_fusion.1, bf16[8,224,576]{2,1,0:T(8,128)(2,1)} %gather_fusion), kind=kLoop, calls=%fused_computation.12 | loop fusion | flops 8257536 | bytes 8257536 | tf_op jit(solution)/shard_map/concatenate | solution.py:55
  69.9 1.4 %constant_dynamic-update-slice_fusion.10 = bf16[2,128,3584]{2,1,0:T(8,128)(2,1)S(1)} fusion(bf16[2,128,3584]{2,1,0:T(8,128)(2,1)S(1)} %constant_dynamic-update-slice_fusion.11, bf16[2,128,1792]{2,1,0:T(8,128)(2,1)} %collective-permute-done.3, s32[]{:T(128)S(6)} %select_n.159), kind=kLoop, calls=%fused_computation.119 | loop fusion | bytes 1835012 | tf_op jit(solution)/shard_map/dynamic_update_slice | solution.py:125
  73.6 2.4 %convolution_add_fusion = f32[512,576]{0,1:T(8,128)S(1)} fusion(bf16[512,3584]{1,0:T(8,128)(2,1)S(1)} %bitcast.140, bf16[3584,576]{1,0:T(8,128)(2,1)S(1)} %bitcast.135, f32[576]{0:T(1024)S(1)} %maximum_select_fusion), kind=kOutput, calls=%fused_computation.28 | convolution fusion | flops 2114224128 | bytes 8980736 | tf_op jit(solution)/shard_map/dot_general | solution.py:139
  79.9 5.4 %collective-permute-done.17 = bf16[2,128,576]{1,0,2:T(2,128)(2,1)S(1)} collective-permute-done((bf16[2,128,576]{1,0,2:T(2,128)(2,1)S(1)}, bf16[2,128,576]{1,0,2:T(2,128)(2,1)S(1)}, u32[]{:S(2)}, u32[]{:S(2)}) %collective-permute-start.17) | collective-permute-done | bytes 294944 | tf_op jit(solution)/shard_map/ppermute | solution.py:150
  86.2 1.8 %collective-permute-start.18 = (bf16[2,128,256]{1,0,2:T(2,128)(2,1)S(1)}, bf16[2,128,256]{1,0,2:T(2,128)(2,1)S(1)}, u32[]{:S(2)}, u32[]{:S(2)}) collective-permute-start(bf16[2,128,256]{1,0,2:T(2,128)(2,1)S(1)} %pad_maximum_fusion.7), channel_id=1, source_target_pairs={{0,4},{4,8},{8,12},{12,14},{14,10},{10,6},{6,2},{2,0},{1,5},{5,9},... | collective-permute-start | bytes 393224 | tf_op jit(solution)/shard_map/ppermute | solution.py:169
  88.4 2.9 %collective-permute-done.18 = bf16[2,128,256]{1,0,2:T(2,128)(2,1)S(1)} collective-permute-done((bf16[2,128,256]{1,0,2:T(2,128)(2,1)S(1)}, bf16[2,128,256]{1,0,2:T(2,128)(2,1)S(1)}, u32[]{:S(2)}, u32[]{:S(2)}) %collective-permute-start.18) | collective-permute-done | bytes 131104 | tf_op jit(solution)/shard_map/ppermute | solution.py:169
  91.4 1.6 %collective-permute-start.19 = (bf16[2,128,256]{1,0,2:T(2,128)(2,1)S(1)}, bf16[2,128,256]{1,0,2:T(2,128)(2,1)S(1)}, u32[]{:S(2)}, u32[]{:S(2)}) collective-permute-start(bf16[2,128,256]{1,0,2:T(2,128)(2,1)S(1)} %collective-permute-done.18), channel_id=1, source_target_pairs={{0,4},{4,8},{8,12},{12,14},{14,10},{10,6},{6,2},{2,0},{1,5},{5,9},... | collective-permute-start | bytes 393224 | tf_op jit(solution)/shard_map/ppermute | solution.py:169
  95.1 1.8 %collective-permute-done.19 = bf16[2,128,256]{1,0,2:T(2,128)(2,1)S(1)} collective-permute-done((bf16[2,128,256]{1,0,2:T(2,128)(2,1)S(1)}, bf16[2,128,256]{1,0,2:T(2,128)(2,1)S(1)}, u32[]{:S(2)}, u32[]{:S(2)}) %collective-permute-start.19) | collective-permute-done | bytes 131104 | tf_op jit(solution)/shard_map/ppermute | solution.py:169
  96.9 1.6 %collective-permute-start.20 = (bf16[2,128,256]{1,0,2:T(2,128)(2,1)S(1)}, bf16[2,128,256]{1,0,2:T(2,128)(2,1)S(1)}, u32[]{:S(2)}, u32[]{:S(2)}) collective-permute-start(bf16[2,128,256]{1,0,2:T(2,128)(2,1)S(1)} %collective-permute-done.19), channel_id=1, source_target_pairs={{0,4},{4,8},{8,12},{12,14},{14,10},{10,6},{6,2},{2,0},{1,5},{5,9},... | collective-permute-start | bytes 393224 | tf_op jit(solution)/shard_map/ppermute | solution.py:169
  98.9 1.8 %copy.52 = bf16[2,2,64,7,128]{4,2,3,1,0:T(8,128)(2,1)S(1)} copy(bf16[2,2,64,7,128]{2,1,0,4,3:T(2,128)(2,1)S(1)} %reshape.378) | data formatting | bytes 917504 | tf_op jit(solution)/shard_map/reshape | solution.py:210
  101.9 1.6 %collective-permute-start.21 = (bf16[2,128,256]{1,0,2:T(2,128)(2,1)S(1)}, bf16[2,128,256]{1,0,2:T(2,128)(2,1)S(1)}, u32[]{:S(2)}, u32[]{:S(2)}) collective-permute-start(bf16[2,128,256]{1,0,2:T(2,128)(2,1)S(1)} %collective-permute-done.20), channel_id=1, source_target_pairs={{0,4},{4,8},{8,12},{12,14},{14,10},{10,6},{6,2},{2,0},{1,5},{5,9},... | collective-permute-start | bytes 393224 | tf_op jit(solution)/shard_map/ppermute | solution.py:169
  103.7 2.2 %collective-permute-done.24 = bf16[2,128,256]{1,0,2:T(2,128)(2,1)S(1)} collective-permute-done((bf16[2,128,256]{1,0,2:T(2,128)(2,1)S(1)}, bf16[2,128,256]{1,0,2:T(2,128)(2,1)S(1)}, u32[]{:S(2)}, u32[]{:S(2)}) %collective-permute-start.24) | collective-permute-done | bytes 131104 | tf_op jit(solution)/shard_map/ppermute | solution.py:172
  107.8 1.4 %gather_fusion.4 = bf16[12,64,256]{2,1,0:T(8,128)(2,1)} fusion(bf16[2,16,64,256]{3,2,0,1:T(8,128)(2,1)S(1)} %bitcast.132, s32[12]{0:T(128)S(1)} %reshape.346), kind=kCustom, calls=%fused_computation.4 | custom fusion | bytes 786528 | tf_op jit(solution)/shard_map/gather | solution.py:196
  117.0 1.3 %convert_element_type.60 = bf16[2,128,896]{2,1,0:T(8,128)(2,1)} reshape(bf16[2,2,64,7,128]{4,3,2,1,0:T(8,128)(2,1)S(1)} %copy.57) | data formatting | bytes 917504 | tf_op jit(solution)/shard_map/convert_element_type | solution.py:272
  (176 shorter events, 41.4 us)
Async XLA Ops:
  0.0 10.3 %copy-start = (s32[2,2,2]{2,1,0:T(2,128)S(1)}, s32[2,2,2]{2,1,0:T(2,128)}, u32[]{:S(2)}) copy-start(s32[2,2,2]{2,1,0:T(2,128)} %param.21) | copy-start | bytes 100
  2.4 7.8 %copy-start.11 = (f32[128]{0:T(128)S(1)}, f32[128]{0:T(128)}, u32[]{:S(2)}) copy-start(f32[128]{0:T(128)} %param.19) | copy-start | bytes 1540
  2.4 7.9 %copy-start.9 = (f32[896]{0:T(1024)S(1)}, f32[896]{0:T(1024)}, u32[]{:S(2)}) copy-start(f32[896]{0:T(1024)} %param.15) | copy-start | bytes 10756
  2.4 7.8 %copy-start.12 = (f32[128]{0:T(128)S(1)}, f32[128]{0:T(128)}, u32[]{:S(2)}) copy-start(f32[128]{0:T(128)} %param.17) | copy-start | bytes 1540
  2.5 8.8 %copy-start.10 = (s32[2,16,14,2]{1,3,2,0:T(2,128)S(1)}, s32[2,16,14,2]{1,3,2,0:T(2,128)}, u32[]{:S(2)}) copy-start(s32[2,16,14,2]{1,3,2,0:T(2,128)} %param.20) | copy-start | bytes 10756
  2.5 8.9 %slice-start = ((f32[896]{0:T(1024)}), f32[512]{0:T(512)S(1)}, s32[]{:S(2)}) async-start(f32[896]{0:T(1024)} %param.15), calls=%async_computation | async-start | bytes 4096 | tf_op jit(solution)/shard_map/slice | solution.py:113
  2.7 9.8 %collective-permute-start.1 = (bf16[224,576]{1,0:T(8,128)(2,1)S(1)}, bf16[224,576]{1,0:T(8,128)(2,1)S(1)}, u32[]{:S(2)}, u32[]{:S(2)}) collective-permute-start(bf16[224,576]{1,0:T(8,128)(2,1)S(1)} %pad_maximum_fusion.5), channel_id=1, source_target_pairs={{0,4},{4,8},{8,12},{12,14},{14,10},{10,6},{6,2},{2,0},{1,5},{5,9},... | collective-permute-start | bytes 774152 | tf_op jit(solution)/shard_map/ppermute | solution.py:47
  6.6 9.2 %collective-permute-start.10 = (bf16[224,576]{1,0:T(8,128)(2,1)}, bf16[224,576]{1,0:T(8,128)(2,1)}, u32[]{:S(2)}, u32[]{:S(2)}) collective-permute-start(bf16[224,576]{1,0:T(8,128)(2,1)} %pad_maximum_fusion.6), channel_id=1, source_target_pairs={{0,2},{4,0},{8,4},{12,8},{14,12},{10,14},{6,10},{2,6},{1,3},{5,1},... | collective-permute-start | bytes 774152 | tf_op jit(solution)/shard_map/ppermute | solution.py:48
  6.6 27.2 %collective-permute-start = (bf16[2,128,1792]{2,1,0:T(8,128)(2,1)S(1)}, bf16[2,128,1792]{2,1,0:T(8,128)(2,1)S(1)}, u32[]{:S(2)}, u32[]{:S(2)}) collective-permute-start(bf16[2,128,1792]{2,1,0:T(8,128)(2,1)S(1)} %copy-done.3), channel_id=1, source_target_pairs={{0,1},{1,0},{2,3},{3,2},{4,5},{5,4},{6,7},{7,6},{8,9},{9,8},{10,11... | collective-permute-start | bytes 2752520 | tf_op jit(solution)/shard_map/ppermute | solution.py:117
  12.5 28.5 %collective-permute-start.2 = (bf16[2,128,1792]{2,1,0:T(8,128)(2,1)S(1)}, bf16[2,128,1792]{2,1,0:T(8,128)(2,1)S(1)}, u32[]{:S(2)}, u32[]{:S(2)}) collective-permute-start(bf16[2,128,1792]{2,1,0:T(8,128)(2,1)S(1)} %copy-done.3), channel_id=1, source_target_pairs={{0,16},{16,0},{1,17},{17,1},{2,18},{18,2},{3,19},{19,3},{4,20},{20... | collective-permute-start | bytes 2752520 | tf_op jit(solution)/shard_map/ppermute | solution.py:119
  14.3 8.5 %collective-permute-start.4 = (bf16[224,576]{1,0:T(8,128)(2,1)S(1)}, bf16[224,576]{1,0:T(8,128)(2,1)S(1)}, u32[]{:S(2)}, u32[]{:S(2)}) collective-permute-start(bf16[224,576]{1,0:T(8,128)(2,1)S(1)} %collective-permute-done.1), channel_id=1, source_target_pairs={{0,4},{4,8},{8,12},{12,14},{14,10},{10,6},{6,2},{2,0},{1,5},{5,9},... | collective-permute-start | bytes 774152 | tf_op jit(solution)/shard_map/ppermute | solution.py:47
  15.8 8.5 %collective-permute-start.11 = (bf16[224,576]{1,0:T(8,128)(2,1)}, bf16[224,576]{1,0:T(8,128)(2,1)S(1)}, u32[]{:S(2)}, u32[]{:S(2)}) collective-permute-start(bf16[224,576]{1,0:T(8,128)(2,1)} %collective-permute-done.10), channel_id=1, source_target_pairs={{0,2},{4,0},{8,4},{12,8},{14,12},{10,14},{6,10},{2,6},{1,3},{5,1},... | collective-permute-start | bytes 774152 | tf_op jit(solution)/shard_map/ppermute | solution.py:48
  22.8 7.6 %collective-permute-start.5 = (bf16[224,576]{1,0:T(8,128)(2,1)S(1)}, bf16[224,576]{1,0:T(8,128)(2,1)S(1)}, u32[]{:S(2)}, u32[]{:S(2)}) collective-permute-start(bf16[224,576]{1,0:T(8,128)(2,1)S(1)} %collective-permute-done.4), channel_id=1, source_target_pairs={{0,4},{4,8},{8,12},{12,14},{14,10},{10,6},{6,2},{2,0},{1,5},{5,9},... | collective-permute-start | bytes 774152 | tf_op jit(solution)/shard_map/ppermute | solution.py:47
  24.3 7.6 %collective-permute-start.12 = (bf16[224,576]{1,0:T(8,128)(2,1)S(1)}, bf16[224,576]{1,0:T(8,128)(2,1)S(1)}, u32[]{:S(2)}, u32[]{:S(2)}) collective-permute-start(bf16[224,576]{1,0:T(8,128)(2,1)S(1)} %collective-permute-done.11), channel_id=1, source_target_pairs={{0,2},{4,0},{8,4},{12,8},{14,12},{10,14},{6,10},{2,6},{1,3},{5,1},... | collective-permute-start | bytes 774152 | tf_op jit(solution)/shard_map/ppermute | solution.py:48
  30.4 7.0 %collective-permute-start.6 = (bf16[224,576]{1,0:T(8,128)(2,1)S(1)}, bf16[224,576]{1,0:T(8,128)(2,1)S(1)}, u32[]{:S(2)}, u32[]{:S(2)}) collective-permute-start(bf16[224,576]{1,0:T(8,128)(2,1)S(1)} %collective-permute-done.5), channel_id=1, source_target_pairs={{0,4},{4,8},{8,12},{12,14},{14,10},{10,6},{6,2},{2,0},{1,5},{5,9},... | collective-permute-start | bytes 774152 | tf_op jit(solution)/shard_map/ppermute | solution.py:47
  31.9 7.2 %collective-permute-start.13 = (bf16[224,576]{1,0:T(8,128)(2,1)S(1)}, bf16[224,576]{1,0:T(8,128)(2,1)S(1)}, u32[]{:S(2)}, u32[]{:S(2)}) collective-permute-start(bf16[224,576]{1,0:T(8,128)(2,1)S(1)} %collective-permute-done.12), channel_id=1, source_target_pairs={{0,2},{4,0},{8,4},{12,8},{14,12},{10,14},{6,10},{2,6},{1,3},{5,1},... | collective-permute-start | bytes 774152 | tf_op jit(solution)/shard_map/ppermute | solution.py:48
  33.9 7.3 %copy-start.1 = (bf16[2,128,3584]{2,1,0:T(8,128)(2,1)}, bf16[2,128,3584]{2,1,0:T(8,128)(2,1)S(1)}, u32[]{:S(2)}) copy-start(bf16[2,128,3584]{2,1,0:T(8,128)(2,1)S(1)} %constant_dynamic-update-slice_fusion.12) | copy-start | bytes 5505028
  37.3 6.6 %collective-permute-start.7 = (bf16[224,576]{1,0:T(8,128)(2,1)S(1)}, bf16[224,576]{1,0:T(8,128)(2,1)S(1)}, u32[]{:S(2)}, u32[]{:S(2)}) collective-permute-start(bf16[224,576]{1,0:T(8,128)(2,1)S(1)} %collective-permute-done.6), channel_id=1, source_target_pairs={{0,4},{4,8},{8,12},{12,14},{14,10},{10,6},{6,2},{2,0},{1,5},{5,9},... | collective-permute-start | bytes 774152 | tf_op jit(solution)/shard_map/ppermute | solution.py:47
  39.1 7.2 %collective-permute-start.14 = (bf16[224,576]{1,0:T(8,128)(2,1)S(1)}, bf16[224,576]{1,0:T(8,128)(2,1)S(1)}, u32[]{:S(2)}, u32[]{:S(2)}) collective-permute-start(bf16[224,576]{1,0:T(8,128)(2,1)S(1)} %collective-permute-done.13), channel_id=1, source_target_pairs={{0,2},{4,0},{8,4},{12,8},{14,12},{10,14},{6,10},{2,6},{1,3},{5,1},... | collective-permute-start | bytes 774152 | tf_op jit(solution)/shard_map/ppermute | solution.py:48
  41.0 28.9 %collective-permute-start.3 = (bf16[2,128,1792]{2,1,0:T(8,128)(2,1)S(1)}, bf16[2,128,1792]{2,1,0:T(8,128)(2,1)}, u32[]{:S(2)}, u32[]{:S(2)}) collective-permute-start(bf16[2,128,1792]{2,1,0:T(8,128)(2,1)S(1)} %collective-permute-done.2), channel_id=1, source_target_pairs={{0,1},{1,0},{2,3},{3,2},{4,5},{5,4},{6,7},{7,6},{8,9},{9,8},{10,11... | collective-permute-start | bytes 2752520 | tf_op jit(solution)/shard_map/ppermute | solution.py:120
  44.0 7.3 %collective-permute-start.8 = (bf16[224,576]{1,0:T(8,128)(2,1)S(1)}, bf16[224,576]{1,0:T(8,128)(2,1)S(1)}, u32[]{:S(2)}, u32[]{:S(2)}) collective-permute-start(bf16[224,576]{1,0:T(8,128)(2,1)S(1)} %collective-permute-done.7), channel_id=1, source_target_pairs={{0,4},{4,8},{8,12},{12,14},{14,10},{10,6},{6,2},{2,0},{1,5},{5,9},... | collective-permute-start | bytes 774152 | tf_op jit(solution)/shard_map/ppermute | solution.py:47
  46.3 7.3 %collective-permute-start.15 = (bf16[224,576]{1,0:T(8,128)(2,1)S(1)}, bf16[224,576]{1,0:T(8,128)(2,1)S(1)}, u32[]{:S(2)}, u32[]{:S(2)}) collective-permute-start(bf16[224,576]{1,0:T(8,128)(2,1)S(1)} %collective-permute-done.14), channel_id=1, source_target_pairs={{0,2},{4,0},{8,4},{12,8},{14,12},{10,14},{6,10},{2,6},{1,3},{5,1},... | collective-permute-start | bytes 774152 | tf_op jit(solution)/shard_map/ppermute | solution.py:48
  51.2 6.6 %collective-permute-start.9 = (bf16[224,576]{1,0:T(8,128)(2,1)S(1)}, bf16[224,576]{1,0:T(8,128)(2,1)S(1)}, u32[]{:S(2)}, u32[]{:S(2)}) collective-permute-start(bf16[224,576]{1,0:T(8,128)(2,1)S(1)} %collective-permute-done.8), channel_id=1, source_target_pairs={{0,4},{4,8},{8,12},{12,14},{14,10},{10,6},{6,2},{2,0},{1,5},{5,9},... | collective-permute-start | bytes 774152 | tf_op jit(solution)/shard_map/ppermute | solution.py:47
  53.6 8.9 %collective-permute-start.16 = (bf16[224,576]{1,0:T(8,128)(2,1)S(1)}, bf16[224,576]{1,0:T(8,128)(2,1)S(1)}, u32[]{:S(2)}, u32[]{:S(2)}) collective-permute-start(bf16[224,576]{1,0:T(8,128)(2,1)S(1)} %collective-permute-done.15), channel_id=1, source_target_pairs={{0,2},{4,0},{8,4},{12,8},{14,12},{10,14},{6,10},{2,6},{1,3},{5,1},... | collective-permute-start | bytes 774152 | tf_op jit(solution)/shard_map/ppermute | solution.py:48
  78.5 6.8 %collective-permute-start.17 = (bf16[2,128,576]{1,0,2:T(2,128)(2,1)S(1)}, bf16[2,128,576]{1,0,2:T(2,128)(2,1)S(1)}, u32[]{:S(2)}, u32[]{:S(2)}) collective-permute-start(bf16[2,128,576]{1,0,2:T(2,128)(2,1)S(1)} %fusion.23), channel_id=1, source_target_pairs={{0,16},{16,0},{1,17},{17,1},{2,18},{18,2},{3,19},{19,3},{4,20},{20... | collective-permute-start | bytes 884744 | tf_op jit(solution)/shard_map/ppermute | solution.py:150
  86.2 5.2 %collective-permute-start.18 = (bf16[2,128,256]{1,0,2:T(2,128)(2,1)S(1)}, bf16[2,128,256]{1,0,2:T(2,128)(2,1)S(1)}, u32[]{:S(2)}, u32[]{:S(2)}) collective-permute-start(bf16[2,128,256]{1,0,2:T(2,128)(2,1)S(1)} %pad_maximum_fusion.7), channel_id=1, source_target_pairs={{0,4},{4,8},{8,12},{12,14},{14,10},{10,6},{6,2},{2,0},{1,5},{5,9},... | collective-permute-start | bytes 393224 | tf_op jit(solution)/shard_map/ppermute | solution.py:169
  88.0 5.9 %collective-permute-start.22 = (bf16[2,128,256]{1,0,2:T(2,128)(2,1)S(1)}, bf16[2,128,256]{1,0,2:T(2,128)(2,1)S(1)}, u32[]{:S(2)}, u32[]{:S(2)}) collective-permute-start(bf16[2,128,256]{1,0,2:T(2,128)(2,1)S(1)} %pad_maximum_fusion.7), channel_id=1, source_target_pairs={{0,2},{4,0},{8,4},{12,8},{14,12},{10,14},{6,10},{2,6},{1,3},{5,1},... | collective-permute-start | bytes 393224 | tf_op jit(solution)/shard_map/ppermute | solution.py:172
  91.4 5.5 %collective-permute-start.19 = (bf16[2,128,256]{1,0,2:T(2,128)(2,1)S(1)}, bf16[2,128,256]{1,0,2:T(2,128)(2,1)S(1)}, u32[]{:S(2)}, u32[]{:S(2)}) collective-permute-start(bf16[2,128,256]{1,0,2:T(2,128)(2,1)S(1)} %collective-permute-done.18), channel_id=1, source_target_pairs={{0,4},{4,8},{8,12},{12,14},{14,10},{10,6},{6,2},{2,0},{1,5},{5,9},... | collective-permute-start | bytes 393224 | tf_op jit(solution)/shard_map/ppermute | solution.py:169
  93.9 7.0 %collective-permute-start.23 = (bf16[2,128,256]{1,0,2:T(2,128)(2,1)S(1)}, bf16[2,128,256]{1,0,2:T(2,128)(2,1)S(1)}, u32[]{:S(2)}, u32[]{:S(2)}) collective-permute-start(bf16[2,128,256]{1,0,2:T(2,128)(2,1)S(1)} %collective-permute-done.22), channel_id=1, source_target_pairs={{0,2},{4,0},{8,4},{12,8},{14,12},{10,14},{6,10},{2,6},{1,3},{5,1},... | collective-permute-start | bytes 393224 | tf_op jit(solution)/shard_map/ppermute | solution.py:172
  96.9 5.0 %collective-permute-start.20 = (bf16[2,128,256]{1,0,2:T(2,128)(2,1)S(1)}, bf16[2,128,256]{1,0,2:T(2,128)(2,1)S(1)}, u32[]{:S(2)}, u32[]{:S(2)}) collective-permute-start(bf16[2,128,256]{1,0,2:T(2,128)(2,1)S(1)} %collective-permute-done.19), channel_id=1, source_target_pairs={{0,4},{4,8},{8,12},{12,14},{14,10},{10,6},{6,2},{2,0},{1,5},{5,9},... | collective-permute-start | bytes 393224 | tf_op jit(solution)/shard_map/ppermute | solution.py:169
  100.9 5.0 %collective-permute-start.24 = (bf16[2,128,256]{1,0,2:T(2,128)(2,1)S(1)}, bf16[2,128,256]{1,0,2:T(2,128)(2,1)S(1)}, u32[]{:S(2)}, u32[]{:S(2)}) collective-permute-start(bf16[2,128,256]{1,0,2:T(2,128)(2,1)S(1)} %collective-permute-done.23), channel_id=1, source_target_pairs={{0,2},{4,0},{8,4},{12,8},{14,12},{10,14},{6,10},{2,6},{1,3},{5,1},... | collective-permute-start | bytes 393224 | tf_op jit(solution)/shard_map/ppermute | solution.py:172
  101.9 5.0 %collective-permute-start.21 = (bf16[2,128,256]{1,0,2:T(2,128)(2,1)S(1)}, bf16[2,128,256]{1,0,2:T(2,128)(2,1)S(1)}, u32[]{:S(2)}, u32[]{:S(2)}) collective-permute-start(bf16[2,128,256]{1,0,2:T(2,128)(2,1)S(1)} %collective-permute-done.20), channel_id=1, source_target_pairs={{0,4},{4,8},{8,12},{12,14},{14,10},{10,6},{6,2},{2,0},{1,5},{5,9},... | collective-permute-start | bytes 393224 | tf_op jit(solution)/shard_map/ppermute | solution.py:169
  (9 other events, 26.4 us)

commit v21 on v17

--- a/solution.py
+++ b/solution.py
@@ -114,21 +114,15 @@
         jnp.concatenate([rotary_b[split:], value_bias[value_split:]]),
     )
 
-    other_half = lax.ppermute(tokens, "col", SWAP)
     late_tokens, _ = lax.optimization_barrier((tokens, first_arrival))
     partner_half = lax.ppermute(late_tokens, "groups", SWAP)
-    partner_other = lax.ppermute(partner_half, "col", SWAP)
-    whole = jnp.where(
+    halves = jnp.concatenate([tokens, partner_half], axis=0)
+    other_halves = lax.ppermute(halves, "col", SWAP)
+    both = jnp.where(
         column == 0,
-        jnp.concatenate([tokens, other_half], axis=2),
-        jnp.concatenate([other_half, tokens], axis=2),
-    )
-    partner = jnp.where(
-        column == 0,
-        jnp.concatenate([partner_half, partner_other], axis=2),
-        jnp.concatenate([partner_other, partner_half], axis=2),
-    )
-    both = jnp.concatenate([whole, partner], axis=0)
+        jnp.concatenate([halves, other_halves], axis=2),
+        jnp.concatenate([other_halves, halves], axis=2),
+    )
     widened = both.astype(jnp.float32)
     power = jnp.mean(widened * widened, axis=-1, keepdims=True)
     normed = (

time: 118 us -> 124 us (1.051)
  matrix products: 6.81 us -> 11.5 us
  waiting for transfers between devices: 36.2 us -> 38.9 us
  local copies, waits for them, and re-layouts: 32.2 us -> 30.4 us
    dot_general x1, matrix products: 2.37 us -> 7.02 us  [shards(): jnp.dot(normed, full_panel, preferred_element_type=jnp.float32) + panel_bias]
    select_n x2 -> x0, other arithmetic: 3.9 us -> none  [the longest x1 1.97 us: shards(): jnp.where(column == 0, jnp.concatenate([tokens, other_half], axis=2), jnp...]
    reduce_sum x1, other arithmetic: 0.79 us -> 4.48 us  [shards(): power = jnp.mean(widened * widened, axis=-1, keepdims=True)]
    ppermute x7, waiting for transfers between devices: 21.2 us -> 24.5 us  [gather_rows(): ahead = lax.ppermute(ahead, 'row', forward)]
    concatenate x2, other arithmetic: 0.05 us -> 1.49 us  [panel_rows(): jnp.concatenate([lax.dynamic_slice_in_dim(rotary_w[start:stop], group * s...]
    gather x1, local copies, waits for them, and re-layouts: 3.9 us -> 2.61 us  [gather_rows(): jnp.stack(ahead_parts)[ahead_pick]]
    unnamed x43 -> x44, local copies, waits for them, and re-layouts: 10.3 us -> 9.64 us
  transfers between devices with their start and end apart: 25 -> 24, of which waited for: 16 -> 15; matrix products, arithmetic and copies ran while one was open for 28% -> 23% of each run, Pallas kernels for 0% -> 0%
where the time goes in v21:
time: 124 us; the launch traced here: 123 us
  waiting for transfers between devices  38.9 us (31%)
  local copies, waits for them, and re-layouts  30.4 us (25%)
  starting transfers between devices  25.2 us (20%)
  other arithmetic  16.3 us (13%)
  matrix products  11.5 us (9%)
    ppermute x7, waiting for transfers between devices, gather_rows(): ahead = lax.ppermute(ahead, 'row', forward)  24.5 us
    ppermute x7, starting transfers between devices, gather_rows(): ahead = lax.ppermute(ahead, 'row', forward)  12.5 us
    unnamed x44, local copies, waits for them, and re-layouts  9.64 us
    dot_general x1, matrix products, shards(): jnp.dot(normed, full_panel, preferred_element_type=jnp.float32) + panel_bias  7.02 us
    ppermute x4, starting transfers between devices, shards(): ahead = lax.ppermute(ahead, 'row', forward)  6.37 us
    ppermute x1, waiting for transfers between devices, shards(): returned = lax.ppermute(result[passages:], 'groups', SWAP)  6.03 us
    ppermute x4, waiting for transfers between devices, shards(): ahead = lax.ppermute(ahead, 'row', forward)  5.74 us
    reduce_sum x1, other arithmetic, shards(): power = jnp.mean(widened * widened, axis=-1, keepdims=True)  4.48 us
  transfers between devices with their start and end apart: 24, of which 15 were waited for; matrix products, arithmetic and copies ran while one was open for 23% of the time, Pallas kernels for 0%

profile of v21, /device:TPU:0, one launch (start us, length us, event | category | flops | bytes accessed | tf_op | source)
XLA Modules:
  0.0 123.1 jit_solution(719890230750307939)
XLA Ops:
  3.3 3.0 %collective-permute-start = (bf16[224,576]{1,0:T(8,128)(2,1)}, bf16[224,576]{1,0:T(8,128)(2,1)S(1)}, u32[]{:S(2)}, u32[]{:S(2)}) collective-permute-start(bf16[224,576]{1,0:T(8,128)(2,1)} %pad_maximum_fusion.4), channel_id=1, source_target_pairs={{0,4},{4,8},{8,12},{12,14},{14,10},{10,6},{6,2},{2,0},{1,5},{5,9},... | collective-permute-start | bytes 774152 | tf_op jit(solution)/shard_map/ppermute | solution.py:47
  11.9 2.2 %constant_dynamic-update-slice_fusion.3 = bf16[4,128,1792]{2,1,0:T(8,128)(2,1)} fusion(bf16[2,128,1792]{2,1,0:T(8,128)(2,1)} %param.12), kind=kLoop, calls=%fused_computation.95 | loop fusion | bytes 1835008
  14.0 2.0 %collective-permute-start.1 = (bf16[2,128,1792]{2,1,0:T(8,128)(2,1)}, bf16[2,128,1792]{2,1,0:T(8,128)(2,1)S(1)}, u32[]{:S(2)}, u32[]{:S(2)}) collective-permute-start(bf16[2,128,1792]{2,1,0:T(8,128)(2,1)} %param.12), channel_id=1, source_target_pairs={{0,16},{16,0},{1,17},{17,1},{2,18},{18,2},{3,19},{19,3},{4,20},{20... | collective-permute-start | bytes 2752520 | tf_op jit(solution)/shard_map/ppermute | solution.py:118
  16.0 1.6 %collective-permute-start.3 = (bf16[224,576]{1,0:T(8,128)(2,1)S(1)}, bf16[224,576]{1,0:T(8,128)(2,1)S(1)}, u32[]{:S(2)}, u32[]{:S(2)}) collective-permute-start(bf16[224,576]{1,0:T(8,128)(2,1)S(1)} %collective-permute-done), channel_id=1, source_target_pairs={{0,4},{4,8},{8,12},{12,14},{14,10},{10,6},{6,2},{2,0},{1,5},{5,9},... | collective-permute-start | bytes 774152 | tf_op jit(solution)/shard_map/ppermute | solution.py:47
  18.8 4.9 %collective-permute-done.3 = bf16[224,576]{1,0:T(8,128)(2,1)S(1)} collective-permute-done((bf16[224,576]{1,0:T(8,128)(2,1)S(1)}, bf16[224,576]{1,0:T(8,128)(2,1)S(1)}, u32[]{:S(2)}, u32[]{:S(2)}) %collective-permute-start.3) | collective-permute-done | bytes 258080 | tf_op jit(solution)/shard_map/ppermute | solution.py:47
  23.7 1.6 %collective-permute-start.4 = (bf16[224,576]{1,0:T(8,128)(2,1)S(1)}, bf16[224,576]{1,0:T(8,128)(2,1)S(1)}, u32[]{:S(2)}, u32[]{:S(2)}) collective-permute-start(bf16[224,576]{1,0:T(8,128)(2,1)S(1)} %collective-permute-done.3), channel_id=1, source_target_pairs={{0,4},{4,8},{8,12},{12,14},{14,10},{10,6},{6,2},{2,0},{1,5},{5,9},... | collective-permute-start | bytes 774152 | tf_op jit(solution)/shard_map/ppermute | solution.py:47
  26.5 4.2 %collective-permute-done.4 = bf16[224,576]{1,0:T(8,128)(2,1)S(1)} collective-permute-done((bf16[224,576]{1,0:T(8,128)(2,1)S(1)}, bf16[224,576]{1,0:T(8,128)(2,1)S(1)}, u32[]{:S(2)}, u32[]{:S(2)}) %collective-permute-start.4) | collective-permute-done | bytes 258080 | tf_op jit(solution)/shard_map/ppermute | solution.py:47
  30.7 1.6 %collective-permute-start.5 = (bf16[224,576]{1,0:T(8,128)(2,1)S(1)}, bf16[224,576]{1,0:T(8,128)(2,1)S(1)}, u32[]{:S(2)}, u32[]{:S(2)}) collective-permute-start(bf16[224,576]{1,0:T(8,128)(2,1)S(1)} %collective-permute-done.4), channel_id=1, source_target_pairs={{0,4},{4,8},{8,12},{12,14},{14,10},{10,6},{6,2},{2,0},{1,5},{5,9},... | collective-permute-start | bytes 774152 | tf_op jit(solution)/shard_map/ppermute | solution.py:47
  33.6 4.8 %collective-permute-done.5 = bf16[224,576]{1,0:T(8,128)(2,1)S(1)} collective-permute-done((bf16[224,576]{1,0:T(8,128)(2,1)S(1)}, bf16[224,576]{1,0:T(8,128)(2,1)S(1)}, u32[]{:S(2)}, u32[]{:S(2)}) %collective-permute-start.5) | collective-permute-done | bytes 258080 | tf_op jit(solution)/shard_map/ppermute | solution.py:47
  38.3 1.6 %collective-permute-start.6 = (bf16[224,576]{1,0:T(8,128)(2,1)S(1)}, bf16[224,576]{1,0:T(8,128)(2,1)S(1)}, u32[]{:S(2)}, u32[]{:S(2)}) collective-permute-start(bf16[224,576]{1,0:T(8,128)(2,1)S(1)} %collective-permute-done.5), channel_id=1, source_target_pairs={{0,4},{4,8},{8,12},{12,14},{14,10},{10,6},{6,2},{2,0},{1,5},{5,9},... | collective-permute-start | bytes 774152 | tf_op jit(solution)/shard_map/ppermute | solution.py:47
  42.4 2.6 %collective-permute-done.6 = bf16[224,576]{1,0:T(8,128)(2,1)S(1)} collective-permute-done((bf16[224,576]{1,0:T(8,128)(2,1)S(1)}, bf16[224,576]{1,0:T(8,128)(2,1)S(1)}, u32[]{:S(2)}, u32[]{:S(2)}) %collective-permute-start.6) | collective-permute-done | bytes 258080 | tf_op jit(solution)/shard_map/ppermute | solution.py:47
  45.0 1.6 %collective-permute-start.7 = (bf16[224,576]{1,0:T(8,128)(2,1)S(1)}, bf16[224,576]{1,0:T(8,128)(2,1)S(1)}, u32[]{:S(2)}, u32[]{:S(2)}) collective-permute-start(bf16[224,576]{1,0:T(8,128)(2,1)S(1)} %collective-permute-done.6), channel_id=1, source_target_pairs={{0,4},{4,8},{8,12},{12,14},{14,10},{10,6},{6,2},{2,0},{1,5},{5,9},... | collective-permute-start | bytes 774152 | tf_op jit(solution)/shard_map/ppermute | solution.py:47
  47.9 4.3 %collective-permute-done.7 = bf16[224,576]{1,0:T(8,128)(2,1)S(1)} collective-permute-done((bf16[224,576]{1,0:T(8,128)(2,1)S(1)}, bf16[224,576]{1,0:T(8,128)(2,1)S(1)}, u32[]{:S(2)}, u32[]{:S(2)}) %collective-permute-start.7) | collective-permute-done | bytes 258080 | tf_op jit(solution)/shard_map/ppermute | solution.py:47
  52.2 1.6 %collective-permute-start.8 = (bf16[224,576]{1,0:T(8,128)(2,1)S(1)}, bf16[224,576]{1,0:T(8,128)(2,1)S(1)}, u32[]{:S(2)}, u32[]{:S(2)}) collective-permute-start(bf16[224,576]{1,0:T(8,128)(2,1)S(1)} %collective-permute-done.7), channel_id=1, source_target_pairs={{0,4},{4,8},{8,12},{12,14},{14,10},{10,6},{6,2},{2,0},{1,5},{5,9},... | collective-permute-start | bytes 774152 | tf_op jit(solution)/shard_map/ppermute | solution.py:47
  55.2 3.7 %collective-permute-done.8 = bf16[224,576]{1,0:T(8,128)(2,1)S(1)} collective-permute-done((bf16[224,576]{1,0:T(8,128)(2,1)S(1)}, bf16[224,576]{1,0:T(8,128)(2,1)S(1)}, u32[]{:S(2)}, u32[]{:S(2)}) %collective-permute-start.8) | collective-permute-done | bytes 258080 | tf_op jit(solution)/shard_map/ppermute | solution.py:47
  58.9 1.4 %copy-done.1 = bf16[8,224,576]{2,1,0:T(8,128)(2,1)} copy-done((bf16[8,224,576]{2,1,0:T(8,128)(2,1)}, bf16[8,224,576]{2,1,0:T(8,128)(2,1)S(1)}, u32[]{:S(2)}) %copy-start.1) | copy-done | bytes 2064408
  60.3 2.6 %gather_fusion = bf16[8,224,576]{2,1,0:T(8,128)(2,1)S(1)} fusion(bf16[8,224,576]{2,1,0:T(8,128)(2,1)} %copy-done.1, s32[1024]{0:T(1024)S(1)} %get-tuple-element.30), kind=kCustom, calls=%fused_computation | custom fusion | bytes 4128800 | tf_op jit(solution)/shard_map/gather | solution.py:56
  63.7 3.9 %gather_fusion.1 = bf16[8,224,576]{2,1,0:T(8,128)(2,1)} fusion(bf16[8,224,576]{2,1,0:T(8,128)(2,1)} %bitcast_dynamic-update-slice_fusion, s32[1024]{0:T(1024)S(1)} %get-tuple-element.29), kind=kCustom, calls=%fused_computation.1 | custom fusion | bytes 4128800 | tf_op jit(solution)/shard_map/gather | solution.py:56
  67.6 2.1 %pad_maximum_fusion = bf16[8,448,576]{2,1,0:T(8,128)(2,1)S(1)} fusion(bf16[8,224,576]{2,1,0:T(8,128)(2,1)} %gather_fusion.1, bf16[8,224,576]{2,1,0:T(8,128)(2,1)S(1)} %gather_fusion), kind=kLoop, calls=%fused_computation.9 | loop fusion | flops 8257536 | bytes 8257536 | tf_op jit(solution)/shard_map/concatenate | solution.py:55
  69.7 4.5 %multiply_reduce_fusion = f32[4,128]{1,0:T(4,128)S(1)} fusion(bf16[4,128,1792]{2,1,0:T(8,128)(2,1)} %collective-permute-done.2, bf16[4,128,1792]{2,1,0:T(8,128)(2,1)} %constant_dynamic-update-slice_fusion.2, pred[]{:T(512)S(6)} %eq.13), kind=kLoop, calls=%fused_computation.8 | loop fusion | flops 22019584 | bytes 3672065 | tf_op jit(solution)/shard_map/reduce_sum | solution.py:127
  74.2 7.0 %fusion.11 = f32[512,576]{0,1:T(8,128)S(1)} fusion(bf16[3584,576]{1,0:T(8,128)(2,1)S(1)} %bitcast.137, bf16[512,1792]{1,0:T(8,128)(2,1)} %bitcast.1, bf16[512,1792]{1,0:T(8,128)(2,1)} %bitcast, f32[3584]{0:T(1024)S(1)} %copy-done.8, f32[512]{0:T(512)S(1)} %rsqrt_bitcast_fusion, pred[]{:T(512)S(6)} %eq.13, f32[576]{0:T(1024)S(1)} %maximum_select_fusion.3), kind=kOutput, calls=%fused_computation.27 | convolution fusion | flops 2138079232 | bytes 8997121 | tf_op jit(solution)/shard_map/dot_general | solution.py:135
  84.1 6.0 %collective-permute-done.16 = bf16[2,128,576]{1,0,2:T(2,128)(2,1)S(1)} collective-permute-done((bf16[2,128,576]{1,0,2:T(2,128)(2,1)S(1)}, bf16[2,128,576]{1,0,2:T(2,128)(2,1)S(1)}, u32[]{:S(2)}, u32[]{:S(2)}) %collective-permute-start.16) | collective-permute-done | bytes 294944 | tf_op jit(solution)/shard_map/ppermute | solution.py:146
  91.0 1.6 %collective-permute-start.17 = (bf16[2,128,256]{1,0,2:T(2,128)(2,1)S(1)}, bf16[2,128,256]{1,0,2:T(2,128)(2,1)S(1)}, u32[]{:S(2)}, u32[]{:S(2)}) collective-permute-start(bf16[2,128,256]{1,0,2:T(2,128)(2,1)S(1)} %pad_maximum_fusion.6), channel_id=1, source_target_pairs={{0,4},{4,8},{8,12},{12,14},{14,10},{10,6},{6,2},{2,0},{1,5},{5,9},... | collective-permute-start | bytes 393224 | tf_op jit(solution)/shard_map/ppermute | solution.py:165
  93.1 2.9 %collective-permute-done.17 = bf16[2,128,256]{1,0,2:T(2,128)(2,1)S(1)} collective-permute-done((bf16[2,128,256]{1,0,2:T(2,128)(2,1)S(1)}, bf16[2,128,256]{1,0,2:T(2,128)(2,1)S(1)}, u32[]{:S(2)}, u32[]{:S(2)}) %collective-permute-start.17) | collective-permute-done | bytes 131104 | tf_op jit(solution)/shard_map/ppermute | solution.py:165
  96.1 1.6 %collective-permute-start.18 = (bf16[2,128,256]{1,0,2:T(2,128)(2,1)S(1)}, bf16[2,128,256]{1,0,2:T(2,128)(2,1)S(1)}, u32[]{:S(2)}, u32[]{:S(2)}) collective-permute-start(bf16[2,128,256]{1,0,2:T(2,128)(2,1)S(1)} %collective-permute-done.17), channel_id=1, source_target_pairs={{0,4},{4,8},{8,12},{12,14},{14,10},{10,6},{6,2},{2,0},{1,5},{5,9},... | collective-permute-start | bytes 393224 | tf_op jit(solution)/shard_map/ppermute | solution.py:165
  100.0 1.8 %collective-permute-done.18 = bf16[2,128,256]{1,0,2:T(2,128)(2,1)S(1)} collective-permute-done((bf16[2,128,256]{1,0,2:T(2,128)(2,1)S(1)}, bf16[2,128,256]{1,0,2:T(2,128)(2,1)S(1)}, u32[]{:S(2)}, u32[]{:S(2)}) %collective-permute-start.18) | collective-permute-done | bytes 131104 | tf_op jit(solution)/shard_map/ppermute | solution.py:165
  101.7 1.6 %collective-permute-start.19 = (bf16[2,128,256]{1,0,2:T(2,128)(2,1)S(1)}, bf16[2,128,256]{1,0,2:T(2,128)(2,1)S(1)}, u32[]{:S(2)}, u32[]{:S(2)}) collective-permute-start(bf16[2,128,256]{1,0,2:T(2,128)(2,1)S(1)} %collective-permute-done.18), channel_id=1, source_target_pairs={{0,4},{4,8},{8,12},{12,14},{14,10},{10,6},{6,2},{2,0},{1,5},{5,9},... | collective-permute-start | bytes 393224 | tf_op jit(solution)/shard_map/ppermute | solution.py:165
  103.7 1.8 %copy.52 = bf16[2,2,64,7,128]{4,2,3,1,0:T(8,128)(2,1)S(1)} copy(bf16[2,2,64,7,128]{2,1,0,4,3:T(2,128)(2,1)S(1)} %reshape.340) | data formatting | bytes 917504 | tf_op jit(solution)/shard_map/reshape | solution.py:206
  106.7 1.6 %collective-permute-start.20 = (bf16[2,128,256]{1,0,2:T(2,128)(2,1)S(1)}, bf16[2,128,256]{1,0,2:T(2,128)(2,1)S(1)}, u32[]{:S(2)}, u32[]{:S(2)}) collective-permute-start(bf16[2,128,256]{1,0,2:T(2,128)(2,1)S(1)} %collective-permute-done.19), channel_id=1, source_target_pairs={{0,4},{4,8},{8,12},{12,14},{14,10},{10,6},{6,2},{2,0},{1,5},{5,9},... | collective-permute-start | bytes 393224 | tf_op jit(solution)/shard_map/ppermute | solution.py:165
  108.5 2.2 %collective-permute-done.23 = bf16[2,128,256]{1,0,2:T(2,128)(2,1)S(1)} collective-permute-done((bf16[2,128,256]{1,0,2:T(2,128)(2,1)S(1)}, bf16[2,128,256]{1,0,2:T(2,128)(2,1)S(1)}, u32[]{:S(2)}, u32[]{:S(2)}) %collective-permute-start.23) | collective-permute-done | bytes 131104 | tf_op jit(solution)/shard_map/ppermute | solution.py:168
  112.6 1.4 %gather_fusion.4 = bf16[12,64,256]{2,1,0:T(8,128)(2,1)} fusion(bf16[2,16,64,256]{3,2,0,1:T(8,128)(2,1)S(1)} %bitcast.134, s32[12]{0:T(128)S(1)} %reshape.308), kind=kCustom, calls=%fused_computation.4 | custom fusion | bytes 786528 | tf_op jit(solution)/shard_map/gather | solution.py:192
  121.8 1.3 %convert_element_type.46 = bf16[2,128,896]{2,1,0:T(8,128)(2,1)} reshape(bf16[2,2,64,7,128]{4,3,2,1,0:T(8,128)(2,1)S(1)} %copy.57) | data formatting | bytes 917504 | tf_op jit(solution)/shard_map/convert_element_type | solution.py:268
  (161 shorter events, 36.0 us)
Async XLA Ops:
  0.0 10.6 %copy-start = (s32[2,2,2]{2,1,0:T(2,128)S(1)}, s32[2,2,2]{2,1,0:T(2,128)}, u32[]{:S(2)}) copy-start(s32[2,2,2]{2,1,0:T(2,128)} %param.21) | copy-start | bytes 100
  2.3 6.4 %copy-start.10 = (s32[8]{0:T(128)S(1)}, s32[8]{0:T(128)}, u32[]{:S(2)}) copy-start(s32[8]{0:T(128)} %constant.151.clone) | copy-start | bytes 100
  2.3 7.5 %copy-start.7 = (s32[8]{0:T(128)S(1)}, s32[8]{0:T(128)}, u32[]{:S(2)}) copy-start(s32[8]{0:T(128)} %constant.152) | copy-start | bytes 100
  2.3 8.1 %copy-start.5 = (f32[128]{0:T(128)S(1)}, f32[128]{0:T(128)}, u32[]{:S(2)}) copy-start(f32[128]{0:T(128)} %param.19) | copy-start | bytes 1540
  2.3 8.2 %copy-start.4 = (f32[896]{0:T(1024)S(1)}, f32[896]{0:T(1024)}, u32[]{:S(2)}) copy-start(f32[896]{0:T(1024)} %param.15) | copy-start | bytes 10756
  2.4 8.2 %copy-start.6 = (f32[128]{0:T(128)S(1)}, f32[128]{0:T(128)}, u32[]{:S(2)}) copy-start(f32[128]{0:T(128)} %param.17) | copy-start | bytes 1540
  2.4 9.3 %slice-start = ((f32[896]{0:T(1024)}), f32[512]{0:T(512)S(1)}, s32[]{:S(2)}) async-start(f32[896]{0:T(1024)} %param.15), calls=%async_computation | async-start | bytes 4096 | tf_op jit(solution)/shard_map/slice | solution.py:113
  3.3 10.7 %collective-permute-start = (bf16[224,576]{1,0:T(8,128)(2,1)}, bf16[224,576]{1,0:T(8,128)(2,1)S(1)}, u32[]{:S(2)}, u32[]{:S(2)}) collective-permute-start(bf16[224,576]{1,0:T(8,128)(2,1)} %pad_maximum_fusion.4), channel_id=1, source_target_pairs={{0,4},{4,8},{8,12},{12,14},{14,10},{10,6},{6,2},{2,0},{1,5},{5,9},... | collective-permute-start | bytes 774152 | tf_op jit(solution)/shard_map/ppermute | solution.py:47
  7.2 10.4 %collective-permute-start.9 = (bf16[224,576]{1,0:T(8,128)(2,1)}, bf16[224,576]{1,0:T(8,128)(2,1)S(1)}, u32[]{:S(2)}, u32[]{:S(2)}) collective-permute-start(bf16[224,576]{1,0:T(8,128)(2,1)} %pad_maximum_fusion.5), channel_id=1, source_target_pairs={{0,2},{4,0},{8,4},{12,8},{14,12},{10,14},{6,10},{2,6},{1,3},{5,1},... | collective-permute-start | bytes 774152 | tf_op jit(solution)/shard_map/ppermute | solution.py:48
  14.0 26.6 %collective-permute-start.1 = (bf16[2,128,1792]{2,1,0:T(8,128)(2,1)}, bf16[2,128,1792]{2,1,0:T(8,128)(2,1)S(1)}, u32[]{:S(2)}, u32[]{:S(2)}) collective-permute-start(bf16[2,128,1792]{2,1,0:T(8,128)(2,1)} %param.12), channel_id=1, source_target_pairs={{0,16},{16,0},{1,17},{17,1},{2,18},{18,2},{3,19},{19,3},{4,20},{20... | collective-permute-start | bytes 2752520 | tf_op jit(solution)/shard_map/ppermute | solution.py:118
  16.0 7.7 %collective-permute-start.3 = (bf16[224,576]{1,0:T(8,128)(2,1)S(1)}, bf16[224,576]{1,0:T(8,128)(2,1)S(1)}, u32[]{:S(2)}, u32[]{:S(2)}) collective-permute-start(bf16[224,576]{1,0:T(8,128)(2,1)S(1)} %collective-permute-done), channel_id=1, source_target_pairs={{0,4},{4,8},{8,12},{12,14},{14,10},{10,6},{6,2},{2,0},{1,5},{5,9},... | collective-permute-start | bytes 774152 | tf_op jit(solution)/shard_map/ppermute | solution.py:47
  17.6 7.7 %collective-permute-start.10 = (bf16[224,576]{1,0:T(8,128)(2,1)S(1)}, bf16[224,576]{1,0:T(8,128)(2,1)S(1)}, u32[]{:S(2)}, u32[]{:S(2)}) collective-permute-start(bf16[224,576]{1,0:T(8,128)(2,1)S(1)} %collective-permute-done.9), channel_id=1, source_target_pairs={{0,2},{4,0},{8,4},{12,8},{14,12},{10,14},{6,10},{2,6},{1,3},{5,1},... | collective-permute-start | bytes 774152 | tf_op jit(solution)/shard_map/ppermute | solution.py:48
  23.7 7.0 %collective-permute-start.4 = (bf16[224,576]{1,0:T(8,128)(2,1)S(1)}, bf16[224,576]{1,0:T(8,128)(2,1)S(1)}, u32[]{:S(2)}, u32[]{:S(2)}) collective-permute-start(bf16[224,576]{1,0:T(8,128)(2,1)S(1)} %collective-permute-done.3), channel_id=1, source_target_pairs={{0,4},{4,8},{8,12},{12,14},{14,10},{10,6},{6,2},{2,0},{1,5},{5,9},... | collective-permute-start | bytes 774152 | tf_op jit(solution)/shard_map/ppermute | solution.py:47
  25.3 7.0 %collective-permute-start.11 = (bf16[224,576]{1,0:T(8,128)(2,1)S(1)}, bf16[224,576]{1,0:T(8,128)(2,1)S(1)}, u32[]{:S(2)}, u32[]{:S(2)}) collective-permute-start(bf16[224,576]{1,0:T(8,128)(2,1)S(1)} %collective-permute-done.10), channel_id=1, source_target_pairs={{0,2},{4,0},{8,4},{12,8},{14,12},{10,14},{6,10},{2,6},{1,3},{5,1},... | collective-permute-start | bytes 774152 | tf_op jit(solution)/shard_map/ppermute | solution.py:48
  30.7 7.6 %collective-permute-start.5 = (bf16[224,576]{1,0:T(8,128)(2,1)S(1)}, bf16[224,576]{1,0:T(8,128)(2,1)S(1)}, u32[]{:S(2)}, u32[]{:S(2)}) collective-permute-start(bf16[224,576]{1,0:T(8,128)(2,1)S(1)} %collective-permute-done.4), channel_id=1, source_target_pairs={{0,4},{4,8},{8,12},{12,14},{14,10},{10,6},{6,2},{2,0},{1,5},{5,9},... | collective-permute-start | bytes 774152 | tf_op jit(solution)/shard_map/ppermute | solution.py:47
  32.3 7.8 %collective-permute-start.12 = (bf16[224,576]{1,0:T(8,128)(2,1)S(1)}, bf16[224,576]{1,0:T(8,128)(2,1)S(1)}, u32[]{:S(2)}, u32[]{:S(2)}) collective-permute-start(bf16[224,576]{1,0:T(8,128)(2,1)S(1)} %collective-permute-done.11), channel_id=1, source_target_pairs={{0,2},{4,0},{8,4},{12,8},{14,12},{10,14},{6,10},{2,6},{1,3},{5,1},... | collective-permute-start | bytes 774152 | tf_op jit(solution)/shard_map/ppermute | solution.py:48
  38.3 6.6 %collective-permute-start.6 = (bf16[224,576]{1,0:T(8,128)(2,1)S(1)}, bf16[224,576]{1,0:T(8,128)(2,1)S(1)}, u32[]{:S(2)}, u32[]{:S(2)}) collective-permute-start(bf16[224,576]{1,0:T(8,128)(2,1)S(1)} %collective-permute-done.5), channel_id=1, source_target_pairs={{0,4},{4,8},{8,12},{12,14},{14,10},{10,6},{6,2},{2,0},{1,5},{5,9},... | collective-permute-start | bytes 774152 | tf_op jit(solution)/shard_map/ppermute | solution.py:47
  40.1 6.6 %collective-permute-start.13 = (bf16[224,576]{1,0:T(8,128)(2,1)S(1)}, bf16[224,576]{1,0:T(8,128)(2,1)S(1)}, u32[]{:S(2)}, u32[]{:S(2)}) collective-permute-start(bf16[224,576]{1,0:T(8,128)(2,1)S(1)} %collective-permute-done.12), channel_id=1, source_target_pairs={{0,2},{4,0},{8,4},{12,8},{14,12},{10,14},{6,10},{2,6},{1,3},{5,1},... | collective-permute-start | bytes 774152 | tf_op jit(solution)/shard_map/ppermute | solution.py:48
  41.7 28.0 %collective-permute-start.2 = (bf16[4,128,1792]{2,1,0:T(8,128)(2,1)}, bf16[4,128,1792]{2,1,0:T(8,128)(2,1)}, u32[]{:S(2)}, u32[]{:S(2)}) collective-permute-start(bf16[4,128,1792]{2,1,0:T(8,128)(2,1)} %constant_dynamic-update-slice_fusion.2), channel_id=1, source_target_pairs={{0,1},{1,0},{2,3},{3,2},{4,5},{5,4},{6,7},{7,6},{8,9},{9,8},{10,11... | collective-permute-start | bytes 5505032 | tf_op jit(solution)/shard_map/ppermute | solution.py:120
  45.0 7.3 %collective-permute-start.7 = (bf16[224,576]{1,0:T(8,128)(2,1)S(1)}, bf16[224,576]{1,0:T(8,128)(2,1)S(1)}, u32[]{:S(2)}, u32[]{:S(2)}) collective-permute-start(bf16[224,576]{1,0:T(8,128)(2,1)S(1)} %collective-permute-done.6), channel_id=1, source_target_pairs={{0,4},{4,8},{8,12},{12,14},{14,10},{10,6},{6,2},{2,0},{1,5},{5,9},... | collective-permute-start | bytes 774152 | tf_op jit(solution)/shard_map/ppermute | solution.py:47
  46.7 7.2 %collective-permute-start.14 = (bf16[224,576]{1,0:T(8,128)(2,1)S(1)}, bf16[224,576]{1,0:T(8,128)(2,1)S(1)}, u32[]{:S(2)}, u32[]{:S(2)}) collective-permute-start(bf16[224,576]{1,0:T(8,128)(2,1)S(1)} %collective-permute-done.13), channel_id=1, source_target_pairs={{0,2},{4,0},{8,4},{12,8},{14,12},{10,14},{6,10},{2,6},{1,3},{5,1},... | collective-permute-start | bytes 774152 | tf_op jit(solution)/shard_map/ppermute | solution.py:48
  52.2 6.6 %collective-permute-start.8 = (bf16[224,576]{1,0:T(8,128)(2,1)S(1)}, bf16[224,576]{1,0:T(8,128)(2,1)S(1)}, u32[]{:S(2)}, u32[]{:S(2)}) collective-permute-start(bf16[224,576]{1,0:T(8,128)(2,1)S(1)} %collective-permute-done.7), channel_id=1, source_target_pairs={{0,4},{4,8},{8,12},{12,14},{14,10},{10,6},{6,2},{2,0},{1,5},{5,9},... | collective-permute-start | bytes 774152 | tf_op jit(solution)/shard_map/ppermute | solution.py:47
  54.0 9.0 %collective-permute-start.15 = (bf16[224,576]{1,0:T(8,128)(2,1)S(1)}, bf16[224,576]{1,0:T(8,128)(2,1)S(1)}, u32[]{:S(2)}, u32[]{:S(2)}) collective-permute-start(bf16[224,576]{1,0:T(8,128)(2,1)S(1)} %collective-permute-done.14), channel_id=1, source_target_pairs={{0,2},{4,0},{8,4},{12,8},{14,12},{10,14},{6,10},{2,6},{1,3},{5,1},... | collective-permute-start | bytes 774152 | tf_op jit(solution)/shard_map/ppermute | solution.py:48
  82.8 14.9 %copy-start.9 = (pred[2,3]{1,0:T(4,128)(4,1)S(1)}, pred[2,3]{1,0:T(4,128)(4,1)}, u32[]{:S(2)}) copy-start(pred[2,3]{1,0:T(4,128)(4,1)} %compare_and_fusion) | copy-start | bytes 22
  83.4 6.8 %collective-permute-start.16 = (bf16[2,128,576]{1,0,2:T(2,128)(2,1)S(1)}, bf16[2,128,576]{1,0,2:T(2,128)(2,1)S(1)}, u32[]{:S(2)}, u32[]{:S(2)}) collective-permute-start(bf16[2,128,576]{1,0,2:T(2,128)(2,1)S(1)} %fusion.30), channel_id=1, source_target_pairs={{0,16},{16,0},{1,17},{17,1},{2,18},{18,2},{3,19},{19,3},{4,20},{20... | collective-permute-start | bytes 884744 | tf_op jit(solution)/shard_map/ppermute | solution.py:146
  91.0 5.0 %collective-permute-start.17 = (bf16[2,128,256]{1,0,2:T(2,128)(2,1)S(1)}, bf16[2,128,256]{1,0,2:T(2,128)(2,1)S(1)}, u32[]{:S(2)}, u32[]{:S(2)}) collective-permute-start(bf16[2,128,256]{1,0,2:T(2,128)(2,1)S(1)} %pad_maximum_fusion.6), channel_id=1, source_target_pairs={{0,4},{4,8},{8,12},{12,14},{14,10},{10,6},{6,2},{2,0},{1,5},{5,9},... | collective-permute-start | bytes 393224 | tf_op jit(solution)/shard_map/ppermute | solution.py:165
  92.7 5.9 %collective-permute-start.21 = (bf16[2,128,256]{1,0,2:T(2,128)(2,1)S(1)}, bf16[2,128,256]{1,0,2:T(2,128)(2,1)S(1)}, u32[]{:S(2)}, u32[]{:S(2)}) collective-permute-start(bf16[2,128,256]{1,0,2:T(2,128)(2,1)S(1)} %pad_maximum_fusion.6), channel_id=1, source_target_pairs={{0,2},{4,0},{8,4},{12,8},{14,12},{10,14},{6,10},{2,6},{1,3},{5,1},... | collective-permute-start | bytes 393224 | tf_op jit(solution)/shard_map/ppermute | solution.py:168
  96.1 5.7 %collective-permute-start.18 = (bf16[2,128,256]{1,0,2:T(2,128)(2,1)S(1)}, bf16[2,128,256]{1,0,2:T(2,128)(2,1)S(1)}, u32[]{:S(2)}, u32[]{:S(2)}) collective-permute-start(bf16[2,128,256]{1,0,2:T(2,128)(2,1)S(1)} %collective-permute-done.17), channel_id=1, source_target_pairs={{0,4},{4,8},{8,12},{12,14},{14,10},{10,6},{6,2},{2,0},{1,5},{5,9},... | collective-permute-start | bytes 393224 | tf_op jit(solution)/shard_map/ppermute | solution.py:165
  98.6 7.1 %collective-permute-start.22 = (bf16[2,128,256]{1,0,2:T(2,128)(2,1)S(1)}, bf16[2,128,256]{1,0,2:T(2,128)(2,1)S(1)}, u32[]{:S(2)}, u32[]{:S(2)}) collective-permute-start(bf16[2,128,256]{1,0,2:T(2,128)(2,1)S(1)} %collective-permute-done.21), channel_id=1, source_target_pairs={{0,2},{4,0},{8,4},{12,8},{14,12},{10,14},{6,10},{2,6},{1,3},{5,1},... | collective-permute-start | bytes 393224 | tf_op jit(solution)/shard_map/ppermute | solution.py:168
  101.7 5.0 %collective-permute-start.19 = (bf16[2,128,256]{1,0,2:T(2,128)(2,1)S(1)}, bf16[2,128,256]{1,0,2:T(2,128)(2,1)S(1)}, u32[]{:S(2)}, u32[]{:S(2)}) collective-permute-start(bf16[2,128,256]{1,0,2:T(2,128)(2,1)S(1)} %collective-permute-done.18), channel_id=1, source_target_pairs={{0,4},{4,8},{8,12},{12,14},{14,10},{10,6},{6,2},{2,0},{1,5},{5,9},... | collective-permute-start | bytes 393224 | tf_op jit(solution)/shard_map/ppermute | solution.py:165
  105.7 5.0 %collective-permute-start.23 = (bf16[2,128,256]{1,0,2:T(2,128)(2,1)S(1)}, bf16[2,128,256]{1,0,2:T(2,128)(2,1)S(1)}, u32[]{:S(2)}, u32[]{:S(2)}) collective-permute-start(bf16[2,128,256]{1,0,2:T(2,128)(2,1)S(1)} %collective-permute-done.22), channel_id=1, source_target_pairs={{0,2},{4,0},{8,4},{12,8},{14,12},{10,14},{6,10},{2,6},{1,3},{5,1},... | collective-permute-start | bytes 393224 | tf_op jit(solution)/shard_map/ppermute | solution.py:168
  106.7 5.0 %collective-permute-start.20 = (bf16[2,128,256]{1,0,2:T(2,128)(2,1)S(1)}, bf16[2,128,256]{1,0,2:T(2,128)(2,1)S(1)}, u32[]{:S(2)}, u32[]{:S(2)}) collective-permute-start(bf16[2,128,256]{1,0,2:T(2,128)(2,1)S(1)} %collective-permute-done.19), channel_id=1, source_target_pairs={{0,4},{4,8},{8,12},{12,14},{14,10},{10,6},{6,2},{2,0},{1,5},{5,9},... | collective-permute-start | bytes 393224 | tf_op jit(solution)/shard_map/ppermute | solution.py:165
  (4 other events, 9.6 us)

commit v22 on v17

--- a/solution.py
+++ b/solution.py
@@ -138,24 +138,33 @@
     )
     token_positions = (here * length + jnp.arange(length, dtype=jnp.int32)).astype(jnp.float32)
 
-    summed = jnp.dot(normed, full_panel, preferred_element_type=jnp.float32) + panel_bias
-    summed = summed.reshape(2 * passages, length, split + value_split)
-    turned = apply_rotation(
-        summed[..., :split].reshape(2 * passages, length, split // HEAD_SIZE, HEAD_SIZE),
-        token_positions,
-    ).astype(jnp.bfloat16)
-    result = jnp.concatenate(
-        [turned.reshape(2 * passages, length, split), summed[..., split:].astype(jnp.bfloat16)],
-        axis=-1,
-    )
-    mine = result[:passages]
-    returned = lax.ppermute(result[passages:], "groups", SWAP)
-    low = jnp.where(first, mine, returned)
-    high = jnp.where(first, returned, mine)
-    rotary_rows = jnp.concatenate([low[..., :split], high[..., :split]], axis=-1)
-    query_rows = rotary_rows[..., : heads_here * HEAD_SIZE]
-    key = rotary_rows[..., heads_here * HEAD_SIZE :]
-    value_rows = jnp.concatenate([low[..., split:], high[..., split:]], axis=-1)
+    lead = split - HEAD_SIZE
+
+    def project(columns, bias, rotary_heads):
+        summed = jnp.dot(normed, columns, preferred_element_type=jnp.float32) + bias
+        summed = summed.reshape(2 * passages, length, -1)
+        width = rotary_heads * HEAD_SIZE
+        turned = apply_rotation(
+            summed[..., :width].reshape(2 * passages, length, rotary_heads, HEAD_SIZE),
+            token_positions,
+        ).astype(jnp.bfloat16)
+        return jnp.concatenate(
+            [turned.reshape(2 * passages, length, width), summed[..., width:].astype(jnp.bfloat16)],
+            axis=-1,
+        )
+
+    result_kv = project(full_panel[:, lead:], panel_bias[lead:], 1)
+    returned_kv = lax.ppermute(result_kv[passages:], "groups", SWAP)
+    result_q = project(full_panel[:, :lead], panel_bias[:lead], lead // HEAD_SIZE)
+    returned_q = lax.ppermute(result_q[passages:], "groups", SWAP)
+    mine_kv, mine_q = result_kv[:passages], result_q[:passages]
+    low_kv = jnp.where(first, mine_kv, returned_kv)
+    high_kv = jnp.where(first, returned_kv, mine_kv)
+    key = high_kv[..., :HEAD_SIZE]
+    value_rows = jnp.concatenate([low_kv[..., HEAD_SIZE:], high_kv[..., HEAD_SIZE:]], axis=-1)
+    low_q = jnp.where(first, mine_q, returned_q)
+    high_q = jnp.where(first, returned_q, mine_q)
+    query_rows = jnp.concatenate([low_q, low_kv[..., :HEAD_SIZE], high_q], axis=-1)
 
     pairs = jnp.concatenate([key, value_rows], axis=-1)
     if row_count == 8:

time: 118 us -> 126 us (1.068)
  matrix products: 6.81 us -> 13.4 us
  waiting for transfers between devices: 36.2 us -> 30.6 us
  local copies, waits for them, and re-layouts: 32.2 us -> 36.7 us
  starting transfers between devices: 25.5 us -> 27.3 us
    ppermute x7, waiting for transfers between devices: 0.7 us -> 21.1 us  [gather_rows(): behind = lax.ppermute(behind, 'row', backward)]
    ppermute x7, waiting for transfers between devices: 21.2 us -> 1.97 us  [gather_rows(): ahead = lax.ppermute(ahead, 'row', forward)]
    ppermute x1 -> x2, waiting for transfers between devices: 5.63 us -> 0.01 us  [the longest x1 0.01 us: shards(): returned_kv = lax.ppermute(result_kv[passages:], 'groups', SWAP)]
    dot_general x1 -> x2, matrix products: 2.37 us -> 6.33 us  [project(): summed = jnp.dot(normed, columns, preferred_element_type=jnp.float32) + bias]
    unnamed x43 -> x55, local copies, waits for them, and re-layouts: 10.3 us -> 12.3 us
    ppermute x4, local copies, waits for them, and re-layouts: 0.45 us -> 2.25 us  [shards(): ahead = lax.ppermute(ahead, 'row', forward)]
    ppermute x3, waiting for transfers between devices: 2.15 us -> 0.36 us  [shards(): behind = lax.ppermute(behind, 'row', backward)]
    ppermute x1 -> x2, starting transfers between devices: 0.49 us -> 2.16 us  [the longest x1 1.99 us: shards(): returned_kv = lax.ppermute(result_kv[passages:], 'groups', SWAP)]
  transfers between devices with their start and end apart: 25 -> 26, of which waited for: 16 -> 13; matrix products, arithmetic and copies ran while one was open for 28% -> 32% of each run, Pallas kernels for 0% -> 0%
where the time goes in v22:
time: 126 us
  local copies, waits for them, and re-layouts  36.7 us (29%)
  waiting for transfers between devices  30.6 us (24%)
  starting transfers between devices  27.3 us (22%)
  other arithmetic  16.9 us (13%)
  matrix products  13.4 us (11%)
    ppermute x7, waiting for transfers between devices, gather_rows(): behind = lax.ppermute(behind, 'row', backward)  21.1 us
    ppermute x7, starting transfers between devices, gather_rows(): ahead = lax.ppermute(ahead, 'row', forward)  12.4 us
    unnamed x55, local copies, waits for them, and re-layouts  12.3 us
    ppermute x4, waiting for transfers between devices, shards(): ahead = lax.ppermute(ahead, 'row', forward)  7.08 us
    ppermute x4, starting transfers between devices, shards(): ahead = lax.ppermute(ahead, 'row', forward)  6.63 us
    dot_general x2, matrix products, project(): summed = jnp.dot(normed, columns, preferred_element_type=jnp.float32) + bias  6.33 us
    gather x1, local copies, waits for them, and re-layouts, gather_rows(): jnp.stack(ahead_parts)[ahead_pick]  3.91 us
    gather x1, local copies, waits for them, and re-layouts, gather_rows(): jnp.stack(behind_parts)[behind_pick]  3.88 us
  transfers between devices with their start and end apart: 26, of which 13 were waited for; matrix products, arithmetic and copies ran while one was open for 32% of the time, Pallas kernels for 0%

profile of v22, /device:TPU:0, one launch (start us, length us, event | category | flops | bytes accessed | tf_op | source)
XLA Modules:
  0.0 125.8 jit_solution(13925365575439232746)
XLA Ops:
  3.5 3.1 %collective-permute-start.1 = (bf16[224,576]{1,0:T(8,128)(2,1)S(1)}, bf16[224,576]{1,0:T(8,128)(2,1)S(1)}, u32[]{:S(2)}, u32[]{:S(2)}) collective-permute-start(bf16[224,576]{1,0:T(8,128)(2,1)S(1)} %pad_maximum_fusion.2), channel_id=1, source_target_pairs={{0,4},{4,8},{8,12},{12,14},{14,10},{10,6},{6,2},{2,0},{1,5},{5,9},... | collective-permute-start | bytes 774152 | tf_op jit(solution)/shard_map/ppermute | solution.py:47
  13.3 1.8 %collective-permute-start.2 = (bf16[2,128,1792]{2,1,0:T(8,128)(2,1)S(1)}, bf16[2,128,1792]{2,1,0:T(8,128)(2,1)}, u32[]{:S(2)}, u32[]{:S(2)}) collective-permute-start(bf16[2,128,1792]{2,1,0:T(8,128)(2,1)S(1)} %copy-done.5), channel_id=1, source_target_pairs={{0,16},{16,0},{1,17},{17,1},{2,18},{18,2},{3,19},{19,3},{4,20},{20... | collective-permute-start | bytes 2752520 | tf_op jit(solution)/shard_map/ppermute | solution.py:119
  15.1 1.6 %collective-permute-start.4 = (bf16[224,576]{1,0:T(8,128)(2,1)S(1)}, bf16[224,576]{1,0:T(8,128)(2,1)S(1)}, u32[]{:S(2)}, u32[]{:S(2)}) collective-permute-start(bf16[224,576]{1,0:T(8,128)(2,1)S(1)} %collective-permute-done.1), channel_id=1, source_target_pairs={{0,4},{4,8},{8,12},{12,14},{14,10},{10,6},{6,2},{2,0},{1,5},{5,9},... | collective-permute-start | bytes 774152 | tf_op jit(solution)/shard_map/ppermute | solution.py:47
  18.6 5.9 %collective-permute-done.11 = bf16[224,576]{1,0:T(8,128)(2,1)S(1)} collective-permute-done((bf16[224,576]{1,0:T(8,128)(2,1)S(1)}, bf16[224,576]{1,0:T(8,128)(2,1)S(1)}, u32[]{:S(2)}, u32[]{:S(2)}) %collective-permute-start.11) | collective-permute-done | bytes 258080 | tf_op jit(solution)/shard_map/ppermute | solution.py:48
  25.0 1.5 %collective-permute-start.5 = (bf16[224,576]{1,0:T(8,128)(2,1)S(1)}, bf16[224,576]{1,0:T(8,128)(2,1)S(1)}, u32[]{:S(2)}, u32[]{:S(2)}) collective-permute-start(bf16[224,576]{1,0:T(8,128)(2,1)S(1)} %collective-permute-done.4), channel_id=1, source_target_pairs={{0,4},{4,8},{8,12},{12,14},{14,10},{10,6},{6,2},{2,0},{1,5},{5,9},... | collective-permute-start | bytes 774152 | tf_op jit(solution)/shard_map/ppermute | solution.py:47
  28.0 3.5 %collective-permute-done.12 = bf16[224,576]{1,0:T(8,128)(2,1)S(1)} collective-permute-done((bf16[224,576]{1,0:T(8,128)(2,1)S(1)}, bf16[224,576]{1,0:T(8,128)(2,1)S(1)}, u32[]{:S(2)}, u32[]{:S(2)}) %collective-permute-start.12) | collective-permute-done | bytes 258080 | tf_op jit(solution)/shard_map/ppermute | solution.py:48
  32.0 1.5 %collective-permute-start.6 = (bf16[224,576]{1,0:T(8,128)(2,1)S(1)}, bf16[224,576]{1,0:T(8,128)(2,1)S(1)}, u32[]{:S(2)}, u32[]{:S(2)}) collective-permute-start(bf16[224,576]{1,0:T(8,128)(2,1)S(1)} %collective-permute-done.5), channel_id=1, source_target_pairs={{0,4},{4,8},{8,12},{12,14},{14,10},{10,6},{6,2},{2,0},{1,5},{5,9},... | collective-permute-start | bytes 774152 | tf_op jit(solution)/shard_map/ppermute | solution.py:47
  35.0 2.0 %maximum_select_fusion = bf16[2,128,3584]{2,1,0:T(8,128)(2,1)S(1)} fusion(bf16[2,128,1792]{2,1,0:T(8,128)(2,1)} %collective-permute-done, bf16[2,128,1792]{2,1,0:T(8,128)(2,1)S(1)} %copy-done.5, pred[]{:T(512)S(6)} %eq.14), kind=kLoop, calls=%fused_computation.17 | loop fusion | flops 8257536 | bytes 3670017 | tf_op jit(solution)/shard_map/jit(_where)/select_n | solution.py:121
  37.1 1.7 %collective-permute-done.13 = bf16[224,576]{1,0:T(8,128)(2,1)S(1)} collective-permute-done((bf16[224,576]{1,0:T(8,128)(2,1)S(1)}, bf16[224,576]{1,0:T(8,128)(2,1)S(1)}, u32[]{:S(2)}, u32[]{:S(2)}) %collective-permute-start.13) | collective-permute-done | bytes 258080 | tf_op jit(solution)/shard_map/ppermute | solution.py:48
  40.0 1.5 %collective-permute-start.7 = (bf16[224,576]{1,0:T(8,128)(2,1)S(1)}, bf16[224,576]{1,0:T(8,128)(2,1)S(1)}, u32[]{:S(2)}, u32[]{:S(2)}) collective-permute-start(bf16[224,576]{1,0:T(8,128)(2,1)S(1)} %collective-permute-done.6), channel_id=1, source_target_pairs={{0,4},{4,8},{8,12},{12,14},{14,10},{10,6},{6,2},{2,0},{1,5},{5,9},... | collective-permute-start | bytes 774152 | tf_op jit(solution)/shard_map/ppermute | solution.py:47
  42.2 3.1 %collective-permute-done.14 = bf16[224,576]{1,0:T(8,128)(2,1)S(1)} collective-permute-done((bf16[224,576]{1,0:T(8,128)(2,1)S(1)}, bf16[224,576]{1,0:T(8,128)(2,1)S(1)}, u32[]{:S(2)}, u32[]{:S(2)}) %collective-permute-start.14) | collective-permute-done | bytes 258080 | tf_op jit(solution)/shard_map/ppermute | solution.py:48
  46.9 1.5 %collective-permute-start.8 = (bf16[224,576]{1,0:T(8,128)(2,1)S(1)}, bf16[224,576]{1,0:T(8,128)(2,1)S(1)}, u32[]{:S(2)}, u32[]{:S(2)}) collective-permute-start(bf16[224,576]{1,0:T(8,128)(2,1)S(1)} %collective-permute-done.7), channel_id=1, source_target_pairs={{0,4},{4,8},{8,12},{12,14},{14,10},{10,6},{6,2},{2,0},{1,5},{5,9},... | collective-permute-start | bytes 774152 | tf_op jit(solution)/shard_map/ppermute | solution.py:47
  49.1 4.0 %collective-permute-done.15 = bf16[224,576]{1,0:T(8,128)(2,1)S(1)} collective-permute-done((bf16[224,576]{1,0:T(8,128)(2,1)S(1)}, bf16[224,576]{1,0:T(8,128)(2,1)S(1)}, u32[]{:S(2)}, u32[]{:S(2)}) %collective-permute-start.15) | collective-permute-done | bytes 258080 | tf_op jit(solution)/shard_map/ppermute | solution.py:48
  54.5 1.5 %collective-permute-start.9 = (bf16[224,576]{1,0:T(8,128)(2,1)S(1)}, bf16[224,576]{1,0:T(8,128)(2,1)S(1)}, u32[]{:S(2)}, u32[]{:S(2)}) collective-permute-start(bf16[224,576]{1,0:T(8,128)(2,1)S(1)} %collective-permute-done.8), channel_id=1, source_target_pairs={{0,4},{4,8},{8,12},{12,14},{14,10},{10,6},{6,2},{2,0},{1,5},{5,9},... | collective-permute-start | bytes 774152 | tf_op jit(solution)/shard_map/ppermute | solution.py:47
  56.8 2.9 %collective-permute-done.16 = bf16[224,576]{1,0:T(8,128)(2,1)S(1)} collective-permute-done((bf16[224,576]{1,0:T(8,128)(2,1)S(1)}, bf16[224,576]{1,0:T(8,128)(2,1)S(1)}, u32[]{:S(2)}, u32[]{:S(2)}) %collective-permute-start.16) | collective-permute-done | bytes 258080 | tf_op jit(solution)/shard_map/ppermute | solution.py:48
  60.5 3.9 %gather_fusion.1 = bf16[8,224,576]{2,1,0:T(8,128)(2,1)} fusion(bf16[8,224,576]{2,1,0:T(8,128)(2,1)} %bitcast_dynamic-update-slice_fusion, s32[1024]{0:T(1024)S(1)} %get-tuple-element.35), kind=kCustom, calls=%fused_computation.1 | custom fusion | bytes 4128800 | tf_op jit(solution)/shard_map/gather | solution.py:56
  65.1 3.9 %gather_fusion = bf16[8,224,576]{2,1,0:T(8,128)(2,1)} fusion(bf16[8,224,576]{2,1,0:T(8,128)(2,1)} %bitcast_dynamic-update-slice_fusion.8, s32[1024]{0:T(1024)S(1)} %get-tuple-element.36), kind=kCustom, calls=%fused_computation | custom fusion | bytes 4128800 | tf_op jit(solution)/shard_map/gather | solution.py:56
  69.0 2.8 %pad_maximum_fusion = bf16[8,448,576]{2,1,0:T(8,128)(2,1)S(1)} fusion(bf16[8,224,576]{2,1,0:T(8,128)(2,1)} %gather_fusion.1, bf16[8,224,576]{2,1,0:T(8,128)(2,1)} %gather_fusion), kind=kLoop, calls=%fused_computation.11 | loop fusion | flops 8257536 | bytes 8257536 | tf_op jit(solution)/shard_map/concatenate | solution.py:55
  71.8 3.3 %maximum_select_fusion.1 = bf16[2,128,3584]{2,1,0:T(8,128)(2,1)S(1)} fusion(bf16[2,128,1792]{2,1,0:T(8,128)(2,1)S(1)} %collective-permute-done.3, bf16[2,128,1792]{2,1,0:T(8,128)(2,1)} %collective-permute-done.2, pred[]{:T(512)S(6)} %eq.14), kind=kLoop, calls=%fused_computation.18 | loop fusion | flops 8257536 | bytes 3670017 | tf_op jit(solution)/shard_map/jit(_where)/select_n | solution.py:126
  77.7 1.8 %copy-done.4 = bf16[512,3584]{1,0:T(8,128)(2,1)} copy-done((bf16[512,3584]{1,0:T(8,128)(2,1)}, bf16[512,3584]{1,0:T(8,128)(2,1)S(1)}, u32[]{:S(2)}) %copy-start.4) | copy-done | bytes 3670040
  81.5 2.0 %collective-permute-start.17 = (bf16[2,128,192]{1,0,2:T(2,128)(2,1)S(1)}, bf16[2,128,192]{1,0,2:T(2,128)(2,1)S(1)}, u32[]{:S(2)}, u32[]{:S(2)}) collective-permute-start(bf16[2,128,192]{1,0,2:T(2,128)(2,1)S(1)} %fusion.36), channel_id=1, source_target_pairs={{0,16},{16,0},{1,17},{17,1},{2,18},{18,2},{3,19},{19,3},{4,20},{20... | collective-permute-start | bytes 294920 | tf_op jit(solution)/shard_map/ppermute | solution.py:157
  83.5 5.0 %fusion.12 = f32[512,384]{1,0:T(8,128)S(1)} fusion(bf16[512,3584]{1,0:T(8,128)(2,1)} %copy-done.4, bf16[3584,576]{1,0:T(8,128)(2,1)} %bitcast.146, f32[384]{0:T(512)S(1)} %slice-done), kind=kOutput, calls=%fused_computation.34 | convolution fusion | flops 1409482752 | bytes 7210496 | tf_op jit(solution)/shard_map/dot_general | solution.py:144
  90.5 1.6 %collective-permute-start.18 = (bf16[2,128,256]{1,0,2:T(2,128)(2,1)S(1)}, bf16[2,128,256]{1,0,2:T(2,128)(2,1)S(1)}, u32[]{:S(2)}, u32[]{:S(2)}) collective-permute-start(bf16[2,128,256]{1,0,2:T(2,128)(2,1)S(1)} %pad_maximum_fusion.4), channel_id=1, source_target_pairs={{0,4},{4,8},{8,12},{12,14},{14,10},{10,6},{6,2},{2,0},{1,5},{5,9},... | collective-permute-start | bytes 393224 | tf_op jit(solution)/shard_map/ppermute | solution.py:180
  93.4 2.1 %collective-permute-done.18 = bf16[2,128,256]{1,0,2:T(2,128)(2,1)S(1)} collective-permute-done((bf16[2,128,256]{1,0,2:T(2,128)(2,1)S(1)}, bf16[2,128,256]{1,0,2:T(2,128)(2,1)S(1)}, u32[]{:S(2)}, u32[]{:S(2)}) %collective-permute-start.18) | collective-permute-done | bytes 131104 | tf_op jit(solution)/shard_map/ppermute | solution.py:180
  95.5 1.6 %collective-permute-start.19 = (bf16[2,128,256]{1,0,2:T(2,128)(2,1)S(1)}, bf16[2,128,256]{1,0,2:T(2,128)(2,1)}, u32[]{:S(2)}, u32[]{:S(2)}) collective-permute-start(bf16[2,128,256]{1,0,2:T(2,128)(2,1)S(1)} %collective-permute-done.18), channel_id=1, source_target_pairs={{0,4},{4,8},{8,12},{12,14},{14,10},{10,6},{6,2},{2,0},{1,5},{5,9},... | collective-permute-start | bytes 393224 | tf_op jit(solution)/shard_map/ppermute | solution.py:180
  97.6 3.0 %collective-permute-done.19 = bf16[2,128,256]{1,0,2:T(2,128)(2,1)} collective-permute-done((bf16[2,128,256]{1,0,2:T(2,128)(2,1)S(1)}, bf16[2,128,256]{1,0,2:T(2,128)(2,1)}, u32[]{:S(2)}, u32[]{:S(2)}) %collective-permute-start.19) | collective-permute-done | bytes 131104 | tf_op jit(solution)/shard_map/ppermute | solution.py:180
  100.6 1.6 %collective-permute-start.20 = (bf16[2,128,256]{1,0,2:T(2,128)(2,1)}, bf16[2,128,256]{1,0,2:T(2,128)(2,1)}, u32[]{:S(2)}, u32[]{:S(2)}) collective-permute-start(bf16[2,128,256]{1,0,2:T(2,128)(2,1)} %collective-permute-done.19), channel_id=1, source_target_pairs={{0,4},{4,8},{8,12},{12,14},{14,10},{10,6},{6,2},{2,0},{1,5},{5,9},... | collective-permute-start | bytes 393224 | tf_op jit(solution)/shard_map/ppermute | solution.py:180
  102.6 1.6 %copy.69 = bf16[2,2,64,7,128]{4,2,3,1,0:T(8,128)(2,1)S(1)} copy(bf16[2,2,64,7,128]{2,1,4,3,0:T(2,128)(2,1)S(1)} %reshape.326) | data formatting | bytes 917504 | tf_op jit(solution)/shard_map/reshape | solution.py:221
  106.1 1.8 %collective-permute-start.21 = (bf16[2,128,256]{1,0,2:T(2,128)(2,1)}, bf16[2,128,256]{1,0,2:T(2,128)(2,1)S(1)}, u32[]{:S(2)}, u32[]{:S(2)}) collective-permute-start(bf16[2,128,256]{1,0,2:T(2,128)(2,1)} %collective-permute-done.20), channel_id=1, source_target_pairs={{0,4},{4,8},{8,12},{12,14},{14,10},{10,6},{6,2},{2,0},{1,5},{5,9},... | collective-permute-start | bytes 393224 | tf_op jit(solution)/shard_map/ppermute | solution.py:180
  109.6 2.0 %collective-permute-done.21 = bf16[2,128,256]{1,0,2:T(2,128)(2,1)S(1)} collective-permute-done((bf16[2,128,256]{1,0,2:T(2,128)(2,1)}, bf16[2,128,256]{1,0,2:T(2,128)(2,1)S(1)}, u32[]{:S(2)}, u32[]{:S(2)}) %collective-permute-start.21) | collective-permute-done | bytes 131104 | tf_op jit(solution)/shard_map/ppermute | solution.py:180
  113.8 1.7 %fusion.56 = (f32[2,2,7,64]{3,2,1,0:T(8,128)S(1)}, f32[2,2,7,64,128]{4,3,2,1,0:T(8,128)}) fusion(bf16[2,2,64,7,128]{4,2,3,1,0:T(8,128)(2,1)S(1)} %copy.69, bf16[2,2,7,128,256]{4,3,2,1,0:T(8,128)(2,1)S(1)} %bitcast.148), kind=kOutput, calls=%fused_computation.170 | convolution fusion | flops 59177216 | bytes 2300928 | tf_op jit(solution)/shard_map/sqbgh,sqgwh->sqgbw/dot_general | solution.py:236
  118.1 1.6 %bitcast_reduce_fusion = (f32[2,2,7,64]{3,2,1,0:T(8,128)S(1)}, f32[2,2,192,64,7]{2,3,4,1,0:T(8,128)S(1)}) fusion(pred[2,192]{1,0:T(4,128)(4,1)S(1)} %broadcast_in_dim.31, bf16[2,2,64,7,128]{4,2,3,1,0:T(8,128)(2,1)S(1)} %copy.69, bf16[2,2,192,256]{3,2,1,0:T(8,128)(2,1)} %bitcast.151), kind=kOutput, calls=%fused_computation.20 | convolution fusion | flops 89110784 | bytes 2039168 | tf_op jit(solution)/shard_map/sqbgh,sqwh->sqgbw/dot_general | solution.py:224
  (188 shorter events, 46.2 us)
Async XLA Ops:
  0.0 11.2 %copy-start = (s32[2,2,2]{2,1,0:T(2,128)S(1)}, s32[2,2,2]{2,1,0:T(2,128)}, u32[]{:S(2)}) copy-start(s32[2,2,2]{2,1,0:T(2,128)} %param.21) | copy-start | bytes 100
  3.2 7.3 %copy-start.11 = (f32[896]{0:T(1024)S(1)}, f32[896]{0:T(1024)}, u32[]{:S(2)}) copy-start(f32[896]{0:T(1024)} %param.15) | copy-start | bytes 10756
  3.2 7.3 %copy-start.14 = (f32[128]{0:T(128)S(1)}, f32[128]{0:T(128)}, u32[]{:S(2)}) copy-start(f32[128]{0:T(128)} %param.17) | copy-start | bytes 1540
  3.3 8.2 %copy-start.12 = (s32[2,16,14,2]{1,3,2,0:T(2,128)S(1)}, s32[2,16,14,2]{1,3,2,0:T(2,128)}, u32[]{:S(2)}) copy-start(s32[2,16,14,2]{1,3,2,0:T(2,128)} %param.20) | copy-start | bytes 10756
  3.3 8.3 %slice-start.1 = ((f32[896]{0:T(1024)}), f32[512]{0:T(512)S(1)}, s32[]{:S(2)}) async-start(f32[896]{0:T(1024)} %param.15), calls=%async_computation.1 | async-start | bytes 4096 | tf_op jit(solution)/shard_map/slice | solution.py:113
  3.5 9.8 %collective-permute-start.1 = (bf16[224,576]{1,0:T(8,128)(2,1)S(1)}, bf16[224,576]{1,0:T(8,128)(2,1)S(1)}, u32[]{:S(2)}, u32[]{:S(2)}) collective-permute-start(bf16[224,576]{1,0:T(8,128)(2,1)S(1)} %pad_maximum_fusion.2), channel_id=1, source_target_pairs={{0,4},{4,8},{8,12},{12,14},{14,10},{10,6},{6,2},{2,0},{1,5},{5,9},... | collective-permute-start | bytes 774152 | tf_op jit(solution)/shard_map/ppermute | solution.py:47
  6.6 28.5 %collective-permute-start = (bf16[2,128,1792]{2,1,0:T(8,128)(2,1)S(1)}, bf16[2,128,1792]{2,1,0:T(8,128)(2,1)}, u32[]{:S(2)}, u32[]{:S(2)}) collective-permute-start(bf16[2,128,1792]{2,1,0:T(8,128)(2,1)S(1)} %copy-done.5), channel_id=1, source_target_pairs={{0,1},{1,0},{2,3},{3,2},{4,5},{5,4},{6,7},{7,6},{8,9},{9,8},{10,11... | collective-permute-start | bytes 2752520 | tf_op jit(solution)/shard_map/ppermute | solution.py:117
  6.7 9.9 %collective-permute-start.10 = (bf16[224,576]{1,0:T(8,128)(2,1)S(1)}, bf16[224,576]{1,0:T(8,128)(2,1)S(1)}, u32[]{:S(2)}, u32[]{:S(2)}) collective-permute-start(bf16[224,576]{1,0:T(8,128)(2,1)S(1)} %pad_maximum_fusion.3), channel_id=1, source_target_pairs={{0,2},{4,0},{8,4},{12,8},{14,12},{10,14},{6,10},{2,6},{1,3},{5,1},... | collective-permute-start | bytes 774152 | tf_op jit(solution)/shard_map/ppermute | solution.py:48
  11.6 25.4 %copy-start.10 = (f32[576]{0:T(1024)}, f32[576]{0:T(1024)S(1)}, u32[]{:S(2)}) copy-start(f32[576]{0:T(1024)S(1)} %maximum_select_fusion.2) | copy-start | bytes 6916
  13.3 28.9 %collective-permute-start.2 = (bf16[2,128,1792]{2,1,0:T(8,128)(2,1)S(1)}, bf16[2,128,1792]{2,1,0:T(8,128)(2,1)}, u32[]{:S(2)}, u32[]{:S(2)}) collective-permute-start(bf16[2,128,1792]{2,1,0:T(8,128)(2,1)S(1)} %copy-done.5), channel_id=1, source_target_pairs={{0,16},{16,0},{1,17},{17,1},{2,18},{18,2},{3,19},{19,3},{4,20},{20... | collective-permute-start | bytes 2752520 | tf_op jit(solution)/shard_map/ppermute | solution.py:119
  15.1 9.9 %collective-permute-start.4 = (bf16[224,576]{1,0:T(8,128)(2,1)S(1)}, bf16[224,576]{1,0:T(8,128)(2,1)S(1)}, u32[]{:S(2)}, u32[]{:S(2)}) collective-permute-start(bf16[224,576]{1,0:T(8,128)(2,1)S(1)} %collective-permute-done.1), channel_id=1, source_target_pairs={{0,4},{4,8},{8,12},{12,14},{14,10},{10,6},{6,2},{2,0},{1,5},{5,9},... | collective-permute-start | bytes 774152 | tf_op jit(solution)/shard_map/ppermute | solution.py:47
  16.6 7.8 %collective-permute-start.11 = (bf16[224,576]{1,0:T(8,128)(2,1)S(1)}, bf16[224,576]{1,0:T(8,128)(2,1)S(1)}, u32[]{:S(2)}, u32[]{:S(2)}) collective-permute-start(bf16[224,576]{1,0:T(8,128)(2,1)S(1)} %collective-permute-done.10), channel_id=1, source_target_pairs={{0,2},{4,0},{8,4},{12,8},{14,12},{10,14},{6,10},{2,6},{1,3},{5,1},... | collective-permute-start | bytes 774152 | tf_op jit(solution)/shard_map/ppermute | solution.py:48
  24.5 7.0 %collective-permute-start.12 = (bf16[224,576]{1,0:T(8,128)(2,1)S(1)}, bf16[224,576]{1,0:T(8,128)(2,1)S(1)}, u32[]{:S(2)}, u32[]{:S(2)}) collective-permute-start(bf16[224,576]{1,0:T(8,128)(2,1)S(1)} %collective-permute-done.11), channel_id=1, source_target_pairs={{0,2},{4,0},{8,4},{12,8},{14,12},{10,14},{6,10},{2,6},{1,3},{5,1},... | collective-permute-start | bytes 774152 | tf_op jit(solution)/shard_map/ppermute | solution.py:48
  25.0 7.0 %collective-permute-start.5 = (bf16[224,576]{1,0:T(8,128)(2,1)S(1)}, bf16[224,576]{1,0:T(8,128)(2,1)S(1)}, u32[]{:S(2)}, u32[]{:S(2)}) collective-permute-start(bf16[224,576]{1,0:T(8,128)(2,1)S(1)} %collective-permute-done.4), channel_id=1, source_target_pairs={{0,4},{4,8},{8,12},{12,14},{14,10},{10,6},{6,2},{2,0},{1,5},{5,9},... | collective-permute-start | bytes 774152 | tf_op jit(solution)/shard_map/ppermute | solution.py:47
  31.5 7.3 %collective-permute-start.13 = (bf16[224,576]{1,0:T(8,128)(2,1)S(1)}, bf16[224,576]{1,0:T(8,128)(2,1)S(1)}, u32[]{:S(2)}, u32[]{:S(2)}) collective-permute-start(bf16[224,576]{1,0:T(8,128)(2,1)S(1)} %collective-permute-done.12), channel_id=1, source_target_pairs={{0,2},{4,0},{8,4},{12,8},{14,12},{10,14},{6,10},{2,6},{1,3},{5,1},... | collective-permute-start | bytes 774152 | tf_op jit(solution)/shard_map/ppermute | solution.py:48
  32.0 8.0 %collective-permute-start.6 = (bf16[224,576]{1,0:T(8,128)(2,1)S(1)}, bf16[224,576]{1,0:T(8,128)(2,1)S(1)}, u32[]{:S(2)}, u32[]{:S(2)}) collective-permute-start(bf16[224,576]{1,0:T(8,128)(2,1)S(1)} %collective-permute-done.5), channel_id=1, source_target_pairs={{0,4},{4,8},{8,12},{12,14},{14,10},{10,6},{6,2},{2,0},{1,5},{5,9},... | collective-permute-start | bytes 774152 | tf_op jit(solution)/shard_map/ppermute | solution.py:47
  38.8 6.6 %collective-permute-start.14 = (bf16[224,576]{1,0:T(8,128)(2,1)S(1)}, bf16[224,576]{1,0:T(8,128)(2,1)S(1)}, u32[]{:S(2)}, u32[]{:S(2)}) collective-permute-start(bf16[224,576]{1,0:T(8,128)(2,1)S(1)} %collective-permute-done.13), channel_id=1, source_target_pairs={{0,2},{4,0},{8,4},{12,8},{14,12},{10,14},{6,10},{2,6},{1,3},{5,1},... | collective-permute-start | bytes 774152 | tf_op jit(solution)/shard_map/ppermute | solution.py:48
  40.0 6.9 %collective-permute-start.7 = (bf16[224,576]{1,0:T(8,128)(2,1)S(1)}, bf16[224,576]{1,0:T(8,128)(2,1)S(1)}, u32[]{:S(2)}, u32[]{:S(2)}) collective-permute-start(bf16[224,576]{1,0:T(8,128)(2,1)S(1)} %collective-permute-done.6), channel_id=1, source_target_pairs={{0,4},{4,8},{8,12},{12,14},{14,10},{10,6},{6,2},{2,0},{1,5},{5,9},... | collective-permute-start | bytes 774152 | tf_op jit(solution)/shard_map/ppermute | solution.py:47
  42.2 29.5 %collective-permute-start.3 = (bf16[2,128,1792]{2,1,0:T(8,128)(2,1)}, bf16[2,128,1792]{2,1,0:T(8,128)(2,1)S(1)}, u32[]{:S(2)}, u32[]{:S(2)}) collective-permute-start(bf16[2,128,1792]{2,1,0:T(8,128)(2,1)} %collective-permute-done.2), channel_id=1, source_target_pairs={{0,1},{1,0},{2,3},{3,2},{4,5},{5,4},{6,7},{7,6},{8,9},{9,8},{10,11... | collective-permute-start | bytes 2752520 | tf_op jit(solution)/shard_map/ppermute | solution.py:120
  45.4 7.7 %collective-permute-start.15 = (bf16[224,576]{1,0:T(8,128)(2,1)S(1)}, bf16[224,576]{1,0:T(8,128)(2,1)S(1)}, u32[]{:S(2)}, u32[]{:S(2)}) collective-permute-start(bf16[224,576]{1,0:T(8,128)(2,1)S(1)} %collective-permute-done.14), channel_id=1, source_target_pairs={{0,2},{4,0},{8,4},{12,8},{14,12},{10,14},{6,10},{2,6},{1,3},{5,1},... | collective-permute-start | bytes 774152 | tf_op jit(solution)/shard_map/ppermute | solution.py:48
  46.9 7.7 %collective-permute-start.8 = (bf16[224,576]{1,0:T(8,128)(2,1)S(1)}, bf16[224,576]{1,0:T(8,128)(2,1)S(1)}, u32[]{:S(2)}, u32[]{:S(2)}) collective-permute-start(bf16[224,576]{1,0:T(8,128)(2,1)S(1)} %collective-permute-done.7), channel_id=1, source_target_pairs={{0,4},{4,8},{8,12},{12,14},{14,10},{10,6},{6,2},{2,0},{1,5},{5,9},... | collective-permute-start | bytes 774152 | tf_op jit(solution)/shard_map/ppermute | solution.py:47
  53.1 6.6 %collective-permute-start.16 = (bf16[224,576]{1,0:T(8,128)(2,1)S(1)}, bf16[224,576]{1,0:T(8,128)(2,1)S(1)}, u32[]{:S(2)}, u32[]{:S(2)}) collective-permute-start(bf16[224,576]{1,0:T(8,128)(2,1)S(1)} %collective-permute-done.15), channel_id=1, source_target_pairs={{0,2},{4,0},{8,4},{12,8},{14,12},{10,14},{6,10},{2,6},{1,3},{5,1},... | collective-permute-start | bytes 774152 | tf_op jit(solution)/shard_map/ppermute | solution.py:48
  54.5 9.8 %collective-permute-start.9 = (bf16[224,576]{1,0:T(8,128)(2,1)S(1)}, bf16[224,576]{1,0:T(8,128)(2,1)S(1)}, u32[]{:S(2)}, u32[]{:S(2)}) collective-permute-start(bf16[224,576]{1,0:T(8,128)(2,1)S(1)} %collective-permute-done.8), channel_id=1, source_target_pairs={{0,4},{4,8},{8,12},{12,14},{14,10},{10,6},{6,2},{2,0},{1,5},{5,9},... | collective-permute-start | bytes 774152 | tf_op jit(solution)/shard_map/ppermute | solution.py:47
  81.5 8.5 %collective-permute-start.17 = (bf16[2,128,192]{1,0,2:T(2,128)(2,1)S(1)}, bf16[2,128,192]{1,0,2:T(2,128)(2,1)S(1)}, u32[]{:S(2)}, u32[]{:S(2)}) collective-permute-start(bf16[2,128,192]{1,0,2:T(2,128)(2,1)S(1)} %fusion.36), channel_id=1, source_target_pairs={{0,16},{16,0},{1,17},{17,1},{2,18},{18,2},{3,19},{19,3},{4,20},{20... | collective-permute-start | bytes 294920 | tf_op jit(solution)/shard_map/ppermute | solution.py:157
  89.8 7.7 %collective-permute-start.25 = (bf16[2,128,384]{1,2,0:T(8,128)(2,1)S(1)}, bf16[2,128,384]{1,2,0:T(8,128)(2,1)S(1)}, u32[]{:S(2)}, u32[]{:S(2)}) collective-permute-start(bf16[2,128,384]{1,2,0:T(8,128)(2,1)S(1)} %bitcast.163), channel_id=1, source_target_pairs={{0,16},{16,0},{1,17},{17,1},{2,18},{18,2},{3,19},{19,3},{4,20},{20... | collective-permute-start | bytes 589832 | tf_op jit(solution)/shard_map/ppermute | solution.py:159
  90.5 5.0 %collective-permute-start.18 = (bf16[2,128,256]{1,0,2:T(2,128)(2,1)S(1)}, bf16[2,128,256]{1,0,2:T(2,128)(2,1)S(1)}, u32[]{:S(2)}, u32[]{:S(2)}) collective-permute-start(bf16[2,128,256]{1,0,2:T(2,128)(2,1)S(1)} %pad_maximum_fusion.4), channel_id=1, source_target_pairs={{0,4},{4,8},{8,12},{12,14},{14,10},{10,6},{6,2},{2,0},{1,5},{5,9},... | collective-permute-start | bytes 393224 | tf_op jit(solution)/shard_map/ppermute | solution.py:180
  92.1 5.0 %collective-permute-start.22 = (bf16[2,128,256]{1,0,2:T(2,128)(2,1)S(1)}, bf16[2,128,256]{1,0,2:T(2,128)(2,1)S(1)}, u32[]{:S(2)}, u32[]{:S(2)}) collective-permute-start(bf16[2,128,256]{1,0,2:T(2,128)(2,1)S(1)} %pad_maximum_fusion.4), channel_id=1, source_target_pairs={{0,2},{4,0},{8,4},{12,8},{14,12},{10,14},{6,10},{2,6},{1,3},{5,1},... | collective-permute-start | bytes 393224 | tf_op jit(solution)/shard_map/ppermute | solution.py:183
  95.5 5.1 %collective-permute-start.19 = (bf16[2,128,256]{1,0,2:T(2,128)(2,1)S(1)}, bf16[2,128,256]{1,0,2:T(2,128)(2,1)}, u32[]{:S(2)}, u32[]{:S(2)}) collective-permute-start(bf16[2,128,256]{1,0,2:T(2,128)(2,1)S(1)} %collective-permute-done.18), channel_id=1, source_target_pairs={{0,4},{4,8},{8,12},{12,14},{14,10},{10,6},{6,2},{2,0},{1,5},{5,9},... | collective-permute-start | bytes 393224 | tf_op jit(solution)/shard_map/ppermute | solution.py:180
  97.1 7.3 %collective-permute-start.23 = (bf16[2,128,256]{1,0,2:T(2,128)(2,1)S(1)}, bf16[2,128,256]{1,0,2:T(2,128)(2,1)S(1)}, u32[]{:S(2)}, u32[]{:S(2)}) collective-permute-start(bf16[2,128,256]{1,0,2:T(2,128)(2,1)S(1)} %collective-permute-done.22), channel_id=1, source_target_pairs={{0,2},{4,0},{8,4},{12,8},{14,12},{10,14},{6,10},{2,6},{1,3},{5,1},... | collective-permute-start | bytes 393224 | tf_op jit(solution)/shard_map/ppermute | solution.py:183
  100.6 5.5 %collective-permute-start.20 = (bf16[2,128,256]{1,0,2:T(2,128)(2,1)}, bf16[2,128,256]{1,0,2:T(2,128)(2,1)}, u32[]{:S(2)}, u32[]{:S(2)}) collective-permute-start(bf16[2,128,256]{1,0,2:T(2,128)(2,1)} %collective-permute-done.19), channel_id=1, source_target_pairs={{0,4},{4,8},{8,12},{12,14},{14,10},{10,6},{6,2},{2,0},{1,5},{5,9},... | collective-permute-start | bytes 393224 | tf_op jit(solution)/shard_map/ppermute | solution.py:180
  104.4 5.0 %collective-permute-start.24 = (bf16[2,128,256]{1,0,2:T(2,128)(2,1)S(1)}, bf16[2,128,256]{1,0,2:T(2,128)(2,1)S(1)}, u32[]{:S(2)}, u32[]{:S(2)}) collective-permute-start(bf16[2,128,256]{1,0,2:T(2,128)(2,1)S(1)} %collective-permute-done.23), channel_id=1, source_target_pairs={{0,2},{4,0},{8,4},{12,8},{14,12},{10,14},{6,10},{2,6},{1,3},{5,1},... | collective-permute-start | bytes 393224 | tf_op jit(solution)/shard_map/ppermute | solution.py:183
  106.1 5.5 %collective-permute-start.21 = (bf16[2,128,256]{1,0,2:T(2,128)(2,1)}, bf16[2,128,256]{1,0,2:T(2,128)(2,1)S(1)}, u32[]{:S(2)}, u32[]{:S(2)}) collective-permute-start(bf16[2,128,256]{1,0,2:T(2,128)(2,1)} %collective-permute-done.20), channel_id=1, source_target_pairs={{0,4},{4,8},{8,12},{12,14},{14,10},{10,6},{6,2},{2,0},{1,5},{5,9},... | collective-permute-start | bytes 393224 | tf_op jit(solution)/shard_map/ppermute | solution.py:180
  (13 other events, 50.3 us)

commit v23 on v17

--- a/solution.py
+++ b/solution.py
@@ -92,14 +92,11 @@
     rows_here = w_query.shape[0]
 
     def panel_rows(start, stop):
-        return jnp.concatenate(
-            [
-                lax.dynamic_slice_in_dim(rotary_w[start:stop], group * split, split, 1),
-                lax.dynamic_slice_in_dim(
-                    value_weight[start:stop], group * value_split, value_split, 1
-                ),
-            ],
-            axis=1,
+        rotary_rows, value_rows_w = rotary_w[start:stop], value_weight[start:stop]
+        return jnp.where(
+            first,
+            jnp.concatenate([rotary_rows[:, :split], value_rows_w[:, :value_split]], axis=1),
+            jnp.concatenate([rotary_rows[:, split:], value_rows_w[:, value_split:]], axis=1),
         )
 
     full_panel, first_arrival = gather_rows(
@@ -149,13 +146,16 @@
         axis=-1,
     )
     mine = result[:passages]
-    returned = lax.ppermute(result[passages:], "groups", SWAP)
-    low = jnp.where(first, mine, returned)
-    high = jnp.where(first, returned, mine)
-    rotary_rows = jnp.concatenate([low[..., :split], high[..., :split]], axis=-1)
-    query_rows = rotary_rows[..., : heads_here * HEAD_SIZE]
-    key = rotary_rows[..., heads_here * HEAD_SIZE :]
-    value_rows = jnp.concatenate([low[..., split:], high[..., split:]], axis=-1)
+    lead = split - HEAD_SIZE
+    returned_kv = lax.ppermute(result[passages:, :, lead:], "groups", SWAP)
+    returned_q = lax.ppermute(result[passages:, :, :lead], "groups", SWAP)
+    low_kv = jnp.where(first, mine[..., lead:], returned_kv)
+    high_kv = jnp.where(first, returned_kv, mine[..., lead:])
+    key = high_kv[..., :HEAD_SIZE]
+    value_rows = jnp.concatenate([low_kv[..., HEAD_SIZE:], high_kv[..., HEAD_SIZE:]], axis=-1)
+    low_q = jnp.where(first, mine[..., :lead], returned_q)
+    high_q = jnp.where(first, returned_q, mine[..., :lead])
+    query_rows = jnp.concatenate([low_q, low_kv[..., :HEAD_SIZE], high_q], axis=-1)
 
     pairs = jnp.concatenate([key, value_rows], axis=-1)
     if row_count == 8:

time: 118 us -> 123 us (1.042)
  other arithmetic: 16.4 us -> 19.4 us
  waiting for transfers between devices: 36.2 us -> 33.5 us
  local copies, waits for them, and re-layouts: 32.2 us -> 34.5 us
  starting transfers between devices: 25.5 us -> 27.3 us
    ppermute x1 -> x2, waiting for transfers between devices: 5.63 us -> 2.31 us  [the longest x1 2.3 us: shards(): returned_kv = lax.ppermute(result[passages:, :, lead:], 'groups', SWAP)]
    concatenate x0 -> x3, local copies, waits for them, and re-layouts: none -> 1.93 us  [the longest x1 1.12 us: panel_rows(): jnp.concatenate([rotary_rows[:, :split], value_rows_w[:, :value_split]],...]
    ppermute x1 -> x2, starting transfers between devices: 0.49 us -> 2.16 us  [the longest x1 1.26 us: shards(): returned_kv = lax.ppermute(result[passages:, :, lead:], 'groups', SWAP)]
  transfers between devices with their start and end apart: 25 -> 26, of which waited for: 16 -> 13; matrix products, arithmetic and copies ran while one was open for 28% -> 31% of each run, Pallas kernels for 0% -> 0%
where the time goes in v23:
time: 123 us; the launch traced here: 122 us
  local copies, waits for them, and re-layouts  34.5 us (28%)
  waiting for transfers between devices  33.5 us (27%)
  starting transfers between devices  27.3 us (22%)
  other arithmetic  19.4 us (16%)
  matrix products  6.8 us (6%)
    ppermute x7, waiting for transfers between devices, gather_rows(): ahead = lax.ppermute(ahead, 'row', forward)  21.3 us
    ppermute x7, starting transfers between devices, gather_rows(): ahead = lax.ppermute(ahead, 'row', forward)  12.5 us
    unnamed x43, local copies, waits for them, and re-layouts  11.3 us
    ppermute x4, waiting for transfers between devices, shards(): ahead = lax.ppermute(ahead, 'row', forward)  7.07 us
    ppermute x4, starting transfers between devices, shards(): ahead = lax.ppermute(ahead, 'row', forward)  5.2 us
    gather x1, local copies, waits for them, and re-layouts, gather_rows(): jnp.stack(behind_parts)[behind_pick]  4.02 us
    gather x1, local copies, waits for them, and re-layouts, gather_rows(): jnp.stack(ahead_parts)[ahead_pick]  4 us
    ppermute x7, starting transfers between devices, gather_rows(): behind = lax.ppermute(behind, 'row', backward)  2.76 us
  transfers between devices with their start and end apart: 26, of which 13 were waited for; matrix products, arithmetic and copies ran while one was open for 31% of the time, Pallas kernels for 0%

profile of v23, /device:TPU:0, one launch (start us, length us, event | category | flops | bytes accessed | tf_op | source)
XLA Modules:
  0.0 122.3 jit_solution(9684549095611155879)
XLA Ops:
  3.5 3.1 %collective-permute-start.1 = (bf16[224,576]{1,0:T(8,128)(2,1)S(1)}, bf16[224,576]{1,0:T(8,128)(2,1)}, u32[]{:S(2)}, u32[]{:S(2)}) collective-permute-start(bf16[224,576]{1,0:T(8,128)(2,1)S(1)} %maximum_select_fusion.2), channel_id=1, source_target_pairs={{0,4},{4,8},{8,12},{12,14},{14,10},{10,6},{6,2},{2,0},{1,5},{5,9},... | collective-permute-start | bytes 774152 | tf_op jit(solution)/shard_map/ppermute | solution.py:47
  12.8 1.9 %fusion.23 = (bf16[8,224,576]{2,1,0:T(8,128)(2,1)}, bf16[8,224,576]{2,1,0:T(8,128)(2,1)}) fusion(bf16[1,224,64]{2,1,0:T(8,128)(2,1)} %get-tuple-element.26, bf16[1,224,512]{2,1,0:T(8,128)(2,1)S(1)} %get-tuple-element.19, bf16[1,224,64]{2,1,0:T(8,128)(2,1)S(1)} %get-tuple-element.25, bf16[1,224,512]{2,1,0:T(8,128)(2,1)S(1)} %get-tuple-element.15, ...), kind=kLoop, calls=%fused_computation.58 | loop fusion | flops 2322430 | bytes 1605633
  15.5 1.9 %collective-permute-start.2 = (bf16[2,128,1792]{2,1,0:T(8,128)(2,1)}, bf16[2,128,1792]{2,1,0:T(8,128)(2,1)}, u32[]{:S(2)}, u32[]{:S(2)}) collective-permute-start(bf16[2,128,1792]{2,1,0:T(8,128)(2,1)} %param.12), channel_id=1, source_target_pairs={{0,16},{16,0},{1,17},{17,1},{2,18},{18,2},{3,19},{19,3},{4,20},{20... | collective-permute-start | bytes 2752520 | tf_op jit(solution)/shard_map/ppermute | solution.py:116
  17.4 1.6 %collective-permute-start.4 = (bf16[224,576]{1,0:T(8,128)(2,1)}, bf16[224,576]{1,0:T(8,128)(2,1)S(1)}, u32[]{:S(2)}, u32[]{:S(2)}) collective-permute-start(bf16[224,576]{1,0:T(8,128)(2,1)} %collective-permute-done.1), channel_id=1, source_target_pairs={{0,4},{4,8},{8,12},{12,14},{14,10},{10,6},{6,2},{2,0},{1,5},{5,9},... | collective-permute-start | bytes 774152 | tf_op jit(solution)/shard_map/ppermute | solution.py:47
  19.5 1.7 %bitcast_dynamic-update-slice_fusion.13 = bf16[8,224,576]{2,1,0:T(8,128)(2,1)} fusion(bf16[8,224,576]{2,1,0:T(8,128)(2,1)} %get-tuple-element.43, bf16[224,576]{1,0:T(8,128)(2,1)} %collective-permute-done.1), kind=kLoop, calls=%fused_computation.75 | loop fusion | bytes 573440
  21.9 4.7 %collective-permute-done.4 = bf16[224,576]{1,0:T(8,128)(2,1)S(1)} collective-permute-done((bf16[224,576]{1,0:T(8,128)(2,1)}, bf16[224,576]{1,0:T(8,128)(2,1)S(1)}, u32[]{:S(2)}, u32[]{:S(2)}) %collective-permute-start.4) | collective-permute-done | bytes 258080 | tf_op jit(solution)/shard_map/ppermute | solution.py:47
  26.6 1.6 %collective-permute-start.5 = (bf16[224,576]{1,0:T(8,128)(2,1)S(1)}, bf16[224,576]{1,0:T(8,128)(2,1)S(1)}, u32[]{:S(2)}, u32[]{:S(2)}) collective-permute-start(bf16[224,576]{1,0:T(8,128)(2,1)S(1)} %collective-permute-done.4), channel_id=1, source_target_pairs={{0,4},{4,8},{8,12},{12,14},{14,10},{10,6},{6,2},{2,0},{1,5},{5,9},... | collective-permute-start | bytes 774152 | tf_op jit(solution)/shard_map/ppermute | solution.py:47
  30.1 4.7 %collective-permute-done.5 = bf16[224,576]{1,0:T(8,128)(2,1)S(1)} collective-permute-done((bf16[224,576]{1,0:T(8,128)(2,1)S(1)}, bf16[224,576]{1,0:T(8,128)(2,1)S(1)}, u32[]{:S(2)}, u32[]{:S(2)}) %collective-permute-start.5) | collective-permute-done | bytes 258080 | tf_op jit(solution)/shard_map/ppermute | solution.py:47
  34.8 1.6 %collective-permute-start.6 = (bf16[224,576]{1,0:T(8,128)(2,1)S(1)}, bf16[224,576]{1,0:T(8,128)(2,1)S(1)}, u32[]{:S(2)}, u32[]{:S(2)}) collective-permute-start(bf16[224,576]{1,0:T(8,128)(2,1)S(1)} %collective-permute-done.5), channel_id=1, source_target_pairs={{0,4},{4,8},{8,12},{12,14},{14,10},{10,6},{6,2},{2,0},{1,5},{5,9},... | collective-permute-start | bytes 774152 | tf_op jit(solution)/shard_map/ppermute | solution.py:47
  38.4 2.0 %maximum_select_fusion = bf16[2,128,3584]{2,1,0:T(8,128)(2,1)S(1)} fusion(bf16[2,128,1792]{2,1,0:T(8,128)(2,1)S(1)} %collective-permute-done, bf16[2,128,1792]{2,1,0:T(8,128)(2,1)} %param.12, pred[]{:T(512)S(6)} %eq.14), kind=kLoop, calls=%fused_computation.14 | loop fusion | flops 8257536 | bytes 3670017 | tf_op jit(solution)/shard_map/jit(_where)/select_n | solution.py:118
  40.4 1.9 %collective-permute-done.6 = bf16[224,576]{1,0:T(8,128)(2,1)S(1)} collective-permute-done((bf16[224,576]{1,0:T(8,128)(2,1)S(1)}, bf16[224,576]{1,0:T(8,128)(2,1)S(1)}, u32[]{:S(2)}, u32[]{:S(2)}) %collective-permute-start.6) | collective-permute-done | bytes 258080 | tf_op jit(solution)/shard_map/ppermute | solution.py:47
  42.3 1.6 %collective-permute-start.7 = (bf16[224,576]{1,0:T(8,128)(2,1)S(1)}, bf16[224,576]{1,0:T(8,128)(2,1)S(1)}, u32[]{:S(2)}, u32[]{:S(2)}) collective-permute-start(bf16[224,576]{1,0:T(8,128)(2,1)S(1)} %collective-permute-done.6), channel_id=1, source_target_pairs={{0,4},{4,8},{8,12},{12,14},{14,10},{10,6},{6,2},{2,0},{1,5},{5,9},... | collective-permute-start | bytes 774152 | tf_op jit(solution)/shard_map/ppermute | solution.py:47
  45.8 3.1 %collective-permute-done.7 = bf16[224,576]{1,0:T(8,128)(2,1)S(1)} collective-permute-done((bf16[224,576]{1,0:T(8,128)(2,1)S(1)}, bf16[224,576]{1,0:T(8,128)(2,1)S(1)}, u32[]{:S(2)}, u32[]{:S(2)}) %collective-permute-start.7) | collective-permute-done | bytes 258080 | tf_op jit(solution)/shard_map/ppermute | solution.py:47
  48.9 1.6 %collective-permute-start.8 = (bf16[224,576]{1,0:T(8,128)(2,1)S(1)}, bf16[224,576]{1,0:T(8,128)(2,1)S(1)}, u32[]{:S(2)}, u32[]{:S(2)}) collective-permute-start(bf16[224,576]{1,0:T(8,128)(2,1)S(1)} %collective-permute-done.7), channel_id=1, source_target_pairs={{0,4},{4,8},{8,12},{12,14},{14,10},{10,6},{6,2},{2,0},{1,5},{5,9},... | collective-permute-start | bytes 774152 | tf_op jit(solution)/shard_map/ppermute | solution.py:47
  52.7 4.0 %collective-permute-done.8 = bf16[224,576]{1,0:T(8,128)(2,1)S(1)} collective-permute-done((bf16[224,576]{1,0:T(8,128)(2,1)S(1)}, bf16[224,576]{1,0:T(8,128)(2,1)S(1)}, u32[]{:S(2)}, u32[]{:S(2)}) %collective-permute-start.8) | collective-permute-done | bytes 258080 | tf_op jit(solution)/shard_map/ppermute | solution.py:47
  56.6 1.6 %collective-permute-start.9 = (bf16[224,576]{1,0:T(8,128)(2,1)S(1)}, bf16[224,576]{1,0:T(8,128)(2,1)S(1)}, u32[]{:S(2)}, u32[]{:S(2)}) collective-permute-start(bf16[224,576]{1,0:T(8,128)(2,1)S(1)} %collective-permute-done.8), channel_id=1, source_target_pairs={{0,4},{4,8},{8,12},{12,14},{14,10},{10,6},{6,2},{2,0},{1,5},{5,9},... | collective-permute-start | bytes 774152 | tf_op jit(solution)/shard_map/ppermute | solution.py:47
  60.3 2.9 %collective-permute-done.9 = bf16[224,576]{1,0:T(8,128)(2,1)S(1)} collective-permute-done((bf16[224,576]{1,0:T(8,128)(2,1)S(1)}, bf16[224,576]{1,0:T(8,128)(2,1)S(1)}, u32[]{:S(2)}, u32[]{:S(2)}) %collective-permute-start.9) | collective-permute-done | bytes 258080 | tf_op jit(solution)/shard_map/ppermute | solution.py:47
  64.0 4.0 %gather_fusion = bf16[8,224,576]{2,1,0:T(8,128)(2,1)} fusion(bf16[8,224,576]{2,1,0:T(8,128)(2,1)} %bitcast_dynamic-update-slice_fusion.7, s32[1024]{0:T(1024)} %get-tuple-element.46), kind=kCustom, calls=%fused_computation | custom fusion | bytes 4128800 | tf_op jit(solution)/shard_map/gather | solution.py:56
  68.8 4.0 %gather_fusion.1 = bf16[8,224,576]{2,1,0:T(8,128)(2,1)} fusion(bf16[8,224,576]{2,1,0:T(8,128)(2,1)} %bitcast_dynamic-update-slice_fusion, s32[1024]{0:T(1024)} %get-tuple-element.45), kind=kCustom, calls=%fused_computation.1 | custom fusion | bytes 4128800 | tf_op jit(solution)/shard_map/gather | solution.py:56
  72.8 2.8 %pad_maximum_fusion = bf16[8,448,576]{2,1,0:T(8,128)(2,1)S(1)} fusion(bf16[8,224,576]{2,1,0:T(8,128)(2,1)} %gather_fusion.1, bf16[8,224,576]{2,1,0:T(8,128)(2,1)} %gather_fusion), kind=kLoop, calls=%fused_computation.12 | loop fusion | flops 8257536 | bytes 8257536 | tf_op jit(solution)/shard_map/concatenate | solution.py:55
  75.6 2.0 %maximum_select_fusion.1 = bf16[2,128,3584]{2,1,0:T(8,128)(2,1)S(1)} fusion(bf16[2,128,1792]{2,1,0:T(8,128)(2,1)S(1)} %collective-permute-done.3, bf16[2,128,1792]{2,1,0:T(8,128)(2,1)} %collective-permute-done.2, pred[]{:T(512)S(6)} %eq.14), kind=kLoop, calls=%fused_computation.15 | loop fusion | flops 8257536 | bytes 3670017 | tf_op jit(solution)/shard_map/jit(_where)/select_n | solution.py:123
  79.5 2.4 %convolution_add_fusion = f32[512,576]{0,1:T(8,128)S(1)} fusion(bf16[512,3584]{1,0:T(8,128)(2,1)S(1)} %bitcast.155, bf16[3584,576]{1,0:T(8,128)(2,1)S(1)} %bitcast.150, f32[576]{0:T(1024)S(1)} %maximum_select_fusion.6), kind=kOutput, calls=%fused_computation.30 | convolution fusion | flops 2114224128 | bytes 8980736 | tf_op jit(solution)/shard_map/dot_general | solution.py:138
  86.0 2.3 %collective-permute-done.17 = bf16[2,128,192]{1,0,2:T(2,128)(2,1)S(1)} collective-permute-done((bf16[2,128,192]{1,0,2:T(2,128)(2,1)S(1)}, bf16[2,128,192]{1,0,2:T(2,128)(2,1)S(1)}, u32[]{:S(2)}, u32[]{:S(2)}) %collective-permute-start.17) | collective-permute-done | bytes 98336 | tf_op jit(solution)/shard_map/ppermute | solution.py:150
  88.8 1.8 %collective-permute-start.18 = (bf16[2,128,256]{1,0,2:T(2,128)(2,1)S(1)}, bf16[2,128,256]{1,0,2:T(2,128)(2,1)S(1)}, u32[]{:S(2)}, u32[]{:S(2)}) collective-permute-start(bf16[2,128,256]{1,0,2:T(2,128)(2,1)S(1)} %pad_maximum_fusion.4), channel_id=1, source_target_pairs={{0,4},{4,8},{8,12},{12,14},{14,10},{10,6},{6,2},{2,0},{1,5},{5,9},... | collective-permute-start | bytes 393224 | tf_op jit(solution)/shard_map/ppermute | solution.py:171
  91.8 2.3 %collective-permute-done.18 = bf16[2,128,256]{1,0,2:T(2,128)(2,1)S(1)} collective-permute-done((bf16[2,128,256]{1,0,2:T(2,128)(2,1)S(1)}, bf16[2,128,256]{1,0,2:T(2,128)(2,1)S(1)}, u32[]{:S(2)}, u32[]{:S(2)}) %collective-permute-start.18) | collective-permute-done | bytes 131104 | tf_op jit(solution)/shard_map/ppermute | solution.py:171
  94.1 1.6 %collective-permute-start.19 = (bf16[2,128,256]{1,0,2:T(2,128)(2,1)S(1)}, bf16[2,128,256]{1,0,2:T(2,128)(2,1)S(1)}, u32[]{:S(2)}, u32[]{:S(2)}) collective-permute-start(bf16[2,128,256]{1,0,2:T(2,128)(2,1)S(1)} %collective-permute-done.18), channel_id=1, source_target_pairs={{0,4},{4,8},{8,12},{12,14},{14,10},{10,6},{6,2},{2,0},{1,5},{5,9},... | collective-permute-start | bytes 393224 | tf_op jit(solution)/shard_map/ppermute | solution.py:171
  96.6 3.1 %collective-permute-done.19 = bf16[2,128,256]{1,0,2:T(2,128)(2,1)S(1)} collective-permute-done((bf16[2,128,256]{1,0,2:T(2,128)(2,1)S(1)}, bf16[2,128,256]{1,0,2:T(2,128)(2,1)S(1)}, u32[]{:S(2)}, u32[]{:S(2)}) %collective-permute-start.19) | collective-permute-done | bytes 131104 | tf_op jit(solution)/shard_map/ppermute | solution.py:171
  102.0 1.8 %copy.52 = bf16[2,2,64,7,128]{4,2,3,1,0:T(8,128)(2,1)S(1)} copy(bf16[2,2,64,7,128]{2,1,0,4,3:T(2,128)(2,1)S(1)} %reshape.488) | data formatting | bytes 917504 | tf_op jit(solution)/shard_map/reshape | solution.py:212
  104.0 1.6 %collective-permute-start.24 = (bf16[2,128,256]{1,0,2:T(2,128)(2,1)S(1)}, bf16[2,128,256]{1,0,2:T(2,128)(2,1)S(1)}, u32[]{:S(2)}, u32[]{:S(2)}) collective-permute-start(bf16[2,128,256]{1,0,2:T(2,128)(2,1)S(1)} %collective-permute-done.23), channel_id=1, source_target_pairs={{0,2},{4,0},{8,4},{12,8},{14,12},{10,14},{6,10},{2,6},{1,3},{5,1},... | collective-permute-start | bytes 393224 | tf_op jit(solution)/shard_map/ppermute | solution.py:174
  106.6 2.4 %collective-permute-done.24 = bf16[2,128,256]{1,0,2:T(2,128)(2,1)S(1)} collective-permute-done((bf16[2,128,256]{1,0,2:T(2,128)(2,1)S(1)}, bf16[2,128,256]{1,0,2:T(2,128)(2,1)S(1)}, u32[]{:S(2)}, u32[]{:S(2)}) %collective-permute-start.24) | collective-permute-done | bytes 131104 | tf_op jit(solution)/shard_map/ppermute | solution.py:174
  109.1 1.7 %collective-permute-done.21 = bf16[2,128,256]{1,0,2:T(2,128)(2,1)S(1)} collective-permute-done((bf16[2,128,256]{1,0,2:T(2,128)(2,1)S(1)}, bf16[2,128,256]{1,0,2:T(2,128)(2,1)S(1)}, u32[]{:S(2)}, u32[]{:S(2)}) %collective-permute-start.21) | collective-permute-done | bytes 131104 | tf_op jit(solution)/shard_map/ppermute | solution.py:171
  111.8 1.4 %gather_fusion.4 = bf16[12,64,256]{2,1,0:T(8,128)(2,1)} fusion(bf16[2,16,64,256]{3,2,0,1:T(8,128)(2,1)S(1)} %bitcast.147, s32[12]{0:T(128)S(1)} %reshape.456), kind=kCustom, calls=%fused_computation.4 | custom fusion | bytes 786528 | tf_op jit(solution)/shard_map/gather | solution.py:198
  (164 shorter events, 45.1 us)
Async XLA Ops:
  0.0 11.3 %copy-start = (s32[2,2,2]{2,1,0:T(2,128)S(1)}, s32[2,2,2]{2,1,0:T(2,128)}, u32[]{:S(2)}) copy-start(s32[2,2,2]{2,1,0:T(2,128)} %param.21) | copy-start | bytes 100
  2.4 8.7 %copy-start.7 = (f32[128]{0:T(128)S(1)}, f32[128]{0:T(128)}, u32[]{:S(2)}) copy-start(f32[128]{0:T(128)} %param.19) | copy-start | bytes 1540
  2.4 8.8 %copy-start.5 = (f32[896]{0:T(1024)S(1)}, f32[896]{0:T(1024)}, u32[]{:S(2)}) copy-start(f32[896]{0:T(1024)} %param.15) | copy-start | bytes 10756
  2.5 8.8 %copy-start.9 = (f32[128]{0:T(128)S(1)}, f32[128]{0:T(128)}, u32[]{:S(2)}) copy-start(f32[128]{0:T(128)} %param.17) | copy-start | bytes 1540
  2.5 10.2 %copy-start.6 = (s32[2,16,14,2]{1,3,2,0:T(2,128)S(1)}, s32[2,16,14,2]{1,3,2,0:T(2,128)}, u32[]{:S(2)}) copy-start(s32[2,16,14,2]{1,3,2,0:T(2,128)} %param.20) | copy-start | bytes 10756
  3.3 11.4 %slice-start = ((f32[896]{0:T(1024)}), f32[512]{0:T(512)S(1)}, s32[]{:S(2)}) async-start(f32[896]{0:T(1024)} %param.15), calls=%async_computation | async-start | bytes 4096 | tf_op jit(solution)/shard_map/slice | solution.py:110
  3.5 12.0 %collective-permute-start.1 = (bf16[224,576]{1,0:T(8,128)(2,1)S(1)}, bf16[224,576]{1,0:T(8,128)(2,1)}, u32[]{:S(2)}, u32[]{:S(2)}) collective-permute-start(bf16[224,576]{1,0:T(8,128)(2,1)S(1)} %maximum_select_fusion.2), channel_id=1, source_target_pairs={{0,4},{4,8},{8,12},{12,14},{14,10},{10,6},{6,2},{2,0},{1,5},{5,9},... | collective-permute-start | bytes 774152 | tf_op jit(solution)/shard_map/ppermute | solution.py:47
  6.6 12.4 %collective-permute-start.10 = (bf16[224,576]{1,0:T(8,128)(2,1)S(1)}, bf16[224,576]{1,0:T(8,128)(2,1)S(1)}, u32[]{:S(2)}, u32[]{:S(2)}) collective-permute-start(bf16[224,576]{1,0:T(8,128)(2,1)S(1)} %maximum_select_fusion.5), channel_id=1, source_target_pairs={{0,2},{4,0},{8,4},{12,8},{14,12},{10,14},{6,10},{2,6},{1,3},{5,1},... | collective-permute-start | bytes 774152 | tf_op jit(solution)/shard_map/ppermute | solution.py:48
  6.7 31.6 %collective-permute-start = (bf16[2,128,1792]{2,1,0:T(8,128)(2,1)}, bf16[2,128,1792]{2,1,0:T(8,128)(2,1)S(1)}, u32[]{:S(2)}, u32[]{:S(2)}) collective-permute-start(bf16[2,128,1792]{2,1,0:T(8,128)(2,1)} %param.12), channel_id=1, source_target_pairs={{0,1},{1,0},{2,3},{3,2},{4,5},{5,4},{6,7},{7,6},{8,9},{9,8},{10,11... | collective-permute-start | bytes 2752520 | tf_op jit(solution)/shard_map/ppermute | solution.py:114
  15.5 30.3 %collective-permute-start.2 = (bf16[2,128,1792]{2,1,0:T(8,128)(2,1)}, bf16[2,128,1792]{2,1,0:T(8,128)(2,1)}, u32[]{:S(2)}, u32[]{:S(2)}) collective-permute-start(bf16[2,128,1792]{2,1,0:T(8,128)(2,1)} %param.12), channel_id=1, source_target_pairs={{0,16},{16,0},{1,17},{17,1},{2,18},{18,2},{3,19},{19,3},{4,20},{20... | collective-permute-start | bytes 2752520 | tf_op jit(solution)/shard_map/ppermute | solution.py:116
  17.4 9.2 %collective-permute-start.4 = (bf16[224,576]{1,0:T(8,128)(2,1)}, bf16[224,576]{1,0:T(8,128)(2,1)S(1)}, u32[]{:S(2)}, u32[]{:S(2)}) collective-permute-start(bf16[224,576]{1,0:T(8,128)(2,1)} %collective-permute-done.1), channel_id=1, source_target_pairs={{0,4},{4,8},{8,12},{12,14},{14,10},{10,6},{6,2},{2,0},{1,5},{5,9},... | collective-permute-start | bytes 774152 | tf_op jit(solution)/shard_map/ppermute | solution.py:47
  19.0 9.2 %collective-permute-start.11 = (bf16[224,576]{1,0:T(8,128)(2,1)S(1)}, bf16[224,576]{1,0:T(8,128)(2,1)S(1)}, u32[]{:S(2)}, u32[]{:S(2)}) collective-permute-start(bf16[224,576]{1,0:T(8,128)(2,1)S(1)} %collective-permute-done.10), channel_id=1, source_target_pairs={{0,2},{4,0},{8,4},{12,8},{14,12},{10,14},{6,10},{2,6},{1,3},{5,1},... | collective-permute-start | bytes 774152 | tf_op jit(solution)/shard_map/ppermute | solution.py:48
  26.6 8.2 %collective-permute-start.5 = (bf16[224,576]{1,0:T(8,128)(2,1)S(1)}, bf16[224,576]{1,0:T(8,128)(2,1)S(1)}, u32[]{:S(2)}, u32[]{:S(2)}) collective-permute-start(bf16[224,576]{1,0:T(8,128)(2,1)S(1)} %collective-permute-done.4), channel_id=1, source_target_pairs={{0,4},{4,8},{8,12},{12,14},{14,10},{10,6},{6,2},{2,0},{1,5},{5,9},... | collective-permute-start | bytes 774152 | tf_op jit(solution)/shard_map/ppermute | solution.py:47
  28.2 8.2 %collective-permute-start.12 = (bf16[224,576]{1,0:T(8,128)(2,1)S(1)}, bf16[224,576]{1,0:T(8,128)(2,1)S(1)}, u32[]{:S(2)}, u32[]{:S(2)}) collective-permute-start(bf16[224,576]{1,0:T(8,128)(2,1)S(1)} %collective-permute-done.11), channel_id=1, source_target_pairs={{0,2},{4,0},{8,4},{12,8},{14,12},{10,14},{6,10},{2,6},{1,3},{5,1},... | collective-permute-start | bytes 774152 | tf_op jit(solution)/shard_map/ppermute | solution.py:48
  34.8 7.4 %collective-permute-start.6 = (bf16[224,576]{1,0:T(8,128)(2,1)S(1)}, bf16[224,576]{1,0:T(8,128)(2,1)S(1)}, u32[]{:S(2)}, u32[]{:S(2)}) collective-permute-start(bf16[224,576]{1,0:T(8,128)(2,1)S(1)} %collective-permute-done.5), channel_id=1, source_target_pairs={{0,4},{4,8},{8,12},{12,14},{14,10},{10,6},{6,2},{2,0},{1,5},{5,9},... | collective-permute-start | bytes 774152 | tf_op jit(solution)/shard_map/ppermute | solution.py:47
  36.4 8.2 %collective-permute-start.13 = (bf16[224,576]{1,0:T(8,128)(2,1)S(1)}, bf16[224,576]{1,0:T(8,128)(2,1)S(1)}, u32[]{:S(2)}, u32[]{:S(2)}) collective-permute-start(bf16[224,576]{1,0:T(8,128)(2,1)S(1)} %collective-permute-done.12), channel_id=1, source_target_pairs={{0,2},{4,0},{8,4},{12,8},{14,12},{10,14},{6,10},{2,6},{1,3},{5,1},... | collective-permute-start | bytes 774152 | tf_op jit(solution)/shard_map/ppermute | solution.py:48
  42.3 6.6 %collective-permute-start.7 = (bf16[224,576]{1,0:T(8,128)(2,1)S(1)}, bf16[224,576]{1,0:T(8,128)(2,1)S(1)}, u32[]{:S(2)}, u32[]{:S(2)}) collective-permute-start(bf16[224,576]{1,0:T(8,128)(2,1)S(1)} %collective-permute-done.6), channel_id=1, source_target_pairs={{0,4},{4,8},{8,12},{12,14},{14,10},{10,6},{6,2},{2,0},{1,5},{5,9},... | collective-permute-start | bytes 774152 | tf_op jit(solution)/shard_map/ppermute | solution.py:47
  44.6 6.9 %collective-permute-start.14 = (bf16[224,576]{1,0:T(8,128)(2,1)S(1)}, bf16[224,576]{1,0:T(8,128)(2,1)S(1)}, u32[]{:S(2)}, u32[]{:S(2)}) collective-permute-start(bf16[224,576]{1,0:T(8,128)(2,1)S(1)} %collective-permute-done.13), channel_id=1, source_target_pairs={{0,2},{4,0},{8,4},{12,8},{14,12},{10,14},{6,10},{2,6},{1,3},{5,1},... | collective-permute-start | bytes 774152 | tf_op jit(solution)/shard_map/ppermute | solution.py:48
  45.8 29.8 %collective-permute-start.3 = (bf16[2,128,1792]{2,1,0:T(8,128)(2,1)}, bf16[2,128,1792]{2,1,0:T(8,128)(2,1)S(1)}, u32[]{:S(2)}, u32[]{:S(2)}) collective-permute-start(bf16[2,128,1792]{2,1,0:T(8,128)(2,1)} %collective-permute-done.2), channel_id=1, source_target_pairs={{0,1},{1,0},{2,3},{3,2},{4,5},{5,4},{6,7},{7,6},{8,9},{9,8},{10,11... | collective-permute-start | bytes 2752520 | tf_op jit(solution)/shard_map/ppermute | solution.py:117
  48.9 7.7 %collective-permute-start.8 = (bf16[224,576]{1,0:T(8,128)(2,1)S(1)}, bf16[224,576]{1,0:T(8,128)(2,1)S(1)}, u32[]{:S(2)}, u32[]{:S(2)}) collective-permute-start(bf16[224,576]{1,0:T(8,128)(2,1)S(1)} %collective-permute-done.7), channel_id=1, source_target_pairs={{0,4},{4,8},{8,12},{12,14},{14,10},{10,6},{6,2},{2,0},{1,5},{5,9},... | collective-permute-start | bytes 774152 | tf_op jit(solution)/shard_map/ppermute | solution.py:47
  51.5 7.7 %collective-permute-start.15 = (bf16[224,576]{1,0:T(8,128)(2,1)S(1)}, bf16[224,576]{1,0:T(8,128)(2,1)S(1)}, u32[]{:S(2)}, u32[]{:S(2)}) collective-permute-start(bf16[224,576]{1,0:T(8,128)(2,1)S(1)} %collective-permute-done.14), channel_id=1, source_target_pairs={{0,2},{4,0},{8,4},{12,8},{14,12},{10,14},{6,10},{2,6},{1,3},{5,1},... | collective-permute-start | bytes 774152 | tf_op jit(solution)/shard_map/ppermute | solution.py:48
  56.6 6.6 %collective-permute-start.9 = (bf16[224,576]{1,0:T(8,128)(2,1)S(1)}, bf16[224,576]{1,0:T(8,128)(2,1)S(1)}, u32[]{:S(2)}, u32[]{:S(2)}) collective-permute-start(bf16[224,576]{1,0:T(8,128)(2,1)S(1)} %collective-permute-done.8), channel_id=1, source_target_pairs={{0,4},{4,8},{8,12},{12,14},{14,10},{10,6},{6,2},{2,0},{1,5},{5,9},... | collective-permute-start | bytes 774152 | tf_op jit(solution)/shard_map/ppermute | solution.py:47
  59.1 8.9 %collective-permute-start.16 = (bf16[224,576]{1,0:T(8,128)(2,1)S(1)}, bf16[224,576]{1,0:T(8,128)(2,1)S(1)}, u32[]{:S(2)}, u32[]{:S(2)}) collective-permute-start(bf16[224,576]{1,0:T(8,128)(2,1)S(1)} %collective-permute-done.15), channel_id=1, source_target_pairs={{0,2},{4,0},{8,4},{12,8},{14,12},{10,14},{6,10},{2,6},{1,3},{5,1},... | collective-permute-start | bytes 774152 | tf_op jit(solution)/shard_map/ppermute | solution.py:48
  83.6 4.7 %collective-permute-start.17 = (bf16[2,128,192]{1,0,2:T(2,128)(2,1)S(1)}, bf16[2,128,192]{1,0,2:T(2,128)(2,1)S(1)}, u32[]{:S(2)}, u32[]{:S(2)}) collective-permute-start(bf16[2,128,192]{1,0,2:T(2,128)(2,1)S(1)} %pad_maximum_fusion.6), channel_id=1, source_target_pairs={{0,16},{16,0},{1,17},{17,1},{2,18},{18,2},{3,19},{19,3},{4,20},{20... | collective-permute-start | bytes 294920 | tf_op jit(solution)/shard_map/ppermute | solution.py:150
  85.1 11.2 %collective-permute-start.25 = (bf16[2,128,384]{1,0,2:T(2,128)(2,1)S(1)}, bf16[2,128,384]{1,0,2:T(2,128)(2,1)S(1)}, u32[]{:S(2)}, u32[]{:S(2)}) collective-permute-start(bf16[2,128,384]{1,0,2:T(2,128)(2,1)S(1)} %slice.167), channel_id=1, source_target_pairs={{0,16},{16,0},{1,17},{17,1},{2,18},{18,2},{3,19},{19,3},{4,20},{20... | collective-permute-start | bytes 589832 | tf_op jit(solution)/shard_map/ppermute | solution.py:151
  88.8 5.3 %collective-permute-start.18 = (bf16[2,128,256]{1,0,2:T(2,128)(2,1)S(1)}, bf16[2,128,256]{1,0,2:T(2,128)(2,1)S(1)}, u32[]{:S(2)}, u32[]{:S(2)}) collective-permute-start(bf16[2,128,256]{1,0,2:T(2,128)(2,1)S(1)} %pad_maximum_fusion.4), channel_id=1, source_target_pairs={{0,4},{4,8},{8,12},{12,14},{14,10},{10,6},{6,2},{2,0},{1,5},{5,9},... | collective-permute-start | bytes 393224 | tf_op jit(solution)/shard_map/ppermute | solution.py:171
  90.6 5.0 %collective-permute-start.22 = (bf16[2,128,256]{1,0,2:T(2,128)(2,1)S(1)}, bf16[2,128,256]{1,0,2:T(2,128)(2,1)S(1)}, u32[]{:S(2)}, u32[]{:S(2)}) collective-permute-start(bf16[2,128,256]{1,0,2:T(2,128)(2,1)S(1)} %pad_maximum_fusion.4), channel_id=1, source_target_pairs={{0,2},{4,0},{8,4},{12,8},{14,12},{10,14},{6,10},{2,6},{1,3},{5,1},... | collective-permute-start | bytes 393224 | tf_op jit(solution)/shard_map/ppermute | solution.py:174
  94.1 5.6 %collective-permute-start.19 = (bf16[2,128,256]{1,0,2:T(2,128)(2,1)S(1)}, bf16[2,128,256]{1,0,2:T(2,128)(2,1)S(1)}, u32[]{:S(2)}, u32[]{:S(2)}) collective-permute-start(bf16[2,128,256]{1,0,2:T(2,128)(2,1)S(1)} %collective-permute-done.18), channel_id=1, source_target_pairs={{0,4},{4,8},{8,12},{12,14},{14,10},{10,6},{6,2},{2,0},{1,5},{5,9},... | collective-permute-start | bytes 393224 | tf_op jit(solution)/shard_map/ppermute | solution.py:171
  95.7 8.3 %collective-permute-start.23 = (bf16[2,128,256]{1,0,2:T(2,128)(2,1)S(1)}, bf16[2,128,256]{1,0,2:T(2,128)(2,1)S(1)}, u32[]{:S(2)}, u32[]{:S(2)}) collective-permute-start(bf16[2,128,256]{1,0,2:T(2,128)(2,1)S(1)} %collective-permute-done.22), channel_id=1, source_target_pairs={{0,2},{4,0},{8,4},{12,8},{14,12},{10,14},{6,10},{2,6},{1,3},{5,1},... | collective-permute-start | bytes 393224 | tf_op jit(solution)/shard_map/ppermute | solution.py:174
  99.7 6.1 %collective-permute-start.20 = (bf16[2,128,256]{1,0,2:T(2,128)(2,1)S(1)}, bf16[2,128,256]{1,0,2:T(2,128)(2,1)S(1)}, u32[]{:S(2)}, u32[]{:S(2)}) collective-permute-start(bf16[2,128,256]{1,0,2:T(2,128)(2,1)S(1)} %collective-permute-done.19), channel_id=1, source_target_pairs={{0,4},{4,8},{8,12},{12,14},{14,10},{10,6},{6,2},{2,0},{1,5},{5,9},... | collective-permute-start | bytes 393224 | tf_op jit(solution)/shard_map/ppermute | solution.py:171
  104.0 5.0 %collective-permute-start.24 = (bf16[2,128,256]{1,0,2:T(2,128)(2,1)S(1)}, bf16[2,128,256]{1,0,2:T(2,128)(2,1)S(1)}, u32[]{:S(2)}, u32[]{:S(2)}) collective-permute-start(bf16[2,128,256]{1,0,2:T(2,128)(2,1)S(1)} %collective-permute-done.23), channel_id=1, source_target_pairs={{0,2},{4,0},{8,4},{12,8},{14,12},{10,14},{6,10},{2,6},{1,3},{5,1},... | collective-permute-start | bytes 393224 | tf_op jit(solution)/shard_map/ppermute | solution.py:174
  105.8 5.0 %collective-permute-start.21 = (bf16[2,128,256]{1,0,2:T(2,128)(2,1)S(1)}, bf16[2,128,256]{1,0,2:T(2,128)(2,1)S(1)}, u32[]{:S(2)}, u32[]{:S(2)}) collective-permute-start(bf16[2,128,256]{1,0,2:T(2,128)(2,1)S(1)} %collective-permute-done.20), channel_id=1, source_target_pairs={{0,4},{4,8},{8,12},{12,14},{14,10},{10,6},{6,2},{2,0},{1,5},{5,9},... | collective-permute-start | bytes 393224 | tf_op jit(solution)/shard_map/ppermute | solution.py:171
  (6 other events, 24.6 us)

commit v24 on v23

--- a/solution.py
+++ b/solution.py
@@ -92,11 +92,14 @@
     rows_here = w_query.shape[0]
 
     def panel_rows(start, stop):
-        rotary_rows, value_rows_w = rotary_w[start:stop], value_weight[start:stop]
-        return jnp.where(
-            first,
-            jnp.concatenate([rotary_rows[:, :split], value_rows_w[:, :value_split]], axis=1),
-            jnp.concatenate([rotary_rows[:, split:], value_rows_w[:, value_split:]], axis=1),
+        return jnp.concatenate(
+            [
+                lax.dynamic_slice_in_dim(rotary_w[start:stop], group * split, split, 1),
+                lax.dynamic_slice_in_dim(
+                    value_weight[start:stop], group * value_split, value_split, 1
+                ),
+            ],
+            axis=1,
         )
 
     full_panel, first_arrival = gather_rows(
@@ -148,11 +151,12 @@
     mine = result[:passages]
     lead = split - HEAD_SIZE
     returned_kv = lax.ppermute(result[passages:, :, lead:], "groups", SWAP)
-    returned_q = lax.ppermute(result[passages:, :, :lead], "groups", SWAP)
     low_kv = jnp.where(first, mine[..., lead:], returned_kv)
     high_kv = jnp.where(first, returned_kv, mine[..., lead:])
     key = high_kv[..., :HEAD_SIZE]
     value_rows = jnp.concatenate([low_kv[..., HEAD_SIZE:], high_kv[..., HEAD_SIZE:]], axis=-1)
+    late_q, _ = lax.optimization_barrier((result[passages:, :, :lead], value_rows))
+    returned_q = lax.ppermute(late_q, "groups", SWAP)
     low_q = jnp.where(first, mine[..., :lead], returned_q)
     high_q = jnp.where(first, returned_q, mine[..., :lead])
     query_rows = jnp.concatenate([low_q, low_kv[..., :HEAD_SIZE], high_q], axis=-1)

time: 123 us -> 116 us (0.943)
  other arithmetic: 19.4 us -> 16 us
  local copies, waits for them, and re-layouts: 34.5 us -> 32.1 us
    concatenate x3 -> x0, local copies, waits for them, and re-layouts: 1.93 us -> none  [the longest x1 1.12 us: panel_rows(): jnp.concatenate([rotary_rows[:, :split], value_rows_w[:, :value_split]],...]
  transfers between devices with their start and end apart: 26 -> 26, of which waited for: 13 -> 14; matrix products, arithmetic and copies ran while one was open for 31% -> 29% of each run, Pallas kernels for 0% -> 0%
where the time goes in v24:
time: 116 us
  waiting for transfers between devices  32.9 us (28%)
  local copies, waits for them, and re-layouts  32.1 us (28%)
  starting transfers between devices  27.1 us (23%)
  other arithmetic  16 us (14%)
  matrix products  6.81 us (6%)
    ppermute x7, waiting for transfers between devices, gather_rows(): ahead = lax.ppermute(ahead, 'row', forward)  20.8 us
    ppermute x7, starting transfers between devices, gather_rows(): ahead = lax.ppermute(ahead, 'row', forward)  12.5 us
    unnamed x43, local copies, waits for them, and re-layouts  10.4 us
    ppermute x4, waiting for transfers between devices, shards(): ahead = lax.ppermute(ahead, 'row', forward)  6.9 us
    ppermute x4, starting transfers between devices, shards(): ahead = lax.ppermute(ahead, 'row', forward)  6.4 us
    gather x1, local copies, waits for them, and re-layouts, gather_rows(): jnp.stack(behind_parts)[behind_pick]  3.9 us
    gather x1, local copies, waits for them, and re-layouts, gather_rows(): jnp.stack(ahead_parts)[ahead_pick]  3.89 us
    ppermute x7, starting transfers between devices, gather_rows(): behind = lax.ppermute(behind, 'row', backward)  2.76 us
  transfers between devices with their start and end apart: 26, of which 14 were waited for; matrix products, arithmetic and copies ran while one was open for 29% of the time, Pallas kernels for 0%

profile of v24, /device:TPU:0, one launch (start us, length us, event | category | flops | bytes accessed | tf_op | source)
XLA Modules:
  0.0 115.8 jit_solution(1828156002331469802)
XLA Ops:
  2.7 3.1 %collective-permute-start.1 = (bf16[224,576]{1,0:T(8,128)(2,1)S(1)}, bf16[224,576]{1,0:T(8,128)(2,1)S(1)}, u32[]{:S(2)}, u32[]{:S(2)}) collective-permute-start(bf16[224,576]{1,0:T(8,128)(2,1)S(1)} %pad_maximum_fusion.4), channel_id=1, source_target_pairs={{0,4},{4,8},{8,12},{12,14},{14,10},{10,6},{6,2},{2,0},{1,5},{5,9},... | collective-permute-start | bytes 774152 | tf_op jit(solution)/shard_map/ppermute | solution.py:47
  11.0 1.5 %collective-permute-done.1 = bf16[224,576]{1,0:T(8,128)(2,1)S(1)} collective-permute-done((bf16[224,576]{1,0:T(8,128)(2,1)S(1)}, bf16[224,576]{1,0:T(8,128)(2,1)S(1)}, u32[]{:S(2)}, u32[]{:S(2)}) %collective-permute-start.1) | collective-permute-done | bytes 258080 | tf_op jit(solution)/shard_map/ppermute | solution.py:47
  12.5 1.8 %collective-permute-start.2 = (bf16[2,128,1792]{2,1,0:T(8,128)(2,1)S(1)}, bf16[2,128,1792]{2,1,0:T(8,128)(2,1)}, u32[]{:S(2)}, u32[]{:S(2)}) collective-permute-start(bf16[2,128,1792]{2,1,0:T(8,128)(2,1)S(1)} %copy-done.1), channel_id=1, source_target_pairs={{0,16},{16,0},{1,17},{17,1},{2,18},{18,2},{3,19},{19,3},{4,20},{20... | collective-permute-start | bytes 2752520 | tf_op jit(solution)/shard_map/ppermute | solution.py:119
  14.3 1.6 %collective-permute-start.4 = (bf16[224,576]{1,0:T(8,128)(2,1)S(1)}, bf16[224,576]{1,0:T(8,128)(2,1)S(1)}, u32[]{:S(2)}, u32[]{:S(2)}) collective-permute-start(bf16[224,576]{1,0:T(8,128)(2,1)S(1)} %collective-permute-done.1), channel_id=1, source_target_pairs={{0,4},{4,8},{8,12},{12,14},{14,10},{10,6},{6,2},{2,0},{1,5},{5,9},... | collective-permute-start | bytes 774152 | tf_op jit(solution)/shard_map/ppermute | solution.py:47
  17.8 4.1 %collective-permute-done.4 = bf16[224,576]{1,0:T(8,128)(2,1)S(1)} collective-permute-done((bf16[224,576]{1,0:T(8,128)(2,1)S(1)}, bf16[224,576]{1,0:T(8,128)(2,1)S(1)}, u32[]{:S(2)}, u32[]{:S(2)}) %collective-permute-start.4) | collective-permute-done | bytes 258080 | tf_op jit(solution)/shard_map/ppermute | solution.py:47
  21.9 1.6 %collective-permute-start.5 = (bf16[224,576]{1,0:T(8,128)(2,1)S(1)}, bf16[224,576]{1,0:T(8,128)(2,1)S(1)}, u32[]{:S(2)}, u32[]{:S(2)}) collective-permute-start(bf16[224,576]{1,0:T(8,128)(2,1)S(1)} %collective-permute-done.4), channel_id=1, source_target_pairs={{0,4},{4,8},{8,12},{12,14},{14,10},{10,6},{6,2},{2,0},{1,5},{5,9},... | collective-permute-start | bytes 774152 | tf_op jit(solution)/shard_map/ppermute | solution.py:47
  25.4 3.4 %collective-permute-done.5 = bf16[224,576]{1,0:T(8,128)(2,1)S(1)} collective-permute-done((bf16[224,576]{1,0:T(8,128)(2,1)S(1)}, bf16[224,576]{1,0:T(8,128)(2,1)S(1)}, u32[]{:S(2)}, u32[]{:S(2)}) %collective-permute-start.5) | collective-permute-done | bytes 258080 | tf_op jit(solution)/shard_map/ppermute | solution.py:47
  28.8 1.6 %collective-permute-start.6 = (bf16[224,576]{1,0:T(8,128)(2,1)S(1)}, bf16[224,576]{1,0:T(8,128)(2,1)S(1)}, u32[]{:S(2)}, u32[]{:S(2)}) collective-permute-start(bf16[224,576]{1,0:T(8,128)(2,1)S(1)} %collective-permute-done.5), channel_id=1, source_target_pairs={{0,4},{4,8},{8,12},{12,14},{14,10},{10,6},{6,2},{2,0},{1,5},{5,9},... | collective-permute-start | bytes 774152 | tf_op jit(solution)/shard_map/ppermute | solution.py:47
  32.3 2.0 %maximum_select_fusion = bf16[2,128,3584]{2,1,0:T(8,128)(2,1)S(1)} fusion(bf16[2,128,1792]{2,1,0:T(8,128)(2,1)} %collective-permute-done, bf16[2,128,1792]{2,1,0:T(8,128)(2,1)S(1)} %copy-done.1, pred[]{:T(512)S(6)} %eq.14), kind=kLoop, calls=%fused_computation.14 | loop fusion | flops 8257536 | bytes 3670017 | tf_op jit(solution)/shard_map/jit(_where)/select_n | solution.py:121
  34.3 1.9 %collective-permute-done.6 = bf16[224,576]{1,0:T(8,128)(2,1)S(1)} collective-permute-done((bf16[224,576]{1,0:T(8,128)(2,1)S(1)}, bf16[224,576]{1,0:T(8,128)(2,1)S(1)}, u32[]{:S(2)}, u32[]{:S(2)}) %collective-permute-start.6) | collective-permute-done | bytes 258080 | tf_op jit(solution)/shard_map/ppermute | solution.py:47
  36.2 1.6 %collective-permute-start.7 = (bf16[224,576]{1,0:T(8,128)(2,1)S(1)}, bf16[224,576]{1,0:T(8,128)(2,1)S(1)}, u32[]{:S(2)}, u32[]{:S(2)}) collective-permute-start(bf16[224,576]{1,0:T(8,128)(2,1)S(1)} %collective-permute-done.6), channel_id=1, source_target_pairs={{0,4},{4,8},{8,12},{12,14},{14,10},{10,6},{6,2},{2,0},{1,5},{5,9},... | collective-permute-start | bytes 774152 | tf_op jit(solution)/shard_map/ppermute | solution.py:47
  39.7 3.1 %collective-permute-done.7 = bf16[224,576]{1,0:T(8,128)(2,1)S(1)} collective-permute-done((bf16[224,576]{1,0:T(8,128)(2,1)S(1)}, bf16[224,576]{1,0:T(8,128)(2,1)S(1)}, u32[]{:S(2)}, u32[]{:S(2)}) %collective-permute-start.7) | collective-permute-done | bytes 258080 | tf_op jit(solution)/shard_map/ppermute | solution.py:47
  42.8 1.6 %collective-permute-start.8 = (bf16[224,576]{1,0:T(8,128)(2,1)S(1)}, bf16[224,576]{1,0:T(8,128)(2,1)S(1)}, u32[]{:S(2)}, u32[]{:S(2)}) collective-permute-start(bf16[224,576]{1,0:T(8,128)(2,1)S(1)} %collective-permute-done.7), channel_id=1, source_target_pairs={{0,4},{4,8},{8,12},{12,14},{14,10},{10,6},{6,2},{2,0},{1,5},{5,9},... | collective-permute-start | bytes 774152 | tf_op jit(solution)/shard_map/ppermute | solution.py:47
  46.6 4.0 %collective-permute-done.8 = bf16[224,576]{1,0:T(8,128)(2,1)S(1)} collective-permute-done((bf16[224,576]{1,0:T(8,128)(2,1)S(1)}, bf16[224,576]{1,0:T(8,128)(2,1)S(1)}, u32[]{:S(2)}, u32[]{:S(2)}) %collective-permute-start.8) | collective-permute-done | bytes 258080 | tf_op jit(solution)/shard_map/ppermute | solution.py:47
  50.5 1.6 %collective-permute-start.9 = (bf16[224,576]{1,0:T(8,128)(2,1)S(1)}, bf16[224,576]{1,0:T(8,128)(2,1)S(1)}, u32[]{:S(2)}, u32[]{:S(2)}) collective-permute-start(bf16[224,576]{1,0:T(8,128)(2,1)S(1)} %collective-permute-done.8), channel_id=1, source_target_pairs={{0,4},{4,8},{8,12},{12,14},{14,10},{10,6},{6,2},{2,0},{1,5},{5,9},... | collective-permute-start | bytes 774152 | tf_op jit(solution)/shard_map/ppermute | solution.py:47
  54.2 2.9 %collective-permute-done.9 = bf16[224,576]{1,0:T(8,128)(2,1)S(1)} collective-permute-done((bf16[224,576]{1,0:T(8,128)(2,1)S(1)}, bf16[224,576]{1,0:T(8,128)(2,1)S(1)}, u32[]{:S(2)}, u32[]{:S(2)}) %collective-permute-start.9) | collective-permute-done | bytes 258080 | tf_op jit(solution)/shard_map/ppermute | solution.py:47
  57.9 3.9 %gather_fusion = bf16[8,224,576]{2,1,0:T(8,128)(2,1)} fusion(bf16[8,224,576]{2,1,0:T(8,128)(2,1)} %bitcast_dynamic-update-slice_fusion.8, s32[1024]{0:T(1024)S(1)} %get-tuple-element.32), kind=kCustom, calls=%fused_computation | custom fusion | bytes 4128800 | tf_op jit(solution)/shard_map/gather | solution.py:56
  62.6 3.9 %gather_fusion.1 = bf16[8,224,576]{2,1,0:T(8,128)(2,1)} fusion(bf16[8,224,576]{2,1,0:T(8,128)(2,1)} %bitcast_dynamic-update-slice_fusion, s32[1024]{0:T(1024)S(1)} %get-tuple-element.31), kind=kCustom, calls=%fused_computation.1 | custom fusion | bytes 4128800 | tf_op jit(solution)/shard_map/gather | solution.py:56
  66.5 2.8 %pad_maximum_fusion = bf16[8,448,576]{2,1,0:T(8,128)(2,1)S(1)} fusion(bf16[8,224,576]{2,1,0:T(8,128)(2,1)} %gather_fusion.1, bf16[8,224,576]{2,1,0:T(8,128)(2,1)} %gather_fusion), kind=kLoop, calls=%fused_computation.12 | loop fusion | flops 8257536 | bytes 8257536 | tf_op jit(solution)/shard_map/concatenate | solution.py:55
  69.2 2.0 %maximum_select_fusion.1 = bf16[2,128,3584]{2,1,0:T(8,128)(2,1)S(1)} fusion(bf16[2,128,1792]{2,1,0:T(8,128)(2,1)S(1)} %collective-permute-done.3, bf16[2,128,1792]{2,1,0:T(8,128)(2,1)} %collective-permute-done.2, pred[]{:T(512)S(6)} %eq.14), kind=kLoop, calls=%fused_computation.15 | loop fusion | flops 8257536 | bytes 3670017 | tf_op jit(solution)/shard_map/jit(_where)/select_n | solution.py:126
  73.1 2.4 %convolution_add_fusion = f32[512,576]{0,1:T(8,128)S(1)} fusion(bf16[512,3584]{1,0:T(8,128)(2,1)S(1)} %bitcast.143, bf16[3584,576]{1,0:T(8,128)(2,1)S(1)} %bitcast.138, f32[576]{0:T(1024)S(1)} %maximum_select_fusion.2), kind=kOutput, calls=%fused_computation.30 | convolution fusion | flops 2114224128 | bytes 8980736 | tf_op jit(solution)/shard_map/dot_general | solution.py:141
  77.9 1.8 %collective-permute-start.25 = (bf16[2,128,384]{1,0,2:T(2,128)(2,1)S(1)}, bf16[2,128,384]{1,0,2:T(2,128)(2,1)S(1)}, u32[]{:S(2)}, u32[]{:S(2)}) collective-permute-start(bf16[2,128,384]{1,0,2:T(2,128)(2,1)S(1)} %slice.137), channel_id=1, source_target_pairs={{0,16},{16,0},{1,17},{17,1},{2,18},{18,2},{3,19},{19,3},{4,20},{20... | collective-permute-start | bytes 589832 | tf_op jit(solution)/shard_map/ppermute | solution.py:159
  79.7 2.3 %collective-permute-done.17 = bf16[2,128,192]{1,0,2:T(2,128)(2,1)S(1)} collective-permute-done((bf16[2,128,192]{1,0,2:T(2,128)(2,1)S(1)}, bf16[2,128,192]{1,0,2:T(2,128)(2,1)S(1)}, u32[]{:S(2)}, u32[]{:S(2)}) %collective-permute-start.17) | collective-permute-done | bytes 98336 | tf_op jit(solution)/shard_map/ppermute | solution.py:153
  82.5 1.6 %collective-permute-start.18 = (bf16[2,128,256]{1,0,2:T(2,128)(2,1)S(1)}, bf16[2,128,256]{1,0,2:T(2,128)(2,1)S(1)}, u32[]{:S(2)}, u32[]{:S(2)}) collective-permute-start(bf16[2,128,256]{1,0,2:T(2,128)(2,1)S(1)} %pad_maximum_fusion.6), channel_id=1, source_target_pairs={{0,4},{4,8},{8,12},{12,14},{14,10},{10,6},{6,2},{2,0},{1,5},{5,9},... | collective-permute-start | bytes 393224 | tf_op jit(solution)/shard_map/ppermute | solution.py:175
  85.3 2.6 %collective-permute-done.18 = bf16[2,128,256]{1,0,2:T(2,128)(2,1)S(1)} collective-permute-done((bf16[2,128,256]{1,0,2:T(2,128)(2,1)S(1)}, bf16[2,128,256]{1,0,2:T(2,128)(2,1)S(1)}, u32[]{:S(2)}, u32[]{:S(2)}) %collective-permute-start.18) | collective-permute-done | bytes 131104 | tf_op jit(solution)/shard_map/ppermute | solution.py:175
  87.9 1.6 %collective-permute-start.19 = (bf16[2,128,256]{1,0,2:T(2,128)(2,1)S(1)}, bf16[2,128,256]{1,0,2:T(2,128)(2,1)S(1)}, u32[]{:S(2)}, u32[]{:S(2)}) collective-permute-start(bf16[2,128,256]{1,0,2:T(2,128)(2,1)S(1)} %collective-permute-done.18), channel_id=1, source_target_pairs={{0,4},{4,8},{8,12},{12,14},{14,10},{10,6},{6,2},{2,0},{1,5},{5,9},... | collective-permute-start | bytes 393224 | tf_op jit(solution)/shard_map/ppermute | solution.py:175
  90.2 3.6 %collective-permute-done.19 = bf16[2,128,256]{1,0,2:T(2,128)(2,1)S(1)} collective-permute-done((bf16[2,128,256]{1,0,2:T(2,128)(2,1)S(1)}, bf16[2,128,256]{1,0,2:T(2,128)(2,1)S(1)}, u32[]{:S(2)}, u32[]{:S(2)}) %collective-permute-start.19) | collective-permute-done | bytes 131104 | tf_op jit(solution)/shard_map/ppermute | solution.py:175
  93.9 1.6 %collective-permute-start.20 = (bf16[2,128,256]{1,0,2:T(2,128)(2,1)S(1)}, bf16[2,128,256]{1,0,2:T(2,128)(2,1)S(1)}, u32[]{:S(2)}, u32[]{:S(2)}) collective-permute-start(bf16[2,128,256]{1,0,2:T(2,128)(2,1)S(1)} %collective-permute-done.19), channel_id=1, source_target_pairs={{0,4},{4,8},{8,12},{12,14},{14,10},{10,6},{6,2},{2,0},{1,5},{5,9},... | collective-permute-start | bytes 393224 | tf_op jit(solution)/shard_map/ppermute | solution.py:175
  96.5 1.8 %copy.52 = bf16[2,2,64,7,128]{4,2,3,1,0:T(8,128)(2,1)S(1)} copy(bf16[2,2,64,7,128]{2,1,0,4,3:T(2,128)(2,1)S(1)} %reshape.378) | data formatting | bytes 917504 | tf_op jit(solution)/shard_map/reshape | solution.py:216
  99.3 1.6 %collective-permute-start.21 = (bf16[2,128,256]{1,0,2:T(2,128)(2,1)S(1)}, bf16[2,128,256]{1,0,2:T(2,128)(2,1)S(1)}, u32[]{:S(2)}, u32[]{:S(2)}) collective-permute-start(bf16[2,128,256]{1,0,2:T(2,128)(2,1)S(1)} %collective-permute-done.20), channel_id=1, source_target_pairs={{0,4},{4,8},{8,12},{12,14},{14,10},{10,6},{6,2},{2,0},{1,5},{5,9},... | collective-permute-start | bytes 393224 | tf_op jit(solution)/shard_map/ppermute | solution.py:175
  101.1 2.4 %collective-permute-done.24 = bf16[2,128,256]{1,0,2:T(2,128)(2,1)S(1)} collective-permute-done((bf16[2,128,256]{1,0,2:T(2,128)(2,1)S(1)}, bf16[2,128,256]{1,0,2:T(2,128)(2,1)S(1)}, u32[]{:S(2)}, u32[]{:S(2)}) %collective-permute-start.24) | collective-permute-done | bytes 131104 | tf_op jit(solution)/shard_map/ppermute | solution.py:178
  105.2 1.4 %gather_fusion.4 = bf16[12,64,256]{2,1,0:T(8,128)(2,1)} fusion(bf16[2,16,64,256]{3,2,0,1:T(8,128)(2,1)S(1)} %bitcast.135, s32[12]{0:T(128)S(1)} %reshape.346), kind=kCustom, calls=%fused_computation.4 | custom fusion | bytes 786528 | tf_op jit(solution)/shard_map/gather | solution.py:202
  (168 shorter events, 40.6 us)
Async XLA Ops:
  0.0 9.8 %copy-start = (s32[2,2,2]{2,1,0:T(2,128)S(1)}, s32[2,2,2]{2,1,0:T(2,128)}, u32[]{:S(2)}) copy-start(s32[2,2,2]{2,1,0:T(2,128)} %param.21) | copy-start | bytes 100
  2.4 7.2 %copy-start.7 = (f32[128]{0:T(128)S(1)}, f32[128]{0:T(128)}, u32[]{:S(2)}) copy-start(f32[128]{0:T(128)} %param.19) | copy-start | bytes 1540
  2.4 7.3 %copy-start.5 = (f32[896]{0:T(1024)S(1)}, f32[896]{0:T(1024)}, u32[]{:S(2)}) copy-start(f32[896]{0:T(1024)} %param.15) | copy-start | bytes 10756
  2.4 7.3 %copy-start.8 = (f32[128]{0:T(128)S(1)}, f32[128]{0:T(128)}, u32[]{:S(2)}) copy-start(f32[128]{0:T(128)} %param.17) | copy-start | bytes 1540
  2.5 7.6 %copy-start.6 = (s32[2,16,14,2]{1,3,2,0:T(2,128)S(1)}, s32[2,16,14,2]{1,3,2,0:T(2,128)}, u32[]{:S(2)}) copy-start(s32[2,16,14,2]{1,3,2,0:T(2,128)} %param.20) | copy-start | bytes 10756
  2.5 7.7 %slice-start = ((f32[896]{0:T(1024)}), f32[512]{0:T(512)S(1)}, s32[]{:S(2)}) async-start(f32[896]{0:T(1024)} %param.15), calls=%async_computation | async-start | bytes 4096 | tf_op jit(solution)/shard_map/slice | solution.py:113
  2.7 9.8 %collective-permute-start.1 = (bf16[224,576]{1,0:T(8,128)(2,1)S(1)}, bf16[224,576]{1,0:T(8,128)(2,1)S(1)}, u32[]{:S(2)}, u32[]{:S(2)}) collective-permute-start(bf16[224,576]{1,0:T(8,128)(2,1)S(1)} %pad_maximum_fusion.4), channel_id=1, source_target_pairs={{0,4},{4,8},{8,12},{12,14},{14,10},{10,6},{6,2},{2,0},{1,5},{5,9},... | collective-permute-start | bytes 774152 | tf_op jit(solution)/shard_map/ppermute | solution.py:47
  5.9 9.9 %collective-permute-start.10 = (bf16[224,576]{1,0:T(8,128)(2,1)S(1)}, bf16[224,576]{1,0:T(8,128)(2,1)S(1)}, u32[]{:S(2)}, u32[]{:S(2)}) collective-permute-start(bf16[224,576]{1,0:T(8,128)(2,1)S(1)} %pad_maximum_fusion.5), channel_id=1, source_target_pairs={{0,2},{4,0},{8,4},{12,8},{14,12},{10,14},{6,10},{2,6},{1,3},{5,1},... | collective-permute-start | bytes 774152 | tf_op jit(solution)/shard_map/ppermute | solution.py:48
  6.0 26.4 %collective-permute-start = (bf16[2,128,1792]{2,1,0:T(8,128)(2,1)S(1)}, bf16[2,128,1792]{2,1,0:T(8,128)(2,1)}, u32[]{:S(2)}, u32[]{:S(2)}) collective-permute-start(bf16[2,128,1792]{2,1,0:T(8,128)(2,1)S(1)} %copy-done.1), channel_id=1, source_target_pairs={{0,1},{1,0},{2,3},{3,2},{4,5},{5,4},{6,7},{7,6},{8,9},{9,8},{10,11... | collective-permute-start | bytes 2752520 | tf_op jit(solution)/shard_map/ppermute | solution.py:117
  12.5 27.2 %collective-permute-start.2 = (bf16[2,128,1792]{2,1,0:T(8,128)(2,1)S(1)}, bf16[2,128,1792]{2,1,0:T(8,128)(2,1)}, u32[]{:S(2)}, u32[]{:S(2)}) collective-permute-start(bf16[2,128,1792]{2,1,0:T(8,128)(2,1)S(1)} %copy-done.1), channel_id=1, source_target_pairs={{0,16},{16,0},{1,17},{17,1},{2,18},{18,2},{3,19},{19,3},{4,20},{20... | collective-permute-start | bytes 2752520 | tf_op jit(solution)/shard_map/ppermute | solution.py:119
  14.3 7.7 %collective-permute-start.4 = (bf16[224,576]{1,0:T(8,128)(2,1)S(1)}, bf16[224,576]{1,0:T(8,128)(2,1)S(1)}, u32[]{:S(2)}, u32[]{:S(2)}) collective-permute-start(bf16[224,576]{1,0:T(8,128)(2,1)S(1)} %collective-permute-done.1), channel_id=1, source_target_pairs={{0,4},{4,8},{8,12},{12,14},{14,10},{10,6},{6,2},{2,0},{1,5},{5,9},... | collective-permute-start | bytes 774152 | tf_op jit(solution)/shard_map/ppermute | solution.py:47
  15.8 7.7 %collective-permute-start.11 = (bf16[224,576]{1,0:T(8,128)(2,1)S(1)}, bf16[224,576]{1,0:T(8,128)(2,1)S(1)}, u32[]{:S(2)}, u32[]{:S(2)}) collective-permute-start(bf16[224,576]{1,0:T(8,128)(2,1)S(1)} %collective-permute-done.10), channel_id=1, source_target_pairs={{0,2},{4,0},{8,4},{12,8},{14,12},{10,14},{6,10},{2,6},{1,3},{5,1},... | collective-permute-start | bytes 774152 | tf_op jit(solution)/shard_map/ppermute | solution.py:48
  21.9 6.9 %collective-permute-start.5 = (bf16[224,576]{1,0:T(8,128)(2,1)S(1)}, bf16[224,576]{1,0:T(8,128)(2,1)S(1)}, u32[]{:S(2)}, u32[]{:S(2)}) collective-permute-start(bf16[224,576]{1,0:T(8,128)(2,1)S(1)} %collective-permute-done.4), channel_id=1, source_target_pairs={{0,4},{4,8},{8,12},{12,14},{14,10},{10,6},{6,2},{2,0},{1,5},{5,9},... | collective-permute-start | bytes 774152 | tf_op jit(solution)/shard_map/ppermute | solution.py:47
  23.5 6.9 %collective-permute-start.12 = (bf16[224,576]{1,0:T(8,128)(2,1)S(1)}, bf16[224,576]{1,0:T(8,128)(2,1)S(1)}, u32[]{:S(2)}, u32[]{:S(2)}) collective-permute-start(bf16[224,576]{1,0:T(8,128)(2,1)S(1)} %collective-permute-done.11), channel_id=1, source_target_pairs={{0,2},{4,0},{8,4},{12,8},{14,12},{10,14},{6,10},{2,6},{1,3},{5,1},... | collective-permute-start | bytes 774152 | tf_op jit(solution)/shard_map/ppermute | solution.py:48
  28.8 7.4 %collective-permute-start.6 = (bf16[224,576]{1,0:T(8,128)(2,1)S(1)}, bf16[224,576]{1,0:T(8,128)(2,1)S(1)}, u32[]{:S(2)}, u32[]{:S(2)}) collective-permute-start(bf16[224,576]{1,0:T(8,128)(2,1)S(1)} %collective-permute-done.5), channel_id=1, source_target_pairs={{0,4},{4,8},{8,12},{12,14},{14,10},{10,6},{6,2},{2,0},{1,5},{5,9},... | collective-permute-start | bytes 774152 | tf_op jit(solution)/shard_map/ppermute | solution.py:47
  30.4 8.1 %collective-permute-start.13 = (bf16[224,576]{1,0:T(8,128)(2,1)S(1)}, bf16[224,576]{1,0:T(8,128)(2,1)S(1)}, u32[]{:S(2)}, u32[]{:S(2)}) collective-permute-start(bf16[224,576]{1,0:T(8,128)(2,1)S(1)} %collective-permute-done.12), channel_id=1, source_target_pairs={{0,2},{4,0},{8,4},{12,8},{14,12},{10,14},{6,10},{2,6},{1,3},{5,1},... | collective-permute-start | bytes 774152 | tf_op jit(solution)/shard_map/ppermute | solution.py:48
  36.2 6.6 %collective-permute-start.7 = (bf16[224,576]{1,0:T(8,128)(2,1)S(1)}, bf16[224,576]{1,0:T(8,128)(2,1)S(1)}, u32[]{:S(2)}, u32[]{:S(2)}) collective-permute-start(bf16[224,576]{1,0:T(8,128)(2,1)S(1)} %collective-permute-done.6), channel_id=1, source_target_pairs={{0,4},{4,8},{8,12},{12,14},{14,10},{10,6},{6,2},{2,0},{1,5},{5,9},... | collective-permute-start | bytes 774152 | tf_op jit(solution)/shard_map/ppermute | solution.py:47
  38.5 6.9 %collective-permute-start.14 = (bf16[224,576]{1,0:T(8,128)(2,1)S(1)}, bf16[224,576]{1,0:T(8,128)(2,1)S(1)}, u32[]{:S(2)}, u32[]{:S(2)}) collective-permute-start(bf16[224,576]{1,0:T(8,128)(2,1)S(1)} %collective-permute-done.13), channel_id=1, source_target_pairs={{0,2},{4,0},{8,4},{12,8},{14,12},{10,14},{6,10},{2,6},{1,3},{5,1},... | collective-permute-start | bytes 774152 | tf_op jit(solution)/shard_map/ppermute | solution.py:48
  39.7 29.5 %collective-permute-start.3 = (bf16[2,128,1792]{2,1,0:T(8,128)(2,1)}, bf16[2,128,1792]{2,1,0:T(8,128)(2,1)S(1)}, u32[]{:S(2)}, u32[]{:S(2)}) collective-permute-start(bf16[2,128,1792]{2,1,0:T(8,128)(2,1)} %collective-permute-done.2), channel_id=1, source_target_pairs={{0,1},{1,0},{2,3},{3,2},{4,5},{5,4},{6,7},{7,6},{8,9},{9,8},{10,11... | collective-permute-start | bytes 2752520 | tf_op jit(solution)/shard_map/ppermute | solution.py:120
  42.8 7.7 %collective-permute-start.8 = (bf16[224,576]{1,0:T(8,128)(2,1)S(1)}, bf16[224,576]{1,0:T(8,128)(2,1)S(1)}, u32[]{:S(2)}, u32[]{:S(2)}) collective-permute-start(bf16[224,576]{1,0:T(8,128)(2,1)S(1)} %collective-permute-done.7), channel_id=1, source_target_pairs={{0,4},{4,8},{8,12},{12,14},{14,10},{10,6},{6,2},{2,0},{1,5},{5,9},... | collective-permute-start | bytes 774152 | tf_op jit(solution)/shard_map/ppermute | solution.py:47
  45.4 7.7 %collective-permute-start.15 = (bf16[224,576]{1,0:T(8,128)(2,1)S(1)}, bf16[224,576]{1,0:T(8,128)(2,1)S(1)}, u32[]{:S(2)}, u32[]{:S(2)}) collective-permute-start(bf16[224,576]{1,0:T(8,128)(2,1)S(1)} %collective-permute-done.14), channel_id=1, source_target_pairs={{0,2},{4,0},{8,4},{12,8},{14,12},{10,14},{6,10},{2,6},{1,3},{5,1},... | collective-permute-start | bytes 774152 | tf_op jit(solution)/shard_map/ppermute | solution.py:48
  50.5 6.6 %collective-permute-start.9 = (bf16[224,576]{1,0:T(8,128)(2,1)S(1)}, bf16[224,576]{1,0:T(8,128)(2,1)S(1)}, u32[]{:S(2)}, u32[]{:S(2)}) collective-permute-start(bf16[224,576]{1,0:T(8,128)(2,1)S(1)} %collective-permute-done.8), channel_id=1, source_target_pairs={{0,4},{4,8},{8,12},{12,14},{14,10},{10,6},{6,2},{2,0},{1,5},{5,9},... | collective-permute-start | bytes 774152 | tf_op jit(solution)/shard_map/ppermute | solution.py:47
  53.0 8.8 %collective-permute-start.16 = (bf16[224,576]{1,0:T(8,128)(2,1)S(1)}, bf16[224,576]{1,0:T(8,128)(2,1)S(1)}, u32[]{:S(2)}, u32[]{:S(2)}) collective-permute-start(bf16[224,576]{1,0:T(8,128)(2,1)S(1)} %collective-permute-done.15), channel_id=1, source_target_pairs={{0,2},{4,0},{8,4},{12,8},{14,12},{10,14},{6,10},{2,6},{1,3},{5,1},... | collective-permute-start | bytes 774152 | tf_op jit(solution)/shard_map/ppermute | solution.py:48
  77.3 4.7 %collective-permute-start.17 = (bf16[2,128,192]{1,0,2:T(2,128)(2,1)S(1)}, bf16[2,128,192]{1,0,2:T(2,128)(2,1)S(1)}, u32[]{:S(2)}, u32[]{:S(2)}) collective-permute-start(bf16[2,128,192]{1,0,2:T(2,128)(2,1)S(1)} %pad_maximum_fusion.8), channel_id=1, source_target_pairs={{0,16},{16,0},{1,17},{17,1},{2,18},{18,2},{3,19},{19,3},{4,20},{20... | collective-permute-start | bytes 294920 | tf_op jit(solution)/shard_map/ppermute | solution.py:153
  77.9 12.0 %collective-permute-start.25 = (bf16[2,128,384]{1,0,2:T(2,128)(2,1)S(1)}, bf16[2,128,384]{1,0,2:T(2,128)(2,1)S(1)}, u32[]{:S(2)}, u32[]{:S(2)}) collective-permute-start(bf16[2,128,384]{1,0,2:T(2,128)(2,1)S(1)} %slice.137), channel_id=1, source_target_pairs={{0,16},{16,0},{1,17},{17,1},{2,18},{18,2},{3,19},{19,3},{4,20},{20... | collective-permute-start | bytes 589832 | tf_op jit(solution)/shard_map/ppermute | solution.py:159
  82.5 5.4 %collective-permute-start.18 = (bf16[2,128,256]{1,0,2:T(2,128)(2,1)S(1)}, bf16[2,128,256]{1,0,2:T(2,128)(2,1)S(1)}, u32[]{:S(2)}, u32[]{:S(2)}) collective-permute-start(bf16[2,128,256]{1,0,2:T(2,128)(2,1)S(1)} %pad_maximum_fusion.6), channel_id=1, source_target_pairs={{0,4},{4,8},{8,12},{12,14},{14,10},{10,6},{6,2},{2,0},{1,5},{5,9},... | collective-permute-start | bytes 393224 | tf_op jit(solution)/shard_map/ppermute | solution.py:175
  84.1 5.4 %collective-permute-start.22 = (bf16[2,128,256]{1,0,2:T(2,128)(2,1)S(1)}, bf16[2,128,256]{1,0,2:T(2,128)(2,1)S(1)}, u32[]{:S(2)}, u32[]{:S(2)}) collective-permute-start(bf16[2,128,256]{1,0,2:T(2,128)(2,1)S(1)} %pad_maximum_fusion.6), channel_id=1, source_target_pairs={{0,2},{4,0},{8,4},{12,8},{14,12},{10,14},{6,10},{2,6},{1,3},{5,1},... | collective-permute-start | bytes 393224 | tf_op jit(solution)/shard_map/ppermute | solution.py:178
  87.9 6.0 %collective-permute-start.19 = (bf16[2,128,256]{1,0,2:T(2,128)(2,1)S(1)}, bf16[2,128,256]{1,0,2:T(2,128)(2,1)S(1)}, u32[]{:S(2)}, u32[]{:S(2)}) collective-permute-start(bf16[2,128,256]{1,0,2:T(2,128)(2,1)S(1)} %collective-permute-done.18), channel_id=1, source_target_pairs={{0,4},{4,8},{8,12},{12,14},{14,10},{10,6},{6,2},{2,0},{1,5},{5,9},... | collective-permute-start | bytes 393224 | tf_op jit(solution)/shard_map/ppermute | solution.py:175
  89.5 9.0 %collective-permute-start.23 = (bf16[2,128,256]{1,0,2:T(2,128)(2,1)S(1)}, bf16[2,128,256]{1,0,2:T(2,128)(2,1)S(1)}, u32[]{:S(2)}, u32[]{:S(2)}) collective-permute-start(bf16[2,128,256]{1,0,2:T(2,128)(2,1)S(1)} %collective-permute-done.22), channel_id=1, source_target_pairs={{0,2},{4,0},{8,4},{12,8},{14,12},{10,14},{6,10},{2,6},{1,3},{5,1},... | collective-permute-start | bytes 393224 | tf_op jit(solution)/shard_map/ppermute | solution.py:178
  93.9 5.4 %collective-permute-start.20 = (bf16[2,128,256]{1,0,2:T(2,128)(2,1)S(1)}, bf16[2,128,256]{1,0,2:T(2,128)(2,1)S(1)}, u32[]{:S(2)}, u32[]{:S(2)}) collective-permute-start(bf16[2,128,256]{1,0,2:T(2,128)(2,1)S(1)} %collective-permute-done.19), channel_id=1, source_target_pairs={{0,4},{4,8},{8,12},{12,14},{14,10},{10,6},{6,2},{2,0},{1,5},{5,9},... | collective-permute-start | bytes 393224 | tf_op jit(solution)/shard_map/ppermute | solution.py:175
  98.5 5.0 %collective-permute-start.24 = (bf16[2,128,256]{1,0,2:T(2,128)(2,1)S(1)}, bf16[2,128,256]{1,0,2:T(2,128)(2,1)S(1)}, u32[]{:S(2)}, u32[]{:S(2)}) collective-permute-start(bf16[2,128,256]{1,0,2:T(2,128)(2,1)S(1)} %collective-permute-done.23), channel_id=1, source_target_pairs={{0,2},{4,0},{8,4},{12,8},{14,12},{10,14},{6,10},{2,6},{1,3},{5,1},... | collective-permute-start | bytes 393224 | tf_op jit(solution)/shard_map/ppermute | solution.py:178
  99.3 5.0 %collective-permute-start.21 = (bf16[2,128,256]{1,0,2:T(2,128)(2,1)S(1)}, bf16[2,128,256]{1,0,2:T(2,128)(2,1)S(1)}, u32[]{:S(2)}, u32[]{:S(2)}) collective-permute-start(bf16[2,128,256]{1,0,2:T(2,128)(2,1)S(1)} %collective-permute-done.20), channel_id=1, source_target_pairs={{0,4},{4,8},{8,12},{12,14},{14,10},{10,6},{6,2},{2,0},{1,5},{5,9},... | collective-permute-start | bytes 393224 | tf_op jit(solution)/shard_map/ppermute | solution.py:175
  (6 other events, 21.2 us)
